TPU v7x, 32 devices: a whole 2x2x4 slice. The times are simulated.
32 devices in a mesh: user: 16 (over z, y, x), item: 2 (over core).
Axes of the slice: x: 2, y: 2, z: 4, core: 2. Of those that a mesh axis runs over, the one named last changes fastest.
Arguments:
- draws_user: float32 [16, 768, 256], P('user', 'item'), may hold values from -200 to 200
- draws_item: float32 [2, 1024, 256], P('item', 'user'), may hold values from -200 to 200
- prior_user: float32 [64, 64], replicated, may hold values from -1 to 5, as said below
- prior_item: float32 [64, 64], replicated, may hold values from -1 to 5, as said below
- count_tiles: int32 [16, 2, 12, 256, 256], P('user', 'item'), may hold values from 0 to 3
- tile_blocks: int32 [16, 2, 12, 2], P('user', 'item'), may hold values from 0 to 3, as said below
- tile_count: int32 [16, 2], P('user', 'item'), may hold values from 4 to 12, as said below
Outputs:
- solution_user: float32 [16, 768, 256], P('user', 'item')
- solution_item: float32 [2, 1024, 256], P('item', 'user')
- residual_user: float32 [16, 768, 256], P('user', 'item')
- residual_item: float32 [2, 1024, 256], P('item', 'user')
Inputs may be any that keep to these rules, and one draw needn't show every extreme that they name: `tile_blocks`: each device's list names 12 distinct pairs (row block from 0 to 2, column block from 0 to 3); entries after tile_count are not in use. `tile_count`: some device uses all 12 tiles. `prior_user`: symmetric, diagonal from 2.5 to 4.5, each off-diagonal entry within 2 / 64 in magnitude. `prior_item`: symmetric, diagonal from 2.5 to 4.5, each off-diagonal entry within 2 / 64 in magnitude.
All inputs are finite; a program needn't handle non-finite values.
Results may differ from a plain program's by a relative error of at most 0.028.
Values may be sent and summed in bfloat16 or wider, within the bound.
No kernel may reach another device: no remote copies, remote signals or barrier semaphores. Data moves between devices by JAX's collectives and lax.ppermute only.
A program may use at most 64 MiB of HBM per device.

v0:
```python
import jax
import jax.numpy as jnp
from jax import lax
from jax.sharding import PartitionSpec as P

DIM = 64
DRAWS = 4
TILE = 256
RB = 3
CB = 4
TMAX = 12
ITERS = 2


top_prec = lax.Precision.HIGHEST
noise_prec = 0.03125


def prior_term(field_vec, prior_mat):
    row_total = field_vec.shape[0]
    grouped = field_vec.reshape(row_total, DRAWS, DIM)
    mixed = jnp.einsum("nde,ef->ndf", grouped, prior_mat, precision=top_prec)
    return mixed.reshape(row_total, DRAWS * DIM)


def per_draw(left, right):
    product = (left * right).reshape(-1, DRAWS, DIM)
    return jnp.sum(product, axis=(0, 2))


def widen(coef):
    return jnp.repeat(coef, DIM)


def per_device(
    draws_user, draws_item, prior_user, prior_item, count_tiles, tile_blocks, tile_count
):
    width = DRAWS * DIM
    user_own = draws_user[0]
    item_own = draws_item[0]
    in_use = jnp.arange(TMAX, dtype=jnp.int32) < tile_count[0, 0]
    counts_bf = jnp.where(in_use[:, None, None], count_tiles[0, 0], 0).astype(jnp.bfloat16)
    row_pick = (
        (tile_blocks[0, 0, :, 0][:, None] == jnp.arange(RB, dtype=jnp.int32)) & in_use[:, None]
    ).astype(jnp.float32)
    col_pick = (
        (tile_blocks[0, 0, :, 1][:, None] == jnp.arange(CB, dtype=jnp.int32)) & in_use[:, None]
    ).astype(jnp.float32)
    row_pick_bf = row_pick.astype(jnp.bfloat16)
    col_pick_bf = col_pick.astype(jnp.bfloat16)
    row_sums = jnp.sum(counts_bf, axis=2, dtype=jnp.float32)
    col_sums = jnp.sum(counts_bf, axis=1, dtype=jnp.float32)

    def cross_parts(user_range, item_range):
        user_sel = jnp.einsum(
            "tr,ris->tis",
            row_pick_bf,
            user_range.reshape(RB, TILE, width),
            preferred_element_type=jnp.float32,
        )
        item_sel = jnp.einsum(
            "tc,cjs->tjs",
            col_pick_bf,
            item_range.reshape(CB, TILE, width),
            preferred_element_type=jnp.float32,
        )
        to_users = (
            jnp.einsum(
                "tij,tjs->tis",
                counts_bf,
                item_sel.astype(jnp.bfloat16),
                preferred_element_type=jnp.float32,
            )
            + row_sums[:, :, None] * user_sel
        )
        to_items = (
            jnp.einsum(
                "tij,tis->tjs",
                counts_bf,
                user_sel.astype(jnp.bfloat16),
                preferred_element_type=jnp.float32,
            )
            + col_sums[:, :, None] * item_sel
        )
        part_user = jnp.einsum("tr,tis->ris", row_pick, to_users, precision=top_prec).reshape(
            RB * TILE, width
        )
        part_item = jnp.einsum("tc,tjs->cjs", col_pick, to_items, precision=top_prec).reshape(
            CB * TILE, width
        )
        return (part_user, part_item)

    def user_range_of(user_vec):
        return lax.all_gather(user_vec.astype(jnp.bfloat16), "item", axis=0, tiled=True)

    def finish_users(user_vec, part_user):
        total = lax.psum_scatter(
            part_user.astype(jnp.bfloat16), "item", scatter_dimension=0, tiled=True
        ).astype(jnp.float32)
        return prior_term(user_vec, prior_user) + noise_prec * total

    def item_range_of(item_vec):
        return lax.all_gather(item_vec.astype(jnp.bfloat16), "user", axis=0, tiled=True)

    def finish_items(item_vec, part_item):
        total = lax.psum_scatter(part_item, "user", scatter_dimension=0, tiled=True)
        return prior_term(item_vec, prior_item) + noise_prec * total

    def operate(user_vec, item_vec):
        part_user, part_item = cross_parts(user_range_of(user_vec), item_range_of(item_vec))
        return (finish_users(user_vec, part_user), finish_items(item_vec, part_item))

    def inner(a_user, a_item, b_user, b_item):
        return per_draw(a_user, b_user) + per_draw(a_item, b_item)

    sol_user = jnp.zeros_like(user_own)
    sol_item = jnp.zeros_like(item_own)
    res_user, res_item = (user_own, item_own)
    dir_user, dir_item = (user_own, item_own)

    def two_sums(u_vec, v_vec, image_u, image_v):
        return lax.psum(
            (inner(u_vec, v_vec, u_vec, v_vec), inner(u_vec, v_vec, image_u, image_v)),
            ("user", "item"),
        )

    along_user, along_item = operate(res_user, res_item)
    norm_now, curve = two_sums(res_user, res_item, along_user, along_item)
    step_len = norm_now / curve
    for iteration in range(ITERS):
        sol_user = sol_user + widen(step_len) * dir_user
        sol_item = sol_item + widen(step_len) * dir_item
        res_user = res_user - widen(step_len) * along_user
        res_item = res_item - widen(step_len) * along_item
        if iteration + 1 < ITERS:
            image_user, image_item = operate(res_user, res_item)
            norm_next, curve = two_sums(res_user, res_item, image_user, image_item)
            beta_coef = norm_next / norm_now
            step_len = norm_next / (curve - beta_coef * norm_next / step_len)
            dir_user = res_user + widen(beta_coef) * dir_user
            dir_item = res_item + widen(beta_coef) * dir_item
            along_user = image_user + widen(beta_coef) * along_user
            along_item = image_item + widen(beta_coef) * along_item
            norm_now = norm_next
    return (sol_user[None], sol_item[None], res_user[None], res_item[None])


def solution(mesh):
    in_specs = (
        P("user", "item", None),
        P("item", "user", None),
        P(),
        P(),
        P("user", "item", None, None, None),
        P("user", "item", None, None),
        P("user", "item"),
    )
    out_specs = (
        P("user", "item", None),
        P("item", "user", None),
        P("user", "item", None),
        P("item", "user", None),
    )
    return jax.shard_map(
        per_device, mesh=mesh, in_specs=in_specs, out_specs=out_specs, check_vma=False
    )
```

profile of v0, /device:TPU:0, one launch (start us, length us, event | category | flops | bytes accessed | tf_op | source)
XLA Modules:
  0.0 385.7 jit_solution(13057737893118011805)
XLA Ops:
  7.9 0.8 slice_bitcast_fusion
  8.7 1.1 multiply_reduce_fusion.2
  9.7 2.2 all_gather.13
  11.9 2.5 convert_reduce_fusion
  14.5 45.4 %all_gather.12 = bf16[1024,256]{1,0:T(8,128)(2,1)S(1)} all-gather(bf16[64,256]{1,0:T(8,128)(2,1)S(1)} %get-tuple-element.28), channel_id=1, replica_groups=mesh['user'=16,'item'=2] {'user'}, dimensions={0}, use_global_device_ids=true | all-gather | bytes 557056 | tf_op jit(solution)/shard_map/all_gather | solution.py:103
  59.9 2.1 fusion.69
  62.0 2.7 fusion.68
  64.8 3.0 fusion.10
  67.8 3.3 fusion.19
  71.1 0.8 copy.75
  71.9 0.1 copy.81
  72.1 2.7 fusion.16
  74.8 0.2 copy-done.2
  75.0 3.8 fusion.3
  78.8 1.2 copy.83
  80.1 0.1 reshape_squeeze.7
  80.2 0.2 copy.68
  80.4 0.2 fusion.40
  80.6 0.1 copy.78
  80.7 0.1 reshape.84
  80.9 0.5 fusion.51
  81.4 0.2 copy.76
  81.7 0.1 reduce_sum.113
  81.8 0.1 reduce_sum.119
  82.0 1.0 fusion.33
  83.0 0.1 reduce_sum.125
  83.1 0.1 reduce_sum.126
  83.2 73.9 %reduce-scatter.7.cloned.1.call-done = f32[64,256]{1,0:T(8,128)} async-done(((f32[1024,256]{1,0:T(8,128)}), f32[64,256]{1,0:T(8,128)}) %reduce-scatter.7.cloned.1.call-update) | async-done | bytes 65552 | tf_op jit(solution)/shard_map/reduce_scatter | solution.py:106
  157.1 0.9 fusion.42
  157.9 0.1 reduce_sum.129
  158.0 0.1 reduce_sum.133
  158.1 37.1 %all-reduce.1 = (f32[4]{0:T(128)S(1)}, f32[4]{0:T(128)S(1)}) all-reduce(f32[4]{0:T(128)S(1)} %add.70, f32[4]{0:T(128)S(1)} %add.75), channel_id=1, replica_groups=mesh['user'=16,'item'=2] {'user','item'}, use_global_device_ids=true, to_apply=%region_4.5 | all-reduce | flops 8 | bytes 64 | tf_op jit(solution)/shard_map/psum | solution.py:122
  195.4 0.9 fusion.65
  196.2 41.8 %all_gather.14 = bf16[1024,256]{1,0:T(8,128)(2,1)S(1)} all-gather(bf16[64,256]{1,0:T(8,128)(2,1)S(1)} %get-tuple-element.16), channel_id=1, replica_groups=mesh['user'=16,'item'=2] {'user'}, dimensions={0}, use_global_device_ids=true | all-gather | bytes 557056 | tf_op jit(solution)/shard_map/all_gather | solution.py:103
  238.1 2.7 fusion.70
  240.9 2.1 all_gather.15
  242.9 2.1 fusion.71
  245.1 3.0 fusion.9
  248.1 3.3 fusion.22
  251.4 0.8 copy.91
  252.3 2.7 fusion.13
  255.0 0.2 copy-done.1
  255.2 3.8 fusion
  259.0 1.2 copy.98
  260.2 0.1 reshape.90
  260.3 0.2 fusion.38
  260.5 0.1 copy.94
  260.6 0.1 reshape.91
  260.8 0.2 copy.84
  260.9 0.5 fusion.49
  261.5 0.2 copy.92
  261.7 1.0 multiply_reduce_fusion
  262.7 0.1 reduce_sum.167
  262.8 0.1 reduce_sum.168
  263.0 0.1 reduce_sum.162
  263.1 74.0 %reduce-scatter.11.cloned.1.call-done = f32[64,256]{1,0:T(8,128)} async-done(((f32[1024,256]{1,0:T(8,128)}), f32[64,256]{1,0:T(8,128)}) %reduce-scatter.11.cloned.1.call-update) | async-done | bytes 65552 | tf_op jit(solution)/shard_map/reduce_scatter | solution.py:106
  337.1 0.9 multiply_reduce_fusion.3
  338.0 0.1 reduce_sum.170
  338.1 0.1 reduce_sum.171
  338.3 0.1 reduce_sum.165
  338.4 36.9 %all-reduce = (f32[4]{0:T(128)S(1)}, f32[4]{0:T(128)S(1)}) all-reduce(f32[4]{0:T(128)S(1)} %add.76, f32[4]{0:T(128)S(1)} %add.81), channel_id=1, replica_groups=mesh['user'=16,'item'=2] {'user','item'}, use_global_device_ids=true, to_apply=%region_18.19 | all-reduce | flops 8 | bytes 64 | tf_op jit(solution)/shard_map/psum | solution.py:122
  375.4 0.1 mul.186
  375.7 1.5 subtract_bitcast_fusion.1
  377.2 2.0 subtract_bitcast_fusion
  (44 shorter events, 1.2 us)
Async XLA Ops:
  7.2 73.7 %copy-start = (f32[64,64]{1,0:T(8,128)S(1)}, f32[64,64]{1,0:T(8,128)}, u32[]{:S(2)}) copy-start(f32[64,64]{1,0:T(8,128)} %param.9) | copy-start | bytes 49156
  7.2 7.3 %copy-start.5 = (f32[1,64,256]{2,1,0:T(8,128)S(1)}, f32[1,64,256]{2,1,0:T(8,128)}, u32[]{:S(2)}) copy-start(f32[1,64,256]{2,1,0:T(8,128)} %param.8) | copy-start | bytes 196612
  7.2 74.8 %reduce-scatter.5.cloned.1.call-start = ((), (), s32[]{:S(2)}) async-start(), calls=%async_computation.4 | async-start | bytes 589824 | tf_op jit(solution)/shard_map/reduce_scatter | solution.py:97
  71.9 85.2 %reduce-scatter.7.cloned.1.call-start = ((), (), s32[]{:S(2)}) async-start(), calls=%async_computation.5 | async-start | bytes 1114112 | tf_op jit(solution)/shard_map/reduce_scatter | solution.py:106
  72.1 3.0 copy-start.2
  78.8 1.4 copy-start.3
  78.8 1.6 copy-start.7
  80.0 181.7 %reduce-scatter.9.cloned.1.call-start = ((), (), s32[]{:S(2)}) async-start(), calls=%async_computation.6 | async-start | bytes 589824 | tf_op jit(solution)/shard_map/reduce_scatter | solution.py:97
  238.1 2.7 copy-start.4
  252.2 84.9 %reduce-scatter.11.cloned.1.call-start = ((), (), s32[]{:S(2)}) async-start(), calls=%async_computation.7 | async-start | bytes 1114112 | tf_op jit(solution)/shard_map/reduce_scatter | solution.py:106
  252.2 3.0 copy-start.1
  260.1 115.5 %copy-start.6 = (f32[64,256]{1,0:T(8,128)S(1)}, f32[64,256]{1,0:T(8,128)}, u32[]{:S(2)}) copy-start(f32[64,256]{1,0:T(8,128)} %reduce-scatter.7.cloned.1.call-done) | copy-start | bytes 196612
Sparse Core Ops, SparseCore 0:
  72.0 3.6 reduce-scatter.4
  80.1 76.8 reduce-scatter.6
  252.3 3.6 reduce-scatter.8
  260.3 76.8 reduce-scatter.10
where the time goes:
time: 387 us; the launch traced here: 386 us
  blocking collectives  165 us (43%)
  waiting for transfers between devices  148 us (38%)
  matrix products  36.7 us (9%)
  between operations  14.7 us (4%)
  other arithmetic  12.9 us (3%)
  local copies, waits for them, and re-layouts  7.79 us (2%)
    reduce_scatter x2, waiting for transfers between devices, finish_items(): total = lax.psum_scatter(part_item, 'user', scatter_dimension=0, tiled=True)  148 us
    all_gather x2, blocking collectives, item_range_of(): lax.all_gather(item_vec.astype(jnp.bfloat16), 'user', axis=0, tiled=True)  87.3 us
    psum x2, blocking collectives, two_sums(): lax.psum((inner(u_vec, v_vec, u_vec, v_vec), inner(u_vec, v_vec, image_u,...  74 us
  transfers between devices with their start and end apart: 4, of which 2 were waited for; matrix products, arithmetic and copies ran while one was open for 6% of the time, Pallas kernels for 0%

commit v1 on v0

--- a/solution.py
+++ b/solution.py
@@ -30,6 +30,60 @@
 
 def widen(coef):
     return jnp.repeat(coef, DIM)
+
+
+def bit_count(axis):
+    size = lax.axis_size(axis)
+    bits = size.bit_length() - 1
+    assert size == 1 << bits
+    return size, bits
+
+
+def swap_with(value, axis, size, bit):
+    pairs = [(i, i ^ (1 << bit)) for i in range(size)]
+    return lax.ppermute(value, axis, pairs)
+
+
+def butterfly_psum(values):
+    values = jnp.stack(values)
+    for axis in ("item", "user"):
+        size, bits = bit_count(axis)
+        for bit in range(bits):
+            values = values + swap_with(values, axis, size, bit)
+    return values[0], values[1]
+
+
+def halve_sum(part, axis, send_type):
+    size, bits = bit_count(axis)
+    me = lax.axis_index(axis)
+    rows, width = part.shape[0] // size, part.shape[1]
+    left = list(range(bits))[::-1]
+    buf = part.reshape([2] * bits + [rows, width])
+    for bit in range(bits):
+        pos = left.index(bit)
+        low = lax.index_in_dim(buf, 0, pos, keepdims=False)
+        high = lax.index_in_dim(buf, 1, pos, keepdims=False)
+        upper = ((me >> bit) & 1) == 1
+        keep = jnp.where(upper, high, low)
+        send = jnp.where(upper, low, high).astype(send_type)
+        buf = keep + swap_with(send, axis, size, bit).astype(jnp.float32)
+        left.remove(bit)
+    return buf.reshape(rows, width)
+
+
+def double_gather(piece, axis):
+    size, bits = bit_count(axis)
+    me = lax.axis_index(axis)
+    buf = piece[None]
+    for step, bit in enumerate(reversed(range(bits))):
+        other = swap_with(buf, axis, size, bit)
+        upper = ((me >> bit) & 1) == 1
+        first = jnp.where(upper, other, buf)
+        second = jnp.where(upper, buf, other)
+        buf = jnp.stack([first, second], axis=step)
+        buf = buf.reshape((-1,) + piece.shape)
+        buf = buf.reshape([2] * (step + 1) + list(piece.shape))
+    return buf.reshape((size * piece.shape[0],) + piece.shape[1:])
 
 
 def per_device(
@@ -94,16 +148,14 @@
         return lax.all_gather(user_vec.astype(jnp.bfloat16), "item", axis=0, tiled=True)
 
     def finish_users(user_vec, part_user):
-        total = lax.psum_scatter(
-            part_user.astype(jnp.bfloat16), "item", scatter_dimension=0, tiled=True
-        ).astype(jnp.float32)
+        total = halve_sum(part_user, "item", jnp.bfloat16)
         return prior_term(user_vec, prior_user) + noise_prec * total
 
     def item_range_of(item_vec):
-        return lax.all_gather(item_vec.astype(jnp.bfloat16), "user", axis=0, tiled=True)
+        return double_gather(item_vec.astype(jnp.bfloat16), "user")
 
     def finish_items(item_vec, part_item):
-        total = lax.psum_scatter(part_item, "user", scatter_dimension=0, tiled=True)
+        total = halve_sum(part_item, "user", jnp.float32)
         return prior_term(item_vec, prior_item) + noise_prec * total
 
     def operate(user_vec, item_vec):
@@ -119,9 +171,8 @@
     dir_user, dir_item = (user_own, item_own)
 
     def two_sums(u_vec, v_vec, image_u, image_v):
-        return lax.psum(
+        return butterfly_psum(
             (inner(u_vec, v_vec, u_vec, v_vec), inner(u_vec, v_vec, image_u, image_v)),
-            ("user", "item"),
         )
 
     along_user, along_item = operate(res_user, res_item)

time: 387 us -> 182 us (0.47)
  blocking collectives: 165 us -> 4.37 us
  waiting for transfers between devices: 148 us -> 62.8 us
  starting transfers between devices: 0.16 us -> 24 us
  local copies, waits for them, and re-layouts: 7.79 us -> 23.7 us
  between operations: 14.7 us -> 1.93 us
  matrix products: 36.7 us -> 46.4 us
  other arithmetic: 12.9 us -> 17.8 us
    reduce_scatter x4 -> x0, waiting for transfers between devices: 148 us -> none  [the longest x2 148 us: finish_items(): total = lax.psum_scatter(part_item, 'user', scatter_dimension=0, tiled=True)]
    all_gather x2 -> x0, blocking collectives: 87.3 us -> none  [item_range_of(): lax.all_gather(item_vec.astype(jnp.bfloat16), 'user', axis=0, tiled=True)]
    psum x2 -> x0, blocking collectives: 74 us -> none  [two_sums(): lax.psum((inner(u_vec, v_vec, u_vec, v_vec), inner(u_vec, v_vec, image_u,...]
    ppermute x0 -> x28, waiting for transfers between devices: none -> 62.8 us  [swap_with(): return lax.ppermute(value, axis, pairs)]
    ppermute x0 -> x28, starting transfers between devices: none -> 24 us  [swap_with(): return lax.ppermute(value, axis, pairs)]
    reshape x4, local copies, waits for them, and re-layouts: 0.6 us -> 6.16 us  [prior_term(): return mixed.reshape(row_total, DRAWS * DIM)]
    another operation x0 -> x6, local copies, waits for them, and re-layouts: none -> 5.25 us  [the longest x2 3.65 us: halve_sum(): buf = part.reshape([2] * bits + [rows, width])]
    dot_general x2, matrix products: 6 us -> 10.3 us  [cross_parts(): jnp.einsum('tij,tjs->tis', counts_bf, item_sel.astype(jnp.bfloat16), pref...]
  transfers between devices with their start and end apart: 4 -> 28, of which waited for: 2 -> 23; matrix products, arithmetic and copies ran while one was open for 6% -> 30% of each run, Pallas kernels for 0% -> 0%
where the time goes in v1:
time: 182 us; the launch traced here: 181 us
  waiting for transfers between devices  62.8 us (35%)
  matrix products  46.4 us (25%)
  starting transfers between devices  24 us (13%)
  local copies, waits for them, and re-layouts  23.7 us (13%)
  other arithmetic  17.8 us (10%)
  blocking collectives  4.37 us (2%)
  between operations  1.93 us (1%)
    ppermute x28, waiting for transfers between devices, swap_with(): return lax.ppermute(value, axis, pairs)  62.8 us
    ppermute x28, starting transfers between devices, swap_with(): return lax.ppermute(value, axis, pairs)  24 us
    dot_general x2, matrix products, cross_parts(): jnp.einsum('tij,tjs->tis', counts_bf, item_sel.astype(jnp.bfloat16), pref...  10.3 us
    dot_general x2, matrix products, cross_parts(): jnp.einsum('tc,tjs->cjs', col_pick, to_items, precision=top_prec)  7.68 us
    dot_general x2, matrix products, cross_parts(): jnp.einsum('tij,tis->tjs', counts_bf, user_sel.astype(jnp.bfloat16), pref...  6.93 us
    dot_general x2, matrix products, cross_parts(): jnp.einsum('tr,ris->tis', row_pick_bf, user_range.reshape(RB, TILE, width...  6.84 us
    dot_general x2, matrix products, cross_parts(): jnp.einsum('tr,tis->ris', row_pick, to_users, precision=top_prec)  6.5 us
    reduce_sum x14, other arithmetic, per_draw(): return jnp.sum(product, axis=(0, 2))  6.32 us
  transfers between devices with their start and end apart: 28, of which 23 were waited for; matrix products, arithmetic and copies ran while one was open for 30% of the time, Pallas kernels for 0%

profile of v1, /device:TPU:0, one launch (start us, length us, event | category | flops | bytes accessed | tf_op | source)
XLA Modules:
  0.0 181.0 jit_solution(10940996595989492387)
XLA Ops:
  0.6 1.5 multiply_reduce_fusion.5
  2.2 4.0 %collective-permute-start = (bf16[1,64,256]{2,1,0:T(8,128)(2,1)S(1)}, bf16[1,64,256]{2,1,0:T(8,128)(2,1)S(1)}, u32[]{:S(2)}, u32[]{:S(2)}) collective-permute-start(bf16[1,64,256]{2,1,0:T(8,128)(2,1)S(1)} %get-tuple-element.48), channel_id=1, source_target_pairs={{0,16},{2,18},{4,20},{6,22},{8,24},{10,26},{12,28},{14,30},{16,0},... | collective-permute-start | bytes 98312 | tf_op jit(solution)/shard_map/ppermute | solution.py:44
  7.6 1.6 multiply_reduce_fusion.2
  9.3 2.1 %all_gather.6 = bf16[768,256]{1,0:T(8,128)(2,1)S(1)} all-gather(bf16[384,256]{1,0:T(8,128)(2,1)S(1)} %get-tuple-element.34), channel_id=1, replica_groups=mesh['user'=16,'item'=2] {'item'}, dimensions={0}, use_global_device_ids=true | all-gather | bytes 589824 | tf_op jit(solution)/shard_map/all_gather | solution.py:148
  11.4 3.5 %fusion.81 = (bf16[12,256,256]{2,0,1:T(8,128)(2,1)}, f32[12,256,256]{2,0,1:T(8,128)}) fusion(bf16[3,256,256]{2,1,0:T(8,128)(2,1)S(1)} %bitcast.261, pred[12,3]{0,1:T(4,128)(4,1)S(1)} %fusion.53), kind=kOutput, calls=%fused_computation.158 | convolution fusion | flops 5505096 | bytes 5111844 | tf_op jit(solution)/shard_map/tr,ris->tis/dot_general | solution.py:109
  14.9 1.6 collective-permute-start.1
  16.5 2.5 %convert_reduce_fusion = (f32[12,256]{1,0:T(8,128)S(1)}, f32[12,256]{1,0:T(8,128)S(1)}, bf16[12,256,256]{2,1,0:T(8,128)(2,1)S(1)}) fusion(s32[1,1,12,256,256]{4,3,2,1,0:T(8,128)} %param.11, pred[12]{0:T(512)(128)(4,1)S(1)} %iota_compare_fusion.2), kind=kLoop, calls=%fused_computation.10 | loop fusion | flops 3926016 | bytes 4743180 | tf_op jit(solution)/shard_map/reduce_sum | solution.py:106
  19.3 1.6 collective-permute-start.2
  20.8 4.3 %fusion.16 = f32[12,256,256]{2,1,0:T(8,128)} fusion(bf16[12,256,256]{2,1,0:T(8,128)(2,1)S(1)} %get-tuple-element.22, bf16[12,256,256]{2,0,1:T(8,128)(2,1)} %get-tuple-element.55), kind=kOutput, calls=%fused_computation.23 | convolution fusion | flops 402653184 | bytes 6291456 | tf_op jit(solution)/shard_map/tij,tis->tjs/dot_general | solution.py:131
  25.2 1.6 collective-permute-start.3
  29.0 4.0 %collective-permute-done.3 = bf16[2,2,2,64,256]{4,3,0,1,2:T(8,128)(2,1)} collective-permute-done((bf16[2,2,2,64,256]{4,3,0,1,2:T(8,128)(2,1)S(1)}, bf16[2,2,2,64,256]{4,3,0,1,2:T(8,128)(2,1)}, u32[]{:S(2)}, u32[]{:S(2)}) %collective-permute-start.3) | collective-permute-done | bytes 262176 | tf_op jit(solution)/shard_map/ppermute | solution.py:44
  33.0 1.0 select_bitcast_fusion.7
  34.9 2.2 %fusion.80 = (bf16[12,256,256]{2,0,1:T(8,128)(2,1)}, f32[12,256,256]{2,0,1:T(8,128)S(1)}) fusion(bf16[4,256,256]{2,0,1:T(4,128)(2,1)S(1)} %reshape_reshape_reshape_reshape.6, pred[12,4]{0,1:T(4,128)(4,1)S(1)} %fusion.54), kind=kOutput, calls=%fused_computation.157 | convolution fusion | flops 7077984 | bytes 5242928 | tf_op jit(solution)/shard_map/tc,cjs->tjs/dot_general | solution.py:115
  37.1 3.9 %fusion.3 = f32[4,256,256]{2,0,1:T(4,128)S(1)} fusion(f32[12,256,256]{2,1,0:T(8,128)S(1)} %copy-done.1, f32[12,256,256]{2,0,1:T(8,128)S(1)} %get-tuple-element.54, f32[12,256]{0,1:T(8,128)S(1)} %copy-done.9, pred[12,4]{0,1:T(4,128)(4,1)S(1)} %fusion.54), kind=kOutput, calls=%fused_computation.5 | convolution fusion | flops 39321600 | bytes 7352368 | tf_op jit(solution)/shard_map/tc,tjs->cjs/dot_general | solution.py:142
  41.0 1.8 %reshape_reshape.13 = f32[2,2,2,2,64,256]{5,1,0,4,3,2:T(2,128)} reshape(f32[4,256,256]{2,0,1:T(4,128)S(1)} %fusion.3) | data formatting | bytes 2097152 | tf_op jit(solution)/shard_map/reshape;reshape | solution.py:61
  42.9 1.6 fusion.79
  44.5 1.0 select_bitcast_fusion.1
  45.4 1.5 collective-permute-start.5
  47.9 1.6 copy.92
  49.5 1.7 reshape.164
  51.2 0.9 copy.90
  54.9 5.2 %fusion.10 = f32[12,256,256]{2,1,0:T(8,128)S(1)} fusion(f32[12,256,256]{2,0,1:T(8,128)} %get-tuple-element.56, bf16[12,256,256]{2,1,0:T(8,128)(2,1)S(1)} %get-tuple-element.22, bf16[12,256,256]{2,0,1:T(8,128)(2,1)} %get-tuple-element.53, f32[12,256]{1,0:T(8,128)S(1)} %get-tuple-element.5), kind=kOutput, calls=%fused_computation.17 | convolution fusion | flops 404226048 | bytes 9449472 | tf_op jit(solution)/shard_map/tij,tjs->tis/dot_general | solution.py:122
  60.0 1.2 bitcast_add_fusion.1
  61.9 3.2 %fusion.4 = f32[3,256,256]{2,0,1:T(4,128)S(1)} fusion(f32[12,256,256]{2,1,0:T(8,128)S(1)} %fusion.10, pred[12,3]{0,1:T(4,128)(4,1)S(1)} %copy-done.24), kind=kOutput, calls=%fused_computation.6 | convolution fusion | flops 28311552 | bytes 3932196 | tf_op jit(solution)/shard_map/tr,tis->ris/dot_general | solution.py:139
  65.4 2.5 %collective-permute-done.6 = f32[2,2,64,256]{3,2,0,1:T(8,128)S(1)} collective-permute-done((f32[2,2,64,256]{3,2,0,1:T(8,128)S(1)}, f32[2,2,64,256]{3,2,0,1:T(8,128)S(1)}, u32[]{:S(2)}, u32[]{:S(2)}) %collective-permute-start.6) | collective-permute-done | bytes 262176 | tf_op jit(solution)/shard_map/ppermute | solution.py:44
  68.9 4.1 %collective-permute-done.7 = f32[2,64,256]{2,1,0:T(8,128)S(1)} collective-permute-done((f32[2,64,256]{2,1,0:T(8,128)S(1)}, f32[2,64,256]{2,1,0:T(8,128)S(1)}, u32[]{:S(2)}, u32[]{:S(2)}) %collective-permute-start.7) | collective-permute-done | bytes 131104 | tf_op jit(solution)/shard_map/ppermute | solution.py:44
  73.7 4.5 %collective-permute-done.8 = f32[64,256]{1,0:T(8,128)S(1)} collective-permute-done((f32[64,256]{1,0:T(8,128)S(1)}, f32[64,256]{1,0:T(8,128)S(1)}, u32[]{:S(2)}, u32[]{:S(2)}) %collective-permute-start.8) | collective-permute-done | bytes 65568 | tf_op jit(solution)/shard_map/ppermute | solution.py:44
  78.6 1.1 collective-permute-done.9
  80.3 3.0 %collective-permute-done.10 = f32[2,4]{1,0:T(2,128)S(1)} collective-permute-done((f32[2,4]{1,0:T(2,128)S(1)}, f32[2,4]{1,0:T(2,128)S(1)}, u32[]{:S(2)}, u32[]{:S(2)}) %collective-permute-start.10) | collective-permute-done | bytes 64 | tf_op jit(solution)/shard_map/ppermute | solution.py:44
  83.9 3.1 %collective-permute-done.11 = f32[2,4]{1,0:T(2,128)S(1)} collective-permute-done((f32[2,4]{1,0:T(2,128)S(1)}, f32[2,4]{1,0:T(2,128)S(1)}, u32[]{:S(2)}, u32[]{:S(2)}) %collective-permute-start.11) | collective-permute-done | bytes 64 | tf_op jit(solution)/shard_map/ppermute | solution.py:44
  87.0 1.5 collective-permute-start.12
  88.5 2.1 %collective-permute-done.12 = f32[2,4]{1,0:T(2,128)S(1)} collective-permute-done((f32[2,4]{1,0:T(2,128)S(1)}, f32[2,4]{1,0:T(2,128)S(1)}, u32[]{:S(2)}, u32[]{:S(2)}) %collective-permute-start.12) | collective-permute-done | bytes 64 | tf_op jit(solution)/shard_map/ppermute | solution.py:44
  91.0 4.0 %collective-permute-done.13 = f32[2,4]{1,0:T(2,128)S(1)} collective-permute-done((f32[2,4]{1,0:T(2,128)S(1)}, f32[2,4]{1,0:T(2,128)S(1)}, u32[]{:S(2)}, u32[]{:S(2)}) %collective-permute-start.13) | collective-permute-done | bytes 64 | tf_op jit(solution)/shard_map/ppermute | solution.py:44
  96.2 4.3 %collective-permute-done.14 = bf16[1,64,256]{2,1,0:T(8,128)(2,1)S(1)} collective-permute-done((bf16[1,64,256]{2,1,0:T(8,128)(2,1)S(1)}, bf16[1,64,256]{2,1,0:T(8,128)(2,1)S(1)}, u32[]{:S(2)}, u32[]{:S(2)}) %collective-permute-start.14) | collective-permute-done | bytes 32800 | tf_op jit(solution)/shard_map/ppermute | solution.py:44
  100.5 1.6 collective-permute-start.15
  102.1 2.3 %all_gather.7 = bf16[768,256]{1,0:T(8,128)(2,1)S(1)} all-gather(bf16[384,256]{1,0:T(8,128)(2,1)S(1)} %get-tuple-element.16), channel_id=1, replica_groups=mesh['user'=16,'item'=2] {'item'}, dimensions={0}, use_global_device_ids=true | all-gather | bytes 589824 | tf_op jit(solution)/shard_map/all_gather | solution.py:148
  105.4 3.4 %fusion.83 = (bf16[12,256,256]{2,0,1:T(8,128)(2,1)S(1)}, f32[12,256,256]{2,0,1:T(8,128)}) fusion(bf16[3,256,256]{2,1,0:T(8,128)(2,1)S(1)} %bitcast.260, pred[12,3]{0,1:T(4,128)(4,1)} %copy-done.23), kind=kOutput, calls=%fused_computation.160 | convolution fusion | flops 5505096 | bytes 5111844 | tf_op jit(solution)/shard_map/tr,ris->tis/dot_general | solution.py:109
  108.8 1.3 collective-permute-done.16
  110.7 2.7 %fusion.13 = f32[12,256,256]{2,1,0:T(8,128)} fusion(bf16[12,256,256]{2,1,0:T(8,128)(2,1)S(1)} %get-tuple-element.22, bf16[12,256,256]{2,0,1:T(8,128)(2,1)S(1)} %get-tuple-element.59), kind=kOutput, calls=%fused_computation.20 | convolution fusion | flops 402653184 | bytes 6291456 | tf_op jit(solution)/shard_map/tij,tis->tjs/dot_general | solution.py:131
  114.3 1.3 fusion.49
  115.6 1.7 collective-permute-done.17
  117.2 1.0 select_bitcast_fusion.4
  119.1 3.0 %fusion.82 = (bf16[12,256,256]{2,0,1:T(8,128)(2,1)}, f32[12,256,256]{2,0,1:T(8,128)S(1)}) fusion(bf16[4,256,256]{2,0,1:T(4,128)(2,1)S(1)} %reshape_reshape_reshape_reshape.7, pred[12,4]{0,1:T(4,128)(4,1)} %copy-done.21), kind=kOutput, calls=%fused_computation.159 | convolution fusion | flops 7077984 | bytes 5242928 | tf_op jit(solution)/shard_map/tc,cjs->tjs/dot_general | solution.py:115
  122.2 3.8 %fusion = f32[4,256,256]{2,0,1:T(4,128)S(1)} fusion(f32[12,256,256]{2,1,0:T(8,128)S(1)} %copy-done.2, f32[12,256,256]{2,0,1:T(8,128)S(1)} %get-tuple-element.58, f32[12,256]{0,1:T(8,128)S(1)} %copy-done.10, pred[12,4]{0,1:T(4,128)(4,1)S(1)} %copy-done.22), kind=kOutput, calls=%fused_computation.1 | convolution fusion | flops 39321600 | bytes 7352368 | tf_op jit(solution)/shard_map/tc,tjs->cjs/dot_general | solution.py:142
  125.9 1.8 %reshape_reshape.15 = f32[2,2,2,2,64,256]{5,1,0,4,3,2:T(2,128)} reshape(f32[4,256,256]{2,0,1:T(4,128)S(1)} %fusion) | data formatting | bytes 2097152 | tf_op jit(solution)/shard_map/reshape;reshape | solution.py:61
  127.8 1.6 fusion.78
  129.4 1.0 select_bitcast_fusion
  131.9 1.7 reshape.170
  133.6 1.9 %copy.107 = f32[384,256]{1,0:T(8,128)} copy(f32[384,256]{0,1:T(8,128)} %bitcast.263) | data formatting | bytes 786432 | tf_op jit(solution)/shard_map/reshape | solution.py:23
  135.5 5.2 %fusion.9 = f32[12,256,256]{2,1,0:T(8,128)S(1)} fusion(f32[12,256,256]{2,0,1:T(8,128)} %get-tuple-element.60, bf16[12,256,256]{2,1,0:T(8,128)(2,1)S(1)} %get-tuple-element.22, bf16[12,256,256]{2,0,1:T(8,128)(2,1)} %get-tuple-element.57, f32[12,256]{1,0:T(8,128)S(1)} %get-tuple-element.5), kind=kOutput, calls=%fused_computation.15 | convolution fusion | flops 404226048 | bytes 9449472 | tf_op jit(solution)/shard_map/tij,tjs->tis/dot_general | solution.py:122
  140.6 1.7 collective-permute-done.19
  142.3 1.2 bitcast_add_fusion
  143.6 1.5 collective-permute-start.20
  145.1 3.2 %fusion.1 = f32[3,256,256]{2,0,1:T(4,128)S(1)} fusion(f32[12,256,256]{2,1,0:T(8,128)S(1)} %fusion.9, pred[12,3]{0,1:T(4,128)(4,1)S(1)} %copy-done.25), kind=kOutput, calls=%fused_computation.2 | convolution fusion | flops 28311552 | bytes 3932196 | tf_op jit(solution)/shard_map/tr,tis->ris/dot_general | solution.py:139
  148.6 1.5 collective-permute-done.20
  150.4 5.5 %collective-permute-done.21 = f32[2,64,256]{2,1,0:T(8,128)S(1)} collective-permute-done((f32[2,64,256]{2,1,0:T(8,128)S(1)}, f32[2,64,256]{2,1,0:T(8,128)S(1)}, u32[]{:S(2)}, u32[]{:S(2)}) %collective-permute-start.21) | collective-permute-done | bytes 131104 | tf_op jit(solution)/shard_map/ppermute | solution.py:44
  157.0 4.1 %collective-permute-done.22 = f32[64,256]{1,0:T(8,128)S(1)} collective-permute-done((f32[64,256]{1,0:T(8,128)S(1)}, f32[64,256]{1,0:T(8,128)S(1)}, u32[]{:S(2)}, u32[]{:S(2)}) %collective-permute-start.22) | collective-permute-done | bytes 65568 | tf_op jit(solution)/shard_map/ppermute | solution.py:44
  162.6 1.1 collective-permute-done.23
  164.4 2.9 %collective-permute-done.24 = f32[2,4]{1,0:T(2,128)S(1)} collective-permute-done((f32[2,4]{1,0:T(2,128)S(1)}, f32[2,4]{1,0:T(2,128)S(1)}, u32[]{:S(2)}, u32[]{:S(2)}) %collective-permute-start.24) | collective-permute-done | bytes 64 | tf_op jit(solution)/shard_map/ppermute | solution.py:44
  167.3 1.6 collective-permute-start.25
  168.9 2.0 %collective-permute-done.25 = f32[2,4]{1,0:T(2,128)S(1)} collective-permute-done((f32[2,4]{1,0:T(2,128)S(1)}, f32[2,4]{1,0:T(2,128)S(1)}, u32[]{:S(2)}, u32[]{:S(2)}) %collective-permute-start.25) | collective-permute-done | bytes 64 | tf_op jit(solution)/shard_map/ppermute | solution.py:44
  171.0 3.6 %collective-permute-done.26 = f32[2,4]{1,0:T(2,128)S(1)} collective-permute-done((f32[2,4]{1,0:T(2,128)S(1)}, f32[2,4]{1,0:T(2,128)S(1)}, u32[]{:S(2)}, u32[]{:S(2)}) %collective-permute-start.26) | collective-permute-done | bytes 64 | tf_op jit(solution)/shard_map/ppermute | solution.py:44
  175.0 4.0 %collective-permute-done.27 = f32[2,4]{1,0:T(2,128)S(1)} collective-permute-done((f32[2,4]{1,0:T(2,128)S(1)}, f32[2,4]{1,0:T(2,128)S(1)}, u32[]{:S(2)}, u32[]{:S(2)}) %collective-permute-start.27) | collective-permute-done | bytes 64 | tf_op jit(solution)/shard_map/ppermute | solution.py:44
  180.0 1.0 subtract_bitcast_fusion
  (177 shorter events, 23.7 us)
Async XLA Ops:
  0.6 27.8 %copy-start = (f32[64,64]{1,0:T(8,128)S(1)}, f32[64,64]{1,0:T(8,128)}, u32[]{:S(2)}) copy-start(f32[64,64]{1,0:T(8,128)} %param.9) | copy-start | bytes 49156
  2.2 12.7 %collective-permute-start = (bf16[1,64,256]{2,1,0:T(8,128)(2,1)S(1)}, bf16[1,64,256]{2,1,0:T(8,128)(2,1)S(1)}, u32[]{:S(2)}, u32[]{:S(2)}) collective-permute-start(bf16[1,64,256]{2,1,0:T(8,128)(2,1)S(1)} %get-tuple-element.48), channel_id=1, source_target_pairs={{0,16},{2,18},{4,20},{6,22},{8,24},{10,26},{12,28},{14,30},{16,0},... | collective-permute-start | bytes 98312 | tf_op jit(solution)/shard_map/ppermute | solution.py:44
  11.3 3.5 %copy-start.23 = (pred[12,3]{0,1:T(4,128)(4,1)}, pred[12,3]{0,1:T(4,128)(4,1)S(1)}, u32[]{:S(2)}) copy-start(pred[12,3]{0,1:T(4,128)(4,1)S(1)} %fusion.53) | copy-start | bytes 112
  14.9 4.3 %collective-permute-start.1 = (bf16[2,64,256]{2,1,0:T(8,128)(2,1)S(1)}, bf16[2,64,256]{2,1,0:T(8,128)(2,1)S(1)}, u32[]{:S(2)}, u32[]{:S(2)}) collective-permute-start(bf16[2,64,256]{2,1,0:T(8,128)(2,1)S(1)} %maximum_bitcast_fusion), channel_id=1, source_target_pairs={{0,8},{2,10},{4,12},{6,14},{8,0},{10,2},{12,4},{14,6},{16,24},{18,... | collective-permute-start | bytes 196616 | tf_op jit(solution)/shard_map/ppermute | solution.py:44
  19.3 5.9 %collective-permute-start.2 = (bf16[2,2,64,256]{3,2,0,1:T(8,128)(2,1)S(1)}, bf16[2,2,64,256]{3,2,0,1:T(8,128)(2,1)S(1)}, u32[]{:S(2)}, u32[]{:S(2)}) collective-permute-start(bf16[2,2,64,256]{3,2,0,1:T(8,128)(2,1)S(1)} %pad_maximum_fusion.4), channel_id=1, source_target_pairs={{0,4},{2,6},{4,0},{6,2},{8,12},{10,14},{12,8},{14,10},{16,20},{18,... | collective-permute-start | bytes 393224 | tf_op jit(solution)/shard_map/ppermute | solution.py:44
  20.8 5.9 %copy-start.6 = (f32[1,64,256]{2,1,0:T(8,128)S(1)}, f32[1,64,256]{2,1,0:T(8,128)}, u32[]{:S(2)}) copy-start(f32[1,64,256]{2,1,0:T(8,128)} %param.8) | copy-start | bytes 196612
  20.8 6.7 %copy-start.3 = (f32[1,384,256]{2,1,0:T(8,128)S(1)}, f32[1,384,256]{2,1,0:T(8,128)}, u32[]{:S(2)}) copy-start(f32[1,384,256]{2,1,0:T(8,128)} %param.7) | copy-start | bytes 1179652
  25.2 7.8 %collective-permute-start.3 = (bf16[2,2,2,64,256]{4,3,0,1,2:T(8,128)(2,1)S(1)}, bf16[2,2,2,64,256]{4,3,0,1,2:T(8,128)(2,1)}, u32[]{:S(2)}, u32[]{:S(2)}) collective-permute-start(bf16[2,2,2,64,256]{4,3,0,1,2:T(8,128)(2,1)S(1)} %pad_maximum_fusion.2), channel_id=1, source_target_pairs={{0,2},{2,0},{4,6},{6,4},{8,10},{10,8},{12,14},{14,12},{16,18},{18,... | collective-permute-start | bytes 786440 | tf_op jit(solution)/shard_map/ppermute | solution.py:44
  26.7 10.3 %copy-start.21 = (pred[12,4]{0,1:T(4,128)(4,1)}, pred[12,4]{0,1:T(4,128)(4,1)S(1)}, u32[]{:S(2)}) copy-start(pred[12,4]{0,1:T(4,128)(4,1)S(1)} %fusion.54) | copy-start | bytes 148
  34.9 2.2 %copy-start.1 = (f32[12,256,256]{2,1,0:T(8,128)S(1)}, f32[12,256,256]{2,1,0:T(8,128)}, u32[]{:S(2)}) copy-start(f32[12,256,256]{2,1,0:T(8,128)} %fusion.16) | copy-start | bytes 9437188
  34.9 2.2 %copy-start.9 = (f32[12,256]{0,1:T(8,128)S(1)}, f32[12,256]{0,1:T(8,128)}, u32[]{:S(2)}) copy-start(f32[12,256]{0,1:T(8,128)} %copy.95) | copy-start | bytes 36868
  41.0 5.9 %copy-start.18 = (f32[64,64]{1,0:T(8,128)S(1)}, f32[64,64]{1,0:T(8,128)}, u32[]{:S(2)}) copy-start(f32[64,64]{1,0:T(8,128)} %param.10) | copy-start | bytes 49156
  42.9 4.1 %copy-start.15 = (f32[64,4,64]{2,1,0:T(4,128)S(1)}, f32[64,4,64]{2,1,0:T(4,128)}, u32[]{:S(2)}) copy-start(f32[64,4,64]{2,1,0:T(4,128)} %reshape_squeeze.7) | copy-start | bytes 196612
  45.4 14.6 %collective-permute-start.5 = (f32[2,2,2,64,256]{4,3,0,1,2:T(8,128)}, f32[2,2,2,64,256]{4,3,0,1,2:T(8,128)}, u32[]{:S(2)}, u32[]{:S(2)}) collective-permute-start(f32[2,2,2,64,256]{4,3,0,1,2:T(8,128)} %select_bitcast_fusion.1), channel_id=1, source_target_pairs={{0,2},{2,0},{4,6},{6,4},{8,10},{10,8},{12,14},{14,12},{16,18},{18,... | collective-permute-start | bytes 1572872 | tf_op jit(solution)/shard_map/ppermute | solution.py:44
  54.9 7.0 %copy-start.24 = (pred[12,3]{0,1:T(4,128)(4,1)S(1)}, pred[12,3]{0,1:T(4,128)(4,1)}, u32[]{:S(2)}) copy-start(pred[12,3]{0,1:T(4,128)(4,1)} %copy-done.23) | copy-start | bytes 112
  61.3 6.5 %collective-permute-start.6 = (f32[2,2,64,256]{3,2,0,1:T(8,128)S(1)}, f32[2,2,64,256]{3,2,0,1:T(8,128)S(1)}, u32[]{:S(2)}, u32[]{:S(2)}) collective-permute-start(f32[2,2,64,256]{3,2,0,1:T(8,128)S(1)} %select_bitcast_fusion.5), channel_id=1, source_target_pairs={{0,4},{2,6},{4,0},{6,2},{8,12},{10,14},{12,8},{14,10},{16,20},{18,... | collective-permute-start | bytes 786440 | tf_op jit(solution)/shard_map/ppermute | solution.py:44
  65.2 8.2 %copy-start.7 = (f32[384,256]{1,0:T(8,128)S(1)}, f32[384,256]{1,0:T(8,128)}, u32[]{:S(2)}) copy-start(f32[384,256]{1,0:T(8,128)} %copy.90) | copy-start | bytes 1179652
  65.2 13.1 %copy-start.17 = (f32[64,256]{1,0:T(8,128)S(1)}, f32[64,256]{1,0:T(8,128)}, u32[]{:S(2)}) copy-start(f32[64,256]{1,0:T(8,128)} %reshape.164) | copy-start | bytes 196612
  65.2 13.3 %copy-start.28 = (f32[4]{0:T(128)S(1)}, f32[4]{0:T(128)}, u32[]{:S(2)}) copy-start(f32[4]{0:T(128)} %reduce_sum.113) | copy-start | bytes 52
  65.2 13.3 %copy-start.29 = (f32[4]{0:T(128)S(1)}, f32[4]{0:T(128)}, u32[]{:S(2)}) copy-start(f32[4]{0:T(128)} %reduce_sum.119) | copy-start | bytes 52
  67.9 5.0 %collective-permute-start.7 = (f32[2,64,256]{2,1,0:T(8,128)S(1)}, f32[2,64,256]{2,1,0:T(8,128)S(1)}, u32[]{:S(2)}, u32[]{:S(2)}) collective-permute-start(f32[2,64,256]{2,1,0:T(8,128)S(1)} %select_bitcast_fusion.11), channel_id=1, source_target_pairs={{0,8},{2,10},{4,12},{6,14},{8,0},{10,2},{12,4},{14,6},{16,24},{18,... | collective-permute-start | bytes 393224 | tf_op jit(solution)/shard_map/ppermute | solution.py:44
  68.8 4.6 %collective-permute-start.4 = (bf16[384,256]{1,0:T(8,128)(2,1)S(1)}, bf16[384,256]{1,0:T(8,128)(2,1)S(1)}, u32[]{:S(2)}, u32[]{:S(2)}) collective-permute-start(bf16[384,256]{1,0:T(8,128)(2,1)S(1)} %fusion.32), channel_id=1, source_target_pairs={{0,1},{1,0},{2,3},{3,2},{4,5},{5,4},{6,7},{7,6},{8,9},{9,8},{10,11... | collective-permute-start | bytes 589832 | tf_op jit(solution)/shard_map/ppermute | solution.py:44
  73.0 5.2 %collective-permute-start.8 = (f32[64,256]{1,0:T(8,128)S(1)}, f32[64,256]{1,0:T(8,128)S(1)}, u32[]{:S(2)}, u32[]{:S(2)}) collective-permute-start(f32[64,256]{1,0:T(8,128)S(1)} %select_bitcast_fusion.17), channel_id=1, source_target_pairs={{0,16},{2,18},{4,20},{6,22},{8,24},{10,26},{12,28},{14,30},{16,0},... | collective-permute-start | bytes 196616 | tf_op jit(solution)/shard_map/ppermute | solution.py:44
  73.5 35.2 %copy-start.4 = (f32[384,256]{1,0:T(8,128)}, f32[384,256]{1,0:T(8,128)S(1)}, u32[]{:S(2)}) copy-start(f32[384,256]{1,0:T(8,128)S(1)} %get-tuple-element.21) | copy-start | bytes 1179652
  78.3 30.5 %copy-start.13 = (f32[64,256]{1,0:T(8,128)}, f32[64,256]{1,0:T(8,128)S(1)}, u32[]{:S(2)}) copy-start(f32[64,256]{1,0:T(8,128)S(1)} %get-tuple-element.19) | copy-start | bytes 196612
  78.5 1.2 collective-permute-start.9
  79.7 3.6 %collective-permute-start.10 = (f32[2,4]{1,0:T(2,128)S(1)}, f32[2,4]{1,0:T(2,128)S(1)}, u32[]{:S(2)}, u32[]{:S(2)}) collective-permute-start(f32[2,4]{1,0:T(2,128)S(1)} %fusion.71), channel_id=1, source_target_pairs={{0,2},{2,0},{4,6},{6,4},{8,10},{10,8},{12,14},{14,12},{16,18},{18,... | collective-permute-start | bytes 104 | tf_op jit(solution)/shard_map/ppermute | solution.py:44
  83.4 3.6 %collective-permute-start.11 = (f32[2,4]{1,0:T(2,128)S(1)}, f32[2,4]{1,0:T(2,128)S(1)}, u32[]{:S(2)}, u32[]{:S(2)}) collective-permute-start(f32[2,4]{1,0:T(2,128)S(1)} %fusion.93), channel_id=1, source_target_pairs={{0,4},{2,6},{4,0},{6,2},{8,12},{10,14},{12,8},{14,10},{16,20},{18,... | collective-permute-start | bytes 104 | tf_op jit(solution)/shard_map/ppermute | solution.py:44
  87.0 3.6 %collective-permute-start.12 = (f32[2,4]{1,0:T(2,128)S(1)}, f32[2,4]{1,0:T(2,128)S(1)}, u32[]{:S(2)}, u32[]{:S(2)}) collective-permute-start(f32[2,4]{1,0:T(2,128)S(1)} %add.169), channel_id=1, source_target_pairs={{0,8},{2,10},{4,12},{6,14},{8,0},{10,2},{12,4},{14,6},{16,24},{18,... | collective-permute-start | bytes 104 | tf_op jit(solution)/shard_map/ppermute | solution.py:44
  90.6 4.5 %collective-permute-start.13 = (f32[2,4]{1,0:T(2,128)S(1)}, f32[2,4]{1,0:T(2,128)S(1)}, u32[]{:S(2)}, u32[]{:S(2)}) collective-permute-start(f32[2,4]{1,0:T(2,128)S(1)} %add.170), channel_id=1, source_target_pairs={{0,16},{2,18},{4,20},{6,22},{8,24},{10,26},{12,28},{14,30},{16,0},... | collective-permute-start | bytes 104 | tf_op jit(solution)/shard_map/ppermute | solution.py:44
  95.1 0.5 copy-start.26
  95.6 0.6 copy-start.19
  95.6 17.7 %copy-start.11 = (f32[64,256]{1,0:T(8,128)}, f32[64,256]{1,0:T(8,128)S(1)}, u32[]{:S(2)}) copy-start(f32[64,256]{1,0:T(8,128)S(1)} %get-tuple-element.15) | copy-start | bytes 196612
  95.6 4.9 %collective-permute-start.14 = (bf16[1,64,256]{2,1,0:T(8,128)(2,1)S(1)}, bf16[1,64,256]{2,1,0:T(8,128)(2,1)S(1)}, u32[]{:S(2)}, u32[]{:S(2)}) collective-permute-start(bf16[1,64,256]{2,1,0:T(8,128)(2,1)S(1)} %get-tuple-element.14), channel_id=1, source_target_pairs={{0,16},{2,18},{4,20},{6,22},{8,24},{10,26},{12,28},{14,30},{16,0},... | collective-permute-start | bytes 98312 | tf_op jit(solution)/shard_map/ppermute | solution.py:44
  100.5 4.3 %collective-permute-start.15 = (bf16[2,64,256]{2,1,0:T(8,128)(2,1)S(1)}, bf16[2,64,256]{2,1,0:T(8,128)(2,1)S(1)}, u32[]{:S(2)}, u32[]{:S(2)}) collective-permute-start(bf16[2,64,256]{2,1,0:T(8,128)(2,1)S(1)} %maximum_bitcast_fusion.1), channel_id=1, source_target_pairs={{0,8},{2,10},{4,12},{6,14},{8,0},{10,2},{12,4},{14,6},{16,24},{18,... | collective-permute-start | bytes 196616 | tf_op jit(solution)/shard_map/ppermute | solution.py:44
  104.9 5.1 %collective-permute-start.16 = (bf16[2,2,64,256]{3,2,0,1:T(8,128)(2,1)S(1)}, bf16[2,2,64,256]{3,2,0,1:T(8,128)(2,1)S(1)}, u32[]{:S(2)}, u32[]{:S(2)}) collective-permute-start(bf16[2,2,64,256]{3,2,0,1:T(8,128)(2,1)S(1)} %pad_maximum_fusion.5), channel_id=1, source_target_pairs={{0,4},{2,6},{4,0},{6,2},{8,12},{10,14},{12,8},{14,10},{16,20},{18,... | collective-permute-start | bytes 393224 | tf_op jit(solution)/shard_map/ppermute | solution.py:44
  110.1 7.1 %collective-permute-start.17 = (bf16[2,2,2,64,256]{4,3,0,1,2:T(8,128)(2,1)S(1)}, bf16[2,2,2,64,256]{4,3,0,1,2:T(8,128)(2,1)}, u32[]{:S(2)}, u32[]{:S(2)}) collective-permute-start(bf16[2,2,2,64,256]{4,3,0,1,2:T(8,128)(2,1)S(1)} %pad_maximum_fusion.3), channel_id=1, source_target_pairs={{0,2},{2,0},{4,6},{6,4},{8,10},{10,8},{12,14},{14,12},{16,18},{18,... | collective-permute-start | bytes 786440 | tf_op jit(solution)/shard_map/ppermute | solution.py:44
  119.1 3.0 %copy-start.2 = (f32[12,256,256]{2,1,0:T(8,128)S(1)}, f32[12,256,256]{2,1,0:T(8,128)}, u32[]{:S(2)}) copy-start(f32[12,256,256]{2,1,0:T(8,128)} %fusion.13) | copy-start | bytes 9437188
  119.1 3.0 %copy-start.10 = (f32[12,256]{0,1:T(8,128)S(1)}, f32[12,256]{0,1:T(8,128)}, u32[]{:S(2)}) copy-start(f32[12,256]{0,1:T(8,128)} %copy.95) | copy-start | bytes 36868
  119.1 3.0 %copy-start.22 = (pred[12,4]{0,1:T(4,128)(4,1)S(1)}, pred[12,4]{0,1:T(4,128)(4,1)}, u32[]{:S(2)}) copy-start(pred[12,4]{0,1:T(4,128)(4,1)} %copy-done.21) | copy-start | bytes 148
  127.8 3.1 %copy-start.16 = (f32[64,4,64]{2,1,0:T(4,128)S(1)}, f32[64,4,64]{2,1,0:T(4,128)}, u32[]{:S(2)}) copy-start(f32[64,4,64]{2,1,0:T(4,128)} %reshape.169) | copy-start | bytes 196612
  130.4 12.0 %collective-permute-start.19 = (f32[2,2,2,64,256]{4,3,0,1,2:T(8,128)}, f32[2,2,2,64,256]{4,3,0,1,2:T(8,128)}, u32[]{:S(2)}, u32[]{:S(2)}) collective-permute-start(f32[2,2,2,64,256]{4,3,0,1,2:T(8,128)} %select_bitcast_fusion), channel_id=1, source_target_pairs={{0,2},{2,0},{4,6},{6,4},{8,10},{10,8},{12,14},{14,12},{16,18},{18,... | collective-permute-start | bytes 1572872 | tf_op jit(solution)/shard_map/ppermute | solution.py:44
  135.5 9.6 %copy-start.25 = (pred[12,3]{0,1:T(4,128)(4,1)S(1)}, pred[12,3]{0,1:T(4,128)(4,1)}, u32[]{:S(2)}) copy-start(pred[12,3]{0,1:T(4,128)(4,1)} %copy-done.23) | copy-start | bytes 112
  143.6 6.4 %collective-permute-start.20 = (f32[2,2,64,256]{3,2,0,1:T(8,128)S(1)}, f32[2,2,64,256]{3,2,0,1:T(8,128)S(1)}, u32[]{:S(2)}, u32[]{:S(2)}) collective-permute-start(f32[2,2,64,256]{3,2,0,1:T(8,128)S(1)} %select_bitcast_fusion.2), channel_id=1, source_target_pairs={{0,4},{2,6},{4,0},{6,2},{8,12},{10,14},{12,8},{14,10},{16,20},{18,... | collective-permute-start | bytes 786440 | tf_op jit(solution)/shard_map/ppermute | solution.py:44
  148.3 8.1 %copy-start.8 = (f32[384,256]{1,0:T(8,128)S(1)}, f32[384,256]{1,0:T(8,128)}, u32[]{:S(2)}) copy-start(f32[384,256]{1,0:T(8,128)} %copy.107) | copy-start | bytes 1179652
  148.4 12.8 %copy-start.12 = (f32[64,256]{1,0:T(8,128)S(1)}, f32[64,256]{1,0:T(8,128)}, u32[]{:S(2)}) copy-start(f32[64,256]{1,0:T(8,128)} %copy-done.11) | copy-start | bytes 196612
  148.4 30.7 %copy-start.27 = (f32[2,4]{1,0:T(2,128)S(1)}, f32[2,4]{1,0:T(2,128)}, u32[]{:S(2)}) copy-start(f32[2,4]{1,0:T(2,128)} %copy-done.26) | copy-start | bytes 100
  148.5 30.8 %copy-start.14 = (f32[64,256]{1,0:T(8,128)S(1)}, f32[64,256]{1,0:T(8,128)}, u32[]{:S(2)}) copy-start(f32[64,256]{1,0:T(8,128)} %copy-done.13) | copy-start | bytes 196612
  148.6 30.8 %copy-start.20 = (f32[256]{0:T(256)S(1)}, f32[256]{0:T(256)}, u32[]{:S(2)}) copy-start(f32[256]{0:T(256)} %copy-done.19) | copy-start | bytes 3076
  148.6 31.5 %copy-start.5 = (f32[384,256]{1,0:T(8,128)S(1)}, f32[384,256]{1,0:T(8,128)}, u32[]{:S(2)}) copy-start(f32[384,256]{1,0:T(8,128)} %copy-done.4) | copy-start | bytes 1179652
  150.2 5.7 %collective-permute-start.21 = (f32[2,64,256]{2,1,0:T(8,128)S(1)}, f32[2,64,256]{2,1,0:T(8,128)S(1)}, u32[]{:S(2)}, u32[]{:S(2)}) collective-permute-start(f32[2,64,256]{2,1,0:T(8,128)S(1)} %select_bitcast_fusion.8), channel_id=1, source_target_pairs={{0,8},{2,10},{4,12},{6,14},{8,0},{10,2},{12,4},{14,6},{16,24},{18,... | collective-permute-start | bytes 393224 | tf_op jit(solution)/shard_map/ppermute | solution.py:44
  150.3 6.2 %collective-permute-start.18 = (bf16[384,256]{1,0:T(8,128)(2,1)S(1)}, bf16[384,256]{1,0:T(8,128)(2,1)S(1)}, u32[]{:S(2)}, u32[]{:S(2)}) collective-permute-start(bf16[384,256]{1,0:T(8,128)(2,1)S(1)} %fusion.33), channel_id=1, source_target_pairs={{0,1},{1,0},{2,3},{3,2},{4,5},{5,4},{6,7},{7,6},{8,9},{9,8},{10,11... | collective-permute-start | bytes 589832 | tf_op jit(solution)/shard_map/ppermute | solution.py:44
  155.9 5.2 %collective-permute-start.22 = (f32[64,256]{1,0:T(8,128)S(1)}, f32[64,256]{1,0:T(8,128)S(1)}, u32[]{:S(2)}, u32[]{:S(2)}) collective-permute-start(f32[64,256]{1,0:T(8,128)S(1)} %select_bitcast_fusion.14), channel_id=1, source_target_pairs={{0,16},{2,18},{4,20},{6,22},{8,24},{10,26},{12,28},{14,30},{16,0},... | collective-permute-start | bytes 196616 | tf_op jit(solution)/shard_map/ppermute | solution.py:44
  162.5 1.2 collective-permute-start.23
  163.7 3.6 %collective-permute-start.24 = (f32[2,4]{1,0:T(2,128)S(1)}, f32[2,4]{1,0:T(2,128)S(1)}, u32[]{:S(2)}, u32[]{:S(2)}) collective-permute-start(f32[2,4]{1,0:T(2,128)S(1)} %fusion.70), channel_id=1, source_target_pairs={{0,2},{2,0},{4,6},{6,4},{8,10},{10,8},{12,14},{14,12},{16,18},{18,... | collective-permute-start | bytes 104 | tf_op jit(solution)/shard_map/ppermute | solution.py:44
  167.3 3.6 %collective-permute-start.25 = (f32[2,4]{1,0:T(2,128)S(1)}, f32[2,4]{1,0:T(2,128)S(1)}, u32[]{:S(2)}, u32[]{:S(2)}) collective-permute-start(f32[2,4]{1,0:T(2,128)S(1)} %fusion.92), channel_id=1, source_target_pairs={{0,4},{2,6},{4,0},{6,2},{8,12},{10,14},{12,8},{14,10},{16,20},{18,... | collective-permute-start | bytes 104 | tf_op jit(solution)/shard_map/ppermute | solution.py:44
  171.0 3.6 %collective-permute-start.26 = (f32[2,4]{1,0:T(2,128)S(1)}, f32[2,4]{1,0:T(2,128)S(1)}, u32[]{:S(2)}, u32[]{:S(2)}) collective-permute-start(f32[2,4]{1,0:T(2,128)S(1)} %add.187), channel_id=1, source_target_pairs={{0,8},{2,10},{4,12},{6,14},{8,0},{10,2},{12,4},{14,6},{16,24},{18,... | collective-permute-start | bytes 104 | tf_op jit(solution)/shard_map/ppermute | solution.py:44
  174.6 4.5 %collective-permute-start.27 = (f32[2,4]{1,0:T(2,128)S(1)}, f32[2,4]{1,0:T(2,128)S(1)}, u32[]{:S(2)}, u32[]{:S(2)}) collective-permute-start(f32[2,4]{1,0:T(2,128)S(1)} %add.188), channel_id=1, source_target_pairs={{0,16},{2,18},{4,20},{6,22},{8,24},{10,26},{12,28},{14,30},{16,0},... | collective-permute-start | bytes 104 | tf_op jit(solution)/shard_map/ppermute | solution.py:44

commit v2 on v1

--- a/solution.py
+++ b/solution.py
@@ -93,56 +93,27 @@
     user_own = draws_user[0]
     item_own = draws_item[0]
     in_use = jnp.arange(TMAX, dtype=jnp.int32) < tile_count[0, 0]
-    counts_bf = jnp.where(in_use[:, None, None], count_tiles[0, 0], 0).astype(jnp.bfloat16)
-    row_pick = (
-        (tile_blocks[0, 0, :, 0][:, None] == jnp.arange(RB, dtype=jnp.int32)) & in_use[:, None]
-    ).astype(jnp.float32)
-    col_pick = (
-        (tile_blocks[0, 0, :, 1][:, None] == jnp.arange(CB, dtype=jnp.int32)) & in_use[:, None]
-    ).astype(jnp.float32)
-    row_pick_bf = row_pick.astype(jnp.bfloat16)
-    col_pick_bf = col_pick.astype(jnp.bfloat16)
-    row_sums = jnp.sum(counts_bf, axis=2, dtype=jnp.float32)
-    col_sums = jnp.sum(counts_bf, axis=1, dtype=jnp.float32)
+    row_pick = (tile_blocks[0, 0, :, 0][:, None] == jnp.arange(RB, dtype=jnp.int32)) & in_use[:, None]
+    col_pick = (tile_blocks[0, 0, :, 1][:, None] == jnp.arange(CB, dtype=jnp.int32)) & in_use[:, None]
+    place = (row_pick[:, :, None] & col_pick[:, None, :]).astype(jnp.bfloat16)
+    block_counts = jnp.einsum(
+        "trc,tij->ricj",
+        place,
+        count_tiles[0, 0].astype(jnp.bfloat16),
+        preferred_element_type=jnp.float32,
+    ).reshape(RB * TILE, CB * TILE)
+    user_deg = jnp.sum(block_counts, axis=1)
+    item_deg = jnp.sum(block_counts, axis=0)
+    counts_bf = block_counts.astype(jnp.bfloat16)
 
     def cross_parts(user_range, item_range):
-        user_sel = jnp.einsum(
-            "tr,ris->tis",
-            row_pick_bf,
-            user_range.reshape(RB, TILE, width),
-            preferred_element_type=jnp.float32,
+        to_users = jnp.dot(counts_bf, item_range, preferred_element_type=jnp.float32)
+        to_users = to_users + user_deg[:, None] * user_range.astype(jnp.float32)
+        to_items = lax.dot_general(
+            counts_bf, user_range, (((0,), (0,)), ((), ())), preferred_element_type=jnp.float32
         )
-        item_sel = jnp.einsum(
-            "tc,cjs->tjs",
-            col_pick_bf,
-            item_range.reshape(CB, TILE, width),
-            preferred_element_type=jnp.float32,
-        )
-        to_users = (
-            jnp.einsum(
-                "tij,tjs->tis",
-                counts_bf,
-                item_sel.astype(jnp.bfloat16),
-                preferred_element_type=jnp.float32,
-            )
-            + row_sums[:, :, None] * user_sel
-        )
-        to_items = (
-            jnp.einsum(
-                "tij,tis->tjs",
-                counts_bf,
-                user_sel.astype(jnp.bfloat16),
-                preferred_element_type=jnp.float32,
-            )
-            + col_sums[:, :, None] * item_sel
-        )
-        part_user = jnp.einsum("tr,tis->ris", row_pick, to_users, precision=top_prec).reshape(
-            RB * TILE, width
-        )
-        part_item = jnp.einsum("tc,tjs->cjs", col_pick, to_items, precision=top_prec).reshape(
-            CB * TILE, width
-        )
-        return (part_user, part_item)
+        to_items = to_items + item_deg[:, None] * item_range.astype(jnp.float32)
+        return (to_users, to_items)
 
     def user_range_of(user_vec):
         return lax.all_gather(user_vec.astype(jnp.bfloat16), "item", axis=0, tiled=True)

time: 182 us -> 161 us (0.88)
  matrix products: 46.4 us -> 9.17 us
  waiting for transfers between devices: 62.8 us -> 90.2 us
  local copies, waits for them, and re-layouts: 23.7 us -> 15.7 us
  starting transfers between devices: 24 us -> 19.4 us
    dot_general x12 -> x5, matrix products: 43.5 us -> 6.74 us  [the longest x1 4.2 us: per_device(): jnp.einsum('trc,tij->ricj', place, count_tiles[0, 0].astype(jnp.bfloat16)...]
    ppermute x28, waiting for transfers between devices: 62.8 us -> 90.2 us  [swap_with(): return lax.ppermute(value, axis, pairs)]
    ppermute x28, starting transfers between devices: 24 us -> 19.4 us  [swap_with(): return lax.ppermute(value, axis, pairs)]
    another operation x4 -> x0, local copies, waits for them, and re-layouts: 4.17 us -> none  [the longest x2 3.65 us: halve_sum(): buf = part.reshape([2] * bits + [rows, width])]
    unnamed x61 -> x35, local copies, waits for them, and re-layouts: 0.7 us -> 4.83 us
    convert_element_type x0 -> x1, other arithmetic: none -> 3.36 us  [per_device(): count_tiles[0, 0].astype(jnp.bfloat16)]
    reshape x4 -> x2, local copies, waits for them, and re-layouts: 6.16 us -> 3.33 us  [prior_term(): return mixed.reshape(row_total, DRAWS * DIM)]
    select_n x8, other arithmetic: 2.1 us -> 4 us  [halve_sum(): send = jnp.where(upper, low, high).astype(send_type)]
  transfers between devices with their start and end apart: 28 -> 28, of which waited for: 23 -> 23; matrix products, arithmetic and copies ran while one was open for 30% -> 17% of each run, Pallas kernels for 0% -> 0%
where the time goes in v2:
time: 161 us; the launch traced here: 160 us
  waiting for transfers between devices  90.2 us (56%)
  other arithmetic  19.4 us (12%)
  starting transfers between devices  19.4 us (12%)
  local copies, waits for them, and re-layouts  15.7 us (10%)
  matrix products  9.17 us (6%)
  blocking collectives  4.36 us (3%)
  between operations  1.9 us (1%)
    ppermute x28, waiting for transfers between devices, swap_with(): return lax.ppermute(value, axis, pairs)  90.2 us
    ppermute x28, starting transfers between devices, swap_with(): return lax.ppermute(value, axis, pairs)  19.4 us
    unnamed x35, local copies, waits for them, and re-layouts  4.83 us
    reduce_sum x14, other arithmetic, per_draw(): return jnp.sum(product, axis=(0, 2))  4.56 us
    all_gather x2, blocking collectives, user_range_of(): lax.all_gather(user_vec.astype(jnp.bfloat16), 'item', axis=0, tiled=True)  4.36 us
    dot_general x1, matrix products, per_device(): jnp.einsum('trc,tij->ricj', place, count_tiles[0, 0].astype(jnp.bfloat16)...  4.2 us
    select_n x8, other arithmetic, halve_sum(): send = jnp.where(upper, low, high).astype(send_type)  4 us
    convert_element_type x1, other arithmetic, per_device(): count_tiles[0, 0].astype(jnp.bfloat16)  3.36 us
  transfers between devices with their start and end apart: 28, of which 23 were waited for; matrix products, arithmetic and copies ran while one was open for 17% of the time, Pallas kernels for 0%

profile of v2, /device:TPU:0, one launch (start us, length us, event | category | flops | bytes accessed | tf_op | source)
XLA Modules:
  0.0 160.2 jit_solution(7065899137774981208)
XLA Ops:
  0.6 1.5 multiply_reduce_fusion.5
  2.1 4.0 %collective-permute-start = (bf16[1,64,256]{2,1,0:T(8,128)(2,1)S(1)}, bf16[1,64,256]{2,1,0:T(8,128)(2,1)S(1)}, u32[]{:S(2)}, u32[]{:S(2)}) collective-permute-start(bf16[1,64,256]{2,1,0:T(8,128)(2,1)S(1)} %get-tuple-element.57), channel_id=1, source_target_pairs={{0,16},{2,18},{4,20},{6,22},{8,24},{10,26},{12,28},{14,30},{16,0},... | collective-permute-start | bytes 98312 | tf_op jit(solution)/shard_map/ppermute | solution.py:44
  6.2 3.4 %convert_bitcast_fusion = bf16[12,256,256]{2,1,0:T(8,128)(2,1)} fusion(s32[1,1,12,256,256]{4,3,2,1,0:T(8,128)} %param.11), kind=kLoop, calls=%fused_computation.6 | loop fusion | flops 786432 | bytes 4718592 | tf_op jit(solution)/shard_map/convert_element_type | solution.py:102
  10.3 1.6 %collective-permute-start.1 = (bf16[2,64,256]{2,1,0:T(8,128)(2,1)S(1)}, bf16[2,64,256]{2,1,0:T(8,128)(2,1)S(1)}, u32[]{:S(2)}, u32[]{:S(2)}) collective-permute-start(bf16[2,64,256]{2,1,0:T(8,128)(2,1)S(1)} %maximum_bitcast_fusion), channel_id=1, source_target_pairs={{0,8},{2,10},{4,12},{6,14},{8,0},{10,2},{12,4},{14,6},{16,24},{18,... | collective-permute-start | bytes 196616 | tf_op jit(solution)/shard_map/ppermute | solution.py:44
  11.9 4.2 %bitcast_convert_fusion = (bf16[3,256,4,256]{3,2,1,0:T(4,128)(2,1)}, f32[3,4,256,256]{3,1,2,0:T(4,128)S(1)}) fusion(bf16[12,256,256]{2,1,0:T(8,128)(2,1)} %convert_bitcast_fusion, pred[12,4]{0,1:T(4,128)(4,1)S(1)} %fusion.32, pred[12,3]{0,1:T(4,128)(4,1)S(1)} %fusion.31), kind=kOutput, calls=%fused_computation.2 | convolution fusion | flops 19660944 | bytes 6291540 | tf_op jit(solution)/shard_map/trc,tij->ricj/dot_general | solution.py:99
  16.2 0.7 pad_maximum_fusion.4
  16.8 1.5 collective-permute-start.2
  18.3 1.8 %bitcast_reduce_fusion = (f32[4,256]{1,0:T(4,128)S(1)}, f32[3,256]{1,0:T(4,128)S(1)}) fusion(f32[3,4,256,256]{3,1,2,0:T(4,128)S(1)} %get-tuple-element.63), kind=kLoop, calls=%fused_computation | loop fusion | flops 1571072 | bytes 3152896 | tf_op jit(solution)/shard_map/reduce_sum | solution.py:106
  20.2 0.8 reshape_squeeze.7
  21.0 1.2 copy.47
  22.1 1.8 %copy.76 = bf16[96,8,4,256]{3,1,2,0:T(8,128)(2,1)S(1)} copy(bf16[96,8,4,256]{3,2,1,0:T(4,128)(2,1)} %bitcast.233) | data formatting | bytes 3145728
  24.0 1.6 collective-permute-start.3
  25.6 2.1 %all_gather.6 = bf16[768,256]{0,1:T(8,128)(2,1)S(1)} all-gather(bf16[384,256]{0,1:T(8,128)(2,1)S(1)} %bitcast_convert_fusion.1), channel_id=1, replica_groups=mesh['user'=16,'item'=2] {'item'}, dimensions={0}, use_global_device_ids=true | all-gather | bytes 589824 | tf_op jit(solution)/shard_map/all_gather | solution.py:119
  27.7 3.6 %collective-permute-done.3 = bf16[2,2,2,64,256]{4,3,0,1,2:T(8,128)(2,1)S(1)} collective-permute-done((bf16[2,2,2,64,256]{4,3,0,1,2:T(8,128)(2,1)S(1)}, bf16[2,2,2,64,256]{4,3,0,1,2:T(8,128)(2,1)S(1)}, u32[]{:S(2)}, u32[]{:S(2)}) %collective-permute-start.3) | collective-permute-done | bytes 262176 | tf_op jit(solution)/shard_map/ppermute | solution.py:44
  31.4 0.7 convolution_add_fusion.1
  32.1 0.9 fusion.42
  33.0 1.9 %select_bitcast_fusion.1 = f32[2,2,2,64,256]{4,3,0,1,2:T(8,128)} fusion(f32[2,2,2,1,64,256]{5,4,3,2,1,0:T(8,128)} %get-tuple-element.37, f32[2,2,2,1,64,256]{5,4,3,2,1,0:T(8,128)S(1)} %get-tuple-element.36, pred[]{:T(512)S(6)} %eq.75), kind=kLoop, calls=%fused_computation.16 | loop fusion | flops 131072 | bytes 1572865 | tf_op jit(solution)/shard_map/jit(_where)/select_n | solution.py:68
  35.0 1.5 collective-permute-start.5
  36.7 0.7 copy.54
  37.4 1.7 %reshape.237 = f32[64,256]{1,0:T(8,128)} reshape(f32[64,4,64]{2,1,0:T(4,128)} %copy.54) | data formatting | bytes 131072 | tf_op jit(solution)/shard_map/reshape | solution.py:23
  39.1 1.1 multiply_reduce_fusion.2
  40.3 0.8 reduce_sum.118
  41.0 0.6 reduce_sum.113
  42.3 4.9 %collective-permute-done.5 = f32[2,2,2,64,256]{4,3,0,1,2:T(8,128)} collective-permute-done((f32[2,2,2,64,256]{4,3,0,1,2:T(8,128)}, f32[2,2,2,64,256]{4,3,0,1,2:T(8,128)}, u32[]{:S(2)}, u32[]{:S(2)}) %collective-permute-start.5) | collective-permute-done | bytes 524320 | tf_op jit(solution)/shard_map/ppermute | solution.py:44
  47.2 1.3 bitcast_add_fusion.1
  49.1 0.6 convolution_add_fusion.3
  49.7 5.2 %collective-permute-done.6 = f32[2,2,64,256]{3,2,0,1:T(8,128)S(1)} collective-permute-done((f32[2,2,64,256]{3,2,0,1:T(8,128)S(1)}, f32[2,2,64,256]{3,2,0,1:T(8,128)S(1)}, u32[]{:S(2)}, u32[]{:S(2)}) %collective-permute-start.6) | collective-permute-done | bytes 262176 | tf_op jit(solution)/shard_map/ppermute | solution.py:44
  55.7 5.1 %collective-permute-done.7 = f32[2,64,256]{2,1,0:T(8,128)S(1)} collective-permute-done((f32[2,64,256]{2,1,0:T(8,128)S(1)}, f32[2,64,256]{2,1,0:T(8,128)S(1)}, u32[]{:S(2)}, u32[]{:S(2)}) %collective-permute-start.7) | collective-permute-done | bytes 131104 | tf_op jit(solution)/shard_map/ppermute | solution.py:44
  61.3 5.3 %collective-permute-done.8 = f32[64,256]{1,0:T(8,128)S(1)} collective-permute-done((f32[64,256]{1,0:T(8,128)S(1)}, f32[64,256]{1,0:T(8,128)S(1)}, u32[]{:S(2)}, u32[]{:S(2)}) %collective-permute-start.8) | collective-permute-done | bytes 65568 | tf_op jit(solution)/shard_map/ppermute | solution.py:44
  67.0 1.1 collective-permute-done.9
  68.1 1.6 collective-permute-start.10
  69.7 2.1 %collective-permute-done.10 = f32[2,4]{1,0:T(2,128)S(1)} collective-permute-done((f32[2,4]{1,0:T(2,128)S(1)}, f32[2,4]{1,0:T(2,128)S(1)}, u32[]{:S(2)}, u32[]{:S(2)}) %collective-permute-start.10) | collective-permute-done | bytes 64 | tf_op jit(solution)/shard_map/ppermute | solution.py:44
  72.4 3.1 %collective-permute-done.11 = f32[2,4]{1,0:T(2,128)S(1)} collective-permute-done((f32[2,4]{1,0:T(2,128)S(1)}, f32[2,4]{1,0:T(2,128)S(1)}, u32[]{:S(2)}, u32[]{:S(2)}) %collective-permute-start.11) | collective-permute-done | bytes 64 | tf_op jit(solution)/shard_map/ppermute | solution.py:44
  75.4 3.6 %collective-permute-done.12 = f32[2,4]{1,0:T(2,128)S(1)} collective-permute-done((f32[2,4]{1,0:T(2,128)S(1)}, f32[2,4]{1,0:T(2,128)S(1)}, u32[]{:S(2)}, u32[]{:S(2)}) %collective-permute-start.12) | collective-permute-done | bytes 64 | tf_op jit(solution)/shard_map/ppermute | solution.py:44
  79.0 4.5 %collective-permute-done.13 = f32[2,4]{1,0:T(2,128)S(1)} collective-permute-done((f32[2,4]{1,0:T(2,128)S(1)}, f32[2,4]{1,0:T(2,128)S(1)}, u32[]{:S(2)}, u32[]{:S(2)}) %collective-permute-start.13) | collective-permute-done | bytes 64 | tf_op jit(solution)/shard_map/ppermute | solution.py:44
  83.6 0.6 convert_bitcast_fusion.1
  84.3 4.8 %collective-permute-done.14 = bf16[1,64,256]{2,1,0:T(8,128)(2,1)S(1)} collective-permute-done((bf16[1,64,256]{2,1,0:T(8,128)(2,1)S(1)}, bf16[1,64,256]{2,1,0:T(8,128)(2,1)S(1)}, u32[]{:S(2)}, u32[]{:S(2)}) %collective-permute-start.14) | collective-permute-done | bytes 32800 | tf_op jit(solution)/shard_map/ppermute | solution.py:44
  89.2 4.3 %collective-permute-done.15 = bf16[2,64,256]{2,1,0:T(8,128)(2,1)S(1)} collective-permute-done((bf16[2,64,256]{2,1,0:T(8,128)(2,1)S(1)}, bf16[2,64,256]{2,1,0:T(8,128)(2,1)S(1)}, u32[]{:S(2)}, u32[]{:S(2)}) %collective-permute-start.15) | collective-permute-done | bytes 65568 | tf_op jit(solution)/shard_map/ppermute | solution.py:44
  94.1 4.5 %collective-permute-done.16 = bf16[2,2,64,256]{3,2,0,1:T(8,128)(2,1)S(1)} collective-permute-done((bf16[2,2,64,256]{3,2,0,1:T(8,128)(2,1)S(1)}, bf16[2,2,64,256]{3,2,0,1:T(8,128)(2,1)S(1)}, u32[]{:S(2)}, u32[]{:S(2)}) %collective-permute-start.16) | collective-permute-done | bytes 131104 | tf_op jit(solution)/shard_map/ppermute | solution.py:44
  98.6 1.6 collective-permute-start.17
  100.3 2.3 %all_gather.7 = bf16[768,256]{0,1:T(8,128)(2,1)S(1)} all-gather(bf16[384,256]{0,1:T(8,128)(2,1)S(1)} %get-tuple-element.26), channel_id=1, replica_groups=mesh['user'=16,'item'=2] {'item'}, dimensions={0}, use_global_device_ids=true | all-gather | bytes 589824 | tf_op jit(solution)/shard_map/all_gather | solution.py:119
  102.6 2.5 %collective-permute-done.17 = bf16[2,2,2,64,256]{4,3,0,1,2:T(8,128)(2,1)S(1)} collective-permute-done((bf16[2,2,2,64,256]{4,3,0,1,2:T(8,128)(2,1)S(1)}, bf16[2,2,2,64,256]{4,3,0,1,2:T(8,128)(2,1)S(1)}, u32[]{:S(2)}, u32[]{:S(2)}) %collective-permute-start.17) | collective-permute-done | bytes 262176 | tf_op jit(solution)/shard_map/ppermute | solution.py:44
  105.2 0.7 convolution_add_fusion
  105.9 0.9 fusion.41
  106.8 1.9 %select_bitcast_fusion = f32[2,2,2,64,256]{4,3,0,1,2:T(8,128)} fusion(f32[2,2,2,1,64,256]{5,4,3,2,1,0:T(8,128)} %get-tuple-element.35, f32[2,2,2,1,64,256]{5,4,3,2,1,0:T(8,128)S(1)} %get-tuple-element.34, pred[]{:T(512)S(6)} %eq.75), kind=kLoop, calls=%fused_computation.15 | loop fusion | flops 131072 | bytes 1572865 | tf_op jit(solution)/shard_map/jit(_where)/select_n | solution.py:68
  108.7 1.5 collective-permute-start.19
  110.2 1.6 reshape.242
  111.8 1.1 fusion.8
  113.0 0.7 copy.61
  113.7 1.7 %reshape.243 = f32[64,256]{1,0:T(8,128)} reshape(f32[64,4,64]{2,1,0:T(4,128)} %copy.61) | data formatting | bytes 131072 | tf_op jit(solution)/shard_map/reshape | solution.py:23
  115.9 5.2 %collective-permute-done.19 = f32[2,2,2,64,256]{4,3,0,1,2:T(8,128)} collective-permute-done((f32[2,2,2,64,256]{4,3,0,1,2:T(8,128)}, f32[2,2,2,64,256]{4,3,0,1,2:T(8,128)}, u32[]{:S(2)}, u32[]{:S(2)}) %collective-permute-start.19) | collective-permute-done | bytes 524320 | tf_op jit(solution)/shard_map/ppermute | solution.py:44
  121.1 1.3 bitcast_add_fusion
  123.0 0.6 convolution_add_fusion.2
  123.6 5.2 %collective-permute-done.20 = f32[2,2,64,256]{3,2,0,1:T(8,128)S(1)} collective-permute-done((f32[2,2,64,256]{3,2,0,1:T(8,128)S(1)}, f32[2,2,64,256]{3,2,0,1:T(8,128)S(1)}, u32[]{:S(2)}, u32[]{:S(2)}) %collective-permute-start.20) | collective-permute-done | bytes 262176 | tf_op jit(solution)/shard_map/ppermute | solution.py:44
  129.2 5.5 %collective-permute-done.21 = f32[2,64,256]{2,1,0:T(8,128)S(1)} collective-permute-done((f32[2,64,256]{2,1,0:T(8,128)S(1)}, f32[2,64,256]{2,1,0:T(8,128)S(1)}, u32[]{:S(2)}, u32[]{:S(2)}) %collective-permute-start.21) | collective-permute-done | bytes 131104 | tf_op jit(solution)/shard_map/ppermute | solution.py:44
  135.5 4.6 %collective-permute-done.22 = f32[64,256]{1,0:T(8,128)S(1)} collective-permute-done((f32[64,256]{1,0:T(8,128)S(1)}, f32[64,256]{1,0:T(8,128)S(1)}, u32[]{:S(2)}, u32[]{:S(2)}) %collective-permute-start.22) | collective-permute-done | bytes 65568 | tf_op jit(solution)/shard_map/ppermute | solution.py:44
  140.7 1.1 collective-permute-done.23
  142.4 3.1 %collective-permute-done.24 = f32[2,4]{1,0:T(2,128)S(1)} collective-permute-done((f32[2,4]{1,0:T(2,128)S(1)}, f32[2,4]{1,0:T(2,128)S(1)}, u32[]{:S(2)}, u32[]{:S(2)}) %collective-permute-start.24) | collective-permute-done | bytes 64 | tf_op jit(solution)/shard_map/ppermute | solution.py:44
  146.0 3.1 %collective-permute-done.25 = f32[2,4]{1,0:T(2,128)S(1)} collective-permute-done((f32[2,4]{1,0:T(2,128)S(1)}, f32[2,4]{1,0:T(2,128)S(1)}, u32[]{:S(2)}, u32[]{:S(2)}) %collective-permute-start.25) | collective-permute-done | bytes 64 | tf_op jit(solution)/shard_map/ppermute | solution.py:44
  149.1 3.6 %collective-permute-done.26 = f32[2,4]{1,0:T(2,128)S(1)} collective-permute-done((f32[2,4]{1,0:T(2,128)S(1)}, f32[2,4]{1,0:T(2,128)S(1)}, u32[]{:S(2)}, u32[]{:S(2)}) %collective-permute-start.26) | collective-permute-done | bytes 64 | tf_op jit(solution)/shard_map/ppermute | solution.py:44
  152.7 4.5 %collective-permute-done.27 = f32[2,4]{1,0:T(2,128)S(1)} collective-permute-done((f32[2,4]{1,0:T(2,128)S(1)}, f32[2,4]{1,0:T(2,128)S(1)}, u32[]{:S(2)}, u32[]{:S(2)}) %collective-permute-start.27) | collective-permute-done | bytes 64 | tf_op jit(solution)/shard_map/ppermute | solution.py:44
  157.7 0.9 copy.64
  158.6 0.7 subtract_bitcast_fusion.1
  159.3 0.9 copy.65
  (137 shorter events, 9.6 us)
Async XLA Ops:
  0.6 41.1 %copy-start = (f32[64,64]{1,0:T(8,128)S(1)}, f32[64,64]{1,0:T(8,128)}, u32[]{:S(2)}) copy-start(f32[64,64]{1,0:T(8,128)} %param.9) | copy-start | bytes 49156
  2.1 7.4 %copy-start.14 = (s32[1,1,12,2]{2,3,1,0:T(2,128)S(1)}, s32[1,1,12,2]{2,3,1,0:T(2,128)}, u32[]{:S(2)}) copy-start(s32[1,1,12,2]{2,3,1,0:T(2,128)} %param.12) | copy-start | bytes 292
  2.1 8.1 %collective-permute-start = (bf16[1,64,256]{2,1,0:T(8,128)(2,1)S(1)}, bf16[1,64,256]{2,1,0:T(8,128)(2,1)S(1)}, u32[]{:S(2)}, u32[]{:S(2)}) collective-permute-start(bf16[1,64,256]{2,1,0:T(8,128)(2,1)S(1)} %get-tuple-element.57), channel_id=1, source_target_pairs={{0,16},{2,18},{4,20},{6,22},{8,24},{10,26},{12,28},{14,30},{16,0},... | collective-permute-start | bytes 98312 | tf_op jit(solution)/shard_map/ppermute | solution.py:44
  10.3 5.8 %collective-permute-start.1 = (bf16[2,64,256]{2,1,0:T(8,128)(2,1)S(1)}, bf16[2,64,256]{2,1,0:T(8,128)(2,1)S(1)}, u32[]{:S(2)}, u32[]{:S(2)}) collective-permute-start(bf16[2,64,256]{2,1,0:T(8,128)(2,1)S(1)} %maximum_bitcast_fusion), channel_id=1, source_target_pairs={{0,8},{2,10},{4,12},{6,14},{8,0},{10,2},{12,4},{14,6},{16,24},{18,... | collective-permute-start | bytes 196616 | tf_op jit(solution)/shard_map/ppermute | solution.py:44
  16.8 7.1 %collective-permute-start.2 = (bf16[2,2,64,256]{3,2,0,1:T(8,128)(2,1)}, bf16[2,2,64,256]{3,2,0,1:T(8,128)(2,1)S(1)}, u32[]{:S(2)}, u32[]{:S(2)}) collective-permute-start(bf16[2,2,64,256]{3,2,0,1:T(8,128)(2,1)} %pad_maximum_fusion.4), channel_id=1, source_target_pairs={{0,4},{2,6},{4,0},{6,2},{8,12},{10,14},{12,8},{14,10},{16,20},{18,... | collective-permute-start | bytes 393224 | tf_op jit(solution)/shard_map/ppermute | solution.py:44
  18.3 1.9 %copy-start.5 = (f32[1,64,256]{2,1,0:T(8,128)S(1)}, f32[1,64,256]{2,1,0:T(8,128)}, u32[]{:S(2)}) copy-start(f32[1,64,256]{2,1,0:T(8,128)} %param.8) | copy-start | bytes 196612
  24.0 7.3 %collective-permute-start.3 = (bf16[2,2,2,64,256]{4,3,0,1,2:T(8,128)(2,1)S(1)}, bf16[2,2,2,64,256]{4,3,0,1,2:T(8,128)(2,1)S(1)}, u32[]{:S(2)}, u32[]{:S(2)}) collective-permute-start(bf16[2,2,2,64,256]{4,3,0,1,2:T(8,128)(2,1)S(1)} %pad_maximum_fusion.2), channel_id=1, source_target_pairs={{0,2},{2,0},{4,6},{6,4},{8,10},{10,8},{12,14},{14,12},{16,18},{18,... | collective-permute-start | bytes 786440 | tf_op jit(solution)/shard_map/ppermute | solution.py:44
  32.1 4.4 %copy-start.9 = (f32[64,4,64]{2,1,0:T(4,128)S(1)}, f32[64,4,64]{2,1,0:T(4,128)}, u32[]{:S(2)}) copy-start(f32[64,4,64]{2,1,0:T(4,128)} %reshape_squeeze.7) | copy-start | bytes 196612
  32.1 4.3 %copy-start.12 = (f32[64,64]{1,0:T(8,128)S(1)}, f32[64,64]{1,0:T(8,128)}, u32[]{:S(2)}) copy-start(f32[64,64]{1,0:T(8,128)} %param.10) | copy-start | bytes 49156
  35.0 12.2 %collective-permute-start.5 = (f32[2,2,2,64,256]{4,3,0,1,2:T(8,128)}, f32[2,2,2,64,256]{4,3,0,1,2:T(8,128)}, u32[]{:S(2)}, u32[]{:S(2)}) collective-permute-start(f32[2,2,2,64,256]{4,3,0,1,2:T(8,128)} %select_bitcast_fusion.1), channel_id=1, source_target_pairs={{0,2},{2,0},{4,6},{6,4},{8,10},{10,8},{12,14},{14,12},{16,18},{18,... | collective-permute-start | bytes 1572872 | tf_op jit(solution)/shard_map/ppermute | solution.py:44
  48.5 6.4 %collective-permute-start.6 = (f32[2,2,64,256]{3,2,0,1:T(8,128)S(1)}, f32[2,2,64,256]{3,2,0,1:T(8,128)S(1)}, u32[]{:S(2)}, u32[]{:S(2)}) collective-permute-start(f32[2,2,64,256]{3,2,0,1:T(8,128)S(1)} %select_bitcast_fusion.5), channel_id=1, source_target_pairs={{0,4},{2,6},{4,0},{6,2},{8,12},{10,14},{12,8},{14,10},{16,20},{18,... | collective-permute-start | bytes 786440 | tf_op jit(solution)/shard_map/ppermute | solution.py:44
  55.0 5.7 %collective-permute-start.7 = (f32[2,64,256]{2,1,0:T(8,128)S(1)}, f32[2,64,256]{2,1,0:T(8,128)S(1)}, u32[]{:S(2)}, u32[]{:S(2)}) collective-permute-start(f32[2,64,256]{2,1,0:T(8,128)S(1)} %select_bitcast_fusion.11), channel_id=1, source_target_pairs={{0,8},{2,10},{4,12},{6,14},{8,0},{10,2},{12,4},{14,6},{16,24},{18,... | collective-permute-start | bytes 393224 | tf_op jit(solution)/shard_map/ppermute | solution.py:44
  55.6 11.0 %copy-start.11 = (f32[64,256]{1,0:T(8,128)S(1)}, f32[64,256]{1,0:T(8,128)}, u32[]{:S(2)}) copy-start(f32[64,256]{1,0:T(8,128)} %reshape.237) | copy-start | bytes 196612
  55.6 11.3 %copy-start.13 = (f32[4]{0:T(128)S(1)}, f32[4]{0:T(128)}, u32[]{:S(2)}) copy-start(f32[4]{0:T(128)} %reduce_sum.113) | copy-start | bytes 52
  55.6 5.3 %collective-permute-start.4 = (bf16[384,256]{0,1:T(8,128)(2,1)S(1)}, bf16[384,256]{0,1:T(8,128)(2,1)S(1)}, u32[]{:S(2)}, u32[]{:S(2)}) collective-permute-start(bf16[384,256]{0,1:T(8,128)(2,1)S(1)} %select_convert_fusion.1), channel_id=1, source_target_pairs={{0,1},{1,0},{2,3},{3,2},{4,5},{5,4},{6,7},{7,6},{8,9},{9,8},{10,11... | collective-permute-start | bytes 589832 | tf_op jit(solution)/shard_map/ppermute | solution.py:44
  60.8 5.8 %collective-permute-start.8 = (f32[64,256]{1,0:T(8,128)S(1)}, f32[64,256]{1,0:T(8,128)S(1)}, u32[]{:S(2)}, u32[]{:S(2)}) collective-permute-start(f32[64,256]{1,0:T(8,128)S(1)} %select_bitcast_fusion.17), channel_id=1, source_target_pairs={{0,16},{2,18},{4,20},{6,22},{8,24},{10,26},{12,28},{14,30},{16,0},... | collective-permute-start | bytes 196616 | tf_op jit(solution)/shard_map/ppermute | solution.py:44
  61.1 39.2 %copy-start.3 = (f32[384,256]{0,1:T(8,128)}, f32[384,256]{0,1:T(8,128)S(1)}, u32[]{:S(2)}) copy-start(f32[384,256]{0,1:T(8,128)S(1)} %get-tuple-element.33) | copy-start | bytes 1179652
  66.7 33.5 %copy-start.7 = (f32[64,256]{1,0:T(8,128)}, f32[64,256]{1,0:T(8,128)S(1)}, u32[]{:S(2)}) copy-start(f32[64,256]{1,0:T(8,128)S(1)} %get-tuple-element.31) | copy-start | bytes 196612
  66.9 1.2 collective-permute-start.9
  68.1 3.6 %collective-permute-start.10 = (f32[2,4]{1,0:T(2,128)S(1)}, f32[2,4]{1,0:T(2,128)S(1)}, u32[]{:S(2)}, u32[]{:S(2)}) collective-permute-start(f32[2,4]{1,0:T(2,128)S(1)} %fusion.37), channel_id=1, source_target_pairs={{0,2},{2,0},{4,6},{6,4},{8,10},{10,8},{12,14},{14,12},{16,18},{18,... | collective-permute-start | bytes 104 | tf_op jit(solution)/shard_map/ppermute | solution.py:44
  71.8 3.6 %collective-permute-start.11 = (f32[2,4]{1,0:T(2,128)S(1)}, f32[2,4]{1,0:T(2,128)S(1)}, u32[]{:S(2)}, u32[]{:S(2)}) collective-permute-start(f32[2,4]{1,0:T(2,128)S(1)} %fusion.54), channel_id=1, source_target_pairs={{0,4},{2,6},{4,0},{6,2},{8,12},{10,14},{12,8},{14,10},{16,20},{18,... | collective-permute-start | bytes 104 | tf_op jit(solution)/shard_map/ppermute | solution.py:44
  75.4 3.6 %collective-permute-start.12 = (f32[2,4]{1,0:T(2,128)S(1)}, f32[2,4]{1,0:T(2,128)S(1)}, u32[]{:S(2)}, u32[]{:S(2)}) collective-permute-start(f32[2,4]{1,0:T(2,128)S(1)} %add.169), channel_id=1, source_target_pairs={{0,8},{2,10},{4,12},{6,14},{8,0},{10,2},{12,4},{14,6},{16,24},{18,... | collective-permute-start | bytes 104 | tf_op jit(solution)/shard_map/ppermute | solution.py:44
  79.0 4.5 %collective-permute-start.13 = (f32[2,4]{1,0:T(2,128)S(1)}, f32[2,4]{1,0:T(2,128)S(1)}, u32[]{:S(2)}, u32[]{:S(2)}) collective-permute-start(f32[2,4]{1,0:T(2,128)S(1)} %add.170), channel_id=1, source_target_pairs={{0,16},{2,18},{4,20},{6,22},{8,24},{10,26},{12,28},{14,30},{16,0},... | collective-permute-start | bytes 104 | tf_op jit(solution)/shard_map/ppermute | solution.py:44
  84.3 4.8 %collective-permute-start.14 = (bf16[1,64,256]{2,1,0:T(8,128)(2,1)S(1)}, bf16[1,64,256]{2,1,0:T(8,128)(2,1)S(1)}, u32[]{:S(2)}, u32[]{:S(2)}) collective-permute-start(bf16[1,64,256]{2,1,0:T(8,128)(2,1)S(1)} %get-tuple-element.28), channel_id=1, source_target_pairs={{0,16},{2,18},{4,20},{6,22},{8,24},{10,26},{12,28},{14,30},{16,0},... | collective-permute-start | bytes 98312 | tf_op jit(solution)/shard_map/ppermute | solution.py:44
  89.1 4.3 %collective-permute-start.15 = (bf16[2,64,256]{2,1,0:T(8,128)(2,1)S(1)}, bf16[2,64,256]{2,1,0:T(8,128)(2,1)S(1)}, u32[]{:S(2)}, u32[]{:S(2)}) collective-permute-start(bf16[2,64,256]{2,1,0:T(8,128)(2,1)S(1)} %maximum_bitcast_fusion.1), channel_id=1, source_target_pairs={{0,8},{2,10},{4,12},{6,14},{8,0},{10,2},{12,4},{14,6},{16,24},{18,... | collective-permute-start | bytes 196616 | tf_op jit(solution)/shard_map/ppermute | solution.py:44
  93.5 5.0 %collective-permute-start.16 = (bf16[2,2,64,256]{3,2,0,1:T(8,128)(2,1)S(1)}, bf16[2,2,64,256]{3,2,0,1:T(8,128)(2,1)S(1)}, u32[]{:S(2)}, u32[]{:S(2)}) collective-permute-start(bf16[2,2,64,256]{3,2,0,1:T(8,128)(2,1)S(1)} %pad_maximum_fusion.5), channel_id=1, source_target_pairs={{0,4},{2,6},{4,0},{6,2},{8,12},{10,14},{12,8},{14,10},{16,20},{18,... | collective-permute-start | bytes 393224 | tf_op jit(solution)/shard_map/ppermute | solution.py:44
  98.6 6.4 %collective-permute-start.17 = (bf16[2,2,2,64,256]{4,3,0,1,2:T(8,128)(2,1)S(1)}, bf16[2,2,2,64,256]{4,3,0,1,2:T(8,128)(2,1)S(1)}, u32[]{:S(2)}, u32[]{:S(2)}) collective-permute-start(bf16[2,2,2,64,256]{4,3,0,1,2:T(8,128)(2,1)S(1)} %pad_maximum_fusion.3), channel_id=1, source_target_pairs={{0,2},{2,0},{4,6},{6,4},{8,10},{10,8},{12,14},{14,12},{16,18},{18,... | collective-permute-start | bytes 786440 | tf_op jit(solution)/shard_map/ppermute | solution.py:44
  102.6 2.6 %copy-start.1 = (bf16[768,256]{0,1:T(8,128)(2,1)}, bf16[768,256]{0,1:T(8,128)(2,1)S(1)}, u32[]{:S(2)}) copy-start(bf16[768,256]{0,1:T(8,128)(2,1)S(1)} %all_gather.7) | copy-start | bytes 1179652
  108.7 12.4 %collective-permute-start.19 = (f32[2,2,2,64,256]{4,3,0,1,2:T(8,128)}, f32[2,2,2,64,256]{4,3,0,1,2:T(8,128)}, u32[]{:S(2)}, u32[]{:S(2)}) collective-permute-start(f32[2,2,2,64,256]{4,3,0,1,2:T(8,128)} %select_bitcast_fusion), channel_id=1, source_target_pairs={{0,2},{2,0},{4,6},{6,4},{8,10},{10,8},{12,14},{14,12},{16,18},{18,... | collective-permute-start | bytes 1572872 | tf_op jit(solution)/shard_map/ppermute | solution.py:44
  115.9 7.1 %copy-start.2 = (bf16[768,256]{0,1:T(8,128)(2,1)S(1)}, bf16[768,256]{0,1:T(8,128)(2,1)}, u32[]{:S(2)}) copy-start(bf16[768,256]{0,1:T(8,128)(2,1)} %copy-done.1) | copy-start | bytes 1179652
  122.4 6.4 %collective-permute-start.20 = (f32[2,2,64,256]{3,2,0,1:T(8,128)S(1)}, f32[2,2,64,256]{3,2,0,1:T(8,128)S(1)}, u32[]{:S(2)}, u32[]{:S(2)}) collective-permute-start(f32[2,2,64,256]{3,2,0,1:T(8,128)S(1)} %select_bitcast_fusion.2), channel_id=1, source_target_pairs={{0,4},{2,6},{4,0},{6,2},{8,12},{10,14},{12,8},{14,10},{16,20},{18,... | collective-permute-start | bytes 786440 | tf_op jit(solution)/shard_map/ppermute | solution.py:44
  129.0 5.7 %collective-permute-start.21 = (f32[2,64,256]{2,1,0:T(8,128)S(1)}, f32[2,64,256]{2,1,0:T(8,128)S(1)}, u32[]{:S(2)}, u32[]{:S(2)}) collective-permute-start(f32[2,64,256]{2,1,0:T(8,128)S(1)} %select_bitcast_fusion.8), channel_id=1, source_target_pairs={{0,8},{2,10},{4,12},{6,14},{8,0},{10,2},{12,4},{14,6},{16,24},{18,... | collective-permute-start | bytes 393224 | tf_op jit(solution)/shard_map/ppermute | solution.py:44
  129.1 11.0 %copy-start.6 = (f32[64,256]{1,0:T(8,128)S(1)}, f32[64,256]{1,0:T(8,128)}, u32[]{:S(2)}) copy-start(f32[64,256]{1,0:T(8,128)} %get-tuple-element.29) | copy-start | bytes 196612
  129.1 11.0 %copy-start.10 = (f32[64,256]{1,0:T(8,128)S(1)}, f32[64,256]{1,0:T(8,128)}, u32[]{:S(2)}) copy-start(f32[64,256]{1,0:T(8,128)} %reshape.243) | copy-start | bytes 196612
  129.1 28.4 %copy-start.4 = (f32[384,256]{0,1:T(8,128)S(1)}, f32[384,256]{0,1:T(8,128)}, u32[]{:S(2)}) copy-start(f32[384,256]{0,1:T(8,128)} %copy-done.3) | copy-start | bytes 1179652
  129.1 5.7 %collective-permute-start.18 = (bf16[384,256]{0,1:T(8,128)(2,1)S(1)}, bf16[384,256]{0,1:T(8,128)(2,1)S(1)}, u32[]{:S(2)}, u32[]{:S(2)}) collective-permute-start(bf16[384,256]{0,1:T(8,128)(2,1)S(1)} %select_convert_fusion), channel_id=1, source_target_pairs={{0,1},{1,0},{2,3},{3,2},{4,5},{5,4},{6,7},{7,6},{8,9},{9,8},{10,11... | collective-permute-start | bytes 589832 | tf_op jit(solution)/shard_map/ppermute | solution.py:44
  134.7 5.4 %collective-permute-start.22 = (f32[64,256]{1,0:T(8,128)S(1)}, f32[64,256]{1,0:T(8,128)S(1)}, u32[]{:S(2)}, u32[]{:S(2)}) collective-permute-start(f32[64,256]{1,0:T(8,128)S(1)} %select_bitcast_fusion.14), channel_id=1, source_target_pairs={{0,16},{2,18},{4,20},{6,22},{8,24},{10,26},{12,28},{14,30},{16,0},... | collective-permute-start | bytes 196616 | tf_op jit(solution)/shard_map/ppermute | solution.py:44
  140.6 1.2 collective-permute-start.23
  141.8 3.6 %collective-permute-start.24 = (f32[2,4]{1,0:T(2,128)S(1)}, f32[2,4]{1,0:T(2,128)S(1)}, u32[]{:S(2)}, u32[]{:S(2)}) collective-permute-start(f32[2,4]{1,0:T(2,128)S(1)} %fusion.36), channel_id=1, source_target_pairs={{0,2},{2,0},{4,6},{6,4},{8,10},{10,8},{12,14},{14,12},{16,18},{18,... | collective-permute-start | bytes 104 | tf_op jit(solution)/shard_map/ppermute | solution.py:44
  145.5 3.6 %collective-permute-start.25 = (f32[2,4]{1,0:T(2,128)S(1)}, f32[2,4]{1,0:T(2,128)S(1)}, u32[]{:S(2)}, u32[]{:S(2)}) collective-permute-start(f32[2,4]{1,0:T(2,128)S(1)} %fusion.53), channel_id=1, source_target_pairs={{0,4},{2,6},{4,0},{6,2},{8,12},{10,14},{12,8},{14,10},{16,20},{18,... | collective-permute-start | bytes 104 | tf_op jit(solution)/shard_map/ppermute | solution.py:44
  149.1 3.6 %collective-permute-start.26 = (f32[2,4]{1,0:T(2,128)S(1)}, f32[2,4]{1,0:T(2,128)S(1)}, u32[]{:S(2)}, u32[]{:S(2)}) collective-permute-start(f32[2,4]{1,0:T(2,128)S(1)} %add.187), channel_id=1, source_target_pairs={{0,8},{2,10},{4,12},{6,14},{8,0},{10,2},{12,4},{14,6},{16,24},{18,... | collective-permute-start | bytes 104 | tf_op jit(solution)/shard_map/ppermute | solution.py:44
  152.7 4.5 %collective-permute-start.27 = (f32[2,4]{1,0:T(2,128)S(1)}, f32[2,4]{1,0:T(2,128)S(1)}, u32[]{:S(2)}, u32[]{:S(2)}) collective-permute-start(f32[2,4]{1,0:T(2,128)S(1)} %add.188), channel_id=1, source_target_pairs={{0,16},{2,18},{4,20},{6,22},{8,24},{10,26},{12,28},{14,30},{16,0},... | collective-permute-start | bytes 104 | tf_op jit(solution)/shard_map/ppermute | solution.py:44
  157.5 1.1 copy-start.8

commit v3 on v2

--- a/solution.py
+++ b/solution.py
@@ -53,7 +53,7 @@
     return values[0], values[1]
 
 
-def halve_sum(part, axis, send_type):
+def halve_sum(part, axis, send_type, extra=None):
     size, bits = bit_count(axis)
     me = lax.axis_index(axis)
     rows, width = part.shape[0] // size, part.shape[1]
@@ -66,9 +66,15 @@
         upper = ((me >> bit) & 1) == 1
         keep = jnp.where(upper, high, low)
         send = jnp.where(upper, low, high).astype(send_type)
-        buf = keep + swap_with(send, axis, size, bit).astype(jnp.float32)
+        if extra is None:
+            buf = keep + swap_with(send, axis, size, bit).astype(jnp.float32)
+        else:
+            message = jnp.concatenate([send.reshape(-1, width), extra])
+            got = swap_with(message, axis, size, bit)
+            buf = keep + got[: -extra.shape[0]].reshape(keep.shape)
+            extra = extra + got[-extra.shape[0] :]
         left.remove(bit)
-    return buf.reshape(rows, width)
+    return buf.reshape(rows, width), extra
 
 
 def double_gather(piece, axis):
@@ -118,36 +124,42 @@
     def user_range_of(user_vec):
         return lax.all_gather(user_vec.astype(jnp.bfloat16), "item", axis=0, tiled=True)
 
-    def finish_users(user_vec, part_user):
-        total = halve_sum(part_user, "item", jnp.bfloat16)
-        return prior_term(user_vec, prior_user) + noise_prec * total
-
     def item_range_of(item_vec):
         return double_gather(item_vec.astype(jnp.bfloat16), "user")
 
-    def finish_items(item_vec, part_item):
-        total = halve_sum(part_item, "user", jnp.float32)
-        return prior_term(item_vec, prior_item) + noise_prec * total
-
     def operate(user_vec, item_vec):
-        part_user, part_item = cross_parts(user_range_of(user_vec), item_range_of(item_vec))
-        return (finish_users(user_vec, part_user), finish_items(item_vec, part_item))
-
-    def inner(a_user, a_item, b_user, b_item):
-        return per_draw(a_user, b_user) + per_draw(a_item, b_item)
+        user_range = user_range_of(user_vec)
+        item_range = item_range_of(item_vec)
+        part_user, part_item = cross_parts(user_range, item_range)
+        prior_user_part = prior_term(user_vec, prior_user)
+        prior_item_part = prior_term(item_vec, prior_item)
+        norm_part = per_draw(user_vec, user_vec) + per_draw(item_vec, item_vec)
+        cross_dot = per_draw(user_range.astype(jnp.float32), part_user) + per_draw(
+            item_range.astype(jnp.float32), part_item
+        )
+        curve_part = (
+            per_draw(user_vec, prior_user_part)
+            + per_draw(item_vec, prior_item_part)
+            + noise_prec * cross_dot
+        )
+        sums = jnp.concatenate([norm_part, curve_part]).reshape(1, 2 * DRAWS)
+        sums = jnp.pad(sums, ((0, 7), (0, width - 2 * DRAWS)))
+        total_user, _ = halve_sum(part_user, "item", jnp.bfloat16)
+        total_item, sums = halve_sum(part_item, "user", jnp.float32, sums)
+        sums = sums[0, : 2 * DRAWS]
+        size, bits = bit_count("item")
+        for bit in range(bits):
+            sums = sums + swap_with(sums, "item", size, bit)
+        image_user = prior_user_part + noise_prec * total_user
+        image_item = prior_item_part + noise_prec * total_item
+        return (image_user, image_item, sums[:DRAWS], sums[DRAWS:])
 
     sol_user = jnp.zeros_like(user_own)
     sol_item = jnp.zeros_like(item_own)
     res_user, res_item = (user_own, item_own)
     dir_user, dir_item = (user_own, item_own)
 
-    def two_sums(u_vec, v_vec, image_u, image_v):
-        return butterfly_psum(
-            (inner(u_vec, v_vec, u_vec, v_vec), inner(u_vec, v_vec, image_u, image_v)),
-        )
-
-    along_user, along_item = operate(res_user, res_item)
-    norm_now, curve = two_sums(res_user, res_item, along_user, along_item)
+    along_user, along_item, norm_now, curve = operate(res_user, res_item)
     step_len = norm_now / curve
     for iteration in range(ITERS):
         sol_user = sol_user + widen(step_len) * dir_user
@@ -155,8 +167,7 @@
         res_user = res_user - widen(step_len) * along_user
         res_item = res_item - widen(step_len) * along_item
         if iteration + 1 < ITERS:
-            image_user, image_item = operate(res_user, res_item)
-            norm_next, curve = two_sums(res_user, res_item, image_user, image_item)
+            image_user, image_item, norm_next, curve = operate(res_user, res_item)
             beta_coef = norm_next / norm_now
             step_len = norm_next / (curve - beta_coef * norm_next / step_len)
             dir_user = res_user + widen(beta_coef) * dir_user

time: 161 us -> 142 us (0.88)
  waiting for transfers between devices: 90.2 us -> 71.4 us
  local copies, waits for them, and re-layouts: 15.7 us -> 11 us
  other arithmetic: 19.4 us -> 21.6 us
    ppermute x28 -> x20, waiting for transfers between devices: 90.2 us -> 71.4 us  [swap_with(): return lax.ppermute(value, axis, pairs)]
    select_n x8, other arithmetic: 4 us -> 0.27 us  [halve_sum(): send = jnp.where(upper, low, high).astype(send_type)]
    reshape x2, local copies, waits for them, and re-layouts: 3.33 us -> 0.28 us  [prior_term(): return mixed.reshape(row_total, DRAWS * DIM)]
    another operation x14, other arithmetic: 1.02 us -> 3.72 us  [double_gather(): buf = jnp.stack([first, second], axis=step)]
    convert_element_type x2, other arithmetic: 0.14 us -> 2.05 us  [user_range_of(): user_vec.astype(jnp.bfloat16)]
    concatenate x0 -> x8, other arithmetic: none -> 1.85 us  [halve_sum(): message = jnp.concatenate([send.reshape(-1, width), extra])]
    reduce_sum x14, other arithmetic: 4.56 us -> 2.91 us  [per_draw(): return jnp.sum(product, axis=(0, 2))]
    unnamed x35 -> x37, local copies, waits for them, and re-layouts: 4.83 us -> 6.06 us
  transfers between devices with their start and end apart: 28 -> 20, of which waited for: 23 -> 16; matrix products, arithmetic and copies ran while one was open for 17% -> 14% of each run, Pallas kernels for 0% -> 0%
where the time goes in v3:
time: 142 us; the launch traced here: 141 us
  waiting for transfers between devices  71.4 us (50%)
  other arithmetic  21.6 us (15%)
  starting transfers between devices  20.2 us (14%)
  local copies, waits for them, and re-layouts  11 us (8%)
  matrix products  10.4 us (7%)
  blocking collectives  4.34 us (3%)
  between operations  1.95 us (1%)
    ppermute x20, waiting for transfers between devices, swap_with(): return lax.ppermute(value, axis, pairs)  71.4 us
    ppermute x20, starting transfers between devices, swap_with(): return lax.ppermute(value, axis, pairs)  20.2 us
    unnamed x37, local copies, waits for them, and re-layouts  6.06 us
    all_gather x2, blocking collectives, user_range_of(): lax.all_gather(user_vec.astype(jnp.bfloat16), 'item', axis=0, tiled=True)  4.34 us
    another operation x14, other arithmetic, double_gather(): buf = jnp.stack([first, second], axis=step)  3.72 us
    dot_general x4, matrix products, prior_term(): mixed = jnp.einsum('nde,ef->ndf', grouped, prior_mat, precision=top_prec)  3.48 us
    reduce_sum x14, other arithmetic, per_draw(): return jnp.sum(product, axis=(0, 2))  2.91 us
  transfers between devices with their start and end apart: 20, of which 16 were waited for; matrix products, arithmetic and copies ran while one was open for 14% of the time, Pallas kernels for 0%

profile of v3, /device:TPU:0, one launch (start us, length us, event | category | flops | bytes accessed | tf_op | source)
XLA Modules:
  0.0 140.9 jit_solution(7381708643731804667)
XLA Ops:
  0.6 0.9 multiply_reduce_fusion.6
  1.6 4.1 %collective-permute-start = (bf16[1,64,256]{2,1,0:T(8,128)(2,1)S(1)}, bf16[1,64,256]{2,1,0:T(8,128)(2,1)S(1)}, u32[]{:S(2)}, u32[]{:S(2)}) collective-permute-start(bf16[1,64,256]{2,1,0:T(8,128)(2,1)S(1)} %get-tuple-element.53), channel_id=1, source_target_pairs={{0,16},{2,18},{4,20},{6,22},{8,24},{10,26},{12,28},{14,30},{16,0},... | collective-permute-start | bytes 98312 | tf_op jit(solution)/shard_map/ppermute | solution.py:44
  5.7 0.8 slice_bitcast_fusion.1
  7.1 2.2 %convert_bitcast_fusion = bf16[12,256,256]{2,1,0:T(8,128)(2,1)S(1)} fusion(s32[1,1,12,256,256]{4,3,2,1,0:T(8,128)} %param.11), kind=kLoop, calls=%fused_computation.6 | loop fusion | flops 786432 | bytes 4718592 | tf_op jit(solution)/shard_map/convert_element_type | solution.py:108
  9.3 2.8 %bitcast_convert_fusion = (bf16[3,256,4,256]{3,2,1,0:T(4,128)(2,1)}, f32[3,4,256,256]{3,1,2,0:T(4,128)S(1)}) fusion(bf16[12,256,256]{2,1,0:T(8,128)(2,1)S(1)} %convert_bitcast_fusion, pred[12,4]{0,1:T(4,128)(4,1)S(1)} %fusion.42, pred[12,3]{0,1:T(4,128)(4,1)S(1)} %fusion.41), kind=kOutput, calls=%fused_computation.2 | convolution fusion | flops 19660944 | bytes 6291540 | tf_op jit(solution)/shard_map/trc,tij->ricj/dot_general | solution.py:105
  12.1 1.9 %bitcast_reduce_fusion = (f32[4,256]{1,0:T(4,128)S(1)}, f32[3,256]{1,0:T(4,128)S(1)}) fusion(f32[3,4,256,256]{3,1,2,0:T(4,128)S(1)} %get-tuple-element.59), kind=kLoop, calls=%fused_computation | loop fusion | flops 1571072 | bytes 3152896 | tf_op jit(solution)/shard_map/reduce_sum | solution.py:112
  14.3 1.6 %collective-permute-start.1 = (bf16[2,64,256]{2,1,0:T(8,128)(2,1)S(1)}, bf16[2,64,256]{2,1,0:T(8,128)(2,1)S(1)}, u32[]{:S(2)}, u32[]{:S(2)}) collective-permute-start(bf16[2,64,256]{2,1,0:T(8,128)(2,1)S(1)} %maximum_bitcast_fusion), channel_id=1, source_target_pairs={{0,8},{2,10},{4,12},{6,14},{8,0},{10,2},{12,4},{14,6},{16,24},{18,... | collective-permute-start | bytes 196616 | tf_op jit(solution)/shard_map/ppermute | solution.py:44
  16.1 2.5 %collective-permute-done.1 = bf16[2,64,256]{2,1,0:T(8,128)(2,1)S(1)} collective-permute-done((bf16[2,64,256]{2,1,0:T(8,128)(2,1)S(1)}, bf16[2,64,256]{2,1,0:T(8,128)(2,1)S(1)}, u32[]{:S(2)}, u32[]{:S(2)}) %collective-permute-start.1) | collective-permute-done | bytes 65568 | tf_op jit(solution)/shard_map/ppermute | solution.py:44
  18.7 1.6 %collective-permute-start.2 = (bf16[2,2,64,256]{3,2,0,1:T(8,128)(2,1)S(1)}, bf16[2,2,64,256]{3,2,0,1:T(8,128)(2,1)S(1)}, u32[]{:S(2)}, u32[]{:S(2)}) collective-permute-start(bf16[2,2,64,256]{3,2,0,1:T(8,128)(2,1)S(1)} %pad_maximum_fusion.10), channel_id=1, source_target_pairs={{0,4},{2,6},{4,0},{6,2},{8,12},{10,14},{12,8},{14,10},{16,20},{18,... | collective-permute-start | bytes 393224 | tf_op jit(solution)/shard_map/ppermute | solution.py:44
  20.3 0.9 multiply_reduce_fusion.3
  21.3 2.4 %collective-permute-done.2 = bf16[2,2,64,256]{3,2,0,1:T(8,128)(2,1)S(1)} collective-permute-done((bf16[2,2,64,256]{3,2,0,1:T(8,128)(2,1)S(1)}, bf16[2,2,64,256]{3,2,0,1:T(8,128)(2,1)S(1)}, u32[]{:S(2)}, u32[]{:S(2)}) %collective-permute-start.2) | collective-permute-done | bytes 131104 | tf_op jit(solution)/shard_map/ppermute | solution.py:44
  23.8 1.6 %collective-permute-start.3 = (bf16[2,2,2,64,256]{4,3,0,1,2:T(8,128)(2,1)S(1)}, bf16[2,2,2,64,256]{4,3,0,1,2:T(8,128)(2,1)}, u32[]{:S(2)}, u32[]{:S(2)}) collective-permute-start(bf16[2,2,2,64,256]{4,3,0,1,2:T(8,128)(2,1)S(1)} %pad_maximum_fusion.6), channel_id=1, source_target_pairs={{0,2},{2,0},{4,6},{6,4},{8,10},{10,8},{12,14},{14,12},{16,18},{18,... | collective-permute-start | bytes 786440 | tf_op jit(solution)/shard_map/ppermute | solution.py:44
  25.3 2.1 %all_gather.6 = bf16[768,256]{0,1:T(8,128)(2,1)S(1)} all-gather(bf16[384,256]{0,1:T(8,128)(2,1)S(1)} %bitcast_convert_fusion.1), channel_id=1, replica_groups=mesh['user'=16,'item'=2] {'item'}, dimensions={0}, use_global_device_ids=true | all-gather | bytes 589824 | tf_op jit(solution)/shard_map/all_gather | solution.py:125
  27.4 1.9 %copy.97 = bf16[96,8,4,256]{3,1,2,0:T(8,128)(2,1)S(1)} copy(bf16[96,8,4,256]{3,2,1,0:T(4,128)(2,1)} %bitcast.212) | data formatting | bytes 3145728
  29.7 0.5 add.130
  30.2 1.8 %multiply_reduce_fusion.1 = (f32[4]{0:T(128)}, f32[384,4,64]{0,2,1:T(8,128)}) fusion(f32[384,4,64]{0,2,1:T(8,128)S(1)} %bitcast.207, f32[64,64]{1,0:T(8,128)S(1)} %copy-done), kind=kOutput, calls=%fused_computation.49 | convolution fusion | flops 75694080 | bytes 802832 | tf_op jit(solution)/shard_map/nde,ef->ndf/dot_general | solution.py:22
  32.0 1.0 select_bitcast_fusion.3
  33.1 0.8 fusion.3
  34.1 0.8 copy-done.1
  35.0 0.8 copy.69
  36.0 0.6 reduce_sum.177
  36.6 1.7 %fusion.5 = (f32[256]{0:T(256)S(1)}, f32[768,256]{0,1:T(8,128)S(1)}) fusion(bf16[768,256]{0,1:T(8,128)(2,1)} %copy-done.7, f32[768]{0:T(1024)S(1)} %mul.189, bf16[768,1024]{1,0:T(8,128)(2,1)S(1)} %bitcast.204, bf16[1024,256]{1,0:T(8,128)(2,1)S(1)} %bitcast.209), kind=kOutput, calls=%fused_computation.21 | convolution fusion | flops 403635968 | bytes 3280896 | tf_op jit(solution)/shard_map/dot_general | solution.py:116
  38.5 0.8 multiply_add_fusion.1
  39.3 0.7 maximum_bitcast_fusion.2
  40.0 1.1 pad_maximum_fusion
  41.1 0.6 collective-permute-start.4
  41.7 13.6 %collective-permute-done.4 = f32[520,256]{1,0:T(8,128)S(1)} collective-permute-done((f32[520,256]{1,0:T(8,128)S(1)}, f32[520,256]{1,0:T(8,128)S(1)}, u32[]{:S(2)}, u32[]{:S(2)}) %collective-permute-start.4) | collective-permute-done | bytes 532512 | tf_op jit(solution)/shard_map/ppermute | solution.py:44
  55.6 1.6 %collective-permute-start.5 = (f32[264,256]{1,0:T(8,128)S(1)}, f32[264,256]{1,0:T(8,128)S(1)}, u32[]{:S(2)}, u32[]{:S(2)}) collective-permute-start(f32[264,256]{1,0:T(8,128)S(1)} %pad_maximum_fusion.4), channel_id=1, source_target_pairs={{0,4},{2,6},{4,0},{6,2},{8,12},{10,14},{12,8},{14,10},{16,20},{18,... | collective-permute-start | bytes 811016 | tf_op jit(solution)/shard_map/ppermute | solution.py:44
  57.2 6.2 %collective-permute-done.5 = f32[264,256]{1,0:T(8,128)S(1)} collective-permute-done((f32[264,256]{1,0:T(8,128)S(1)}, f32[264,256]{1,0:T(8,128)S(1)}, u32[]{:S(2)}, u32[]{:S(2)}) %collective-permute-start.5) | collective-permute-done | bytes 270368 | tf_op jit(solution)/shard_map/ppermute | solution.py:44
  63.5 0.7 pad_maximum_fusion.8
  64.1 1.6 %collective-permute-start.6 = (f32[136,256]{1,0:T(8,128)}, f32[136,256]{1,0:T(8,128)}, u32[]{:S(2)}, u32[]{:S(2)}) collective-permute-start(f32[136,256]{1,0:T(8,128)} %pad_maximum_fusion.8), channel_id=1, source_target_pairs={{0,8},{2,10},{4,12},{6,14},{8,0},{10,2},{12,4},{14,6},{16,24},{18,... | collective-permute-start | bytes 417800 | tf_op jit(solution)/shard_map/ppermute | solution.py:44
  65.9 3.6 %collective-permute-done.6 = f32[136,256]{1,0:T(8,128)} collective-permute-done((f32[136,256]{1,0:T(8,128)}, f32[136,256]{1,0:T(8,128)}, u32[]{:S(2)}, u32[]{:S(2)}) %collective-permute-start.6) | collective-permute-done | bytes 139296 | tf_op jit(solution)/shard_map/ppermute | solution.py:44
  69.5 0.9 slice.191
  70.5 0.7 slice_add_fusion.5
  71.6 0.7 select_convert_fusion.1
  72.3 4.2 %collective-permute-done.7 = f32[72,256]{1,0:T(8,128)S(1)} collective-permute-done((f32[72,256]{1,0:T(8,128)S(1)}, f32[72,256]{1,0:T(8,128)S(1)}, u32[]{:S(2)}, u32[]{:S(2)}) %collective-permute-start.7) | collective-permute-done | bytes 73760 | tf_op jit(solution)/shard_map/ppermute | solution.py:44
  76.5 1.1 collective-permute-done.8
  78.4 0.7 convert_bitcast_fusion.1
  79.4 0.7 copy-done.12
  80.1 2.0 %fusion.45 = (bf16[384,256]{0,1:T(8,128)(2,1)}, f32[384,256]{0,1:T(8,128)S(1)}, f32[384,256]{0,1:T(8,128)}) fusion(f32[256]{0:T(256)S(1)} %mul.198, f32[1,384,256]{1,2,0:T(8,128)S(1)} %copy.59, bf16[384,256]{0,1:T(8,128)(2,1)} %copy-done.12, f32[768,256]{0,1:T(8,128)S(1)} %get-tuple-element.61, pred[]{:T(512)S(6)} %eq.78, f32[384,4,64]{0,2,1:T(8,128)} %get-tuple-element.65), kind=kLoop, calls=%fused_computation.149 | loop fusion | flops 786432 | bytes 2753537 | tf_op jit(solution)/shard_map/convert_element_type | solution.py:125
  82.2 2.2 %collective-permute-done.10 = bf16[1,64,256]{2,1,0:T(8,128)(2,1)S(1)} collective-permute-done((bf16[1,64,256]{2,1,0:T(8,128)(2,1)}, bf16[1,64,256]{2,1,0:T(8,128)(2,1)S(1)}, u32[]{:S(2)}, u32[]{:S(2)}) %collective-permute-start.10) | collective-permute-done | bytes 32800 | tf_op jit(solution)/shard_map/ppermute | solution.py:44
  84.4 0.8 select_bitcast_fusion.15
  85.2 1.3 collective-permute-start.11
  86.9 2.6 %collective-permute-done.11 = bf16[2,64,256]{2,1,0:T(8,128)(2,1)S(1)} collective-permute-done((bf16[2,64,256]{2,1,0:T(8,128)(2,1)S(1)}, bf16[2,64,256]{2,1,0:T(8,128)(2,1)S(1)}, u32[]{:S(2)}, u32[]{:S(2)}) %collective-permute-start.11) | collective-permute-done | bytes 65568 | tf_op jit(solution)/shard_map/ppermute | solution.py:44
  89.6 1.2 collective-permute-start.12
  91.3 3.3 %collective-permute-done.12 = bf16[2,2,64,256]{3,2,0,1:T(8,128)(2,1)S(1)} collective-permute-done((bf16[2,2,64,256]{3,2,0,1:T(8,128)(2,1)S(1)}, bf16[2,2,64,256]{3,2,0,1:T(8,128)(2,1)S(1)}, u32[]{:S(2)}, u32[]{:S(2)}) %collective-permute-start.12) | collective-permute-done | bytes 131104 | tf_op jit(solution)/shard_map/ppermute | solution.py:44
  94.6 0.7 pad_maximum_fusion.7
  96.6 2.3 %all_gather.7 = bf16[768,256]{0,1:T(8,128)(2,1)S(1)} all-gather(bf16[384,256]{0,1:T(8,128)(2,1)S(1)} %copy-done.10), channel_id=1, replica_groups=mesh['user'=16,'item'=2] {'item'}, dimensions={0}, use_global_device_ids=true | all-gather | bytes 589824 | tf_op jit(solution)/shard_map/all_gather | solution.py:125
  98.8 3.2 %collective-permute-done.13 = bf16[2,2,2,64,256]{4,3,0,1,2:T(8,128)(2,1)} collective-permute-done((bf16[2,2,2,64,256]{4,3,0,1,2:T(8,128)(2,1)}, bf16[2,2,2,64,256]{4,3,0,1,2:T(8,128)(2,1)}, u32[]{:S(2)}, u32[]{:S(2)}) %collective-permute-start.13) | collective-permute-done | bytes 262176 | tf_op jit(solution)/shard_map/ppermute | solution.py:44
  102.0 1.0 select_bitcast_fusion.1
  103.1 0.8 fusion.4
  104.0 0.8 fusion.6
  105.7 10.8 %collective-permute-done.14 = f32[520,256]{1,0:T(8,128)S(1)} collective-permute-done((f32[520,256]{1,0:T(8,128)S(1)}, f32[520,256]{1,0:T(8,128)S(1)}, u32[]{:S(2)}, u32[]{:S(2)}) %collective-permute-start.14) | collective-permute-done | bytes 532512 | tf_op jit(solution)/shard_map/ppermute | solution.py:44
  116.8 1.5 %collective-permute-start.15 = (f32[264,256]{1,0:T(8,128)S(1)}, f32[264,256]{1,0:T(8,128)S(1)}, u32[]{:S(2)}, u32[]{:S(2)}) collective-permute-start(f32[264,256]{1,0:T(8,128)S(1)} %pad_maximum_fusion.5), channel_id=1, source_target_pairs={{0,4},{2,6},{4,0},{6,2},{8,12},{10,14},{12,8},{14,10},{16,20},{18,... | collective-permute-start | bytes 811016 | tf_op jit(solution)/shard_map/ppermute | solution.py:44
  118.3 5.0 %collective-permute-done.15 = f32[264,256]{1,0:T(8,128)S(1)} collective-permute-done((f32[264,256]{1,0:T(8,128)S(1)}, f32[264,256]{1,0:T(8,128)S(1)}, u32[]{:S(2)}, u32[]{:S(2)}) %collective-permute-start.15) | collective-permute-done | bytes 270368 | tf_op jit(solution)/shard_map/ppermute | solution.py:44
  123.5 1.6 %collective-permute-start.16 = (f32[136,256]{1,0:T(8,128)S(1)}, f32[136,256]{1,0:T(8,128)S(1)}, u32[]{:S(2)}, u32[]{:S(2)}) collective-permute-start(f32[136,256]{1,0:T(8,128)S(1)} %pad_maximum_fusion.9), channel_id=1, source_target_pairs={{0,8},{2,10},{4,12},{6,14},{8,0},{10,2},{12,4},{14,6},{16,24},{18,... | collective-permute-start | bytes 417800 | tf_op jit(solution)/shard_map/ppermute | solution.py:44
  125.1 4.3 %collective-permute-done.16 = f32[136,256]{1,0:T(8,128)S(1)} collective-permute-done((f32[136,256]{1,0:T(8,128)S(1)}, f32[136,256]{1,0:T(8,128)S(1)}, u32[]{:S(2)}, u32[]{:S(2)}) %collective-permute-start.16) | collective-permute-done | bytes 139296 | tf_op jit(solution)/shard_map/ppermute | solution.py:44
  129.5 0.7 collective-permute-start.17
  130.3 5.3 %collective-permute-done.17 = f32[72,256]{1,0:T(8,128)S(1)} collective-permute-done((f32[72,256]{1,0:T(8,128)S(1)}, f32[72,256]{1,0:T(8,128)S(1)}, u32[]{:S(2)}, u32[]{:S(2)}) %collective-permute-start.17) | collective-permute-done | bytes 73760 | tf_op jit(solution)/shard_map/ppermute | solution.py:44
  135.6 1.1 collective-permute-done.18
  137.1 1.3 fusion.10
  138.4 0.9 copy.85
  139.3 0.9 copy.86
  140.2 0.7 fusion.24
  (148 shorter events, 8.1 us)
Async XLA Ops:
  0.6 29.6 %copy-start = (f32[64,64]{1,0:T(8,128)S(1)}, f32[64,64]{1,0:T(8,128)}, u32[]{:S(2)}) copy-start(f32[64,64]{1,0:T(8,128)} %param.9) | copy-start | bytes 49156
  1.6 12.7 %collective-permute-start = (bf16[1,64,256]{2,1,0:T(8,128)(2,1)S(1)}, bf16[1,64,256]{2,1,0:T(8,128)(2,1)S(1)}, u32[]{:S(2)}, u32[]{:S(2)}) collective-permute-start(bf16[1,64,256]{2,1,0:T(8,128)(2,1)S(1)} %get-tuple-element.53), channel_id=1, source_target_pairs={{0,16},{2,18},{4,20},{6,22},{8,24},{10,26},{12,28},{14,30},{16,0},... | collective-permute-start | bytes 98312 | tf_op jit(solution)/shard_map/ppermute | solution.py:44
  12.1 1.9 %copy-start.8 = (f32[1,384,256]{2,1,0:T(8,128)S(1)}, f32[1,384,256]{2,1,0:T(8,128)}, u32[]{:S(2)}) copy-start(f32[1,384,256]{2,1,0:T(8,128)} %param.7) | copy-start | bytes 1179652
  14.0 1.9 %copy-start.9 = (f32[1,64,256]{2,1,0:T(8,128)S(1)}, f32[1,64,256]{2,1,0:T(8,128)}, u32[]{:S(2)}) copy-start(f32[1,64,256]{2,1,0:T(8,128)} %param.8) | copy-start | bytes 196612
  14.0 6.2 %copy-start.13 = (f32[64,64]{1,0:T(8,128)S(1)}, f32[64,64]{1,0:T(8,128)}, u32[]{:S(2)}) copy-start(f32[64,64]{1,0:T(8,128)} %param.10) | copy-start | bytes 49156
  14.3 4.3 %collective-permute-start.1 = (bf16[2,64,256]{2,1,0:T(8,128)(2,1)S(1)}, bf16[2,64,256]{2,1,0:T(8,128)(2,1)S(1)}, u32[]{:S(2)}, u32[]{:S(2)}) collective-permute-start(bf16[2,64,256]{2,1,0:T(8,128)(2,1)S(1)} %maximum_bitcast_fusion), channel_id=1, source_target_pairs={{0,8},{2,10},{4,12},{6,14},{8,0},{10,2},{12,4},{14,6},{16,24},{18,... | collective-permute-start | bytes 196616 | tf_op jit(solution)/shard_map/ppermute | solution.py:44
  18.7 5.0 %collective-permute-start.2 = (bf16[2,2,64,256]{3,2,0,1:T(8,128)(2,1)S(1)}, bf16[2,2,64,256]{3,2,0,1:T(8,128)(2,1)S(1)}, u32[]{:S(2)}, u32[]{:S(2)}) collective-permute-start(bf16[2,2,64,256]{3,2,0,1:T(8,128)(2,1)S(1)} %pad_maximum_fusion.10), channel_id=1, source_target_pairs={{0,4},{2,6},{4,0},{6,2},{8,12},{10,14},{12,8},{14,10},{16,20},{18,... | collective-permute-start | bytes 393224 | tf_op jit(solution)/shard_map/ppermute | solution.py:44
  23.8 8.3 %collective-permute-start.3 = (bf16[2,2,2,64,256]{4,3,0,1,2:T(8,128)(2,1)S(1)}, bf16[2,2,2,64,256]{4,3,0,1,2:T(8,128)(2,1)}, u32[]{:S(2)}, u32[]{:S(2)}) collective-permute-start(bf16[2,2,2,64,256]{4,3,0,1,2:T(8,128)(2,1)S(1)} %pad_maximum_fusion.6), channel_id=1, source_target_pairs={{0,2},{2,0},{4,6},{6,4},{8,10},{10,8},{12,14},{14,12},{16,18},{18,... | collective-permute-start | bytes 786440 | tf_op jit(solution)/shard_map/ppermute | solution.py:44
  27.4 6.5 %copy-start.7 = (bf16[768,256]{0,1:T(8,128)(2,1)}, bf16[768,256]{0,1:T(8,128)(2,1)S(1)}, u32[]{:S(2)}) copy-start(bf16[768,256]{0,1:T(8,128)(2,1)S(1)} %all_gather.6) | copy-start | bytes 1179652
  34.0 0.8 copy-start.1
  34.0 1.0 copy-start.3
  38.3 17.0 %copy-start.2 = (f32[2,2,2,1,64,256]{5,4,3,2,1,0:T(8,128)S(1)}, f32[2,2,2,1,64,256]{5,4,3,2,1,0:T(8,128)}, u32[]{:S(2)}) copy-start(f32[2,2,2,1,64,256]{5,4,3,2,1,0:T(8,128)} %copy-done.1) | copy-start | bytes 1572868
  38.5 16.8 %copy-start.4 = (f32[2,2,2,1,64,256]{5,4,3,2,1,0:T(8,128)S(1)}, f32[2,2,2,1,64,256]{5,4,3,2,1,0:T(8,128)}, u32[]{:S(2)}) copy-start(f32[2,2,2,1,64,256]{5,4,3,2,1,0:T(8,128)} %copy-done.3) | copy-start | bytes 1572868
  41.1 14.2 %collective-permute-start.4 = (f32[520,256]{1,0:T(8,128)S(1)}, f32[520,256]{1,0:T(8,128)S(1)}, u32[]{:S(2)}, u32[]{:S(2)}) collective-permute-start(f32[520,256]{1,0:T(8,128)S(1)} %pad_maximum_fusion), channel_id=1, source_target_pairs={{0,2},{2,0},{4,6},{6,4},{8,10},{10,8},{12,14},{14,12},{16,18},{18,... | collective-permute-start | bytes 1597448 | tf_op jit(solution)/shard_map/ppermute | solution.py:44
  55.6 7.8 %collective-permute-start.5 = (f32[264,256]{1,0:T(8,128)S(1)}, f32[264,256]{1,0:T(8,128)S(1)}, u32[]{:S(2)}, u32[]{:S(2)}) collective-permute-start(f32[264,256]{1,0:T(8,128)S(1)} %pad_maximum_fusion.4), channel_id=1, source_target_pairs={{0,4},{2,6},{4,0},{6,2},{8,12},{10,14},{12,8},{14,10},{16,20},{18,... | collective-permute-start | bytes 811016 | tf_op jit(solution)/shard_map/ppermute | solution.py:44
  64.1 5.4 %collective-permute-start.6 = (f32[136,256]{1,0:T(8,128)}, f32[136,256]{1,0:T(8,128)}, u32[]{:S(2)}, u32[]{:S(2)}) collective-permute-start(f32[136,256]{1,0:T(8,128)} %pad_maximum_fusion.8), channel_id=1, source_target_pairs={{0,8},{2,10},{4,12},{6,14},{8,0},{10,2},{12,4},{14,6},{16,24},{18,... | collective-permute-start | bytes 417800 | tf_op jit(solution)/shard_map/ppermute | solution.py:44
  71.2 5.3 %collective-permute-start.7 = (f32[72,256]{1,0:T(8,128)S(1)}, f32[72,256]{1,0:T(8,128)S(1)}, u32[]{:S(2)}, u32[]{:S(2)}) collective-permute-start(f32[72,256]{1,0:T(8,128)S(1)} %pad_maximum_fusion.12), channel_id=1, source_target_pairs={{0,16},{2,18},{4,20},{6,22},{8,24},{10,26},{12,28},{14,30},{16,0},... | collective-permute-start | bytes 221192 | tf_op jit(solution)/shard_map/ppermute | solution.py:44
  72.3 7.1 %collective-permute-start.9 = (bf16[384,256]{0,1:T(8,128)(2,1)}, bf16[384,256]{0,1:T(8,128)(2,1)S(1)}, u32[]{:S(2)}, u32[]{:S(2)}) collective-permute-start(bf16[384,256]{0,1:T(8,128)(2,1)} %select_convert_fusion.1), channel_id=1, source_target_pairs={{0,1},{1,0},{2,3},{3,2},{4,5},{5,4},{6,7},{7,6},{8,9},{9,8},{10,11... | collective-permute-start | bytes 589832 | tf_op jit(solution)/shard_map/ppermute | solution.py:44
  76.5 1.1 collective-permute-start.8
  77.6 0.6 copy-start.14
  79.0 5.4 %collective-permute-start.10 = (bf16[1,64,256]{2,1,0:T(8,128)(2,1)}, bf16[1,64,256]{2,1,0:T(8,128)(2,1)S(1)}, u32[]{:S(2)}, u32[]{:S(2)}) collective-permute-start(bf16[1,64,256]{2,1,0:T(8,128)(2,1)} %get-tuple-element.27), channel_id=1, source_target_pairs={{0,16},{2,18},{4,20},{6,22},{8,24},{10,26},{12,28},{14,30},{16,0},... | collective-permute-start | bytes 98312 | tf_op jit(solution)/shard_map/ppermute | solution.py:44
  79.4 0.7 copy-start.12
  85.2 4.3 %collective-permute-start.11 = (bf16[2,64,256]{2,1,0:T(8,128)(2,1)S(1)}, bf16[2,64,256]{2,1,0:T(8,128)(2,1)S(1)}, u32[]{:S(2)}, u32[]{:S(2)}) collective-permute-start(bf16[2,64,256]{2,1,0:T(8,128)(2,1)S(1)} %maximum_bitcast_fusion.1), channel_id=1, source_target_pairs={{0,8},{2,10},{4,12},{6,14},{8,0},{10,2},{12,4},{14,6},{16,24},{18,... | collective-permute-start | bytes 196616 | tf_op jit(solution)/shard_map/ppermute | solution.py:44
  89.5 7.0 %copy-start.10 = (bf16[384,256]{0,1:T(8,128)(2,1)S(1)}, bf16[384,256]{0,1:T(8,128)(2,1)}, u32[]{:S(2)}) copy-start(bf16[384,256]{0,1:T(8,128)(2,1)} %get-tuple-element.24) | copy-start | bytes 589828
  89.6 5.0 %collective-permute-start.12 = (bf16[2,2,64,256]{3,2,0,1:T(8,128)(2,1)S(1)}, bf16[2,2,64,256]{3,2,0,1:T(8,128)(2,1)S(1)}, u32[]{:S(2)}, u32[]{:S(2)}) collective-permute-start(bf16[2,2,64,256]{3,2,0,1:T(8,128)(2,1)S(1)} %pad_maximum_fusion.11), channel_id=1, source_target_pairs={{0,4},{2,6},{4,0},{6,2},{8,12},{10,14},{12,8},{14,10},{16,20},{18,... | collective-permute-start | bytes 393224 | tf_op jit(solution)/shard_map/ppermute | solution.py:44
  91.3 11.7 %copy-start.5 = (f32[384,4,64]{0,2,1:T(8,128)}, f32[384,4,64]{0,2,1:T(8,128)S(1)}, u32[]{:S(2)}) copy-start(f32[384,4,64]{0,2,1:T(8,128)S(1)} %fusion.33) | copy-start | bytes 1179652
  95.3 6.7 %collective-permute-start.13 = (bf16[2,2,2,64,256]{4,3,0,1,2:T(8,128)(2,1)}, bf16[2,2,2,64,256]{4,3,0,1,2:T(8,128)(2,1)}, u32[]{:S(2)}, u32[]{:S(2)}) collective-permute-start(bf16[2,2,2,64,256]{4,3,0,1,2:T(8,128)(2,1)} %pad_maximum_fusion.7), channel_id=1, source_target_pairs={{0,2},{2,0},{4,6},{6,4},{8,10},{10,8},{12,14},{14,12},{16,18},{18,... | collective-permute-start | bytes 786440 | tf_op jit(solution)/shard_map/ppermute | solution.py:44
  105.5 11.1 %collective-permute-start.14 = (f32[520,256]{1,0:T(8,128)S(1)}, f32[520,256]{1,0:T(8,128)S(1)}, u32[]{:S(2)}, u32[]{:S(2)}) collective-permute-start(f32[520,256]{1,0:T(8,128)S(1)} %pad_maximum_fusion.1), channel_id=1, source_target_pairs={{0,2},{2,0},{4,6},{6,4},{8,10},{10,8},{12,14},{14,12},{16,18},{18,... | collective-permute-start | bytes 1597448 | tf_op jit(solution)/shard_map/ppermute | solution.py:44
  116.8 6.5 %collective-permute-start.15 = (f32[264,256]{1,0:T(8,128)S(1)}, f32[264,256]{1,0:T(8,128)S(1)}, u32[]{:S(2)}, u32[]{:S(2)}) collective-permute-start(f32[264,256]{1,0:T(8,128)S(1)} %pad_maximum_fusion.5), channel_id=1, source_target_pairs={{0,4},{2,6},{4,0},{6,2},{8,12},{10,14},{12,8},{14,10},{16,20},{18,... | collective-permute-start | bytes 811016 | tf_op jit(solution)/shard_map/ppermute | solution.py:44
  123.4 13.4 %copy-start.15 = (f32[8]{0:T(128)S(1)}, f32[8]{0:T(128)}, u32[]{:S(2)}) copy-start(f32[8]{0:T(128)} %copy-done.14) | copy-start | bytes 100
  123.4 13.7 %copy-start.6 = (f32[384,4,64]{0,2,1:T(8,128)S(1)}, f32[384,4,64]{0,2,1:T(8,128)}, u32[]{:S(2)}) copy-start(f32[384,4,64]{0,2,1:T(8,128)} %copy-done.5) | copy-start | bytes 1179652
  123.5 5.9 %collective-permute-start.16 = (f32[136,256]{1,0:T(8,128)S(1)}, f32[136,256]{1,0:T(8,128)S(1)}, u32[]{:S(2)}, u32[]{:S(2)}) collective-permute-start(f32[136,256]{1,0:T(8,128)S(1)} %pad_maximum_fusion.9), channel_id=1, source_target_pairs={{0,8},{2,10},{4,12},{6,14},{8,0},{10,2},{12,4},{14,6},{16,24},{18,... | collective-permute-start | bytes 417800 | tf_op jit(solution)/shard_map/ppermute | solution.py:44
  129.5 6.1 %collective-permute-start.17 = (f32[72,256]{1,0:T(8,128)S(1)}, f32[72,256]{1,0:T(8,128)S(1)}, u32[]{:S(2)}, u32[]{:S(2)}) collective-permute-start(f32[72,256]{1,0:T(8,128)S(1)} %pad_maximum_fusion.13), channel_id=1, source_target_pairs={{0,16},{2,18},{4,20},{6,22},{8,24},{10,26},{12,28},{14,30},{16,0},... | collective-permute-start | bytes 221192 | tf_op jit(solution)/shard_map/ppermute | solution.py:44
  130.3 6.9 %collective-permute-start.19 = (bf16[384,256]{0,1:T(8,128)(2,1)S(1)}, bf16[384,256]{0,1:T(8,128)(2,1)S(1)}, u32[]{:S(2)}, u32[]{:S(2)}) collective-permute-start(bf16[384,256]{0,1:T(8,128)(2,1)S(1)} %select_convert_fusion), channel_id=1, source_target_pairs={{0,1},{1,0},{2,3},{3,2},{4,5},{5,4},{6,7},{7,6},{8,9},{9,8},{10,11... | collective-permute-start | bytes 589832 | tf_op jit(solution)/shard_map/ppermute | solution.py:44
  135.6 1.1 collective-permute-start.18
  138.4 1.8 %copy-start.11 = (f32[64,256]{1,0:T(8,128)S(1)}, f32[64,256]{1,0:T(8,128)}, u32[]{:S(2)}) copy-start(f32[64,256]{1,0:T(8,128)} %get-tuple-element.29) | copy-start | bytes 196612

commit v4 on v3

--- a/solution.py
+++ b/solution.py
@@ -69,10 +69,9 @@
         if extra is None:
             buf = keep + swap_with(send, axis, size, bit).astype(jnp.float32)
         else:
-            message = jnp.concatenate([send.reshape(-1, width), extra])
-            got = swap_with(message, axis, size, bit)
-            buf = keep + got[: -extra.shape[0]].reshape(keep.shape)
-            extra = extra + got[-extra.shape[0] :]
+            got, got_extra = swap_with((send, extra), axis, size, bit)
+            buf = keep + got
+            extra = extra + got_extra
         left.remove(bit)
     return buf.reshape(rows, width), extra
 

time: 142 us -> 142 us (level)
  waiting for transfers between devices: 71.4 us -> 56.9 us
  starting transfers between devices: 20.2 us -> 33.5 us
  other arithmetic: 21.6 us -> 26.5 us
  local copies, waits for them, and re-layouts: 11 us -> 7.92 us
    ppermute x20 -> x28, waiting for transfers between devices: 71.4 us -> 56.9 us  [swap_with(): return lax.ppermute(value, axis, pairs)]
    ppermute x20 -> x28, starting transfers between devices: 20.2 us -> 33.5 us  [swap_with(): return lax.ppermute(value, axis, pairs)]
    unnamed x37 -> x27, local copies, waits for them, and re-layouts: 6.06 us -> 3.95 us
    select_n x8, other arithmetic: 0.27 us -> 2.28 us  [halve_sum(): send = jnp.where(upper, low, high).astype(send_type)]
    concatenate x8 -> x0, other arithmetic: 1.85 us -> none  [halve_sum(): message = jnp.concatenate([send.reshape(-1, width), extra])]
    add x12, other arithmetic: 1.1 us -> 2.79 us  [the longest x6 2.76 us: halve_sum(): buf = keep + got]
  transfers between devices with their start and end apart: 20 -> 28, of which waited for: 16 -> 19; matrix products, arithmetic and copies ran while one was open for 14% -> 23% of each run, Pallas kernels for 0% -> 0%
where the time goes in v4:
time: 142 us
  waiting for transfers between devices  56.9 us (40%)
  starting transfers between devices  33.5 us (24%)
  other arithmetic  26.5 us (19%)
  matrix products  10.8 us (8%)
  local copies, waits for them, and re-layouts  7.92 us (6%)
  blocking collectives  4.33 us (3%)
  between operations  1.75 us (1%)
    ppermute x28, waiting for transfers between devices, swap_with(): return lax.ppermute(value, axis, pairs)  56.9 us
    ppermute x28, starting transfers between devices, swap_with(): return lax.ppermute(value, axis, pairs)  33.5 us
    another operation x14, other arithmetic, double_gather(): buf = jnp.stack([first, second], axis=step)  4.51 us
    all_gather x2, blocking collectives, user_range_of(): lax.all_gather(user_vec.astype(jnp.bfloat16), 'item', axis=0, tiled=True)  4.33 us
    reduce_sum x14, other arithmetic, per_draw(): return jnp.sum(product, axis=(0, 2))  3.96 us
    unnamed x27, local copies, waits for them, and re-layouts  3.95 us
    dot_general x2, matrix products, cross_parts(): jnp.dot(counts_bf, item_range, preferred_element_type=jnp.float32)  3.48 us
    dot_general x4, matrix products, prior_term(): mixed = jnp.einsum('nde,ef->ndf', grouped, prior_mat, precision=top_prec)  2.87 us
  transfers between devices with their start and end apart: 28, of which 19 were waited for; matrix products, arithmetic and copies ran while one was open for 23% of the time, Pallas kernels for 0%

profile of v4, /device:TPU:0, one launch (start us, length us, event | category | flops | bytes accessed | tf_op | source)
XLA Modules:
  0.0 141.7 jit_solution(16712697393276099799)
XLA Ops:
  0.6 0.9 multiply_reduce_fusion.6
  1.6 4.1 %collective-permute-start = (bf16[1,64,256]{2,1,0:T(8,128)(2,1)S(1)}, bf16[1,64,256]{2,1,0:T(8,128)(2,1)S(1)}, u32[]{:S(2)}, u32[]{:S(2)}) collective-permute-start(bf16[1,64,256]{2,1,0:T(8,128)(2,1)S(1)} %get-tuple-element.53), channel_id=1, source_target_pairs={{0,16},{2,18},{4,20},{6,22},{8,24},{10,26},{12,28},{14,30},{16,0},... | collective-permute-start | bytes 98312 | tf_op jit(solution)/shard_map/ppermute | solution.py:44
  5.7 0.8 slice_bitcast_fusion.1
  7.1 2.2 %convert_bitcast_fusion = bf16[12,256,256]{2,1,0:T(8,128)(2,1)S(1)} fusion(s32[1,1,12,256,256]{4,3,2,1,0:T(8,128)} %param.11), kind=kLoop, calls=%fused_computation.6 | loop fusion | flops 786432 | bytes 4718592 | tf_op jit(solution)/shard_map/convert_element_type | solution.py:107
  9.3 2.8 %bitcast_convert_fusion = (bf16[3,256,4,256]{3,2,1,0:T(4,128)(2,1)}, f32[3,4,256,256]{3,1,2,0:T(4,128)S(1)}) fusion(bf16[12,256,256]{2,1,0:T(8,128)(2,1)S(1)} %convert_bitcast_fusion, pred[12,4]{0,1:T(4,128)(4,1)S(1)} %fusion.42, pred[12,3]{0,1:T(4,128)(4,1)S(1)} %fusion.41), kind=kOutput, calls=%fused_computation.2 | convolution fusion | flops 19660944 | bytes 6291540 | tf_op jit(solution)/shard_map/trc,tij->ricj/dot_general | solution.py:104
  12.1 1.9 %bitcast_reduce_fusion = (f32[4,256]{1,0:T(4,128)S(1)}, f32[3,256]{1,0:T(4,128)S(1)}) fusion(f32[3,4,256,256]{3,1,2,0:T(4,128)S(1)} %get-tuple-element.59), kind=kLoop, calls=%fused_computation | loop fusion | flops 1571072 | bytes 3152896 | tf_op jit(solution)/shard_map/reduce_sum | solution.py:111
  14.3 1.6 %collective-permute-start.1 = (bf16[2,64,256]{2,1,0:T(8,128)(2,1)S(1)}, bf16[2,64,256]{2,1,0:T(8,128)(2,1)S(1)}, u32[]{:S(2)}, u32[]{:S(2)}) collective-permute-start(bf16[2,64,256]{2,1,0:T(8,128)(2,1)S(1)} %maximum_bitcast_fusion), channel_id=1, source_target_pairs={{0,8},{2,10},{4,12},{6,14},{8,0},{10,2},{12,4},{14,6},{16,24},{18,... | collective-permute-start | bytes 196616 | tf_op jit(solution)/shard_map/ppermute | solution.py:44
  16.1 2.5 %collective-permute-done.1 = bf16[2,64,256]{2,1,0:T(8,128)(2,1)S(1)} collective-permute-done((bf16[2,64,256]{2,1,0:T(8,128)(2,1)S(1)}, bf16[2,64,256]{2,1,0:T(8,128)(2,1)S(1)}, u32[]{:S(2)}, u32[]{:S(2)}) %collective-permute-start.1) | collective-permute-done | bytes 65568 | tf_op jit(solution)/shard_map/ppermute | solution.py:44
  18.7 1.6 %collective-permute-start.2 = (bf16[2,2,64,256]{3,2,0,1:T(8,128)(2,1)S(1)}, bf16[2,2,64,256]{3,2,0,1:T(8,128)(2,1)S(1)}, u32[]{:S(2)}, u32[]{:S(2)}) collective-permute-start(bf16[2,2,64,256]{3,2,0,1:T(8,128)(2,1)S(1)} %pad_maximum_fusion.4), channel_id=1, source_target_pairs={{0,4},{2,6},{4,0},{6,2},{8,12},{10,14},{12,8},{14,10},{16,20},{18,... | collective-permute-start | bytes 393224 | tf_op jit(solution)/shard_map/ppermute | solution.py:44
  20.7 3.0 %collective-permute-done.2 = bf16[2,2,64,256]{3,2,0,1:T(8,128)(2,1)S(1)} collective-permute-done((bf16[2,2,64,256]{3,2,0,1:T(8,128)(2,1)S(1)}, bf16[2,2,64,256]{3,2,0,1:T(8,128)(2,1)S(1)}, u32[]{:S(2)}, u32[]{:S(2)}) %collective-permute-start.2) | collective-permute-done | bytes 131104 | tf_op jit(solution)/shard_map/ppermute | solution.py:44
  23.8 1.6 %collective-permute-start.3 = (bf16[2,2,2,64,256]{4,3,0,1,2:T(8,128)(2,1)S(1)}, bf16[2,2,2,64,256]{4,3,0,1,2:T(8,128)(2,1)}, u32[]{:S(2)}, u32[]{:S(2)}) collective-permute-start(bf16[2,2,2,64,256]{4,3,0,1,2:T(8,128)(2,1)S(1)} %pad_maximum_fusion.2), channel_id=1, source_target_pairs={{0,2},{2,0},{4,6},{6,4},{8,10},{10,8},{12,14},{14,12},{16,18},{18,... | collective-permute-start | bytes 786440 | tf_op jit(solution)/shard_map/ppermute | solution.py:44
  25.3 2.1 %all_gather.6 = bf16[768,256]{0,1:T(8,128)(2,1)S(1)} all-gather(bf16[384,256]{0,1:T(8,128)(2,1)S(1)} %bitcast_convert_fusion.1), channel_id=1, replica_groups=mesh['user'=16,'item'=2] {'item'}, dimensions={0}, use_global_device_ids=true | all-gather | bytes 589824 | tf_op jit(solution)/shard_map/all_gather | solution.py:124
  27.4 1.9 %copy.77 = bf16[96,8,4,256]{3,1,2,0:T(8,128)(2,1)S(1)} copy(bf16[96,8,4,256]{3,2,1,0:T(4,128)(2,1)} %bitcast.228) | data formatting | bytes 3145728
  30.2 1.8 %multiply_reduce_fusion.1 = (f32[4]{0:T(128)}, f32[384,4,64]{0,2,1:T(8,128)}) fusion(f32[384,4,64]{0,2,1:T(8,128)S(1)} %bitcast.223, f32[64,64]{1,0:T(8,128)S(1)} %copy-done), kind=kOutput, calls=%fused_computation.47 | convolution fusion | flops 75694080 | bytes 802832 | tf_op jit(solution)/shard_map/nde,ef->ndf/dot_general | solution.py:22
  32.0 1.0 select_bitcast_fusion.7
  33.1 0.8 fusion.3
  33.9 1.1 fusion.48
  35.0 2.1 %select_bitcast_fusion.1 = f32[2,2,2,64,256]{4,3,0,1,2:T(8,128)} fusion(f32[2,2,2,1,64,256]{5,4,3,2,1,0:T(8,128)} %get-tuple-element.33, f32[2,2,2,1,64,256]{5,4,3,2,1,0:T(8,128)} %get-tuple-element.32, pred[]{:T(512)S(6)} %eq.74), kind=kLoop, calls=%fused_computation.28 | loop fusion | flops 131072 | bytes 1572865 | tf_op jit(solution)/shard_map/jit(_where)/select_n | solution.py:68
  38.3 1.7 %fusion.5 = (f32[256]{0:T(256)S(1)}, f32[768,256]{0,1:T(8,128)S(1)}) fusion(bf16[768,256]{0,1:T(8,128)(2,1)} %copy-done.3, f32[768]{0:T(1024)S(1)} %mul.189, bf16[768,1024]{1,0:T(8,128)(2,1)S(1)} %bitcast.220, bf16[1024,256]{1,0:T(8,128)(2,1)S(1)} %bitcast.225), kind=kOutput, calls=%fused_computation.21 | convolution fusion | flops 403635968 | bytes 3280896 | tf_op jit(solution)/shard_map/dot_general | solution.py:115
  40.3 0.7 multiply_add_fusion.1
  41.0 0.7 maximum_bitcast_fusion.2
  41.7 1.5 %collective-permute-start.4 = (f32[8,256]{1,0:T(8,128)S(1)}, f32[8,256]{1,0:T(8,128)S(1)}, u32[]{:S(2)}, u32[]{:S(2)}) collective-permute-start(f32[8,256]{1,0:T(8,128)S(1)} %pad.7), channel_id=1, source_target_pairs={{0,2},{2,0},{4,6},{6,4},{8,10},{10,8},{12,14},{14,12},{16,18},{18,... | collective-permute-start | bytes 24584 | tf_op jit(solution)/shard_map/ppermute | solution.py:44
  43.4 8.1 %collective-permute-done.4 = f32[8,256]{1,0:T(8,128)S(1)} collective-permute-done((f32[8,256]{1,0:T(8,128)S(1)}, f32[8,256]{1,0:T(8,128)S(1)}, u32[]{:S(2)}, u32[]{:S(2)}) %collective-permute-start.4) | collective-permute-done | bytes 8224 | tf_op jit(solution)/shard_map/ppermute | solution.py:44
  51.5 1.5 %collective-permute-start.5 = (f32[8,256]{1,0:T(8,128)S(1)}, f32[8,256]{1,0:T(8,128)S(1)}, u32[]{:S(2)}, u32[]{:S(2)}) collective-permute-start(f32[8,256]{1,0:T(8,128)S(1)} %pad_add_fusion.1), channel_id=1, source_target_pairs={{0,4},{2,6},{4,0},{6,2},{8,12},{10,14},{12,8},{14,10},{16,20},{18,... | collective-permute-start | bytes 24584 | tf_op jit(solution)/shard_map/ppermute | solution.py:44
  53.0 1.5 %bitcast_add_fusion.1 = f32[2,2,2,64,256]{4,3,0,1,2:T(8,128)S(1)} fusion(f32[2,2,2,64,256]{4,3,0,1,2:T(8,128)} %collective-permute-done.10, f32[2,2,2,1,64,256]{5,4,3,2,1,0:T(8,128)} %get-tuple-element.33, f32[2,2,2,1,64,256]{5,4,3,2,1,0:T(8,128)} %get-tuple-element.32, pred[]{:T(512)S(6)} %eq.74), kind=kLoop, calls=%fused_computation.26 | loop fusion | flops 262144 | bytes 2097153 | tf_op jit(solution)/shard_map/add | solution.py:73
  55.1 1.6 %collective-permute-start.6 = (f32[8,256]{1,0:T(8,128)S(1)}, f32[8,256]{1,0:T(8,128)S(1)}, u32[]{:S(2)}, u32[]{:S(2)}) collective-permute-start(f32[8,256]{1,0:T(8,128)S(1)} %fusion.60), channel_id=1, source_target_pairs={{0,8},{2,10},{4,12},{6,14},{8,0},{10,2},{12,4},{14,6},{16,24},{18,... | collective-permute-start | bytes 24584 | tf_op jit(solution)/shard_map/ppermute | solution.py:44
  56.7 0.7 select_convert_fusion.1
  57.5 1.4 collective-permute-done.6
  59.2 2.7 %collective-permute-done.11 = f32[2,2,64,256]{3,2,0,1:T(8,128)S(1)} collective-permute-done((f32[2,2,64,256]{3,2,0,1:T(8,128)S(1)}, f32[2,2,64,256]{3,2,0,1:T(8,128)S(1)}, u32[]{:S(2)}, u32[]{:S(2)}) %collective-permute-start.11) | collective-permute-done | bytes 262176 | tf_op jit(solution)/shard_map/ppermute | solution.py:44
  62.0 1.6 %collective-permute-start.12 = (f32[2,64,256]{2,1,0:T(8,128)S(1)}, f32[2,64,256]{2,1,0:T(8,128)S(1)}, u32[]{:S(2)}, u32[]{:S(2)}) collective-permute-start(f32[2,64,256]{2,1,0:T(8,128)S(1)} %select_bitcast_fusion.11), channel_id=1, source_target_pairs={{0,8},{2,10},{4,12},{6,14},{8,0},{10,2},{12,4},{14,6},{16,24},{18,... | collective-permute-start | bytes 393224 | tf_op jit(solution)/shard_map/ppermute | solution.py:44
  63.6 1.1 collective-permute-done.8
  64.8 2.3 %collective-permute-done.12 = f32[2,64,256]{2,1,0:T(8,128)S(1)} collective-permute-done((f32[2,64,256]{2,1,0:T(8,128)S(1)}, f32[2,64,256]{2,1,0:T(8,128)S(1)}, u32[]{:S(2)}, u32[]{:S(2)}) %collective-permute-start.12) | collective-permute-done | bytes 131104 | tf_op jit(solution)/shard_map/ppermute | solution.py:44
  67.7 4.6 %collective-permute-done.13 = f32[64,256]{1,0:T(8,128)S(1)} collective-permute-done((f32[64,256]{1,0:T(8,128)S(1)}, f32[64,256]{1,0:T(8,128)S(1)}, u32[]{:S(2)}, u32[]{:S(2)}) %collective-permute-start.13) | collective-permute-done | bytes 65568 | tf_op jit(solution)/shard_map/ppermute | solution.py:44
  73.3 2.0 %fusion.45 = (bf16[384,256]{0,1:T(8,128)(2,1)}, f32[384,256]{0,1:T(8,128)S(1)}, f32[384,256]{0,1:T(8,128)}) fusion(f32[256]{0:T(256)S(1)} %mul.198, f32[1,384,256]{1,2,0:T(8,128)S(1)} %copy.47, bf16[384,256]{0,1:T(8,128)(2,1)} %collective-permute-done.9, f32[768,256]{0,1:T(8,128)S(1)} %get-tuple-element.61, pred[]{:T(512)S(6)} %eq.78, ...), kind=kLoop, calls=%fused_computation.137 | loop fusion | flops 786432 | bytes 2753537 | tf_op jit(solution)/shard_map/convert_element_type | solution.py:124
  75.3 2.5 %collective-permute-done.14 = bf16[1,64,256]{2,1,0:T(8,128)(2,1)S(1)} collective-permute-done((bf16[1,64,256]{2,1,0:T(8,128)(2,1)S(1)}, bf16[1,64,256]{2,1,0:T(8,128)(2,1)S(1)}, u32[]{:S(2)}, u32[]{:S(2)}) %collective-permute-start.14) | collective-permute-done | bytes 32800 | tf_op jit(solution)/shard_map/ppermute | solution.py:44
  77.9 2.2 %collective-permute-start.15 = (bf16[2,64,256]{2,1,0:T(8,128)(2,1)S(1)}, bf16[2,64,256]{2,1,0:T(8,128)(2,1)S(1)}, u32[]{:S(2)}, u32[]{:S(2)}) collective-permute-start(bf16[2,64,256]{2,1,0:T(8,128)(2,1)S(1)} %maximum_bitcast_fusion.1), channel_id=1, source_target_pairs={{0,8},{2,10},{4,12},{6,14},{8,0},{10,2},{12,4},{14,6},{16,24},{18,... | collective-permute-start | bytes 196616 | tf_op jit(solution)/shard_map/ppermute | solution.py:44
  80.6 1.7 %collective-permute-done.15 = bf16[2,64,256]{2,1,0:T(8,128)(2,1)S(1)} collective-permute-done((bf16[2,64,256]{2,1,0:T(8,128)(2,1)S(1)}, bf16[2,64,256]{2,1,0:T(8,128)(2,1)S(1)}, u32[]{:S(2)}, u32[]{:S(2)}) %collective-permute-start.15) | collective-permute-done | bytes 65568 | tf_op jit(solution)/shard_map/ppermute | solution.py:44
  85.0 2.3 %all_gather.7 = bf16[768,256]{0,1:T(8,128)(2,1)S(1)} all-gather(bf16[384,256]{0,1:T(8,128)(2,1)S(1)} %copy-done.7), channel_id=1, replica_groups=mesh['user'=16,'item'=2] {'item'}, dimensions={0}, use_global_device_ids=true | all-gather | bytes 589824 | tf_op jit(solution)/shard_map/all_gather | solution.py:124
  87.4 0.9 collective-permute-done.16
  88.3 0.9 select_bitcast_fusion.10
  89.3 0.7 pad_maximum_fusion.3
  92.1 5.7 %collective-permute-done.17 = bf16[2,2,2,64,256]{4,3,0,1,2:T(8,128)(2,1)} collective-permute-done((bf16[2,2,2,64,256]{4,3,0,1,2:T(8,128)(2,1)}, bf16[2,2,2,64,256]{4,3,0,1,2:T(8,128)(2,1)}, u32[]{:S(2)}, u32[]{:S(2)}) %collective-permute-start.17) | collective-permute-done | bytes 262176 | tf_op jit(solution)/shard_map/ppermute | solution.py:44
  97.8 1.0 select_bitcast_fusion.4
  98.9 0.8 fusion.4
  99.7 1.7 %fusion.6 = (f32[256]{0:T(256)S(1)}, f32[768,256]{0,1:T(8,128)S(1)}) fusion(bf16[768,256]{0,1:T(8,128)(2,1)} %copy-done.4, f32[768]{0:T(1024)S(1)} %mul.189, bf16[768,1024]{1,0:T(8,128)(2,1)S(1)} %bitcast.222, bf16[1024,256]{1,0:T(8,128)(2,1)S(1)} %bitcast.227), kind=kOutput, calls=%fused_computation.22 | convolution fusion | flops 403635968 | bytes 3280896 | tf_op jit(solution)/shard_map/dot_general | solution.py:115
  102.7 1.5 %collective-permute-start.18 = (f32[8,256]{1,0:T(8,128)S(1)}, f32[8,256]{1,0:T(8,128)S(1)}, u32[]{:S(2)}, u32[]{:S(2)}) collective-permute-start(f32[8,256]{1,0:T(8,128)S(1)} %pad.8), channel_id=1, source_target_pairs={{0,2},{2,0},{4,6},{6,4},{8,10},{10,8},{12,14},{14,12},{16,18},{18,... | collective-permute-start | bytes 24584 | tf_op jit(solution)/shard_map/ppermute | solution.py:44
  104.2 9.8 %collective-permute-done.18 = f32[8,256]{1,0:T(8,128)S(1)} collective-permute-done((f32[8,256]{1,0:T(8,128)S(1)}, f32[8,256]{1,0:T(8,128)S(1)}, u32[]{:S(2)}, u32[]{:S(2)}) %collective-permute-start.18) | collective-permute-done | bytes 8224 | tf_op jit(solution)/shard_map/ppermute | solution.py:44
  114.0 2.6 %collective-permute-start.19 = (f32[8,256]{1,0:T(8,128)S(1)}, f32[8,256]{1,0:T(8,128)S(1)}, u32[]{:S(2)}, u32[]{:S(2)}) collective-permute-start(f32[8,256]{1,0:T(8,128)S(1)} %pad_add_fusion), channel_id=1, source_target_pairs={{0,4},{2,6},{4,0},{6,2},{8,12},{10,14},{12,8},{14,10},{16,20},{18,... | collective-permute-start | bytes 24584 | tf_op jit(solution)/shard_map/ppermute | solution.py:44
  116.7 1.6 %collective-permute-done.19 = f32[8,256]{1,0:T(8,128)S(1)} collective-permute-done((f32[8,256]{1,0:T(8,128)S(1)}, f32[8,256]{1,0:T(8,128)S(1)}, u32[]{:S(2)}, u32[]{:S(2)}) %collective-permute-start.19) | collective-permute-done | bytes 8224 | tf_op jit(solution)/shard_map/ppermute | solution.py:44
  118.3 2.0 %collective-permute-start.20 = (f32[8,256]{1,0:T(8,128)S(1)}, f32[8,256]{1,0:T(8,128)S(1)}, u32[]{:S(2)}, u32[]{:S(2)}) collective-permute-start(f32[8,256]{1,0:T(8,128)S(1)} %fusion.59), channel_id=1, source_target_pairs={{0,8},{2,10},{4,12},{6,14},{8,0},{10,2},{12,4},{14,6},{16,24},{18,... | collective-permute-start | bytes 24584 | tf_op jit(solution)/shard_map/ppermute | solution.py:44
  120.3 1.6 %collective-permute-done.20 = f32[8,256]{1,0:T(8,128)S(1)} collective-permute-done((f32[8,256]{1,0:T(8,128)S(1)}, f32[8,256]{1,0:T(8,128)S(1)}, u32[]{:S(2)}, u32[]{:S(2)}) %collective-permute-start.20) | collective-permute-done | bytes 8224 | tf_op jit(solution)/shard_map/ppermute | solution.py:44
  122.0 1.0 collective-permute-start.21
  123.0 1.1 bitcast_add_fusion
  124.2 1.1 collective-permute-start.25
  125.3 0.7 select_convert_fusion
  126.5 1.1 collective-permute-done.22
  127.6 3.0 %collective-permute-done.25 = f32[2,2,64,256]{3,2,0,1:T(8,128)S(1)} collective-permute-done((f32[2,2,64,256]{3,2,0,1:T(8,128)S(1)}, f32[2,2,64,256]{3,2,0,1:T(8,128)S(1)}, u32[]{:S(2)}, u32[]{:S(2)}) %collective-permute-start.25) | collective-permute-done | bytes 262176 | tf_op jit(solution)/shard_map/ppermute | solution.py:44
  130.7 2.1 %collective-permute-start.26 = (f32[2,64,256]{2,1,0:T(8,128)S(1)}, f32[2,64,256]{2,1,0:T(8,128)S(1)}, u32[]{:S(2)}, u32[]{:S(2)}) collective-permute-start(f32[2,64,256]{2,1,0:T(8,128)S(1)} %select_bitcast_fusion.8), channel_id=1, source_target_pairs={{0,8},{2,10},{4,12},{6,14},{8,0},{10,2},{12,4},{14,6},{16,24},{18,... | collective-permute-start | bytes 393224 | tf_op jit(solution)/shard_map/ppermute | solution.py:44
  133.2 2.6 %collective-permute-done.26 = f32[2,64,256]{2,1,0:T(8,128)S(1)} collective-permute-done((f32[2,64,256]{2,1,0:T(8,128)S(1)}, f32[2,64,256]{2,1,0:T(8,128)S(1)}, u32[]{:S(2)}, u32[]{:S(2)}) %collective-permute-start.26) | collective-permute-done | bytes 131104 | tf_op jit(solution)/shard_map/ppermute | solution.py:44
  135.8 2.1 %collective-permute-start.27 = (f32[64,256]{1,0:T(8,128)S(1)}, f32[64,256]{1,0:T(8,128)S(1)}, u32[]{:S(2)}, u32[]{:S(2)}) collective-permute-start(f32[64,256]{1,0:T(8,128)S(1)} %select_bitcast_fusion.14), channel_id=1, source_target_pairs={{0,16},{2,18},{4,20},{6,22},{8,24},{10,26},{12,28},{14,30},{16,0},... | collective-permute-start | bytes 196616 | tf_op jit(solution)/shard_map/ppermute | solution.py:44
  137.9 1.3 fusion.10
  139.2 0.9 copy.65
  140.1 0.9 copy.66
  141.0 0.7 fusion.24
  (134 shorter events, 14.2 us)
Async XLA Ops:
  0.6 29.6 %copy-start = (f32[64,64]{1,0:T(8,128)S(1)}, f32[64,64]{1,0:T(8,128)}, u32[]{:S(2)}) copy-start(f32[64,64]{1,0:T(8,128)} %param.9) | copy-start | bytes 49156
  1.6 12.7 %collective-permute-start = (bf16[1,64,256]{2,1,0:T(8,128)(2,1)S(1)}, bf16[1,64,256]{2,1,0:T(8,128)(2,1)S(1)}, u32[]{:S(2)}, u32[]{:S(2)}) collective-permute-start(bf16[1,64,256]{2,1,0:T(8,128)(2,1)S(1)} %get-tuple-element.53), channel_id=1, source_target_pairs={{0,16},{2,18},{4,20},{6,22},{8,24},{10,26},{12,28},{14,30},{16,0},... | collective-permute-start | bytes 98312 | tf_op jit(solution)/shard_map/ppermute | solution.py:44
  12.1 1.9 %copy-start.5 = (f32[1,384,256]{2,1,0:T(8,128)S(1)}, f32[1,384,256]{2,1,0:T(8,128)}, u32[]{:S(2)}) copy-start(f32[1,384,256]{2,1,0:T(8,128)} %param.7) | copy-start | bytes 1179652
  14.0 1.9 %copy-start.6 = (f32[1,64,256]{2,1,0:T(8,128)S(1)}, f32[1,64,256]{2,1,0:T(8,128)}, u32[]{:S(2)}) copy-start(f32[1,64,256]{2,1,0:T(8,128)} %param.8) | copy-start | bytes 196612
  14.0 6.2 %copy-start.9 = (f32[64,64]{1,0:T(8,128)S(1)}, f32[64,64]{1,0:T(8,128)}, u32[]{:S(2)}) copy-start(f32[64,64]{1,0:T(8,128)} %param.10) | copy-start | bytes 49156
  14.3 4.3 %collective-permute-start.1 = (bf16[2,64,256]{2,1,0:T(8,128)(2,1)S(1)}, bf16[2,64,256]{2,1,0:T(8,128)(2,1)S(1)}, u32[]{:S(2)}, u32[]{:S(2)}) collective-permute-start(bf16[2,64,256]{2,1,0:T(8,128)(2,1)S(1)} %maximum_bitcast_fusion), channel_id=1, source_target_pairs={{0,8},{2,10},{4,12},{6,14},{8,0},{10,2},{12,4},{14,6},{16,24},{18,... | collective-permute-start | bytes 196616 | tf_op jit(solution)/shard_map/ppermute | solution.py:44
  18.7 5.0 %collective-permute-start.2 = (bf16[2,2,64,256]{3,2,0,1:T(8,128)(2,1)S(1)}, bf16[2,2,64,256]{3,2,0,1:T(8,128)(2,1)S(1)}, u32[]{:S(2)}, u32[]{:S(2)}) collective-permute-start(bf16[2,2,64,256]{3,2,0,1:T(8,128)(2,1)S(1)} %pad_maximum_fusion.4), channel_id=1, source_target_pairs={{0,4},{2,6},{4,0},{6,2},{8,12},{10,14},{12,8},{14,10},{16,20},{18,... | collective-permute-start | bytes 393224 | tf_op jit(solution)/shard_map/ppermute | solution.py:44
  23.8 8.3 %collective-permute-start.3 = (bf16[2,2,2,64,256]{4,3,0,1,2:T(8,128)(2,1)S(1)}, bf16[2,2,2,64,256]{4,3,0,1,2:T(8,128)(2,1)}, u32[]{:S(2)}, u32[]{:S(2)}) collective-permute-start(bf16[2,2,2,64,256]{4,3,0,1,2:T(8,128)(2,1)S(1)} %pad_maximum_fusion.2), channel_id=1, source_target_pairs={{0,2},{2,0},{4,6},{6,4},{8,10},{10,8},{12,14},{14,12},{16,18},{18,... | collective-permute-start | bytes 786440 | tf_op jit(solution)/shard_map/ppermute | solution.py:44
  27.4 6.5 %copy-start.3 = (bf16[768,256]{0,1:T(8,128)(2,1)}, bf16[768,256]{0,1:T(8,128)(2,1)S(1)}, u32[]{:S(2)}) copy-start(bf16[768,256]{0,1:T(8,128)(2,1)S(1)} %all_gather.6) | copy-start | bytes 1179652
  37.1 15.9 %collective-permute-start.10 = (f32[2,2,2,64,256]{4,3,0,1,2:T(8,128)}, f32[2,2,2,64,256]{4,3,0,1,2:T(8,128)}, u32[]{:S(2)}, u32[]{:S(2)}) collective-permute-start(f32[2,2,2,64,256]{4,3,0,1,2:T(8,128)} %select_bitcast_fusion.1), channel_id=1, source_target_pairs={{0,2},{2,0},{4,6},{6,4},{8,10},{10,8},{12,14},{14,12},{16,18},{18,... | collective-permute-start | bytes 1572872 | tf_op jit(solution)/shard_map/ppermute | solution.py:44
  41.7 9.8 %collective-permute-start.4 = (f32[8,256]{1,0:T(8,128)S(1)}, f32[8,256]{1,0:T(8,128)S(1)}, u32[]{:S(2)}, u32[]{:S(2)}) collective-permute-start(f32[8,256]{1,0:T(8,128)S(1)} %pad.7), channel_id=1, source_target_pairs={{0,2},{2,0},{4,6},{6,4},{8,10},{10,8},{12,14},{14,12},{16,18},{18,... | collective-permute-start | bytes 24584 | tf_op jit(solution)/shard_map/ppermute | solution.py:44
  51.5 3.7 %collective-permute-start.5 = (f32[8,256]{1,0:T(8,128)S(1)}, f32[8,256]{1,0:T(8,128)S(1)}, u32[]{:S(2)}, u32[]{:S(2)}) collective-permute-start(f32[8,256]{1,0:T(8,128)S(1)} %pad_add_fusion.1), channel_id=1, source_target_pairs={{0,4},{2,6},{4,0},{6,2},{8,12},{10,14},{12,8},{14,10},{16,20},{18,... | collective-permute-start | bytes 24584 | tf_op jit(solution)/shard_map/ppermute | solution.py:44
  54.5 7.4 %collective-permute-start.11 = (f32[2,2,64,256]{3,2,0,1:T(8,128)S(1)}, f32[2,2,64,256]{3,2,0,1:T(8,128)S(1)}, u32[]{:S(2)}, u32[]{:S(2)}) collective-permute-start(f32[2,2,64,256]{3,2,0,1:T(8,128)S(1)} %select_bitcast_fusion.5), channel_id=1, source_target_pairs={{0,4},{2,6},{4,0},{6,2},{8,12},{10,14},{12,8},{14,10},{16,20},{18,... | collective-permute-start | bytes 786440 | tf_op jit(solution)/shard_map/ppermute | solution.py:44
  55.1 3.7 %collective-permute-start.6 = (f32[8,256]{1,0:T(8,128)S(1)}, f32[8,256]{1,0:T(8,128)S(1)}, u32[]{:S(2)}, u32[]{:S(2)}) collective-permute-start(f32[8,256]{1,0:T(8,128)S(1)} %fusion.60), channel_id=1, source_target_pairs={{0,8},{2,10},{4,12},{6,14},{8,0},{10,2},{12,4},{14,6},{16,24},{18,... | collective-permute-start | bytes 24584 | tf_op jit(solution)/shard_map/ppermute | solution.py:44
  57.5 15.9 %collective-permute-start.9 = (bf16[384,256]{0,1:T(8,128)(2,1)}, bf16[384,256]{0,1:T(8,128)(2,1)}, u32[]{:S(2)}, u32[]{:S(2)}) collective-permute-start(bf16[384,256]{0,1:T(8,128)(2,1)} %select_convert_fusion.1), channel_id=1, source_target_pairs={{0,1},{1,0},{2,3},{3,2},{4,5},{5,4},{6,7},{7,6},{8,9},{9,8},{10,11... | collective-permute-start | bytes 589832 | tf_op jit(solution)/shard_map/ppermute | solution.py:44
  58.8 4.8 %collective-permute-start.7 = (f32[8,256]{1,0:T(8,128)S(1)}, f32[8,256]{1,0:T(8,128)S(1)}, u32[]{:S(2)}, u32[]{:S(2)}) collective-permute-start(f32[8,256]{1,0:T(8,128)S(1)} %add.138), channel_id=1, source_target_pairs={{0,16},{2,18},{4,20},{6,22},{8,24},{10,26},{12,28},{14,30},{16,0},... | collective-permute-start | bytes 24584 | tf_op jit(solution)/shard_map/ppermute | solution.py:44
  62.0 5.0 %collective-permute-start.12 = (f32[2,64,256]{2,1,0:T(8,128)S(1)}, f32[2,64,256]{2,1,0:T(8,128)S(1)}, u32[]{:S(2)}, u32[]{:S(2)}) collective-permute-start(f32[2,64,256]{2,1,0:T(8,128)S(1)} %select_bitcast_fusion.11), channel_id=1, source_target_pairs={{0,8},{2,10},{4,12},{6,14},{8,0},{10,2},{12,4},{14,6},{16,24},{18,... | collective-permute-start | bytes 393224 | tf_op jit(solution)/shard_map/ppermute | solution.py:44
  63.6 1.1 collective-permute-start.8
  67.1 5.2 %collective-permute-start.13 = (f32[64,256]{1,0:T(8,128)S(1)}, f32[64,256]{1,0:T(8,128)S(1)}, u32[]{:S(2)}, u32[]{:S(2)}) collective-permute-start(f32[64,256]{1,0:T(8,128)S(1)} %select_bitcast_fusion.17), channel_id=1, source_target_pairs={{0,16},{2,18},{4,20},{6,22},{8,24},{10,26},{12,28},{14,30},{16,0},... | collective-permute-start | bytes 196616 | tf_op jit(solution)/shard_map/ppermute | solution.py:44
  72.9 4.9 %collective-permute-start.14 = (bf16[1,64,256]{2,1,0:T(8,128)(2,1)S(1)}, bf16[1,64,256]{2,1,0:T(8,128)(2,1)S(1)}, u32[]{:S(2)}, u32[]{:S(2)}) collective-permute-start(bf16[1,64,256]{2,1,0:T(8,128)(2,1)S(1)} %get-tuple-element.27), channel_id=1, source_target_pairs={{0,16},{2,18},{4,20},{6,22},{8,24},{10,26},{12,28},{14,30},{16,0},... | collective-permute-start | bytes 98312 | tf_op jit(solution)/shard_map/ppermute | solution.py:44
  75.3 9.7 %copy-start.7 = (bf16[384,256]{0,1:T(8,128)(2,1)S(1)}, bf16[384,256]{0,1:T(8,128)(2,1)}, u32[]{:S(2)}) copy-start(bf16[384,256]{0,1:T(8,128)(2,1)} %get-tuple-element.24) | copy-start | bytes 589828
  77.9 4.5 %collective-permute-start.15 = (bf16[2,64,256]{2,1,0:T(8,128)(2,1)S(1)}, bf16[2,64,256]{2,1,0:T(8,128)(2,1)S(1)}, u32[]{:S(2)}, u32[]{:S(2)}) collective-permute-start(bf16[2,64,256]{2,1,0:T(8,128)(2,1)S(1)} %maximum_bitcast_fusion.1), channel_id=1, source_target_pairs={{0,8},{2,10},{4,12},{6,14},{8,0},{10,2},{12,4},{14,6},{16,24},{18,... | collective-permute-start | bytes 196616 | tf_op jit(solution)/shard_map/ppermute | solution.py:44
  80.6 2.8 %copy-start.1 = (f32[384,4,64]{0,2,1:T(8,128)}, f32[384,4,64]{0,2,1:T(8,128)S(1)}, u32[]{:S(2)}) copy-start(f32[384,4,64]{0,2,1:T(8,128)S(1)} %fusion.33) | copy-start | bytes 1179652
  83.0 5.3 %collective-permute-start.16 = (bf16[2,2,64,256]{3,2,0,1:T(8,128)(2,1)}, bf16[2,2,64,256]{3,2,0,1:T(8,128)(2,1)}, u32[]{:S(2)}, u32[]{:S(2)}) collective-permute-start(bf16[2,2,64,256]{3,2,0,1:T(8,128)(2,1)} %pad_maximum_fusion.5), channel_id=1, source_target_pairs={{0,4},{2,6},{4,0},{6,2},{8,12},{10,14},{12,8},{14,10},{16,20},{18,... | collective-permute-start | bytes 393224 | tf_op jit(solution)/shard_map/ppermute | solution.py:44
  87.3 11.6 %copy-start.4 = (bf16[768,256]{0,1:T(8,128)(2,1)}, bf16[768,256]{0,1:T(8,128)(2,1)S(1)}, u32[]{:S(2)}) copy-start(bf16[768,256]{0,1:T(8,128)(2,1)S(1)} %all_gather.7) | copy-start | bytes 1179652
  90.0 7.8 %collective-permute-start.17 = (bf16[2,2,2,64,256]{4,3,0,1,2:T(8,128)(2,1)}, bf16[2,2,2,64,256]{4,3,0,1,2:T(8,128)(2,1)}, u32[]{:S(2)}, u32[]{:S(2)}) collective-permute-start(bf16[2,2,2,64,256]{4,3,0,1,2:T(8,128)(2,1)} %pad_maximum_fusion.3), channel_id=1, source_target_pairs={{0,2},{2,0},{4,6},{6,4},{8,10},{10,8},{12,14},{14,12},{16,18},{18,... | collective-permute-start | bytes 786440 | tf_op jit(solution)/shard_map/ppermute | solution.py:44
  101.4 1.2 copy-start.10
  101.6 21.4 %collective-permute-start.24 = (f32[2,2,2,64,256]{4,3,0,1,2:T(8,128)S(1)}, f32[2,2,2,64,256]{4,3,0,1,2:T(8,128)}, u32[]{:S(2)}, u32[]{:S(2)}) collective-permute-start(f32[2,2,2,64,256]{4,3,0,1,2:T(8,128)S(1)} %select_bitcast_fusion), channel_id=1, source_target_pairs={{0,2},{2,0},{4,6},{6,4},{8,10},{10,8},{12,14},{14,12},{16,18},{18,... | collective-permute-start | bytes 1572872 | tf_op jit(solution)/shard_map/ppermute | solution.py:44
  102.7 11.3 %collective-permute-start.18 = (f32[8,256]{1,0:T(8,128)S(1)}, f32[8,256]{1,0:T(8,128)S(1)}, u32[]{:S(2)}, u32[]{:S(2)}) collective-permute-start(f32[8,256]{1,0:T(8,128)S(1)} %pad.8), channel_id=1, source_target_pairs={{0,2},{2,0},{4,6},{6,4},{8,10},{10,8},{12,14},{14,12},{16,18},{18,... | collective-permute-start | bytes 24584 | tf_op jit(solution)/shard_map/ppermute | solution.py:44
  114.0 4.2 %collective-permute-start.19 = (f32[8,256]{1,0:T(8,128)S(1)}, f32[8,256]{1,0:T(8,128)S(1)}, u32[]{:S(2)}, u32[]{:S(2)}) collective-permute-start(f32[8,256]{1,0:T(8,128)S(1)} %pad_add_fusion), channel_id=1, source_target_pairs={{0,4},{2,6},{4,0},{6,2},{8,12},{10,14},{12,8},{14,10},{16,20},{18,... | collective-permute-start | bytes 24584 | tf_op jit(solution)/shard_map/ppermute | solution.py:44
  118.3 3.7 %collective-permute-start.20 = (f32[8,256]{1,0:T(8,128)S(1)}, f32[8,256]{1,0:T(8,128)S(1)}, u32[]{:S(2)}, u32[]{:S(2)}) collective-permute-start(f32[8,256]{1,0:T(8,128)S(1)} %fusion.59), channel_id=1, source_target_pairs={{0,8},{2,10},{4,12},{6,14},{8,0},{10,2},{12,4},{14,6},{16,24},{18,... | collective-permute-start | bytes 24584 | tf_op jit(solution)/shard_map/ppermute | solution.py:44
  122.0 4.5 %collective-permute-start.21 = (f32[8,256]{1,0:T(8,128)S(1)}, f32[8,256]{1,0:T(8,128)S(1)}, u32[]{:S(2)}, u32[]{:S(2)}) collective-permute-start(f32[8,256]{1,0:T(8,128)S(1)} %add.156), channel_id=1, source_target_pairs={{0,16},{2,18},{4,20},{6,22},{8,24},{10,26},{12,28},{14,30},{16,0},... | collective-permute-start | bytes 24584 | tf_op jit(solution)/shard_map/ppermute | solution.py:44
  124.2 13.7 %copy-start.2 = (f32[384,4,64]{0,2,1:T(8,128)S(1)}, f32[384,4,64]{0,2,1:T(8,128)}, u32[]{:S(2)}) copy-start(f32[384,4,64]{0,2,1:T(8,128)} %copy-done.1) | copy-start | bytes 1179652
  124.2 6.4 %collective-permute-start.25 = (f32[2,2,64,256]{3,2,0,1:T(8,128)S(1)}, f32[2,2,64,256]{3,2,0,1:T(8,128)S(1)}, u32[]{:S(2)}, u32[]{:S(2)}) collective-permute-start(f32[2,2,64,256]{3,2,0,1:T(8,128)S(1)} %select_bitcast_fusion.2), channel_id=1, source_target_pairs={{0,4},{2,6},{4,0},{6,2},{8,12},{10,14},{12,8},{14,10},{16,20},{18,... | collective-permute-start | bytes 786440 | tf_op jit(solution)/shard_map/ppermute | solution.py:44
  126.0 11.9 %collective-permute-start.23 = (bf16[384,256]{0,1:T(8,128)(2,1)}, bf16[384,256]{0,1:T(8,128)(2,1)}, u32[]{:S(2)}, u32[]{:S(2)}) collective-permute-start(bf16[384,256]{0,1:T(8,128)(2,1)} %select_convert_fusion), channel_id=1, source_target_pairs={{0,1},{1,0},{2,3},{3,2},{4,5},{5,4},{6,7},{7,6},{8,9},{9,8},{10,11... | collective-permute-start | bytes 589832 | tf_op jit(solution)/shard_map/ppermute | solution.py:44
  126.5 1.1 collective-permute-start.22
  130.7 5.0 %collective-permute-start.26 = (f32[2,64,256]{2,1,0:T(8,128)S(1)}, f32[2,64,256]{2,1,0:T(8,128)S(1)}, u32[]{:S(2)}, u32[]{:S(2)}) collective-permute-start(f32[2,64,256]{2,1,0:T(8,128)S(1)} %select_bitcast_fusion.8), channel_id=1, source_target_pairs={{0,8},{2,10},{4,12},{6,14},{8,0},{10,2},{12,4},{14,6},{16,24},{18,... | collective-permute-start | bytes 393224 | tf_op jit(solution)/shard_map/ppermute | solution.py:44
  135.8 5.3 %collective-permute-start.27 = (f32[64,256]{1,0:T(8,128)S(1)}, f32[64,256]{1,0:T(8,128)S(1)}, u32[]{:S(2)}, u32[]{:S(2)}) collective-permute-start(f32[64,256]{1,0:T(8,128)S(1)} %select_bitcast_fusion.14), channel_id=1, source_target_pairs={{0,16},{2,18},{4,20},{6,22},{8,24},{10,26},{12,28},{14,30},{16,0},... | collective-permute-start | bytes 196616 | tf_op jit(solution)/shard_map/ppermute | solution.py:44
  139.2 1.8 %copy-start.8 = (f32[64,256]{1,0:T(8,128)S(1)}, f32[64,256]{1,0:T(8,128)}, u32[]{:S(2)}) copy-start(f32[64,256]{1,0:T(8,128)} %get-tuple-element.29) | copy-start | bytes 196612

commit v5 on v4

--- a/solution.py
+++ b/solution.py
@@ -39,8 +39,9 @@
     return size, bits
 
 
-def swap_with(value, axis, size, bit):
-    pairs = [(i, i ^ (1 << bit)) for i in range(size)]
+def swap_with(value, axis, size, bit, mask=None):
+    mask = (1 << bit) if mask is None else mask
+    pairs = [(i, i ^ mask) for i in range(size)]
     return lax.ppermute(value, axis, pairs)
 
 
@@ -79,17 +80,22 @@
 def double_gather(piece, axis):
     size, bits = bit_count(axis)
     me = lax.axis_index(axis)
+    order = list(range(bits))[::-1]
+    groups = [order[:1]] if bits % 2 else []
+    groups += [order[i : i + 2] for i in range(bits % 2, bits, 2)]
     buf = piece[None]
-    for step, bit in enumerate(reversed(range(bits))):
-        other = swap_with(buf, axis, size, bit)
-        upper = ((me >> bit) & 1) == 1
-        first = jnp.where(upper, other, buf)
-        second = jnp.where(upper, buf, other)
-        buf = jnp.stack([first, second], axis=step)
-        buf = buf.reshape((-1,) + piece.shape)
-        buf = buf.reshape([2] * (step + 1) + list(piece.shape))
+    for group in groups:
+        masks = [sum(1 << group[-1 - j] for j in range(len(group)) if (k >> j) & 1) for k in range(1 << len(group))]
+        pieces = [buf] + [swap_with(buf, axis, size, None, mask) for mask in masks[1:]]
+        digit = sum(((me >> group[-1 - j]) & 1) << j for j in range(len(group)))
+        ordered = []
+        for place in range(len(masks)):
+            pick = pieces[place]
+            for held in range(1, len(masks)):
+                pick = jnp.where(digit == held, pieces[place ^ held], pick)
+            ordered.append(pick)
+        buf = jnp.stack(ordered, axis=1).reshape((-1,) + piece.shape)
     return buf.reshape((size * piece.shape[0],) + piece.shape[1:])
-
 
 def per_device(
     draws_user, draws_item, prior_user, prior_item, count_tiles, tile_blocks, tile_count
@@ -121,7 +127,7 @@
         return (to_users, to_items)
 
     def user_range_of(user_vec):
-        return lax.all_gather(user_vec.astype(jnp.bfloat16), "item", axis=0, tiled=True)
+        return double_gather(user_vec.astype(jnp.bfloat16), "item")
 
     def item_range_of(item_vec):
         return double_gather(item_vec.astype(jnp.bfloat16), "user")

time: 142 us -> 135 us (0.951)
  other arithmetic: 26.5 us -> 15.1 us
  starting transfers between devices: 33.5 us -> 37.9 us
  blocking collectives: 4.33 us -> 0 us
  waiting for transfers between devices: 56.9 us -> 59.8 us
  local copies, waits for them, and re-layouts: 7.92 us -> 10.2 us
    ppermute x28 -> x34, starting transfers between devices: 33.5 us -> 37.9 us  [swap_with(): return lax.ppermute(value, axis, pairs)]
    all_gather x2 -> x0, blocking collectives: 4.33 us -> none  [user_range_of(): lax.all_gather(user_vec.astype(jnp.bfloat16), 'item', axis=0, tiled=True)]
    another operation x14 -> x12, other arithmetic: 4.51 us -> 0.5 us  [double_gather(): buf = jnp.stack(ordered, axis=1).reshape((-1,) + piece.shape)]
    dot_general x2, matrix products: 1.62 us -> 4.82 us  [cross_parts(): lax.dot_general(counts_bf, user_range, (((0,), (0,)), ((), ())), preferre...]
    ppermute x28 -> x34, waiting for transfers between devices: 56.9 us -> 59.8 us  [swap_with(): return lax.ppermute(value, axis, pairs)]
    dot_general x2, matrix products: 3.48 us -> 1.38 us  [cross_parts(): jnp.dot(counts_bf, item_range, preferred_element_type=jnp.float32)]
    convert_element_type x2 -> x0, other arithmetic: 2.05 us -> none  [user_range_of(): user_vec.astype(jnp.bfloat16)]
    unnamed x27, local copies, waits for them, and re-layouts: 3.95 us -> 5.53 us
  transfers between devices with their start and end apart: 28 -> 34, of which waited for: 19 -> 26; matrix products, arithmetic and copies ran while one was open for 23% -> 17% of each run, Pallas kernels for 0% -> 0%
where the time goes in v5:
time: 135 us; the launch traced here: 134 us
  waiting for transfers between devices  59.8 us (44%)
  starting transfers between devices  37.9 us (28%)
  other arithmetic  15.1 us (11%)
  local copies, waits for them, and re-layouts  10.2 us (8%)
  matrix products  9.58 us (7%)
  between operations  1.88 us (1%)
    ppermute x34, waiting for transfers between devices, swap_with(): return lax.ppermute(value, axis, pairs)  59.8 us
    ppermute x34, starting transfers between devices, swap_with(): return lax.ppermute(value, axis, pairs)  37.9 us
    unnamed x27, local copies, waits for them, and re-layouts  5.53 us
    dot_general x2, matrix products, cross_parts(): lax.dot_general(counts_bf, user_range, (((0,), (0,)), ((), ())), preferre...  4.82 us
    reduce_sum x14, other arithmetic, per_draw(): return jnp.sum(product, axis=(0, 2))  3.54 us
  transfers between devices with their start and end apart: 34, of which 26 were waited for; matrix products, arithmetic and copies ran while one was open for 17% of the time, Pallas kernels for 0%

profile of v5, /device:TPU:0, one launch (start us, length us, event | category | flops | bytes accessed | tf_op | source)
XLA Modules:
  0.0 134.5 jit_solution(7207210696139183366)
XLA Ops:
  0.6 0.9 multiply_reduce_fusion.7
  1.6 5.1 %collective-permute-start.1 = (bf16[1,64,256]{2,1,0:T(8,128)(2,1)S(1)}, bf16[1,64,256]{2,1,0:T(8,128)(2,1)S(1)}, u32[]{:S(2)}, u32[]{:S(2)}) collective-permute-start(bf16[1,64,256]{2,1,0:T(8,128)(2,1)S(1)} %get-tuple-element.47), channel_id=1, source_target_pairs={{0,24},{2,26},{4,28},{6,30},{8,16},{10,18},{12,20},{14,22},{16,8},... | collective-permute-start | bytes 98312 | tf_op jit(solution)/shard_map/ppermute | solution.py:45
  6.7 0.6 collective-permute-start.3
  7.3 1.3 multiply_reduce_fusion.3
  8.7 1.2 copy.44
  9.9 2.2 %convert_bitcast_fusion = bf16[12,256,256]{2,1,0:T(8,128)(2,1)S(1)} fusion(s32[1,1,12,256,256]{4,3,2,1,0:T(8,128)} %param.11), kind=kLoop, calls=%fused_computation.6 | loop fusion | flops 786432 | bytes 4718592 | tf_op jit(solution)/shard_map/convert_element_type | solution.py:113
  12.8 1.6 %bitcast_convert_fusion = (bf16[3,256,4,256]{3,2,1,0:T(4,128)(2,1)S(1)}, f32[3,4,256,256]{3,1,2,0:T(4,128)S(1)}) fusion(bf16[12,256,256]{2,1,0:T(8,128)(2,1)S(1)} %convert_bitcast_fusion, pred[12,4]{0,1:T(4,128)(4,1)S(1)} %fusion.38, pred[12,3]{0,1:T(4,128)(4,1)S(1)} %fusion.37), kind=kOutput, calls=%fused_computation.2 | convolution fusion | flops 19660944 | bytes 6291540 | tf_op jit(solution)/shard_map/trc,tij->ricj/dot_general | solution.py:110
  14.4 1.9 %bitcast_reduce_fusion = (f32[4,256]{1,0:T(4,128)S(1)}, f32[3,256]{1,0:T(4,128)S(1)}) fusion(f32[3,4,256,256]{3,1,2,0:T(4,128)S(1)} %get-tuple-element.51), kind=kLoop, calls=%fused_computation | loop fusion | flops 1571072 | bytes 3152896 | tf_op jit(solution)/shard_map/reduce_sum | solution.py:117
  16.3 0.6 multiply_reduce_fusion.2
  17.1 1.5 %copy.72 = bf16[96,8,4,256]{3,1,2,0:T(8,128)(2,1)} copy(bf16[96,8,4,256]{3,2,1,0:T(4,128)(2,1)S(1)} %bitcast.227) | data formatting | bytes 3145728
  19.6 2.7 %collective-permute-start.4 = (bf16[4,64,256]{2,1,0:T(8,128)(2,1)S(1)}, bf16[4,64,256]{2,1,0:T(8,128)(2,1)S(1)}, u32[]{:S(2)}, u32[]{:S(2)}) collective-permute-start(bf16[4,64,256]{2,1,0:T(8,128)(2,1)S(1)} %maximum_bitcast_fusion), channel_id=1, source_target_pairs={{0,6},{2,4},{4,2},{6,0},{8,14},{10,12},{12,10},{14,8},{16,22},{18,... | collective-permute-start | bytes 393224 | tf_op jit(solution)/shard_map/ppermute | solution.py:45
  23.6 3.1 %collective-permute-done.4 = bf16[4,64,256]{2,1,0:T(8,128)(2,1)S(1)} collective-permute-done((bf16[4,64,256]{2,1,0:T(8,128)(2,1)S(1)}, bf16[4,64,256]{2,1,0:T(8,128)(2,1)S(1)}, u32[]{:S(2)}, u32[]{:S(2)}) %collective-permute-start.4) | collective-permute-done | bytes 131104 | tf_op jit(solution)/shard_map/ppermute | solution.py:45
  26.7 2.7 %collective-permute-done.5 = bf16[4,64,256]{2,1,0:T(8,128)(2,1)S(1)} collective-permute-done((bf16[4,64,256]{2,1,0:T(8,128)(2,1)S(1)}, bf16[4,64,256]{2,1,0:T(8,128)(2,1)S(1)}, u32[]{:S(2)}, u32[]{:S(2)}) %collective-permute-start.5) | collective-permute-done | bytes 131104 | tf_op jit(solution)/shard_map/ppermute | solution.py:45
  29.9 1.6 %copy-done.2 = bf16[96,8,4,256]{3,1,2,0:T(8,128)(2,1)S(1)} copy-done((bf16[96,8,4,256]{3,1,2,0:T(8,128)(2,1)S(1)}, bf16[96,8,4,256]{3,1,2,0:T(8,128)(2,1)}, u32[]{:S(2)}) %copy-start.2) | copy-done | bytes 1572888
  31.5 0.6 fusion.5
  32.3 3.1 %fusion.3 = (f32[256]{0:T(256)S(1)}, f32[1024,256]{1,0:T(8,128)}) fusion(bf16[4,4,64,256]{3,2,1,0:T(8,128)(2,1)} %copy-done.6, bf16[1024,256]{1,0:T(8,128)(2,1)} %bitcast.239, f32[1024]{0:T(1024)S(1)} %bitcast.247, bf16[768,1024]{1,0:T(8,128)(2,1)S(1)} %bitcast.229, bf16[768,256]{1,0:T(8,128)(2,1)} %bitcast.245), kind=kOutput, calls=%fused_computation.15 | convolution fusion | flops 404225792 | bytes 4068352 | tf_op jit(solution)/shard_map/dot_general | solution.py:123
  35.7 1.5 %collective-permute-start.7 = (f32[8,256]{1,0:T(8,128)S(1)}, f32[8,256]{1,0:T(8,128)S(1)}, u32[]{:S(2)}, u32[]{:S(2)}) collective-permute-start(f32[8,256]{1,0:T(8,128)S(1)} %pad.7), channel_id=1, source_target_pairs={{0,2},{2,0},{4,6},{6,4},{8,10},{10,8},{12,14},{14,12},{16,18},{18,... | collective-permute-start | bytes 24584 | tf_op jit(solution)/shard_map/ppermute | solution.py:45
  37.2 0.9 copy.50
  38.3 1.0 collective-permute-done.7
  39.3 1.4 %collective-permute-start.8 = (f32[8,256]{1,0:T(8,128)S(1)}, f32[8,256]{1,0:T(8,128)S(1)}, u32[]{:S(2)}, u32[]{:S(2)}) collective-permute-start(f32[8,256]{1,0:T(8,128)S(1)} %pad_add_fusion.1), channel_id=1, source_target_pairs={{0,4},{2,6},{4,0},{6,2},{8,12},{10,14},{12,8},{14,10},{16,20},{18,... | collective-permute-start | bytes 24584 | tf_op jit(solution)/shard_map/ppermute | solution.py:45
  40.8 1.3 fusion.43
  42.1 0.9 collective-permute-done.8
  43.0 1.2 collective-permute-start.9
  44.3 1.6 %collective-permute-start.13 = (f32[2,2,2,64,256]{4,3,0,1,2:T(8,128)S(1)}, f32[2,2,2,64,256]{4,3,0,1,2:T(8,128)}, u32[]{:S(2)}, u32[]{:S(2)}) collective-permute-start(f32[2,2,2,64,256]{4,3,0,1,2:T(8,128)S(1)} %select_bitcast_fusion.1), channel_id=1, source_target_pairs={{0,2},{2,0},{4,6},{6,4},{8,10},{10,8},{12,14},{14,12},{16,18},{18,... | collective-permute-start | bytes 1572872 | tf_op jit(solution)/shard_map/ppermute | solution.py:45
  45.9 0.8 collective-permute-done.9
  46.7 2.2 %collective-permute-start.10 = (f32[8,256]{1,0:T(8,128)S(1)}, f32[8,256]{1,0:T(8,128)S(1)}, u32[]{:S(2)}, u32[]{:S(2)}) collective-permute-start(f32[8,256]{1,0:T(8,128)S(1)} %add.148), channel_id=1, source_target_pairs={{0,16},{2,18},{4,20},{6,22},{8,24},{10,26},{12,28},{14,30},{16,0},... | collective-permute-start | bytes 24584 | tf_op jit(solution)/shard_map/ppermute | solution.py:45
  48.9 2.3 %collective-permute-done.10 = f32[8,256]{1,0:T(8,128)S(1)} collective-permute-done((f32[8,256]{1,0:T(8,128)S(1)}, f32[8,256]{1,0:T(8,128)S(1)}, u32[]{:S(2)}, u32[]{:S(2)}) %collective-permute-start.10) | collective-permute-done | bytes 8224 | tf_op jit(solution)/shard_map/ppermute | solution.py:45
  51.2 1.1 collective-permute-done.11
  52.6 3.2 %collective-permute-done.13 = f32[2,2,2,64,256]{4,3,0,1,2:T(8,128)} collective-permute-done((f32[2,2,2,64,256]{4,3,0,1,2:T(8,128)S(1)}, f32[2,2,2,64,256]{4,3,0,1,2:T(8,128)}, u32[]{:S(2)}, u32[]{:S(2)}) %collective-permute-start.13) | collective-permute-done | bytes 524320 | tf_op jit(solution)/shard_map/ppermute | solution.py:45
  55.8 1.1 bitcast_add_fusion.1
  57.0 1.5 %collective-permute-start.14 = (f32[2,2,64,256]{3,2,0,1:T(8,128)S(1)}, f32[2,2,64,256]{3,2,0,1:T(8,128)S(1)}, u32[]{:S(2)}, u32[]{:S(2)}) collective-permute-start(f32[2,2,64,256]{3,2,0,1:T(8,128)S(1)} %select_bitcast_fusion.3), channel_id=1, source_target_pairs={{0,4},{2,6},{4,0},{6,2},{8,12},{10,14},{12,8},{14,10},{16,20},{18,... | collective-permute-start | bytes 786440 | tf_op jit(solution)/shard_map/ppermute | solution.py:45
  58.5 1.9 %convert_bitcast_fusion.1 = (bf16[1,384,256]{2,1,0:T(8,128)(2,1)S(1)}, f32[384,256]{1,0:T(8,128)S(1)}, f32[384,256]{1,0:T(8,128)}) fusion(f32[256]{0:T(256)S(1)} %mul.198, f32[1,384,256]{2,1,0:T(8,128)S(1)} %copy-done.1, f32[384,256]{1,0:T(8,128)} %copy.50, bf16[384,256]{1,0:T(8,128)(2,1)S(1)} %collective-permute-done.12, ...), kind=kLoop, calls=%fused_computation.52 | loop fusion | flops 786432 | bytes 2753537 | tf_op jit(solution)/shard_map/broadcast_in_dim | solution.py:86
  61.3 2.2 %collective-permute-done.14 = f32[2,2,64,256]{3,2,0,1:T(8,128)S(1)} collective-permute-done((f32[2,2,64,256]{3,2,0,1:T(8,128)S(1)}, f32[2,2,64,256]{3,2,0,1:T(8,128)S(1)}, u32[]{:S(2)}, u32[]{:S(2)}) %collective-permute-start.14) | collective-permute-done | bytes 262176 | tf_op jit(solution)/shard_map/ppermute | solution.py:45
  63.5 0.8 collective-permute-start.15
  64.9 3.7 %collective-permute-done.15 = f32[2,64,256]{2,1,0:T(8,128)S(1)} collective-permute-done((f32[2,64,256]{2,1,0:T(8,128)S(1)}, f32[2,64,256]{2,1,0:T(8,128)S(1)}, u32[]{:S(2)}, u32[]{:S(2)}) %collective-permute-start.15) | collective-permute-done | bytes 131104 | tf_op jit(solution)/shard_map/ppermute | solution.py:45
  68.6 3.7 %collective-permute-start.16 = (f32[64,256]{1,0:T(8,128)S(1)}, f32[64,256]{1,0:T(8,128)S(1)}, u32[]{:S(2)}, u32[]{:S(2)}) collective-permute-start(f32[64,256]{1,0:T(8,128)S(1)} %select_bitcast_fusion.19), channel_id=1, source_target_pairs={{0,16},{2,18},{4,20},{6,22},{8,24},{10,26},{12,28},{14,30},{16,0},... | collective-permute-start | bytes 196616 | tf_op jit(solution)/shard_map/ppermute | solution.py:45
  72.3 2.8 %collective-permute-done.16 = f32[64,256]{1,0:T(8,128)S(1)} collective-permute-done((f32[64,256]{1,0:T(8,128)S(1)}, f32[64,256]{1,0:T(8,128)S(1)}, u32[]{:S(2)}, u32[]{:S(2)}) %collective-permute-start.16) | collective-permute-done | bytes 65568 | tf_op jit(solution)/shard_map/ppermute | solution.py:45
  75.1 1.6 %collective-permute-start.18 = (bf16[1,64,256]{2,1,0:T(8,128)(2,1)S(1)}, bf16[1,64,256]{2,1,0:T(8,128)(2,1)S(1)}, u32[]{:S(2)}, u32[]{:S(2)}) collective-permute-start(bf16[1,64,256]{2,1,0:T(8,128)(2,1)S(1)} %get-tuple-element.15), channel_id=1, source_target_pairs={{0,24},{2,26},{4,28},{6,30},{8,16},{10,18},{12,20},{14,22},{16,8},... | collective-permute-start | bytes 98312 | tf_op jit(solution)/shard_map/ppermute | solution.py:45
  76.8 1.0 collective-permute-start.19
  77.7 1.9 %collective-permute-start.20 = (bf16[1,64,256]{2,1,0:T(8,128)(2,1)S(1)}, bf16[1,64,256]{2,1,0:T(8,128)(2,1)S(1)}, u32[]{:S(2)}, u32[]{:S(2)}) collective-permute-start(bf16[1,64,256]{2,1,0:T(8,128)(2,1)S(1)} %get-tuple-element.15), channel_id=1, source_target_pairs={{0,8},{2,10},{4,12},{6,14},{8,0},{10,2},{12,4},{14,6},{16,24},{18,... | collective-permute-start | bytes 98312 | tf_op jit(solution)/shard_map/ppermute | solution.py:45
  79.8 1.2 collective-permute-done.18
  80.9 0.7 collective-permute-done.19
  82.0 1.5 %collective-permute-start.21 = (bf16[4,64,256]{2,1,0:T(8,128)(2,1)S(1)}, bf16[4,64,256]{2,1,0:T(8,128)(2,1)S(1)}, u32[]{:S(2)}, u32[]{:S(2)}) collective-permute-start(bf16[4,64,256]{2,1,0:T(8,128)(2,1)S(1)} %maximum_bitcast_fusion.1), channel_id=1, source_target_pairs={{0,6},{2,4},{4,2},{6,0},{8,14},{10,12},{12,10},{14,8},{16,22},{18,... | collective-permute-start | bytes 393224 | tf_op jit(solution)/shard_map/ppermute | solution.py:45
  83.5 2.7 %collective-permute-start.22 = (bf16[4,64,256]{2,1,0:T(8,128)(2,1)S(1)}, bf16[4,64,256]{2,1,0:T(8,128)(2,1)S(1)}, u32[]{:S(2)}, u32[]{:S(2)}) collective-permute-start(bf16[4,64,256]{2,1,0:T(8,128)(2,1)S(1)} %maximum_bitcast_fusion.1), channel_id=1, source_target_pairs={{0,4},{2,6},{4,0},{6,2},{8,12},{10,14},{12,8},{14,10},{16,20},{18,... | collective-permute-start | bytes 393224 | tf_op jit(solution)/shard_map/ppermute | solution.py:45
  87.2 0.8 collective-permute-done.21
  87.9 1.6 %collective-permute-done.22 = bf16[4,64,256]{2,1,0:T(8,128)(2,1)S(1)} collective-permute-done((bf16[4,64,256]{2,1,0:T(8,128)(2,1)S(1)}, bf16[4,64,256]{2,1,0:T(8,128)(2,1)S(1)}, u32[]{:S(2)}, u32[]{:S(2)}) %collective-permute-start.22) | collective-permute-done | bytes 131104 | tf_op jit(solution)/shard_map/ppermute | solution.py:45
  89.5 3.0 %collective-permute-done.23 = bf16[4,64,256]{2,1,0:T(8,128)(2,1)S(1)} collective-permute-done((bf16[4,64,256]{2,1,0:T(8,128)(2,1)S(1)}, bf16[4,64,256]{2,1,0:T(8,128)(2,1)S(1)}, u32[]{:S(2)}, u32[]{:S(2)}) %collective-permute-start.23) | collective-permute-done | bytes 131104 | tf_op jit(solution)/shard_map/ppermute | solution.py:45
  92.8 1.2 copy-done.3
  94.0 0.8 fusion.6
  94.8 1.7 %fusion.4 = (f32[256]{0:T(256)S(1)}, f32[1024,256]{1,0:T(8,128)S(1)}) fusion(bf16[4,4,64,256]{3,2,1,0:T(8,128)(2,1)S(1)} %copy.59, bf16[1024,256]{1,0:T(8,128)(2,1)S(1)} %bitcast.241, f32[1024]{0:T(1024)S(1)} %bitcast.248, bf16[768,1024]{1,0:T(8,128)(2,1)S(1)} %bitcast.231, bf16[768,256]{1,0:T(8,128)(2,1)} %bitcast.243), kind=kOutput, calls=%fused_computation.16 | convolution fusion | flops 404225792 | bytes 4068352 | tf_op jit(solution)/shard_map/dot_general | solution.py:123
  97.4 2.0 %collective-permute-start.24 = (f32[8,256]{1,0:T(8,128)S(1)}, f32[8,256]{1,0:T(8,128)S(1)}, u32[]{:S(2)}, u32[]{:S(2)}) collective-permute-start(f32[8,256]{1,0:T(8,128)S(1)} %pad.8), channel_id=1, source_target_pairs={{0,2},{2,0},{4,6},{6,4},{8,10},{10,8},{12,14},{14,12},{16,18},{18,... | collective-permute-start | bytes 24584 | tf_op jit(solution)/shard_map/ppermute | solution.py:45
  99.4 7.1 %collective-permute-done.24 = f32[8,256]{1,0:T(8,128)S(1)} collective-permute-done((f32[8,256]{1,0:T(8,128)S(1)}, f32[8,256]{1,0:T(8,128)S(1)}, u32[]{:S(2)}, u32[]{:S(2)}) %collective-permute-start.24) | collective-permute-done | bytes 8224 | tf_op jit(solution)/shard_map/ppermute | solution.py:45
  106.5 3.6 %collective-permute-done.25 = f32[8,256]{1,0:T(8,128)S(1)} collective-permute-done((f32[8,256]{1,0:T(8,128)S(1)}, f32[8,256]{1,0:T(8,128)S(1)}, u32[]{:S(2)}, u32[]{:S(2)}) %collective-permute-start.25) | collective-permute-done | bytes 8224 | tf_op jit(solution)/shard_map/ppermute | solution.py:45
  110.2 3.6 %collective-permute-done.26 = f32[8,256]{1,0:T(8,128)S(1)} collective-permute-done((f32[8,256]{1,0:T(8,128)S(1)}, f32[8,256]{1,0:T(8,128)S(1)}, u32[]{:S(2)}, u32[]{:S(2)}) %collective-permute-start.26) | collective-permute-done | bytes 8224 | tf_op jit(solution)/shard_map/ppermute | solution.py:45
  113.8 2.0 %collective-permute-start.27 = (f32[8,256]{1,0:T(8,128)S(1)}, f32[8,256]{1,0:T(8,128)S(1)}, u32[]{:S(2)}, u32[]{:S(2)}) collective-permute-start(f32[8,256]{1,0:T(8,128)S(1)} %add.166), channel_id=1, source_target_pairs={{0,16},{2,18},{4,20},{6,22},{8,24},{10,26},{12,28},{14,30},{16,0},... | collective-permute-start | bytes 24584 | tf_op jit(solution)/shard_map/ppermute | solution.py:45
  116.2 2.2 %collective-permute-done.27 = f32[8,256]{1,0:T(8,128)S(1)} collective-permute-done((f32[8,256]{1,0:T(8,128)S(1)}, f32[8,256]{1,0:T(8,128)S(1)}, u32[]{:S(2)}, u32[]{:S(2)}) %collective-permute-start.27) | collective-permute-done | bytes 8224 | tf_op jit(solution)/shard_map/ppermute | solution.py:45
  118.4 1.1 collective-permute-done.28
  119.5 2.9 %collective-permute-done.31 = f32[2,2,64,256]{3,2,0,1:T(8,128)S(1)} collective-permute-done((f32[2,2,64,256]{3,2,0,1:T(8,128)S(1)}, f32[2,2,64,256]{3,2,0,1:T(8,128)S(1)}, u32[]{:S(2)}, u32[]{:S(2)}) %collective-permute-start.31) | collective-permute-done | bytes 262176 | tf_op jit(solution)/shard_map/ppermute | solution.py:45
  122.4 0.7 select_bitcast_fusion.8
  123.5 5.0 %collective-permute-done.32 = f32[2,64,256]{2,1,0:T(8,128)S(1)} collective-permute-done((f32[2,64,256]{2,1,0:T(8,128)}, f32[2,64,256]{2,1,0:T(8,128)S(1)}, u32[]{:S(2)}, u32[]{:S(2)}) %collective-permute-start.32) | collective-permute-done | bytes 131104 | tf_op jit(solution)/shard_map/ppermute | solution.py:45
  128.6 1.5 %collective-permute-start.33 = (f32[64,256]{1,0:T(8,128)S(1)}, f32[64,256]{1,0:T(8,128)S(1)}, u32[]{:S(2)}, u32[]{:S(2)}) collective-permute-start(f32[64,256]{1,0:T(8,128)S(1)} %select_bitcast_fusion.18), channel_id=1, source_target_pairs={{0,16},{2,18},{4,20},{6,22},{8,24},{10,26},{12,28},{14,30},{16,0},... | collective-permute-start | bytes 196616 | tf_op jit(solution)/shard_map/ppermute | solution.py:45
  130.1 1.1 subtract_bitcast_fusion
  131.1 2.6 %collective-permute-done.33 = f32[64,256]{1,0:T(8,128)S(1)} collective-permute-done((f32[64,256]{1,0:T(8,128)S(1)}, f32[64,256]{1,0:T(8,128)S(1)}, u32[]{:S(2)}, u32[]{:S(2)}) %collective-permute-start.33) | collective-permute-done | bytes 65568 | tf_op jit(solution)/shard_map/ppermute | solution.py:45
  133.8 0.7 fusion.20
  (144 shorter events, 9.0 us)
Async XLA Ops:
  0.6 15.7 %copy-start = (f32[64,64]{1,0:T(8,128)S(1)}, f32[64,64]{1,0:T(8,128)}, u32[]{:S(2)}) copy-start(f32[64,64]{1,0:T(8,128)} %param.9) | copy-start | bytes 49156
  1.6 18.0 %collective-permute-start.1 = (bf16[1,64,256]{2,1,0:T(8,128)(2,1)S(1)}, bf16[1,64,256]{2,1,0:T(8,128)(2,1)S(1)}, u32[]{:S(2)}, u32[]{:S(2)}) collective-permute-start(bf16[1,64,256]{2,1,0:T(8,128)(2,1)S(1)} %get-tuple-element.47), channel_id=1, source_target_pairs={{0,24},{2,26},{4,28},{6,30},{8,16},{10,18},{12,20},{14,22},{16,8},... | collective-permute-start | bytes 98312 | tf_op jit(solution)/shard_map/ppermute | solution.py:45
  6.7 12.9 %collective-permute-start.2 = (bf16[1,64,256]{2,1,0:T(8,128)(2,1)S(1)}, bf16[1,64,256]{2,1,0:T(8,128)(2,1)S(1)}, u32[]{:S(2)}, u32[]{:S(2)}) collective-permute-start(bf16[1,64,256]{2,1,0:T(8,128)(2,1)S(1)} %get-tuple-element.47), channel_id=1, source_target_pairs={{0,16},{2,18},{4,20},{6,22},{8,24},{10,26},{12,28},{14,30},{16,0},... | collective-permute-start | bytes 98312 | tf_op jit(solution)/shard_map/ppermute | solution.py:45
  6.7 12.9 %collective-permute-start.3 = (bf16[1,64,256]{2,1,0:T(8,128)(2,1)S(1)}, bf16[1,64,256]{2,1,0:T(8,128)(2,1)S(1)}, u32[]{:S(2)}, u32[]{:S(2)}) collective-permute-start(bf16[1,64,256]{2,1,0:T(8,128)(2,1)S(1)} %get-tuple-element.47), channel_id=1, source_target_pairs={{0,8},{2,10},{4,12},{6,14},{8,0},{10,2},{12,4},{14,6},{16,24},{18,... | collective-permute-start | bytes 98312 | tf_op jit(solution)/shard_map/ppermute | solution.py:45
  8.6 21.2 %collective-permute-start = (bf16[1,384,256]{2,1,0:T(8,128)(2,1)S(1)}, bf16[1,384,256]{2,1,0:T(8,128)(2,1)S(1)}, u32[]{:S(2)}, u32[]{:S(2)}) collective-permute-start(bf16[1,384,256]{2,1,0:T(8,128)(2,1)S(1)} %get-tuple-element.33), channel_id=1, source_target_pairs={{0,1},{1,0},{2,3},{3,2},{4,5},{5,4},{6,7},{7,6},{8,9},{9,8},{10,11... | collective-permute-start | bytes 589832 | tf_op jit(solution)/shard_map/ppermute | solution.py:45
  9.9 2.2 %copy-start.10 = (s32[1,1,12,2]{2,3,1,0:T(2,128)S(1)}, s32[1,1,12,2]{2,3,1,0:T(2,128)}, u32[]{:S(2)}) copy-start(s32[1,1,12,2]{2,3,1,0:T(2,128)} %param.12) | copy-start | bytes 292
  14.4 2.6 %copy-start.5 = (f32[1,64,256]{2,1,0:T(8,128)S(1)}, f32[1,64,256]{2,1,0:T(8,128)}, u32[]{:S(2)}) copy-start(f32[1,64,256]{2,1,0:T(8,128)} %param.8) | copy-start | bytes 196612
  17.1 6.1 %copy-start.9 = (f32[64,64]{1,0:T(8,128)S(1)}, f32[64,64]{1,0:T(8,128)}, u32[]{:S(2)}) copy-start(f32[64,64]{1,0:T(8,128)} %param.10) | copy-start | bytes 49156
  19.6 7.0 %collective-permute-start.4 = (bf16[4,64,256]{2,1,0:T(8,128)(2,1)S(1)}, bf16[4,64,256]{2,1,0:T(8,128)(2,1)S(1)}, u32[]{:S(2)}, u32[]{:S(2)}) collective-permute-start(bf16[4,64,256]{2,1,0:T(8,128)(2,1)S(1)} %maximum_bitcast_fusion), channel_id=1, source_target_pairs={{0,6},{2,4},{4,2},{6,0},{8,14},{10,12},{12,10},{14,8},{16,22},{18,... | collective-permute-start | bytes 393224 | tf_op jit(solution)/shard_map/ppermute | solution.py:45
  22.3 7.0 %collective-permute-start.5 = (bf16[4,64,256]{2,1,0:T(8,128)(2,1)S(1)}, bf16[4,64,256]{2,1,0:T(8,128)(2,1)S(1)}, u32[]{:S(2)}, u32[]{:S(2)}) collective-permute-start(bf16[4,64,256]{2,1,0:T(8,128)(2,1)S(1)} %maximum_bitcast_fusion), channel_id=1, source_target_pairs={{0,4},{2,6},{4,0},{6,2},{8,12},{10,14},{12,8},{14,10},{16,20},{18,... | collective-permute-start | bytes 393224 | tf_op jit(solution)/shard_map/ppermute | solution.py:45
  22.8 6.7 %collective-permute-start.6 = (bf16[4,64,256]{2,1,0:T(8,128)(2,1)S(1)}, bf16[4,64,256]{2,1,0:T(8,128)(2,1)S(1)}, u32[]{:S(2)}, u32[]{:S(2)}) collective-permute-start(bf16[4,64,256]{2,1,0:T(8,128)(2,1)S(1)} %maximum_bitcast_fusion), channel_id=1, source_target_pairs={{0,2},{2,0},{4,6},{6,4},{8,10},{10,8},{12,14},{14,12},{16,18},{18,... | collective-permute-start | bytes 393224 | tf_op jit(solution)/shard_map/ppermute | solution.py:45
  29.7 1.7 %copy-start.2 = (bf16[96,8,4,256]{3,1,2,0:T(8,128)(2,1)S(1)}, bf16[96,8,4,256]{3,1,2,0:T(8,128)(2,1)}, u32[]{:S(2)}) copy-start(bf16[96,8,4,256]{3,1,2,0:T(8,128)(2,1)} %copy.72) | copy-start | bytes 4718596
  29.8 2.3 %copy-start.6 = (bf16[4,4,64,256]{3,2,1,0:T(8,128)(2,1)}, bf16[4,4,64,256]{3,2,1,0:T(8,128)(2,1)S(1)}, u32[]{:S(2)}) copy-start(bf16[4,4,64,256]{3,2,1,0:T(8,128)(2,1)S(1)} %copy.49) | copy-start | bytes 1572868
  29.9 2.2 %copy-start.8 = (bf16[1,2,384,256]{3,2,1,0:T(8,128)(2,1)}, bf16[1,2,384,256]{3,2,1,0:T(8,128)(2,1)S(1)}, u32[]{:S(2)}) copy-start(bf16[1,2,384,256]{3,2,1,0:T(8,128)(2,1)S(1)} %pad_maximum_fusion.2) | copy-start | bytes 1179652
  32.3 3.3 %copy-start.11 = (f32[4]{0:T(128)S(1)}, f32[4]{0:T(128)}, u32[]{:S(2)}) copy-start(f32[4]{0:T(128)} %add.138) | copy-start | bytes 52
  35.7 3.7 %collective-permute-start.7 = (f32[8,256]{1,0:T(8,128)S(1)}, f32[8,256]{1,0:T(8,128)S(1)}, u32[]{:S(2)}, u32[]{:S(2)}) collective-permute-start(f32[8,256]{1,0:T(8,128)S(1)} %pad.7), channel_id=1, source_target_pairs={{0,2},{2,0},{4,6},{6,4},{8,10},{10,8},{12,14},{14,12},{16,18},{18,... | collective-permute-start | bytes 24584 | tf_op jit(solution)/shard_map/ppermute | solution.py:45
  39.3 3.7 %collective-permute-start.8 = (f32[8,256]{1,0:T(8,128)S(1)}, f32[8,256]{1,0:T(8,128)S(1)}, u32[]{:S(2)}, u32[]{:S(2)}) collective-permute-start(f32[8,256]{1,0:T(8,128)S(1)} %pad_add_fusion.1), channel_id=1, source_target_pairs={{0,4},{2,6},{4,0},{6,2},{8,12},{10,14},{12,8},{14,10},{16,20},{18,... | collective-permute-start | bytes 24584 | tf_op jit(solution)/shard_map/ppermute | solution.py:45
  43.0 3.7 %collective-permute-start.9 = (f32[8,256]{1,0:T(8,128)S(1)}, f32[8,256]{1,0:T(8,128)S(1)}, u32[]{:S(2)}, u32[]{:S(2)}) collective-permute-start(f32[8,256]{1,0:T(8,128)S(1)} %fusion.55), channel_id=1, source_target_pairs={{0,8},{2,10},{4,12},{6,14},{8,0},{10,2},{12,4},{14,6},{16,24},{18,... | collective-permute-start | bytes 24584 | tf_op jit(solution)/shard_map/ppermute | solution.py:45
  44.3 11.5 %collective-permute-start.13 = (f32[2,2,2,64,256]{4,3,0,1,2:T(8,128)S(1)}, f32[2,2,2,64,256]{4,3,0,1,2:T(8,128)}, u32[]{:S(2)}, u32[]{:S(2)}) collective-permute-start(f32[2,2,2,64,256]{4,3,0,1,2:T(8,128)S(1)} %select_bitcast_fusion.1), channel_id=1, source_target_pairs={{0,2},{2,0},{4,6},{6,4},{8,10},{10,8},{12,14},{14,12},{16,18},{18,... | collective-permute-start | bytes 1572872 | tf_op jit(solution)/shard_map/ppermute | solution.py:45
  46.7 4.5 %collective-permute-start.10 = (f32[8,256]{1,0:T(8,128)S(1)}, f32[8,256]{1,0:T(8,128)S(1)}, u32[]{:S(2)}, u32[]{:S(2)}) collective-permute-start(f32[8,256]{1,0:T(8,128)S(1)} %add.148), channel_id=1, source_target_pairs={{0,16},{2,18},{4,20},{6,22},{8,24},{10,26},{12,28},{14,30},{16,0},... | collective-permute-start | bytes 24584 | tf_op jit(solution)/shard_map/ppermute | solution.py:45
  48.9 9.6 %copy-start.1 = (f32[1,384,256]{2,1,0:T(8,128)S(1)}, f32[1,384,256]{2,1,0:T(8,128)}, u32[]{:S(2)}) copy-start(f32[1,384,256]{2,1,0:T(8,128)} %param.7) | copy-start | bytes 1179652
  48.9 9.6 %collective-permute-start.12 = (bf16[384,256]{1,0:T(8,128)(2,1)S(1)}, bf16[384,256]{1,0:T(8,128)(2,1)S(1)}, u32[]{:S(2)}, u32[]{:S(2)}) collective-permute-start(bf16[384,256]{1,0:T(8,128)(2,1)S(1)} %select_convert_fusion.1), channel_id=1, source_target_pairs={{0,1},{1,0},{2,3},{3,2},{4,5},{5,4},{6,7},{7,6},{8,9},{9,8},{10,11... | collective-permute-start | bytes 589832 | tf_op jit(solution)/shard_map/ppermute | solution.py:45
  51.2 1.1 collective-permute-start.11
  57.0 6.4 %collective-permute-start.14 = (f32[2,2,64,256]{3,2,0,1:T(8,128)S(1)}, f32[2,2,64,256]{3,2,0,1:T(8,128)S(1)}, u32[]{:S(2)}, u32[]{:S(2)}) collective-permute-start(f32[2,2,64,256]{3,2,0,1:T(8,128)S(1)} %select_bitcast_fusion.3), channel_id=1, source_target_pairs={{0,4},{2,6},{4,0},{6,2},{8,12},{10,14},{12,8},{14,10},{16,20},{18,... | collective-permute-start | bytes 786440 | tf_op jit(solution)/shard_map/ppermute | solution.py:45
  61.2 11.1 %collective-permute-start.17 = (bf16[1,384,256]{2,1,0:T(8,128)(2,1)S(1)}, bf16[1,384,256]{2,1,0:T(8,128)(2,1)S(1)}, u32[]{:S(2)}, u32[]{:S(2)}) collective-permute-start(bf16[1,384,256]{2,1,0:T(8,128)(2,1)S(1)} %get-tuple-element.12), channel_id=1, source_target_pairs={{0,1},{1,0},{2,3},{3,2},{4,5},{5,4},{6,7},{7,6},{8,9},{9,8},{10,11... | collective-permute-start | bytes 589832 | tf_op jit(solution)/shard_map/ppermute | solution.py:45
  63.5 5.0 %collective-permute-start.15 = (f32[2,64,256]{2,1,0:T(8,128)S(1)}, f32[2,64,256]{2,1,0:T(8,128)S(1)}, u32[]{:S(2)}, u32[]{:S(2)}) collective-permute-start(f32[2,64,256]{2,1,0:T(8,128)S(1)} %select_bitcast_fusion.13), channel_id=1, source_target_pairs={{0,8},{2,10},{4,12},{6,14},{8,0},{10,2},{12,4},{14,6},{16,24},{18,... | collective-permute-start | bytes 393224 | tf_op jit(solution)/shard_map/ppermute | solution.py:45
  68.6 6.5 %collective-permute-start.16 = (f32[64,256]{1,0:T(8,128)S(1)}, f32[64,256]{1,0:T(8,128)S(1)}, u32[]{:S(2)}, u32[]{:S(2)}) collective-permute-start(f32[64,256]{1,0:T(8,128)S(1)} %select_bitcast_fusion.19), channel_id=1, source_target_pairs={{0,16},{2,18},{4,20},{6,22},{8,24},{10,26},{12,28},{14,30},{16,0},... | collective-permute-start | bytes 196616 | tf_op jit(solution)/shard_map/ppermute | solution.py:45
  75.1 5.8 %collective-permute-start.18 = (bf16[1,64,256]{2,1,0:T(8,128)(2,1)S(1)}, bf16[1,64,256]{2,1,0:T(8,128)(2,1)S(1)}, u32[]{:S(2)}, u32[]{:S(2)}) collective-permute-start(bf16[1,64,256]{2,1,0:T(8,128)(2,1)S(1)} %get-tuple-element.15), channel_id=1, source_target_pairs={{0,24},{2,26},{4,28},{6,30},{8,16},{10,18},{12,20},{14,22},{16,8},... | collective-permute-start | bytes 98312 | tf_op jit(solution)/shard_map/ppermute | solution.py:45
  76.8 4.8 %collective-permute-start.19 = (bf16[1,64,256]{2,1,0:T(8,128)(2,1)S(1)}, bf16[1,64,256]{2,1,0:T(8,128)(2,1)S(1)}, u32[]{:S(2)}, u32[]{:S(2)}) collective-permute-start(bf16[1,64,256]{2,1,0:T(8,128)(2,1)S(1)} %get-tuple-element.15), channel_id=1, source_target_pairs={{0,16},{2,18},{4,20},{6,22},{8,24},{10,26},{12,28},{14,30},{16,0},... | collective-permute-start | bytes 98312 | tf_op jit(solution)/shard_map/ppermute | solution.py:45
  77.7 4.2 %collective-permute-start.20 = (bf16[1,64,256]{2,1,0:T(8,128)(2,1)S(1)}, bf16[1,64,256]{2,1,0:T(8,128)(2,1)S(1)}, u32[]{:S(2)}, u32[]{:S(2)}) collective-permute-start(bf16[1,64,256]{2,1,0:T(8,128)(2,1)S(1)} %get-tuple-element.15), channel_id=1, source_target_pairs={{0,8},{2,10},{4,12},{6,14},{8,0},{10,2},{12,4},{14,6},{16,24},{18,... | collective-permute-start | bytes 98312 | tf_op jit(solution)/shard_map/ppermute | solution.py:45
  79.6 13.2 %copy-start.7 = (bf16[1,2,384,256]{3,2,1,0:T(8,128)(2,1)}, bf16[1,2,384,256]{3,2,1,0:T(8,128)(2,1)S(1)}, u32[]{:S(2)}) copy-start(bf16[1,2,384,256]{3,2,1,0:T(8,128)(2,1)S(1)} %pad_maximum_fusion.3) | copy-start | bytes 1179652
  82.0 5.9 %collective-permute-start.21 = (bf16[4,64,256]{2,1,0:T(8,128)(2,1)S(1)}, bf16[4,64,256]{2,1,0:T(8,128)(2,1)S(1)}, u32[]{:S(2)}, u32[]{:S(2)}) collective-permute-start(bf16[4,64,256]{2,1,0:T(8,128)(2,1)S(1)} %maximum_bitcast_fusion.1), channel_id=1, source_target_pairs={{0,6},{2,4},{4,2},{6,0},{8,14},{10,12},{12,10},{14,8},{16,22},{18,... | collective-permute-start | bytes 393224 | tf_op jit(solution)/shard_map/ppermute | solution.py:45
  83.5 6.1 %collective-permute-start.22 = (bf16[4,64,256]{2,1,0:T(8,128)(2,1)S(1)}, bf16[4,64,256]{2,1,0:T(8,128)(2,1)S(1)}, u32[]{:S(2)}, u32[]{:S(2)}) collective-permute-start(bf16[4,64,256]{2,1,0:T(8,128)(2,1)S(1)} %maximum_bitcast_fusion.1), channel_id=1, source_target_pairs={{0,4},{2,6},{4,0},{6,2},{8,12},{10,14},{12,8},{14,10},{16,20},{18,... | collective-permute-start | bytes 393224 | tf_op jit(solution)/shard_map/ppermute | solution.py:45
  86.2 6.4 %collective-permute-start.23 = (bf16[4,64,256]{2,1,0:T(8,128)(2,1)S(1)}, bf16[4,64,256]{2,1,0:T(8,128)(2,1)S(1)}, u32[]{:S(2)}, u32[]{:S(2)}) collective-permute-start(bf16[4,64,256]{2,1,0:T(8,128)(2,1)S(1)} %maximum_bitcast_fusion.1), channel_id=1, source_target_pairs={{0,2},{2,0},{4,6},{6,4},{8,10},{10,8},{12,14},{14,12},{16,18},{18,... | collective-permute-start | bytes 393224 | tf_op jit(solution)/shard_map/ppermute | solution.py:45
  92.6 1.4 %copy-start.3 = (bf16[96,8,4,256]{3,1,2,0:T(8,128)(2,1)S(1)}, bf16[96,8,4,256]{3,1,2,0:T(8,128)(2,1)}, u32[]{:S(2)}) copy-start(bf16[96,8,4,256]{3,1,2,0:T(8,128)(2,1)} %copy.72) | copy-start | bytes 4718596
  97.2 18.6 %collective-permute-start.30 = (f32[2,2,2,64,256]{4,3,0,1,2:T(8,128)S(1)}, f32[2,2,2,64,256]{4,3,0,1,2:T(8,128)S(1)}, u32[]{:S(2)}, u32[]{:S(2)}) collective-permute-start(f32[2,2,2,64,256]{4,3,0,1,2:T(8,128)S(1)} %select_bitcast_fusion), channel_id=1, source_target_pairs={{0,2},{2,0},{4,6},{6,4},{8,10},{10,8},{12,14},{14,12},{16,18},{18,... | collective-permute-start | bytes 1572872 | tf_op jit(solution)/shard_map/ppermute | solution.py:45
  97.4 9.2 %collective-permute-start.24 = (f32[8,256]{1,0:T(8,128)S(1)}, f32[8,256]{1,0:T(8,128)S(1)}, u32[]{:S(2)}, u32[]{:S(2)}) collective-permute-start(f32[8,256]{1,0:T(8,128)S(1)} %pad.8), channel_id=1, source_target_pairs={{0,2},{2,0},{4,6},{6,4},{8,10},{10,8},{12,14},{14,12},{16,18},{18,... | collective-permute-start | bytes 24584 | tf_op jit(solution)/shard_map/ppermute | solution.py:45
  106.5 3.7 %collective-permute-start.25 = (f32[8,256]{1,0:T(8,128)S(1)}, f32[8,256]{1,0:T(8,128)S(1)}, u32[]{:S(2)}, u32[]{:S(2)}) collective-permute-start(f32[8,256]{1,0:T(8,128)S(1)} %pad_add_fusion), channel_id=1, source_target_pairs={{0,4},{2,6},{4,0},{6,2},{8,12},{10,14},{12,8},{14,10},{16,20},{18,... | collective-permute-start | bytes 24584 | tf_op jit(solution)/shard_map/ppermute | solution.py:45
  110.2 3.7 %collective-permute-start.26 = (f32[8,256]{1,0:T(8,128)S(1)}, f32[8,256]{1,0:T(8,128)S(1)}, u32[]{:S(2)}, u32[]{:S(2)}) collective-permute-start(f32[8,256]{1,0:T(8,128)S(1)} %fusion.54), channel_id=1, source_target_pairs={{0,8},{2,10},{4,12},{6,14},{8,0},{10,2},{12,4},{14,6},{16,24},{18,... | collective-permute-start | bytes 24584 | tf_op jit(solution)/shard_map/ppermute | solution.py:45
  113.8 4.5 %collective-permute-start.27 = (f32[8,256]{1,0:T(8,128)S(1)}, f32[8,256]{1,0:T(8,128)S(1)}, u32[]{:S(2)}, u32[]{:S(2)}) collective-permute-start(f32[8,256]{1,0:T(8,128)S(1)} %add.166), channel_id=1, source_target_pairs={{0,16},{2,18},{4,20},{6,22},{8,24},{10,26},{12,28},{14,30},{16,0},... | collective-permute-start | bytes 24584 | tf_op jit(solution)/shard_map/ppermute | solution.py:45
  115.9 14.1 %copy-start.4 = (f32[384,256]{1,0:T(8,128)S(1)}, f32[384,256]{1,0:T(8,128)}, u32[]{:S(2)}) copy-start(f32[384,256]{1,0:T(8,128)} %get-tuple-element.14) | copy-start | bytes 1179652
  116.0 6.4 %collective-permute-start.31 = (f32[2,2,64,256]{3,2,0,1:T(8,128)S(1)}, f32[2,2,64,256]{3,2,0,1:T(8,128)S(1)}, u32[]{:S(2)}, u32[]{:S(2)}) collective-permute-start(f32[2,2,64,256]{3,2,0,1:T(8,128)S(1)} %select_bitcast_fusion.2), channel_id=1, source_target_pairs={{0,4},{2,6},{4,0},{6,2},{8,12},{10,14},{12,8},{14,10},{16,20},{18,... | collective-permute-start | bytes 786440 | tf_op jit(solution)/shard_map/ppermute | solution.py:45
  116.1 14.0 %collective-permute-start.29 = (bf16[384,256]{1,0:T(8,128)(2,1)S(1)}, bf16[384,256]{1,0:T(8,128)(2,1)S(1)}, u32[]{:S(2)}, u32[]{:S(2)}) collective-permute-start(bf16[384,256]{1,0:T(8,128)(2,1)S(1)} %select_convert_fusion), channel_id=1, source_target_pairs={{0,1},{1,0},{2,3},{3,2},{4,5},{5,4},{6,7},{7,6},{8,9},{9,8},{10,11... | collective-permute-start | bytes 589832 | tf_op jit(solution)/shard_map/ppermute | solution.py:45
  118.4 1.1 collective-permute-start.28
  123.1 5.4 %collective-permute-start.32 = (f32[2,64,256]{2,1,0:T(8,128)}, f32[2,64,256]{2,1,0:T(8,128)S(1)}, u32[]{:S(2)}, u32[]{:S(2)}) collective-permute-start(f32[2,64,256]{2,1,0:T(8,128)} %select_bitcast_fusion.8), channel_id=1, source_target_pairs={{0,8},{2,10},{4,12},{6,14},{8,0},{10,2},{12,4},{14,6},{16,24},{18,... | collective-permute-start | bytes 393224 | tf_op jit(solution)/shard_map/ppermute | solution.py:45
  128.6 5.2 %collective-permute-start.33 = (f32[64,256]{1,0:T(8,128)S(1)}, f32[64,256]{1,0:T(8,128)S(1)}, u32[]{:S(2)}, u32[]{:S(2)}) collective-permute-start(f32[64,256]{1,0:T(8,128)S(1)} %select_bitcast_fusion.18), channel_id=1, source_target_pairs={{0,16},{2,18},{4,20},{6,22},{8,24},{10,26},{12,28},{14,30},{16,0},... | collective-permute-start | bytes 196616 | tf_op jit(solution)/shard_map/ppermute | solution.py:45

commit v6 on v5

--- a/solution.py
+++ b/solution.py
@@ -58,22 +58,33 @@
     size, bits = bit_count(axis)
     me = lax.axis_index(axis)
     rows, width = part.shape[0] // size, part.shape[1]
+    groups = [list(range(bits))[i : i + 2] for i in range(0, bits, 2)]
     left = list(range(bits))[::-1]
     buf = part.reshape([2] * bits + [rows, width])
-    for bit in range(bits):
-        pos = left.index(bit)
-        low = lax.index_in_dim(buf, 0, pos, keepdims=False)
-        high = lax.index_in_dim(buf, 1, pos, keepdims=False)
-        upper = ((me >> bit) & 1) == 1
-        keep = jnp.where(upper, high, low)
-        send = jnp.where(upper, low, high).astype(send_type)
-        if extra is None:
-            buf = keep + swap_with(send, axis, size, bit).astype(jnp.float32)
-        else:
-            got, got_extra = swap_with((send, extra), axis, size, bit)
-            buf = keep + got
-            extra = extra + got_extra
-        left.remove(bit)
+    for group in groups:
+        masks = [sum(1 << group[j] for j in range(len(group)) if (k >> j) & 1) for k in range(1 << len(group))]
+        digit = sum(((me >> group[j]) & 1) << j for j in range(len(group)))
+
+        def block_of(value):
+            out = buf
+            for j in sorted(range(len(group)), key=lambda j: -left.index(group[j])):
+                out = lax.dynamic_index_in_dim(out, (value >> j) & 1, left.index(group[j]), keepdims=False)
+            return out
+
+        total = block_of(digit)
+        sent_extra = extra
+        for k in range(1, len(masks)):
+            send = block_of(digit ^ k).astype(send_type)
+            if extra is None:
+                total = total + swap_with(send, axis, size, None, masks[k]).astype(jnp.float32)
+            else:
+                message = jnp.concatenate([send.reshape(-1, width), sent_extra])
+                got = swap_with(message, axis, size, None, masks[k])
+                total = total + got[: -extra.shape[0]].reshape(total.shape)
+                extra = extra + got[-extra.shape[0] :]
+        for bit in group:
+            left.remove(bit)
+        buf = total
     return buf.reshape(rows, width), extra
 
 

time: 135 us -> 132 us (0.978)
  waiting for transfers between devices: 59.8 us -> 41.2 us
  local copies, waits for them, and re-layouts: 10.2 us -> 19.2 us
  matrix products: 9.58 us -> 14.9 us
  other arithmetic: 15.1 us -> 20.1 us
  starting transfers between devices: 37.9 us -> 33.4 us
    ppermute x34 -> x30, waiting for transfers between devices: 59.8 us -> 41.2 us  [swap_with(): return lax.ppermute(value, axis, pairs)]
    ppermute x34 -> x30, starting transfers between devices: 37.9 us -> 33.4 us  [swap_with(): return lax.ppermute(value, axis, pairs)]
    dot_general x2, matrix products: 1.38 us -> 5.81 us  [cross_parts(): jnp.dot(counts_bf, item_range, preferred_element_type=jnp.float32)]
    slice x2 -> x12, local copies, waits for them, and re-layouts: 1.39 us -> 5.82 us  [the longest x6 5.81 us: halve_sum(): total = total + got[:-extra.shape[0]].reshape(total.shape)]
    concatenate x0 -> x4, other arithmetic: none -> 2.36 us  [halve_sum(): message = jnp.concatenate([send.reshape(-1, width), sent_extra])]
    unnamed x27 -> x67, local copies, waits for them, and re-layouts: 5.53 us -> 7.37 us
    dynamic_slice x0 -> x8, local copies, waits for them, and re-layouts: none -> 1.54 us  [block_of(): lax.dynamic_index_in_dim(out, value >> j & 1, left.index(group[j]), keepd...]
  transfers between devices with their start and end apart: 34 -> 30, of which waited for: 26 -> 17; matrix products, arithmetic and copies ran while one was open for 17% -> 20% of each run, Pallas kernels for 0% -> 0%
where the time goes in v6:
time: 132 us; the launch traced here: 131 us
  waiting for transfers between devices  41.2 us (31%)
  starting transfers between devices  33.4 us (25%)
  other arithmetic  20.1 us (15%)
  local copies, waits for them, and re-layouts  19.2 us (15%)
  matrix products  14.9 us (11%)
  between operations  2.02 us (2%)
    ppermute x30, waiting for transfers between devices, swap_with(): return lax.ppermute(value, axis, pairs)  41.2 us
    ppermute x30, starting transfers between devices, swap_with(): return lax.ppermute(value, axis, pairs)  33.4 us
    unnamed x67, local copies, waits for them, and re-layouts  7.37 us
    dot_general x2, matrix products, cross_parts(): jnp.dot(counts_bf, item_range, preferred_element_type=jnp.float32)  5.81 us
    slice x6, local copies, waits for them, and re-layouts, halve_sum(): total = total + got[:-extra.shape[0]].reshape(total.shape)  5.81 us
    dot_general x2, matrix products, cross_parts(): lax.dot_general(counts_bf, user_range, (((0,), (0,)), ((), ())), preferre...  4.69 us
    broadcast_in_dim x2, other arithmetic, per_device(): return (sol_user[None], sol_item[None], res_user[None], res_item[None])  2.84 us
    dot_general x4, matrix products, prior_term(): mixed = jnp.einsum('nde,ef->ndf', grouped, prior_mat, precision=top_prec)  2.79 us
  transfers between devices with their start and end apart: 30, of which 17 were waited for; matrix products, arithmetic and copies ran while one was open for 20% of the time, Pallas kernels for 0%

profile of v6, /device:TPU:0, one launch (start us, length us, event | category | flops | bytes accessed | tf_op | source)
XLA Modules:
  0.0 130.9 jit_solution(7894910386462623939)
XLA Ops:
  0.6 0.9 multiply_reduce_fusion.6
  1.6 5.1 %collective-permute-start.1 = (bf16[1,64,256]{2,1,0:T(8,128)(2,1)S(1)}, bf16[1,64,256]{2,1,0:T(8,128)(2,1)S(1)}, u32[]{:S(2)}, u32[]{:S(2)}) collective-permute-start(bf16[1,64,256]{2,1,0:T(8,128)(2,1)S(1)} %get-tuple-element.60), channel_id=1, source_target_pairs={{0,24},{2,26},{4,28},{6,30},{8,16},{10,18},{12,20},{14,22},{16,8},... | collective-permute-start | bytes 98312 | tf_op jit(solution)/shard_map/ppermute | solution.py:45
  7.3 1.2 copy.43
  9.2 2.2 %convert_bitcast_fusion = bf16[12,256,256]{2,1,0:T(8,128)(2,1)S(1)} fusion(s32[1,1,12,256,256]{4,3,2,1,0:T(8,128)} %param.11), kind=kLoop, calls=%fused_computation.6 | loop fusion | flops 786432 | bytes 4718592 | tf_op jit(solution)/shard_map/convert_element_type | solution.py:124
  12.1 1.6 %bitcast_convert_fusion = (bf16[3,256,4,256]{3,2,1,0:T(4,128)(2,1)S(1)}, f32[3,4,256,256]{3,1,2,0:T(4,128)S(1)}) fusion(bf16[12,256,256]{2,1,0:T(8,128)(2,1)S(1)} %convert_bitcast_fusion, pred[12,4]{0,1:T(4,128)(4,1)S(1)} %fusion.51, pred[12,3]{0,1:T(4,128)(4,1)S(1)} %fusion.50), kind=kOutput, calls=%fused_computation.2 | convolution fusion | flops 19660944 | bytes 6291540 | tf_op jit(solution)/shard_map/trc,tij->ricj/dot_general | solution.py:121
  13.8 1.9 %bitcast_reduce_fusion = (f32[4,256]{1,0:T(4,128)S(1)}, f32[3,256]{1,0:T(4,128)S(1)}) fusion(f32[3,4,256,256]{3,1,2,0:T(4,128)S(1)} %get-tuple-element.76), kind=kLoop, calls=%fused_computation | loop fusion | flops 1571072 | bytes 3152896 | tf_op jit(solution)/shard_map/reduce_sum | solution.py:128
  15.7 1.1 multiply_reduce_fusion.1
  17.1 1.5 %copy.71 = bf16[96,8,4,256]{3,1,2,0:T(8,128)(2,1)} copy(bf16[96,8,4,256]{3,2,1,0:T(4,128)(2,1)S(1)} %bitcast.264) | data formatting | bytes 3145728
  19.7 2.7 %collective-permute-start.4 = (bf16[4,64,256]{2,1,0:T(8,128)(2,1)S(1)}, bf16[4,64,256]{2,1,0:T(8,128)(2,1)S(1)}, u32[]{:S(2)}, u32[]{:S(2)}) collective-permute-start(bf16[4,64,256]{2,1,0:T(8,128)(2,1)S(1)} %maximum_bitcast_fusion), channel_id=1, source_target_pairs={{0,6},{2,4},{4,2},{6,0},{8,14},{10,12},{12,10},{14,8},{16,22},{18,... | collective-permute-start | bytes 393224 | tf_op jit(solution)/shard_map/ppermute | solution.py:45
  23.3 0.9 multiply_reduce_fusion.3
  24.2 2.5 %collective-permute-done.4 = bf16[4,64,256]{2,1,0:T(8,128)(2,1)S(1)} collective-permute-done((bf16[4,64,256]{2,1,0:T(8,128)(2,1)S(1)}, bf16[4,64,256]{2,1,0:T(8,128)(2,1)S(1)}, u32[]{:S(2)}, u32[]{:S(2)}) %collective-permute-start.4) | collective-permute-done | bytes 131104 | tf_op jit(solution)/shard_map/ppermute | solution.py:45
  26.7 2.7 %collective-permute-done.5 = bf16[4,64,256]{2,1,0:T(8,128)(2,1)S(1)} collective-permute-done((bf16[4,64,256]{2,1,0:T(8,128)(2,1)S(1)}, bf16[4,64,256]{2,1,0:T(8,128)(2,1)S(1)}, u32[]{:S(2)}, u32[]{:S(2)}) %collective-permute-start.5) | collective-permute-done | bytes 131104 | tf_op jit(solution)/shard_map/ppermute | solution.py:45
  29.9 1.2 select_bitcast_fusion.3
  31.1 0.9 copy.48
  32.1 2.6 %fusion.5 = (f32[256]{0:T(256)S(1)}, f32[768,256]{1,0:T(8,128)}) fusion(bf16[1,2,384,256]{3,2,1,0:T(8,128)(2,1)} %copy.48, bf16[768,256]{1,0:T(8,128)(2,1)} %bitcast.293, f32[768]{0:T(1024)S(1)} %mul.189, bf16[768,1024]{1,0:T(8,128)(2,1)S(1)} %bitcast.266, bf16[1024,256]{1,0:T(8,128)(2,1)S(1)} %bitcast.285), kind=kOutput, calls=%fused_computation.21 | convolution fusion | flops 403832576 | bytes 3674112 | tf_op jit(solution)/shard_map/dot_general | solution.py:132
  34.9 2.6 %fusion.3 = (f32[256]{0:T(256)}, f32[1024,256]{1,0:T(8,128)S(1)}) fusion(bf16[4,4,64,256]{3,2,1,0:T(8,128)(2,1)} %copy-done.7, bf16[1024,256]{1,0:T(8,128)(2,1)} %bitcast.286, f32[1024]{0:T(1024)S(1)} %bitcast.300, bf16[768,1024]{1,0:T(8,128)(2,1)S(1)} %bitcast.267, bf16[768,256]{1,0:T(8,128)(2,1)} %bitcast.294), kind=kOutput, calls=%fused_computation.15 | convolution fusion | flops 404225792 | bytes 4068352 | tf_op jit(solution)/shard_map/dot_general | solution.py:134
  37.6 0.8 reduce_sum.173
  38.5 0.7 maximum_bitcast_fusion.2
  39.9 0.8 pad_maximum_fusion.4
  40.6 1.5 %collective-permute-start.9 = (f32[264,256]{1,0:T(8,128)}, f32[264,256]{1,0:T(8,128)}, u32[]{:S(2)}, u32[]{:S(2)}) collective-permute-start(f32[264,256]{1,0:T(8,128)} %get-tuple-element.71), channel_id=1, source_target_pairs={{0,6},{2,4},{4,2},{6,0},{8,14},{10,12},{12,10},{14,8},{16,22},{18,... | collective-permute-start | bytes 811016 | tf_op jit(solution)/shard_map/ppermute | solution.py:45
  42.2 1.4 %collective-permute-start.8 = (f32[264,256]{1,0:T(8,128)S(1)}, f32[264,256]{1,0:T(8,128)}, u32[]{:S(2)}, u32[]{:S(2)}) collective-permute-start(f32[264,256]{1,0:T(8,128)S(1)} %get-tuple-element.72), channel_id=1, source_target_pairs={{0,4},{2,6},{4,0},{6,2},{8,12},{10,14},{12,8},{14,10},{16,20},{18,... | collective-permute-start | bytes 811016 | tf_op jit(solution)/shard_map/ppermute | solution.py:45
  44.2 0.8 reshape.253
  45.0 0.8 copy.69
  45.8 5.4 %collective-permute-done.9 = f32[264,256]{1,0:T(8,128)} collective-permute-done((f32[264,256]{1,0:T(8,128)}, f32[264,256]{1,0:T(8,128)}, u32[]{:S(2)}, u32[]{:S(2)}) %collective-permute-start.9) | collective-permute-done | bytes 270368 | tf_op jit(solution)/shard_map/ppermute | solution.py:45
  51.2 1.0 slice.133
  52.2 3.6 %collective-permute-done.8 = f32[264,256]{1,0:T(8,128)} collective-permute-done((f32[264,256]{1,0:T(8,128)S(1)}, f32[264,256]{1,0:T(8,128)}, u32[]{:S(2)}, u32[]{:S(2)}) %collective-permute-start.8) | collective-permute-done | bytes 270368 | tf_op jit(solution)/shard_map/ppermute | solution.py:45
  55.8 1.0 slice.132
  56.8 1.0 slice.131
  57.9 0.7 slice_add_fusion.9
  58.7 3.7 %collective-permute-start.12 = (f32[72,256]{1,0:T(8,128)S(1)}, f32[72,256]{1,0:T(8,128)S(1)}, u32[]{:S(2)}, u32[]{:S(2)}) collective-permute-start(f32[72,256]{1,0:T(8,128)S(1)} %get-tuple-element.69), channel_id=1, source_target_pairs={{0,24},{2,26},{4,28},{6,30},{8,16},{10,18},{12,20},{14,22},{16,8},... | collective-permute-start | bytes 221192 | tf_op jit(solution)/shard_map/ppermute | solution.py:45
  62.3 0.8 collective-permute-start.10
  63.3 2.4 %collective-permute-done.12 = f32[72,256]{1,0:T(8,128)S(1)} collective-permute-done((f32[72,256]{1,0:T(8,128)S(1)}, f32[72,256]{1,0:T(8,128)S(1)}, u32[]{:S(2)}, u32[]{:S(2)}) %collective-permute-start.12) | collective-permute-done | bytes 73760 | tf_op jit(solution)/shard_map/ppermute | solution.py:45
  65.7 2.8 %collective-permute-done.11 = f32[72,256]{1,0:T(8,128)S(1)} collective-permute-done((f32[72,256]{1,0:T(8,128)S(1)}, f32[72,256]{1,0:T(8,128)S(1)}, u32[]{:S(2)}, u32[]{:S(2)}) %collective-permute-start.11) | collective-permute-done | bytes 73760 | tf_op jit(solution)/shard_map/ppermute | solution.py:45
  68.6 1.1 collective-permute-done.13
  71.0 2.4 %collective-permute-start.16 = (bf16[1,64,256]{2,1,0:T(8,128)(2,1)S(1)}, bf16[1,64,256]{2,1,0:T(8,128)(2,1)S(1)}, u32[]{:S(2)}, u32[]{:S(2)}) collective-permute-start(bf16[1,64,256]{2,1,0:T(8,128)(2,1)S(1)} %get-tuple-element.22), channel_id=1, source_target_pairs={{0,24},{2,26},{4,28},{6,30},{8,16},{10,18},{12,20},{14,22},{16,8},... | collective-permute-start | bytes 98312 | tf_op jit(solution)/shard_map/ppermute | solution.py:45
  73.5 1.9 %collective-permute-start.18 = (bf16[1,64,256]{2,1,0:T(8,128)(2,1)S(1)}, bf16[1,64,256]{2,1,0:T(8,128)(2,1)S(1)}, u32[]{:S(2)}, u32[]{:S(2)}) collective-permute-start(bf16[1,64,256]{2,1,0:T(8,128)(2,1)S(1)} %get-tuple-element.22), channel_id=1, source_target_pairs={{0,8},{2,10},{4,12},{6,14},{8,0},{10,2},{12,4},{14,6},{16,24},{18,... | collective-permute-start | bytes 98312 | tf_op jit(solution)/shard_map/ppermute | solution.py:45
  75.4 1.0 convert_bitcast_fusion.2
  77.5 0.7 collective-permute-done.17
  78.3 1.4 %collective-permute-start.19 = (bf16[4,64,256]{2,1,0:T(8,128)(2,1)S(1)}, bf16[4,64,256]{2,1,0:T(8,128)(2,1)S(1)}, u32[]{:S(2)}, u32[]{:S(2)}) collective-permute-start(bf16[4,64,256]{2,1,0:T(8,128)(2,1)S(1)} %maximum_bitcast_fusion.1), channel_id=1, source_target_pairs={{0,6},{2,4},{4,2},{6,0},{8,14},{10,12},{12,10},{14,8},{16,22},{18,... | collective-permute-start | bytes 393224 | tf_op jit(solution)/shard_map/ppermute | solution.py:45
  79.7 1.8 %collective-permute-start.20 = (bf16[4,64,256]{2,1,0:T(8,128)(2,1)S(1)}, bf16[4,64,256]{2,1,0:T(8,128)(2,1)S(1)}, u32[]{:S(2)}, u32[]{:S(2)}) collective-permute-start(bf16[4,64,256]{2,1,0:T(8,128)(2,1)S(1)} %maximum_bitcast_fusion.1), channel_id=1, source_target_pairs={{0,4},{2,6},{4,0},{6,2},{8,12},{10,14},{12,8},{14,10},{16,20},{18,... | collective-permute-start | bytes 393224 | tf_op jit(solution)/shard_map/ppermute | solution.py:45
  83.1 2.6 %collective-permute-done.19 = bf16[4,64,256]{2,1,0:T(8,128)(2,1)S(1)} collective-permute-done((bf16[4,64,256]{2,1,0:T(8,128)(2,1)S(1)}, bf16[4,64,256]{2,1,0:T(8,128)(2,1)S(1)}, u32[]{:S(2)}, u32[]{:S(2)}) %collective-permute-start.19) | collective-permute-done | bytes 131104 | tf_op jit(solution)/shard_map/ppermute | solution.py:45
  85.6 1.6 %collective-permute-done.20 = bf16[4,64,256]{2,1,0:T(8,128)(2,1)S(1)} collective-permute-done((bf16[4,64,256]{2,1,0:T(8,128)(2,1)S(1)}, bf16[4,64,256]{2,1,0:T(8,128)(2,1)S(1)}, u32[]{:S(2)}, u32[]{:S(2)}) %collective-permute-start.20) | collective-permute-done | bytes 131104 | tf_op jit(solution)/shard_map/ppermute | solution.py:45
  88.8 3.2 %fusion.6 = (f32[256]{0:T(256)S(1)}, f32[768,256]{1,0:T(8,128)}) fusion(bf16[1,2,384,256]{3,2,1,0:T(8,128)(2,1)S(1)} %copy.58, bf16[768,256]{1,0:T(8,128)(2,1)S(1)} %bitcast.295, f32[768]{0:T(1024)S(1)} %copy-done.21, bf16[768,1024]{1,0:T(8,128)(2,1)} %bitcast.265, bf16[1024,256]{1,0:T(8,128)(2,1)S(1)} %bitcast.287), kind=kOutput, calls=%fused_computation.22 | convolution fusion | flops 403832576 | bytes 3674112 | tf_op jit(solution)/shard_map/dot_general | solution.py:132
  91.9 2.1 %fusion.4 = (f32[256]{0:T(256)S(1)}, f32[1024,256]{1,0:T(8,128)S(1)}) fusion(bf16[4,4,64,256]{3,2,1,0:T(8,128)(2,1)} %copy-done.8, bf16[1024,256]{1,0:T(8,128)(2,1)} %bitcast.288, f32[1024]{0:T(1024)S(1)} %bitcast.301, bf16[768,1024]{1,0:T(8,128)(2,1)S(1)} %bitcast.268, bf16[768,256]{1,0:T(8,128)(2,1)} %bitcast.296), kind=kOutput, calls=%fused_computation.16 | convolution fusion | flops 404225792 | bytes 4068352 | tf_op jit(solution)/shard_map/dot_general | solution.py:134
  94.6 0.9 pad_maximum_fusion.7
  95.5 1.4 %collective-permute-start.24 = (f32[264,256]{1,0:T(8,128)}, f32[264,256]{1,0:T(8,128)}, u32[]{:S(2)}, u32[]{:S(2)}) collective-permute-start(f32[264,256]{1,0:T(8,128)} %get-tuple-element.65), channel_id=1, source_target_pairs={{0,6},{2,4},{4,2},{6,0},{8,14},{10,12},{12,10},{14,8},{16,22},{18,... | collective-permute-start | bytes 811016 | tf_op jit(solution)/shard_map/ppermute | solution.py:45
  96.9 1.5 %collective-permute-start.23 = (f32[264,256]{1,0:T(8,128)}, f32[264,256]{1,0:T(8,128)}, u32[]{:S(2)}, u32[]{:S(2)}) collective-permute-start(f32[264,256]{1,0:T(8,128)} %get-tuple-element.66), channel_id=1, source_target_pairs={{0,4},{2,6},{4,0},{6,2},{8,12},{10,14},{12,8},{14,10},{16,20},{18,... | collective-permute-start | bytes 811016 | tf_op jit(solution)/shard_map/ppermute | solution.py:45
  99.2 6.9 %collective-permute-done.24 = f32[264,256]{1,0:T(8,128)} collective-permute-done((f32[264,256]{1,0:T(8,128)}, f32[264,256]{1,0:T(8,128)}, u32[]{:S(2)}, u32[]{:S(2)}) %collective-permute-start.24) | collective-permute-done | bytes 270368 | tf_op jit(solution)/shard_map/ppermute | solution.py:45
  106.1 1.0 slice.149
  107.1 3.6 %collective-permute-done.23 = f32[264,256]{1,0:T(8,128)} collective-permute-done((f32[264,256]{1,0:T(8,128)}, f32[264,256]{1,0:T(8,128)}, u32[]{:S(2)}, u32[]{:S(2)}) %collective-permute-start.23) | collective-permute-done | bytes 270368 | tf_op jit(solution)/shard_map/ppermute | solution.py:45
  110.6 1.0 slice.148
  111.6 1.0 slice.147
  112.6 1.0 fusion.21
  113.7 0.8 slice_add_fusion.6
  115.2 2.4 %collective-permute-start.27 = (f32[72,256]{1,0:T(8,128)}, f32[72,256]{1,0:T(8,128)S(1)}, u32[]{:S(2)}, u32[]{:S(2)}) collective-permute-start(f32[72,256]{1,0:T(8,128)} %get-tuple-element.63), channel_id=1, source_target_pairs={{0,24},{2,26},{4,28},{6,30},{8,16},{10,18},{12,20},{14,22},{16,8},... | collective-permute-start | bytes 221192 | tf_op jit(solution)/shard_map/ppermute | solution.py:45
  117.6 2.0 %collective-permute-start.25 = (f32[72,256]{1,0:T(8,128)}, f32[72,256]{1,0:T(8,128)S(1)}, u32[]{:S(2)}, u32[]{:S(2)}) collective-permute-start(f32[72,256]{1,0:T(8,128)} %get-tuple-element.61), channel_id=1, source_target_pairs={{0,8},{2,10},{4,12},{6,14},{8,0},{10,2},{12,4},{14,6},{16,24},{18,... | collective-permute-start | bytes 221192 | tf_op jit(solution)/shard_map/ppermute | solution.py:45
  119.6 1.0 constant_dynamic-slice_fusion
  120.8 1.4 %collective-permute-done.27 = f32[72,256]{1,0:T(8,128)S(1)} collective-permute-done((f32[72,256]{1,0:T(8,128)}, f32[72,256]{1,0:T(8,128)S(1)}, u32[]{:S(2)}, u32[]{:S(2)}) %collective-permute-start.27) | collective-permute-done | bytes 73760 | tf_op jit(solution)/shard_map/ppermute | solution.py:45
  122.3 2.3 %collective-permute-done.26 = f32[72,256]{1,0:T(8,128)S(1)} collective-permute-done((f32[72,256]{1,0:T(8,128)}, f32[72,256]{1,0:T(8,128)S(1)}, u32[]{:S(2)}, u32[]{:S(2)}) %collective-permute-start.26) | collective-permute-done | bytes 73760 | tf_op jit(solution)/shard_map/ppermute | solution.py:45
  124.7 1.1 collective-permute-done.28
  126.2 1.3 fusion.12
  127.5 0.9 copy.62
  128.4 0.9 copy.63
  129.3 1.5 %fusion.33 = (f32[1,64,256]{2,1,0:T(8,128)}, f32[1,64,256]{2,1,0:T(8,128)}) fusion(f32[64,256]{1,0:T(8,128)S(1)} %get-tuple-element.23, f32[64,256]{1,0:T(8,128)S(1)} %reshape.257, f32[72,256]{1,0:T(8,128)S(1)} %collective-permute-done.27, f32[72,256]{1,0:T(8,128)S(1)} %collective-permute-done.26, f32[72,256]{1,0:T(8,128)S(1)} %copy-done.17, ...), kind=kLoop, calls=%fused_computation.95 | loop fusion | flops 229376 | bytes 658440 | tf_op jit(solution)/shard_map/broadcast_in_dim | solution.py:194
  (182 shorter events, 14.3 us)
Async XLA Ops:
  0.6 15.1 %copy-start = (f32[64,64]{1,0:T(8,128)S(1)}, f32[64,64]{1,0:T(8,128)}, u32[]{:S(2)}) copy-start(f32[64,64]{1,0:T(8,128)} %param.9) | copy-start | bytes 49156
  1.6 18.1 %collective-permute-start.1 = (bf16[1,64,256]{2,1,0:T(8,128)(2,1)S(1)}, bf16[1,64,256]{2,1,0:T(8,128)(2,1)S(1)}, u32[]{:S(2)}, u32[]{:S(2)}) collective-permute-start(bf16[1,64,256]{2,1,0:T(8,128)(2,1)S(1)} %get-tuple-element.60), channel_id=1, source_target_pairs={{0,24},{2,26},{4,28},{6,30},{8,16},{10,18},{12,20},{14,22},{16,8},... | collective-permute-start | bytes 98312 | tf_op jit(solution)/shard_map/ppermute | solution.py:45
  6.7 12.9 %collective-permute-start.2 = (bf16[1,64,256]{2,1,0:T(8,128)(2,1)S(1)}, bf16[1,64,256]{2,1,0:T(8,128)(2,1)S(1)}, u32[]{:S(2)}, u32[]{:S(2)}) collective-permute-start(bf16[1,64,256]{2,1,0:T(8,128)(2,1)S(1)} %get-tuple-element.60), channel_id=1, source_target_pairs={{0,16},{2,18},{4,20},{6,22},{8,24},{10,26},{12,28},{14,30},{16,0},... | collective-permute-start | bytes 98312 | tf_op jit(solution)/shard_map/ppermute | solution.py:45
  6.7 12.9 %collective-permute-start.3 = (bf16[1,64,256]{2,1,0:T(8,128)(2,1)S(1)}, bf16[1,64,256]{2,1,0:T(8,128)(2,1)S(1)}, u32[]{:S(2)}, u32[]{:S(2)}) collective-permute-start(bf16[1,64,256]{2,1,0:T(8,128)(2,1)S(1)} %get-tuple-element.60), channel_id=1, source_target_pairs={{0,8},{2,10},{4,12},{6,14},{8,0},{10,2},{12,4},{14,6},{16,24},{18,... | collective-permute-start | bytes 98312 | tf_op jit(solution)/shard_map/ppermute | solution.py:45
  9.2 2.2 %copy-start.29 = (s32[1,1,12,2]{2,3,1,0:T(2,128)S(1)}, s32[1,1,12,2]{2,3,1,0:T(2,128)}, u32[]{:S(2)}) copy-start(s32[1,1,12,2]{2,3,1,0:T(2,128)} %param.12) | copy-start | bytes 292
  9.2 20.7 %collective-permute-start = (bf16[1,384,256]{1,2,0:T(8,128)(2,1)}, bf16[1,384,256]{1,2,0:T(8,128)(2,1)}, u32[]{:S(2)}, u32[]{:S(2)}) collective-permute-start(bf16[1,384,256]{1,2,0:T(8,128)(2,1)} %convert_element_type.67), channel_id=1, source_target_pairs={{0,1},{1,0},{2,3},{3,2},{4,5},{5,4},{6,7},{7,6},{8,9},{9,8},{10,11... | collective-permute-start | bytes 589832 | tf_op jit(solution)/shard_map/ppermute | solution.py:45
  13.8 3.0 %copy-start.3 = (f32[1,384,256]{2,1,0:T(8,128)S(1)}, f32[1,384,256]{2,1,0:T(8,128)}, u32[]{:S(2)}) copy-start(f32[1,384,256]{2,1,0:T(8,128)} %param.7) | copy-start | bytes 1179652
  13.8 3.1 %copy-start.4 = (f32[1,64,256]{2,1,0:T(8,128)S(1)}, f32[1,64,256]{2,1,0:T(8,128)}, u32[]{:S(2)}) copy-start(f32[1,64,256]{2,1,0:T(8,128)} %param.8) | copy-start | bytes 196612
  17.1 15.0 %copy-start.20 = (f32[768]{0:T(1024)}, f32[768]{0:T(1024)S(1)}, u32[]{:S(2)}) copy-start(f32[768]{0:T(1024)S(1)} %mul.189) | copy-start | bytes 9220
  17.1 6.2 %copy-start.15 = (f32[64,64]{1,0:T(8,128)S(1)}, f32[64,64]{1,0:T(8,128)}, u32[]{:S(2)}) copy-start(f32[64,64]{1,0:T(8,128)} %param.10) | copy-start | bytes 49156
  18.6 16.3 %copy-start.22 = (f32[1,2,4,128]{3,1,2,0:T(2,128)}, f32[1,2,4,128]{3,1,2,0:T(2,128)S(1)}, u32[]{:S(2)}) copy-start(f32[1,2,4,128]{3,1,2,0:T(2,128)S(1)} %copy.72) | copy-start | bytes 12292
  19.7 7.0 %collective-permute-start.4 = (bf16[4,64,256]{2,1,0:T(8,128)(2,1)S(1)}, bf16[4,64,256]{2,1,0:T(8,128)(2,1)S(1)}, u32[]{:S(2)}, u32[]{:S(2)}) collective-permute-start(bf16[4,64,256]{2,1,0:T(8,128)(2,1)S(1)} %maximum_bitcast_fusion), channel_id=1, source_target_pairs={{0,6},{2,4},{4,2},{6,0},{8,14},{10,12},{12,10},{14,8},{16,22},{18,... | collective-permute-start | bytes 393224 | tf_op jit(solution)/shard_map/ppermute | solution.py:45
  22.4 7.0 %collective-permute-start.5 = (bf16[4,64,256]{2,1,0:T(8,128)(2,1)S(1)}, bf16[4,64,256]{2,1,0:T(8,128)(2,1)S(1)}, u32[]{:S(2)}, u32[]{:S(2)}) collective-permute-start(bf16[4,64,256]{2,1,0:T(8,128)(2,1)S(1)} %maximum_bitcast_fusion), channel_id=1, source_target_pairs={{0,4},{2,6},{4,0},{6,2},{8,12},{10,14},{12,8},{14,10},{16,20},{18,... | collective-permute-start | bytes 393224 | tf_op jit(solution)/shard_map/ppermute | solution.py:45
  22.9 6.7 %collective-permute-start.6 = (bf16[4,64,256]{2,1,0:T(8,128)(2,1)S(1)}, bf16[4,64,256]{2,1,0:T(8,128)(2,1)S(1)}, u32[]{:S(2)}, u32[]{:S(2)}) collective-permute-start(bf16[4,64,256]{2,1,0:T(8,128)(2,1)S(1)} %maximum_bitcast_fusion), channel_id=1, source_target_pairs={{0,2},{2,0},{4,6},{6,4},{8,10},{10,8},{12,14},{14,12},{16,18},{18,... | collective-permute-start | bytes 393224 | tf_op jit(solution)/shard_map/ppermute | solution.py:45
  29.8 2.3 %copy-start.1 = (bf16[96,8,4,256]{3,1,2,0:T(8,128)(2,1)S(1)}, bf16[96,8,4,256]{3,1,2,0:T(8,128)(2,1)}, u32[]{:S(2)}) copy-start(bf16[96,8,4,256]{3,1,2,0:T(8,128)(2,1)} %copy.71) | copy-start | bytes 4718596
  29.9 4.9 %copy-start.7 = (bf16[4,4,64,256]{3,2,1,0:T(8,128)(2,1)}, bf16[4,4,64,256]{3,2,1,0:T(8,128)(2,1)S(1)}, u32[]{:S(2)}) copy-start(bf16[4,4,64,256]{3,2,1,0:T(8,128)(2,1)S(1)} %copy.50) | copy-start | bytes 1572868
  34.9 3.5 %copy-start.28 = (f32[4]{0:T(128)S(1)}, f32[4]{0:T(128)}, u32[]{:S(2)}) copy-start(f32[4]{0:T(128)} %get-tuple-element.81) | copy-start | bytes 52
  39.2 0.6 copy-start.24
  39.8 4.4 %copy-start.9 = (f32[64,4,64]{2,0,1:T(8,128)S(1)}, f32[64,4,64]{2,0,1:T(8,128)}, u32[]{:S(2)}) copy-start(f32[64,4,64]{2,0,1:T(8,128)} %get-tuple-element.84) | copy-start | bytes 196612
  39.8 5.2 %copy-start.10 = (f32[768,256]{1,0:T(8,128)S(1)}, f32[768,256]{1,0:T(8,128)}, u32[]{:S(2)}) copy-start(f32[768,256]{1,0:T(8,128)} %get-tuple-element.78) | copy-start | bytes 2359300
  40.6 10.6 %collective-permute-start.9 = (f32[264,256]{1,0:T(8,128)}, f32[264,256]{1,0:T(8,128)}, u32[]{:S(2)}, u32[]{:S(2)}) collective-permute-start(f32[264,256]{1,0:T(8,128)} %get-tuple-element.71), channel_id=1, source_target_pairs={{0,6},{2,4},{4,2},{6,0},{8,14},{10,12},{12,10},{14,8},{16,22},{18,... | collective-permute-start | bytes 811016 | tf_op jit(solution)/shard_map/ppermute | solution.py:45
  42.2 13.6 %collective-permute-start.8 = (f32[264,256]{1,0:T(8,128)S(1)}, f32[264,256]{1,0:T(8,128)}, u32[]{:S(2)}, u32[]{:S(2)}) collective-permute-start(f32[264,256]{1,0:T(8,128)S(1)} %get-tuple-element.72), channel_id=1, source_target_pairs={{0,4},{2,6},{4,0},{6,2},{8,12},{10,14},{12,8},{14,10},{16,20},{18,... | collective-permute-start | bytes 811016 | tf_op jit(solution)/shard_map/ppermute | solution.py:45
  43.6 13.2 %collective-permute-start.7 = (f32[264,256]{1,0:T(8,128)S(1)}, f32[264,256]{1,0:T(8,128)}, u32[]{:S(2)}, u32[]{:S(2)}) collective-permute-start(f32[264,256]{1,0:T(8,128)S(1)} %get-tuple-element.70), channel_id=1, source_target_pairs={{0,2},{2,0},{4,6},{6,4},{8,10},{10,8},{12,14},{14,12},{16,18},{18,... | collective-permute-start | bytes 811016 | tf_op jit(solution)/shard_map/ppermute | solution.py:45
  45.8 12.1 %copy-start.25 = (f32[1,8]{1,0:T(1,128)S(1)}, f32[1,8]{1,0:T(1,128)}, u32[]{:S(2)}) copy-start(f32[1,8]{1,0:T(1,128)} %copy-done.24) | copy-start | bytes 100
  45.8 29.6 %collective-permute-start.14 = (bf16[384,256]{0,1:T(8,128)(2,1)}, bf16[384,256]{0,1:T(8,128)(2,1)}, u32[]{:S(2)}, u32[]{:S(2)}) collective-permute-start(bf16[384,256]{0,1:T(8,128)(2,1)} %bitcast.297), channel_id=1, source_target_pairs={{0,1},{1,0},{2,3},{3,2},{4,5},{5,4},{6,7},{7,6},{8,9},{9,8},{10,11... | collective-permute-start | bytes 589832 | tf_op jit(solution)/shard_map/ppermute | solution.py:45
  57.8 12.5 %copy-start.14 = (f32[64,256]{1,0:T(8,128)S(1)}, f32[64,256]{1,0:T(8,128)}, u32[]{:S(2)}) copy-start(f32[64,256]{1,0:T(8,128)} %reshape.253) | copy-start | bytes 196612
  58.7 7.0 %collective-permute-start.12 = (f32[72,256]{1,0:T(8,128)S(1)}, f32[72,256]{1,0:T(8,128)S(1)}, u32[]{:S(2)}, u32[]{:S(2)}) collective-permute-start(f32[72,256]{1,0:T(8,128)S(1)} %get-tuple-element.69), channel_id=1, source_target_pairs={{0,24},{2,26},{4,28},{6,30},{8,16},{10,18},{12,20},{14,22},{16,8},... | collective-permute-start | bytes 221192 | tf_op jit(solution)/shard_map/ppermute | solution.py:45
  62.3 6.2 %collective-permute-start.11 = (f32[72,256]{1,0:T(8,128)S(1)}, f32[72,256]{1,0:T(8,128)S(1)}, u32[]{:S(2)}, u32[]{:S(2)}) collective-permute-start(f32[72,256]{1,0:T(8,128)S(1)} %get-tuple-element.68), channel_id=1, source_target_pairs={{0,16},{2,18},{4,20},{6,22},{8,24},{10,26},{12,28},{14,30},{16,0},... | collective-permute-start | bytes 221192 | tf_op jit(solution)/shard_map/ppermute | solution.py:45
  62.3 6.2 %collective-permute-start.10 = (f32[72,256]{1,0:T(8,128)S(1)}, f32[72,256]{1,0:T(8,128)S(1)}, u32[]{:S(2)}, u32[]{:S(2)}) collective-permute-start(f32[72,256]{1,0:T(8,128)S(1)} %get-tuple-element.67), channel_id=1, source_target_pairs={{0,8},{2,10},{4,12},{6,14},{8,0},{10,2},{12,4},{14,6},{16,24},{18,... | collective-permute-start | bytes 221192 | tf_op jit(solution)/shard_map/ppermute | solution.py:45
  68.5 1.2 collective-permute-start.13
  69.7 0.5 copy-start.26
  70.4 6.7 %copy-start.18 = (f32[256]{0:T(256)}, f32[256]{0:T(256)S(1)}, u32[]{:S(2)}) copy-start(f32[256]{0:T(256)S(1)} %mul.198) | copy-start | bytes 3076
  71.0 6.4 %collective-permute-start.16 = (bf16[1,64,256]{2,1,0:T(8,128)(2,1)S(1)}, bf16[1,64,256]{2,1,0:T(8,128)(2,1)S(1)}, u32[]{:S(2)}, u32[]{:S(2)}) collective-permute-start(bf16[1,64,256]{2,1,0:T(8,128)(2,1)S(1)} %get-tuple-element.22), channel_id=1, source_target_pairs={{0,24},{2,26},{4,28},{6,30},{8,16},{10,18},{12,20},{14,22},{16,8},... | collective-permute-start | bytes 98312 | tf_op jit(solution)/shard_map/ppermute | solution.py:45
  73.4 4.8 %collective-permute-start.17 = (bf16[1,64,256]{2,1,0:T(8,128)(2,1)S(1)}, bf16[1,64,256]{2,1,0:T(8,128)(2,1)S(1)}, u32[]{:S(2)}, u32[]{:S(2)}) collective-permute-start(bf16[1,64,256]{2,1,0:T(8,128)(2,1)S(1)} %get-tuple-element.22), channel_id=1, source_target_pairs={{0,16},{2,18},{4,20},{6,22},{8,24},{10,26},{12,28},{14,30},{16,0},... | collective-permute-start | bytes 98312 | tf_op jit(solution)/shard_map/ppermute | solution.py:45
  73.5 4.7 %collective-permute-start.18 = (bf16[1,64,256]{2,1,0:T(8,128)(2,1)S(1)}, bf16[1,64,256]{2,1,0:T(8,128)(2,1)S(1)}, u32[]{:S(2)}, u32[]{:S(2)}) collective-permute-start(bf16[1,64,256]{2,1,0:T(8,128)(2,1)S(1)} %get-tuple-element.22), channel_id=1, source_target_pairs={{0,8},{2,10},{4,12},{6,14},{8,0},{10,2},{12,4},{14,6},{16,24},{18,... | collective-permute-start | bytes 98312 | tf_op jit(solution)/shard_map/ppermute | solution.py:45
  76.5 11.2 %collective-permute-start.15 = (bf16[1,384,256]{1,2,0:T(8,128)(2,1)S(1)}, bf16[1,384,256]{1,2,0:T(8,128)(2,1)S(1)}, u32[]{:S(2)}, u32[]{:S(2)}) collective-permute-start(bf16[1,384,256]{1,2,0:T(8,128)(2,1)S(1)} %get-tuple-element.20), channel_id=1, source_target_pairs={{0,1},{1,0},{2,3},{3,2},{4,5},{5,4},{6,7},{7,6},{8,9},{9,8},{10,11... | collective-permute-start | bytes 589832 | tf_op jit(solution)/shard_map/ppermute | solution.py:45
  78.3 7.4 %collective-permute-start.19 = (bf16[4,64,256]{2,1,0:T(8,128)(2,1)S(1)}, bf16[4,64,256]{2,1,0:T(8,128)(2,1)S(1)}, u32[]{:S(2)}, u32[]{:S(2)}) collective-permute-start(bf16[4,64,256]{2,1,0:T(8,128)(2,1)S(1)} %maximum_bitcast_fusion.1), channel_id=1, source_target_pairs={{0,6},{2,4},{4,2},{6,0},{8,14},{10,12},{12,10},{14,8},{16,22},{18,... | collective-permute-start | bytes 393224 | tf_op jit(solution)/shard_map/ppermute | solution.py:45
  79.7 7.5 %collective-permute-start.20 = (bf16[4,64,256]{2,1,0:T(8,128)(2,1)S(1)}, bf16[4,64,256]{2,1,0:T(8,128)(2,1)S(1)}, u32[]{:S(2)}, u32[]{:S(2)}) collective-permute-start(bf16[4,64,256]{2,1,0:T(8,128)(2,1)S(1)} %maximum_bitcast_fusion.1), channel_id=1, source_target_pairs={{0,4},{2,6},{4,0},{6,2},{8,12},{10,14},{12,8},{14,10},{16,20},{18,... | collective-permute-start | bytes 393224 | tf_op jit(solution)/shard_map/ppermute | solution.py:45
  81.5 6.0 %collective-permute-start.21 = (bf16[4,64,256]{2,1,0:T(8,128)(2,1)S(1)}, bf16[4,64,256]{2,1,0:T(8,128)(2,1)S(1)}, u32[]{:S(2)}, u32[]{:S(2)}) collective-permute-start(bf16[4,64,256]{2,1,0:T(8,128)(2,1)S(1)} %maximum_bitcast_fusion.1), channel_id=1, source_target_pairs={{0,2},{2,0},{4,6},{6,4},{8,10},{10,8},{12,14},{14,12},{16,18},{18,... | collective-permute-start | bytes 393224 | tf_op jit(solution)/shard_map/ppermute | solution.py:45
  87.6 1.1 copy-start.21
  87.7 0.8 copy-start.8
  88.0 0.7 copy-start.12
  88.8 3.2 %copy-start.2 = (bf16[96,8,4,256]{3,1,2,0:T(8,128)(2,1)S(1)}, bf16[96,8,4,256]{3,1,2,0:T(8,128)(2,1)}, u32[]{:S(2)}) copy-start(bf16[96,8,4,256]{3,1,2,0:T(8,128)(2,1)} %copy.71) | copy-start | bytes 4718596
  88.8 3.2 %copy-start.23 = (f32[1,2,4,128]{3,1,2,0:T(2,128)S(1)}, f32[1,2,4,128]{3,1,2,0:T(2,128)}, u32[]{:S(2)}) copy-start(f32[1,2,4,128]{3,1,2,0:T(2,128)} %copy-done.22) | copy-start | bytes 12292
  94.0 1.5 %copy-start.6 = (f32[1024,256]{1,0:T(8,128)}, f32[1024,256]{1,0:T(8,128)S(1)}, u32[]{:S(2)}) copy-start(f32[1024,256]{1,0:T(8,128)S(1)} %get-tuple-element.88) | copy-start | bytes 3145732
  94.5 4.4 %copy-start.11 = (f32[768,256]{1,0:T(8,128)S(1)}, f32[768,256]{1,0:T(8,128)}, u32[]{:S(2)}) copy-start(f32[768,256]{1,0:T(8,128)} %get-tuple-element.86) | copy-start | bytes 2359300
  95.5 10.6 %collective-permute-start.24 = (f32[264,256]{1,0:T(8,128)}, f32[264,256]{1,0:T(8,128)}, u32[]{:S(2)}, u32[]{:S(2)}) collective-permute-start(f32[264,256]{1,0:T(8,128)} %get-tuple-element.65), channel_id=1, source_target_pairs={{0,6},{2,4},{4,2},{6,0},{8,14},{10,12},{12,10},{14,8},{16,22},{18,... | collective-permute-start | bytes 811016 | tf_op jit(solution)/shard_map/ppermute | solution.py:45
  96.9 13.7 %collective-permute-start.23 = (f32[264,256]{1,0:T(8,128)}, f32[264,256]{1,0:T(8,128)}, u32[]{:S(2)}, u32[]{:S(2)}) collective-permute-start(f32[264,256]{1,0:T(8,128)} %get-tuple-element.66), channel_id=1, source_target_pairs={{0,4},{2,6},{4,0},{6,2},{8,12},{10,14},{12,8},{14,10},{16,20},{18,... | collective-permute-start | bytes 811016 | tf_op jit(solution)/shard_map/ppermute | solution.py:45
  98.4 13.3 %collective-permute-start.22 = (f32[264,256]{1,0:T(8,128)S(1)}, f32[264,256]{1,0:T(8,128)}, u32[]{:S(2)}, u32[]{:S(2)}) collective-permute-start(f32[264,256]{1,0:T(8,128)S(1)} %get-tuple-element.64), channel_id=1, source_target_pairs={{0,2},{2,0},{4,6},{6,4},{8,10},{10,8},{12,14},{14,12},{16,18},{18,... | collective-permute-start | bytes 811016 | tf_op jit(solution)/shard_map/ppermute | solution.py:45
  112.6 13.2 %copy-start.27 = (f32[8]{0:T(128)S(1)}, f32[8]{0:T(128)}, u32[]{:S(2)}) copy-start(f32[8]{0:T(128)} %copy-done.26) | copy-start | bytes 100
  112.6 13.6 %copy-start.19 = (f32[256]{0:T(256)S(1)}, f32[256]{0:T(256)}, u32[]{:S(2)}) copy-start(f32[256]{0:T(256)} %copy-done.18) | copy-start | bytes 3076
  113.7 12.5 %copy-start.5 = (f32[2,2,64,256]{3,2,1,0:T(8,128)}, f32[2,2,64,256]{3,2,1,0:T(8,128)S(1)}, u32[]{:S(2)}) copy-start(f32[2,2,64,256]{3,2,1,0:T(8,128)S(1)} %fusion.21) | copy-start | bytes 786436
  115.2 7.1 %collective-permute-start.27 = (f32[72,256]{1,0:T(8,128)}, f32[72,256]{1,0:T(8,128)S(1)}, u32[]{:S(2)}, u32[]{:S(2)}) collective-permute-start(f32[72,256]{1,0:T(8,128)} %get-tuple-element.63), channel_id=1, source_target_pairs={{0,24},{2,26},{4,28},{6,30},{8,16},{10,18},{12,20},{14,22},{16,8},... | collective-permute-start | bytes 221192 | tf_op jit(solution)/shard_map/ppermute | solution.py:45
  117.6 7.0 %collective-permute-start.26 = (f32[72,256]{1,0:T(8,128)}, f32[72,256]{1,0:T(8,128)S(1)}, u32[]{:S(2)}, u32[]{:S(2)}) collective-permute-start(f32[72,256]{1,0:T(8,128)} %get-tuple-element.62), channel_id=1, source_target_pairs={{0,16},{2,18},{4,20},{6,22},{8,24},{10,26},{12,28},{14,30},{16,0},... | collective-permute-start | bytes 221192 | tf_op jit(solution)/shard_map/ppermute | solution.py:45
  117.6 7.0 %collective-permute-start.25 = (f32[72,256]{1,0:T(8,128)}, f32[72,256]{1,0:T(8,128)S(1)}, u32[]{:S(2)}, u32[]{:S(2)}) collective-permute-start(f32[72,256]{1,0:T(8,128)} %get-tuple-element.61), channel_id=1, source_target_pairs={{0,8},{2,10},{4,12},{6,14},{8,0},{10,2},{12,4},{14,6},{16,24},{18,... | collective-permute-start | bytes 221192 | tf_op jit(solution)/shard_map/ppermute | solution.py:45
  120.8 5.4 %collective-permute-start.29 = (bf16[384,256]{0,1:T(8,128)(2,1)S(1)}, bf16[384,256]{0,1:T(8,128)(2,1)}, u32[]{:S(2)}, u32[]{:S(2)}) collective-permute-start(bf16[384,256]{0,1:T(8,128)(2,1)S(1)} %bitcast.298), channel_id=1, source_target_pairs={{0,1},{1,0},{2,3},{3,2},{4,5},{5,4},{6,7},{7,6},{8,9},{9,8},{10,11... | collective-permute-start | bytes 589832 | tf_op jit(solution)/shard_map/ppermute | solution.py:45
  124.6 1.6 %copy-start.16 = (f32[72,256]{1,0:T(8,128)}, f32[72,256]{1,0:T(8,128)S(1)}, u32[]{:S(2)}) copy-start(f32[72,256]{1,0:T(8,128)S(1)} %collective-permute-done.25) | copy-start | bytes 221188
  124.6 1.2 collective-permute-start.28
  127.5 1.9 %copy-start.13 = (f32[64,256]{1,0:T(8,128)S(1)}, f32[64,256]{1,0:T(8,128)}, u32[]{:S(2)}) copy-start(f32[64,256]{1,0:T(8,128)} %get-tuple-element.24) | copy-start | bytes 196612
  127.5 1.8 %copy-start.17 = (f32[72,256]{1,0:T(8,128)S(1)}, f32[72,256]{1,0:T(8,128)}, u32[]{:S(2)}) copy-start(f32[72,256]{1,0:T(8,128)} %copy-done.16) | copy-start | bytes 221188

commit v7 on v6

--- a/solution.py
+++ b/solution.py
@@ -72,16 +72,17 @@
             return out
 
         total = block_of(digit)
-        sent_extra = extra
+        shape = total.shape
+        if extra is not None:
+            total = jnp.concatenate([total.reshape(-1, width), extra])
         for k in range(1, len(masks)):
             send = block_of(digit ^ k).astype(send_type)
-            if extra is None:
-                total = total + swap_with(send, axis, size, None, masks[k]).astype(jnp.float32)
-            else:
-                message = jnp.concatenate([send.reshape(-1, width), sent_extra])
-                got = swap_with(message, axis, size, None, masks[k])
-                total = total + got[: -extra.shape[0]].reshape(total.shape)
-                extra = extra + got[-extra.shape[0] :]
+            if extra is not None:
+                send = jnp.concatenate([send.reshape(-1, width), extra])
+            total = total + swap_with(send, axis, size, None, masks[k]).astype(jnp.float32)
+        if extra is not None:
+            extra = total[-extra.shape[0] :]
+            total = total[: -extra.shape[0]].reshape(shape)
         for bit in group:
             left.remove(bit)
         buf = total
@@ -118,15 +119,14 @@
     row_pick = (tile_blocks[0, 0, :, 0][:, None] == jnp.arange(RB, dtype=jnp.int32)) & in_use[:, None]
     col_pick = (tile_blocks[0, 0, :, 1][:, None] == jnp.arange(CB, dtype=jnp.int32)) & in_use[:, None]
     place = (row_pick[:, :, None] & col_pick[:, None, :]).astype(jnp.bfloat16)
-    block_counts = jnp.einsum(
-        "trc,tij->ricj",
-        place,
-        count_tiles[0, 0].astype(jnp.bfloat16),
-        preferred_element_type=jnp.float32,
+    tiles_bf = count_tiles[0, 0].astype(jnp.bfloat16)
+    counts_bf = jnp.einsum(
+        "trc,tij->ricj", place, tiles_bf, preferred_element_type=jnp.bfloat16
     ).reshape(RB * TILE, CB * TILE)
-    user_deg = jnp.sum(block_counts, axis=1)
-    item_deg = jnp.sum(block_counts, axis=0)
-    counts_bf = block_counts.astype(jnp.bfloat16)
+    tile_rows = jnp.sum(tiles_bf, axis=2, dtype=jnp.float32)
+    tile_cols = jnp.sum(tiles_bf, axis=1, dtype=jnp.float32)
+    user_deg = jnp.sum(jnp.where(row_pick[:, :, None], tile_rows[:, None, :], 0.0), axis=0).reshape(-1)
+    item_deg = jnp.sum(jnp.where(col_pick[:, :, None], tile_cols[:, None, :], 0.0), axis=0).reshape(-1)
 
     def cross_parts(user_range, item_range):
         to_users = jnp.dot(counts_bf, item_range, preferred_element_type=jnp.float32)

time: 132 us -> 126 us (0.955)
  local copies, waits for them, and re-layouts: 19.2 us -> 13.1 us
  other arithmetic: 20.1 us -> 17.2 us
  waiting for transfers between devices: 41.2 us -> 44.1 us
    slice x12 -> x4, local copies, waits for them, and re-layouts: 5.82 us -> 0.05 us  [the longest x2 0.04 us: halve_sum(): total = total[:-extra.shape[0]].reshape(shape)]
    ppermute x30, waiting for transfers between devices: 41.2 us -> 44.1 us  [swap_with(): return lax.ppermute(value, axis, pairs)]
    convert_element_type x1 -> x0, other arithmetic: 2.2 us -> none  [per_device(): count_tiles[0, 0].astype(jnp.bfloat16)]
    broadcast_in_dim x2, other arithmetic: 1.7 us -> 0.13 us  [double_gather(): buf = piece[None]]
    unnamed x67 -> x45, local copies, waits for them, and re-layouts: 7.37 us -> 6.55 us
  transfers between devices with their start and end apart: 30 -> 30, of which waited for: 17 -> 21; matrix products, arithmetic and copies ran while one was open for 20% -> 17% of each run, Pallas kernels for 0% -> 0%
where the time goes in v7:
time: 126 us; the launch traced here: 125 us
  waiting for transfers between devices  44.1 us (35%)
  starting transfers between devices  33.4 us (27%)
  other arithmetic  17.2 us (14%)
  matrix products  15.4 us (12%)
  local copies, waits for them, and re-layouts  13.1 us (10%)
  between operations  1.94 us (2%)
    ppermute x30, waiting for transfers between devices, swap_with(): return lax.ppermute(value, axis, pairs)  44.1 us
    ppermute x30, starting transfers between devices, swap_with(): return lax.ppermute(value, axis, pairs)  33.4 us
    unnamed x45, local copies, waits for them, and re-layouts  6.55 us
    dot_general x2, matrix products, cross_parts(): jnp.dot(counts_bf, item_range, preferred_element_type=jnp.float32)  5.81 us
    dot_general x2, matrix products, cross_parts(): lax.dot_general(counts_bf, user_range, (((0,), (0,)), ((), ())), preferre...  4.37 us
    dot_general x4, matrix products, prior_term(): mixed = jnp.einsum('nde,ef->ndf', grouped, prior_mat, precision=top_prec)  2.82 us
  transfers between devices with their start and end apart: 30, of which 21 were waited for; matrix products, arithmetic and copies ran while one was open for 17% of the time, Pallas kernels for 0%

profile of v7, /device:TPU:0, one launch (start us, length us, event | category | flops | bytes accessed | tf_op | source)
XLA Modules:
  0.0 125.2 jit_solution(12832856188939899165)
XLA Ops:
  0.7 0.9 multiply_reduce_fusion.6
  1.6 5.1 %collective-permute-start.1 = (bf16[1,64,256]{2,1,0:T(8,128)(2,1)S(1)}, bf16[1,64,256]{2,1,0:T(8,128)(2,1)S(1)}, u32[]{:S(2)}, u32[]{:S(2)}) collective-permute-start(bf16[1,64,256]{2,1,0:T(8,128)(2,1)S(1)} %get-tuple-element.64), channel_id=1, source_target_pairs={{0,24},{2,26},{4,28},{6,30},{8,16},{10,18},{12,20},{14,22},{16,8},... | collective-permute-start | bytes 98312 | tf_op jit(solution)/shard_map/ppermute | solution.py:45
  6.7 0.6 collective-permute-start.3
  7.4 1.2 copy.49
  8.5 0.7 convert_element_type.64
  9.3 2.4 %convert_reduce_fusion.1 = (f32[12,256]{1,0:T(8,128)S(1)}, f32[12,256]{1,0:T(8,128)S(1)}, bf16[12,256,256]{2,1,0:T(8,128)(2,1)S(1)}) fusion(s32[1,1,12,256,256]{4,3,2,1,0:T(8,128)} %param.11), kind=kLoop, calls=%fused_computation.1 | loop fusion | flops 3139584 | bytes 4743168 | tf_op jit(solution)/shard_map/reduce_sum | solution.py:127
  12.7 1.1 multiply_reduce_fusion.1
  13.8 2.4 %fusion = bf16[3,4,256,256]{3,1,2,0:T(4,128)(2,1)} fusion(bf16[12,256,256]{2,1,0:T(8,128)(2,1)S(1)} %get-tuple-element.24, pred[12,4]{0,1:T(4,128)(4,1)S(1)} %copy.47, pred[12,3]{0,1:T(4,128)(4,1)S(1)} %fusion.66), kind=kOutput, calls=%fused_computation.2 | convolution fusion | flops 18874512 | bytes 3145812 | tf_op jit(solution)/shard_map/trc,tij->ricj/dot_general | solution.py:123
  16.6 1.8 %copy.76 = bf16[96,8,4,256]{3,1,2,0:T(8,128)(2,1)S(1)} copy(bf16[96,8,4,256]{3,2,1,0:T(4,128)(2,1)} %bitcast.246) | data formatting | bytes 3145728
  18.8 0.6 add.292
  19.4 2.7 %collective-permute-start.4 = (bf16[4,64,256]{2,1,0:T(8,128)(2,1)S(1)}, bf16[4,64,256]{2,1,0:T(8,128)(2,1)S(1)}, u32[]{:S(2)}, u32[]{:S(2)}) collective-permute-start(bf16[4,64,256]{2,1,0:T(8,128)(2,1)S(1)} %maximum_bitcast_fusion), channel_id=1, source_target_pairs={{0,6},{2,4},{4,2},{6,0},{8,14},{10,12},{12,10},{14,8},{16,22},{18,... | collective-permute-start | bytes 393224 | tf_op jit(solution)/shard_map/ppermute | solution.py:45
  23.0 0.9 multiply_reduce_fusion.3
  23.9 2.6 %collective-permute-done.4 = bf16[4,64,256]{2,1,0:T(8,128)(2,1)S(1)} collective-permute-done((bf16[4,64,256]{2,1,0:T(8,128)(2,1)S(1)}, bf16[4,64,256]{2,1,0:T(8,128)(2,1)S(1)}, u32[]{:S(2)}, u32[]{:S(2)}) %collective-permute-start.4) | collective-permute-done | bytes 131104 | tf_op jit(solution)/shard_map/ppermute | solution.py:45
  26.4 2.7 %collective-permute-done.5 = bf16[4,64,256]{2,1,0:T(8,128)(2,1)S(1)} collective-permute-done((bf16[4,64,256]{2,1,0:T(8,128)(2,1)S(1)}, bf16[4,64,256]{2,1,0:T(8,128)(2,1)S(1)}, u32[]{:S(2)}, u32[]{:S(2)}) %collective-permute-start.5) | collective-permute-done | bytes 131104 | tf_op jit(solution)/shard_map/ppermute | solution.py:45
  29.5 0.9 copy.51
  30.4 1.0 select_bitcast_fusion.3
  31.6 2.7 %fusion.5 = (f32[256]{0:T(256)S(1)}, f32[768,256]{1,0:T(8,128)}) fusion(bf16[1,2,384,256]{3,2,1,0:T(8,128)(2,1)S(1)} %copy.50, bf16[768,256]{1,0:T(8,128)(2,1)S(1)} %bitcast.272, f32[768]{0:T(1024)S(1)} %mul.192, bf16[768,1024]{1,0:T(8,128)(2,1)S(1)} %bitcast.248, bf16[1024,256]{1,0:T(8,128)(2,1)} %bitcast.264), kind=kOutput, calls=%fused_computation.20 | convolution fusion | flops 403832576 | bytes 3674112 | tf_op jit(solution)/shard_map/dot_general | solution.py:132
  34.5 2.6 %fusion.3 = (f32[256]{0:T(256)}, f32[1024,256]{1,0:T(8,128)S(1)}) fusion(bf16[4,4,64,256]{3,2,1,0:T(8,128)(2,1)} %copy.51, bf16[1024,256]{1,0:T(8,128)(2,1)} %bitcast.265, f32[1024]{0:T(1024)S(1)} %bitcast.279, bf16[768,1024]{1,0:T(8,128)(2,1)S(1)} %bitcast.249, bf16[768,256]{1,0:T(8,128)(2,1)} %bitcast.273), kind=kOutput, calls=%fused_computation.14 | convolution fusion | flops 404225792 | bytes 4068352 | tf_op jit(solution)/shard_map/dot_general | solution.py:134
  37.1 0.8 reduce_sum.230
  38.0 0.7 multiply_add_fusion.1
  38.7 0.7 maximum_bitcast_fusion.2
  39.5 0.9 fusion.29
  40.4 1.5 %collective-permute-start.9 = (f32[264,256]{1,0:T(8,128)}, f32[264,256]{1,0:T(8,128)S(1)}, u32[]{:S(2)}, u32[]{:S(2)}) collective-permute-start(f32[264,256]{1,0:T(8,128)} %get-tuple-element.78), channel_id=1, source_target_pairs={{0,6},{2,4},{4,2},{6,0},{8,14},{10,12},{12,10},{14,8},{16,22},{18,... | collective-permute-start | bytes 811016 | tf_op jit(solution)/shard_map/ppermute | solution.py:45
  41.9 1.4 %collective-permute-start.8 = (f32[264,256]{1,0:T(8,128)}, f32[264,256]{1,0:T(8,128)S(1)}, u32[]{:S(2)}, u32[]{:S(2)}) collective-permute-start(f32[264,256]{1,0:T(8,128)} %get-tuple-element.77), channel_id=1, source_target_pairs={{0,4},{2,6},{4,0},{6,2},{8,12},{10,14},{12,8},{14,10},{16,20},{18,... | collective-permute-start | bytes 811016 | tf_op jit(solution)/shard_map/ppermute | solution.py:45
  44.2 0.8 copy.74
  45.0 5.9 %collective-permute-done.9 = f32[264,256]{1,0:T(8,128)S(1)} collective-permute-done((f32[264,256]{1,0:T(8,128)}, f32[264,256]{1,0:T(8,128)S(1)}, u32[]{:S(2)}, u32[]{:S(2)}) %collective-permute-start.9) | collective-permute-done | bytes 270368 | tf_op jit(solution)/shard_map/ppermute | solution.py:45
  50.9 4.6 %collective-permute-done.8 = f32[264,256]{1,0:T(8,128)S(1)} collective-permute-done((f32[264,256]{1,0:T(8,128)}, f32[264,256]{1,0:T(8,128)S(1)}, u32[]{:S(2)}, u32[]{:S(2)}) %collective-permute-start.8) | collective-permute-done | bytes 270368 | tf_op jit(solution)/shard_map/ppermute | solution.py:45
  55.9 3.7 %collective-permute-start.12 = (f32[72,256]{1,0:T(8,128)S(1)}, f32[72,256]{1,0:T(8,128)S(1)}, u32[]{:S(2)}, u32[]{:S(2)}) collective-permute-start(f32[72,256]{1,0:T(8,128)S(1)} %get-tuple-element.70), channel_id=1, source_target_pairs={{0,24},{2,26},{4,28},{6,30},{8,16},{10,18},{12,20},{14,22},{16,8},... | collective-permute-start | bytes 221192 | tf_op jit(solution)/shard_map/ppermute | solution.py:45
  59.6 0.8 collective-permute-start.10
  60.6 2.4 %collective-permute-done.12 = f32[72,256]{1,0:T(8,128)S(1)} collective-permute-done((f32[72,256]{1,0:T(8,128)S(1)}, f32[72,256]{1,0:T(8,128)S(1)}, u32[]{:S(2)}, u32[]{:S(2)}) %collective-permute-start.12) | collective-permute-done | bytes 73760 | tf_op jit(solution)/shard_map/ppermute | solution.py:45
  63.0 2.8 %collective-permute-done.11 = f32[72,256]{1,0:T(8,128)S(1)} collective-permute-done((f32[72,256]{1,0:T(8,128)S(1)}, f32[72,256]{1,0:T(8,128)S(1)}, u32[]{:S(2)}, u32[]{:S(2)}) %collective-permute-start.11) | collective-permute-done | bytes 73760 | tf_op jit(solution)/shard_map/ppermute | solution.py:45
  65.9 1.1 collective-permute-done.13
  67.3 2.4 %collective-permute-start.16 = (bf16[1,64,256]{2,1,0:T(8,128)(2,1)S(1)}, bf16[1,64,256]{2,1,0:T(8,128)(2,1)S(1)}, u32[]{:S(2)}, u32[]{:S(2)}) collective-permute-start(bf16[1,64,256]{2,1,0:T(8,128)(2,1)S(1)} %get-tuple-element.22), channel_id=1, source_target_pairs={{0,24},{2,26},{4,28},{6,30},{8,16},{10,18},{12,20},{14,22},{16,8},... | collective-permute-start | bytes 98312 | tf_op jit(solution)/shard_map/ppermute | solution.py:45
  69.9 1.8 %collective-permute-start.18 = (bf16[1,64,256]{2,1,0:T(8,128)(2,1)S(1)}, bf16[1,64,256]{2,1,0:T(8,128)(2,1)S(1)}, u32[]{:S(2)}, u32[]{:S(2)}) collective-permute-start(bf16[1,64,256]{2,1,0:T(8,128)(2,1)S(1)} %get-tuple-element.22), channel_id=1, source_target_pairs={{0,8},{2,10},{4,12},{6,14},{8,0},{10,2},{12,4},{14,6},{16,24},{18,... | collective-permute-start | bytes 98312 | tf_op jit(solution)/shard_map/ppermute | solution.py:45
  73.1 1.5 %collective-permute-done.17 = bf16[1,64,256]{2,1,0:T(8,128)(2,1)S(1)} collective-permute-done((bf16[1,64,256]{2,1,0:T(8,128)(2,1)S(1)}, bf16[1,64,256]{2,1,0:T(8,128)(2,1)S(1)}, u32[]{:S(2)}, u32[]{:S(2)}) %collective-permute-start.17) | collective-permute-done | bytes 32800 | tf_op jit(solution)/shard_map/ppermute | solution.py:45
  74.6 1.5 %collective-permute-start.19 = (bf16[4,64,256]{2,1,0:T(8,128)(2,1)S(1)}, bf16[4,64,256]{2,1,0:T(8,128)(2,1)S(1)}, u32[]{:S(2)}, u32[]{:S(2)}) collective-permute-start(bf16[4,64,256]{2,1,0:T(8,128)(2,1)S(1)} %maximum_bitcast_fusion.1), channel_id=1, source_target_pairs={{0,6},{2,4},{4,2},{6,0},{8,14},{10,12},{12,10},{14,8},{16,22},{18,... | collective-permute-start | bytes 393224 | tf_op jit(solution)/shard_map/ppermute | solution.py:45
  76.1 1.4 %collective-permute-start.20 = (bf16[4,64,256]{2,1,0:T(8,128)(2,1)S(1)}, bf16[4,64,256]{2,1,0:T(8,128)(2,1)S(1)}, u32[]{:S(2)}, u32[]{:S(2)}) collective-permute-start(bf16[4,64,256]{2,1,0:T(8,128)(2,1)S(1)} %maximum_bitcast_fusion.1), channel_id=1, source_target_pairs={{0,4},{2,6},{4,0},{6,2},{8,12},{10,14},{12,8},{14,10},{16,20},{18,... | collective-permute-start | bytes 393224 | tf_op jit(solution)/shard_map/ppermute | solution.py:45
  77.5 0.6 collective-permute-start.21
  79.4 2.1 %collective-permute-done.19 = bf16[4,64,256]{2,1,0:T(8,128)(2,1)S(1)} collective-permute-done((bf16[4,64,256]{2,1,0:T(8,128)(2,1)S(1)}, bf16[4,64,256]{2,1,0:T(8,128)(2,1)S(1)}, u32[]{:S(2)}, u32[]{:S(2)}) %collective-permute-start.19) | collective-permute-done | bytes 131104 | tf_op jit(solution)/shard_map/ppermute | solution.py:45
  81.5 1.3 %collective-permute-done.20 = bf16[4,64,256]{2,1,0:T(8,128)(2,1)S(1)} collective-permute-done((bf16[4,64,256]{2,1,0:T(8,128)(2,1)S(1)}, bf16[4,64,256]{2,1,0:T(8,128)(2,1)S(1)}, u32[]{:S(2)}, u32[]{:S(2)}) %collective-permute-start.20) | collective-permute-done | bytes 131104 | tf_op jit(solution)/shard_map/ppermute | solution.py:45
  83.1 0.9 copy.61
  83.9 1.0 select_bitcast_fusion.1
  85.2 0.7 copy-done.16
  85.9 3.1 %fusion.6 = (f32[256]{0:T(256)S(1)}, f32[768,256]{1,0:T(8,128)}) fusion(bf16[1,2,384,256]{3,2,1,0:T(8,128)(2,1)S(1)} %copy.59, bf16[768,256]{1,0:T(8,128)(2,1)S(1)} %bitcast.274, f32[768]{0:T(1024)S(1)} %mul.192, bf16[768,1024]{1,0:T(8,128)(2,1)} %bitcast.250, bf16[1024,256]{1,0:T(8,128)(2,1)} %bitcast.266), kind=kOutput, calls=%fused_computation.21 | convolution fusion | flops 403832576 | bytes 3674112 | tf_op jit(solution)/shard_map/dot_general | solution.py:132
  89.1 1.7 %fusion.4 = (f32[256]{0:T(256)S(1)}, f32[1024,256]{1,0:T(8,128)S(1)}) fusion(bf16[4,4,64,256]{3,2,1,0:T(8,128)(2,1)S(1)} %copy-done.11, bf16[1024,256]{1,0:T(8,128)(2,1)S(1)} %bitcast.267, f32[1024]{0:T(1024)S(1)} %bitcast.280, bf16[768,1024]{1,0:T(8,128)(2,1)S(1)} %bitcast.251, bf16[768,256]{1,0:T(8,128)(2,1)} %bitcast.275), kind=kOutput, calls=%fused_computation.15 | convolution fusion | flops 404225792 | bytes 4068352 | tf_op jit(solution)/shard_map/dot_general | solution.py:134
  91.4 0.9 fusion.21
  92.3 1.5 %collective-permute-start.24 = (f32[264,256]{1,0:T(8,128)}, f32[264,256]{1,0:T(8,128)}, u32[]{:S(2)}, u32[]{:S(2)}) collective-permute-start(f32[264,256]{1,0:T(8,128)} %get-tuple-element.75), channel_id=1, source_target_pairs={{0,6},{2,4},{4,2},{6,0},{8,14},{10,12},{12,10},{14,8},{16,22},{18,... | collective-permute-start | bytes 811016 | tf_op jit(solution)/shard_map/ppermute | solution.py:45
  93.8 1.4 %collective-permute-start.23 = (f32[264,256]{1,0:T(8,128)}, f32[264,256]{1,0:T(8,128)}, u32[]{:S(2)}, u32[]{:S(2)}) collective-permute-start(f32[264,256]{1,0:T(8,128)} %get-tuple-element.74), channel_id=1, source_target_pairs={{0,4},{2,6},{4,0},{6,2},{8,12},{10,14},{12,8},{14,10},{16,20},{18,... | collective-permute-start | bytes 811016 | tf_op jit(solution)/shard_map/ppermute | solution.py:45
  95.2 0.6 collective-permute-start.22
  96.0 7.0 %collective-permute-done.24 = f32[264,256]{1,0:T(8,128)} collective-permute-done((f32[264,256]{1,0:T(8,128)}, f32[264,256]{1,0:T(8,128)}, u32[]{:S(2)}, u32[]{:S(2)}) %collective-permute-start.24) | collective-permute-done | bytes 270368 | tf_op jit(solution)/shard_map/ppermute | solution.py:45
  103.0 4.0 %collective-permute-done.23 = f32[264,256]{1,0:T(8,128)} collective-permute-done((f32[264,256]{1,0:T(8,128)}, f32[264,256]{1,0:T(8,128)}, u32[]{:S(2)}, u32[]{:S(2)}) %collective-permute-start.23) | collective-permute-done | bytes 270368 | tf_op jit(solution)/shard_map/ppermute | solution.py:45
  107.1 1.2 fusion.26
  108.4 0.7 pad_maximum_fusion.10
  109.1 3.4 %collective-permute-start.27 = (f32[72,256]{1,0:T(8,128)}, f32[72,256]{1,0:T(8,128)S(1)}, u32[]{:S(2)}, u32[]{:S(2)}) collective-permute-start(f32[72,256]{1,0:T(8,128)} %get-tuple-element.67), channel_id=1, source_target_pairs={{0,24},{2,26},{4,28},{6,30},{8,16},{10,18},{12,20},{14,22},{16,8},... | collective-permute-start | bytes 221192 | tf_op jit(solution)/shard_map/ppermute | solution.py:45
  112.5 1.0 collective-permute-start.25
  113.5 1.0 constant_dynamic-slice_fusion
  114.8 1.3 %collective-permute-done.27 = f32[72,256]{1,0:T(8,128)S(1)} collective-permute-done((f32[72,256]{1,0:T(8,128)}, f32[72,256]{1,0:T(8,128)S(1)}, u32[]{:S(2)}, u32[]{:S(2)}) %collective-permute-start.27) | collective-permute-done | bytes 73760 | tf_op jit(solution)/shard_map/ppermute | solution.py:45
  116.1 2.4 %collective-permute-done.26 = f32[72,256]{1,0:T(8,128)} collective-permute-done((f32[72,256]{1,0:T(8,128)}, f32[72,256]{1,0:T(8,128)}, u32[]{:S(2)}, u32[]{:S(2)}) %collective-permute-start.26) | collective-permute-done | bytes 73760 | tf_op jit(solution)/shard_map/ppermute | solution.py:45
  118.9 0.9 fusion.41
  119.9 1.1 collective-permute-done.28
  121.4 0.7 fusion.49
  122.1 1.2 fusion.12
  123.3 0.9 copy.67
  124.3 0.9 copy.68
  (152 shorter events, 10.1 us)
Async XLA Ops:
  0.6 12.0 %copy-start = (f32[64,64]{1,0:T(8,128)S(1)}, f32[64,64]{1,0:T(8,128)}, u32[]{:S(2)}) copy-start(f32[64,64]{1,0:T(8,128)} %param.9) | copy-start | bytes 49156
  0.6 8.6 %copy-start.3 = (f32[1,384,256]{2,1,0:T(8,128)S(1)}, f32[1,384,256]{2,1,0:T(8,128)}, u32[]{:S(2)}) copy-start(f32[1,384,256]{2,1,0:T(8,128)} %param.7) | copy-start | bytes 1179652
  1.6 17.7 %collective-permute-start.1 = (bf16[1,64,256]{2,1,0:T(8,128)(2,1)S(1)}, bf16[1,64,256]{2,1,0:T(8,128)(2,1)S(1)}, u32[]{:S(2)}, u32[]{:S(2)}) collective-permute-start(bf16[1,64,256]{2,1,0:T(8,128)(2,1)S(1)} %get-tuple-element.64), channel_id=1, source_target_pairs={{0,24},{2,26},{4,28},{6,30},{8,16},{10,18},{12,20},{14,22},{16,8},... | collective-permute-start | bytes 98312 | tf_op jit(solution)/shard_map/ppermute | solution.py:45
  6.7 12.6 %collective-permute-start.2 = (bf16[1,64,256]{2,1,0:T(8,128)(2,1)S(1)}, bf16[1,64,256]{2,1,0:T(8,128)(2,1)S(1)}, u32[]{:S(2)}, u32[]{:S(2)}) collective-permute-start(bf16[1,64,256]{2,1,0:T(8,128)(2,1)S(1)} %get-tuple-element.64), channel_id=1, source_target_pairs={{0,16},{2,18},{4,20},{6,22},{8,24},{10,26},{12,28},{14,30},{16,0},... | collective-permute-start | bytes 98312 | tf_op jit(solution)/shard_map/ppermute | solution.py:45
  6.7 12.6 %collective-permute-start.3 = (bf16[1,64,256]{2,1,0:T(8,128)(2,1)S(1)}, bf16[1,64,256]{2,1,0:T(8,128)(2,1)S(1)}, u32[]{:S(2)}, u32[]{:S(2)}) collective-permute-start(bf16[1,64,256]{2,1,0:T(8,128)(2,1)S(1)} %get-tuple-element.64), channel_id=1, source_target_pairs={{0,8},{2,10},{4,12},{6,14},{8,0},{10,2},{12,4},{14,6},{16,24},{18,... | collective-permute-start | bytes 98312 | tf_op jit(solution)/shard_map/ppermute | solution.py:45
  9.2 21.2 %collective-permute-start = (bf16[1,384,256]{1,2,0:T(8,128)(2,1)}, bf16[1,384,256]{1,2,0:T(8,128)(2,1)}, u32[]{:S(2)}, u32[]{:S(2)}) collective-permute-start(bf16[1,384,256]{1,2,0:T(8,128)(2,1)} %convert_element_type.64), channel_id=1, source_target_pairs={{0,1},{1,0},{2,3},{3,2},{4,5},{5,4},{6,7},{7,6},{8,9},{9,8},{10,11... | collective-permute-start | bytes 589832 | tf_op jit(solution)/shard_map/ppermute | solution.py:45
  9.3 2.4 %copy-start.18 = (s32[1,1,12,2]{2,3,1,0:T(2,128)S(1)}, s32[1,1,12,2]{2,3,1,0:T(2,128)}, u32[]{:S(2)}) copy-start(s32[1,1,12,2]{2,3,1,0:T(2,128)} %param.12) | copy-start | bytes 292
  13.8 2.6 %copy-start.4 = (f32[1,64,256]{2,1,0:T(8,128)S(1)}, f32[1,64,256]{2,1,0:T(8,128)}, u32[]{:S(2)}) copy-start(f32[1,64,256]{2,1,0:T(8,128)} %param.8) | copy-start | bytes 196612
  16.5 6.4 %copy-start.17 = (f32[64,64]{1,0:T(8,128)S(1)}, f32[64,64]{1,0:T(8,128)}, u32[]{:S(2)}) copy-start(f32[64,64]{1,0:T(8,128)} %param.10) | copy-start | bytes 49156
  18.3 16.2 %copy-start.1 = (bf16[96,8,4,256]{3,1,2,0:T(8,128)(2,1)}, bf16[96,8,4,256]{3,1,2,0:T(8,128)(2,1)S(1)}, u32[]{:S(2)}) copy-start(bf16[96,8,4,256]{3,1,2,0:T(8,128)(2,1)S(1)} %copy.76) | copy-start | bytes 4718596
  19.4 7.0 %collective-permute-start.4 = (bf16[4,64,256]{2,1,0:T(8,128)(2,1)S(1)}, bf16[4,64,256]{2,1,0:T(8,128)(2,1)S(1)}, u32[]{:S(2)}, u32[]{:S(2)}) collective-permute-start(bf16[4,64,256]{2,1,0:T(8,128)(2,1)S(1)} %maximum_bitcast_fusion), channel_id=1, source_target_pairs={{0,6},{2,4},{4,2},{6,0},{8,14},{10,12},{12,10},{14,8},{16,22},{18,... | collective-permute-start | bytes 393224 | tf_op jit(solution)/shard_map/ppermute | solution.py:45
  22.1 7.0 %collective-permute-start.5 = (bf16[4,64,256]{2,1,0:T(8,128)(2,1)S(1)}, bf16[4,64,256]{2,1,0:T(8,128)(2,1)S(1)}, u32[]{:S(2)}, u32[]{:S(2)}) collective-permute-start(bf16[4,64,256]{2,1,0:T(8,128)(2,1)S(1)} %maximum_bitcast_fusion), channel_id=1, source_target_pairs={{0,4},{2,6},{4,0},{6,2},{8,12},{10,14},{12,8},{14,10},{16,20},{18,... | collective-permute-start | bytes 393224 | tf_op jit(solution)/shard_map/ppermute | solution.py:45
  22.6 6.8 %collective-permute-start.6 = (bf16[4,64,256]{2,1,0:T(8,128)(2,1)S(1)}, bf16[4,64,256]{2,1,0:T(8,128)(2,1)S(1)}, u32[]{:S(2)}, u32[]{:S(2)}) collective-permute-start(bf16[4,64,256]{2,1,0:T(8,128)(2,1)S(1)} %maximum_bitcast_fusion), channel_id=1, source_target_pairs={{0,2},{2,0},{4,6},{6,4},{8,10},{10,8},{12,14},{14,12},{16,18},{18,... | collective-permute-start | bytes 393224 | tf_op jit(solution)/shard_map/ppermute | solution.py:45
  31.6 2.7 %copy-start.15 = (bf16[1,2,384,256]{3,2,1,0:T(8,128)(2,1)}, bf16[1,2,384,256]{3,2,1,0:T(8,128)(2,1)S(1)}, u32[]{:S(2)}) copy-start(bf16[1,2,384,256]{3,2,1,0:T(8,128)(2,1)S(1)} %copy.50) | copy-start | bytes 1179652
  39.4 4.5 %copy-start.12 = (f32[64,4,64]{2,0,1:T(8,128)S(1)}, f32[64,4,64]{2,0,1:T(8,128)}, u32[]{:S(2)}) copy-start(f32[64,4,64]{2,0,1:T(8,128)} %get-tuple-element.86) | copy-start | bytes 196612
  39.5 4.6 %copy-start.13 = (f32[768,256]{1,0:T(8,128)S(1)}, f32[768,256]{1,0:T(8,128)}, u32[]{:S(2)}) copy-start(f32[768,256]{1,0:T(8,128)} %get-tuple-element.80) | copy-start | bytes 2359300
  40.4 10.5 %collective-permute-start.9 = (f32[264,256]{1,0:T(8,128)}, f32[264,256]{1,0:T(8,128)S(1)}, u32[]{:S(2)}, u32[]{:S(2)}) collective-permute-start(f32[264,256]{1,0:T(8,128)} %get-tuple-element.78), channel_id=1, source_target_pairs={{0,6},{2,4},{4,2},{6,0},{8,14},{10,12},{12,10},{14,8},{16,22},{18,... | collective-permute-start | bytes 811016 | tf_op jit(solution)/shard_map/ppermute | solution.py:45
  41.9 13.6 %collective-permute-start.8 = (f32[264,256]{1,0:T(8,128)}, f32[264,256]{1,0:T(8,128)S(1)}, u32[]{:S(2)}, u32[]{:S(2)}) collective-permute-start(f32[264,256]{1,0:T(8,128)} %get-tuple-element.77), channel_id=1, source_target_pairs={{0,4},{2,6},{4,0},{6,2},{8,12},{10,14},{12,8},{14,10},{16,20},{18,... | collective-permute-start | bytes 811016 | tf_op jit(solution)/shard_map/ppermute | solution.py:45
  43.4 12.4 %collective-permute-start.7 = (f32[264,256]{1,0:T(8,128)}, f32[264,256]{1,0:T(8,128)S(1)}, u32[]{:S(2)}, u32[]{:S(2)}) collective-permute-start(f32[264,256]{1,0:T(8,128)} %get-tuple-element.76), channel_id=1, source_target_pairs={{0,2},{2,0},{4,6},{6,4},{8,10},{10,8},{12,14},{14,12},{16,18},{18,... | collective-permute-start | bytes 811016 | tf_op jit(solution)/shard_map/ppermute | solution.py:45
  44.1 23.1 %copy-start.7 = (f32[64,256]{1,0:T(8,128)}, f32[64,256]{1,0:T(8,128)S(1)}, u32[]{:S(2)}) copy-start(f32[64,256]{1,0:T(8,128)S(1)} %reshape.283) | copy-start | bytes 196612
  45.0 26.7 %collective-permute-start.14 = (bf16[384,256]{0,1:T(8,128)(2,1)}, bf16[384,256]{0,1:T(8,128)(2,1)S(1)}, u32[]{:S(2)}, u32[]{:S(2)}) collective-permute-start(bf16[384,256]{0,1:T(8,128)(2,1)} %bitcast.276), channel_id=1, source_target_pairs={{0,1},{1,0},{2,3},{3,2},{4,5},{5,4},{6,7},{7,6},{8,9},{9,8},{10,11... | collective-permute-start | bytes 589832 | tf_op jit(solution)/shard_map/ppermute | solution.py:45
  55.9 7.1 %collective-permute-start.12 = (f32[72,256]{1,0:T(8,128)S(1)}, f32[72,256]{1,0:T(8,128)S(1)}, u32[]{:S(2)}, u32[]{:S(2)}) collective-permute-start(f32[72,256]{1,0:T(8,128)S(1)} %get-tuple-element.70), channel_id=1, source_target_pairs={{0,24},{2,26},{4,28},{6,30},{8,16},{10,18},{12,20},{14,22},{16,8},... | collective-permute-start | bytes 221192 | tf_op jit(solution)/shard_map/ppermute | solution.py:45
  59.6 6.2 %collective-permute-start.11 = (f32[72,256]{1,0:T(8,128)S(1)}, f32[72,256]{1,0:T(8,128)S(1)}, u32[]{:S(2)}, u32[]{:S(2)}) collective-permute-start(f32[72,256]{1,0:T(8,128)S(1)} %get-tuple-element.69), channel_id=1, source_target_pairs={{0,16},{2,18},{4,20},{6,22},{8,24},{10,26},{12,28},{14,30},{16,0},... | collective-permute-start | bytes 221192 | tf_op jit(solution)/shard_map/ppermute | solution.py:45
  59.6 6.2 %collective-permute-start.10 = (f32[72,256]{1,0:T(8,128)S(1)}, f32[72,256]{1,0:T(8,128)S(1)}, u32[]{:S(2)}, u32[]{:S(2)}) collective-permute-start(f32[72,256]{1,0:T(8,128)S(1)} %get-tuple-element.68), channel_id=1, source_target_pairs={{0,8},{2,10},{4,12},{6,14},{8,0},{10,2},{12,4},{14,6},{16,24},{18,... | collective-permute-start | bytes 221192 | tf_op jit(solution)/shard_map/ppermute | solution.py:45
  65.8 5.9 %copy-start.9 = (f32[72,256]{1,0:T(8,128)}, f32[72,256]{1,0:T(8,128)S(1)}, u32[]{:S(2)}) copy-start(f32[72,256]{1,0:T(8,128)S(1)} %fusion.44) | copy-start | bytes 221188
  65.8 1.2 collective-permute-start.13
  67.3 5.8 %collective-permute-start.16 = (bf16[1,64,256]{2,1,0:T(8,128)(2,1)S(1)}, bf16[1,64,256]{2,1,0:T(8,128)(2,1)S(1)}, u32[]{:S(2)}, u32[]{:S(2)}) collective-permute-start(bf16[1,64,256]{2,1,0:T(8,128)(2,1)S(1)} %get-tuple-element.22), channel_id=1, source_target_pairs={{0,24},{2,26},{4,28},{6,30},{8,16},{10,18},{12,20},{14,22},{16,8},... | collective-permute-start | bytes 98312 | tf_op jit(solution)/shard_map/ppermute | solution.py:45
  69.7 4.8 %collective-permute-start.17 = (bf16[1,64,256]{2,1,0:T(8,128)(2,1)S(1)}, bf16[1,64,256]{2,1,0:T(8,128)(2,1)S(1)}, u32[]{:S(2)}, u32[]{:S(2)}) collective-permute-start(bf16[1,64,256]{2,1,0:T(8,128)(2,1)S(1)} %get-tuple-element.22), channel_id=1, source_target_pairs={{0,16},{2,18},{4,20},{6,22},{8,24},{10,26},{12,28},{14,30},{16,0},... | collective-permute-start | bytes 98312 | tf_op jit(solution)/shard_map/ppermute | solution.py:45
  69.9 4.6 %collective-permute-start.18 = (bf16[1,64,256]{2,1,0:T(8,128)(2,1)S(1)}, bf16[1,64,256]{2,1,0:T(8,128)(2,1)S(1)}, u32[]{:S(2)}, u32[]{:S(2)}) collective-permute-start(bf16[1,64,256]{2,1,0:T(8,128)(2,1)S(1)} %get-tuple-element.22), channel_id=1, source_target_pairs={{0,8},{2,10},{4,12},{6,14},{8,0},{10,2},{12,4},{14,6},{16,24},{18,... | collective-permute-start | bytes 98312 | tf_op jit(solution)/shard_map/ppermute | solution.py:45
  71.7 1.1 copy-start.5
  71.9 12.1 %collective-permute-start.15 = (bf16[1,384,256]{1,2,0:T(8,128)(2,1)S(1)}, bf16[1,384,256]{1,2,0:T(8,128)(2,1)}, u32[]{:S(2)}, u32[]{:S(2)}) collective-permute-start(bf16[1,384,256]{1,2,0:T(8,128)(2,1)S(1)} %get-tuple-element.20), channel_id=1, source_target_pairs={{0,1},{1,0},{2,3},{3,2},{4,5},{5,4},{6,7},{7,6},{8,9},{9,8},{10,11... | collective-permute-start | bytes 589832 | tf_op jit(solution)/shard_map/ppermute | solution.py:45
  74.6 6.9 %collective-permute-start.19 = (bf16[4,64,256]{2,1,0:T(8,128)(2,1)S(1)}, bf16[4,64,256]{2,1,0:T(8,128)(2,1)S(1)}, u32[]{:S(2)}, u32[]{:S(2)}) collective-permute-start(bf16[4,64,256]{2,1,0:T(8,128)(2,1)S(1)} %maximum_bitcast_fusion.1), channel_id=1, source_target_pairs={{0,6},{2,4},{4,2},{6,0},{8,14},{10,12},{12,10},{14,8},{16,22},{18,... | collective-permute-start | bytes 393224 | tf_op jit(solution)/shard_map/ppermute | solution.py:45
  76.1 6.8 %collective-permute-start.20 = (bf16[4,64,256]{2,1,0:T(8,128)(2,1)S(1)}, bf16[4,64,256]{2,1,0:T(8,128)(2,1)S(1)}, u32[]{:S(2)}, u32[]{:S(2)}) collective-permute-start(bf16[4,64,256]{2,1,0:T(8,128)(2,1)S(1)} %maximum_bitcast_fusion.1), channel_id=1, source_target_pairs={{0,4},{2,6},{4,0},{6,2},{8,12},{10,14},{12,8},{14,10},{16,20},{18,... | collective-permute-start | bytes 393224 | tf_op jit(solution)/shard_map/ppermute | solution.py:45
  77.5 5.4 %collective-permute-start.21 = (bf16[4,64,256]{2,1,0:T(8,128)(2,1)S(1)}, bf16[4,64,256]{2,1,0:T(8,128)(2,1)S(1)}, u32[]{:S(2)}, u32[]{:S(2)}) collective-permute-start(bf16[4,64,256]{2,1,0:T(8,128)(2,1)S(1)} %maximum_bitcast_fusion.1), channel_id=1, source_target_pairs={{0,2},{2,0},{4,6},{6,4},{8,10},{10,8},{12,14},{14,12},{16,18},{18,... | collective-permute-start | bytes 393224 | tf_op jit(solution)/shard_map/ppermute | solution.py:45
  85.1 0.7 copy-start.16
  85.9 3.2 %copy-start.2 = (bf16[96,8,4,256]{3,1,2,0:T(8,128)(2,1)S(1)}, bf16[96,8,4,256]{3,1,2,0:T(8,128)(2,1)}, u32[]{:S(2)}) copy-start(bf16[96,8,4,256]{3,1,2,0:T(8,128)(2,1)} %copy-done.1) | copy-start | bytes 4718596
  85.9 3.2 %copy-start.11 = (bf16[4,4,64,256]{3,2,1,0:T(8,128)(2,1)S(1)}, bf16[4,4,64,256]{3,2,1,0:T(8,128)(2,1)}, u32[]{:S(2)}) copy-start(bf16[4,4,64,256]{3,2,1,0:T(8,128)(2,1)} %copy.61) | copy-start | bytes 1572868
  91.2 4.6 %copy-start.14 = (f32[768,256]{1,0:T(8,128)S(1)}, f32[768,256]{1,0:T(8,128)}, u32[]{:S(2)}) copy-start(f32[768,256]{1,0:T(8,128)} %get-tuple-element.88) | copy-start | bytes 2359300
  92.3 10.7 %collective-permute-start.24 = (f32[264,256]{1,0:T(8,128)}, f32[264,256]{1,0:T(8,128)}, u32[]{:S(2)}, u32[]{:S(2)}) collective-permute-start(f32[264,256]{1,0:T(8,128)} %get-tuple-element.75), channel_id=1, source_target_pairs={{0,6},{2,4},{4,2},{6,0},{8,14},{10,12},{12,10},{14,8},{16,22},{18,... | collective-permute-start | bytes 811016 | tf_op jit(solution)/shard_map/ppermute | solution.py:45
  93.8 13.2 %collective-permute-start.23 = (f32[264,256]{1,0:T(8,128)}, f32[264,256]{1,0:T(8,128)}, u32[]{:S(2)}, u32[]{:S(2)}) collective-permute-start(f32[264,256]{1,0:T(8,128)} %get-tuple-element.74), channel_id=1, source_target_pairs={{0,4},{2,6},{4,0},{6,2},{8,12},{10,14},{12,8},{14,10},{16,20},{18,... | collective-permute-start | bytes 811016 | tf_op jit(solution)/shard_map/ppermute | solution.py:45
  95.2 11.9 %collective-permute-start.22 = (f32[264,256]{1,0:T(8,128)}, f32[264,256]{1,0:T(8,128)}, u32[]{:S(2)}, u32[]{:S(2)}) collective-permute-start(f32[264,256]{1,0:T(8,128)} %get-tuple-element.73), channel_id=1, source_target_pairs={{0,2},{2,0},{4,6},{6,4},{8,10},{10,8},{12,14},{14,12},{16,18},{18,... | collective-permute-start | bytes 811016 | tf_op jit(solution)/shard_map/ppermute | solution.py:45
  108.3 13.1 %copy-start.8 = (f32[64,256]{1,0:T(8,128)S(1)}, f32[64,256]{1,0:T(8,128)}, u32[]{:S(2)}) copy-start(f32[64,256]{1,0:T(8,128)} %copy-done.7) | copy-start | bytes 196612
  108.3 13.1 %copy-start.10 = (f32[72,256]{1,0:T(8,128)S(1)}, f32[72,256]{1,0:T(8,128)}, u32[]{:S(2)}) copy-start(f32[72,256]{1,0:T(8,128)} %copy-done.9) | copy-start | bytes 221188
  108.3 13.8 %copy-start.6 = (bf16[384,256]{0,1:T(8,128)(2,1)S(1)}, bf16[384,256]{0,1:T(8,128)(2,1)}, u32[]{:S(2)}) copy-start(bf16[384,256]{0,1:T(8,128)(2,1)} %copy-done.5) | copy-start | bytes 589828
  109.1 7.0 %collective-permute-start.27 = (f32[72,256]{1,0:T(8,128)}, f32[72,256]{1,0:T(8,128)S(1)}, u32[]{:S(2)}, u32[]{:S(2)}) collective-permute-start(f32[72,256]{1,0:T(8,128)} %get-tuple-element.67), channel_id=1, source_target_pairs={{0,24},{2,26},{4,28},{6,30},{8,16},{10,18},{12,20},{14,22},{16,8},... | collective-permute-start | bytes 221192 | tf_op jit(solution)/shard_map/ppermute | solution.py:45
  112.5 6.0 %collective-permute-start.26 = (f32[72,256]{1,0:T(8,128)}, f32[72,256]{1,0:T(8,128)}, u32[]{:S(2)}, u32[]{:S(2)}) collective-permute-start(f32[72,256]{1,0:T(8,128)} %get-tuple-element.66), channel_id=1, source_target_pairs={{0,16},{2,18},{4,20},{6,22},{8,24},{10,26},{12,28},{14,30},{16,0},... | collective-permute-start | bytes 221192 | tf_op jit(solution)/shard_map/ppermute | solution.py:45
  112.5 6.4 %collective-permute-start.25 = (f32[72,256]{1,0:T(8,128)}, f32[72,256]{1,0:T(8,128)}, u32[]{:S(2)}, u32[]{:S(2)}) collective-permute-start(f32[72,256]{1,0:T(8,128)} %get-tuple-element.65), channel_id=1, source_target_pairs={{0,8},{2,10},{4,12},{6,14},{8,0},{10,2},{12,4},{14,6},{16,24},{18,... | collective-permute-start | bytes 221192 | tf_op jit(solution)/shard_map/ppermute | solution.py:45
  114.7 7.5 %collective-permute-start.29 = (bf16[384,256]{0,1:T(8,128)(2,1)S(1)}, bf16[384,256]{0,1:T(8,128)(2,1)}, u32[]{:S(2)}, u32[]{:S(2)}) collective-permute-start(bf16[384,256]{0,1:T(8,128)(2,1)S(1)} %bitcast.277), channel_id=1, source_target_pairs={{0,1},{1,0},{2,3},{3,2},{4,5},{5,4},{6,7},{7,6},{8,9},{9,8},{10,11... | collective-permute-start | bytes 589832 | tf_op jit(solution)/shard_map/ppermute | solution.py:45
  119.9 1.2 collective-permute-start.28

commit v8 on v7

--- a/solution.py
+++ b/solution.py
@@ -17,15 +17,13 @@
 
 
 def prior_term(field_vec, prior_mat):
-    row_total = field_vec.shape[0]
-    grouped = field_vec.reshape(row_total, DRAWS, DIM)
-    mixed = jnp.einsum("nde,ef->ndf", grouped, prior_mat, precision=top_prec)
-    return mixed.reshape(row_total, DRAWS * DIM)
+    per_draw_block = jnp.kron(jnp.eye(DRAWS, dtype=prior_mat.dtype), prior_mat)
+    return jnp.dot(field_vec, per_draw_block, precision=top_prec)
 
 
 def per_draw(left, right):
-    product = (left * right).reshape(-1, DRAWS, DIM)
-    return jnp.sum(product, axis=(0, 2))
+    column_sums = jnp.sum(left * right, axis=0)
+    return jnp.sum(column_sums.reshape(DRAWS, DIM), axis=1)
 
 
 def widen(coef):

time: 126 us -> 133 us (1.056)
  other arithmetic: 17.2 us -> 23.3 us
  local copies, waits for them, and re-layouts: 13.1 us -> 14.6 us
  waiting for transfers between devices: 44.1 us -> 42.6 us
    mul x0 -> x1, other arithmetic: none -> 1.76 us  [prior_term(): per_draw_block = jnp.kron(jnp.eye(DRAWS, dtype=prior_mat.dtype), prior_mat)]
    ppermute x30, waiting for transfers between devices: 44.1 us -> 42.6 us  [swap_with(): return lax.ppermute(value, axis, pairs)]
    reduce_sum x10 -> x0, local copies, waits for them, and re-layouts: 1.5 us -> none  [per_draw(): return jnp.sum(product, axis=(0, 2))]
    convert_element_type x0 -> x2, other arithmetic: none -> 1.46 us  [the longest x1 1.46 us: item_range_of(): return double_gather(item_vec.astype(jnp.bfloat16), 'user')]
    dot_general x4, matrix products: 2.82 us -> 4.22 us  [prior_term(): return jnp.dot(field_vec, per_draw_block, precision=top_prec)]
    unnamed x45 -> x61, local copies, waits for them, and re-layouts: 6.55 us -> 6.91 us
  transfers between devices with their start and end apart: 30 -> 30, of which waited for: 21 -> 17; matrix products, arithmetic and copies ran while one was open for 17% -> 21% of each run, Pallas kernels for 0% -> 0%
where the time goes in v8:
time: 133 us; the launch traced here: 132 us
  waiting for transfers between devices  42.6 us (32%)
  starting transfers between devices  33.2 us (25%)
  other arithmetic  23.3 us (18%)
  matrix products  16.3 us (12%)
  local copies, waits for them, and re-layouts  14.6 us (11%)
  between operations  1.97 us (1%)
    ppermute x30, waiting for transfers between devices, swap_with(): return lax.ppermute(value, axis, pairs)  42.6 us
    ppermute x30, starting transfers between devices, swap_with(): return lax.ppermute(value, axis, pairs)  33.2 us
    unnamed x61, local copies, waits for them, and re-layouts  6.91 us
    dot_general x2, matrix products, cross_parts(): jnp.dot(counts_bf, item_range, preferred_element_type=jnp.float32)  6.05 us
    dot_general x4, matrix products, prior_term(): return jnp.dot(field_vec, per_draw_block, precision=top_prec)  4.22 us
    dot_general x2, matrix products, cross_parts(): lax.dot_general(counts_bf, user_range, (((0,), (0,)), ((), ())), preferre...  4.08 us
    another operation x12, other arithmetic, double_gather(): buf = jnp.stack(ordered, axis=1).reshape((-1,) + piece.shape)  3.19 us
    add x4, other arithmetic, halve_sum(): total + swap_with(send, axis, size, None, masks[k]).astype(jnp.float32)  3.09 us
  transfers between devices with their start and end apart: 30, of which 17 were waited for; matrix products, arithmetic and copies ran while one was open for 21% of the time, Pallas kernels for 0%

profile of v8, /device:TPU:0, one launch (start us, length us, event | category | flops | bytes accessed | tf_op | source)
XLA Modules:
  0.0 131.9 jit_solution(13178922496947643940)
XLA Ops:
  0.6 1.5 %convert_element_type.78 = bf16[1,64,256]{2,1,0:T(8,128)(2,1)} convert(f32[1,64,256]{2,1,0:T(8,128)} %param.8) | non-fusion elementwise | flops 16384 | bytes 98304 | tf_op jit(solution)/shard_map/convert_element_type | solution.py:142
  2.1 5.0 %collective-permute-start.1 = (bf16[1,64,256]{2,1,0:T(8,128)(2,1)}, bf16[1,64,256]{2,1,0:T(8,128)(2,1)}, u32[]{:S(2)}, u32[]{:S(2)}) collective-permute-start(bf16[1,64,256]{2,1,0:T(8,128)(2,1)} %convert_element_type.78), channel_id=1, source_target_pairs={{0,24},{2,26},{4,28},{6,30},{8,16},{10,18},{12,20},{14,22},{16,8},... | collective-permute-start | bytes 98312 | tf_op jit(solution)/shard_map/ppermute | solution.py:43
  7.7 1.2 copy.41
  8.9 0.7 convert_element_type.76
  9.6 1.8 %broadcast_multiply_fusion = (f32[4,64,4,64]{3,2,1,0:T(4,128)}, f32[4,64,4,64]{3,2,1,0:T(4,128)S(1)}) fusion(f32[64,64]{1,0:T(8,128)} %param.10, f32[4,4]{1,0:T(4,128)S(1)} %fusion.62, f32[64,64]{1,0:T(8,128)} %param.9), kind=kLoop, calls=%fused_computation.69 | loop fusion | flops 131072 | bytes 557120 | tf_op jit(solution)/shard_map/jit(kron)/mul | solution.py:20
  11.7 2.3 %fusion.16 = (f32[256]{0:T(256)}, f32[256]{0:T(256)}, f32[384,256]{0,1:T(8,128)}) fusion(f32[1,384,256]{1,2,0:T(8,128)S(1)} %copy.41, f32[256,256]{1,0:T(8,128)S(1)} %mul.256, f32[1,384,256]{2,1,0:T(8,128)S(1)} %copy-done.6), kind=kOutput, calls=%fused_computation.44 | convolution fusion | flops 302382592 | bytes 1443840 | tf_op jit(solution)/shard_map/dot_general | solution.py:21
  14.1 2.4 %convert_reduce_fusion.1 = (f32[12,256]{1,0:T(8,128)S(1)}, f32[12,256]{1,0:T(8,128)S(1)}, bf16[12,256,256]{2,1,0:T(8,128)(2,1)S(1)}) fusion(s32[1,1,12,256,256]{4,3,2,1,0:T(8,128)} %param.11), kind=kLoop, calls=%fused_computation.1 | loop fusion | flops 3139584 | bytes 4743168 | tf_op jit(solution)/shard_map/reduce_sum | solution.py:125
  17.7 0.7 copy.39
  18.4 0.7 select_reduce_fusion.1
  19.1 2.0 %fusion = bf16[3,4,256,256]{3,1,2,0:T(4,128)(2,1)S(1)} fusion(bf16[12,256,256]{2,1,0:T(8,128)(2,1)S(1)} %get-tuple-element.32, pred[12,4]{0,1:T(4,128)(4,1)} %copy.39, pred[12,3]{0,1:T(4,128)(4,1)} %fusion.61), kind=kOutput, calls=%fused_computation.2 | convolution fusion | flops 18874512 | bytes 3145812 | tf_op jit(solution)/shard_map/trc,tij->ricj/dot_general | solution.py:121
  21.2 1.5 %copy.59 = bf16[96,8,4,256]{3,1,2,0:T(8,128)(2,1)} copy(bf16[96,8,4,256]{3,2,1,0:T(4,128)(2,1)S(1)} %bitcast.245) | data formatting | bytes 3145728
  23.3 0.8 select_bitcast_fusion.19
  24.1 2.7 %collective-permute-start.4 = (bf16[4,64,256]{2,1,0:T(8,128)(2,1)S(1)}, bf16[4,64,256]{2,1,0:T(8,128)(2,1)S(1)}, u32[]{:S(2)}, u32[]{:S(2)}) collective-permute-start(bf16[4,64,256]{2,1,0:T(8,128)(2,1)S(1)} %maximum_bitcast_fusion), channel_id=1, source_target_pairs={{0,6},{2,4},{4,2},{6,0},{8,14},{10,12},{12,10},{14,8},{16,22},{18,... | collective-permute-start | bytes 393224 | tf_op jit(solution)/shard_map/ppermute | solution.py:43
  28.7 2.4 %collective-permute-done.4 = bf16[4,64,256]{2,1,0:T(8,128)(2,1)S(1)} collective-permute-done((bf16[4,64,256]{2,1,0:T(8,128)(2,1)S(1)}, bf16[4,64,256]{2,1,0:T(8,128)(2,1)S(1)}, u32[]{:S(2)}, u32[]{:S(2)}) %collective-permute-start.4) | collective-permute-done | bytes 131104 | tf_op jit(solution)/shard_map/ppermute | solution.py:43
  31.1 2.7 %collective-permute-done.5 = bf16[4,64,256]{2,1,0:T(8,128)(2,1)S(1)} collective-permute-done((bf16[4,64,256]{2,1,0:T(8,128)(2,1)S(1)}, bf16[4,64,256]{2,1,0:T(8,128)(2,1)S(1)}, u32[]{:S(2)}, u32[]{:S(2)}) %collective-permute-start.5) | collective-permute-done | bytes 131104 | tf_op jit(solution)/shard_map/ppermute | solution.py:43
  34.3 1.0 select_bitcast_fusion.3
  35.6 2.9 %fusion.5 = (f32[256]{0:T(256)S(1)}, f32[768,256]{1,0:T(8,128)}) fusion(bf16[1,2,384,256]{3,2,1,0:T(8,128)(2,1)S(1)} %copy.42, bf16[768,256]{1,0:T(8,128)(2,1)S(1)} %bitcast.270, f32[768]{0:T(1024)S(1)} %mul.262, bf16[768,1024]{1,0:T(8,128)(2,1)} %bitcast.246, bf16[1024,256]{1,0:T(8,128)(2,1)S(1)} %bitcast.262), kind=kOutput, calls=%fused_computation.22 | convolution fusion | flops 403832576 | bytes 3674112 | tf_op jit(solution)/shard_map/dot_general | solution.py:130
  38.7 2.2 %fusion.3 = (f32[256]{0:T(256)S(1)}, f32[1024,256]{1,0:T(8,128)S(1)}) fusion(bf16[4,4,64,256]{3,2,1,0:T(8,128)(2,1)S(1)} %copy.43, bf16[1024,256]{1,0:T(8,128)(2,1)S(1)} %bitcast.263, f32[1024]{0:T(1024)S(1)} %bitcast.277, bf16[768,1024]{1,0:T(8,128)(2,1)} %bitcast.247, bf16[768,256]{1,0:T(8,128)(2,1)S(1)} %bitcast.271), kind=kOutput, calls=%fused_computation.16 | convolution fusion | flops 404225792 | bytes 4068352 | tf_op jit(solution)/shard_map/dot_general | solution.py:132
  41.2 0.9 fusion.31
  42.1 1.5 %collective-permute-start.9 = (f32[264,256]{1,0:T(8,128)}, f32[264,256]{1,0:T(8,128)S(1)}, u32[]{:S(2)}, u32[]{:S(2)}) collective-permute-start(f32[264,256]{1,0:T(8,128)} %get-tuple-element.86), channel_id=1, source_target_pairs={{0,6},{2,4},{4,2},{6,0},{8,14},{10,12},{12,10},{14,8},{16,22},{18,... | collective-permute-start | bytes 811016 | tf_op jit(solution)/shard_map/ppermute | solution.py:43
  43.6 1.4 %collective-permute-start.8 = (f32[264,256]{1,0:T(8,128)}, f32[264,256]{1,0:T(8,128)S(1)}, u32[]{:S(2)}, u32[]{:S(2)}) collective-permute-start(f32[264,256]{1,0:T(8,128)} %get-tuple-element.85), channel_id=1, source_target_pairs={{0,4},{2,6},{4,0},{6,2},{8,12},{10,14},{12,8},{14,10},{16,20},{18,... | collective-permute-start | bytes 811016 | tf_op jit(solution)/shard_map/ppermute | solution.py:43
  45.6 0.8 copy.57
  46.4 6.2 %collective-permute-done.9 = f32[264,256]{1,0:T(8,128)S(1)} collective-permute-done((f32[264,256]{1,0:T(8,128)}, f32[264,256]{1,0:T(8,128)S(1)}, u32[]{:S(2)}, u32[]{:S(2)}) %collective-permute-start.9) | collective-permute-done | bytes 270368 | tf_op jit(solution)/shard_map/ppermute | solution.py:43
  52.6 4.5 %collective-permute-done.8 = f32[264,256]{1,0:T(8,128)S(1)} collective-permute-done((f32[264,256]{1,0:T(8,128)}, f32[264,256]{1,0:T(8,128)S(1)}, u32[]{:S(2)}, u32[]{:S(2)}) %collective-permute-start.8) | collective-permute-done | bytes 270368 | tf_op jit(solution)/shard_map/ppermute | solution.py:43
  57.6 0.7 dynamic-slice_bitcast_fusion.7
  58.2 0.7 pad_maximum_fusion.6
  58.9 3.6 %collective-permute-start.12 = (f32[72,256]{1,0:T(8,128)}, f32[72,256]{1,0:T(8,128)S(1)}, u32[]{:S(2)}, u32[]{:S(2)}) collective-permute-start(f32[72,256]{1,0:T(8,128)} %get-tuple-element.76), channel_id=1, source_target_pairs={{0,24},{2,26},{4,28},{6,30},{8,16},{10,18},{12,20},{14,22},{16,8},... | collective-permute-start | bytes 221192 | tf_op jit(solution)/shard_map/ppermute | solution.py:43
  62.5 0.8 collective-permute-start.10
  63.5 2.6 %collective-permute-done.12 = f32[72,256]{1,0:T(8,128)S(1)} collective-permute-done((f32[72,256]{1,0:T(8,128)}, f32[72,256]{1,0:T(8,128)S(1)}, u32[]{:S(2)}, u32[]{:S(2)}) %collective-permute-start.12) | collective-permute-done | bytes 73760 | tf_op jit(solution)/shard_map/ppermute | solution.py:43
  66.1 2.8 %collective-permute-done.11 = f32[72,256]{1,0:T(8,128)S(1)} collective-permute-done((f32[72,256]{1,0:T(8,128)}, f32[72,256]{1,0:T(8,128)S(1)}, u32[]{:S(2)}, u32[]{:S(2)}) %collective-permute-start.11) | collective-permute-done | bytes 73760 | tf_op jit(solution)/shard_map/ppermute | solution.py:43
  68.9 0.9 fusion.42
  69.9 1.1 collective-permute-done.13
  71.3 2.4 %collective-permute-start.16 = (bf16[1,64,256]{2,1,0:T(8,128)(2,1)S(1)}, bf16[1,64,256]{2,1,0:T(8,128)(2,1)S(1)}, u32[]{:S(2)}, u32[]{:S(2)}) collective-permute-start(bf16[1,64,256]{2,1,0:T(8,128)(2,1)S(1)} %get-tuple-element.30), channel_id=1, source_target_pairs={{0,24},{2,26},{4,28},{6,30},{8,16},{10,18},{12,20},{14,22},{16,8},... | collective-permute-start | bytes 98312 | tf_op jit(solution)/shard_map/ppermute | solution.py:43
  74.0 1.7 %collective-permute-start.18 = (bf16[1,64,256]{2,1,0:T(8,128)(2,1)S(1)}, bf16[1,64,256]{2,1,0:T(8,128)(2,1)S(1)}, u32[]{:S(2)}, u32[]{:S(2)}) collective-permute-start(bf16[1,64,256]{2,1,0:T(8,128)(2,1)S(1)} %get-tuple-element.30), channel_id=1, source_target_pairs={{0,8},{2,10},{4,12},{6,14},{8,0},{10,2},{12,4},{14,6},{16,24},{18,... | collective-permute-start | bytes 98312 | tf_op jit(solution)/shard_map/ppermute | solution.py:43
  75.9 0.7 multiply_reduce_fusion.1
  77.4 1.1 collective-permute-done.17
  78.6 1.5 %collective-permute-start.19 = (bf16[4,64,256]{2,1,0:T(8,128)(2,1)S(1)}, bf16[4,64,256]{2,1,0:T(8,128)(2,1)S(1)}, u32[]{:S(2)}, u32[]{:S(2)}) collective-permute-start(bf16[4,64,256]{2,1,0:T(8,128)(2,1)S(1)} %maximum_bitcast_fusion.1), channel_id=1, source_target_pairs={{0,6},{2,4},{4,2},{6,0},{8,14},{10,12},{12,10},{14,8},{16,22},{18,... | collective-permute-start | bytes 393224 | tf_op jit(solution)/shard_map/ppermute | solution.py:43
  80.1 1.4 %collective-permute-start.20 = (bf16[4,64,256]{2,1,0:T(8,128)(2,1)S(1)}, bf16[4,64,256]{2,1,0:T(8,128)(2,1)S(1)}, u32[]{:S(2)}, u32[]{:S(2)}) collective-permute-start(bf16[4,64,256]{2,1,0:T(8,128)(2,1)S(1)} %maximum_bitcast_fusion.1), channel_id=1, source_target_pairs={{0,4},{2,6},{4,0},{6,2},{8,12},{10,14},{12,8},{14,10},{16,20},{18,... | collective-permute-start | bytes 393224 | tf_op jit(solution)/shard_map/ppermute | solution.py:43
  82.1 0.9 multiply_reduce_fusion.3
  84.6 1.1 collective-permute-done.19
  85.7 1.4 %collective-permute-done.20 = bf16[4,64,256]{2,1,0:T(8,128)(2,1)S(1)} collective-permute-done((bf16[4,64,256]{2,1,0:T(8,128)(2,1)S(1)}, bf16[4,64,256]{2,1,0:T(8,128)(2,1)S(1)}, u32[]{:S(2)}, u32[]{:S(2)}) %collective-permute-start.20) | collective-permute-done | bytes 131104 | tf_op jit(solution)/shard_map/ppermute | solution.py:43
  87.3 0.8 copy.48
  88.1 1.0 select_bitcast_fusion.1
  89.4 3.2 %fusion.6 = (f32[256]{0:T(256)S(1)}, f32[768,256]{1,0:T(8,128)}) fusion(bf16[1,2,384,256]{3,2,1,0:T(8,128)(2,1)S(1)} %copy.47, bf16[768,256]{1,0:T(8,128)(2,1)S(1)} %bitcast.272, f32[768]{0:T(1024)S(1)} %mul.262, bf16[768,1024]{1,0:T(8,128)(2,1)} %bitcast.248, bf16[1024,256]{1,0:T(8,128)(2,1)} %bitcast.264), kind=kOutput, calls=%fused_computation.23 | convolution fusion | flops 403832576 | bytes 3674112 | tf_op jit(solution)/shard_map/dot_general | solution.py:130
  92.5 1.9 %fusion.4 = (f32[256]{0:T(256)S(1)}, f32[1024,256]{1,0:T(8,128)}) fusion(bf16[4,4,64,256]{3,2,1,0:T(8,128)(2,1)S(1)} %copy-done.12, bf16[1024,256]{1,0:T(8,128)(2,1)S(1)} %bitcast.265, f32[1024]{0:T(1024)S(1)} %bitcast.278, bf16[768,1024]{1,0:T(8,128)(2,1)S(1)} %bitcast.249, bf16[768,256]{1,0:T(8,128)(2,1)S(1)} %bitcast.273), kind=kOutput, calls=%fused_computation.17 | convolution fusion | flops 404225792 | bytes 4068352 | tf_op jit(solution)/shard_map/dot_general | solution.py:132
  94.9 1.4 %constant_dynamic-slice_fusion.5 = (f32[2,2,1,1,64,256]{5,4,3,2,1,0:T(8,128)S(1)}, f32[2,2,1,1,64,256]{5,4,3,2,1,0:T(8,128)S(1)}, f32[2,2,1,1,64,256]{5,4,3,2,1,0:T(8,128)S(1)}, f32[2,2,1,1,64,256]{5,4,3,2,1,0:T(8,128)S(1)}) fusion(f32[2,2,2,2,64,256]{5,4,3,2,1,0:T(8,128)} %bitcast.250, s32[]{:T(128)S(6)} %select_n.380, s32[]{:T(128)S(6)} %select_n.382, ...), kind=kLoop, calls=%fused_computation.152 | loop fusion | bytes 2097184 | tf_op jit(solution)/shard_map/jit(dynamic_index_in_dim)/dynamic_slice | solution.py:69
  96.4 0.9 fusion.23
  97.3 1.5 %collective-permute-start.24 = (f32[264,256]{1,0:T(8,128)}, f32[264,256]{1,0:T(8,128)}, u32[]{:S(2)}, u32[]{:S(2)}) collective-permute-start(f32[264,256]{1,0:T(8,128)} %get-tuple-element.83), channel_id=1, source_target_pairs={{0,6},{2,4},{4,2},{6,0},{8,14},{10,12},{12,10},{14,8},{16,22},{18,... | collective-permute-start | bytes 811016 | tf_op jit(solution)/shard_map/ppermute | solution.py:43
  98.7 1.4 %collective-permute-start.23 = (f32[264,256]{1,0:T(8,128)}, f32[264,256]{1,0:T(8,128)}, u32[]{:S(2)}, u32[]{:S(2)}) collective-permute-start(f32[264,256]{1,0:T(8,128)} %get-tuple-element.82), channel_id=1, source_target_pairs={{0,4},{2,6},{4,0},{6,2},{8,12},{10,14},{12,8},{14,10},{16,20},{18,... | collective-permute-start | bytes 811016 | tf_op jit(solution)/shard_map/ppermute | solution.py:43
  100.9 7.0 %collective-permute-done.24 = f32[264,256]{1,0:T(8,128)} collective-permute-done((f32[264,256]{1,0:T(8,128)}, f32[264,256]{1,0:T(8,128)}, u32[]{:S(2)}, u32[]{:S(2)}) %collective-permute-start.24) | collective-permute-done | bytes 270368 | tf_op jit(solution)/shard_map/ppermute | solution.py:43
  107.9 4.3 %collective-permute-done.23 = f32[264,256]{1,0:T(8,128)} collective-permute-done((f32[264,256]{1,0:T(8,128)}, f32[264,256]{1,0:T(8,128)}, u32[]{:S(2)}, u32[]{:S(2)}) %collective-permute-start.23) | collective-permute-done | bytes 270368 | tf_op jit(solution)/shard_map/ppermute | solution.py:43
  112.2 1.2 fusion.28
  114.1 3.0 %collective-permute-start.27 = (f32[72,256]{1,0:T(8,128)}, f32[72,256]{1,0:T(8,128)S(1)}, u32[]{:S(2)}, u32[]{:S(2)}) collective-permute-start(f32[72,256]{1,0:T(8,128)} %get-tuple-element.73), channel_id=1, source_target_pairs={{0,24},{2,26},{4,28},{6,30},{8,16},{10,18},{12,20},{14,22},{16,8},... | collective-permute-start | bytes 221192 | tf_op jit(solution)/shard_map/ppermute | solution.py:43
  117.1 1.4 %collective-permute-start.25 = (f32[72,256]{1,0:T(8,128)S(1)}, f32[72,256]{1,0:T(8,128)S(1)}, u32[]{:S(2)}, u32[]{:S(2)}) collective-permute-start(f32[72,256]{1,0:T(8,128)S(1)} %get-tuple-element.71), channel_id=1, source_target_pairs={{0,8},{2,10},{4,12},{6,14},{8,0},{10,2},{12,4},{14,6},{16,24},{18,... | collective-permute-start | bytes 221192 | tf_op jit(solution)/shard_map/ppermute | solution.py:43
  118.5 1.0 constant_dynamic-slice_fusion
  119.8 1.4 %collective-permute-done.27 = f32[72,256]{1,0:T(8,128)S(1)} collective-permute-done((f32[72,256]{1,0:T(8,128)}, f32[72,256]{1,0:T(8,128)S(1)}, u32[]{:S(2)}, u32[]{:S(2)}) %collective-permute-start.27) | collective-permute-done | bytes 73760 | tf_op jit(solution)/shard_map/ppermute | solution.py:43
  121.2 2.3 %collective-permute-done.26 = f32[72,256]{1,0:T(8,128)S(1)} collective-permute-done((f32[72,256]{1,0:T(8,128)S(1)}, f32[72,256]{1,0:T(8,128)S(1)}, u32[]{:S(2)}, u32[]{:S(2)}) %collective-permute-start.26) | collective-permute-done | bytes 73760 | tf_op jit(solution)/shard_map/ppermute | solution.py:43
  124.1 0.9 fusion.39
  125.1 1.1 collective-permute-done.28
  126.6 0.7 copy-done.17
  127.3 1.2 fusion.13
  128.5 0.9 copy.53
  129.4 1.6 %fusion.47 = (f32[1,64,256]{2,1,0:T(8,128)}, f32[1,64,256]{2,1,0:T(8,128)}) fusion(f32[64,256]{1,0:T(8,128)S(1)} %copy-done.10, f32[64,256]{1,0:T(8,128)} %get-tuple-element.98, f32[72,256]{1,0:T(8,128)} %copy-done.15, f32[256]{0:T(256)S(1)} %mul.288, f32[256]{0:T(256)S(1)} %mul.286, f32[64,256]{1,0:T(8,128)S(1)} %copy-done.8, f32[72,256]{1,0:T(8,128)} %copy-done.11, ...), kind=kLoop, calls=%fused_computation.107 | loop fusion | flops 212992 | bytes 527360 | tf_op jit(solution)/shard_map/broadcast_in_dim | solution.py:192
  131.0 0.9 copy.54
  (167 shorter events, 14.1 us)
Async XLA Ops:
  2.1 9.6 %copy-start.6 = (f32[1,384,256]{2,1,0:T(8,128)S(1)}, f32[1,384,256]{2,1,0:T(8,128)}, u32[]{:S(2)}) copy-start(f32[1,384,256]{2,1,0:T(8,128)} %param.7) | copy-start | bytes 1179652
  2.1 21.1 %collective-permute-start.1 = (bf16[1,64,256]{2,1,0:T(8,128)(2,1)}, bf16[1,64,256]{2,1,0:T(8,128)(2,1)}, u32[]{:S(2)}, u32[]{:S(2)}) collective-permute-start(bf16[1,64,256]{2,1,0:T(8,128)(2,1)} %convert_element_type.78), channel_id=1, source_target_pairs={{0,24},{2,26},{4,28},{6,30},{8,16},{10,18},{12,20},{14,22},{16,8},... | collective-permute-start | bytes 98312 | tf_op jit(solution)/shard_map/ppermute | solution.py:43
  7.1 16.1 %collective-permute-start.2 = (bf16[1,64,256]{2,1,0:T(8,128)(2,1)}, bf16[1,64,256]{2,1,0:T(8,128)(2,1)}, u32[]{:S(2)}, u32[]{:S(2)}) collective-permute-start(bf16[1,64,256]{2,1,0:T(8,128)(2,1)} %convert_element_type.78), channel_id=1, source_target_pairs={{0,16},{2,18},{4,20},{6,22},{8,24},{10,26},{12,28},{14,30},{16,0},... | collective-permute-start | bytes 98312 | tf_op jit(solution)/shard_map/ppermute | solution.py:43
  7.1 16.1 %collective-permute-start.3 = (bf16[1,64,256]{2,1,0:T(8,128)(2,1)}, bf16[1,64,256]{2,1,0:T(8,128)(2,1)}, u32[]{:S(2)}, u32[]{:S(2)}) collective-permute-start(bf16[1,64,256]{2,1,0:T(8,128)(2,1)} %convert_element_type.78), channel_id=1, source_target_pairs={{0,8},{2,10},{4,12},{6,14},{8,0},{10,2},{12,4},{14,6},{16,24},{18,... | collective-permute-start | bytes 98312 | tf_op jit(solution)/shard_map/ppermute | solution.py:43
  9.6 24.8 %collective-permute-start = (bf16[1,384,256]{1,2,0:T(8,128)(2,1)}, bf16[1,384,256]{1,2,0:T(8,128)(2,1)}, u32[]{:S(2)}, u32[]{:S(2)}) collective-permute-start(bf16[1,384,256]{1,2,0:T(8,128)(2,1)} %convert_element_type.76), channel_id=1, source_target_pairs={{0,1},{1,0},{2,3},{3,2},{4,5},{5,4},{6,7},{7,6},{8,9},{9,8},{10,11... | collective-permute-start | bytes 589832 | tf_op jit(solution)/shard_map/ppermute | solution.py:43
  11.7 4.8 %copy-start.1 = (f32[256,256]{1,0:T(8,128)}, f32[256,256]{1,0:T(8,128)S(1)}, u32[]{:S(2)}) copy-start(f32[256,256]{1,0:T(8,128)S(1)} %mul.256) | copy-start | bytes 786436
  14.1 2.4 %copy-start.25 = (s32[1,1,12,2]{2,3,1,0:T(2,128)S(1)}, s32[1,1,12,2]{2,3,1,0:T(2,128)}, u32[]{:S(2)}) copy-start(s32[1,1,12,2]{2,3,1,0:T(2,128)} %param.12) | copy-start | bytes 292
  19.1 2.0 %copy-start.22 = (pred[12,3]{0,1:T(4,128)(4,1)S(1)}, pred[12,3]{0,1:T(4,128)(4,1)}, u32[]{:S(2)}) copy-start(pred[12,3]{0,1:T(4,128)(4,1)} %fusion.61) | copy-start | bytes 112
  21.2 1.6 %copy-start.19 = (f32[4,256]{1,0:T(4,128)S(1)}, f32[4,256]{1,0:T(4,128)}, u32[]{:S(2)}) copy-start(f32[4,256]{1,0:T(4,128)} %select_reduce_fusion.1) | copy-start | bytes 12292
  21.2 1.6 %copy-start.21 = (f32[256]{0:T(256)S(1)}, f32[256]{0:T(256)}, u32[]{:S(2)}) copy-start(f32[256]{0:T(256)} %get-tuple-element.21) | copy-start | bytes 3076
  21.2 1.6 %copy-start.3 = (f32[4,64,4,64]{3,2,1,0:T(4,128)S(1)}, f32[4,64,4,64]{3,2,1,0:T(4,128)}, u32[]{:S(2)}) copy-start(f32[4,64,4,64]{3,2,1,0:T(4,128)} %get-tuple-element.77) | copy-start | bytes 786436
  21.2 2.0 %copy-start.4 = (f32[1,64,256]{2,1,0:T(8,128)S(1)}, f32[1,64,256]{2,1,0:T(8,128)}, u32[]{:S(2)}) copy-start(f32[1,64,256]{2,1,0:T(8,128)} %param.8) | copy-start | bytes 196612
  22.8 5.5 %copy-start.20 = (f32[256]{0:T(256)S(1)}, f32[256]{0:T(256)}, u32[]{:S(2)}) copy-start(f32[256]{0:T(256)} %get-tuple-element.20) | copy-start | bytes 3076
  24.1 7.0 %collective-permute-start.4 = (bf16[4,64,256]{2,1,0:T(8,128)(2,1)S(1)}, bf16[4,64,256]{2,1,0:T(8,128)(2,1)S(1)}, u32[]{:S(2)}, u32[]{:S(2)}) collective-permute-start(bf16[4,64,256]{2,1,0:T(8,128)(2,1)S(1)} %maximum_bitcast_fusion), channel_id=1, source_target_pairs={{0,6},{2,4},{4,2},{6,0},{8,14},{10,12},{12,10},{14,8},{16,22},{18,... | collective-permute-start | bytes 393224 | tf_op jit(solution)/shard_map/ppermute | solution.py:43
  26.8 7.0 %collective-permute-start.5 = (bf16[4,64,256]{2,1,0:T(8,128)(2,1)S(1)}, bf16[4,64,256]{2,1,0:T(8,128)(2,1)S(1)}, u32[]{:S(2)}, u32[]{:S(2)}) collective-permute-start(bf16[4,64,256]{2,1,0:T(8,128)(2,1)S(1)} %maximum_bitcast_fusion), channel_id=1, source_target_pairs={{0,4},{2,6},{4,0},{6,2},{8,12},{10,14},{12,8},{14,10},{16,20},{18,... | collective-permute-start | bytes 393224 | tf_op jit(solution)/shard_map/ppermute | solution.py:43
  27.3 6.8 %collective-permute-start.6 = (bf16[4,64,256]{2,1,0:T(8,128)(2,1)S(1)}, bf16[4,64,256]{2,1,0:T(8,128)(2,1)S(1)}, u32[]{:S(2)}, u32[]{:S(2)}) collective-permute-start(bf16[4,64,256]{2,1,0:T(8,128)(2,1)S(1)} %maximum_bitcast_fusion), channel_id=1, source_target_pairs={{0,2},{2,0},{4,6},{6,4},{8,10},{10,8},{12,14},{14,12},{16,18},{18,... | collective-permute-start | bytes 393224 | tf_op jit(solution)/shard_map/ppermute | solution.py:43
  28.0 43.3 %copy-start.7 = (f32[64,256]{1,0:T(8,128)}, f32[64,256]{1,0:T(8,128)S(1)}, u32[]{:S(2)}) copy-start(f32[64,256]{1,0:T(8,128)S(1)} %get-tuple-element.92) | copy-start | bytes 196612
  41.1 4.5 %copy-start.13 = (f32[768,256]{1,0:T(8,128)S(1)}, f32[768,256]{1,0:T(8,128)}, u32[]{:S(2)}) copy-start(f32[768,256]{1,0:T(8,128)} %get-tuple-element.88) | copy-start | bytes 2359300
  42.1 10.5 %collective-permute-start.9 = (f32[264,256]{1,0:T(8,128)}, f32[264,256]{1,0:T(8,128)S(1)}, u32[]{:S(2)}, u32[]{:S(2)}) collective-permute-start(f32[264,256]{1,0:T(8,128)} %get-tuple-element.86), channel_id=1, source_target_pairs={{0,6},{2,4},{4,2},{6,0},{8,14},{10,12},{12,10},{14,8},{16,22},{18,... | collective-permute-start | bytes 811016 | tf_op jit(solution)/shard_map/ppermute | solution.py:43
  43.6 13.5 %collective-permute-start.8 = (f32[264,256]{1,0:T(8,128)}, f32[264,256]{1,0:T(8,128)S(1)}, u32[]{:S(2)}, u32[]{:S(2)}) collective-permute-start(f32[264,256]{1,0:T(8,128)} %get-tuple-element.85), channel_id=1, source_target_pairs={{0,4},{2,6},{4,0},{6,2},{8,12},{10,14},{12,8},{14,10},{16,20},{18,... | collective-permute-start | bytes 811016 | tf_op jit(solution)/shard_map/ppermute | solution.py:43
  45.0 12.4 %collective-permute-start.7 = (f32[264,256]{1,0:T(8,128)S(1)}, f32[264,256]{1,0:T(8,128)S(1)}, u32[]{:S(2)}, u32[]{:S(2)}) collective-permute-start(f32[264,256]{1,0:T(8,128)S(1)} %get-tuple-element.84), channel_id=1, source_target_pairs={{0,2},{2,0},{4,6},{6,4},{8,10},{10,8},{12,14},{14,12},{16,18},{18,... | collective-permute-start | bytes 811016 | tf_op jit(solution)/shard_map/ppermute | solution.py:43
  46.4 29.3 %collective-permute-start.14 = (bf16[384,256]{0,1:T(8,128)(2,1)}, bf16[384,256]{0,1:T(8,128)(2,1)S(1)}, u32[]{:S(2)}, u32[]{:S(2)}) collective-permute-start(bf16[384,256]{0,1:T(8,128)(2,1)} %bitcast.274), channel_id=1, source_target_pairs={{0,1},{1,0},{2,3},{3,2},{4,5},{5,4},{6,7},{7,6},{8,9},{9,8},{10,11... | collective-permute-start | bytes 589832 | tf_op jit(solution)/shard_map/ppermute | solution.py:43
  57.6 18.2 %copy-start = (f32[384,256]{0,1:T(8,128)S(1)}, f32[384,256]{0,1:T(8,128)}, u32[]{:S(2)}) copy-start(f32[384,256]{0,1:T(8,128)} %get-tuple-element.91) | copy-start | bytes 1179652
  58.2 10.6 %copy-start.16 = (f32[64,256]{1,0:T(8,128)S(1)}, f32[64,256]{1,0:T(8,128)}, u32[]{:S(2)}) copy-start(f32[64,256]{1,0:T(8,128)} %get-tuple-element.57) | copy-start | bytes 196612
  58.9 7.2 %collective-permute-start.12 = (f32[72,256]{1,0:T(8,128)}, f32[72,256]{1,0:T(8,128)S(1)}, u32[]{:S(2)}, u32[]{:S(2)}) collective-permute-start(f32[72,256]{1,0:T(8,128)} %get-tuple-element.76), channel_id=1, source_target_pairs={{0,24},{2,26},{4,28},{6,30},{8,16},{10,18},{12,20},{14,22},{16,8},... | collective-permute-start | bytes 221192 | tf_op jit(solution)/shard_map/ppermute | solution.py:43
  62.5 6.4 %collective-permute-start.11 = (f32[72,256]{1,0:T(8,128)}, f32[72,256]{1,0:T(8,128)S(1)}, u32[]{:S(2)}, u32[]{:S(2)}) collective-permute-start(f32[72,256]{1,0:T(8,128)} %get-tuple-element.75), channel_id=1, source_target_pairs={{0,16},{2,18},{4,20},{6,22},{8,24},{10,26},{12,28},{14,30},{16,0},... | collective-permute-start | bytes 221192 | tf_op jit(solution)/shard_map/ppermute | solution.py:43
  62.5 6.4 %collective-permute-start.10 = (f32[72,256]{1,0:T(8,128)S(1)}, f32[72,256]{1,0:T(8,128)}, u32[]{:S(2)}, u32[]{:S(2)}) collective-permute-start(f32[72,256]{1,0:T(8,128)S(1)} %get-tuple-element.74), channel_id=1, source_target_pairs={{0,8},{2,10},{4,12},{6,14},{8,0},{10,2},{12,4},{14,6},{16,24},{18,... | collective-permute-start | bytes 221192 | tf_op jit(solution)/shard_map/ppermute | solution.py:43
  63.3 12.5 %copy-start.2 = (f32[256,256]{1,0:T(8,128)S(1)}, f32[256,256]{1,0:T(8,128)}, u32[]{:S(2)}) copy-start(f32[256,256]{1,0:T(8,128)} %copy-done.1) | copy-start | bytes 786436
  69.8 5.9 %copy-start.11 = (f32[72,256]{1,0:T(8,128)}, f32[72,256]{1,0:T(8,128)S(1)}, u32[]{:S(2)}) copy-start(f32[72,256]{1,0:T(8,128)S(1)} %fusion.42) | copy-start | bytes 221188
  69.8 1.2 collective-permute-start.13
  71.3 10.9 %copy-start.9 = (f32[64,256]{1,0:T(8,128)}, f32[64,256]{1,0:T(8,128)S(1)}, u32[]{:S(2)}) copy-start(f32[64,256]{1,0:T(8,128)S(1)} %get-tuple-element.31) | copy-start | bytes 196612
  71.3 6.1 %collective-permute-start.16 = (bf16[1,64,256]{2,1,0:T(8,128)(2,1)S(1)}, bf16[1,64,256]{2,1,0:T(8,128)(2,1)S(1)}, u32[]{:S(2)}, u32[]{:S(2)}) collective-permute-start(bf16[1,64,256]{2,1,0:T(8,128)(2,1)S(1)} %get-tuple-element.30), channel_id=1, source_target_pairs={{0,24},{2,26},{4,28},{6,30},{8,16},{10,18},{12,20},{14,22},{16,8},... | collective-permute-start | bytes 98312 | tf_op jit(solution)/shard_map/ppermute | solution.py:43
  73.7 4.8 %collective-permute-start.17 = (bf16[1,64,256]{2,1,0:T(8,128)(2,1)S(1)}, bf16[1,64,256]{2,1,0:T(8,128)(2,1)S(1)}, u32[]{:S(2)}, u32[]{:S(2)}) collective-permute-start(bf16[1,64,256]{2,1,0:T(8,128)(2,1)S(1)} %get-tuple-element.30), channel_id=1, source_target_pairs={{0,16},{2,18},{4,20},{6,22},{8,24},{10,26},{12,28},{14,30},{16,0},... | collective-permute-start | bytes 98312 | tf_op jit(solution)/shard_map/ppermute | solution.py:43
  74.0 4.5 %collective-permute-start.18 = (bf16[1,64,256]{2,1,0:T(8,128)(2,1)S(1)}, bf16[1,64,256]{2,1,0:T(8,128)(2,1)S(1)}, u32[]{:S(2)}, u32[]{:S(2)}) collective-permute-start(bf16[1,64,256]{2,1,0:T(8,128)(2,1)S(1)} %get-tuple-element.30), channel_id=1, source_target_pairs={{0,8},{2,10},{4,12},{6,14},{8,0},{10,2},{12,4},{14,6},{16,24},{18,... | collective-permute-start | bytes 98312 | tf_op jit(solution)/shard_map/ppermute | solution.py:43
  76.6 11.6 %collective-permute-start.15 = (bf16[1,384,256]{1,2,0:T(8,128)(2,1)S(1)}, bf16[1,384,256]{1,2,0:T(8,128)(2,1)}, u32[]{:S(2)}, u32[]{:S(2)}) collective-permute-start(bf16[1,384,256]{1,2,0:T(8,128)(2,1)S(1)} %get-tuple-element.28), channel_id=1, source_target_pairs={{0,1},{1,0},{2,3},{3,2},{4,5},{5,4},{6,7},{7,6},{8,9},{9,8},{10,11... | collective-permute-start | bytes 589832 | tf_op jit(solution)/shard_map/ppermute | solution.py:43
  78.6 7.2 %collective-permute-start.19 = (bf16[4,64,256]{2,1,0:T(8,128)(2,1)S(1)}, bf16[4,64,256]{2,1,0:T(8,128)(2,1)S(1)}, u32[]{:S(2)}, u32[]{:S(2)}) collective-permute-start(bf16[4,64,256]{2,1,0:T(8,128)(2,1)S(1)} %maximum_bitcast_fusion.1), channel_id=1, source_target_pairs={{0,6},{2,4},{4,2},{6,0},{8,14},{10,12},{12,10},{14,8},{16,22},{18,... | collective-permute-start | bytes 393224 | tf_op jit(solution)/shard_map/ppermute | solution.py:43
  80.1 7.0 %collective-permute-start.20 = (bf16[4,64,256]{2,1,0:T(8,128)(2,1)S(1)}, bf16[4,64,256]{2,1,0:T(8,128)(2,1)S(1)}, u32[]{:S(2)}, u32[]{:S(2)}) collective-permute-start(bf16[4,64,256]{2,1,0:T(8,128)(2,1)S(1)} %maximum_bitcast_fusion.1), channel_id=1, source_target_pairs={{0,4},{2,6},{4,0},{6,2},{8,12},{10,14},{12,8},{14,10},{16,20},{18,... | collective-permute-start | bytes 393224 | tf_op jit(solution)/shard_map/ppermute | solution.py:43
  81.5 5.6 %collective-permute-start.21 = (bf16[4,64,256]{2,1,0:T(8,128)(2,1)S(1)}, bf16[4,64,256]{2,1,0:T(8,128)(2,1)S(1)}, u32[]{:S(2)}, u32[]{:S(2)}) collective-permute-start(bf16[4,64,256]{2,1,0:T(8,128)(2,1)S(1)} %maximum_bitcast_fusion.1), channel_id=1, source_target_pairs={{0,2},{2,0},{4,6},{6,4},{8,10},{10,8},{12,14},{14,12},{16,18},{18,... | collective-permute-start | bytes 393224 | tf_op jit(solution)/shard_map/ppermute | solution.py:43
  89.3 3.2 %copy-start.5 = (bf16[96,8,4,256]{3,1,2,0:T(8,128)(2,1)S(1)}, bf16[96,8,4,256]{3,1,2,0:T(8,128)(2,1)}, u32[]{:S(2)}) copy-start(bf16[96,8,4,256]{3,1,2,0:T(8,128)(2,1)} %copy.59) | copy-start | bytes 4718596
  89.4 3.2 %copy-start.12 = (bf16[4,4,64,256]{3,2,1,0:T(8,128)(2,1)S(1)}, bf16[4,4,64,256]{3,2,1,0:T(8,128)(2,1)}, u32[]{:S(2)}) copy-start(bf16[4,4,64,256]{3,2,1,0:T(8,128)(2,1)} %copy.48) | copy-start | bytes 1572868
  94.5 1.8 %copy-start.23 = (f32[4]{0:T(128)S(1)}, f32[4]{0:T(128)}, u32[]{:S(2)}) copy-start(f32[4]{0:T(128)} %reduce_sum.273) | copy-start | bytes 52
  94.5 1.8 %copy-start.24 = (f32[4]{0:T(128)S(1)}, f32[4]{0:T(128)}, u32[]{:S(2)}) copy-start(f32[4]{0:T(128)} %reduce_sum.275) | copy-start | bytes 52
  94.5 1.8 %copy-start.26 = (f32[4]{0:T(128)S(1)}, f32[4]{0:T(128)}, u32[]{:S(2)}) copy-start(f32[4]{0:T(128)} %add.324) | copy-start | bytes 52
  94.9 5.9 %copy-start.14 = (f32[768,256]{1,0:T(8,128)S(1)}, f32[768,256]{1,0:T(8,128)}, u32[]{:S(2)}) copy-start(f32[768,256]{1,0:T(8,128)} %get-tuple-element.94) | copy-start | bytes 2359300
  97.3 10.7 %collective-permute-start.24 = (f32[264,256]{1,0:T(8,128)}, f32[264,256]{1,0:T(8,128)}, u32[]{:S(2)}, u32[]{:S(2)}) collective-permute-start(f32[264,256]{1,0:T(8,128)} %get-tuple-element.83), channel_id=1, source_target_pairs={{0,6},{2,4},{4,2},{6,0},{8,14},{10,12},{12,10},{14,8},{16,22},{18,... | collective-permute-start | bytes 811016 | tf_op jit(solution)/shard_map/ppermute | solution.py:43
  98.7 13.5 %collective-permute-start.23 = (f32[264,256]{1,0:T(8,128)}, f32[264,256]{1,0:T(8,128)}, u32[]{:S(2)}, u32[]{:S(2)}) collective-permute-start(f32[264,256]{1,0:T(8,128)} %get-tuple-element.82), channel_id=1, source_target_pairs={{0,4},{2,6},{4,0},{6,2},{8,12},{10,14},{12,8},{14,10},{16,20},{18,... | collective-permute-start | bytes 811016 | tf_op jit(solution)/shard_map/ppermute | solution.py:43
  100.1 12.1 %collective-permute-start.22 = (f32[264,256]{1,0:T(8,128)}, f32[264,256]{1,0:T(8,128)}, u32[]{:S(2)}, u32[]{:S(2)}) collective-permute-start(f32[264,256]{1,0:T(8,128)} %get-tuple-element.81), channel_id=1, source_target_pairs={{0,2},{2,0},{4,6},{6,4},{8,10},{10,8},{12,14},{14,12},{16,18},{18,... | collective-permute-start | bytes 811016 | tf_op jit(solution)/shard_map/ppermute | solution.py:43
  114.1 7.1 %collective-permute-start.27 = (f32[72,256]{1,0:T(8,128)}, f32[72,256]{1,0:T(8,128)S(1)}, u32[]{:S(2)}, u32[]{:S(2)}) collective-permute-start(f32[72,256]{1,0:T(8,128)} %get-tuple-element.73), channel_id=1, source_target_pairs={{0,24},{2,26},{4,28},{6,30},{8,16},{10,18},{12,20},{14,22},{16,8},... | collective-permute-start | bytes 221192 | tf_op jit(solution)/shard_map/ppermute | solution.py:43
  117.1 6.3 %collective-permute-start.26 = (f32[72,256]{1,0:T(8,128)S(1)}, f32[72,256]{1,0:T(8,128)S(1)}, u32[]{:S(2)}, u32[]{:S(2)}) collective-permute-start(f32[72,256]{1,0:T(8,128)S(1)} %get-tuple-element.72), channel_id=1, source_target_pairs={{0,16},{2,18},{4,20},{6,22},{8,24},{10,26},{12,28},{14,30},{16,0},... | collective-permute-start | bytes 221192 | tf_op jit(solution)/shard_map/ppermute | solution.py:43
  117.1 6.3 %collective-permute-start.25 = (f32[72,256]{1,0:T(8,128)S(1)}, f32[72,256]{1,0:T(8,128)S(1)}, u32[]{:S(2)}, u32[]{:S(2)}) collective-permute-start(f32[72,256]{1,0:T(8,128)S(1)} %get-tuple-element.71), channel_id=1, source_target_pairs={{0,8},{2,10},{4,12},{6,14},{8,0},{10,2},{12,4},{14,6},{16,24},{18,... | collective-permute-start | bytes 221192 | tf_op jit(solution)/shard_map/ppermute | solution.py:43
  119.7 6.9 %collective-permute-start.29 = (bf16[384,256]{0,1:T(8,128)(2,1)S(1)}, bf16[384,256]{0,1:T(8,128)(2,1)S(1)}, u32[]{:S(2)}, u32[]{:S(2)}) collective-permute-start(bf16[384,256]{0,1:T(8,128)(2,1)S(1)} %bitcast.275), channel_id=1, source_target_pairs={{0,1},{1,0},{2,3},{3,2},{4,5},{5,4},{6,7},{7,6},{8,9},{9,8},{10,11... | collective-permute-start | bytes 589832 | tf_op jit(solution)/shard_map/ppermute | solution.py:43
  123.5 0.6 copy-start.18
  125.0 1.6 %copy-start.15 = (f32[72,256]{1,0:T(8,128)}, f32[72,256]{1,0:T(8,128)S(1)}, u32[]{:S(2)}) copy-start(f32[72,256]{1,0:T(8,128)S(1)} %fusion.39) | copy-start | bytes 221188
  125.0 1.2 collective-permute-start.28
  126.6 0.7 copy-start.17
  127.3 2.1 %copy-start.8 = (f32[64,256]{1,0:T(8,128)S(1)}, f32[64,256]{1,0:T(8,128)}, u32[]{:S(2)}) copy-start(f32[64,256]{1,0:T(8,128)} %copy-done.7) | copy-start | bytes 196612
  127.3 2.1 %copy-start.10 = (f32[64,256]{1,0:T(8,128)S(1)}, f32[64,256]{1,0:T(8,128)}, u32[]{:S(2)}) copy-start(f32[64,256]{1,0:T(8,128)} %copy-done.9) | copy-start | bytes 196612

commit v9 on v7

--- a/solution.py
+++ b/solution.py
@@ -54,14 +54,22 @@
     return values[0], values[1]
 
 
-def halve_sum(part, axis, send_type, extra=None):
+def code_rows(extra):
+    high = extra.astype(jnp.bfloat16)
+    rest = extra - high.astype(jnp.float32)
+    mid = rest.astype(jnp.bfloat16)
+    low = (rest - mid.astype(jnp.float32)).astype(jnp.bfloat16)
+    return jnp.concatenate([high, mid, low])
+
+
+def halve_sum(part, axis, send_type, extra=None, first_type=None):
     size, bits = bit_count(axis)
     me = lax.axis_index(axis)
     rows, width = part.shape[0] // size, part.shape[1]
     groups = [list(range(bits))[i : i + 2] for i in range(0, bits, 2)]
     left = list(range(bits))[::-1]
     buf = part.reshape([2] * bits + [rows, width])
-    for group in groups:
+    for stage, group in enumerate(groups):
         masks = [sum(1 << group[j] for j in range(len(group)) if (k >> j) & 1) for k in range(1 << len(group))]
         digit = sum(((me >> group[j]) & 1) << j for j in range(len(group)))
 
@@ -71,18 +79,28 @@
                 out = lax.dynamic_index_in_dim(out, (value >> j) & 1, left.index(group[j]), keepdims=False)
             return out
 
+        coded = extra is not None and stage == 0 and first_type is not None
+        stage_type = first_type if (stage == 0 and first_type is not None) else send_type
         total = block_of(digit)
         shape = total.shape
         if extra is not None:
-            total = jnp.concatenate([total.reshape(-1, width), extra])
+            tail = jnp.concatenate([extra, jnp.zeros((2 * extra.shape[0], width), extra.dtype)]) if coded else extra
+            total = jnp.concatenate([total.reshape(-1, width), tail])
         for k in range(1, len(masks)):
-            send = block_of(digit ^ k).astype(send_type)
+            send = block_of(digit ^ k).astype(stage_type)
             if extra is not None:
-                send = jnp.concatenate([send.reshape(-1, width), extra])
+                tail = code_rows(extra) if coded else extra
+                send = jnp.concatenate([send.reshape(-1, width), tail.astype(stage_type)])
             total = total + swap_with(send, axis, size, None, masks[k]).astype(jnp.float32)
         if extra is not None:
-            extra = total[-extra.shape[0] :]
-            total = total[: -extra.shape[0]].reshape(shape)
+            count = extra.shape[0]
+            if coded:
+                tail = total[-3 * count :]
+                total = total[: -3 * count].reshape(shape)
+                extra = tail[:count] + tail[count : 2 * count] + tail[2 * count :]
+            else:
+                extra = total[-count:]
+                total = total[:-count].reshape(shape)
         for bit in group:
             left.remove(bit)
         buf = total
@@ -161,7 +179,7 @@
         sums = jnp.concatenate([norm_part, curve_part]).reshape(1, 2 * DRAWS)
         sums = jnp.pad(sums, ((0, 7), (0, width - 2 * DRAWS)))
         total_user, _ = halve_sum(part_user, "item", jnp.bfloat16)
-        total_item, sums = halve_sum(part_item, "user", jnp.float32, sums)
+        total_item, sums = halve_sum(part_item, "user", jnp.float32, sums, jnp.bfloat16)
         sums = sums[0, : 2 * DRAWS]
         size, bits = bit_count("item")
         for bit in range(bits):

time: 126 us -> 115 us (0.913)
  waiting for transfers between devices: 44.1 us -> 31.6 us
  local copies, waits for them, and re-layouts: 13.1 us -> 18.2 us
  matrix products: 15.4 us -> 13.7 us
  other arithmetic: 17.2 us -> 15.6 us
    ppermute x30, waiting for transfers between devices: 44.1 us -> 31.6 us  [swap_with(): return lax.ppermute(value, axis, pairs)]
    dynamic_slice x8, local copies, waits for them, and re-layouts: 1.63 us -> 4.37 us  [block_of(): lax.dynamic_index_in_dim(out, value >> j & 1, left.index(group[j]), keepd...]
    convert_element_type x0 -> x4, local copies, waits for them, and re-layouts: none -> 2.35 us  [the longest x2 2.33 us: halve_sum(): send = block_of(digit ^ k).astype(stage_type)]
    unnamed x45 -> x41, local copies, waits for them, and re-layouts: 6.55 us -> 5.64 us
  transfers between devices with their start and end apart: 30 -> 30, of which waited for: 21 -> 21; matrix products, arithmetic and copies ran while one was open for 17% -> 21% of each run, Pallas kernels for 0% -> 0%
where the time goes in v9:
time: 115 us
  starting transfers between devices  33.4 us (29%)
  waiting for transfers between devices  31.6 us (27%)
  local copies, waits for them, and re-layouts  18.2 us (16%)
  other arithmetic  15.6 us (14%)
  matrix products  13.7 us (12%)
  between operations  2.03 us (2%)
    ppermute x30, starting transfers between devices, swap_with(): return lax.ppermute(value, axis, pairs)  33.4 us
    ppermute x30, waiting for transfers between devices, swap_with(): return lax.ppermute(value, axis, pairs)  31.6 us
    dot_general x2, matrix products, cross_parts(): jnp.dot(counts_bf, item_range, preferred_element_type=jnp.float32)  6.04 us
    unnamed x41, local copies, waits for them, and re-layouts  5.64 us
    dynamic_slice x8, local copies, waits for them, and re-layouts, block_of(): lax.dynamic_index_in_dim(out, value >> j & 1, left.index(group[j]), keepd...  4.37 us
    dot_general x2, matrix products, cross_parts(): lax.dot_general(counts_bf, user_range, (((0,), (0,)), ((), ())), preferre...  3.47 us
    another operation x4, local copies, waits for them, and re-layouts, double_gather(): buf = jnp.stack(ordered, axis=1).reshape((-1,) + piece.shape)  2.75 us
    dot_general x1, matrix products, per_device(): jnp.einsum('trc,tij->ricj', place, tiles_bf, preferred_element_type=jnp.b...  2.45 us
  transfers between devices with their start and end apart: 30, of which 21 were waited for; matrix products, arithmetic and copies ran while one was open for 21% of the time, Pallas kernels for 0%

profile of v9, /device:TPU:0, one launch (start us, length us, event | category | flops | bytes accessed | tf_op | source)
XLA Modules:
  0.0 114.5 jit_solution(2876971135220786223)
XLA Ops:
  0.7 0.9 multiply_reduce_fusion.6
  1.6 5.1 %collective-permute-start.1 = (bf16[1,64,256]{2,1,0:T(8,128)(2,1)S(1)}, bf16[1,64,256]{2,1,0:T(8,128)(2,1)S(1)}, u32[]{:S(2)}, u32[]{:S(2)}) collective-permute-start(bf16[1,64,256]{2,1,0:T(8,128)(2,1)S(1)} %get-tuple-element.62), channel_id=1, source_target_pairs={{0,24},{2,26},{4,28},{6,30},{8,16},{10,18},{12,20},{14,22},{16,8},... | collective-permute-start | bytes 98312 | tf_op jit(solution)/shard_map/ppermute | solution.py:45
  6.7 0.6 collective-permute-start.3
  7.4 1.2 %copy.49 = f32[1,384,256]{1,2,0:T(8,128)S(1)} copy(f32[1,384,256]{2,1,0:T(8,128)} %param.7) | data formatting | bytes 786432 | tf_op args[0]
  8.5 0.7 convert_element_type.174
  9.2 0.9 squeeze.83
  10.3 2.4 %convert_reduce_fusion.1 = (f32[12,256]{1,0:T(8,128)S(1)}, f32[12,256]{1,0:T(8,128)S(1)}, bf16[12,256,256]{2,1,0:T(8,128)(2,1)S(1)}) fusion(s32[1,1,12,256,256]{4,3,2,1,0:T(8,128)} %param.11), kind=kLoop, calls=%fused_computation.1 | loop fusion | flops 3139584 | bytes 4743168 | tf_op jit(solution)/shard_map/reduce_sum | solution.py:145
  14.0 2.5 %fusion = bf16[3,4,256,256]{3,1,2,0:T(4,128)(2,1)} fusion(bf16[12,256,256]{2,1,0:T(8,128)(2,1)S(1)} %get-tuple-element.24, pred[12,4]{0,1:T(4,128)(4,1)S(1)} %copy.47, pred[12,3]{0,1:T(4,128)(4,1)S(1)} %fusion.57), kind=kOutput, calls=%fused_computation.2 | convolution fusion | flops 18874512 | bytes 3145812 | tf_op jit(solution)/shard_map/trc,tij->ricj/dot_general | solution.py:141
  16.6 1.8 %copy.76 = bf16[96,8,4,256]{3,1,2,0:T(8,128)(2,1)S(1)} copy(bf16[96,8,4,256]{3,2,1,0:T(4,128)(2,1)} %bitcast.246) | data formatting | bytes 3145728
  19.3 2.7 %collective-permute-start.4 = (bf16[4,64,256]{2,1,0:T(8,128)(2,1)S(1)}, bf16[4,64,256]{2,1,0:T(8,128)(2,1)S(1)}, u32[]{:S(2)}, u32[]{:S(2)}) collective-permute-start(bf16[4,64,256]{2,1,0:T(8,128)(2,1)S(1)} %maximum_bitcast_fusion), channel_id=1, source_target_pairs={{0,6},{2,4},{4,2},{6,0},{8,14},{10,12},{12,10},{14,8},{16,22},{18,... | collective-permute-start | bytes 393224 | tf_op jit(solution)/shard_map/ppermute | solution.py:45
  22.8 0.6 multiply_reduce_fusion.1
  23.5 2.8 %collective-permute-done.4 = bf16[4,64,256]{2,1,0:T(8,128)(2,1)S(1)} collective-permute-done((bf16[4,64,256]{2,1,0:T(8,128)(2,1)S(1)}, bf16[4,64,256]{2,1,0:T(8,128)(2,1)S(1)}, u32[]{:S(2)}, u32[]{:S(2)}) %collective-permute-start.4) | collective-permute-done | bytes 131104 | tf_op jit(solution)/shard_map/ppermute | solution.py:45
  26.3 2.7 %collective-permute-done.5 = bf16[4,64,256]{2,1,0:T(8,128)(2,1)S(1)} collective-permute-done((bf16[4,64,256]{2,1,0:T(8,128)(2,1)S(1)}, bf16[4,64,256]{2,1,0:T(8,128)(2,1)S(1)}, u32[]{:S(2)}, u32[]{:S(2)}) %collective-permute-start.5) | collective-permute-done | bytes 131104 | tf_op jit(solution)/shard_map/ppermute | solution.py:45
  29.4 1.0 select_bitcast_fusion.3
  30.5 0.9 copy.50
  31.4 2.7 %fusion.5 = (f32[256]{0:T(256)S(1)}, f32[768,256]{1,0:T(8,128)}) fusion(bf16[1,2,384,256]{3,2,1,0:T(8,128)(2,1)} %copy.50, bf16[768,256]{1,0:T(8,128)(2,1)} %bitcast.274, f32[768]{0:T(1024)S(1)} %mul.192, bf16[768,1024]{1,0:T(8,128)(2,1)S(1)} %bitcast.248, bf16[1024,256]{1,0:T(8,128)(2,1)S(1)} %bitcast.256), kind=kOutput, calls=%fused_computation.20 | convolution fusion | flops 403832576 | bytes 3674112 | tf_op jit(solution)/shard_map/dot_general | solution.py:150
  34.3 1.7 %fusion.3 = (f32[256]{0:T(256)S(1)}, f32[1024,256]{1,0:T(8,128)}) fusion(bf16[4,4,64,256]{3,2,1,0:T(8,128)(2,1)S(1)} %copy.51, bf16[1024,256]{1,0:T(8,128)(2,1)S(1)} %bitcast.257, f32[1024]{0:T(1024)S(1)} %bitcast.281, bf16[768,1024]{1,0:T(8,128)(2,1)S(1)} %bitcast.249, bf16[768,256]{1,0:T(8,128)(2,1)S(1)} %bitcast.275), kind=kOutput, calls=%fused_computation.14 | convolution fusion | flops 404225792 | bytes 4068352 | tf_op jit(solution)/shard_map/dot_general | solution.py:152
  36.3 1.2 %dynamic-slice_convert_fusion.5 = (bf16[2,2,1,1,64,256]{5,4,3,2,1,0:T(8,128)(2,1)S(1)}, bf16[2,2,1,1,64,256]{5,4,3,2,1,0:T(8,128)(2,1)S(1)}, bf16[2,2,1,1,64,256]{5,4,3,2,1,0:T(8,128)(2,1)S(1)}) fusion(f32[2,2,2,2,64,256]{5,4,3,2,1,0:T(8,128)} %bitcast.272, s32[]{:T(128)S(6)} %select_n.385, s32[]{:T(128)S(6)} %select_n.387, s32[]{:T(128)S(6)} %select_n.393, ...), kind=kLoop, calls=%fused_computation.59 | loop fusion | bytes 786456 | tf_op jit(solution)/shard_map/convert_element_type | solution.py:90
  37.6 1.6 %collective-permute-start.9 = (bf16[280,256]{1,0:T(8,128)(2,1)S(1)}, bf16[280,256]{1,0:T(8,128)(2,1)S(1)}, u32[]{:S(2)}, u32[]{:S(2)}) collective-permute-start(bf16[280,256]{1,0:T(8,128)(2,1)S(1)} %get-tuple-element.68), channel_id=1, source_target_pairs={{0,6},{2,4},{4,2},{6,0},{8,14},{10,12},{12,10},{14,8},{16,22},{18,... | collective-permute-start | bytes 430088 | tf_op jit(solution)/shard_map/ppermute | solution.py:45
  39.2 1.4 %collective-permute-start.8 = (bf16[280,256]{1,0:T(8,128)(2,1)S(1)}, bf16[280,256]{1,0:T(8,128)(2,1)S(1)}, u32[]{:S(2)}, u32[]{:S(2)}) collective-permute-start(bf16[280,256]{1,0:T(8,128)(2,1)S(1)} %get-tuple-element.67), channel_id=1, source_target_pairs={{0,4},{2,6},{4,0},{6,2},{8,12},{10,14},{12,8},{14,10},{16,20},{18,... | collective-permute-start | bytes 430088 | tf_op jit(solution)/shard_map/ppermute | solution.py:45
  41.4 1.0 constant_dynamic-slice_fusion.5
  42.4 2.8 %collective-permute-done.9 = bf16[280,256]{1,0:T(8,128)(2,1)S(1)} collective-permute-done((bf16[280,256]{1,0:T(8,128)(2,1)S(1)}, bf16[280,256]{1,0:T(8,128)(2,1)S(1)}, u32[]{:S(2)}, u32[]{:S(2)}) %collective-permute-start.9) | collective-permute-done | bytes 143392 | tf_op jit(solution)/shard_map/ppermute | solution.py:45
  45.2 1.9 %collective-permute-done.8 = bf16[280,256]{1,0:T(8,128)(2,1)S(1)} collective-permute-done((bf16[280,256]{1,0:T(8,128)(2,1)S(1)}, bf16[280,256]{1,0:T(8,128)(2,1)S(1)}, u32[]{:S(2)}, u32[]{:S(2)}) %collective-permute-start.8) | collective-permute-done | bytes 143392 | tf_op jit(solution)/shard_map/ppermute | solution.py:45
  47.6 0.7 pad_maximum_fusion.24
  48.2 3.6 %collective-permute-start.12 = (f32[72,256]{1,0:T(8,128)}, f32[72,256]{1,0:T(8,128)S(1)}, u32[]{:S(2)}, u32[]{:S(2)}) collective-permute-start(f32[72,256]{1,0:T(8,128)} %get-tuple-element.74), channel_id=1, source_target_pairs={{0,24},{2,26},{4,28},{6,30},{8,16},{10,18},{12,20},{14,22},{16,8},... | collective-permute-start | bytes 221192 | tf_op jit(solution)/shard_map/ppermute | solution.py:45
  51.8 0.8 collective-permute-start.10
  52.8 2.6 %collective-permute-done.12 = f32[72,256]{1,0:T(8,128)S(1)} collective-permute-done((f32[72,256]{1,0:T(8,128)}, f32[72,256]{1,0:T(8,128)S(1)}, u32[]{:S(2)}, u32[]{:S(2)}) %collective-permute-start.12) | collective-permute-done | bytes 73760 | tf_op jit(solution)/shard_map/ppermute | solution.py:45
  55.5 2.8 %collective-permute-done.11 = f32[72,256]{1,0:T(8,128)S(1)} collective-permute-done((f32[72,256]{1,0:T(8,128)}, f32[72,256]{1,0:T(8,128)S(1)}, u32[]{:S(2)}, u32[]{:S(2)}) %collective-permute-start.11) | collective-permute-done | bytes 73760 | tf_op jit(solution)/shard_map/ppermute | solution.py:45
  58.3 1.1 collective-permute-done.13
  60.2 2.4 %collective-permute-start.16 = (bf16[1,64,256]{2,1,0:T(8,128)(2,1)S(1)}, bf16[1,64,256]{2,1,0:T(8,128)(2,1)S(1)}, u32[]{:S(2)}, u32[]{:S(2)}) collective-permute-start(bf16[1,64,256]{2,1,0:T(8,128)(2,1)S(1)} %get-tuple-element.22), channel_id=1, source_target_pairs={{0,24},{2,26},{4,28},{6,30},{8,16},{10,18},{12,20},{14,22},{16,8},... | collective-permute-start | bytes 98312 | tf_op jit(solution)/shard_map/ppermute | solution.py:45
  62.8 1.8 %collective-permute-start.18 = (bf16[1,64,256]{2,1,0:T(8,128)(2,1)S(1)}, bf16[1,64,256]{2,1,0:T(8,128)(2,1)S(1)}, u32[]{:S(2)}, u32[]{:S(2)}) collective-permute-start(bf16[1,64,256]{2,1,0:T(8,128)(2,1)S(1)} %get-tuple-element.22), channel_id=1, source_target_pairs={{0,8},{2,10},{4,12},{6,14},{8,0},{10,2},{12,4},{14,6},{16,24},{18,... | collective-permute-start | bytes 98312 | tf_op jit(solution)/shard_map/ppermute | solution.py:45
  66.0 1.5 %collective-permute-done.17 = bf16[1,64,256]{2,1,0:T(8,128)(2,1)S(1)} collective-permute-done((bf16[1,64,256]{2,1,0:T(8,128)(2,1)S(1)}, bf16[1,64,256]{2,1,0:T(8,128)(2,1)S(1)}, u32[]{:S(2)}, u32[]{:S(2)}) %collective-permute-start.17) | collective-permute-done | bytes 32800 | tf_op jit(solution)/shard_map/ppermute | solution.py:45
  67.5 0.7 maximum_bitcast_fusion.1
  68.1 1.4 %collective-permute-start.19 = (bf16[4,64,256]{2,1,0:T(8,128)(2,1)}, bf16[4,64,256]{2,1,0:T(8,128)(2,1)S(1)}, u32[]{:S(2)}, u32[]{:S(2)}) collective-permute-start(bf16[4,64,256]{2,1,0:T(8,128)(2,1)} %maximum_bitcast_fusion.1), channel_id=1, source_target_pairs={{0,6},{2,4},{4,2},{6,0},{8,14},{10,12},{12,10},{14,8},{16,22},{18,... | collective-permute-start | bytes 393224 | tf_op jit(solution)/shard_map/ppermute | solution.py:45
  69.5 1.4 %collective-permute-start.20 = (bf16[4,64,256]{2,1,0:T(8,128)(2,1)}, bf16[4,64,256]{2,1,0:T(8,128)(2,1)S(1)}, u32[]{:S(2)}, u32[]{:S(2)}) collective-permute-start(bf16[4,64,256]{2,1,0:T(8,128)(2,1)} %maximum_bitcast_fusion.1), channel_id=1, source_target_pairs={{0,4},{2,6},{4,0},{6,2},{8,12},{10,14},{12,8},{14,10},{16,20},{18,... | collective-permute-start | bytes 393224 | tf_op jit(solution)/shard_map/ppermute | solution.py:45
  71.0 0.6 collective-permute-start.21
  72.9 2.3 %collective-permute-done.19 = bf16[4,64,256]{2,1,0:T(8,128)(2,1)S(1)} collective-permute-done((bf16[4,64,256]{2,1,0:T(8,128)(2,1)}, bf16[4,64,256]{2,1,0:T(8,128)(2,1)S(1)}, u32[]{:S(2)}, u32[]{:S(2)}) %collective-permute-start.19) | collective-permute-done | bytes 131104 | tf_op jit(solution)/shard_map/ppermute | solution.py:45
  75.2 1.3 %collective-permute-done.20 = bf16[4,64,256]{2,1,0:T(8,128)(2,1)S(1)} collective-permute-done((bf16[4,64,256]{2,1,0:T(8,128)(2,1)}, bf16[4,64,256]{2,1,0:T(8,128)(2,1)S(1)}, u32[]{:S(2)}, u32[]{:S(2)}) %collective-permute-start.20) | collective-permute-done | bytes 131104 | tf_op jit(solution)/shard_map/ppermute | solution.py:45
  76.8 0.9 copy.61
  77.6 1.0 select_bitcast_fusion.1
  78.7 0.9 copy.59
  79.6 3.4 %fusion.6 = (f32[256]{0:T(256)S(1)}, f32[768,256]{1,0:T(8,128)}) fusion(bf16[1,2,384,256]{3,2,1,0:T(8,128)(2,1)} %copy.59, bf16[768,256]{1,0:T(8,128)(2,1)} %bitcast.276, f32[768]{0:T(1024)S(1)} %copy-done.13, bf16[768,1024]{1,0:T(8,128)(2,1)} %bitcast.250, bf16[1024,256]{1,0:T(8,128)(2,1)} %bitcast.258), kind=kOutput, calls=%fused_computation.21 | convolution fusion | flops 403832576 | bytes 3674112 | tf_op jit(solution)/shard_map/dot_general | solution.py:150
  83.0 1.7 %fusion.4 = (f32[256]{0:T(256)S(1)}, f32[1024,256]{1,0:T(8,128)}) fusion(bf16[4,4,64,256]{3,2,1,0:T(8,128)(2,1)S(1)} %copy-done.5, bf16[1024,256]{1,0:T(8,128)(2,1)S(1)} %bitcast.259, f32[1024]{0:T(1024)S(1)} %bitcast.282, bf16[768,1024]{1,0:T(8,128)(2,1)S(1)} %bitcast.251, bf16[768,256]{1,0:T(8,128)(2,1)S(1)} %bitcast.277), kind=kOutput, calls=%fused_computation.15 | convolution fusion | flops 404225792 | bytes 4068352 | tf_op jit(solution)/shard_map/dot_general | solution.py:152
  85.3 1.2 %dynamic-slice_convert_fusion.2 = (bf16[2,2,1,1,64,256]{5,4,3,2,1,0:T(8,128)(2,1)S(1)}, bf16[2,2,1,1,64,256]{5,4,3,2,1,0:T(8,128)(2,1)S(1)}, bf16[2,2,1,1,64,256]{5,4,3,2,1,0:T(8,128)(2,1)S(1)}) fusion(f32[2,2,2,2,64,256]{5,4,3,2,1,0:T(8,128)} %bitcast.270, s32[]{:T(128)S(6)} %select_n.385, s32[]{:T(128)S(6)} %select_n.387, s32[]{:T(128)S(6)} %select_n.393, ...), kind=kLoop, calls=%fused_computation.56 | loop fusion | bytes 786456 | tf_op jit(solution)/shard_map/convert_element_type | solution.py:90
  86.4 0.8 pad_maximum_fusion.15
  87.2 1.5 %collective-permute-start.24 = (bf16[280,256]{1,0:T(8,128)(2,1)}, bf16[280,256]{1,0:T(8,128)(2,1)S(1)}, u32[]{:S(2)}, u32[]{:S(2)}) collective-permute-start(bf16[280,256]{1,0:T(8,128)(2,1)} %get-tuple-element.65), channel_id=1, source_target_pairs={{0,6},{2,4},{4,2},{6,0},{8,14},{10,12},{12,10},{14,8},{16,22},{18,... | collective-permute-start | bytes 430088 | tf_op jit(solution)/shard_map/ppermute | solution.py:45
  88.7 1.4 %collective-permute-start.23 = (bf16[280,256]{1,0:T(8,128)(2,1)}, bf16[280,256]{1,0:T(8,128)(2,1)}, u32[]{:S(2)}, u32[]{:S(2)}) collective-permute-start(bf16[280,256]{1,0:T(8,128)(2,1)} %get-tuple-element.64), channel_id=1, source_target_pairs={{0,4},{2,6},{4,0},{6,2},{8,12},{10,14},{12,8},{14,10},{16,20},{18,... | collective-permute-start | bytes 430088 | tf_op jit(solution)/shard_map/ppermute | solution.py:45
  90.7 1.0 constant_dynamic-slice_fusion.1
  91.9 1.0 constant_dynamic-slice_fusion.2
  92.9 2.0 %collective-permute-done.24 = bf16[280,256]{1,0:T(8,128)(2,1)S(1)} collective-permute-done((bf16[280,256]{1,0:T(8,128)(2,1)}, bf16[280,256]{1,0:T(8,128)(2,1)S(1)}, u32[]{:S(2)}, u32[]{:S(2)}) %collective-permute-start.24) | collective-permute-done | bytes 143392 | tf_op jit(solution)/shard_map/ppermute | solution.py:45
  94.8 1.6 %collective-permute-done.23 = bf16[280,256]{1,0:T(8,128)(2,1)} collective-permute-done((bf16[280,256]{1,0:T(8,128)(2,1)}, bf16[280,256]{1,0:T(8,128)(2,1)}, u32[]{:S(2)}, u32[]{:S(2)}) %collective-permute-start.23) | collective-permute-done | bytes 143392 | tf_op jit(solution)/shard_map/ppermute | solution.py:45
  96.5 1.1 fusion.23
  97.8 0.7 pad_maximum_fusion.28
  98.4 3.4 %collective-permute-start.27 = (f32[72,256]{1,0:T(8,128)}, f32[72,256]{1,0:T(8,128)S(1)}, u32[]{:S(2)}, u32[]{:S(2)}) collective-permute-start(f32[72,256]{1,0:T(8,128)} %get-tuple-element.71), channel_id=1, source_target_pairs={{0,24},{2,26},{4,28},{6,30},{8,16},{10,18},{12,20},{14,22},{16,8},... | collective-permute-start | bytes 221192 | tf_op jit(solution)/shard_map/ppermute | solution.py:45
  101.8 1.0 collective-permute-start.25
  102.8 1.0 constant_dynamic-slice_fusion
  104.1 1.3 %collective-permute-done.27 = f32[72,256]{1,0:T(8,128)S(1)} collective-permute-done((f32[72,256]{1,0:T(8,128)}, f32[72,256]{1,0:T(8,128)S(1)}, u32[]{:S(2)}, u32[]{:S(2)}) %collective-permute-start.27) | collective-permute-done | bytes 73760 | tf_op jit(solution)/shard_map/ppermute | solution.py:45
  105.4 2.4 %collective-permute-done.26 = f32[72,256]{1,0:T(8,128)} collective-permute-done((f32[72,256]{1,0:T(8,128)}, f32[72,256]{1,0:T(8,128)}, u32[]{:S(2)}, u32[]{:S(2)}) %collective-permute-start.26) | collective-permute-done | bytes 73760 | tf_op jit(solution)/shard_map/ppermute | solution.py:45
  108.3 0.9 fusion.30
  109.3 1.1 collective-permute-done.28
  110.8 0.7 fusion.38
  111.5 1.2 %fusion.12 = (f32[1,384,256]{1,2,0:T(8,128)S(1)}, f32[1,384,256]{1,2,0:T(8,128)S(1)}) fusion(f32[384,256]{0,1:T(8,128)S(1)} %get-tuple-element.21, f32[1,384,256]{1,2,0:T(8,128)S(1)} %copy.65, f32[384,4,64]{0,2,1:T(8,128)S(1)} %fusion.46, bf16[384,256]{0,1:T(8,128)(2,1)} %collective-permute-done.29, f32[256]{0:T(256)S(1)} %mul.218, f32[256]{0:T(256)S(1)} %mul.216, ...), kind=kLoop, calls=%fused_computation.32 | loop fusion | flops 1671168 | bytes 3542016 | tf_op jit(solution)/shard_map/broadcast_in_dim | solution.py:212
  112.7 0.9 copy.67
  113.6 0.9 copy.68
  (156 shorter events, 11.4 us)
Async XLA Ops:
  0.6 22.2 %copy-start = (f32[64,64]{1,0:T(8,128)S(1)}, f32[64,64]{1,0:T(8,128)}, u32[]{:S(2)}) copy-start(f32[64,64]{1,0:T(8,128)} %param.9) | copy-start | bytes 49156
  0.6 9.5 %copy-start.3 = (f32[1,384,256]{2,1,0:T(8,128)S(1)}, f32[1,384,256]{2,1,0:T(8,128)}, u32[]{:S(2)}) copy-start(f32[1,384,256]{2,1,0:T(8,128)} %param.7) | copy-start | bytes 1179652
  1.6 17.6 %collective-permute-start.1 = (bf16[1,64,256]{2,1,0:T(8,128)(2,1)S(1)}, bf16[1,64,256]{2,1,0:T(8,128)(2,1)S(1)}, u32[]{:S(2)}, u32[]{:S(2)}) collective-permute-start(bf16[1,64,256]{2,1,0:T(8,128)(2,1)S(1)} %get-tuple-element.62), channel_id=1, source_target_pairs={{0,24},{2,26},{4,28},{6,30},{8,16},{10,18},{12,20},{14,22},{16,8},... | collective-permute-start | bytes 98312 | tf_op jit(solution)/shard_map/ppermute | solution.py:45
  6.7 12.5 %collective-permute-start.2 = (bf16[1,64,256]{2,1,0:T(8,128)(2,1)S(1)}, bf16[1,64,256]{2,1,0:T(8,128)(2,1)S(1)}, u32[]{:S(2)}, u32[]{:S(2)}) collective-permute-start(bf16[1,64,256]{2,1,0:T(8,128)(2,1)S(1)} %get-tuple-element.62), channel_id=1, source_target_pairs={{0,16},{2,18},{4,20},{6,22},{8,24},{10,26},{12,28},{14,30},{16,0},... | collective-permute-start | bytes 98312 | tf_op jit(solution)/shard_map/ppermute | solution.py:45
  6.7 12.5 %collective-permute-start.3 = (bf16[1,64,256]{2,1,0:T(8,128)(2,1)S(1)}, bf16[1,64,256]{2,1,0:T(8,128)(2,1)S(1)}, u32[]{:S(2)}, u32[]{:S(2)}) collective-permute-start(bf16[1,64,256]{2,1,0:T(8,128)(2,1)S(1)} %get-tuple-element.62), channel_id=1, source_target_pairs={{0,8},{2,10},{4,12},{6,14},{8,0},{10,2},{12,4},{14,6},{16,24},{18,... | collective-permute-start | bytes 98312 | tf_op jit(solution)/shard_map/ppermute | solution.py:45
  9.2 20.2 %collective-permute-start = (bf16[1,384,256]{1,2,0:T(8,128)(2,1)}, bf16[1,384,256]{1,2,0:T(8,128)(2,1)}, u32[]{:S(2)}, u32[]{:S(2)}) collective-permute-start(bf16[1,384,256]{1,2,0:T(8,128)(2,1)} %convert_element_type.174), channel_id=1, source_target_pairs={{0,1},{1,0},{2,3},{3,2},{4,5},{5,4},{6,7},{7,6},{8,9},{9,8},{10,11... | collective-permute-start | bytes 589832 | tf_op jit(solution)/shard_map/ppermute | solution.py:45
  10.3 2.4 %copy-start.16 = (s32[1,1,12,2]{2,3,1,0:T(2,128)S(1)}, s32[1,1,12,2]{2,3,1,0:T(2,128)}, u32[]{:S(2)}) copy-start(s32[1,1,12,2]{2,3,1,0:T(2,128)} %param.12) | copy-start | bytes 292
  10.3 3.4 %copy-start.9 = (f32[64,64]{1,0:T(8,128)S(1)}, f32[64,64]{1,0:T(8,128)}, u32[]{:S(2)}) copy-start(f32[64,64]{1,0:T(8,128)} %param.10) | copy-start | bytes 49156
  16.6 14.8 %copy-start.12 = (f32[768]{0:T(1024)}, f32[768]{0:T(1024)S(1)}, u32[]{:S(2)}) copy-start(f32[768]{0:T(1024)S(1)} %mul.192) | copy-start | bytes 9220
  18.4 15.9 %copy-start.1 = (bf16[96,8,4,256]{3,1,2,0:T(8,128)(2,1)}, bf16[96,8,4,256]{3,1,2,0:T(8,128)(2,1)S(1)}, u32[]{:S(2)}) copy-start(bf16[96,8,4,256]{3,1,2,0:T(8,128)(2,1)S(1)} %copy.76) | copy-start | bytes 4718596
  18.4 15.9 %copy-start.10 = (f32[1,2,4,128]{3,1,2,0:T(2,128)}, f32[1,2,4,128]{3,1,2,0:T(2,128)S(1)}, u32[]{:S(2)}) copy-start(f32[1,2,4,128]{3,1,2,0:T(2,128)S(1)} %copy.77) | copy-start | bytes 12292
  19.3 7.0 %collective-permute-start.4 = (bf16[4,64,256]{2,1,0:T(8,128)(2,1)S(1)}, bf16[4,64,256]{2,1,0:T(8,128)(2,1)S(1)}, u32[]{:S(2)}, u32[]{:S(2)}) collective-permute-start(bf16[4,64,256]{2,1,0:T(8,128)(2,1)S(1)} %maximum_bitcast_fusion), channel_id=1, source_target_pairs={{0,6},{2,4},{4,2},{6,0},{8,14},{10,12},{12,10},{14,8},{16,22},{18,... | collective-permute-start | bytes 393224 | tf_op jit(solution)/shard_map/ppermute | solution.py:45
  21.9 7.0 %collective-permute-start.5 = (bf16[4,64,256]{2,1,0:T(8,128)(2,1)S(1)}, bf16[4,64,256]{2,1,0:T(8,128)(2,1)S(1)}, u32[]{:S(2)}, u32[]{:S(2)}) collective-permute-start(bf16[4,64,256]{2,1,0:T(8,128)(2,1)S(1)} %maximum_bitcast_fusion), channel_id=1, source_target_pairs={{0,4},{2,6},{4,0},{6,2},{8,12},{10,14},{12,8},{14,10},{16,20},{18,... | collective-permute-start | bytes 393224 | tf_op jit(solution)/shard_map/ppermute | solution.py:45
  22.5 6.8 %collective-permute-start.6 = (bf16[4,64,256]{2,1,0:T(8,128)(2,1)S(1)}, bf16[4,64,256]{2,1,0:T(8,128)(2,1)S(1)}, u32[]{:S(2)}, u32[]{:S(2)}) collective-permute-start(bf16[4,64,256]{2,1,0:T(8,128)(2,1)S(1)} %maximum_bitcast_fusion), channel_id=1, source_target_pairs={{0,2},{2,0},{4,6},{6,4},{8,10},{10,8},{12,14},{14,12},{16,18},{18,... | collective-permute-start | bytes 393224 | tf_op jit(solution)/shard_map/ppermute | solution.py:45
  31.4 2.9 %copy-start.7 = (bf16[1,2,384,256]{3,2,1,0:T(8,128)(2,1)S(1)}, bf16[1,2,384,256]{3,2,1,0:T(8,128)(2,1)}, u32[]{:S(2)}) copy-start(bf16[1,2,384,256]{3,2,1,0:T(8,128)(2,1)} %copy.50) | copy-start | bytes 1179652
  36.0 5.1 %copy-start.6 = (f32[768,256]{1,0:T(8,128)S(1)}, f32[768,256]{1,0:T(8,128)}, u32[]{:S(2)}) copy-start(f32[768,256]{1,0:T(8,128)} %get-tuple-element.84) | copy-start | bytes 2359300
  37.6 7.6 %collective-permute-start.9 = (bf16[280,256]{1,0:T(8,128)(2,1)S(1)}, bf16[280,256]{1,0:T(8,128)(2,1)S(1)}, u32[]{:S(2)}, u32[]{:S(2)}) collective-permute-start(bf16[280,256]{1,0:T(8,128)(2,1)S(1)} %get-tuple-element.68), channel_id=1, source_target_pairs={{0,6},{2,4},{4,2},{6,0},{8,14},{10,12},{12,10},{14,8},{16,22},{18,... | collective-permute-start | bytes 430088 | tf_op jit(solution)/shard_map/ppermute | solution.py:45
  39.2 7.9 %collective-permute-start.8 = (bf16[280,256]{1,0:T(8,128)(2,1)S(1)}, bf16[280,256]{1,0:T(8,128)(2,1)S(1)}, u32[]{:S(2)}, u32[]{:S(2)}) collective-permute-start(bf16[280,256]{1,0:T(8,128)(2,1)S(1)} %get-tuple-element.67), channel_id=1, source_target_pairs={{0,4},{2,6},{4,0},{6,2},{8,12},{10,14},{12,8},{14,10},{16,20},{18,... | collective-permute-start | bytes 430088 | tf_op jit(solution)/shard_map/ppermute | solution.py:45
  40.6 6.7 %collective-permute-start.7 = (bf16[280,256]{1,0:T(8,128)(2,1)S(1)}, bf16[280,256]{1,0:T(8,128)(2,1)S(1)}, u32[]{:S(2)}, u32[]{:S(2)}) collective-permute-start(bf16[280,256]{1,0:T(8,128)(2,1)S(1)} %get-tuple-element.66), channel_id=1, source_target_pairs={{0,2},{2,0},{4,6},{6,4},{8,10},{10,8},{12,14},{14,12},{16,18},{18,... | collective-permute-start | bytes 430088 | tf_op jit(solution)/shard_map/ppermute | solution.py:45
  41.3 23.3 %collective-permute-start.14 = (bf16[384,256]{0,1:T(8,128)(2,1)S(1)}, bf16[384,256]{0,1:T(8,128)(2,1)S(1)}, u32[]{:S(2)}, u32[]{:S(2)}) collective-permute-start(bf16[384,256]{0,1:T(8,128)(2,1)S(1)} %bitcast.278), channel_id=1, source_target_pairs={{0,1},{1,0},{2,3},{3,2},{4,5},{5,4},{6,7},{7,6},{8,9},{9,8},{10,11... | collective-permute-start | bytes 589832 | tf_op jit(solution)/shard_map/ppermute | solution.py:45
  47.5 12.7 %copy-start.4 = (f32[1,64,256]{2,1,0:T(8,128)S(1)}, f32[1,64,256]{2,1,0:T(8,128)}, u32[]{:S(2)}) copy-start(f32[1,64,256]{2,1,0:T(8,128)} %param.8) | copy-start | bytes 196612
  48.2 7.2 %collective-permute-start.12 = (f32[72,256]{1,0:T(8,128)}, f32[72,256]{1,0:T(8,128)S(1)}, u32[]{:S(2)}, u32[]{:S(2)}) collective-permute-start(f32[72,256]{1,0:T(8,128)} %get-tuple-element.74), channel_id=1, source_target_pairs={{0,24},{2,26},{4,28},{6,30},{8,16},{10,18},{12,20},{14,22},{16,8},... | collective-permute-start | bytes 221192 | tf_op jit(solution)/shard_map/ppermute | solution.py:45
  51.8 6.4 %collective-permute-start.11 = (f32[72,256]{1,0:T(8,128)}, f32[72,256]{1,0:T(8,128)S(1)}, u32[]{:S(2)}, u32[]{:S(2)}) collective-permute-start(f32[72,256]{1,0:T(8,128)} %get-tuple-element.73), channel_id=1, source_target_pairs={{0,16},{2,18},{4,20},{6,22},{8,24},{10,26},{12,28},{14,30},{16,0},... | collective-permute-start | bytes 221192 | tf_op jit(solution)/shard_map/ppermute | solution.py:45
  51.8 6.4 %collective-permute-start.10 = (f32[72,256]{1,0:T(8,128)S(1)}, f32[72,256]{1,0:T(8,128)S(1)}, u32[]{:S(2)}, u32[]{:S(2)}) collective-permute-start(f32[72,256]{1,0:T(8,128)S(1)} %get-tuple-element.72), channel_id=1, source_target_pairs={{0,8},{2,10},{4,12},{6,14},{8,0},{10,2},{12,4},{14,6},{16,24},{18,... | collective-permute-start | bytes 221192 | tf_op jit(solution)/shard_map/ppermute | solution.py:45
  58.3 1.2 %collective-permute-start.13 = (f32[8]{0:T(128)S(1)}, f32[8]{0:T(128)S(1)}, u32[]{:S(2)}, u32[]{:S(2)}) collective-permute-start(f32[8]{0:T(128)S(1)} %slice_bitcast_fusion.1), channel_id=1, source_target_pairs={{0,1},{1,0},{2,3},{3,2},{4,5},{5,4},{6,7},{7,6},{8,9},{9,8},{10,11... | collective-permute-start | bytes 104 | tf_op jit(solution)/shard_map/ppermute | solution.py:45
  59.4 0.6 copy-start.14
  60.2 5.8 %collective-permute-start.16 = (bf16[1,64,256]{2,1,0:T(8,128)(2,1)S(1)}, bf16[1,64,256]{2,1,0:T(8,128)(2,1)S(1)}, u32[]{:S(2)}, u32[]{:S(2)}) collective-permute-start(bf16[1,64,256]{2,1,0:T(8,128)(2,1)S(1)} %get-tuple-element.22), channel_id=1, source_target_pairs={{0,24},{2,26},{4,28},{6,30},{8,16},{10,18},{12,20},{14,22},{16,8},... | collective-permute-start | bytes 98312 | tf_op jit(solution)/shard_map/ppermute | solution.py:45
  62.6 4.8 %collective-permute-start.17 = (bf16[1,64,256]{2,1,0:T(8,128)(2,1)S(1)}, bf16[1,64,256]{2,1,0:T(8,128)(2,1)S(1)}, u32[]{:S(2)}, u32[]{:S(2)}) collective-permute-start(bf16[1,64,256]{2,1,0:T(8,128)(2,1)S(1)} %get-tuple-element.22), channel_id=1, source_target_pairs={{0,16},{2,18},{4,20},{6,22},{8,24},{10,26},{12,28},{14,30},{16,0},... | collective-permute-start | bytes 98312 | tf_op jit(solution)/shard_map/ppermute | solution.py:45
  62.8 4.6 %collective-permute-start.18 = (bf16[1,64,256]{2,1,0:T(8,128)(2,1)S(1)}, bf16[1,64,256]{2,1,0:T(8,128)(2,1)S(1)}, u32[]{:S(2)}, u32[]{:S(2)}) collective-permute-start(bf16[1,64,256]{2,1,0:T(8,128)(2,1)S(1)} %get-tuple-element.22), channel_id=1, source_target_pairs={{0,8},{2,10},{4,12},{6,14},{8,0},{10,2},{12,4},{14,6},{16,24},{18,... | collective-permute-start | bytes 98312 | tf_op jit(solution)/shard_map/ppermute | solution.py:45
  64.8 12.9 %collective-permute-start.15 = (bf16[1,384,256]{1,2,0:T(8,128)(2,1)S(1)}, bf16[1,384,256]{1,2,0:T(8,128)(2,1)}, u32[]{:S(2)}, u32[]{:S(2)}) collective-permute-start(bf16[1,384,256]{1,2,0:T(8,128)(2,1)S(1)} %get-tuple-element.20), channel_id=1, source_target_pairs={{0,1},{1,0},{2,3},{3,2},{4,5},{5,4},{6,7},{7,6},{8,9},{9,8},{10,11... | collective-permute-start | bytes 589832 | tf_op jit(solution)/shard_map/ppermute | solution.py:45
  68.1 7.1 %collective-permute-start.19 = (bf16[4,64,256]{2,1,0:T(8,128)(2,1)}, bf16[4,64,256]{2,1,0:T(8,128)(2,1)S(1)}, u32[]{:S(2)}, u32[]{:S(2)}) collective-permute-start(bf16[4,64,256]{2,1,0:T(8,128)(2,1)} %maximum_bitcast_fusion.1), channel_id=1, source_target_pairs={{0,6},{2,4},{4,2},{6,0},{8,14},{10,12},{12,10},{14,8},{16,22},{18,... | collective-permute-start | bytes 393224 | tf_op jit(solution)/shard_map/ppermute | solution.py:45
  69.5 7.0 %collective-permute-start.20 = (bf16[4,64,256]{2,1,0:T(8,128)(2,1)}, bf16[4,64,256]{2,1,0:T(8,128)(2,1)S(1)}, u32[]{:S(2)}, u32[]{:S(2)}) collective-permute-start(bf16[4,64,256]{2,1,0:T(8,128)(2,1)} %maximum_bitcast_fusion.1), channel_id=1, source_target_pairs={{0,4},{2,6},{4,0},{6,2},{8,12},{10,14},{12,8},{14,10},{16,20},{18,... | collective-permute-start | bytes 393224 | tf_op jit(solution)/shard_map/ppermute | solution.py:45
  71.0 5.6 %collective-permute-start.21 = (bf16[4,64,256]{2,1,0:T(8,128)(2,1)}, bf16[4,64,256]{2,1,0:T(8,128)(2,1)S(1)}, u32[]{:S(2)}, u32[]{:S(2)}) collective-permute-start(bf16[4,64,256]{2,1,0:T(8,128)(2,1)} %maximum_bitcast_fusion.1), channel_id=1, source_target_pairs={{0,2},{2,0},{4,6},{6,4},{8,10},{10,8},{12,14},{14,12},{16,18},{18,... | collective-permute-start | bytes 393224 | tf_op jit(solution)/shard_map/ppermute | solution.py:45
  76.8 2.8 %copy-start.13 = (f32[768]{0:T(1024)S(1)}, f32[768]{0:T(1024)}, u32[]{:S(2)}) copy-start(f32[768]{0:T(1024)} %copy-done.12) | copy-start | bytes 9220
  79.6 3.4 %copy-start.2 = (bf16[96,8,4,256]{3,1,2,0:T(8,128)(2,1)S(1)}, bf16[96,8,4,256]{3,1,2,0:T(8,128)(2,1)}, u32[]{:S(2)}) copy-start(bf16[96,8,4,256]{3,1,2,0:T(8,128)(2,1)} %copy-done.1) | copy-start | bytes 4718596
  79.6 3.4 %copy-start.5 = (bf16[4,4,64,256]{3,2,1,0:T(8,128)(2,1)S(1)}, bf16[4,4,64,256]{3,2,1,0:T(8,128)(2,1)}, u32[]{:S(2)}) copy-start(bf16[4,4,64,256]{3,2,1,0:T(8,128)(2,1)} %copy.61) | copy-start | bytes 1572868
  79.6 3.4 %copy-start.8 = (bf16[1,2,384,256]{3,2,1,0:T(8,128)(2,1)S(1)}, bf16[1,2,384,256]{3,2,1,0:T(8,128)(2,1)}, u32[]{:S(2)}) copy-start(bf16[1,2,384,256]{3,2,1,0:T(8,128)(2,1)} %copy.59) | copy-start | bytes 1179652
  79.6 3.4 %copy-start.11 = (f32[1,2,4,128]{3,1,2,0:T(2,128)S(1)}, f32[1,2,4,128]{3,1,2,0:T(2,128)}, u32[]{:S(2)}) copy-start(f32[1,2,4,128]{3,1,2,0:T(2,128)} %copy-done.10) | copy-start | bytes 12292
  87.2 7.6 %collective-permute-start.24 = (bf16[280,256]{1,0:T(8,128)(2,1)}, bf16[280,256]{1,0:T(8,128)(2,1)S(1)}, u32[]{:S(2)}, u32[]{:S(2)}) collective-permute-start(bf16[280,256]{1,0:T(8,128)(2,1)} %get-tuple-element.65), channel_id=1, source_target_pairs={{0,6},{2,4},{4,2},{6,0},{8,14},{10,12},{12,10},{14,8},{16,22},{18,... | collective-permute-start | bytes 430088 | tf_op jit(solution)/shard_map/ppermute | solution.py:45
  88.7 7.8 %collective-permute-start.23 = (bf16[280,256]{1,0:T(8,128)(2,1)}, bf16[280,256]{1,0:T(8,128)(2,1)}, u32[]{:S(2)}, u32[]{:S(2)}) collective-permute-start(bf16[280,256]{1,0:T(8,128)(2,1)} %get-tuple-element.64), channel_id=1, source_target_pairs={{0,4},{2,6},{4,0},{6,2},{8,12},{10,14},{12,8},{14,10},{16,20},{18,... | collective-permute-start | bytes 430088 | tf_op jit(solution)/shard_map/ppermute | solution.py:45
  90.1 6.5 %collective-permute-start.22 = (bf16[280,256]{1,0:T(8,128)(2,1)}, bf16[280,256]{1,0:T(8,128)(2,1)}, u32[]{:S(2)}, u32[]{:S(2)}) collective-permute-start(bf16[280,256]{1,0:T(8,128)(2,1)} %get-tuple-element.63), channel_id=1, source_target_pairs={{0,2},{2,0},{4,6},{6,4},{8,10},{10,8},{12,14},{14,12},{16,18},{18,... | collective-permute-start | bytes 430088 | tf_op jit(solution)/shard_map/ppermute | solution.py:45
  97.7 12.7 %copy-start.15 = (f32[8]{0:T(128)S(1)}, f32[8]{0:T(128)}, u32[]{:S(2)}) copy-start(f32[8]{0:T(128)} %copy-done.14) | copy-start | bytes 100
  98.4 7.0 %collective-permute-start.27 = (f32[72,256]{1,0:T(8,128)}, f32[72,256]{1,0:T(8,128)S(1)}, u32[]{:S(2)}, u32[]{:S(2)}) collective-permute-start(f32[72,256]{1,0:T(8,128)} %get-tuple-element.71), channel_id=1, source_target_pairs={{0,24},{2,26},{4,28},{6,30},{8,16},{10,18},{12,20},{14,22},{16,8},... | collective-permute-start | bytes 221192 | tf_op jit(solution)/shard_map/ppermute | solution.py:45
  101.8 6.0 %collective-permute-start.26 = (f32[72,256]{1,0:T(8,128)}, f32[72,256]{1,0:T(8,128)}, u32[]{:S(2)}, u32[]{:S(2)}) collective-permute-start(f32[72,256]{1,0:T(8,128)} %get-tuple-element.70), channel_id=1, source_target_pairs={{0,16},{2,18},{4,20},{6,22},{8,24},{10,26},{12,28},{14,30},{16,0},... | collective-permute-start | bytes 221192 | tf_op jit(solution)/shard_map/ppermute | solution.py:45
  101.8 6.4 %collective-permute-start.25 = (f32[72,256]{1,0:T(8,128)}, f32[72,256]{1,0:T(8,128)}, u32[]{:S(2)}, u32[]{:S(2)}) collective-permute-start(f32[72,256]{1,0:T(8,128)} %get-tuple-element.69), channel_id=1, source_target_pairs={{0,8},{2,10},{4,12},{6,14},{8,0},{10,2},{12,4},{14,6},{16,24},{18,... | collective-permute-start | bytes 221192 | tf_op jit(solution)/shard_map/ppermute | solution.py:45
  104.0 7.5 %collective-permute-start.29 = (bf16[384,256]{0,1:T(8,128)(2,1)S(1)}, bf16[384,256]{0,1:T(8,128)(2,1)}, u32[]{:S(2)}, u32[]{:S(2)}) collective-permute-start(bf16[384,256]{0,1:T(8,128)(2,1)S(1)} %bitcast.279), channel_id=1, source_target_pairs={{0,1},{1,0},{2,3},{3,2},{4,5},{5,4},{6,7},{7,6},{8,9},{9,8},{10,11... | collective-permute-start | bytes 589832 | tf_op jit(solution)/shard_map/ppermute | solution.py:45
  109.2 1.2 %collective-permute-start.28 = (f32[8]{0:T(128)S(1)}, f32[8]{0:T(128)S(1)}, u32[]{:S(2)}, u32[]{:S(2)}) collective-permute-start(f32[8]{0:T(128)S(1)} %slice_bitcast_fusion), channel_id=1, source_target_pairs={{0,1},{1,0},{2,3},{3,2},{4,5},{5,4},{6,7},{7,6},{8,9},{9,8},{10,11... | collective-permute-start | bytes 104 | tf_op jit(solution)/shard_map/ppermute | solution.py:45

commit v10 on v9

--- a/solution.py
+++ b/solution.py
@@ -107,13 +107,14 @@
     return buf.reshape(rows, width), extra
 
 
-def double_gather(piece, axis):
+def double_gather(piece, axis, hold=None):
     size, bits = bit_count(axis)
     me = lax.axis_index(axis)
     order = list(range(bits))[::-1]
     groups = [order[:1]] if bits % 2 else []
     groups += [order[i : i + 2] for i in range(bits % 2, bits, 2)]
     buf = piece[None]
+    kept = None
     for group in groups:
         masks = [sum(1 << group[-1 - j] for j in range(len(group)) if (k >> j) & 1) for k in range(1 << len(group))]
         pieces = [buf] + [swap_with(buf, axis, size, None, mask) for mask in masks[1:]]
@@ -125,7 +126,10 @@
                 pick = jnp.where(digit == held, pieces[place ^ held], pick)
             ordered.append(pick)
         buf = jnp.stack(ordered, axis=1).reshape((-1,) + piece.shape)
-    return buf.reshape((size * piece.shape[0],) + piece.shape[1:])
+        if hold is not None and kept is None:
+            buf, kept = lax.optimization_barrier((buf, hold))
+    result = buf.reshape((size * piece.shape[0],) + piece.shape[1:])
+    return result if hold is None else (result, kept)
 
 def per_device(
     draws_user, draws_item, prior_user, prior_item, count_tiles, tile_blocks, tile_count
@@ -137,16 +141,20 @@
     row_pick = (tile_blocks[0, 0, :, 0][:, None] == jnp.arange(RB, dtype=jnp.int32)) & in_use[:, None]
     col_pick = (tile_blocks[0, 0, :, 1][:, None] == jnp.arange(CB, dtype=jnp.int32)) & in_use[:, None]
     place = (row_pick[:, :, None] & col_pick[:, None, :]).astype(jnp.bfloat16)
-    tiles_bf = count_tiles[0, 0].astype(jnp.bfloat16)
-    counts_bf = jnp.einsum(
-        "trc,tij->ricj", place, tiles_bf, preferred_element_type=jnp.bfloat16
-    ).reshape(RB * TILE, CB * TILE)
-    tile_rows = jnp.sum(tiles_bf, axis=2, dtype=jnp.float32)
-    tile_cols = jnp.sum(tiles_bf, axis=1, dtype=jnp.float32)
-    user_deg = jnp.sum(jnp.where(row_pick[:, :, None], tile_rows[:, None, :], 0.0), axis=0).reshape(-1)
-    item_deg = jnp.sum(jnp.where(col_pick[:, :, None], tile_cols[:, None, :], 0.0), axis=0).reshape(-1)
-
-    def cross_parts(user_range, item_range):
+
+    def build_counts(tiles):
+        tiles_bf = tiles.astype(jnp.bfloat16)
+        counts_bf = jnp.einsum(
+            "trc,tij->ricj", place, tiles_bf, preferred_element_type=jnp.bfloat16
+        ).reshape(RB * TILE, CB * TILE)
+        tile_rows = jnp.sum(tiles_bf, axis=2, dtype=jnp.float32)
+        tile_cols = jnp.sum(tiles_bf, axis=1, dtype=jnp.float32)
+        user_deg = jnp.sum(jnp.where(row_pick[:, :, None], tile_rows[:, None, :], 0.0), axis=0)
+        item_deg = jnp.sum(jnp.where(col_pick[:, :, None], tile_cols[:, None, :], 0.0), axis=0)
+        return (counts_bf, user_deg.reshape(-1), item_deg.reshape(-1))
+
+    def cross_parts(user_range, item_range, counts):
+        counts_bf, user_deg, item_deg = counts
         to_users = jnp.dot(counts_bf, item_range, preferred_element_type=jnp.float32)
         to_users = to_users + user_deg[:, None] * user_range.astype(jnp.float32)
         to_items = lax.dot_general(
@@ -158,13 +166,14 @@
     def user_range_of(user_vec):
         return double_gather(user_vec.astype(jnp.bfloat16), "item")
 
-    def item_range_of(item_vec):
-        return double_gather(item_vec.astype(jnp.bfloat16), "user")
-
-    def operate(user_vec, item_vec):
+    def operate(user_vec, item_vec, counts):
         user_range = user_range_of(user_vec)
-        item_range = item_range_of(item_vec)
-        part_user, part_item = cross_parts(user_range, item_range)
+        if counts is None:
+            item_range, tiles = double_gather(item_vec.astype(jnp.bfloat16), "user", count_tiles[0, 0])
+            counts = build_counts(tiles)
+        else:
+            item_range = double_gather(item_vec.astype(jnp.bfloat16), "user")
+        part_user, part_item = cross_parts(user_range, item_range, counts)
         prior_user_part = prior_term(user_vec, prior_user)
         prior_item_part = prior_term(item_vec, prior_item)
         norm_part = per_draw(user_vec, user_vec) + per_draw(item_vec, item_vec)
@@ -186,14 +195,14 @@
             sums = sums + swap_with(sums, "item", size, bit)
         image_user = prior_user_part + noise_prec * total_user
         image_item = prior_item_part + noise_prec * total_item
-        return (image_user, image_item, sums[:DRAWS], sums[DRAWS:])
+        return (image_user, image_item, sums[:DRAWS], sums[DRAWS:], counts)
 
     sol_user = jnp.zeros_like(user_own)
     sol_item = jnp.zeros_like(item_own)
     res_user, res_item = (user_own, item_own)
     dir_user, dir_item = (user_own, item_own)
 
-    along_user, along_item, norm_now, curve = operate(res_user, res_item)
+    along_user, along_item, norm_now, curve, counts = operate(res_user, res_item, None)
     step_len = norm_now / curve
     for iteration in range(ITERS):
         sol_user = sol_user + widen(step_len) * dir_user
@@ -201,7 +210,7 @@
         res_user = res_user - widen(step_len) * along_user
         res_item = res_item - widen(step_len) * along_item
         if iteration + 1 < ITERS:
-            image_user, image_item, norm_next, curve = operate(res_user, res_item)
+            image_user, image_item, norm_next, curve, _ = operate(res_user, res_item, counts)
             beta_coef = norm_next / norm_now
             step_len = norm_next / (curve - beta_coef * norm_next / step_len)
             dir_user = res_user + widen(beta_coef) * dir_user

time: 115 us -> 113 us (0.983)
  waiting for transfers between devices: 31.6 us -> 29.7 us
  other arithmetic: 15.6 us -> 17.1 us
    ppermute x30, waiting for transfers between devices: 31.6 us -> 29.7 us  [swap_with(): return lax.ppermute(value, axis, pairs)]
    unnamed x41 -> x43, local copies, waits for them, and re-layouts: 5.64 us -> 4.39 us
    another operation x12 -> x11, other arithmetic: 2.4 us -> 3.28 us  [double_gather(): buf = jnp.stack(ordered, axis=1).reshape((-1,) + piece.shape)]
  transfers between devices with their start and end apart: 30 -> 30, of which waited for: 21 -> 20; matrix products, arithmetic and copies ran while one was open for 21% -> 20% of each run, Pallas kernels for 0% -> 0%
where the time goes in v10:
time: 113 us; the launch traced here: 112 us
  starting transfers between devices  33.4 us (30%)
  waiting for transfers between devices  29.7 us (26%)
  local copies, waits for them, and re-layouts  17.5 us (15%)
  other arithmetic  17.1 us (15%)
  matrix products  12.7 us (11%)
  between operations  2.02 us (2%)
    ppermute x30, starting transfers between devices, swap_with(): return lax.ppermute(value, axis, pairs)  33.4 us
    ppermute x30, waiting for transfers between devices, swap_with(): return lax.ppermute(value, axis, pairs)  29.7 us
    dot_general x2, matrix products, cross_parts(): jnp.dot(counts_bf, item_range, preferred_element_type=jnp.float32)  6.04 us
    unnamed x43, local copies, waits for them, and re-layouts  4.39 us
    dynamic_slice x8, local copies, waits for them, and re-layouts, block_of(): lax.dynamic_index_in_dim(out, value >> j & 1, left.index(group[j]), keepd...  4.37 us
    dot_general x2, matrix products, cross_parts(): lax.dot_general(counts_bf, user_range, (((0,), (0,)), ((), ())), preferre...  3.66 us
    another operation x11, other arithmetic, double_gather(): buf = jnp.stack(ordered, axis=1).reshape((-1,) + piece.shape)  3.28 us
    another operation x4, local copies, waits for them, and re-layouts, double_gather(): buf = jnp.stack(ordered, axis=1).reshape((-1,) + piece.shape)  2.73 us
  transfers between devices with their start and end apart: 30, of which 20 were waited for; matrix products, arithmetic and copies ran while one was open for 20% of the time, Pallas kernels for 0%

profile of v10, /device:TPU:0, one launch (start us, length us, event | category | flops | bytes accessed | tf_op | source)
XLA Modules:
  0.0 112.5 jit_solution(9720446529379249811)
XLA Ops:
  0.7 0.9 multiply_reduce_fusion.6
  1.6 5.1 %collective-permute-start = (bf16[1,64,256]{2,1,0:T(8,128)(2,1)S(1)}, bf16[1,64,256]{2,1,0:T(8,128)(2,1)S(1)}, u32[]{:S(2)}, u32[]{:S(2)}) collective-permute-start(bf16[1,64,256]{2,1,0:T(8,128)(2,1)S(1)} %get-tuple-element.66), channel_id=1, source_target_pairs={{0,24},{2,26},{4,28},{6,30},{8,16},{10,18},{12,20},{14,22},{16,8},... | collective-permute-start | bytes 98312 | tf_op jit(solution)/shard_map/ppermute | solution.py:45
  6.7 0.6 collective-permute-start.2
  7.4 1.2 %copy.51 = f32[1,384,256]{1,2,0:T(8,128)S(1)} copy(f32[1,384,256]{2,1,0:T(8,128)} %param.7) | data formatting | bytes 786432 | tf_op args[0]
  8.5 0.7 convert_element_type.171
  9.2 0.9 squeeze.86
  11.0 0.6 multiply_reduce_fusion.1
  13.1 2.6 %convert_reduce_fusion.1 = (f32[12,256]{1,0:T(8,128)S(1)}, f32[12,256]{1,0:T(8,128)S(1)}) fusion(s32[12,256,256]{2,1,0:T(8,128)} %bitcast.234), kind=kLoop, calls=%fused_computation.1 | loop fusion | flops 3139584 | bytes 3170304 | tf_op jit(solution)/shard_map/reduce_sum | solution.py:151
  16.2 2.7 %collective-permute-start.4 = (bf16[4,64,256]{2,1,0:T(8,128)(2,1)S(1)}, bf16[4,64,256]{2,1,0:T(8,128)(2,1)S(1)}, u32[]{:S(2)}, u32[]{:S(2)}) collective-permute-start(bf16[4,64,256]{2,1,0:T(8,128)(2,1)S(1)} %maximum_bitcast_fusion), channel_id=1, source_target_pairs={{0,6},{2,4},{4,2},{6,0},{8,14},{10,12},{12,10},{14,8},{16,22},{18,... | collective-permute-start | bytes 393224 | tf_op jit(solution)/shard_map/ppermute | solution.py:45
  19.8 1.3 %fusion.2 = bf16[3,256,4,256]{3,2,0,1:T(4,128)(2,1)S(1)} fusion(bf16[12,256,256,1]{2,1,0,3:T(8,128)(2,1)S(1)} %convert_bitcast_fusion.4, pred[12,4]{0,1:T(4,128)(4,1)S(1)} %copy.48, pred[12,3]{0,1:T(4,128)(4,1)S(1)} %fusion.59), kind=kOutput, calls=%fused_computation.4 | convolution fusion | flops 18874512 | bytes 3145812 | tf_op jit(solution)/shard_map/trc,tij->ricj/dot_general | solution.py:147
  22.2 1.0 collective-permute-done.4
  23.3 2.7 %collective-permute-done.5 = bf16[4,64,256]{2,1,0:T(8,128)(2,1)S(1)} collective-permute-done((bf16[4,64,256]{2,1,0:T(8,128)(2,1)S(1)}, bf16[4,64,256]{2,1,0:T(8,128)(2,1)S(1)}, u32[]{:S(2)}, u32[]{:S(2)}) %collective-permute-start.5) | collective-permute-done | bytes 131104 | tf_op jit(solution)/shard_map/ppermute | solution.py:45
  26.3 1.0 select_bitcast_fusion.11
  27.4 1.0 select_bitcast_fusion.3
  28.4 0.9 copy.52
  29.3 2.7 %fusion.7 = (f32[256]{0:T(256)S(1)}, f32[768,256]{1,0:T(8,128)}) fusion(bf16[1,2,384,256]{3,2,1,0:T(8,128)(2,1)} %copy.52, bf16[768,256]{1,0:T(8,128)(2,1)} %bitcast.264, f32[768]{0:T(1024)S(1)} %mul.192, bf16[768,1024]{1,0:T(8,128)(2,1)S(1)} %bitcast.238, bf16[1024,256]{1,0:T(8,128)(2,1)S(1)} %bitcast.246), kind=kOutput, calls=%fused_computation.19 | convolution fusion | flops 403832576 | bytes 3674112 | tf_op jit(solution)/shard_map/dot_general | solution.py:158
  32.2 1.7 %fusion.5 = (f32[256]{0:T(256)S(1)}, f32[1024,256]{1,0:T(8,128)}) fusion(bf16[4,4,64,256]{3,2,1,0:T(8,128)(2,1)S(1)} %copy.53, bf16[1024,256]{1,0:T(8,128)(2,1)S(1)} %bitcast.247, f32[1024]{0:T(1024)S(1)} %bitcast.271, bf16[768,1024]{1,0:T(8,128)(2,1)S(1)} %bitcast.239, bf16[768,256]{1,0:T(8,128)(2,1)S(1)} %bitcast.265), kind=kOutput, calls=%fused_computation.13 | convolution fusion | flops 404225792 | bytes 4068352 | tf_op jit(solution)/shard_map/dot_general | solution.py:160
  34.3 1.2 %dynamic-slice_convert_fusion.5 = (bf16[2,2,1,1,64,256]{5,4,3,2,1,0:T(8,128)(2,1)S(1)}, bf16[2,2,1,1,64,256]{5,4,3,2,1,0:T(8,128)(2,1)S(1)}, bf16[2,2,1,1,64,256]{5,4,3,2,1,0:T(8,128)(2,1)S(1)}) fusion(f32[2,2,2,2,64,256]{5,4,3,2,1,0:T(8,128)} %bitcast.262, s32[]{:T(128)S(6)} %select_n.385, s32[]{:T(128)S(6)} %select_n.387, s32[]{:T(128)S(6)} %select_n.393, ...), kind=kLoop, calls=%fused_computation.58 | loop fusion | bytes 786456 | tf_op jit(solution)/shard_map/convert_element_type | solution.py:90
  35.5 1.5 %collective-permute-start.9 = (bf16[280,256]{1,0:T(8,128)(2,1)S(1)}, bf16[280,256]{1,0:T(8,128)(2,1)S(1)}, u32[]{:S(2)}, u32[]{:S(2)}) collective-permute-start(bf16[280,256]{1,0:T(8,128)(2,1)S(1)} %get-tuple-element.72), channel_id=1, source_target_pairs={{0,6},{2,4},{4,2},{6,0},{8,14},{10,12},{12,10},{14,8},{16,22},{18,... | collective-permute-start | bytes 430088 | tf_op jit(solution)/shard_map/ppermute | solution.py:45
  37.0 1.5 %collective-permute-start.8 = (bf16[280,256]{1,0:T(8,128)(2,1)S(1)}, bf16[280,256]{1,0:T(8,128)(2,1)S(1)}, u32[]{:S(2)}, u32[]{:S(2)}) collective-permute-start(bf16[280,256]{1,0:T(8,128)(2,1)S(1)} %get-tuple-element.71), channel_id=1, source_target_pairs={{0,4},{2,6},{4,0},{6,2},{8,12},{10,14},{12,8},{14,10},{16,20},{18,... | collective-permute-start | bytes 430088 | tf_op jit(solution)/shard_map/ppermute | solution.py:45
  39.3 1.0 constant_dynamic-slice_fusion.5
  40.3 2.8 %collective-permute-done.9 = bf16[280,256]{1,0:T(8,128)(2,1)S(1)} collective-permute-done((bf16[280,256]{1,0:T(8,128)(2,1)S(1)}, bf16[280,256]{1,0:T(8,128)(2,1)S(1)}, u32[]{:S(2)}, u32[]{:S(2)}) %collective-permute-start.9) | collective-permute-done | bytes 143392 | tf_op jit(solution)/shard_map/ppermute | solution.py:45
  43.1 1.9 %collective-permute-done.8 = bf16[280,256]{1,0:T(8,128)(2,1)S(1)} collective-permute-done((bf16[280,256]{1,0:T(8,128)(2,1)S(1)}, bf16[280,256]{1,0:T(8,128)(2,1)S(1)}, u32[]{:S(2)}, u32[]{:S(2)}) %collective-permute-start.8) | collective-permute-done | bytes 143392 | tf_op jit(solution)/shard_map/ppermute | solution.py:45
  45.4 0.7 pad_maximum_fusion.24
  46.0 3.6 %collective-permute-start.12 = (f32[72,256]{1,0:T(8,128)}, f32[72,256]{1,0:T(8,128)S(1)}, u32[]{:S(2)}, u32[]{:S(2)}) collective-permute-start(f32[72,256]{1,0:T(8,128)} %get-tuple-element.78), channel_id=1, source_target_pairs={{0,24},{2,26},{4,28},{6,30},{8,16},{10,18},{12,20},{14,22},{16,8},... | collective-permute-start | bytes 221192 | tf_op jit(solution)/shard_map/ppermute | solution.py:45
  49.7 0.8 collective-permute-start.10
  50.6 2.6 %collective-permute-done.12 = f32[72,256]{1,0:T(8,128)S(1)} collective-permute-done((f32[72,256]{1,0:T(8,128)}, f32[72,256]{1,0:T(8,128)S(1)}, u32[]{:S(2)}, u32[]{:S(2)}) %collective-permute-start.12) | collective-permute-done | bytes 73760 | tf_op jit(solution)/shard_map/ppermute | solution.py:45
  53.2 2.8 %collective-permute-done.11 = f32[72,256]{1,0:T(8,128)S(1)} collective-permute-done((f32[72,256]{1,0:T(8,128)}, f32[72,256]{1,0:T(8,128)S(1)}, u32[]{:S(2)}, u32[]{:S(2)}) %collective-permute-start.11) | collective-permute-done | bytes 73760 | tf_op jit(solution)/shard_map/ppermute | solution.py:45
  56.1 1.1 collective-permute-done.13
  58.0 2.4 %collective-permute-start.16 = (bf16[1,64,256]{2,1,0:T(8,128)(2,1)S(1)}, bf16[1,64,256]{2,1,0:T(8,128)(2,1)S(1)}, u32[]{:S(2)}, u32[]{:S(2)}) collective-permute-start(bf16[1,64,256]{2,1,0:T(8,128)(2,1)S(1)} %get-tuple-element.26), channel_id=1, source_target_pairs={{0,24},{2,26},{4,28},{6,30},{8,16},{10,18},{12,20},{14,22},{16,8},... | collective-permute-start | bytes 98312 | tf_op jit(solution)/shard_map/ppermute | solution.py:45
  60.7 1.7 %collective-permute-start.18 = (bf16[1,64,256]{2,1,0:T(8,128)(2,1)S(1)}, bf16[1,64,256]{2,1,0:T(8,128)(2,1)S(1)}, u32[]{:S(2)}, u32[]{:S(2)}) collective-permute-start(bf16[1,64,256]{2,1,0:T(8,128)(2,1)S(1)} %get-tuple-element.26), channel_id=1, source_target_pairs={{0,8},{2,10},{4,12},{6,14},{8,0},{10,2},{12,4},{14,6},{16,24},{18,... | collective-permute-start | bytes 98312 | tf_op jit(solution)/shard_map/ppermute | solution.py:45
  63.7 1.5 %collective-permute-done.17 = bf16[1,64,256]{2,1,0:T(8,128)(2,1)S(1)} collective-permute-done((bf16[1,64,256]{2,1,0:T(8,128)(2,1)S(1)}, bf16[1,64,256]{2,1,0:T(8,128)(2,1)S(1)}, u32[]{:S(2)}, u32[]{:S(2)}) %collective-permute-start.17) | collective-permute-done | bytes 32800 | tf_op jit(solution)/shard_map/ppermute | solution.py:45
  65.2 0.7 maximum_bitcast_fusion.1
  65.9 1.5 %collective-permute-start.19 = (bf16[4,64,256]{2,1,0:T(8,128)(2,1)}, bf16[4,64,256]{2,1,0:T(8,128)(2,1)S(1)}, u32[]{:S(2)}, u32[]{:S(2)}) collective-permute-start(bf16[4,64,256]{2,1,0:T(8,128)(2,1)} %maximum_bitcast_fusion.1), channel_id=1, source_target_pairs={{0,6},{2,4},{4,2},{6,0},{8,14},{10,12},{12,10},{14,8},{16,22},{18,... | collective-permute-start | bytes 393224 | tf_op jit(solution)/shard_map/ppermute | solution.py:45
  67.4 1.4 %collective-permute-start.20 = (bf16[4,64,256]{2,1,0:T(8,128)(2,1)}, bf16[4,64,256]{2,1,0:T(8,128)(2,1)S(1)}, u32[]{:S(2)}, u32[]{:S(2)}) collective-permute-start(bf16[4,64,256]{2,1,0:T(8,128)(2,1)} %maximum_bitcast_fusion.1), channel_id=1, source_target_pairs={{0,4},{2,6},{4,0},{6,2},{8,12},{10,14},{12,8},{14,10},{16,20},{18,... | collective-permute-start | bytes 393224 | tf_op jit(solution)/shard_map/ppermute | solution.py:45
  70.7 2.4 %collective-permute-done.19 = bf16[4,64,256]{2,1,0:T(8,128)(2,1)S(1)} collective-permute-done((bf16[4,64,256]{2,1,0:T(8,128)(2,1)}, bf16[4,64,256]{2,1,0:T(8,128)(2,1)S(1)}, u32[]{:S(2)}, u32[]{:S(2)}) %collective-permute-start.19) | collective-permute-done | bytes 131104 | tf_op jit(solution)/shard_map/ppermute | solution.py:45
  73.1 1.3 %collective-permute-done.20 = bf16[4,64,256]{2,1,0:T(8,128)(2,1)S(1)} collective-permute-done((bf16[4,64,256]{2,1,0:T(8,128)(2,1)}, bf16[4,64,256]{2,1,0:T(8,128)(2,1)S(1)}, u32[]{:S(2)}, u32[]{:S(2)}) %collective-permute-start.20) | collective-permute-done | bytes 131104 | tf_op jit(solution)/shard_map/ppermute | solution.py:45
  74.7 0.8 copy.63
  75.5 1.0 select_bitcast_fusion.1
  76.5 0.9 copy.61
  77.5 3.4 %fusion.8 = (f32[256]{0:T(256)S(1)}, f32[768,256]{1,0:T(8,128)}) fusion(bf16[1,2,384,256]{3,2,1,0:T(8,128)(2,1)} %copy.61, bf16[768,256]{1,0:T(8,128)(2,1)} %bitcast.266, f32[768]{0:T(1024)S(1)} %copy-done.12, bf16[768,1024]{1,0:T(8,128)(2,1)} %bitcast.240, bf16[1024,256]{1,0:T(8,128)(2,1)} %bitcast.248), kind=kOutput, calls=%fused_computation.20 | convolution fusion | flops 403832576 | bytes 3674112 | tf_op jit(solution)/shard_map/dot_general | solution.py:158
  80.9 1.9 %fusion.6 = (f32[256]{0:T(256)S(1)}, f32[1024,256]{1,0:T(8,128)}) fusion(bf16[4,4,64,256]{3,2,1,0:T(8,128)(2,1)S(1)} %copy-done.6, bf16[1024,256]{1,0:T(8,128)(2,1)S(1)} %bitcast.249, f32[1024]{0:T(1024)S(1)} %bitcast.272, bf16[768,1024]{1,0:T(8,128)(2,1)S(1)} %bitcast.241, bf16[768,256]{1,0:T(8,128)(2,1)S(1)} %bitcast.267), kind=kOutput, calls=%fused_computation.14 | convolution fusion | flops 404225792 | bytes 4068352 | tf_op jit(solution)/shard_map/dot_general | solution.py:160
  83.3 1.2 %dynamic-slice_convert_fusion.2 = (bf16[2,2,1,1,64,256]{5,4,3,2,1,0:T(8,128)(2,1)S(1)}, bf16[2,2,1,1,64,256]{5,4,3,2,1,0:T(8,128)(2,1)S(1)}, bf16[2,2,1,1,64,256]{5,4,3,2,1,0:T(8,128)(2,1)S(1)}) fusion(f32[2,2,2,2,64,256]{5,4,3,2,1,0:T(8,128)} %bitcast.260, s32[]{:T(128)S(6)} %select_n.385, s32[]{:T(128)S(6)} %select_n.387, s32[]{:T(128)S(6)} %select_n.393, ...), kind=kLoop, calls=%fused_computation.55 | loop fusion | bytes 786456 | tf_op jit(solution)/shard_map/convert_element_type | solution.py:90
  84.5 0.8 pad_maximum_fusion.15
  85.3 1.4 %collective-permute-start.24 = (bf16[280,256]{1,0:T(8,128)(2,1)}, bf16[280,256]{1,0:T(8,128)(2,1)S(1)}, u32[]{:S(2)}, u32[]{:S(2)}) collective-permute-start(bf16[280,256]{1,0:T(8,128)(2,1)} %get-tuple-element.69), channel_id=1, source_target_pairs={{0,6},{2,4},{4,2},{6,0},{8,14},{10,12},{12,10},{14,8},{16,22},{18,... | collective-permute-start | bytes 430088 | tf_op jit(solution)/shard_map/ppermute | solution.py:45
  86.7 1.5 %collective-permute-start.23 = (bf16[280,256]{1,0:T(8,128)(2,1)}, bf16[280,256]{1,0:T(8,128)(2,1)}, u32[]{:S(2)}, u32[]{:S(2)}) collective-permute-start(bf16[280,256]{1,0:T(8,128)(2,1)} %get-tuple-element.68), channel_id=1, source_target_pairs={{0,4},{2,6},{4,0},{6,2},{8,12},{10,14},{12,8},{14,10},{16,20},{18,... | collective-permute-start | bytes 430088 | tf_op jit(solution)/shard_map/ppermute | solution.py:45
  88.1 0.6 collective-permute-start.22
  88.8 1.0 constant_dynamic-slice_fusion.1
  89.9 1.0 constant_dynamic-slice_fusion.2
  90.9 1.9 %collective-permute-done.24 = bf16[280,256]{1,0:T(8,128)(2,1)S(1)} collective-permute-done((bf16[280,256]{1,0:T(8,128)(2,1)}, bf16[280,256]{1,0:T(8,128)(2,1)S(1)}, u32[]{:S(2)}, u32[]{:S(2)}) %collective-permute-start.24) | collective-permute-done | bytes 143392 | tf_op jit(solution)/shard_map/ppermute | solution.py:45
  92.9 1.6 %collective-permute-done.23 = bf16[280,256]{1,0:T(8,128)(2,1)} collective-permute-done((bf16[280,256]{1,0:T(8,128)(2,1)}, bf16[280,256]{1,0:T(8,128)(2,1)}, u32[]{:S(2)}, u32[]{:S(2)}) %collective-permute-start.23) | collective-permute-done | bytes 143392 | tf_op jit(solution)/shard_map/ppermute | solution.py:45
  94.5 1.1 fusion.25
  95.7 0.7 pad_maximum_fusion.28
  96.4 3.4 %collective-permute-start.27 = (f32[72,256]{1,0:T(8,128)}, f32[72,256]{1,0:T(8,128)S(1)}, u32[]{:S(2)}, u32[]{:S(2)}) collective-permute-start(f32[72,256]{1,0:T(8,128)} %get-tuple-element.75), channel_id=1, source_target_pairs={{0,24},{2,26},{4,28},{6,30},{8,16},{10,18},{12,20},{14,22},{16,8},... | collective-permute-start | bytes 221192 | tf_op jit(solution)/shard_map/ppermute | solution.py:45
  99.8 1.0 collective-permute-start.25
  100.8 1.0 constant_dynamic-slice_fusion
  102.0 1.3 %collective-permute-done.27 = f32[72,256]{1,0:T(8,128)S(1)} collective-permute-done((f32[72,256]{1,0:T(8,128)}, f32[72,256]{1,0:T(8,128)S(1)}, u32[]{:S(2)}, u32[]{:S(2)}) %collective-permute-start.27) | collective-permute-done | bytes 73760 | tf_op jit(solution)/shard_map/ppermute | solution.py:45
  103.3 2.4 %collective-permute-done.26 = f32[72,256]{1,0:T(8,128)} collective-permute-done((f32[72,256]{1,0:T(8,128)}, f32[72,256]{1,0:T(8,128)}, u32[]{:S(2)}, u32[]{:S(2)}) %collective-permute-start.26) | collective-permute-done | bytes 73760 | tf_op jit(solution)/shard_map/ppermute | solution.py:45
  106.2 0.9 fusion.32
  107.2 1.1 collective-permute-done.28
  108.7 0.7 fusion.40
  109.4 1.2 %fusion.14 = (f32[1,384,256]{1,2,0:T(8,128)S(1)}, f32[1,384,256]{1,2,0:T(8,128)S(1)}) fusion(f32[384,256]{0,1:T(8,128)S(1)} %get-tuple-element.25, f32[1,384,256]{1,2,0:T(8,128)S(1)} %copy.67, f32[384,4,64]{0,2,1:T(8,128)S(1)} %fusion.48, bf16[384,256]{0,1:T(8,128)(2,1)} %collective-permute-done.29, f32[256]{0:T(256)S(1)} %mul.218, f32[256]{0:T(256)S(1)} %mul.216, ...), kind=kLoop, calls=%fused_computation.31 | loop fusion | flops 1671168 | bytes 3542016 | tf_op jit(solution)/shard_map/broadcast_in_dim | solution.py:221
  110.6 0.9 copy.69
  111.6 0.9 copy.70
  (159 shorter events, 12.7 us)
Async XLA Ops:
  0.6 10.3 %copy-start = (f32[64,64]{1,0:T(8,128)S(1)}, f32[64,64]{1,0:T(8,128)}, u32[]{:S(2)}) copy-start(f32[64,64]{1,0:T(8,128)} %param.9) | copy-start | bytes 49156
  0.6 11.3 %copy-start.4 = (f32[1,384,256]{2,1,0:T(8,128)S(1)}, f32[1,384,256]{2,1,0:T(8,128)}, u32[]{:S(2)}) copy-start(f32[1,384,256]{2,1,0:T(8,128)} %param.7) | copy-start | bytes 1179652
  0.7 9.5 %copy-start.17 = (s32[1,1,12,2]{2,3,1,0:T(2,128)S(1)}, s32[1,1,12,2]{2,3,1,0:T(2,128)}, u32[]{:S(2)}) copy-start(s32[1,1,12,2]{2,3,1,0:T(2,128)} %param.12) | copy-start | bytes 292
  0.7 10.9 %copy-start.10 = (f32[64,64]{1,0:T(8,128)S(1)}, f32[64,64]{1,0:T(8,128)}, u32[]{:S(2)}) copy-start(f32[64,64]{1,0:T(8,128)} %param.10) | copy-start | bytes 49156
  1.6 11.4 %collective-permute-start = (bf16[1,64,256]{2,1,0:T(8,128)(2,1)S(1)}, bf16[1,64,256]{2,1,0:T(8,128)(2,1)S(1)}, u32[]{:S(2)}, u32[]{:S(2)}) collective-permute-start(bf16[1,64,256]{2,1,0:T(8,128)(2,1)S(1)} %get-tuple-element.66), channel_id=1, source_target_pairs={{0,24},{2,26},{4,28},{6,30},{8,16},{10,18},{12,20},{14,22},{16,8},... | collective-permute-start | bytes 98312 | tf_op jit(solution)/shard_map/ppermute | solution.py:45
  6.7 6.3 %collective-permute-start.1 = (bf16[1,64,256]{2,1,0:T(8,128)(2,1)S(1)}, bf16[1,64,256]{2,1,0:T(8,128)(2,1)S(1)}, u32[]{:S(2)}, u32[]{:S(2)}) collective-permute-start(bf16[1,64,256]{2,1,0:T(8,128)(2,1)S(1)} %get-tuple-element.66), channel_id=1, source_target_pairs={{0,16},{2,18},{4,20},{6,22},{8,24},{10,26},{12,28},{14,30},{16,0},... | collective-permute-start | bytes 98312 | tf_op jit(solution)/shard_map/ppermute | solution.py:45
  6.7 6.3 %collective-permute-start.2 = (bf16[1,64,256]{2,1,0:T(8,128)(2,1)S(1)}, bf16[1,64,256]{2,1,0:T(8,128)(2,1)S(1)}, u32[]{:S(2)}, u32[]{:S(2)}) collective-permute-start(bf16[1,64,256]{2,1,0:T(8,128)(2,1)S(1)} %get-tuple-element.66), channel_id=1, source_target_pairs={{0,8},{2,10},{4,12},{6,14},{8,0},{10,2},{12,4},{14,6},{16,24},{18,... | collective-permute-start | bytes 98312 | tf_op jit(solution)/shard_map/ppermute | solution.py:45
  9.2 18.1 %collective-permute-start.3 = (bf16[1,384,256]{1,2,0:T(8,128)(2,1)}, bf16[1,384,256]{1,2,0:T(8,128)(2,1)}, u32[]{:S(2)}, u32[]{:S(2)}) collective-permute-start(bf16[1,384,256]{1,2,0:T(8,128)(2,1)} %convert_element_type.171), channel_id=1, source_target_pairs={{0,1},{1,0},{2,3},{3,2},{4,5},{5,4},{6,7},{7,6},{8,9},{9,8},{10,11... | collective-permute-start | bytes 589832 | tf_op jit(solution)/shard_map/ppermute | solution.py:45
  13.1 2.8 %copy-start.1 = (s32[1,1,12,256,256]{4,3,2,1,0:T(8,128)S(1)}, s32[1,1,12,256,256]{4,3,2,1,0:T(8,128)}, u32[]{:S(2)}) copy-start(s32[1,1,12,256,256]{4,3,2,1,0:T(8,128)} %param.11) | copy-start | bytes 9437188
  16.2 7.0 %collective-permute-start.4 = (bf16[4,64,256]{2,1,0:T(8,128)(2,1)S(1)}, bf16[4,64,256]{2,1,0:T(8,128)(2,1)S(1)}, u32[]{:S(2)}, u32[]{:S(2)}) collective-permute-start(bf16[4,64,256]{2,1,0:T(8,128)(2,1)S(1)} %maximum_bitcast_fusion), channel_id=1, source_target_pairs={{0,6},{2,4},{4,2},{6,0},{8,14},{10,12},{12,10},{14,8},{16,22},{18,... | collective-permute-start | bytes 393224 | tf_op jit(solution)/shard_map/ppermute | solution.py:45
  18.9 7.0 %collective-permute-start.5 = (bf16[4,64,256]{2,1,0:T(8,128)(2,1)S(1)}, bf16[4,64,256]{2,1,0:T(8,128)(2,1)S(1)}, u32[]{:S(2)}, u32[]{:S(2)}) collective-permute-start(bf16[4,64,256]{2,1,0:T(8,128)(2,1)S(1)} %maximum_bitcast_fusion), channel_id=1, source_target_pairs={{0,4},{2,6},{4,0},{6,2},{8,12},{10,14},{12,8},{14,10},{16,20},{18,... | collective-permute-start | bytes 393224 | tf_op jit(solution)/shard_map/ppermute | solution.py:45
  19.4 6.9 %collective-permute-start.6 = (bf16[4,64,256]{2,1,0:T(8,128)(2,1)S(1)}, bf16[4,64,256]{2,1,0:T(8,128)(2,1)}, u32[]{:S(2)}, u32[]{:S(2)}) collective-permute-start(bf16[4,64,256]{2,1,0:T(8,128)(2,1)S(1)} %maximum_bitcast_fusion), channel_id=1, source_target_pairs={{0,2},{2,0},{4,6},{6,4},{8,10},{10,8},{12,14},{14,12},{16,18},{18,... | collective-permute-start | bytes 393224 | tf_op jit(solution)/shard_map/ppermute | solution.py:45
  21.2 8.1 %copy-start.11 = (f32[768]{0:T(1024)}, f32[768]{0:T(1024)S(1)}, u32[]{:S(2)}) copy-start(f32[768]{0:T(1024)S(1)} %mul.192) | copy-start | bytes 9220
  22.1 10.1 %copy-start.2 = (bf16[96,8,4,256]{3,1,2,0:T(8,128)(2,1)}, bf16[96,8,4,256]{3,1,2,0:T(8,128)(2,1)S(1)}, u32[]{:S(2)}) copy-start(bf16[96,8,4,256]{3,1,2,0:T(8,128)(2,1)S(1)} %copy.80) | copy-start | bytes 4718596
  22.2 10.0 %copy-start.13 = (f32[1,2,4,128]{3,1,2,0:T(2,128)}, f32[1,2,4,128]{3,1,2,0:T(2,128)S(1)}, u32[]{:S(2)}) copy-start(f32[1,2,4,128]{3,1,2,0:T(2,128)S(1)} %copy.81) | copy-start | bytes 12292
  29.3 2.9 %copy-start.8 = (bf16[1,2,384,256]{3,2,1,0:T(8,128)(2,1)S(1)}, bf16[1,2,384,256]{3,2,1,0:T(8,128)(2,1)}, u32[]{:S(2)}) copy-start(bf16[1,2,384,256]{3,2,1,0:T(8,128)(2,1)} %copy.52) | copy-start | bytes 1179652
  33.9 5.1 %copy-start.7 = (f32[768,256]{1,0:T(8,128)S(1)}, f32[768,256]{1,0:T(8,128)}, u32[]{:S(2)}) copy-start(f32[768,256]{1,0:T(8,128)} %get-tuple-element.88) | copy-start | bytes 2359300
  35.5 7.6 %collective-permute-start.9 = (bf16[280,256]{1,0:T(8,128)(2,1)S(1)}, bf16[280,256]{1,0:T(8,128)(2,1)S(1)}, u32[]{:S(2)}, u32[]{:S(2)}) collective-permute-start(bf16[280,256]{1,0:T(8,128)(2,1)S(1)} %get-tuple-element.72), channel_id=1, source_target_pairs={{0,6},{2,4},{4,2},{6,0},{8,14},{10,12},{12,10},{14,8},{16,22},{18,... | collective-permute-start | bytes 430088 | tf_op jit(solution)/shard_map/ppermute | solution.py:45
  37.0 8.0 %collective-permute-start.8 = (bf16[280,256]{1,0:T(8,128)(2,1)S(1)}, bf16[280,256]{1,0:T(8,128)(2,1)S(1)}, u32[]{:S(2)}, u32[]{:S(2)}) collective-permute-start(bf16[280,256]{1,0:T(8,128)(2,1)S(1)} %get-tuple-element.71), channel_id=1, source_target_pairs={{0,4},{2,6},{4,0},{6,2},{8,12},{10,14},{12,8},{14,10},{16,20},{18,... | collective-permute-start | bytes 430088 | tf_op jit(solution)/shard_map/ppermute | solution.py:45
  38.5 6.6 %collective-permute-start.7 = (bf16[280,256]{1,0:T(8,128)(2,1)S(1)}, bf16[280,256]{1,0:T(8,128)(2,1)S(1)}, u32[]{:S(2)}, u32[]{:S(2)}) collective-permute-start(bf16[280,256]{1,0:T(8,128)(2,1)S(1)} %get-tuple-element.70), channel_id=1, source_target_pairs={{0,2},{2,0},{4,6},{6,4},{8,10},{10,8},{12,14},{14,12},{16,18},{18,... | collective-permute-start | bytes 430088 | tf_op jit(solution)/shard_map/ppermute | solution.py:45
  39.2 23.2 %collective-permute-start.14 = (bf16[384,256]{0,1:T(8,128)(2,1)S(1)}, bf16[384,256]{0,1:T(8,128)(2,1)S(1)}, u32[]{:S(2)}, u32[]{:S(2)}) collective-permute-start(bf16[384,256]{0,1:T(8,128)(2,1)S(1)} %bitcast.268), channel_id=1, source_target_pairs={{0,1},{1,0},{2,3},{3,2},{4,5},{5,4},{6,7},{7,6},{8,9},{9,8},{10,11... | collective-permute-start | bytes 589832 | tf_op jit(solution)/shard_map/ppermute | solution.py:45
  45.3 12.6 %copy-start.5 = (f32[1,64,256]{2,1,0:T(8,128)S(1)}, f32[1,64,256]{2,1,0:T(8,128)}, u32[]{:S(2)}) copy-start(f32[1,64,256]{2,1,0:T(8,128)} %param.8) | copy-start | bytes 196612
  46.0 7.2 %collective-permute-start.12 = (f32[72,256]{1,0:T(8,128)}, f32[72,256]{1,0:T(8,128)S(1)}, u32[]{:S(2)}, u32[]{:S(2)}) collective-permute-start(f32[72,256]{1,0:T(8,128)} %get-tuple-element.78), channel_id=1, source_target_pairs={{0,24},{2,26},{4,28},{6,30},{8,16},{10,18},{12,20},{14,22},{16,8},... | collective-permute-start | bytes 221192 | tf_op jit(solution)/shard_map/ppermute | solution.py:45
  49.7 6.4 %collective-permute-start.11 = (f32[72,256]{1,0:T(8,128)}, f32[72,256]{1,0:T(8,128)S(1)}, u32[]{:S(2)}, u32[]{:S(2)}) collective-permute-start(f32[72,256]{1,0:T(8,128)} %get-tuple-element.77), channel_id=1, source_target_pairs={{0,16},{2,18},{4,20},{6,22},{8,24},{10,26},{12,28},{14,30},{16,0},... | collective-permute-start | bytes 221192 | tf_op jit(solution)/shard_map/ppermute | solution.py:45
  49.7 6.4 %collective-permute-start.10 = (f32[72,256]{1,0:T(8,128)S(1)}, f32[72,256]{1,0:T(8,128)S(1)}, u32[]{:S(2)}, u32[]{:S(2)}) collective-permute-start(f32[72,256]{1,0:T(8,128)S(1)} %get-tuple-element.76), channel_id=1, source_target_pairs={{0,8},{2,10},{4,12},{6,14},{8,0},{10,2},{12,4},{14,6},{16,24},{18,... | collective-permute-start | bytes 221192 | tf_op jit(solution)/shard_map/ppermute | solution.py:45
  56.1 1.2 %collective-permute-start.13 = (f32[8]{0:T(128)S(1)}, f32[8]{0:T(128)S(1)}, u32[]{:S(2)}, u32[]{:S(2)}) collective-permute-start(f32[8]{0:T(128)S(1)} %slice_bitcast_fusion.1), channel_id=1, source_target_pairs={{0,1},{1,0},{2,3},{3,2},{4,5},{5,4},{6,7},{7,6},{8,9},{9,8},{10,11... | collective-permute-start | bytes 104 | tf_op jit(solution)/shard_map/ppermute | solution.py:45
  57.3 0.5 copy-start.15
  58.0 5.8 %collective-permute-start.16 = (bf16[1,64,256]{2,1,0:T(8,128)(2,1)S(1)}, bf16[1,64,256]{2,1,0:T(8,128)(2,1)S(1)}, u32[]{:S(2)}, u32[]{:S(2)}) collective-permute-start(bf16[1,64,256]{2,1,0:T(8,128)(2,1)S(1)} %get-tuple-element.26), channel_id=1, source_target_pairs={{0,24},{2,26},{4,28},{6,30},{8,16},{10,18},{12,20},{14,22},{16,8},... | collective-permute-start | bytes 98312 | tf_op jit(solution)/shard_map/ppermute | solution.py:45
  60.4 4.8 %collective-permute-start.17 = (bf16[1,64,256]{2,1,0:T(8,128)(2,1)S(1)}, bf16[1,64,256]{2,1,0:T(8,128)(2,1)S(1)}, u32[]{:S(2)}, u32[]{:S(2)}) collective-permute-start(bf16[1,64,256]{2,1,0:T(8,128)(2,1)S(1)} %get-tuple-element.26), channel_id=1, source_target_pairs={{0,16},{2,18},{4,20},{6,22},{8,24},{10,26},{12,28},{14,30},{16,0},... | collective-permute-start | bytes 98312 | tf_op jit(solution)/shard_map/ppermute | solution.py:45
  60.7 4.5 %collective-permute-start.18 = (bf16[1,64,256]{2,1,0:T(8,128)(2,1)S(1)}, bf16[1,64,256]{2,1,0:T(8,128)(2,1)S(1)}, u32[]{:S(2)}, u32[]{:S(2)}) collective-permute-start(bf16[1,64,256]{2,1,0:T(8,128)(2,1)S(1)} %get-tuple-element.26), channel_id=1, source_target_pairs={{0,8},{2,10},{4,12},{6,14},{8,0},{10,2},{12,4},{14,6},{16,24},{18,... | collective-permute-start | bytes 98312 | tf_op jit(solution)/shard_map/ppermute | solution.py:45
  62.5 13.0 %collective-permute-start.15 = (bf16[1,384,256]{1,2,0:T(8,128)(2,1)S(1)}, bf16[1,384,256]{1,2,0:T(8,128)(2,1)}, u32[]{:S(2)}, u32[]{:S(2)}) collective-permute-start(bf16[1,384,256]{1,2,0:T(8,128)(2,1)S(1)} %get-tuple-element.24), channel_id=1, source_target_pairs={{0,1},{1,0},{2,3},{3,2},{4,5},{5,4},{6,7},{7,6},{8,9},{9,8},{10,11... | collective-permute-start | bytes 589832 | tf_op jit(solution)/shard_map/ppermute | solution.py:45
  65.9 7.1 %collective-permute-start.19 = (bf16[4,64,256]{2,1,0:T(8,128)(2,1)}, bf16[4,64,256]{2,1,0:T(8,128)(2,1)S(1)}, u32[]{:S(2)}, u32[]{:S(2)}) collective-permute-start(bf16[4,64,256]{2,1,0:T(8,128)(2,1)} %maximum_bitcast_fusion.1), channel_id=1, source_target_pairs={{0,6},{2,4},{4,2},{6,0},{8,14},{10,12},{12,10},{14,8},{16,22},{18,... | collective-permute-start | bytes 393224 | tf_op jit(solution)/shard_map/ppermute | solution.py:45
  67.4 6.9 %collective-permute-start.20 = (bf16[4,64,256]{2,1,0:T(8,128)(2,1)}, bf16[4,64,256]{2,1,0:T(8,128)(2,1)S(1)}, u32[]{:S(2)}, u32[]{:S(2)}) collective-permute-start(bf16[4,64,256]{2,1,0:T(8,128)(2,1)} %maximum_bitcast_fusion.1), channel_id=1, source_target_pairs={{0,4},{2,6},{4,0},{6,2},{8,12},{10,14},{12,8},{14,10},{16,20},{18,... | collective-permute-start | bytes 393224 | tf_op jit(solution)/shard_map/ppermute | solution.py:45
  68.9 5.6 %collective-permute-start.21 = (bf16[4,64,256]{2,1,0:T(8,128)(2,1)}, bf16[4,64,256]{2,1,0:T(8,128)(2,1)S(1)}, u32[]{:S(2)}, u32[]{:S(2)}) collective-permute-start(bf16[4,64,256]{2,1,0:T(8,128)(2,1)} %maximum_bitcast_fusion.1), channel_id=1, source_target_pairs={{0,2},{2,0},{4,6},{6,4},{8,10},{10,8},{12,14},{14,12},{16,18},{18,... | collective-permute-start | bytes 393224 | tf_op jit(solution)/shard_map/ppermute | solution.py:45
  74.7 2.8 %copy-start.12 = (f32[768]{0:T(1024)S(1)}, f32[768]{0:T(1024)}, u32[]{:S(2)}) copy-start(f32[768]{0:T(1024)} %copy-done.11) | copy-start | bytes 9220
  77.5 3.4 %copy-start.3 = (bf16[96,8,4,256]{3,1,2,0:T(8,128)(2,1)S(1)}, bf16[96,8,4,256]{3,1,2,0:T(8,128)(2,1)}, u32[]{:S(2)}) copy-start(bf16[96,8,4,256]{3,1,2,0:T(8,128)(2,1)} %copy-done.2) | copy-start | bytes 4718596
  77.5 3.4 %copy-start.6 = (bf16[4,4,64,256]{3,2,1,0:T(8,128)(2,1)S(1)}, bf16[4,4,64,256]{3,2,1,0:T(8,128)(2,1)}, u32[]{:S(2)}) copy-start(bf16[4,4,64,256]{3,2,1,0:T(8,128)(2,1)} %copy.63) | copy-start | bytes 1572868
  77.5 3.4 %copy-start.9 = (bf16[1,2,384,256]{3,2,1,0:T(8,128)(2,1)S(1)}, bf16[1,2,384,256]{3,2,1,0:T(8,128)(2,1)}, u32[]{:S(2)}) copy-start(bf16[1,2,384,256]{3,2,1,0:T(8,128)(2,1)} %copy.61) | copy-start | bytes 1179652
  77.5 3.4 %copy-start.14 = (f32[1,2,4,128]{3,1,2,0:T(2,128)S(1)}, f32[1,2,4,128]{3,1,2,0:T(2,128)}, u32[]{:S(2)}) copy-start(f32[1,2,4,128]{3,1,2,0:T(2,128)} %copy-done.13) | copy-start | bytes 12292
  85.3 7.6 %collective-permute-start.24 = (bf16[280,256]{1,0:T(8,128)(2,1)}, bf16[280,256]{1,0:T(8,128)(2,1)S(1)}, u32[]{:S(2)}, u32[]{:S(2)}) collective-permute-start(bf16[280,256]{1,0:T(8,128)(2,1)} %get-tuple-element.69), channel_id=1, source_target_pairs={{0,6},{2,4},{4,2},{6,0},{8,14},{10,12},{12,10},{14,8},{16,22},{18,... | collective-permute-start | bytes 430088 | tf_op jit(solution)/shard_map/ppermute | solution.py:45
  86.7 7.8 %collective-permute-start.23 = (bf16[280,256]{1,0:T(8,128)(2,1)}, bf16[280,256]{1,0:T(8,128)(2,1)}, u32[]{:S(2)}, u32[]{:S(2)}) collective-permute-start(bf16[280,256]{1,0:T(8,128)(2,1)} %get-tuple-element.68), channel_id=1, source_target_pairs={{0,4},{2,6},{4,0},{6,2},{8,12},{10,14},{12,8},{14,10},{16,20},{18,... | collective-permute-start | bytes 430088 | tf_op jit(solution)/shard_map/ppermute | solution.py:45
  88.1 6.4 %collective-permute-start.22 = (bf16[280,256]{1,0:T(8,128)(2,1)}, bf16[280,256]{1,0:T(8,128)(2,1)}, u32[]{:S(2)}, u32[]{:S(2)}) collective-permute-start(bf16[280,256]{1,0:T(8,128)(2,1)} %get-tuple-element.67), channel_id=1, source_target_pairs={{0,2},{2,0},{4,6},{6,4},{8,10},{10,8},{12,14},{14,12},{16,18},{18,... | collective-permute-start | bytes 430088 | tf_op jit(solution)/shard_map/ppermute | solution.py:45
  95.6 12.7 %copy-start.16 = (f32[8]{0:T(128)S(1)}, f32[8]{0:T(128)}, u32[]{:S(2)}) copy-start(f32[8]{0:T(128)} %copy-done.15) | copy-start | bytes 100
  96.4 7.0 %collective-permute-start.27 = (f32[72,256]{1,0:T(8,128)}, f32[72,256]{1,0:T(8,128)S(1)}, u32[]{:S(2)}, u32[]{:S(2)}) collective-permute-start(f32[72,256]{1,0:T(8,128)} %get-tuple-element.75), channel_id=1, source_target_pairs={{0,24},{2,26},{4,28},{6,30},{8,16},{10,18},{12,20},{14,22},{16,8},... | collective-permute-start | bytes 221192 | tf_op jit(solution)/shard_map/ppermute | solution.py:45
  99.8 6.0 %collective-permute-start.26 = (f32[72,256]{1,0:T(8,128)}, f32[72,256]{1,0:T(8,128)}, u32[]{:S(2)}, u32[]{:S(2)}) collective-permute-start(f32[72,256]{1,0:T(8,128)} %get-tuple-element.74), channel_id=1, source_target_pairs={{0,16},{2,18},{4,20},{6,22},{8,24},{10,26},{12,28},{14,30},{16,0},... | collective-permute-start | bytes 221192 | tf_op jit(solution)/shard_map/ppermute | solution.py:45
  99.8 6.4 %collective-permute-start.25 = (f32[72,256]{1,0:T(8,128)}, f32[72,256]{1,0:T(8,128)}, u32[]{:S(2)}, u32[]{:S(2)}) collective-permute-start(f32[72,256]{1,0:T(8,128)} %get-tuple-element.73), channel_id=1, source_target_pairs={{0,8},{2,10},{4,12},{6,14},{8,0},{10,2},{12,4},{14,6},{16,24},{18,... | collective-permute-start | bytes 221192 | tf_op jit(solution)/shard_map/ppermute | solution.py:45
  102.0 7.5 %collective-permute-start.29 = (bf16[384,256]{0,1:T(8,128)(2,1)S(1)}, bf16[384,256]{0,1:T(8,128)(2,1)}, u32[]{:S(2)}, u32[]{:S(2)}) collective-permute-start(bf16[384,256]{0,1:T(8,128)(2,1)S(1)} %bitcast.269), channel_id=1, source_target_pairs={{0,1},{1,0},{2,3},{3,2},{4,5},{5,4},{6,7},{7,6},{8,9},{9,8},{10,11... | collective-permute-start | bytes 589832 | tf_op jit(solution)/shard_map/ppermute | solution.py:45
  107.2 1.2 %collective-permute-start.28 = (f32[8]{0:T(128)S(1)}, f32[8]{0:T(128)S(1)}, u32[]{:S(2)}, u32[]{:S(2)}) collective-permute-start(f32[8]{0:T(128)S(1)} %slice_bitcast_fusion), channel_id=1, source_target_pairs={{0,1},{1,0},{2,3},{3,2},{4,5},{5,4},{6,7},{7,6},{8,9},{9,8},{10,11... | collective-permute-start | bytes 104 | tf_op jit(solution)/shard_map/ppermute | solution.py:45

commit v11 on v10

--- a/solution.py
+++ b/solution.py
@@ -64,30 +64,28 @@
 
 def halve_sum(part, axis, send_type, extra=None, first_type=None):
     size, bits = bit_count(axis)
-    me = lax.axis_index(axis)
     rows, width = part.shape[0] // size, part.shape[1]
     groups = [list(range(bits))[i : i + 2] for i in range(0, bits, 2)]
     left = list(range(bits))[::-1]
     buf = part.reshape([2] * bits + [rows, width])
     for stage, group in enumerate(groups):
         masks = [sum(1 << group[j] for j in range(len(group)) if (k >> j) & 1) for k in range(1 << len(group))]
-        digit = sum(((me >> group[j]) & 1) << j for j in range(len(group)))
 
         def block_of(value):
             out = buf
             for j in sorted(range(len(group)), key=lambda j: -left.index(group[j])):
-                out = lax.dynamic_index_in_dim(out, (value >> j) & 1, left.index(group[j]), keepdims=False)
+                out = lax.index_in_dim(out, (value >> j) & 1, left.index(group[j]), keepdims=False)
             return out
 
         coded = extra is not None and stage == 0 and first_type is not None
         stage_type = first_type if (stage == 0 and first_type is not None) else send_type
-        total = block_of(digit)
+        total = block_of(0)
         shape = total.shape
         if extra is not None:
             tail = jnp.concatenate([extra, jnp.zeros((2 * extra.shape[0], width), extra.dtype)]) if coded else extra
             total = jnp.concatenate([total.reshape(-1, width), tail])
         for k in range(1, len(masks)):
-            send = block_of(digit ^ k).astype(stage_type)
+            send = block_of(k).astype(stage_type)
             if extra is not None:
                 tail = code_rows(extra) if coded else extra
                 send = jnp.concatenate([send.reshape(-1, width), tail.astype(stage_type)])
@@ -109,7 +107,6 @@
 
 def double_gather(piece, axis, hold=None):
     size, bits = bit_count(axis)
-    me = lax.axis_index(axis)
     order = list(range(bits))[::-1]
     groups = [order[:1]] if bits % 2 else []
     groups += [order[i : i + 2] for i in range(bits % 2, bits, 2)]
@@ -118,18 +115,20 @@
     for group in groups:
         masks = [sum(1 << group[-1 - j] for j in range(len(group)) if (k >> j) & 1) for k in range(1 << len(group))]
         pieces = [buf] + [swap_with(buf, axis, size, None, mask) for mask in masks[1:]]
-        digit = sum(((me >> group[-1 - j]) & 1) << j for j in range(len(group)))
-        ordered = []
-        for place in range(len(masks)):
-            pick = pieces[place]
-            for held in range(1, len(masks)):
-                pick = jnp.where(digit == held, pieces[place ^ held], pick)
-            ordered.append(pick)
-        buf = jnp.stack(ordered, axis=1).reshape((-1,) + piece.shape)
+        buf = jnp.stack(pieces, axis=1).reshape((-1,) + piece.shape)
         if hold is not None and kept is None:
             buf, kept = lax.optimization_barrier((buf, hold))
     result = buf.reshape((size * piece.shape[0],) + piece.shape[1:])
     return result if hold is None else (result, kept)
+
+
+def xor_order(value, axis, dim):
+    size = lax.axis_size(axis)
+    me = lax.axis_index(axis)
+    shape = value.shape
+    split = shape[:dim] + (size, shape[dim] // size) + shape[dim + 1 :]
+    picked = jnp.take(value.reshape(split), jnp.arange(size) ^ me, axis=dim)
+    return picked.reshape(shape)
 
 def per_device(
     draws_user, draws_item, prior_user, prior_item, count_tiles, tile_blocks, tile_count
@@ -151,7 +150,10 @@
         tile_cols = jnp.sum(tiles_bf, axis=1, dtype=jnp.float32)
         user_deg = jnp.sum(jnp.where(row_pick[:, :, None], tile_rows[:, None, :], 0.0), axis=0)
         item_deg = jnp.sum(jnp.where(col_pick[:, :, None], tile_cols[:, None, :], 0.0), axis=0)
-        return (counts_bf, user_deg.reshape(-1), item_deg.reshape(-1))
+        counts_bf = xor_order(xor_order(counts_bf, "item", 0), "user", 1)
+        user_deg = xor_order(user_deg.reshape(-1), "item", 0)
+        item_deg = xor_order(item_deg.reshape(-1), "user", 0)
+        return (counts_bf, user_deg, item_deg)
 
     def cross_parts(user_range, item_range, counts):
         counts_bf, user_deg, item_deg = counts

time: 113 us -> 118 us (1.044)
  other arithmetic: 17.1 us -> 25.9 us
  waiting for transfers between devices: 29.7 us -> 25.8 us
  local copies, waits for them, and re-layouts: 17.5 us -> 19.2 us
  matrix products: 12.7 us -> 11.1 us
    gather x0 -> x7, local copies, waits for them, and re-layouts: none -> 6.55 us  [xor_order(): picked = jnp.take(value.reshape(split), jnp.arange(size) ^ me, axis=dim)]
    another operation x11 -> x7, other arithmetic: 3.28 us -> 8.19 us  [double_gather(): buf = jnp.stack(pieces, axis=1).reshape((-1,) + piece.shape)]
    dynamic_slice x8 -> x0, local copies, waits for them, and re-layouts: 4.37 us -> none  [block_of(): lax.dynamic_index_in_dim(out, value >> j & 1, left.index(group[j]), keepd...]
    ppermute x30, waiting for transfers between devices: 29.7 us -> 25.8 us  [swap_with(): return lax.ppermute(value, axis, pairs)]
    dot_general x2, matrix products: 6.04 us -> 3.21 us  [cross_parts(): jnp.dot(counts_bf, item_range, preferred_element_type=jnp.float32)]
    unnamed x43 -> x65, local copies, waits for them, and re-layouts: 4.39 us -> 1.83 us
    reduce_sum x14, other arithmetic: 2.4 us -> 4.78 us  [per_draw(): return jnp.sum(product, axis=(0, 2))]
    select_n x0 -> x6, other arithmetic: none -> 2.37 us  [xor_order(): picked = jnp.take(value.reshape(split), jnp.arange(size) ^ me, axis=dim)]
  transfers between devices with their start and end apart: 30 -> 30, of which waited for: 20 -> 12; matrix products, arithmetic and copies ran while one was open for 20% -> 32% of each run, Pallas kernels for 0% -> 0%
where the time goes in v11:
time: 118 us
  starting transfers between devices  33.4 us (28%)
  other arithmetic  25.9 us (22%)
  waiting for transfers between devices  25.8 us (22%)
  local copies, waits for them, and re-layouts  19.2 us (16%)
  matrix products  11.1 us (9%)
  between operations  2.12 us (2%)
    ppermute x30, starting transfers between devices, swap_with(): return lax.ppermute(value, axis, pairs)  33.4 us
    ppermute x30, waiting for transfers between devices, swap_with(): return lax.ppermute(value, axis, pairs)  25.8 us
    another operation x7, other arithmetic, double_gather(): buf = jnp.stack(pieces, axis=1).reshape((-1,) + piece.shape)  8.19 us
    gather x7, local copies, waits for them, and re-layouts, xor_order(): picked = jnp.take(value.reshape(split), jnp.arange(size) ^ me, axis=dim)  6.55 us
    reduce_sum x14, other arithmetic, per_draw(): return jnp.sum(product, axis=(0, 2))  4.78 us
    dot_general x4, matrix products, prior_term(): mixed = jnp.einsum('nde,ef->ndf', grouped, prior_mat, precision=top_prec)  3.45 us
    dot_general x2, matrix products, cross_parts(): jnp.dot(counts_bf, item_range, preferred_element_type=jnp.float32)  3.21 us
    dot_general x2, matrix products, cross_parts(): lax.dot_general(counts_bf, user_range, (((0,), (0,)), ((), ())), preferre...  3.14 us
  transfers between devices with their start and end apart: 30, of which 12 were waited for; matrix products, arithmetic and copies ran while one was open for 32% of the time, Pallas kernels for 0%

profile of v11, /device:TPU:0, one launch (start us, length us, event | category | flops | bytes accessed | tf_op | source)
XLA Modules:
  0.0 117.5 jit_solution(14000477296119209734)
XLA Ops:
  0.7 0.9 multiply_reduce_fusion.7
  1.6 5.1 %collective-permute-start.2 = (bf16[1,64,256]{2,1,0:T(8,128)(2,1)S(1)}, bf16[1,64,256]{2,1,0:T(8,128)(2,1)S(1)}, u32[]{:S(2)}, u32[]{:S(2)}) collective-permute-start(bf16[1,64,256]{2,1,0:T(8,128)(2,1)S(1)} %get-tuple-element.43), channel_id=1, source_target_pairs={{0,24},{2,26},{4,28},{6,30},{8,16},{10,18},{12,20},{14,22},{16,8},... | collective-permute-start | bytes 98312 | tf_op jit(solution)/shard_map/ppermute | solution.py:45
  7.4 1.3 %multiply_reduce_fusion.3 = (f32[256]{0:T(256)S(1)}, bf16[1,384,256]{2,1,0:T(8,128)(2,1)S(1)}) fusion(f32[1,384,256]{2,1,0:T(8,128)} %param.7), kind=kLoop, calls=%fused_computation.57 | loop fusion | flops 294656 | bytes 590848 | tf_op jit(solution)/shard_map/reduce_sum | solution.py:28
  9.3 0.9 squeeze.84
  10.2 1.2 copy.47
  12.8 0.9 multiply_reduce_fusion.4
  13.7 1.8 %multiply_reduce_fusion.2 = (f32[4]{0:T(128)}, f32[384,4,64]{0,2,1:T(8,128)}) fusion(f32[384,4,64]{0,2,1:T(8,128)S(1)} %bitcast.192, f32[64,64]{1,0:T(8,128)S(1)} %copy-done), kind=kOutput, calls=%fused_computation.56 | convolution fusion | flops 75694080 | bytes 802832 | tf_op jit(solution)/shard_map/nde,ef->ndf/dot_general | solution.py:22
  17.2 0.7 maximum_bitcast_fusion
  17.9 2.6 %collective-permute-start.6 = (bf16[4,64,256]{2,1,0:T(8,128)(2,1)}, bf16[4,64,256]{2,1,0:T(8,128)(2,1)}, u32[]{:S(2)}, u32[]{:S(2)}) collective-permute-start(bf16[4,64,256]{2,1,0:T(8,128)(2,1)} %maximum_bitcast_fusion), channel_id=1, source_target_pairs={{0,6},{2,4},{4,2},{6,0},{8,14},{10,12},{12,10},{14,8},{16,22},{18,... | collective-permute-start | bytes 393224 | tf_op jit(solution)/shard_map/ppermute | solution.py:45
  21.3 2.5 %convert_reduce_fusion.1 = (f32[12,256]{1,0:T(8,128)S(1)}, f32[12,256]{1,0:T(8,128)S(1)}) fusion(s32[12,256,256]{2,1,0:T(8,128)} %bitcast.181), kind=kLoop, calls=%fused_computation.5 | loop fusion | flops 3139584 | bytes 3170304 | tf_op jit(solution)/shard_map/reduce_sum | solution.py:150
  25.6 1.3 %fusion.2 = bf16[3,256,4,256]{3,2,0,1:T(4,128)(2,1)S(1)} fusion(bf16[12,256,256,1]{2,1,0,3:T(8,128)(2,1)S(1)} %convert_bitcast_fusion.4, pred[12,4]{0,1:T(4,128)(4,1)S(1)} %copy.42, pred[12,3]{0,1:T(4,128)(4,1)S(1)} %fusion.62), kind=kOutput, calls=%fused_computation.10 | convolution fusion | flops 18874512 | bytes 3145812 | tf_op jit(solution)/shard_map/trc,tij->ricj/dot_general | solution.py:146
  27.5 1.3 %reshape_reshape.22 = bf16[2,384,1024]{2,1,0:T(8,128)(2,1)S(1)} reshape(bf16[3,256,4,256]{3,2,1,0:T(4,128)(2,1)S(1)} %copy.44) | data formatting | bytes 3145728 | tf_op jit(solution)/shard_map/reshape;reshape | solution.py:130
  28.8 0.6 gather_fusion
  29.5 2.2 %copy.45 = bf16[2,384,1024]{1,0,2:T(2,128)(2,1)S(1)} copy(bf16[2,384,1024]{2,1,0:T(8,128)(2,1)S(1)} %gather_fusion) | data formatting | bytes 3145728 | tf_op jit(solution)/shard_map/jit(_take)/gather | solution.py:130
  31.7 1.0 gather.21
  32.8 0.7 gather_fusion.2
  33.4 0.8 broadcast_select_fusion.1
  34.3 0.8 gather_fusion.1
  35.0 0.7 broadcast_select_fusion.2
  35.7 0.8 broadcast_select_fusion
  36.7 1.2 pad_maximum_fusion
  37.9 1.0 pad_maximum_fusion.2
  38.9 1.6 %fusion.7 = (f32[256]{0:T(256)S(1)}, f32[768,256]{1,0:T(8,128)}) fusion(bf16[1,2,384,256]{3,2,1,0:T(8,128)(2,1)S(1)} %pad_maximum_fusion.2, bf16[768,256]{1,0:T(8,128)(2,1)S(1)} %bitcast.195, f32[768]{0:T(1024)S(1)} %broadcast_select_fusion.3, bf16[768,1024]{0,1:T(8,128)(2,1)S(1)} %bitcast.177, bf16[1024,256]{1,0:T(8,128)(2,1)S(1)} %bitcast.185), kind=kOutput, calls=%fused_computation.25 | convolution fusion | flops 403832576 | bytes 3674112 | tf_op jit(solution)/shard_map/dot_general | solution.py:160
  40.8 1.6 %fusion.5 = (f32[256]{0:T(256)S(1)}, f32[1024,256]{1,0:T(8,128)S(1)}) fusion(bf16[4,4,64,256]{3,2,1,0:T(8,128)(2,1)S(1)} %copy.46, bf16[1024,256]{1,0:T(8,128)(2,1)S(1)} %bitcast.186, f32[1024]{0:T(1024)S(1)} %select_n.103, bf16[768,1024]{0,1:T(8,128)(2,1)S(1)} %bitcast.178, bf16[768,256]{1,0:T(8,128)(2,1)} %bitcast.196), kind=kOutput, calls=%fused_computation.19 | convolution fusion | flops 404225792 | bytes 4068352 | tf_op jit(solution)/shard_map/dot_general | solution.py:162
  42.9 1.7 %collective-permute-start.7 = (bf16[280,256]{1,0:T(8,128)(2,1)S(1)}, bf16[280,256]{1,0:T(8,128)(2,1)S(1)}, u32[]{:S(2)}, u32[]{:S(2)}) collective-permute-start(bf16[280,256]{1,0:T(8,128)(2,1)S(1)} %get-tuple-element.47), channel_id=1, source_target_pairs={{0,2},{2,0},{4,6},{6,4},{8,10},{10,8},{12,14},{14,12},{16,18},{18,... | collective-permute-start | bytes 430088 | tf_op jit(solution)/shard_map/ppermute | solution.py:45
  44.6 1.5 %collective-permute-start.8 = (bf16[280,256]{1,0:T(8,128)(2,1)S(1)}, bf16[280,256]{1,0:T(8,128)(2,1)S(1)}, u32[]{:S(2)}, u32[]{:S(2)}) collective-permute-start(bf16[280,256]{1,0:T(8,128)(2,1)S(1)} %get-tuple-element.48), channel_id=1, source_target_pairs={{0,4},{2,6},{4,0},{6,2},{8,12},{10,14},{12,8},{14,10},{16,20},{18,... | collective-permute-start | bytes 430088 | tf_op jit(solution)/shard_map/ppermute | solution.py:45
  46.5 2.2 %collective-permute-done.7 = bf16[280,256]{1,0:T(8,128)(2,1)S(1)} collective-permute-done((bf16[280,256]{1,0:T(8,128)(2,1)S(1)}, bf16[280,256]{1,0:T(8,128)(2,1)S(1)}, u32[]{:S(2)}, u32[]{:S(2)}) %collective-permute-start.7) | collective-permute-done | bytes 143392 | tf_op jit(solution)/shard_map/ppermute | solution.py:45
  48.8 4.0 %collective-permute-done.8 = bf16[280,256]{1,0:T(8,128)(2,1)S(1)} collective-permute-done((bf16[280,256]{1,0:T(8,128)(2,1)S(1)}, bf16[280,256]{1,0:T(8,128)(2,1)S(1)}, u32[]{:S(2)}, u32[]{:S(2)}) %collective-permute-start.8) | collective-permute-done | bytes 143392 | tf_op jit(solution)/shard_map/ppermute | solution.py:45
  53.0 0.7 pad_maximum_fusion.24
  53.7 1.2 %collective-permute-start.10 = (f32[72,256]{1,0:T(8,128)}, f32[72,256]{1,0:T(8,128)S(1)}, u32[]{:S(2)}, u32[]{:S(2)}) collective-permute-start(f32[72,256]{1,0:T(8,128)} %get-tuple-element.53), channel_id=1, source_target_pairs={{0,8},{2,10},{4,12},{6,14},{8,0},{10,2},{12,4},{14,6},{16,24},{18,... | collective-permute-start | bytes 221192 | tf_op jit(solution)/shard_map/ppermute | solution.py:45
  54.9 2.9 %collective-permute-start.11 = (f32[72,256]{1,0:T(8,128)}, f32[72,256]{1,0:T(8,128)S(1)}, u32[]{:S(2)}, u32[]{:S(2)}) collective-permute-start(f32[72,256]{1,0:T(8,128)} %get-tuple-element.54), channel_id=1, source_target_pairs={{0,16},{2,18},{4,20},{6,22},{8,24},{10,26},{12,28},{14,30},{16,0},... | collective-permute-start | bytes 221192 | tf_op jit(solution)/shard_map/ppermute | solution.py:45
  58.5 1.2 slice.351
  59.7 2.2 %collective-permute-done.11 = f32[72,256]{1,0:T(8,128)S(1)} collective-permute-done((f32[72,256]{1,0:T(8,128)}, f32[72,256]{1,0:T(8,128)S(1)}, u32[]{:S(2)}, u32[]{:S(2)}) %collective-permute-start.11) | collective-permute-done | bytes 73760 | tf_op jit(solution)/shard_map/ppermute | solution.py:45
  62.0 2.1 %collective-permute-done.12 = f32[72,256]{1,0:T(8,128)} collective-permute-done((f32[72,256]{1,0:T(8,128)S(1)}, f32[72,256]{1,0:T(8,128)}, u32[]{:S(2)}, u32[]{:S(2)}) %collective-permute-start.12) | collective-permute-done | bytes 73760 | tf_op jit(solution)/shard_map/ppermute | solution.py:45
  64.1 0.9 fusion.36
  65.1 1.1 collective-permute-done.13
  68.9 1.1 collective-permute-start.18
  70.0 3.3 %collective-permute-start.16 = (bf16[1,64,256]{2,1,0:T(8,128)(2,1)}, bf16[1,64,256]{2,1,0:T(8,128)(2,1)}, u32[]{:S(2)}, u32[]{:S(2)}) collective-permute-start(bf16[1,64,256]{2,1,0:T(8,128)(2,1)} %get-tuple-element.41), channel_id=1, source_target_pairs={{0,8},{2,10},{4,12},{6,14},{8,0},{10,2},{12,4},{14,6},{16,24},{18,... | collective-permute-start | bytes 98312 | tf_op jit(solution)/shard_map/ppermute | solution.py:45
  73.3 1.8 %convert_bitcast_fusion.1 = (bf16[1,1,384,256]{3,2,1,0:T(8,128)(2,1)}, f32[384,256]{1,0:T(8,128)S(1)}) fusion(f32[384,256]{1,0:T(8,128)S(1)} %copy.51, bf16[384,256]{1,0:T(8,128)(2,1)S(1)} %collective-permute-done.14, f32[768,256]{1,0:T(8,128)} %get-tuple-element.65, f32[256]{0:T(256)S(1)} %mul.192, f32[1,384,256]{2,1,0:T(8,128)S(1)} %copy-done.2), kind=kLoop, calls=%fused_computation.102 | loop fusion | flops 688128 | bytes 1967104 | tf_op jit(solution)/shard_map/stack;broadcast_in_dim | solution.py:118
  76.0 1.6 %fusion.54 = (bf16[4,1,64,256]{3,2,0,1:T(8,128)(2,1)S(1)}, bf16[4,64,256]{2,1,0:T(8,128)(2,1)}) fusion(bf16[1,1,64,256]{3,2,1,0:T(8,128)(2,1)} %bitcast.53, bf16[1,1,64,256]{3,2,1,0:T(8,128)(2,1)} %bitcast.52, bf16[1,1,64,256]{3,2,1,0:T(8,128)(2,1)} %bitcast.51, bf16[1,1,64,256]{3,2,1,0:T(8,128)(2,1)S(1)} %copy-done.19), kind=kLoop, calls=%fused_computation.144 | loop fusion | flops 196608 | bytes 393216 | tf_op jit(solution)/shard_map/stack;reshape | solution.py:118
  77.5 1.4 %collective-permute-start.21 = (bf16[4,64,256]{2,1,0:T(8,128)(2,1)}, bf16[4,64,256]{2,1,0:T(8,128)(2,1)}, u32[]{:S(2)}, u32[]{:S(2)}) collective-permute-start(bf16[4,64,256]{2,1,0:T(8,128)(2,1)} %get-tuple-element.38), channel_id=1, source_target_pairs={{0,6},{2,4},{4,2},{6,0},{8,14},{10,12},{12,10},{14,8},{16,22},{18,... | collective-permute-start | bytes 393224 | tf_op jit(solution)/shard_map/ppermute | solution.py:45
  79.0 1.2 %collective-permute-start.20 = (bf16[4,64,256]{2,1,0:T(8,128)(2,1)}, bf16[4,64,256]{2,1,0:T(8,128)(2,1)}, u32[]{:S(2)}, u32[]{:S(2)}) collective-permute-start(bf16[4,64,256]{2,1,0:T(8,128)(2,1)} %get-tuple-element.38), channel_id=1, source_target_pairs={{0,4},{2,6},{4,0},{6,2},{8,12},{10,14},{12,8},{14,10},{16,20},{18,... | collective-permute-start | bytes 393224 | tf_op jit(solution)/shard_map/ppermute | solution.py:45
  80.2 0.9 collective-permute-start.19
  81.0 0.7 multiply_reduce_fusion.1
  82.6 2.6 %collective-permute-done.21 = bf16[4,64,256]{2,1,0:T(8,128)(2,1)} collective-permute-done((bf16[4,64,256]{2,1,0:T(8,128)(2,1)}, bf16[4,64,256]{2,1,0:T(8,128)(2,1)}, u32[]{:S(2)}, u32[]{:S(2)}) %collective-permute-start.21) | collective-permute-done | bytes 131104 | tf_op jit(solution)/shard_map/ppermute | solution.py:45
  85.2 1.6 %collective-permute-done.20 = bf16[4,64,256]{2,1,0:T(8,128)(2,1)} collective-permute-done((bf16[4,64,256]{2,1,0:T(8,128)(2,1)}, bf16[4,64,256]{2,1,0:T(8,128)(2,1)}, u32[]{:S(2)}, u32[]{:S(2)}) %collective-permute-start.20) | collective-permute-done | bytes 131104 | tf_op jit(solution)/shard_map/ppermute | solution.py:45
  86.7 1.1 pad_maximum_fusion.1
  87.9 1.0 pad_maximum_fusion.3
  88.9 1.6 %fusion.8 = (f32[256]{0:T(256)S(1)}, f32[768,256]{1,0:T(8,128)}) fusion(bf16[1,2,384,256]{3,2,1,0:T(8,128)(2,1)S(1)} %pad_maximum_fusion.3, bf16[768,256]{1,0:T(8,128)(2,1)S(1)} %bitcast.197, f32[768]{0:T(1024)S(1)} %copy-done.25, bf16[768,1024]{0,1:T(8,128)(2,1)S(1)} %bitcast.179, bf16[1024,256]{1,0:T(8,128)(2,1)S(1)} %bitcast.183), kind=kOutput, calls=%fused_computation.26 | convolution fusion | flops 403832576 | bytes 3674112 | tf_op jit(solution)/shard_map/dot_general | solution.py:160
  90.5 1.6 %fusion.6 = (f32[256]{0:T(256)S(1)}, f32[1024,256]{1,0:T(8,128)}) fusion(bf16[4,4,64,256]{3,2,1,0:T(8,128)(2,1)S(1)} %copy.53, bf16[1024,256]{1,0:T(8,128)(2,1)S(1)} %bitcast.184, f32[1024]{0:T(1024)S(1)} %select_n.103, bf16[768,1024]{0,1:T(8,128)(2,1)S(1)} %bitcast.180, bf16[768,256]{1,0:T(8,128)(2,1)S(1)} %bitcast.198), kind=kOutput, calls=%fused_computation.20 | convolution fusion | flops 404225792 | bytes 4068352 | tf_op jit(solution)/shard_map/dot_general | solution.py:162
  92.5 1.1 fusion.26
  93.6 1.1 slice_bitcast_fusion
  94.8 1.3 %collective-permute-start.22 = (bf16[280,256]{1,0:T(8,128)(2,1)S(1)}, bf16[280,256]{1,0:T(8,128)(2,1)S(1)}, u32[]{:S(2)}, u32[]{:S(2)}) collective-permute-start(bf16[280,256]{1,0:T(8,128)(2,1)S(1)} %get-tuple-element.44), channel_id=1, source_target_pairs={{0,2},{2,0},{4,6},{6,4},{8,10},{10,8},{12,14},{14,12},{16,18},{18,... | collective-permute-start | bytes 430088 | tf_op jit(solution)/shard_map/ppermute | solution.py:45
  96.1 0.7 collective-permute-start.23
  96.8 1.5 %collective-permute-start.24 = (bf16[280,256]{1,0:T(8,128)(2,1)S(1)}, bf16[280,256]{1,0:T(8,128)(2,1)S(1)}, u32[]{:S(2)}, u32[]{:S(2)}) collective-permute-start(bf16[280,256]{1,0:T(8,128)(2,1)S(1)} %get-tuple-element.46), channel_id=1, source_target_pairs={{0,6},{2,4},{4,2},{6,0},{8,14},{10,12},{12,10},{14,8},{16,22},{18,... | collective-permute-start | bytes 430088 | tf_op jit(solution)/shard_map/ppermute | solution.py:45
  98.4 3.1 %collective-permute-done.22 = bf16[280,256]{1,0:T(8,128)(2,1)S(1)} collective-permute-done((bf16[280,256]{1,0:T(8,128)(2,1)S(1)}, bf16[280,256]{1,0:T(8,128)(2,1)S(1)}, u32[]{:S(2)}, u32[]{:S(2)}) %collective-permute-start.22) | collective-permute-done | bytes 143392 | tf_op jit(solution)/shard_map/ppermute | solution.py:45
  101.5 0.9 collective-permute-done.23
  102.4 2.1 %collective-permute-done.24 = bf16[280,256]{1,0:T(8,128)(2,1)S(1)} collective-permute-done((bf16[280,256]{1,0:T(8,128)(2,1)S(1)}, bf16[280,256]{1,0:T(8,128)(2,1)S(1)}, u32[]{:S(2)}, u32[]{:S(2)}) %collective-permute-start.24) | collective-permute-done | bytes 143392 | tf_op jit(solution)/shard_map/ppermute | solution.py:45
  105.5 3.7 %collective-permute-start.27 = (f32[72,256]{1,0:T(8,128)S(1)}, f32[72,256]{1,0:T(8,128)S(1)}, u32[]{:S(2)}, u32[]{:S(2)}) collective-permute-start(f32[72,256]{1,0:T(8,128)S(1)} %get-tuple-element.52), channel_id=1, source_target_pairs={{0,24},{2,26},{4,28},{6,30},{8,16},{10,18},{12,20},{14,22},{16,8},... | collective-permute-start | bytes 221192 | tf_op jit(solution)/shard_map/ppermute | solution.py:45
  109.2 1.0 slice.350
  110.4 2.7 %collective-permute-done.26 = f32[72,256]{1,0:T(8,128)S(1)} collective-permute-done((f32[72,256]{1,0:T(8,128)S(1)}, f32[72,256]{1,0:T(8,128)S(1)}, u32[]{:S(2)}, u32[]{:S(2)}) %collective-permute-start.26) | collective-permute-done | bytes 73760 | tf_op jit(solution)/shard_map/ppermute | solution.py:45
  113.2 1.1 collective-permute-done.28
  114.7 0.7 fusion.41
  115.4 2.1 %fusion.14 = (f32[1,384,256]{2,1,0:T(8,128)}, f32[1,384,256]{2,1,0:T(8,128)}) fusion(f32[384,256]{1,0:T(8,128)S(1)} %get-tuple-element.17, f32[384,256]{1,0:T(8,128)S(1)} %copy-done.6, f32[768,256]{1,0:T(8,128)} %get-tuple-element.73, bf16[384,256]{1,0:T(8,128)(2,1)S(1)} %collective-permute-done.29, f32[256]{0:T(256)S(1)} %mul.212, f32[256]{0:T(256)S(1)} %mul.210, ...), kind=kLoop, calls=%fused_computation.40 | loop fusion | flops 1671168 | bytes 3542016 | tf_op jit(solution)/shard_map/broadcast_in_dim | solution.py:223
  (198 shorter events, 15.5 us)
Async XLA Ops:
  0.6 13.0 %copy-start = (f32[64,64]{1,0:T(8,128)S(1)}, f32[64,64]{1,0:T(8,128)}, u32[]{:S(2)}) copy-start(f32[64,64]{1,0:T(8,128)} %param.9) | copy-start | bytes 49156
  0.6 11.4 %copy-start.30 = (s32[1,1,12,2]{2,3,1,0:T(2,128)S(1)}, s32[1,1,12,2]{2,3,1,0:T(2,128)}, u32[]{:S(2)}) copy-start(s32[1,1,12,2]{2,3,1,0:T(2,128)} %param.12) | copy-start | bytes 292
  0.7 12.1 %copy-start.18 = (f32[64,64]{1,0:T(8,128)S(1)}, f32[64,64]{1,0:T(8,128)}, u32[]{:S(2)}) copy-start(f32[64,64]{1,0:T(8,128)} %param.10) | copy-start | bytes 49156
  1.6 15.6 %collective-permute-start.2 = (bf16[1,64,256]{2,1,0:T(8,128)(2,1)S(1)}, bf16[1,64,256]{2,1,0:T(8,128)(2,1)S(1)}, u32[]{:S(2)}, u32[]{:S(2)}) collective-permute-start(bf16[1,64,256]{2,1,0:T(8,128)(2,1)S(1)} %get-tuple-element.43), channel_id=1, source_target_pairs={{0,24},{2,26},{4,28},{6,30},{8,16},{10,18},{12,20},{14,22},{16,8},... | collective-permute-start | bytes 98312 | tf_op jit(solution)/shard_map/ppermute | solution.py:45
  6.7 10.4 %collective-permute-start.1 = (bf16[1,64,256]{2,1,0:T(8,128)(2,1)S(1)}, bf16[1,64,256]{2,1,0:T(8,128)(2,1)S(1)}, u32[]{:S(2)}, u32[]{:S(2)}) collective-permute-start(bf16[1,64,256]{2,1,0:T(8,128)(2,1)S(1)} %get-tuple-element.43), channel_id=1, source_target_pairs={{0,16},{2,18},{4,20},{6,22},{8,24},{10,26},{12,28},{14,30},{16,0},... | collective-permute-start | bytes 98312 | tf_op jit(solution)/shard_map/ppermute | solution.py:45
  6.7 10.4 %collective-permute-start = (bf16[1,64,256]{2,1,0:T(8,128)(2,1)S(1)}, bf16[1,64,256]{2,1,0:T(8,128)(2,1)S(1)}, u32[]{:S(2)}, u32[]{:S(2)}) collective-permute-start(bf16[1,64,256]{2,1,0:T(8,128)(2,1)S(1)} %get-tuple-element.43), channel_id=1, source_target_pairs={{0,8},{2,10},{4,12},{6,14},{8,0},{10,2},{12,4},{14,6},{16,24},{18,... | collective-permute-start | bytes 98312 | tf_op jit(solution)/shard_map/ppermute | solution.py:45
  8.6 29.3 %collective-permute-start.3 = (bf16[1,384,256]{2,1,0:T(8,128)(2,1)S(1)}, bf16[1,384,256]{2,1,0:T(8,128)(2,1)}, u32[]{:S(2)}, u32[]{:S(2)}) collective-permute-start(bf16[1,384,256]{2,1,0:T(8,128)(2,1)S(1)} %get-tuple-element.24), channel_id=1, source_target_pairs={{0,1},{1,0},{2,3},{3,2},{4,5},{5,4},{6,7},{7,6},{8,9},{9,8},{10,11... | collective-permute-start | bytes 589832 | tf_op jit(solution)/shard_map/ppermute | solution.py:45
  17.8 6.0 %copy-start.1 = (s32[1,1,12,256,256]{4,3,2,1,0:T(8,128)S(1)}, s32[1,1,12,256,256]{4,3,2,1,0:T(8,128)}, u32[]{:S(2)}) copy-start(s32[1,1,12,256,256]{4,3,2,1,0:T(8,128)} %param.11) | copy-start | bytes 9437188
  17.9 18.9 %collective-permute-start.6 = (bf16[4,64,256]{2,1,0:T(8,128)(2,1)}, bf16[4,64,256]{2,1,0:T(8,128)(2,1)}, u32[]{:S(2)}, u32[]{:S(2)}) collective-permute-start(bf16[4,64,256]{2,1,0:T(8,128)(2,1)} %maximum_bitcast_fusion), channel_id=1, source_target_pairs={{0,6},{2,4},{4,2},{6,0},{8,14},{10,12},{12,10},{14,8},{16,22},{18,... | collective-permute-start | bytes 393224 | tf_op jit(solution)/shard_map/ppermute | solution.py:45
  20.4 16.3 %collective-permute-start.5 = (bf16[4,64,256]{2,1,0:T(8,128)(2,1)}, bf16[4,64,256]{2,1,0:T(8,128)(2,1)}, u32[]{:S(2)}, u32[]{:S(2)}) collective-permute-start(bf16[4,64,256]{2,1,0:T(8,128)(2,1)} %maximum_bitcast_fusion), channel_id=1, source_target_pairs={{0,4},{2,6},{4,0},{6,2},{8,12},{10,14},{12,8},{14,10},{16,20},{18,... | collective-permute-start | bytes 393224 | tf_op jit(solution)/shard_map/ppermute | solution.py:45
  20.9 15.8 %collective-permute-start.4 = (bf16[4,64,256]{2,1,0:T(8,128)(2,1)}, bf16[4,64,256]{2,1,0:T(8,128)(2,1)}, u32[]{:S(2)}, u32[]{:S(2)}) collective-permute-start(bf16[4,64,256]{2,1,0:T(8,128)(2,1)} %maximum_bitcast_fusion), channel_id=1, source_target_pairs={{0,2},{2,0},{4,6},{6,4},{8,10},{10,8},{12,14},{14,12},{16,18},{18,... | collective-permute-start | bytes 393224 | tf_op jit(solution)/shard_map/ppermute | solution.py:45
  35.7 0.9 copy-start.22
  35.7 0.9 copy-start.23
  36.6 3.9 %copy-start.24 = (f32[768]{0:T(1024)}, f32[768]{0:T(1024)S(1)}, u32[]{:S(2)}) copy-start(f32[768]{0:T(1024)S(1)} %broadcast_select_fusion.3) | copy-start | bytes 9220
  38.9 1.7 %copy-start.8 = (bf16[1,2,384,256]{3,2,1,0:T(8,128)(2,1)}, bf16[1,2,384,256]{3,2,1,0:T(8,128)(2,1)S(1)}, u32[]{:S(2)}) copy-start(bf16[1,2,384,256]{3,2,1,0:T(8,128)(2,1)S(1)} %pad_maximum_fusion.2) | copy-start | bytes 1179652
  40.7 1.8 %copy-start.26 = (f32[4]{0:T(128)S(1)}, f32[4]{0:T(128)}, u32[]{:S(2)}) copy-start(f32[4]{0:T(128)} %get-tuple-element.70) | copy-start | bytes 52
  40.7 1.8 %copy-start.29 = (f32[4]{0:T(128)S(1)}, f32[4]{0:T(128)}, u32[]{:S(2)}) copy-start(f32[4]{0:T(128)} %get-tuple-element.68) | copy-start | bytes 52
  40.8 1.8 %copy-start.31 = (f32[4]{0:T(128)S(1)}, f32[4]{0:T(128)}, u32[]{:S(2)}) copy-start(f32[4]{0:T(128)} %add.169) | copy-start | bytes 52
  42.9 5.9 %collective-permute-start.7 = (bf16[280,256]{1,0:T(8,128)(2,1)S(1)}, bf16[280,256]{1,0:T(8,128)(2,1)S(1)}, u32[]{:S(2)}, u32[]{:S(2)}) collective-permute-start(bf16[280,256]{1,0:T(8,128)(2,1)S(1)} %get-tuple-element.47), channel_id=1, source_target_pairs={{0,2},{2,0},{4,6},{6,4},{8,10},{10,8},{12,14},{14,12},{16,18},{18,... | collective-permute-start | bytes 430088 | tf_op jit(solution)/shard_map/ppermute | solution.py:45
  44.6 8.2 %collective-permute-start.8 = (bf16[280,256]{1,0:T(8,128)(2,1)S(1)}, bf16[280,256]{1,0:T(8,128)(2,1)S(1)}, u32[]{:S(2)}, u32[]{:S(2)}) collective-permute-start(bf16[280,256]{1,0:T(8,128)(2,1)S(1)} %get-tuple-element.48), channel_id=1, source_target_pairs={{0,4},{2,6},{4,0},{6,2},{8,12},{10,14},{12,8},{14,10},{16,20},{18,... | collective-permute-start | bytes 430088 | tf_op jit(solution)/shard_map/ppermute | solution.py:45
  46.1 6.7 %collective-permute-start.9 = (bf16[280,256]{1,0:T(8,128)(2,1)S(1)}, bf16[280,256]{1,0:T(8,128)(2,1)S(1)}, u32[]{:S(2)}, u32[]{:S(2)}) collective-permute-start(bf16[280,256]{1,0:T(8,128)(2,1)S(1)} %get-tuple-element.49), channel_id=1, source_target_pairs={{0,6},{2,4},{4,2},{6,0},{8,14},{10,12},{12,10},{14,8},{16,22},{18,... | collective-permute-start | bytes 430088 | tf_op jit(solution)/shard_map/ppermute | solution.py:45
  46.5 6.4 %copy-start.20 = (f32[280]{0:T(512)}, f32[280]{0:T(512)S(1)}, u32[]{:S(2)}) copy-start(f32[280]{0:T(512)S(1)} %pad.66.clone) | copy-start | bytes 3364
  46.5 11.8 %copy-start.7 = (f32[384,4,64]{0,2,1:T(8,128)S(1)}, f32[384,4,64]{0,2,1:T(8,128)}, u32[]{:S(2)}) copy-start(f32[384,4,64]{0,2,1:T(8,128)} %get-tuple-element.69) | copy-start | bytes 1179652
  52.9 14.0 %copy-start.10 = (f32[1,64,256]{2,1,0:T(8,128)S(1)}, f32[1,64,256]{2,1,0:T(8,128)}, u32[]{:S(2)}) copy-start(f32[1,64,256]{2,1,0:T(8,128)} %param.8) | copy-start | bytes 196612
  53.7 6.1 %collective-permute-start.10 = (f32[72,256]{1,0:T(8,128)}, f32[72,256]{1,0:T(8,128)S(1)}, u32[]{:S(2)}, u32[]{:S(2)}) collective-permute-start(f32[72,256]{1,0:T(8,128)} %get-tuple-element.53), channel_id=1, source_target_pairs={{0,8},{2,10},{4,12},{6,14},{8,0},{10,2},{12,4},{14,6},{16,24},{18,... | collective-permute-start | bytes 221192 | tf_op jit(solution)/shard_map/ppermute | solution.py:45
  54.9 7.0 %collective-permute-start.11 = (f32[72,256]{1,0:T(8,128)}, f32[72,256]{1,0:T(8,128)S(1)}, u32[]{:S(2)}, u32[]{:S(2)}) collective-permute-start(f32[72,256]{1,0:T(8,128)} %get-tuple-element.54), channel_id=1, source_target_pairs={{0,16},{2,18},{4,20},{6,22},{8,24},{10,26},{12,28},{14,30},{16,0},... | collective-permute-start | bytes 221192 | tf_op jit(solution)/shard_map/ppermute | solution.py:45
  57.8 6.3 %collective-permute-start.12 = (f32[72,256]{1,0:T(8,128)S(1)}, f32[72,256]{1,0:T(8,128)}, u32[]{:S(2)}, u32[]{:S(2)}) collective-permute-start(f32[72,256]{1,0:T(8,128)S(1)} %get-tuple-element.55), channel_id=1, source_target_pairs={{0,24},{2,26},{4,28},{6,30},{8,16},{10,18},{12,20},{14,22},{16,8},... | collective-permute-start | bytes 221192 | tf_op jit(solution)/shard_map/ppermute | solution.py:45
  58.1 15.1 %copy-start.2 = (f32[1,384,256]{2,1,0:T(8,128)S(1)}, f32[1,384,256]{2,1,0:T(8,128)}, u32[]{:S(2)}) copy-start(f32[1,384,256]{2,1,0:T(8,128)} %param.7) | copy-start | bytes 1179652
  58.3 16.7 %copy-start.12 = (f32[64,256]{1,0:T(8,128)}, f32[64,256]{1,0:T(8,128)S(1)}, u32[]{:S(2)}) copy-start(f32[64,256]{1,0:T(8,128)S(1)} %reshape.438) | copy-start | bytes 196612
  58.5 16.6 %copy-start.3 = (f32[384,256]{1,0:T(8,128)}, f32[384,256]{1,0:T(8,128)S(1)}, u32[]{:S(2)}) copy-start(f32[384,256]{1,0:T(8,128)S(1)} %copy.51) | copy-start | bytes 1179652
  59.6 13.6 %collective-permute-start.14 = (bf16[384,256]{1,0:T(8,128)(2,1)S(1)}, bf16[384,256]{1,0:T(8,128)(2,1)S(1)}, u32[]{:S(2)}, u32[]{:S(2)}) collective-permute-start(bf16[384,256]{1,0:T(8,128)(2,1)S(1)} %slice.351), channel_id=1, source_target_pairs={{0,1},{1,0},{2,3},{3,2},{4,5},{5,4},{6,7},{7,6},{8,9},{9,8},{10,11... | collective-permute-start | bytes 589832 | tf_op jit(solution)/shard_map/ppermute | solution.py:45
  65.0 3.0 %copy-start.16 = (f32[72,256]{1,0:T(8,128)}, f32[72,256]{1,0:T(8,128)S(1)}, u32[]{:S(2)}) copy-start(f32[72,256]{1,0:T(8,128)S(1)} %fusion.36) | copy-start | bytes 221188
  65.0 1.2 %collective-permute-start.13 = (f32[8]{0:T(128)S(1)}, f32[8]{0:T(128)S(1)}, u32[]{:S(2)}, u32[]{:S(2)}) collective-permute-start(f32[8]{0:T(128)S(1)} %slice_bitcast_fusion.11), channel_id=1, source_target_pairs={{0,1},{1,0},{2,3},{3,2},{4,5},{5,4},{6,7},{7,6},{8,9},{9,8},{10,11... | collective-permute-start | bytes 104 | tf_op jit(solution)/shard_map/ppermute | solution.py:45
  66.2 0.5 copy-start.27
  68.2 7.0 %copy-start.14 = (f32[64,256]{1,0:T(8,128)}, f32[64,256]{1,0:T(8,128)S(1)}, u32[]{:S(2)}) copy-start(f32[64,256]{1,0:T(8,128)S(1)} %reshape.444) | copy-start | bytes 196612
  68.9 7.1 %collective-permute-start.18 = (bf16[1,64,256]{2,1,0:T(8,128)(2,1)}, bf16[1,64,256]{2,1,0:T(8,128)(2,1)}, u32[]{:S(2)}, u32[]{:S(2)}) collective-permute-start(bf16[1,64,256]{2,1,0:T(8,128)(2,1)} %get-tuple-element.41), channel_id=1, source_target_pairs={{0,24},{2,26},{4,28},{6,30},{8,16},{10,18},{12,20},{14,22},{16,8},... | collective-permute-start | bytes 98312 | tf_op jit(solution)/shard_map/ppermute | solution.py:45
  70.0 5.9 %collective-permute-start.17 = (bf16[1,64,256]{2,1,0:T(8,128)(2,1)}, bf16[1,64,256]{2,1,0:T(8,128)(2,1)}, u32[]{:S(2)}, u32[]{:S(2)}) collective-permute-start(bf16[1,64,256]{2,1,0:T(8,128)(2,1)} %get-tuple-element.41), channel_id=1, source_target_pairs={{0,16},{2,18},{4,20},{6,22},{8,24},{10,26},{12,28},{14,30},{16,0},... | collective-permute-start | bytes 98312 | tf_op jit(solution)/shard_map/ppermute | solution.py:45
  70.0 5.9 %collective-permute-start.16 = (bf16[1,64,256]{2,1,0:T(8,128)(2,1)}, bf16[1,64,256]{2,1,0:T(8,128)(2,1)}, u32[]{:S(2)}, u32[]{:S(2)}) collective-permute-start(bf16[1,64,256]{2,1,0:T(8,128)(2,1)} %get-tuple-element.41), channel_id=1, source_target_pairs={{0,8},{2,10},{4,12},{6,14},{8,0},{10,2},{12,4},{14,6},{16,24},{18,... | collective-permute-start | bytes 98312 | tf_op jit(solution)/shard_map/ppermute | solution.py:45
  75.0 0.9 copy-start.19
  75.9 10.8 %copy-start.5 = (f32[384,256]{1,0:T(8,128)}, f32[384,256]{1,0:T(8,128)S(1)}, u32[]{:S(2)}) copy-start(f32[384,256]{1,0:T(8,128)S(1)} %copy.56) | copy-start | bytes 1179652
  77.5 10.3 %copy-start.11 = (bf16[1,1,384,256]{3,2,1,0:T(8,128)(2,1)S(1)}, bf16[1,1,384,256]{3,2,1,0:T(8,128)(2,1)}, u32[]{:S(2)}) copy-start(bf16[1,1,384,256]{3,2,1,0:T(8,128)(2,1)} %get-tuple-element.16) | copy-start | bytes 589828
  77.5 7.6 %collective-permute-start.21 = (bf16[4,64,256]{2,1,0:T(8,128)(2,1)}, bf16[4,64,256]{2,1,0:T(8,128)(2,1)}, u32[]{:S(2)}, u32[]{:S(2)}) collective-permute-start(bf16[4,64,256]{2,1,0:T(8,128)(2,1)} %get-tuple-element.38), channel_id=1, source_target_pairs={{0,6},{2,4},{4,2},{6,0},{8,14},{10,12},{12,10},{14,8},{16,22},{18,... | collective-permute-start | bytes 393224 | tf_op jit(solution)/shard_map/ppermute | solution.py:45
  79.0 7.7 %collective-permute-start.20 = (bf16[4,64,256]{2,1,0:T(8,128)(2,1)}, bf16[4,64,256]{2,1,0:T(8,128)(2,1)}, u32[]{:S(2)}, u32[]{:S(2)}) collective-permute-start(bf16[4,64,256]{2,1,0:T(8,128)(2,1)} %get-tuple-element.38), channel_id=1, source_target_pairs={{0,4},{2,6},{4,0},{6,2},{8,12},{10,14},{12,8},{14,10},{16,20},{18,... | collective-permute-start | bytes 393224 | tf_op jit(solution)/shard_map/ppermute | solution.py:45
  80.2 6.6 %collective-permute-start.19 = (bf16[4,64,256]{2,1,0:T(8,128)(2,1)}, bf16[4,64,256]{2,1,0:T(8,128)(2,1)}, u32[]{:S(2)}, u32[]{:S(2)}) collective-permute-start(bf16[4,64,256]{2,1,0:T(8,128)(2,1)} %get-tuple-element.38), channel_id=1, source_target_pairs={{0,2},{2,0},{4,6},{6,4},{8,10},{10,8},{12,14},{14,12},{16,18},{18,... | collective-permute-start | bytes 393224 | tf_op jit(solution)/shard_map/ppermute | solution.py:45
  81.8 7.1 %copy-start.25 = (f32[768]{0:T(1024)S(1)}, f32[768]{0:T(1024)}, u32[]{:S(2)}) copy-start(f32[768]{0:T(1024)} %copy-done.24) | copy-start | bytes 9220
  81.8 6.1 %collective-permute-start.15 = (bf16[1,384,256]{2,1,0:T(8,128)(2,1)}, bf16[1,384,256]{2,1,0:T(8,128)(2,1)}, u32[]{:S(2)}, u32[]{:S(2)}) collective-permute-start(bf16[1,384,256]{2,1,0:T(8,128)(2,1)} %get-tuple-element.22), channel_id=1, source_target_pairs={{0,1},{1,0},{2,3},{3,2},{4,5},{5,4},{6,7},{7,6},{8,9},{9,8},{10,11... | collective-permute-start | bytes 589832 | tf_op jit(solution)/shard_map/ppermute | solution.py:45
  93.6 10.9 %copy-start.21 = (f32[280]{0:T(512)S(1)}, f32[280]{0:T(512)}, u32[]{:S(2)}) copy-start(f32[280]{0:T(512)} %copy-done.20) | copy-start | bytes 3364
  94.8 6.7 %collective-permute-start.22 = (bf16[280,256]{1,0:T(8,128)(2,1)S(1)}, bf16[280,256]{1,0:T(8,128)(2,1)S(1)}, u32[]{:S(2)}, u32[]{:S(2)}) collective-permute-start(bf16[280,256]{1,0:T(8,128)(2,1)S(1)} %get-tuple-element.44), channel_id=1, source_target_pairs={{0,2},{2,0},{4,6},{6,4},{8,10},{10,8},{12,14},{14,12},{16,18},{18,... | collective-permute-start | bytes 430088 | tf_op jit(solution)/shard_map/ppermute | solution.py:45
  96.1 6.3 %collective-permute-start.23 = (bf16[280,256]{1,0:T(8,128)(2,1)S(1)}, bf16[280,256]{1,0:T(8,128)(2,1)S(1)}, u32[]{:S(2)}, u32[]{:S(2)}) collective-permute-start(bf16[280,256]{1,0:T(8,128)(2,1)S(1)} %get-tuple-element.45), channel_id=1, source_target_pairs={{0,4},{2,6},{4,0},{6,2},{8,12},{10,14},{12,8},{14,10},{16,20},{18,... | collective-permute-start | bytes 430088 | tf_op jit(solution)/shard_map/ppermute | solution.py:45
  96.8 7.7 %collective-permute-start.24 = (bf16[280,256]{1,0:T(8,128)(2,1)S(1)}, bf16[280,256]{1,0:T(8,128)(2,1)S(1)}, u32[]{:S(2)}, u32[]{:S(2)}) collective-permute-start(bf16[280,256]{1,0:T(8,128)(2,1)S(1)} %get-tuple-element.46), channel_id=1, source_target_pairs={{0,6},{2,4},{4,2},{6,0},{8,14},{10,12},{12,10},{14,8},{16,22},{18,... | collective-permute-start | bytes 430088 | tf_op jit(solution)/shard_map/ppermute | solution.py:45
  104.5 9.8 %copy-start.28 = (f32[8]{0:T(128)S(1)}, f32[8]{0:T(128)}, u32[]{:S(2)}) copy-start(f32[8]{0:T(128)} %copy-done.27) | copy-start | bytes 100
  104.5 10.2 %copy-start.13 = (f32[64,256]{1,0:T(8,128)S(1)}, f32[64,256]{1,0:T(8,128)}, u32[]{:S(2)}) copy-start(f32[64,256]{1,0:T(8,128)} %copy-done.12) | copy-start | bytes 196612
  104.5 10.2 %copy-start.15 = (f32[64,256]{1,0:T(8,128)S(1)}, f32[64,256]{1,0:T(8,128)}, u32[]{:S(2)}) copy-start(f32[64,256]{1,0:T(8,128)} %copy-done.14) | copy-start | bytes 196612
  104.5 10.2 %copy-start.17 = (f32[72,256]{1,0:T(8,128)S(1)}, f32[72,256]{1,0:T(8,128)}, u32[]{:S(2)}) copy-start(f32[72,256]{1,0:T(8,128)} %copy-done.16) | copy-start | bytes 221188
  104.7 10.8 %copy-start.4 = (f32[384,256]{1,0:T(8,128)S(1)}, f32[384,256]{1,0:T(8,128)}, u32[]{:S(2)}) copy-start(f32[384,256]{1,0:T(8,128)} %copy-done.3) | copy-start | bytes 1179652
  104.7 10.8 %copy-start.6 = (f32[384,256]{1,0:T(8,128)S(1)}, f32[384,256]{1,0:T(8,128)}, u32[]{:S(2)}) copy-start(f32[384,256]{1,0:T(8,128)} %copy-done.5) | copy-start | bytes 1179652
  104.7 10.8 %copy-start.9 = (f32[768,256]{1,0:T(8,128)S(1)}, f32[768,256]{1,0:T(8,128)}, u32[]{:S(2)}) copy-start(f32[768,256]{1,0:T(8,128)} %get-tuple-element.65) | copy-start | bytes 2359300
  104.8 5.6 %collective-permute-start.25 = (f32[72,256]{1,0:T(8,128)S(1)}, f32[72,256]{1,0:T(8,128)S(1)}, u32[]{:S(2)}, u32[]{:S(2)}) collective-permute-start(f32[72,256]{1,0:T(8,128)S(1)} %get-tuple-element.50), channel_id=1, source_target_pairs={{0,8},{2,10},{4,12},{6,14},{8,0},{10,2},{12,4},{14,6},{16,24},{18,... | collective-permute-start | bytes 221192 | tf_op jit(solution)/shard_map/ppermute | solution.py:45
  104.9 8.2 %collective-permute-start.26 = (f32[72,256]{1,0:T(8,128)S(1)}, f32[72,256]{1,0:T(8,128)S(1)}, u32[]{:S(2)}, u32[]{:S(2)}) collective-permute-start(f32[72,256]{1,0:T(8,128)S(1)} %get-tuple-element.51), channel_id=1, source_target_pairs={{0,16},{2,18},{4,20},{6,22},{8,24},{10,26},{12,28},{14,30},{16,0},... | collective-permute-start | bytes 221192 | tf_op jit(solution)/shard_map/ppermute | solution.py:45
  105.5 7.6 %collective-permute-start.27 = (f32[72,256]{1,0:T(8,128)S(1)}, f32[72,256]{1,0:T(8,128)S(1)}, u32[]{:S(2)}, u32[]{:S(2)}) collective-permute-start(f32[72,256]{1,0:T(8,128)S(1)} %get-tuple-element.52), channel_id=1, source_target_pairs={{0,24},{2,26},{4,28},{6,30},{8,16},{10,18},{12,20},{14,22},{16,8},... | collective-permute-start | bytes 221192 | tf_op jit(solution)/shard_map/ppermute | solution.py:45
  110.3 5.2 %collective-permute-start.29 = (bf16[384,256]{1,0:T(8,128)(2,1)S(1)}, bf16[384,256]{1,0:T(8,128)(2,1)S(1)}, u32[]{:S(2)}, u32[]{:S(2)}) collective-permute-start(bf16[384,256]{1,0:T(8,128)(2,1)S(1)} %slice.350), channel_id=1, source_target_pairs={{0,1},{1,0},{2,3},{3,2},{4,5},{5,4},{6,7},{7,6},{8,9},{9,8},{10,11... | collective-permute-start | bytes 589832 | tf_op jit(solution)/shard_map/ppermute | solution.py:45
  113.1 1.2 %collective-permute-start.28 = (f32[8]{0:T(128)S(1)}, f32[8]{0:T(128)S(1)}, u32[]{:S(2)}, u32[]{:S(2)}) collective-permute-start(f32[8]{0:T(128)S(1)} %slice_bitcast_fusion.10), channel_id=1, source_target_pairs={{0,1},{1,0},{2,3},{3,2},{4,5},{5,4},{6,7},{7,6},{8,9},{9,8},{10,11... | collective-permute-start | bytes 104 | tf_op jit(solution)/shard_map/ppermute | solution.py:45

commit v12 on v11

--- a/solution.py
+++ b/solution.py
@@ -127,6 +127,12 @@
     me = lax.axis_index(axis)
     shape = value.shape
     split = shape[:dim] + (size, shape[dim] // size) + shape[dim + 1 :]
+    if size == 2:
+        parts = value.reshape(split)
+        swapped = jnp.concatenate(
+            [lax.index_in_dim(parts, 1, dim), lax.index_in_dim(parts, 0, dim)], axis=dim
+        )
+        return jnp.where(me == 1, swapped, parts).reshape(shape)
     picked = jnp.take(value.reshape(split), jnp.arange(size) ^ me, axis=dim)
     return picked.reshape(shape)
 
@@ -142,18 +148,25 @@
     place = (row_pick[:, :, None] & col_pick[:, None, :]).astype(jnp.bfloat16)
 
     def build_counts(tiles):
-        tiles_bf = tiles.astype(jnp.bfloat16)
+        me_user = lax.axis_index("user")
+        n_user, _ = bit_count("user")
+        subs = n_user // CB
+        low = me_user & (subs - 1)
+        high = me_user // subs
+        tiles_bf = tiles.astype(jnp.bfloat16).reshape(TMAX, TILE, subs, TILE // subs)
+        tiles_bf = jnp.take(tiles_bf, jnp.arange(subs) ^ low, axis=2).reshape(TMAX, TILE, TILE)
+        moved = jnp.take(place, jnp.arange(CB) ^ high, axis=2)
         counts_bf = jnp.einsum(
-            "trc,tij->ricj", place, tiles_bf, preferred_element_type=jnp.bfloat16
+            "trc,tij->ricj", moved, tiles_bf, preferred_element_type=jnp.bfloat16
         ).reshape(RB * TILE, CB * TILE)
         tile_rows = jnp.sum(tiles_bf, axis=2, dtype=jnp.float32)
         tile_cols = jnp.sum(tiles_bf, axis=1, dtype=jnp.float32)
+        moved_cols = jnp.take(col_pick, jnp.arange(CB) ^ high, axis=1)
         user_deg = jnp.sum(jnp.where(row_pick[:, :, None], tile_rows[:, None, :], 0.0), axis=0)
-        item_deg = jnp.sum(jnp.where(col_pick[:, :, None], tile_cols[:, None, :], 0.0), axis=0)
-        counts_bf = xor_order(xor_order(counts_bf, "item", 0), "user", 1)
+        item_deg = jnp.sum(jnp.where(moved_cols[:, :, None], tile_cols[:, None, :], 0.0), axis=0)
+        counts_bf = xor_order(counts_bf, "item", 0)
         user_deg = xor_order(user_deg.reshape(-1), "item", 0)
-        item_deg = xor_order(item_deg.reshape(-1), "user", 0)
-        return (counts_bf, user_deg, item_deg)
+        return (counts_bf, user_deg, item_deg.reshape(-1))
 
     def cross_parts(user_range, item_range, counts):
         counts_bf, user_deg, item_deg = counts

time: 118 us -> 123 us (1.042)
  local copies, waits for them, and re-layouts: 19.2 us -> 24.9 us
  waiting for transfers between devices: 25.8 us -> 24.2 us
    gather x7 -> x4, local copies, waits for them, and re-layouts: 6.55 us -> 2.01 us  [the longest x2 0.87 us: build_counts(): jnp.take(tiles_bf, jnp.arange(subs) ^ low, axis=2).reshape(TMAX, TILE, TILE)]
    unnamed x65 -> x57, local copies, waits for them, and re-layouts: 1.83 us -> 6.23 us
    select_n x1 -> x2, local copies, waits for them, and re-layouts: 0.07 us -> 3.62 us  [the longest x1 3.51 us: build_counts(): jnp.take(tiles_bf, jnp.arange(subs) ^ low, axis=2).reshape(TMAX, TILE, TILE)]
    convert_element_type x1 -> x2, other arithmetic: 0.34 us -> 2.2 us  [the longest x1 2.19 us: build_counts(): tiles.astype(jnp.bfloat16).reshape(TMAX, TILE, subs, TILE // subs)]
    ppermute x30, waiting for transfers between devices: 25.8 us -> 24.2 us  [swap_with(): return lax.ppermute(value, axis, pairs)]
    reduce_sum x10, local copies, waits for them, and re-layouts: 0.81 us -> 2.15 us  [per_draw(): return jnp.sum(product, axis=(0, 2))]
  transfers between devices with their start and end apart: 30 -> 30, of which waited for: 12 -> 12; matrix products, arithmetic and copies ran while one was open for 32% -> 36% of each run, Pallas kernels for 0% -> 0%
where the time goes in v12:
time: 123 us; the launch traced here: 122 us
  starting transfers between devices  33.5 us (27%)
  other arithmetic  26.1 us (21%)
  local copies, waits for them, and re-layouts  24.9 us (20%)
  waiting for transfers between devices  24.2 us (20%)
  matrix products  11.6 us (9%)
  between operations  2.09 us (2%)
    ppermute x30, starting transfers between devices, swap_with(): return lax.ppermute(value, axis, pairs)  33.5 us
    ppermute x30, waiting for transfers between devices, swap_with(): return lax.ppermute(value, axis, pairs)  24.2 us
    another operation x7, other arithmetic, double_gather(): buf = jnp.stack(pieces, axis=1).reshape((-1,) + piece.shape)  8.15 us
    unnamed x57, local copies, waits for them, and re-layouts  6.23 us
    reduce_sum x14, other arithmetic, per_draw(): return jnp.sum(product, axis=(0, 2))  5.28 us
    dot_general x4, matrix products, prior_term(): mixed = jnp.einsum('nde,ef->ndf', grouped, prior_mat, precision=top_prec)  4.21 us
    select_n x1, local copies, waits for them, and re-layouts, build_counts(): jnp.take(tiles_bf, jnp.arange(subs) ^ low, axis=2).reshape(TMAX, TILE, TILE)  3.51 us
    dot_general x2, matrix products, cross_parts(): lax.dot_general(counts_bf, user_range, (((0,), (0,)), ((), ())), preferre...  3.46 us
  transfers between devices with their start and end apart: 30, of which 12 were waited for; matrix products, arithmetic and copies ran while one was open for 36% of the time, Pallas kernels for 0%

profile of v12, /device:TPU:0, one launch (start us, length us, event | category | flops | bytes accessed | tf_op | source)
XLA Modules:
  0.0 122.3 jit_solution(16054818674210524624)
XLA Ops:
  0.7 0.9 multiply_reduce_fusion.7
  1.6 5.1 %collective-permute-start.2 = (bf16[1,64,256]{2,1,0:T(8,128)(2,1)S(1)}, bf16[1,64,256]{2,1,0:T(8,128)(2,1)S(1)}, u32[]{:S(2)}, u32[]{:S(2)}) collective-permute-start(bf16[1,64,256]{2,1,0:T(8,128)(2,1)S(1)} %get-tuple-element.45), channel_id=1, source_target_pairs={{0,24},{2,26},{4,28},{6,30},{8,16},{10,18},{12,20},{14,22},{16,8},... | collective-permute-start | bytes 98312 | tf_op jit(solution)/shard_map/ppermute | solution.py:45
  7.4 1.2 multiply_reduce_fusion.3
  8.7 1.0 squeeze.84
  9.6 1.2 copy.95
  13.5 0.9 multiply_reduce_fusion.4
  14.4 1.8 %multiply_reduce_fusion.2 = (f32[4]{0:T(128)}, f32[384,4,64]{0,2,1:T(8,128)}) fusion(f32[384,4,64]{0,2,1:T(8,128)S(1)} %bitcast.194, f32[64,64]{1,0:T(8,128)S(1)} %copy-done), kind=kOutput, calls=%fused_computation.54 | convolution fusion | flops 75694080 | bytes 802832 | tf_op jit(solution)/shard_map/nde,ef->ndf/dot_general | solution.py:22
  17.3 3.5 %copy.87 = s32[1,1,12,256,256]{3,4,2,1,0:T(8,128)} copy(s32[1,1,12,256,256]{4,3,2,1,0:T(8,128)} %param.11) | data formatting | bytes 6291456 | tf_op args[4]
  22.1 2.2 %convert_element_type.173 = bf16[12,256,256]{1,2,0:T(8,128)(2,1)S(1)} convert(s32[12,256,256]{1,2,0:T(8,128)} %bitcast.187) | non-fusion elementwise | flops 786432 | bytes 4718592 | tf_op jit(solution)/shard_map/convert_element_type | solution.py:156
  24.3 0.8 gather_fusion
  25.1 1.4 %convert_reduce_fusion.1 = (f32[12,4,64]{2,0,1:T(8,128)}, f32[12,256]{1,0:T(8,128)S(1)}) fusion(pred[4]{0:T(512)(128)(4,1)S(1)} %copy-done.24, bf16[4,12,256,64]{2,3,1,0:T(8,128)(2,1)S(1)} %gather_fusion), kind=kLoop, calls=%fused_computation.4 | loop fusion | flops 3139584 | bytes 1597444 | tf_op jit(solution)/shard_map/reduce_sum | solution.py:163
  26.6 2.7 %collective-permute-start.6 = (bf16[4,64,256]{2,1,0:T(8,128)(2,1)}, bf16[4,64,256]{2,1,0:T(8,128)(2,1)}, u32[]{:S(2)}, u32[]{:S(2)}) collective-permute-start(bf16[4,64,256]{2,1,0:T(8,128)(2,1)} %maximum_bitcast_fusion), channel_id=1, source_target_pairs={{0,6},{2,4},{4,2},{6,0},{8,14},{10,12},{12,10},{14,8},{16,22},{18,... | collective-permute-start | bytes 393224 | tf_op jit(solution)/shard_map/ppermute | solution.py:45
  30.7 1.5 %bitcast_select_fusion = bf16[12,256,256]{1,2,0:T(8,128)(2,1)} fusion(bf16[12,256,4,64]{1,3,2,0:T(8,128)(2,1)S(1)} %copy.88, pred[256]{0:T(512)(128)(4,1)S(1)} %copy-done.25), kind=kLoop, calls=%fused_computation.6 | loop fusion | flops 786432 | bytes 3145984 | tf_op jit(solution)/shard_map/jit(_take)/select_n | solution.py:157
  32.2 3.5 %copy.108 = bf16[12,256,256,1]{2,0,3,1:T(8,128)(2,1)S(1)} copy(bf16[12,256,256,1]{1,2,0,3:T(8,128)(2,1)} %bitcast.188) | data formatting | bytes 3145728 | tf_op jit(solution)/shard_map/jit(_take)/select_n | solution.py:157
  35.8 0.9 convolution_bitcast_fusion
  37.3 1.3 %reshape_reshape.20 = bf16[2,384,1024]{2,1,0:T(8,128)(2,1)S(1)} reshape(bf16[3,256,4,256]{3,2,1,0:T(4,128)(2,1)S(1)} %copy.91) | data formatting | bytes 3145728 | tf_op jit(solution)/shard_map/reshape;reshape | solution.py:131
  39.7 1.2 pad_maximum_fusion
  40.9 1.0 pad_maximum_fusion.2
  41.9 1.5 %fusion.2 = (f32[256]{0:T(256)S(1)}, f32[768,256]{1,0:T(8,128)}) fusion(bf16[1,2,384,256]{3,2,1,0:T(8,128)(2,1)S(1)} %pad_maximum_fusion.2, bf16[768,256]{1,0:T(8,128)(2,1)S(1)} %bitcast.216, f32[768]{0:T(1024)S(1)} %broadcast_select_fusion.1, bf16[768,1024]{1,0:T(8,128)(2,1)S(1)} %bitcast.189, bf16[1024,256]{1,0:T(8,128)(2,1)S(1)} %bitcast.210), kind=kOutput, calls=%fused_computation.23 | convolution fusion | flops 403832576 | bytes 3674112 | tf_op jit(solution)/shard_map/dot_general | solution.py:173
  43.6 1.7 %fusion = (f32[256]{0:T(256)S(1)}, f32[1024,256]{1,0:T(8,128)S(1)}) fusion(bf16[4,4,64,256]{3,2,1,0:T(8,128)(2,1)S(1)} %copy.94, bf16[1024,256]{1,0:T(8,128)(2,1)S(1)} %bitcast.211, f32[1024]{0:T(1024)S(1)} %bitcast.225, bf16[768,1024]{1,0:T(8,128)(2,1)S(1)} %bitcast.190, bf16[768,256]{1,0:T(8,128)(2,1)} %bitcast.217), kind=kOutput, calls=%fused_computation.17 | convolution fusion | flops 404225792 | bytes 4068352 | tf_op jit(solution)/shard_map/dot_general | solution.py:175
  45.9 1.7 %collective-permute-start.7 = (bf16[280,256]{1,0:T(8,128)(2,1)S(1)}, bf16[280,256]{1,0:T(8,128)(2,1)S(1)}, u32[]{:S(2)}, u32[]{:S(2)}) collective-permute-start(bf16[280,256]{1,0:T(8,128)(2,1)S(1)} %get-tuple-element.49), channel_id=1, source_target_pairs={{0,2},{2,0},{4,6},{6,4},{8,10},{10,8},{12,14},{14,12},{16,18},{18,... | collective-permute-start | bytes 430088 | tf_op jit(solution)/shard_map/ppermute | solution.py:45
  47.6 1.5 %collective-permute-start.8 = (bf16[280,256]{1,0:T(8,128)(2,1)S(1)}, bf16[280,256]{1,0:T(8,128)(2,1)S(1)}, u32[]{:S(2)}, u32[]{:S(2)}) collective-permute-start(bf16[280,256]{1,0:T(8,128)(2,1)S(1)} %get-tuple-element.50), channel_id=1, source_target_pairs={{0,4},{2,6},{4,0},{6,2},{8,12},{10,14},{12,8},{14,10},{16,20},{18,... | collective-permute-start | bytes 430088 | tf_op jit(solution)/shard_map/ppermute | solution.py:45
  49.6 2.3 %collective-permute-done.7 = bf16[280,256]{1,0:T(8,128)(2,1)S(1)} collective-permute-done((bf16[280,256]{1,0:T(8,128)(2,1)S(1)}, bf16[280,256]{1,0:T(8,128)(2,1)S(1)}, u32[]{:S(2)}, u32[]{:S(2)}) %collective-permute-start.7) | collective-permute-done | bytes 143392 | tf_op jit(solution)/shard_map/ppermute | solution.py:45
  51.8 4.0 %collective-permute-done.8 = bf16[280,256]{1,0:T(8,128)(2,1)S(1)} collective-permute-done((bf16[280,256]{1,0:T(8,128)(2,1)S(1)}, bf16[280,256]{1,0:T(8,128)(2,1)S(1)}, u32[]{:S(2)}, u32[]{:S(2)}) %collective-permute-start.8) | collective-permute-done | bytes 143392 | tf_op jit(solution)/shard_map/ppermute | solution.py:45
  56.7 1.2 %collective-permute-start.10 = (f32[72,256]{1,0:T(8,128)}, f32[72,256]{1,0:T(8,128)S(1)}, u32[]{:S(2)}, u32[]{:S(2)}) collective-permute-start(f32[72,256]{1,0:T(8,128)} %get-tuple-element.55), channel_id=1, source_target_pairs={{0,8},{2,10},{4,12},{6,14},{8,0},{10,2},{12,4},{14,6},{16,24},{18,... | collective-permute-start | bytes 221192 | tf_op jit(solution)/shard_map/ppermute | solution.py:45
  57.9 2.9 %collective-permute-start.11 = (f32[72,256]{1,0:T(8,128)}, f32[72,256]{1,0:T(8,128)S(1)}, u32[]{:S(2)}, u32[]{:S(2)}) collective-permute-start(f32[72,256]{1,0:T(8,128)} %get-tuple-element.56), channel_id=1, source_target_pairs={{0,16},{2,18},{4,20},{6,22},{8,24},{10,26},{12,28},{14,30},{16,0},... | collective-permute-start | bytes 221192 | tf_op jit(solution)/shard_map/ppermute | solution.py:45
  61.5 1.0 slice.369
  62.6 2.4 %collective-permute-done.11 = f32[72,256]{1,0:T(8,128)S(1)} collective-permute-done((f32[72,256]{1,0:T(8,128)}, f32[72,256]{1,0:T(8,128)S(1)}, u32[]{:S(2)}, u32[]{:S(2)}) %collective-permute-start.11) | collective-permute-done | bytes 73760 | tf_op jit(solution)/shard_map/ppermute | solution.py:45
  65.0 2.1 %collective-permute-done.12 = f32[72,256]{1,0:T(8,128)} collective-permute-done((f32[72,256]{1,0:T(8,128)S(1)}, f32[72,256]{1,0:T(8,128)}, u32[]{:S(2)}, u32[]{:S(2)}) %collective-permute-start.12) | collective-permute-done | bytes 73760 | tf_op jit(solution)/shard_map/ppermute | solution.py:45
  67.1 0.9 fusion.31
  68.1 1.1 collective-permute-done.13
  71.1 1.2 multiply_reduce_fusion.6
  72.3 1.1 collective-permute-start.18
  73.5 3.2 %collective-permute-start.16 = (bf16[1,64,256]{2,1,0:T(8,128)(2,1)}, bf16[1,64,256]{2,1,0:T(8,128)(2,1)}, u32[]{:S(2)}, u32[]{:S(2)}) collective-permute-start(bf16[1,64,256]{2,1,0:T(8,128)(2,1)} %get-tuple-element.43), channel_id=1, source_target_pairs={{0,8},{2,10},{4,12},{6,14},{8,0},{10,2},{12,4},{14,6},{16,24},{18,... | collective-permute-start | bytes 98312 | tf_op jit(solution)/shard_map/ppermute | solution.py:45
  76.7 1.8 %convert_bitcast_fusion.1 = (bf16[1,1,384,256]{3,2,1,0:T(8,128)(2,1)}, f32[384,256]{1,0:T(8,128)S(1)}) fusion(f32[384,256]{1,0:T(8,128)S(1)} %copy.99, bf16[384,256]{1,0:T(8,128)(2,1)S(1)} %collective-permute-done.14, f32[768,256]{1,0:T(8,128)} %get-tuple-element.69, f32[256]{0:T(256)S(1)} %mul.195, f32[1,384,256]{2,1,0:T(8,128)S(1)} %copy-done.1), kind=kLoop, calls=%fused_computation.100 | loop fusion | flops 688128 | bytes 1967104 | tf_op jit(solution)/shard_map/stack;broadcast_in_dim | solution.py:118
  78.7 1.3 %fusion.44 = f32[384,4,64]{0,2,1:T(8,128)} fusion(f32[384,4,64]{0,2,1:T(8,128)S(1)} %bitcast.196, f32[64,64]{1,0:T(8,128)S(1)} %copy-done), kind=kOutput, calls=%fused_computation.137 | convolution fusion | flops 75497472 | bytes 802816 | tf_op jit(solution)/shard_map/nde,ef->ndf/dot_general | solution.py:22
  79.9 1.2 copy.104
  81.2 1.5 %fusion.49 = (bf16[4,1,64,256]{3,2,0,1:T(8,128)(2,1)}, bf16[4,64,256]{2,1,0:T(8,128)(2,1)}) fusion(bf16[1,1,64,256]{3,2,1,0:T(8,128)(2,1)} %bitcast.56, bf16[1,1,64,256]{3,2,1,0:T(8,128)(2,1)} %bitcast.55, bf16[1,1,64,256]{3,2,1,0:T(8,128)(2,1)} %bitcast.54, bf16[1,1,64,256]{3,2,1,0:T(8,128)(2,1)S(1)} %copy-done.15), kind=kLoop, calls=%fused_computation.142 | loop fusion | flops 196608 | bytes 393216 | tf_op jit(solution)/shard_map/stack;reshape | solution.py:118
  82.7 1.4 %collective-permute-start.21 = (bf16[4,64,256]{2,1,0:T(8,128)(2,1)}, bf16[4,64,256]{2,1,0:T(8,128)(2,1)}, u32[]{:S(2)}, u32[]{:S(2)}) collective-permute-start(bf16[4,64,256]{2,1,0:T(8,128)(2,1)} %get-tuple-element.40), channel_id=1, source_target_pairs={{0,6},{2,4},{4,2},{6,0},{8,14},{10,12},{12,10},{14,8},{16,22},{18,... | collective-permute-start | bytes 393224 | tf_op jit(solution)/shard_map/ppermute | solution.py:45
  84.1 1.2 collective-permute-start.20
  85.3 0.9 collective-permute-start.19
  86.2 0.7 multiply_reduce_fusion.1
  86.9 0.7 reduce_sum.236
  87.8 0.8 reduce_sum.242
  89.1 1.0 collective-permute-done.21
  90.1 1.4 %collective-permute-done.20 = bf16[4,64,256]{2,1,0:T(8,128)(2,1)} collective-permute-done((bf16[4,64,256]{2,1,0:T(8,128)(2,1)}, bf16[4,64,256]{2,1,0:T(8,128)(2,1)}, u32[]{:S(2)}, u32[]{:S(2)}) %collective-permute-start.20) | collective-permute-done | bytes 131104 | tf_op jit(solution)/shard_map/ppermute | solution.py:45
  91.5 1.2 pad_maximum_fusion.1
  92.7 1.0 pad_maximum_fusion.3
  93.7 1.5 %fusion.3 = (f32[256]{0:T(256)S(1)}, f32[768,256]{1,0:T(8,128)}) fusion(bf16[1,2,384,256]{3,2,1,0:T(8,128)(2,1)S(1)} %pad_maximum_fusion.3, bf16[768,256]{1,0:T(8,128)(2,1)S(1)} %bitcast.218, f32[768]{0:T(1024)S(1)} %broadcast_select_fusion.1, bf16[768,1024]{1,0:T(8,128)(2,1)S(1)} %bitcast.191, bf16[1024,256]{1,0:T(8,128)(2,1)S(1)} %bitcast.208), kind=kOutput, calls=%fused_computation.24 | convolution fusion | flops 403832576 | bytes 3674112 | tf_op jit(solution)/shard_map/dot_general | solution.py:173
  95.1 1.7 %fusion.1 = (f32[256]{0:T(256)S(1)}, f32[1024,256]{1,0:T(8,128)}) fusion(bf16[4,4,64,256]{3,2,1,0:T(8,128)(2,1)S(1)} %copy.101, bf16[1024,256]{1,0:T(8,128)(2,1)S(1)} %bitcast.209, f32[1024]{0:T(1024)S(1)} %bitcast.226, bf16[768,1024]{1,0:T(8,128)(2,1)S(1)} %bitcast.192, bf16[768,256]{1,0:T(8,128)(2,1)S(1)} %bitcast.219), kind=kOutput, calls=%fused_computation.18 | convolution fusion | flops 404225792 | bytes 4068352 | tf_op jit(solution)/shard_map/dot_general | solution.py:175
  97.4 1.1 fusion.21
  98.4 1.1 slice_bitcast_fusion
  99.6 1.2 collective-permute-start.22
  100.8 0.8 collective-permute-start.23
  101.6 1.5 %collective-permute-start.24 = (bf16[280,256]{1,0:T(8,128)(2,1)S(1)}, bf16[280,256]{1,0:T(8,128)(2,1)S(1)}, u32[]{:S(2)}, u32[]{:S(2)}) collective-permute-start(bf16[280,256]{1,0:T(8,128)(2,1)S(1)} %get-tuple-element.48), channel_id=1, source_target_pairs={{0,6},{2,4},{4,2},{6,0},{8,14},{10,12},{12,10},{14,8},{16,22},{18,... | collective-permute-start | bytes 430088 | tf_op jit(solution)/shard_map/ppermute | solution.py:45
  103.2 2.9 %collective-permute-done.22 = bf16[280,256]{1,0:T(8,128)(2,1)S(1)} collective-permute-done((bf16[280,256]{1,0:T(8,128)(2,1)S(1)}, bf16[280,256]{1,0:T(8,128)(2,1)S(1)}, u32[]{:S(2)}, u32[]{:S(2)}) %collective-permute-start.22) | collective-permute-done | bytes 143392 | tf_op jit(solution)/shard_map/ppermute | solution.py:45
  106.1 1.2 %collective-permute-done.23 = bf16[280,256]{1,0:T(8,128)(2,1)S(1)} collective-permute-done((bf16[280,256]{1,0:T(8,128)(2,1)S(1)}, bf16[280,256]{1,0:T(8,128)(2,1)S(1)}, u32[]{:S(2)}, u32[]{:S(2)}) %collective-permute-start.23) | collective-permute-done | bytes 143392 | tf_op jit(solution)/shard_map/ppermute | solution.py:45
  107.4 1.6 %collective-permute-done.24 = bf16[280,256]{1,0:T(8,128)(2,1)S(1)} collective-permute-done((bf16[280,256]{1,0:T(8,128)(2,1)S(1)}, bf16[280,256]{1,0:T(8,128)(2,1)S(1)}, u32[]{:S(2)}, u32[]{:S(2)}) %collective-permute-start.24) | collective-permute-done | bytes 143392 | tf_op jit(solution)/shard_map/ppermute | solution.py:45
  109.9 1.1 collective-permute-start.26
  111.0 2.7 %collective-permute-start.27 = (f32[72,256]{1,0:T(8,128)S(1)}, f32[72,256]{1,0:T(8,128)S(1)}, u32[]{:S(2)}, u32[]{:S(2)}) collective-permute-start(f32[72,256]{1,0:T(8,128)S(1)} %get-tuple-element.54), channel_id=1, source_target_pairs={{0,24},{2,26},{4,28},{6,30},{8,16},{10,18},{12,20},{14,22},{16,8},... | collective-permute-start | bytes 221192 | tf_op jit(solution)/shard_map/ppermute | solution.py:45
  113.7 1.0 slice.368
  114.8 3.0 %collective-permute-done.26 = f32[72,256]{1,0:T(8,128)S(1)} collective-permute-done((f32[72,256]{1,0:T(8,128)S(1)}, f32[72,256]{1,0:T(8,128)S(1)}, u32[]{:S(2)}, u32[]{:S(2)}) %collective-permute-start.26) | collective-permute-done | bytes 73760 | tf_op jit(solution)/shard_map/ppermute | solution.py:45
  117.9 1.1 collective-permute-done.28
  120.1 2.1 %fusion.9 = (f32[1,384,256]{2,1,0:T(8,128)}, f32[1,384,256]{2,1,0:T(8,128)}) fusion(f32[384,256]{1,0:T(8,128)S(1)} %get-tuple-element.17, f32[384,256]{1,0:T(8,128)S(1)} %copy.104, f32[768,256]{1,0:T(8,128)} %get-tuple-element.77, bf16[384,256]{1,0:T(8,128)(2,1)S(1)} %collective-permute-done.29, f32[256]{0:T(256)S(1)} %mul.215, f32[256]{0:T(256)S(1)} %mul.213, ...), kind=kLoop, calls=%fused_computation.38 | loop fusion | flops 1671168 | bytes 3542016 | tf_op jit(solution)/shard_map/broadcast_in_dim | solution.py:236
  (195 shorter events, 16.6 us)
Async XLA Ops:
  0.6 13.7 %copy-start = (f32[64,64]{1,0:T(8,128)S(1)}, f32[64,64]{1,0:T(8,128)}, u32[]{:S(2)}) copy-start(f32[64,64]{1,0:T(8,128)} %param.9) | copy-start | bytes 49156
  0.6 10.8 %copy-start.22 = (s32[1,1,12,2]{2,3,1,0:T(2,128)S(1)}, s32[1,1,12,2]{2,3,1,0:T(2,128)}, u32[]{:S(2)}) copy-start(s32[1,1,12,2]{2,3,1,0:T(2,128)} %param.12) | copy-start | bytes 292
  0.7 12.8 %copy-start.13 = (f32[64,64]{1,0:T(8,128)S(1)}, f32[64,64]{1,0:T(8,128)}, u32[]{:S(2)}) copy-start(f32[64,64]{1,0:T(8,128)} %param.10) | copy-start | bytes 49156
  1.6 19.8 %collective-permute-start.2 = (bf16[1,64,256]{2,1,0:T(8,128)(2,1)S(1)}, bf16[1,64,256]{2,1,0:T(8,128)(2,1)S(1)}, u32[]{:S(2)}, u32[]{:S(2)}) collective-permute-start(bf16[1,64,256]{2,1,0:T(8,128)(2,1)S(1)} %get-tuple-element.45), channel_id=1, source_target_pairs={{0,24},{2,26},{4,28},{6,30},{8,16},{10,18},{12,20},{14,22},{16,8},... | collective-permute-start | bytes 98312 | tf_op jit(solution)/shard_map/ppermute | solution.py:45
  6.7 14.7 %collective-permute-start.1 = (bf16[1,64,256]{2,1,0:T(8,128)(2,1)S(1)}, bf16[1,64,256]{2,1,0:T(8,128)(2,1)S(1)}, u32[]{:S(2)}, u32[]{:S(2)}) collective-permute-start(bf16[1,64,256]{2,1,0:T(8,128)(2,1)S(1)} %get-tuple-element.45), channel_id=1, source_target_pairs={{0,16},{2,18},{4,20},{6,22},{8,24},{10,26},{12,28},{14,30},{16,0},... | collective-permute-start | bytes 98312 | tf_op jit(solution)/shard_map/ppermute | solution.py:45
  6.7 14.7 %collective-permute-start = (bf16[1,64,256]{2,1,0:T(8,128)(2,1)S(1)}, bf16[1,64,256]{2,1,0:T(8,128)(2,1)S(1)}, u32[]{:S(2)}, u32[]{:S(2)}) collective-permute-start(bf16[1,64,256]{2,1,0:T(8,128)(2,1)S(1)} %get-tuple-element.45), channel_id=1, source_target_pairs={{0,8},{2,10},{4,12},{6,14},{8,0},{10,2},{12,4},{14,6},{16,24},{18,... | collective-permute-start | bytes 98312 | tf_op jit(solution)/shard_map/ppermute | solution.py:45
  8.6 32.4 %collective-permute-start.3 = (bf16[1,384,256]{2,1,0:T(8,128)(2,1)S(1)}, bf16[1,384,256]{2,1,0:T(8,128)(2,1)}, u32[]{:S(2)}, u32[]{:S(2)}) collective-permute-start(bf16[1,384,256]{2,1,0:T(8,128)(2,1)S(1)} %get-tuple-element.26), channel_id=1, source_target_pairs={{0,1},{1,0},{2,3},{3,2},{4,5},{5,4},{6,7},{7,6},{8,9},{9,8},{10,11... | collective-permute-start | bytes 589832 | tf_op jit(solution)/shard_map/ppermute | solution.py:45
  11.5 5.4 %copy-start.19 = (pred[12,3]{0,1:T(4,128)(4,1)}, pred[12,3]{0,1:T(4,128)(4,1)S(1)}, u32[]{:S(2)}) copy-start(pred[12,3]{0,1:T(4,128)(4,1)S(1)} %fusion.54) | copy-start | bytes 112
  16.2 4.7 %copy-start.23 = (pred[4]{0:T(512)(128)(4,1)}, pred[4]{0:T(512)(128)(4,1)S(1)}, u32[]{:S(2)}) copy-start(pred[4]{0:T(512)(128)(4,1)S(1)} %compare_and_fusion.1) | copy-start | bytes 16
  24.3 0.8 copy-start.24
  25.1 1.4 %copy-start.20 = (pred[12,3]{0,1:T(4,128)(4,1)S(1)}, pred[12,3]{0,1:T(4,128)(4,1)}, u32[]{:S(2)}) copy-start(pred[12,3]{0,1:T(4,128)(4,1)} %copy-done.19) | copy-start | bytes 112
  26.6 13.1 %collective-permute-start.6 = (bf16[4,64,256]{2,1,0:T(8,128)(2,1)}, bf16[4,64,256]{2,1,0:T(8,128)(2,1)}, u32[]{:S(2)}, u32[]{:S(2)}) collective-permute-start(bf16[4,64,256]{2,1,0:T(8,128)(2,1)} %maximum_bitcast_fusion), channel_id=1, source_target_pairs={{0,6},{2,4},{4,2},{6,0},{8,14},{10,12},{12,10},{14,8},{16,22},{18,... | collective-permute-start | bytes 393224 | tf_op jit(solution)/shard_map/ppermute | solution.py:45
  29.2 10.5 %collective-permute-start.5 = (bf16[4,64,256]{2,1,0:T(8,128)(2,1)}, bf16[4,64,256]{2,1,0:T(8,128)(2,1)}, u32[]{:S(2)}, u32[]{:S(2)}) collective-permute-start(bf16[4,64,256]{2,1,0:T(8,128)(2,1)} %maximum_bitcast_fusion), channel_id=1, source_target_pairs={{0,4},{2,6},{4,0},{6,2},{8,12},{10,14},{12,8},{14,10},{16,20},{18,... | collective-permute-start | bytes 393224 | tf_op jit(solution)/shard_map/ppermute | solution.py:45
  29.7 10.0 %collective-permute-start.4 = (bf16[4,64,256]{2,1,0:T(8,128)(2,1)}, bf16[4,64,256]{2,1,0:T(8,128)(2,1)}, u32[]{:S(2)}, u32[]{:S(2)}) collective-permute-start(bf16[4,64,256]{2,1,0:T(8,128)(2,1)} %maximum_bitcast_fusion), channel_id=1, source_target_pairs={{0,2},{2,0},{4,6},{6,4},{8,10},{10,8},{12,14},{14,12},{16,18},{18,... | collective-permute-start | bytes 393224 | tf_op jit(solution)/shard_map/ppermute | solution.py:45
  30.1 0.6 copy-start.25
  38.7 0.8 copy-start.14
  41.9 1.5 %copy-start.12 = (bf16[1,2,384,256]{3,2,1,0:T(8,128)(2,1)}, bf16[1,2,384,256]{3,2,1,0:T(8,128)(2,1)S(1)}, u32[]{:S(2)}) copy-start(bf16[1,2,384,256]{3,2,1,0:T(8,128)(2,1)S(1)} %pad_maximum_fusion.2) | copy-start | bytes 1179652
  43.6 2.0 %copy-start.16 = (f32[4]{0:T(128)S(1)}, f32[4]{0:T(128)}, u32[]{:S(2)}) copy-start(f32[4]{0:T(128)} %get-tuple-element.74) | copy-start | bytes 52
  43.6 2.0 %copy-start.21 = (f32[4]{0:T(128)S(1)}, f32[4]{0:T(128)}, u32[]{:S(2)}) copy-start(f32[4]{0:T(128)} %get-tuple-element.72) | copy-start | bytes 52
  43.6 2.0 %copy-start.26 = (f32[4]{0:T(128)S(1)}, f32[4]{0:T(128)}, u32[]{:S(2)}) copy-start(f32[4]{0:T(128)} %add.168) | copy-start | bytes 52
  45.9 5.9 %collective-permute-start.7 = (bf16[280,256]{1,0:T(8,128)(2,1)S(1)}, bf16[280,256]{1,0:T(8,128)(2,1)S(1)}, u32[]{:S(2)}, u32[]{:S(2)}) collective-permute-start(bf16[280,256]{1,0:T(8,128)(2,1)S(1)} %get-tuple-element.49), channel_id=1, source_target_pairs={{0,2},{2,0},{4,6},{6,4},{8,10},{10,8},{12,14},{14,12},{16,18},{18,... | collective-permute-start | bytes 430088 | tf_op jit(solution)/shard_map/ppermute | solution.py:45
  47.6 8.2 %collective-permute-start.8 = (bf16[280,256]{1,0:T(8,128)(2,1)S(1)}, bf16[280,256]{1,0:T(8,128)(2,1)S(1)}, u32[]{:S(2)}, u32[]{:S(2)}) collective-permute-start(bf16[280,256]{1,0:T(8,128)(2,1)S(1)} %get-tuple-element.50), channel_id=1, source_target_pairs={{0,4},{2,6},{4,0},{6,2},{8,12},{10,14},{12,8},{14,10},{16,20},{18,... | collective-permute-start | bytes 430088 | tf_op jit(solution)/shard_map/ppermute | solution.py:45
  49.1 6.6 %collective-permute-start.9 = (bf16[280,256]{1,0:T(8,128)(2,1)S(1)}, bf16[280,256]{1,0:T(8,128)(2,1)S(1)}, u32[]{:S(2)}, u32[]{:S(2)}) collective-permute-start(bf16[280,256]{1,0:T(8,128)(2,1)S(1)} %get-tuple-element.51), channel_id=1, source_target_pairs={{0,6},{2,4},{4,2},{6,0},{8,14},{10,12},{12,10},{14,8},{16,22},{18,... | collective-permute-start | bytes 430088 | tf_op jit(solution)/shard_map/ppermute | solution.py:45
  49.6 11.7 %copy-start.2 = (f32[384,4,64]{0,2,1:T(8,128)S(1)}, f32[384,4,64]{0,2,1:T(8,128)}, u32[]{:S(2)}) copy-start(f32[384,4,64]{0,2,1:T(8,128)} %get-tuple-element.73) | copy-start | bytes 1179652
  56.0 13.9 %copy-start.4 = (f32[1,64,256]{2,1,0:T(8,128)S(1)}, f32[1,64,256]{2,1,0:T(8,128)}, u32[]{:S(2)}) copy-start(f32[1,64,256]{2,1,0:T(8,128)} %param.8) | copy-start | bytes 196612
  56.7 5.9 %collective-permute-start.10 = (f32[72,256]{1,0:T(8,128)}, f32[72,256]{1,0:T(8,128)S(1)}, u32[]{:S(2)}, u32[]{:S(2)}) collective-permute-start(f32[72,256]{1,0:T(8,128)} %get-tuple-element.55), channel_id=1, source_target_pairs={{0,8},{2,10},{4,12},{6,14},{8,0},{10,2},{12,4},{14,6},{16,24},{18,... | collective-permute-start | bytes 221192 | tf_op jit(solution)/shard_map/ppermute | solution.py:45
  57.9 7.0 %collective-permute-start.11 = (f32[72,256]{1,0:T(8,128)}, f32[72,256]{1,0:T(8,128)S(1)}, u32[]{:S(2)}, u32[]{:S(2)}) collective-permute-start(f32[72,256]{1,0:T(8,128)} %get-tuple-element.56), channel_id=1, source_target_pairs={{0,16},{2,18},{4,20},{6,22},{8,24},{10,26},{12,28},{14,30},{16,0},... | collective-permute-start | bytes 221192 | tf_op jit(solution)/shard_map/ppermute | solution.py:45
  60.8 6.3 %collective-permute-start.12 = (f32[72,256]{1,0:T(8,128)S(1)}, f32[72,256]{1,0:T(8,128)}, u32[]{:S(2)}, u32[]{:S(2)}) collective-permute-start(f32[72,256]{1,0:T(8,128)S(1)} %get-tuple-element.57), channel_id=1, source_target_pairs={{0,24},{2,26},{4,28},{6,30},{8,16},{10,18},{12,20},{14,22},{16,8},... | collective-permute-start | bytes 221192 | tf_op jit(solution)/shard_map/ppermute | solution.py:45
  61.1 15.6 %copy-start.1 = (f32[1,384,256]{2,1,0:T(8,128)S(1)}, f32[1,384,256]{2,1,0:T(8,128)}, u32[]{:S(2)}) copy-start(f32[1,384,256]{2,1,0:T(8,128)} %param.7) | copy-start | bytes 1179652
  61.3 17.2 %copy-start.6 = (f32[64,256]{1,0:T(8,128)}, f32[64,256]{1,0:T(8,128)S(1)}, u32[]{:S(2)}) copy-start(f32[64,256]{1,0:T(8,128)S(1)} %reshape.345) | copy-start | bytes 196612
  62.5 14.2 %collective-permute-start.14 = (bf16[384,256]{1,0:T(8,128)(2,1)S(1)}, bf16[384,256]{1,0:T(8,128)(2,1)S(1)}, u32[]{:S(2)}, u32[]{:S(2)}) collective-permute-start(bf16[384,256]{1,0:T(8,128)(2,1)S(1)} %slice.369), channel_id=1, source_target_pairs={{0,1},{1,0},{2,3},{3,2},{4,5},{5,4},{6,7},{7,6},{8,9},{9,8},{10,11... | collective-permute-start | bytes 589832 | tf_op jit(solution)/shard_map/ppermute | solution.py:45
  68.0 2.9 %copy-start.10 = (f32[72,256]{1,0:T(8,128)}, f32[72,256]{1,0:T(8,128)S(1)}, u32[]{:S(2)}) copy-start(f32[72,256]{1,0:T(8,128)S(1)} %fusion.31) | copy-start | bytes 221188
  68.0 1.2 collective-permute-start.13
  69.2 0.5 copy-start.17
  71.1 7.4 %copy-start.8 = (f32[64,256]{1,0:T(8,128)}, f32[64,256]{1,0:T(8,128)S(1)}, u32[]{:S(2)}) copy-start(f32[64,256]{1,0:T(8,128)S(1)} %reshape.351) | copy-start | bytes 196612
  72.3 8.8 %collective-permute-start.18 = (bf16[1,64,256]{2,1,0:T(8,128)(2,1)}, bf16[1,64,256]{2,1,0:T(8,128)(2,1)}, u32[]{:S(2)}, u32[]{:S(2)}) collective-permute-start(bf16[1,64,256]{2,1,0:T(8,128)(2,1)} %get-tuple-element.43), channel_id=1, source_target_pairs={{0,24},{2,26},{4,28},{6,30},{8,16},{10,18},{12,20},{14,22},{16,8},... | collective-permute-start | bytes 98312 | tf_op jit(solution)/shard_map/ppermute | solution.py:45
  73.5 7.6 %collective-permute-start.17 = (bf16[1,64,256]{2,1,0:T(8,128)(2,1)}, bf16[1,64,256]{2,1,0:T(8,128)(2,1)}, u32[]{:S(2)}, u32[]{:S(2)}) collective-permute-start(bf16[1,64,256]{2,1,0:T(8,128)(2,1)} %get-tuple-element.43), channel_id=1, source_target_pairs={{0,16},{2,18},{4,20},{6,22},{8,24},{10,26},{12,28},{14,30},{16,0},... | collective-permute-start | bytes 98312 | tf_op jit(solution)/shard_map/ppermute | solution.py:45
  73.5 7.7 %collective-permute-start.16 = (bf16[1,64,256]{2,1,0:T(8,128)(2,1)}, bf16[1,64,256]{2,1,0:T(8,128)(2,1)}, u32[]{:S(2)}, u32[]{:S(2)}) collective-permute-start(bf16[1,64,256]{2,1,0:T(8,128)(2,1)} %get-tuple-element.43), channel_id=1, source_target_pairs={{0,8},{2,10},{4,12},{6,14},{8,0},{10,2},{12,4},{14,6},{16,24},{18,... | collective-permute-start | bytes 98312 | tf_op jit(solution)/shard_map/ppermute | solution.py:45
  78.5 2.6 %copy-start.15 = (bf16[1,1,64,256]{3,2,1,0:T(8,128)(2,1)S(1)}, bf16[1,1,64,256]{3,2,1,0:T(8,128)(2,1)}, u32[]{:S(2)}) copy-start(bf16[1,1,64,256]{3,2,1,0:T(8,128)(2,1)} %get-tuple-element.18) | copy-start | bytes 98308
  82.7 7.4 %collective-permute-start.21 = (bf16[4,64,256]{2,1,0:T(8,128)(2,1)}, bf16[4,64,256]{2,1,0:T(8,128)(2,1)}, u32[]{:S(2)}, u32[]{:S(2)}) collective-permute-start(bf16[4,64,256]{2,1,0:T(8,128)(2,1)} %get-tuple-element.40), channel_id=1, source_target_pairs={{0,6},{2,4},{4,2},{6,0},{8,14},{10,12},{12,10},{14,8},{16,22},{18,... | collective-permute-start | bytes 393224 | tf_op jit(solution)/shard_map/ppermute | solution.py:45
  84.1 7.4 %collective-permute-start.20 = (bf16[4,64,256]{2,1,0:T(8,128)(2,1)}, bf16[4,64,256]{2,1,0:T(8,128)(2,1)}, u32[]{:S(2)}, u32[]{:S(2)}) collective-permute-start(bf16[4,64,256]{2,1,0:T(8,128)(2,1)} %get-tuple-element.40), channel_id=1, source_target_pairs={{0,4},{2,6},{4,0},{6,2},{8,12},{10,14},{12,8},{14,10},{16,20},{18,... | collective-permute-start | bytes 393224 | tf_op jit(solution)/shard_map/ppermute | solution.py:45
  85.3 6.2 %collective-permute-start.19 = (bf16[4,64,256]{2,1,0:T(8,128)(2,1)}, bf16[4,64,256]{2,1,0:T(8,128)(2,1)}, u32[]{:S(2)}, u32[]{:S(2)}) collective-permute-start(bf16[4,64,256]{2,1,0:T(8,128)(2,1)} %get-tuple-element.40), channel_id=1, source_target_pairs={{0,2},{2,0},{4,6},{6,4},{8,10},{10,8},{12,14},{14,12},{16,18},{18,... | collective-permute-start | bytes 393224 | tf_op jit(solution)/shard_map/ppermute | solution.py:45
  86.9 5.8 %collective-permute-start.15 = (bf16[1,384,256]{2,1,0:T(8,128)(2,1)}, bf16[1,384,256]{2,1,0:T(8,128)(2,1)}, u32[]{:S(2)}, u32[]{:S(2)}) collective-permute-start(bf16[1,384,256]{2,1,0:T(8,128)(2,1)} %get-tuple-element.24), channel_id=1, source_target_pairs={{0,1},{1,0},{2,3},{3,2},{4,5},{5,4},{6,7},{7,6},{8,9},{9,8},{10,11... | collective-permute-start | bytes 589832 | tf_op jit(solution)/shard_map/ppermute | solution.py:45
  89.0 3.7 %copy-start.5 = (bf16[1,1,384,256]{3,2,1,0:T(8,128)(2,1)S(1)}, bf16[1,1,384,256]{3,2,1,0:T(8,128)(2,1)}, u32[]{:S(2)}) copy-start(bf16[1,1,384,256]{3,2,1,0:T(8,128)(2,1)} %get-tuple-element.16) | copy-start | bytes 589828
  99.6 6.5 %collective-permute-start.22 = (bf16[280,256]{1,0:T(8,128)(2,1)S(1)}, bf16[280,256]{1,0:T(8,128)(2,1)S(1)}, u32[]{:S(2)}, u32[]{:S(2)}) collective-permute-start(bf16[280,256]{1,0:T(8,128)(2,1)S(1)} %get-tuple-element.46), channel_id=1, source_target_pairs={{0,2},{2,0},{4,6},{6,4},{8,10},{10,8},{12,14},{14,12},{16,18},{18,... | collective-permute-start | bytes 430088 | tf_op jit(solution)/shard_map/ppermute | solution.py:45
  100.8 6.6 %collective-permute-start.23 = (bf16[280,256]{1,0:T(8,128)(2,1)S(1)}, bf16[280,256]{1,0:T(8,128)(2,1)S(1)}, u32[]{:S(2)}, u32[]{:S(2)}) collective-permute-start(bf16[280,256]{1,0:T(8,128)(2,1)S(1)} %get-tuple-element.47), channel_id=1, source_target_pairs={{0,4},{2,6},{4,0},{6,2},{8,12},{10,14},{12,8},{14,10},{16,20},{18,... | collective-permute-start | bytes 430088 | tf_op jit(solution)/shard_map/ppermute | solution.py:45
  101.6 7.3 %collective-permute-start.24 = (bf16[280,256]{1,0:T(8,128)(2,1)S(1)}, bf16[280,256]{1,0:T(8,128)(2,1)S(1)}, u32[]{:S(2)}, u32[]{:S(2)}) collective-permute-start(bf16[280,256]{1,0:T(8,128)(2,1)S(1)} %get-tuple-element.48), channel_id=1, source_target_pairs={{0,6},{2,4},{4,2},{6,0},{8,14},{10,12},{12,10},{14,8},{16,22},{18,... | collective-permute-start | bytes 430088 | tf_op jit(solution)/shard_map/ppermute | solution.py:45
  109.0 10.0 %copy-start.18 = (f32[8]{0:T(128)S(1)}, f32[8]{0:T(128)}, u32[]{:S(2)}) copy-start(f32[8]{0:T(128)} %copy-done.17) | copy-start | bytes 100
  109.0 10.4 %copy-start.7 = (f32[64,256]{1,0:T(8,128)S(1)}, f32[64,256]{1,0:T(8,128)}, u32[]{:S(2)}) copy-start(f32[64,256]{1,0:T(8,128)} %copy-done.6) | copy-start | bytes 196612
  109.0 10.4 %copy-start.9 = (f32[64,256]{1,0:T(8,128)S(1)}, f32[64,256]{1,0:T(8,128)}, u32[]{:S(2)}) copy-start(f32[64,256]{1,0:T(8,128)} %copy-done.8) | copy-start | bytes 196612
  109.0 10.4 %copy-start.11 = (f32[72,256]{1,0:T(8,128)S(1)}, f32[72,256]{1,0:T(8,128)}, u32[]{:S(2)}) copy-start(f32[72,256]{1,0:T(8,128)} %copy-done.10) | copy-start | bytes 221188
  109.2 11.0 %copy-start.3 = (f32[768,256]{1,0:T(8,128)S(1)}, f32[768,256]{1,0:T(8,128)}, u32[]{:S(2)}) copy-start(f32[768,256]{1,0:T(8,128)} %get-tuple-element.69) | copy-start | bytes 2359300
  109.3 5.6 %collective-permute-start.25 = (f32[72,256]{1,0:T(8,128)S(1)}, f32[72,256]{1,0:T(8,128)S(1)}, u32[]{:S(2)}, u32[]{:S(2)}) collective-permute-start(f32[72,256]{1,0:T(8,128)S(1)} %get-tuple-element.52), channel_id=1, source_target_pairs={{0,8},{2,10},{4,12},{6,14},{8,0},{10,2},{12,4},{14,6},{16,24},{18,... | collective-permute-start | bytes 221192 | tf_op jit(solution)/shard_map/ppermute | solution.py:45
  109.9 7.9 %collective-permute-start.26 = (f32[72,256]{1,0:T(8,128)S(1)}, f32[72,256]{1,0:T(8,128)S(1)}, u32[]{:S(2)}, u32[]{:S(2)}) collective-permute-start(f32[72,256]{1,0:T(8,128)S(1)} %get-tuple-element.53), channel_id=1, source_target_pairs={{0,16},{2,18},{4,20},{6,22},{8,24},{10,26},{12,28},{14,30},{16,0},... | collective-permute-start | bytes 221192 | tf_op jit(solution)/shard_map/ppermute | solution.py:45
  111.0 6.8 %collective-permute-start.27 = (f32[72,256]{1,0:T(8,128)S(1)}, f32[72,256]{1,0:T(8,128)S(1)}, u32[]{:S(2)}, u32[]{:S(2)}) collective-permute-start(f32[72,256]{1,0:T(8,128)S(1)} %get-tuple-element.54), channel_id=1, source_target_pairs={{0,24},{2,26},{4,28},{6,30},{8,16},{10,18},{12,20},{14,22},{16,8},... | collective-permute-start | bytes 221192 | tf_op jit(solution)/shard_map/ppermute | solution.py:45
  114.7 5.4 %collective-permute-start.29 = (bf16[384,256]{1,0:T(8,128)(2,1)S(1)}, bf16[384,256]{1,0:T(8,128)(2,1)S(1)}, u32[]{:S(2)}, u32[]{:S(2)}) collective-permute-start(bf16[384,256]{1,0:T(8,128)(2,1)S(1)} %slice.368), channel_id=1, source_target_pairs={{0,1},{1,0},{2,3},{3,2},{4,5},{5,4},{6,7},{7,6},{8,9},{9,8},{10,11... | collective-permute-start | bytes 589832 | tf_op jit(solution)/shard_map/ppermute | solution.py:45
  117.8 1.2 collective-permute-start.28

commit v13 on v10

--- a/solution.py
+++ b/solution.py
@@ -18,8 +18,8 @@
 
 def prior_term(field_vec, prior_mat):
     row_total = field_vec.shape[0]
-    grouped = field_vec.reshape(row_total, DRAWS, DIM)
-    mixed = jnp.einsum("nde,ef->ndf", grouped, prior_mat, precision=top_prec)
+    grouped = field_vec.reshape(row_total * DRAWS, DIM)
+    mixed = jnp.dot(grouped, prior_mat, precision=top_prec)
     return mixed.reshape(row_total, DRAWS * DIM)
 
 

time: 113 us -> 113 us (level)
  waiting for transfers between devices: 29.7 us -> 27.4 us
    reduce_sum x14 -> x16, other arithmetic: 2.4 us -> 6.54 us  [per_draw(): return jnp.sum(product, axis=(0, 2))]
    dot_general x2, matrix products: 6.04 us -> 2.29 us  [cross_parts(): jnp.dot(counts_bf, item_range, preferred_element_type=jnp.float32)]
    dot_general x4, matrix products: 1.74 us -> 4.96 us  [prior_term(): mixed = jnp.dot(grouped, prior_mat, precision=top_prec)]
    another operation x1 -> x3, local copies, waits for them, and re-layouts: 0.01 us -> 2.98 us  [the longest x2 2.98 us: prior_term(): grouped = field_vec.reshape(row_total * DRAWS, DIM)]
    another operation x4 -> x2, local copies, waits for them, and re-layouts: 2.73 us -> 0.07 us  [double_gather(): buf = jnp.stack(ordered, axis=1).reshape((-1,) + piece.shape)]
    reshape x2 -> x6, local copies, waits for them, and re-layouts: 0.28 us -> 2.85 us  [prior_term(): return mixed.reshape(row_total, DRAWS * DIM)]
    dynamic_slice x8 -> x2, local copies, waits for them, and re-layouts: 4.37 us -> 1.94 us  [block_of(): lax.dynamic_index_in_dim(out, value >> j & 1, left.index(group[j]), keepd...]
    ppermute x30, waiting for transfers between devices: 29.7 us -> 27.4 us  [swap_with(): return lax.ppermute(value, axis, pairs)]
  transfers between devices with their start and end apart: 30 -> 30, of which waited for: 20 -> 13; matrix products, arithmetic and copies ran while one was open for 20% -> 26% of each run, Pallas kernels for 0% -> 0%
where the time goes in v13:
time: 113 us; the launch traced here: 112 us
  starting transfers between devices  33.5 us (30%)
  waiting for transfers between devices  27.4 us (24%)
  other arithmetic  18.2 us (16%)
  local copies, waits for them, and re-layouts  17.7 us (16%)
  matrix products  13.1 us (12%)
  between operations  2.09 us (2%)
    ppermute x30, starting transfers between devices, swap_with(): return lax.ppermute(value, axis, pairs)  33.5 us
    ppermute x30, waiting for transfers between devices, swap_with(): return lax.ppermute(value, axis, pairs)  27.4 us
    reduce_sum x16, other arithmetic, per_draw(): return jnp.sum(product, axis=(0, 2))  6.54 us
    another operation x11, other arithmetic, double_gather(): buf = jnp.stack(ordered, axis=1).reshape((-1,) + piece.shape)  5.12 us
    dot_general x4, matrix products, prior_term(): mixed = jnp.dot(grouped, prior_mat, precision=top_prec)  4.96 us
    dot_general x2, matrix products, cross_parts(): lax.dot_general(counts_bf, user_range, (((0,), (0,)), ((), ())), preferre...  4.52 us
    convert_element_type x4, local copies, waits for them, and re-layouts, halve_sum(): send = block_of(digit ^ k).astype(stage_type)  3.37 us
    another operation x2, local copies, waits for them, and re-layouts, prior_term(): grouped = field_vec.reshape(row_total * DRAWS, DIM)  2.98 us
  transfers between devices with their start and end apart: 30, of which 13 were waited for; matrix products, arithmetic and copies ran while one was open for 26% of the time, Pallas kernels for 0%

profile of v13, /device:TPU:0, one launch (start us, length us, event | category | flops | bytes accessed | tf_op | source)
XLA Modules:
  0.0 112.0 jit_solution(3372482725118623087)
XLA Ops:
  0.6 0.9 reshape_squeeze.7
  1.6 1.0 fusion.54
  2.7 0.9 multiply_reduce_fusion.7
  3.6 3.1 %collective-permute-start.2 = (bf16[1,64,256]{2,1,0:T(8,128)(2,1)S(1)}, bf16[1,64,256]{2,1,0:T(8,128)(2,1)}, u32[]{:S(2)}, u32[]{:S(2)}) collective-permute-start(bf16[1,64,256]{2,1,0:T(8,128)(2,1)S(1)} %get-tuple-element.62), channel_id=1, source_target_pairs={{0,8},{2,10},{4,12},{6,14},{8,0},{10,2},{12,4},{14,6},{16,24},{18,... | collective-permute-start | bytes 98312 | tf_op jit(solution)/shard_map/ppermute | solution.py:45
  6.7 2.6 %collective-permute-start.1 = (bf16[1,64,256]{2,1,0:T(8,128)(2,1)S(1)}, bf16[1,64,256]{2,1,0:T(8,128)(2,1)}, u32[]{:S(2)}, u32[]{:S(2)}) collective-permute-start(bf16[1,64,256]{2,1,0:T(8,128)(2,1)S(1)} %get-tuple-element.62), channel_id=1, source_target_pairs={{0,16},{2,18},{4,20},{6,22},{8,24},{10,26},{12,28},{14,30},{16,0},... | collective-permute-start | bytes 98312 | tf_op jit(solution)/shard_map/ppermute | solution.py:45
  9.3 2.1 %reshape_squeeze.6 = f32[1536,64]{1,0:T(8,128)} reshape(f32[1,384,256]{2,1,0:T(8,128)} %param.7) | data formatting | bytes 786432 | tf_op jit(solution)/shard_map/reshape;squeeze | solution.py:21
  11.4 2.9 %fusion.53 = f32[1536,64]{1,0:T(8,128)} fusion(f32[1536,64]{1,0:T(8,128)} %reshape_squeeze.6, f32[64,64]{1,0:T(8,128)S(1)} %copy-done), kind=kOutput, calls=%fused_computation.184 | convolution fusion | flops 75497472 | bytes 802816 | tf_op jit(solution)/shard_map/dot_general | solution.py:22
  14.3 2.1 %reshape.279 = f32[1,384,256]{2,1,0:T(8,128)} reshape(f32[1536,64]{1,0:T(8,128)} %fusion.53) | data formatting | bytes 786432 | tf_op jit(solution)/shard_map/reshape | solution.py:23
  16.4 1.9 %multiply_reduce_fusion.3 = (f32[256]{0:T(256)}, f32[256]{0:T(256)}, bf16[1,384,256]{2,1,0:T(8,128)(2,1)S(1)}) fusion(f32[1,384,256]{2,1,0:T(8,128)} %param.7, f32[1,384,256]{2,1,0:T(8,128)} %reshape.279), kind=kLoop, calls=%fused_computation.47 | loop fusion | flops 491008 | bytes 985088 | tf_op jit(solution)/shard_map/reduce_sum | solution.py:28
  20.5 0.6 reduce_sum.195
  21.1 0.8 reduce_sum.179
  22.0 0.8 reduce_sum.188
  22.7 0.6 reduce_sum.192
  23.9 0.8 select_bitcast_fusion.19
  24.7 0.7 maximum_bitcast_fusion
  25.4 1.7 %collective-permute-start.6 = (bf16[4,64,256]{2,1,0:T(8,128)(2,1)}, bf16[4,64,256]{2,1,0:T(8,128)(2,1)}, u32[]{:S(2)}, u32[]{:S(2)}) collective-permute-start(bf16[4,64,256]{2,1,0:T(8,128)(2,1)} %maximum_bitcast_fusion), channel_id=1, source_target_pairs={{0,2},{2,0},{4,6},{6,4},{8,10},{10,8},{12,14},{14,12},{16,18},{18,... | collective-permute-start | bytes 393224 | tf_op jit(solution)/shard_map/ppermute | solution.py:45
  27.1 1.5 %collective-permute-start.5 = (bf16[4,64,256]{2,1,0:T(8,128)(2,1)}, bf16[4,64,256]{2,1,0:T(8,128)(2,1)}, u32[]{:S(2)}, u32[]{:S(2)}) collective-permute-start(bf16[4,64,256]{2,1,0:T(8,128)(2,1)} %maximum_bitcast_fusion), channel_id=1, source_target_pairs={{0,4},{2,6},{4,0},{6,2},{8,12},{10,14},{12,8},{14,10},{16,20},{18,... | collective-permute-start | bytes 393224 | tf_op jit(solution)/shard_map/ppermute | solution.py:45
  28.9 0.6 convert_reduce_fusion.1
  30.1 1.3 %fusion.2 = bf16[3,256,4,256]{3,2,0,1:T(4,128)(2,1)S(1)} fusion(bf16[12,256,256,1]{2,1,0,3:T(8,128)(2,1)S(1)} %convert_bitcast_fusion.2, pred[12,4]{0,1:T(4,128)(4,1)S(1)} %copy-done.19, pred[12,3]{0,1:T(4,128)(4,1)S(1)} %copy-done.22), kind=kOutput, calls=%fused_computation.4 | convolution fusion | flops 18874512 | bytes 3145812 | tf_op jit(solution)/shard_map/trc,tij->ricj/dot_general | solution.py:147
  32.6 3.3 %collective-permute-done.5 = bf16[4,64,256]{2,1,0:T(8,128)(2,1)} collective-permute-done((bf16[4,64,256]{2,1,0:T(8,128)(2,1)}, bf16[4,64,256]{2,1,0:T(8,128)(2,1)}, u32[]{:S(2)}, u32[]{:S(2)}) %collective-permute-start.5) | collective-permute-done | bytes 131104 | tf_op jit(solution)/shard_map/ppermute | solution.py:45
  35.9 1.2 %select_bitcast_fusion.11 = (bf16[4,1,64,256]{3,2,0,1:T(8,128)(2,1)S(1)}, bf16[4,1,64,256]{3,2,0,1:T(8,128)(2,1)S(1)}, bf16[4,1,64,256]{3,2,0,1:T(8,128)(2,1)S(1)}, bf16[4,1,64,256]{3,2,0,1:T(8,128)(2,1)S(1)}) fusion(bf16[4,64,256]{2,1,0:T(8,128)(2,1)} %collective-permute-done.4, bf16[4,64,256]{2,1,0:T(8,128)(2,1)} %collective-permute-done.5, ...), kind=kLoop, calls=%fused_computation.102 | loop fusion | flops 786432 | bytes 1048579 | tf_op jit(solution)/shard_map/stack | solution.py:128
  37.1 1.0 select_bitcast_fusion.3
  38.2 0.6 fusion.7
  39.1 2.8 %fusion.5 = (f32[256]{0:T(256)S(1)}, f32[1024,256]{1,0:T(8,128)}) fusion(bf16[4,4,64,256]{3,2,1,0:T(8,128)(2,1)S(1)} %copy.31, bf16[1024,256]{1,0:T(8,128)(2,1)S(1)} %bitcast.223, f32[1024]{0:T(1024)S(1)} %bitcast.243, bf16[768,1024]{1,0:T(8,128)(2,1)S(1)} %bitcast.212, bf16[768,256]{1,0:T(8,128)(2,1)} %bitcast.239), kind=kOutput, calls=%fused_computation.13 | convolution fusion | flops 404225792 | bytes 4068352 | tf_op jit(solution)/shard_map/dot_general | solution.py:160
  42.3 1.2 %dynamic-slice_convert_fusion.7 = (bf16[2,2,1,1,64,256]{5,4,3,2,1,0:T(8,128)(2,1)S(1)}, bf16[2,2,1,1,64,256]{5,4,3,2,1,0:T(8,128)(2,1)S(1)}, bf16[2,2,1,1,64,256]{5,4,3,2,1,0:T(8,128)(2,1)S(1)}) fusion(f32[2,2,2,2,64,256]{5,4,3,2,1,0:T(8,128)} %bitcast.234, s32[]{:T(128)S(6)} %select_n.385, s32[]{:T(128)S(6)} %select_n.387, s32[]{:T(128)S(6)} %select_n.393, ...), kind=kLoop, calls=%fused_computation.59 | loop fusion | bytes 786456 | tf_op jit(solution)/shard_map/convert_element_type | solution.py:90
  43.5 1.3 %collective-permute-start.7 = (bf16[280,256]{1,0:T(8,128)(2,1)S(1)}, bf16[280,256]{1,0:T(8,128)(2,1)S(1)}, u32[]{:S(2)}, u32[]{:S(2)}) collective-permute-start(bf16[280,256]{1,0:T(8,128)(2,1)S(1)} %get-tuple-element.66), channel_id=1, source_target_pairs={{0,2},{2,0},{4,6},{6,4},{8,10},{10,8},{12,14},{14,12},{16,18},{18,... | collective-permute-start | bytes 430088 | tf_op jit(solution)/shard_map/ppermute | solution.py:45
  44.8 0.8 collective-permute-start.8
  45.6 1.4 %collective-permute-start.9 = (bf16[280,256]{1,0:T(8,128)(2,1)S(1)}, bf16[280,256]{1,0:T(8,128)(2,1)S(1)}, u32[]{:S(2)}, u32[]{:S(2)}) collective-permute-start(bf16[280,256]{1,0:T(8,128)(2,1)S(1)} %get-tuple-element.68), channel_id=1, source_target_pairs={{0,6},{2,4},{4,2},{6,0},{8,14},{10,12},{12,10},{14,8},{16,22},{18,... | collective-permute-start | bytes 430088 | tf_op jit(solution)/shard_map/ppermute | solution.py:45
  47.5 1.0 constant_dynamic-slice_fusion.1
  48.5 0.8 collective-permute-done.7
  49.3 3.6 %collective-permute-done.8 = bf16[280,256]{1,0:T(8,128)(2,1)S(1)} collective-permute-done((bf16[280,256]{1,0:T(8,128)(2,1)S(1)}, bf16[280,256]{1,0:T(8,128)(2,1)S(1)}, u32[]{:S(2)}, u32[]{:S(2)}) %collective-permute-start.8) | collective-permute-done | bytes 143392 | tf_op jit(solution)/shard_map/ppermute | solution.py:45
  53.3 0.7 collective-permute-start.10
  54.0 3.5 %collective-permute-start.11 = (f32[72,256]{1,0:T(8,128)S(1)}, f32[72,256]{1,0:T(8,128)S(1)}, u32[]{:S(2)}, u32[]{:S(2)}) collective-permute-start(f32[72,256]{1,0:T(8,128)S(1)} %get-tuple-element.73), channel_id=1, source_target_pairs={{0,16},{2,18},{4,20},{6,22},{8,24},{10,26},{12,28},{14,30},{16,0},... | collective-permute-start | bytes 221192 | tf_op jit(solution)/shard_map/ppermute | solution.py:45
  57.9 3.5 %collective-permute-done.11 = f32[72,256]{1,0:T(8,128)S(1)} collective-permute-done((f32[72,256]{1,0:T(8,128)S(1)}, f32[72,256]{1,0:T(8,128)S(1)}, u32[]{:S(2)}, u32[]{:S(2)}) %collective-permute-start.11) | collective-permute-done | bytes 73760 | tf_op jit(solution)/shard_map/ppermute | solution.py:45
  61.4 2.2 %collective-permute-done.12 = f32[72,256]{1,0:T(8,128)S(1)} collective-permute-done((f32[72,256]{1,0:T(8,128)S(1)}, f32[72,256]{1,0:T(8,128)S(1)}, u32[]{:S(2)}, u32[]{:S(2)}) %collective-permute-start.12) | collective-permute-done | bytes 73760 | tf_op jit(solution)/shard_map/ppermute | solution.py:45
  63.8 1.1 collective-permute-done.13
  65.8 1.4 %collective-permute-start.17 = (bf16[1,64,256]{2,1,0:T(8,128)(2,1)S(1)}, bf16[1,64,256]{2,1,0:T(8,128)(2,1)}, u32[]{:S(2)}, u32[]{:S(2)}) collective-permute-start(bf16[1,64,256]{2,1,0:T(8,128)(2,1)S(1)} %get-tuple-element.22), channel_id=1, source_target_pairs={{0,16},{2,18},{4,20},{6,22},{8,24},{10,26},{12,28},{14,30},{16,0},... | collective-permute-start | bytes 98312 | tf_op jit(solution)/shard_map/ppermute | solution.py:45
  67.2 2.9 %collective-permute-start.16 = (bf16[1,64,256]{2,1,0:T(8,128)(2,1)S(1)}, bf16[1,64,256]{2,1,0:T(8,128)(2,1)}, u32[]{:S(2)}, u32[]{:S(2)}) collective-permute-start(bf16[1,64,256]{2,1,0:T(8,128)(2,1)S(1)} %get-tuple-element.22), channel_id=1, source_target_pairs={{0,24},{2,26},{4,28},{6,30},{8,16},{10,18},{12,20},{14,22},{16,8},... | collective-permute-start | bytes 98312 | tf_op jit(solution)/shard_map/ppermute | solution.py:45
  70.7 0.7 reduce_sum.255
  71.5 0.7 reduce_sum.261
  72.9 0.8 fusion.55
  73.9 0.8 select_bitcast_fusion.15
  74.8 0.8 collective-permute-start.21
  75.6 1.4 %collective-permute-start.20 = (bf16[4,64,256]{2,1,0:T(8,128)(2,1)S(1)}, bf16[4,64,256]{2,1,0:T(8,128)(2,1)S(1)}, u32[]{:S(2)}, u32[]{:S(2)}) collective-permute-start(bf16[4,64,256]{2,1,0:T(8,128)(2,1)S(1)} %maximum_bitcast_fusion.1), channel_id=1, source_target_pairs={{0,4},{2,6},{4,0},{6,2},{8,12},{10,14},{12,8},{14,10},{16,20},{18,... | collective-permute-start | bytes 393224 | tf_op jit(solution)/shard_map/ppermute | solution.py:45
  77.0 1.3 %collective-permute-start.19 = (bf16[4,64,256]{2,1,0:T(8,128)(2,1)S(1)}, bf16[4,64,256]{2,1,0:T(8,128)(2,1)S(1)}, u32[]{:S(2)}, u32[]{:S(2)}) collective-permute-start(bf16[4,64,256]{2,1,0:T(8,128)(2,1)S(1)} %maximum_bitcast_fusion.1), channel_id=1, source_target_pairs={{0,6},{2,4},{4,2},{6,0},{8,14},{10,12},{12,10},{14,8},{16,22},{18,... | collective-permute-start | bytes 393224 | tf_op jit(solution)/shard_map/ppermute | solution.py:45
  78.8 2.3 %collective-permute-done.21 = bf16[4,64,256]{2,1,0:T(8,128)(2,1)S(1)} collective-permute-done((bf16[4,64,256]{2,1,0:T(8,128)(2,1)S(1)}, bf16[4,64,256]{2,1,0:T(8,128)(2,1)S(1)}, u32[]{:S(2)}, u32[]{:S(2)}) %collective-permute-start.21) | collective-permute-done | bytes 131104 | tf_op jit(solution)/shard_map/ppermute | solution.py:45
  81.2 2.6 %collective-permute-done.20 = bf16[4,64,256]{2,1,0:T(8,128)(2,1)S(1)} collective-permute-done((bf16[4,64,256]{2,1,0:T(8,128)(2,1)S(1)}, bf16[4,64,256]{2,1,0:T(8,128)(2,1)S(1)}, u32[]{:S(2)}, u32[]{:S(2)}) %collective-permute-start.20) | collective-permute-done | bytes 131104 | tf_op jit(solution)/shard_map/ppermute | solution.py:45
  84.0 1.1 select_bitcast_fusion.1
  85.4 1.7 %fusion.8 = (f32[256]{0:T(256)S(1)}, f32[768,256]{1,0:T(8,128)}) fusion(bf16[1,2,384,256]{3,2,1,0:T(8,128)(2,1)S(1)} %pad_maximum_fusion.3, bf16[768,256]{1,0:T(8,128)(2,1)S(1)} %bitcast.240, f32[768]{0:T(1024)S(1)} %mul.194, bf16[768,1024]{1,0:T(8,128)(2,1)S(1)} %bitcast.213, bf16[1024,256]{1,0:T(8,128)(2,1)S(1)} %bitcast.224), kind=kOutput, calls=%fused_computation.20 | convolution fusion | flops 403832576 | bytes 3674112 | tf_op jit(solution)/shard_map/dot_general | solution.py:158
  87.1 1.7 %fusion.6 = (f32[256]{0:T(256)S(1)}, f32[1024,256]{1,0:T(8,128)}) fusion(bf16[4,4,64,256]{3,2,1,0:T(8,128)(2,1)S(1)} %copy.36, bf16[1024,256]{1,0:T(8,128)(2,1)S(1)} %bitcast.225, f32[1024]{0:T(1024)S(1)} %bitcast.244, bf16[768,1024]{1,0:T(8,128)(2,1)S(1)} %bitcast.214, bf16[768,256]{1,0:T(8,128)(2,1)S(1)} %bitcast.241), kind=kOutput, calls=%fused_computation.14 | convolution fusion | flops 404225792 | bytes 4068352 | tf_op jit(solution)/shard_map/dot_general | solution.py:160
  89.4 1.2 %dynamic-slice_convert_fusion.4 = (bf16[2,2,1,1,64,256]{5,4,3,2,1,0:T(8,128)(2,1)S(1)}, bf16[2,2,1,1,64,256]{5,4,3,2,1,0:T(8,128)(2,1)S(1)}, bf16[2,2,1,1,64,256]{5,4,3,2,1,0:T(8,128)(2,1)S(1)}) fusion(f32[2,2,2,2,64,256]{5,4,3,2,1,0:T(8,128)} %bitcast.236, s32[]{:T(128)S(6)} %select_n.385, s32[]{:T(128)S(6)} %select_n.387, s32[]{:T(128)S(6)} %select_n.393, ...), kind=kLoop, calls=%fused_computation.56 | loop fusion | bytes 786456 | tf_op jit(solution)/shard_map/convert_element_type | solution.py:90
  90.6 1.3 %collective-permute-start.22 = (bf16[280,256]{1,0:T(8,128)(2,1)S(1)}, bf16[280,256]{1,0:T(8,128)(2,1)S(1)}, u32[]{:S(2)}, u32[]{:S(2)}) collective-permute-start(bf16[280,256]{1,0:T(8,128)(2,1)S(1)} %get-tuple-element.63), channel_id=1, source_target_pairs={{0,2},{2,0},{4,6},{6,4},{8,10},{10,8},{12,14},{14,12},{16,18},{18,... | collective-permute-start | bytes 430088 | tf_op jit(solution)/shard_map/ppermute | solution.py:45
  91.9 0.8 collective-permute-start.23
  92.7 1.4 %collective-permute-start.24 = (bf16[280,256]{1,0:T(8,128)(2,1)S(1)}, bf16[280,256]{1,0:T(8,128)(2,1)S(1)}, u32[]{:S(2)}, u32[]{:S(2)}) collective-permute-start(bf16[280,256]{1,0:T(8,128)(2,1)S(1)} %get-tuple-element.65), channel_id=1, source_target_pairs={{0,6},{2,4},{4,2},{6,0},{8,14},{10,12},{12,10},{14,8},{16,22},{18,... | collective-permute-start | bytes 430088 | tf_op jit(solution)/shard_map/ppermute | solution.py:45
  94.1 1.0 constant_dynamic-slice_fusion
  95.1 1.8 %collective-permute-done.22 = bf16[280,256]{1,0:T(8,128)(2,1)S(1)} collective-permute-done((bf16[280,256]{1,0:T(8,128)(2,1)S(1)}, bf16[280,256]{1,0:T(8,128)(2,1)S(1)}, u32[]{:S(2)}, u32[]{:S(2)}) %collective-permute-start.22) | collective-permute-done | bytes 143392 | tf_op jit(solution)/shard_map/ppermute | solution.py:45
  96.9 2.7 %collective-permute-done.23 = bf16[280,256]{1,0:T(8,128)(2,1)S(1)} collective-permute-done((bf16[280,256]{1,0:T(8,128)(2,1)S(1)}, bf16[280,256]{1,0:T(8,128)(2,1)S(1)}, u32[]{:S(2)}, u32[]{:S(2)}) %collective-permute-start.23) | collective-permute-done | bytes 143392 | tf_op jit(solution)/shard_map/ppermute | solution.py:45
  100.0 1.3 %collective-permute-start.26 = (f32[72,256]{1,0:T(8,128)S(1)}, f32[72,256]{1,0:T(8,128)S(1)}, u32[]{:S(2)}, u32[]{:S(2)}) collective-permute-start(f32[72,256]{1,0:T(8,128)S(1)} %get-tuple-element.70), channel_id=1, source_target_pairs={{0,16},{2,18},{4,20},{6,22},{8,24},{10,26},{12,28},{14,30},{16,0},... | collective-permute-start | bytes 221192 | tf_op jit(solution)/shard_map/ppermute | solution.py:45
  101.3 3.1 %collective-permute-start.27 = (f32[72,256]{1,0:T(8,128)S(1)}, f32[72,256]{1,0:T(8,128)S(1)}, u32[]{:S(2)}, u32[]{:S(2)}) collective-permute-start(f32[72,256]{1,0:T(8,128)S(1)} %get-tuple-element.71), channel_id=1, source_target_pairs={{0,24},{2,26},{4,28},{6,30},{8,16},{10,18},{12,20},{14,22},{16,8},... | collective-permute-start | bytes 221192 | tf_op jit(solution)/shard_map/ppermute | solution.py:45
  104.4 1.0 fusion.26
  105.9 1.7 %collective-permute-done.27 = f32[72,256]{1,0:T(8,128)S(1)} collective-permute-done((f32[72,256]{1,0:T(8,128)S(1)}, f32[72,256]{1,0:T(8,128)S(1)}, u32[]{:S(2)}, u32[]{:S(2)}) %collective-permute-start.27) | collective-permute-done | bytes 73760 | tf_op jit(solution)/shard_map/ppermute | solution.py:45
  107.7 1.1 collective-permute-done.28
  109.2 0.7 fusion.37
  109.9 2.1 %fusion.14 = (f32[1,384,256]{2,1,0:T(8,128)}, f32[1,384,256]{2,1,0:T(8,128)}) fusion(f32[384,256]{1,0:T(8,128)S(1)} %get-tuple-element.21, f32[384,256]{1,0:T(8,128)S(1)} %reshape.290, bf16[384,256]{1,0:T(8,128)(2,1)S(1)} %collective-permute-done.29, f32[2,384,256]{2,1,0:T(8,128)} %bitcast.233, s32[]{:T(128)S(6)} %select_n.412, f32[256]{0:T(256)S(1)} %mul.220, ...), kind=kLoop, calls=%fused_computation.31 | loop fusion | flops 1671168 | bytes 3542020 | tf_op jit(solution)/shard_map/broadcast_in_dim | solution.py:221
  (177 shorter events, 11.5 us)
Async XLA Ops:
  0.6 10.7 %copy-start = (f32[64,64]{1,0:T(8,128)S(1)}, f32[64,64]{1,0:T(8,128)}, u32[]{:S(2)}) copy-start(f32[64,64]{1,0:T(8,128)} %param.9) | copy-start | bytes 49156
  3.6 20.2 %collective-permute-start.2 = (bf16[1,64,256]{2,1,0:T(8,128)(2,1)S(1)}, bf16[1,64,256]{2,1,0:T(8,128)(2,1)}, u32[]{:S(2)}, u32[]{:S(2)}) collective-permute-start(bf16[1,64,256]{2,1,0:T(8,128)(2,1)S(1)} %get-tuple-element.62), channel_id=1, source_target_pairs={{0,8},{2,10},{4,12},{6,14},{8,0},{10,2},{12,4},{14,6},{16,24},{18,... | collective-permute-start | bytes 98312 | tf_op jit(solution)/shard_map/ppermute | solution.py:45
  6.7 17.2 %collective-permute-start.1 = (bf16[1,64,256]{2,1,0:T(8,128)(2,1)S(1)}, bf16[1,64,256]{2,1,0:T(8,128)(2,1)}, u32[]{:S(2)}, u32[]{:S(2)}) collective-permute-start(bf16[1,64,256]{2,1,0:T(8,128)(2,1)S(1)} %get-tuple-element.62), channel_id=1, source_target_pairs={{0,16},{2,18},{4,20},{6,22},{8,24},{10,26},{12,28},{14,30},{16,0},... | collective-permute-start | bytes 98312 | tf_op jit(solution)/shard_map/ppermute | solution.py:45
  9.3 14.6 %collective-permute-start = (bf16[1,64,256]{2,1,0:T(8,128)(2,1)S(1)}, bf16[1,64,256]{2,1,0:T(8,128)(2,1)}, u32[]{:S(2)}, u32[]{:S(2)}) collective-permute-start(bf16[1,64,256]{2,1,0:T(8,128)(2,1)S(1)} %get-tuple-element.62), channel_id=1, source_target_pairs={{0,24},{2,26},{4,28},{6,30},{8,16},{10,18},{12,20},{14,22},{16,8},... | collective-permute-start | bytes 98312 | tf_op jit(solution)/shard_map/ppermute | solution.py:45
  11.4 7.6 %copy-start.26 = (s32[1,1,12,2]{2,3,1,0:T(2,128)S(1)}, s32[1,1,12,2]{2,3,1,0:T(2,128)}, u32[]{:S(2)}) copy-start(s32[1,1,12,2]{2,3,1,0:T(2,128)} %param.12) | copy-start | bytes 292
  11.4 17.5 %copy-start.1 = (s32[1,1,12,256,256]{4,3,2,1,0:T(8,128)S(1)}, s32[1,1,12,256,256]{4,3,2,1,0:T(8,128)}, u32[]{:S(2)}) copy-start(s32[1,1,12,256,256]{4,3,2,1,0:T(8,128)} %param.11) | copy-start | bytes 9437188
  18.3 18.8 %collective-permute-start.3 = (bf16[1,384,256]{2,1,0:T(8,128)(2,1)S(1)}, bf16[1,384,256]{2,1,0:T(8,128)(2,1)}, u32[]{:S(2)}, u32[]{:S(2)}) collective-permute-start(bf16[1,384,256]{2,1,0:T(8,128)(2,1)S(1)} %get-tuple-element.41), channel_id=1, source_target_pairs={{0,1},{1,0},{2,3},{3,2},{4,5},{5,4},{6,7},{7,6},{8,9},{9,8},{10,11... | collective-permute-start | bytes 589832 | tf_op jit(solution)/shard_map/ppermute | solution.py:45
  25.4 7.2 %collective-permute-start.6 = (bf16[4,64,256]{2,1,0:T(8,128)(2,1)}, bf16[4,64,256]{2,1,0:T(8,128)(2,1)}, u32[]{:S(2)}, u32[]{:S(2)}) collective-permute-start(bf16[4,64,256]{2,1,0:T(8,128)(2,1)} %maximum_bitcast_fusion), channel_id=1, source_target_pairs={{0,2},{2,0},{4,6},{6,4},{8,10},{10,8},{12,14},{14,12},{16,18},{18,... | collective-permute-start | bytes 393224 | tf_op jit(solution)/shard_map/ppermute | solution.py:45
  27.1 8.8 %collective-permute-start.5 = (bf16[4,64,256]{2,1,0:T(8,128)(2,1)}, bf16[4,64,256]{2,1,0:T(8,128)(2,1)}, u32[]{:S(2)}, u32[]{:S(2)}) collective-permute-start(bf16[4,64,256]{2,1,0:T(8,128)(2,1)} %maximum_bitcast_fusion), channel_id=1, source_target_pairs={{0,4},{2,6},{4,0},{6,2},{8,12},{10,14},{12,8},{14,10},{16,20},{18,... | collective-permute-start | bytes 393224 | tf_op jit(solution)/shard_map/ppermute | solution.py:45
  28.6 7.2 %collective-permute-start.4 = (bf16[4,64,256]{2,1,0:T(8,128)(2,1)}, bf16[4,64,256]{2,1,0:T(8,128)(2,1)}, u32[]{:S(2)}, u32[]{:S(2)}) collective-permute-start(bf16[4,64,256]{2,1,0:T(8,128)(2,1)} %maximum_bitcast_fusion), channel_id=1, source_target_pairs={{0,6},{2,4},{4,2},{6,0},{8,14},{10,12},{12,10},{14,8},{16,22},{18,... | collective-permute-start | bytes 393224 | tf_op jit(solution)/shard_map/ppermute | solution.py:45
  29.5 0.6 copy-start.19
  29.5 0.7 copy-start.22
  32.6 6.6 %copy-start.4 = (bf16[96,8,4,256]{3,1,2,0:T(8,128)(2,1)}, bf16[96,8,4,256]{3,1,2,0:T(8,128)(2,1)S(1)}, u32[]{:S(2)}) copy-start(bf16[96,8,4,256]{3,1,2,0:T(8,128)(2,1)S(1)} %copy.46) | copy-start | bytes 4718596
  38.2 0.7 copy-start.17
  38.9 33.3 %copy-start.6 = (f32[768,256]{1,0:T(8,128)}, f32[768,256]{1,0:T(8,128)S(1)}, u32[]{:S(2)}) copy-start(f32[768,256]{1,0:T(8,128)S(1)} %get-tuple-element.84) | copy-start | bytes 2359300
  39.1 3.0 %copy-start.24 = (f32[4]{0:T(128)S(1)}, f32[4]{0:T(128)}, u32[]{:S(2)}) copy-start(f32[4]{0:T(128)} %reduce_sum.195) | copy-start | bytes 52
  39.1 3.0 %copy-start.25 = (f32[4]{0:T(128)S(1)}, f32[4]{0:T(128)}, u32[]{:S(2)}) copy-start(f32[4]{0:T(128)} %reduce_sum.192) | copy-start | bytes 52
  39.1 3.0 %copy-start.28 = (f32[4]{0:T(128)S(1)}, f32[4]{0:T(128)}, u32[]{:S(2)}) copy-start(f32[4]{0:T(128)} %add.304) | copy-start | bytes 52
  41.9 5.2 %copy-start.2 = (f32[1536,64]{1,0:T(8,128)S(1)}, f32[1536,64]{1,0:T(8,128)}, u32[]{:S(2)}) copy-start(f32[1536,64]{1,0:T(8,128)} %fusion.53) | copy-start | bytes 1179652
  43.5 5.8 %collective-permute-start.7 = (bf16[280,256]{1,0:T(8,128)(2,1)S(1)}, bf16[280,256]{1,0:T(8,128)(2,1)S(1)}, u32[]{:S(2)}, u32[]{:S(2)}) collective-permute-start(bf16[280,256]{1,0:T(8,128)(2,1)S(1)} %get-tuple-element.66), channel_id=1, source_target_pairs={{0,2},{2,0},{4,6},{6,4},{8,10},{10,8},{12,14},{14,12},{16,18},{18,... | collective-permute-start | bytes 430088 | tf_op jit(solution)/shard_map/ppermute | solution.py:45
  44.8 8.2 %collective-permute-start.8 = (bf16[280,256]{1,0:T(8,128)(2,1)S(1)}, bf16[280,256]{1,0:T(8,128)(2,1)S(1)}, u32[]{:S(2)}, u32[]{:S(2)}) collective-permute-start(bf16[280,256]{1,0:T(8,128)(2,1)S(1)} %get-tuple-element.67), channel_id=1, source_target_pairs={{0,4},{2,6},{4,0},{6,2},{8,12},{10,14},{12,8},{14,10},{16,20},{18,... | collective-permute-start | bytes 430088 | tf_op jit(solution)/shard_map/ppermute | solution.py:45
  45.6 7.4 %collective-permute-start.9 = (bf16[280,256]{1,0:T(8,128)(2,1)S(1)}, bf16[280,256]{1,0:T(8,128)(2,1)S(1)}, u32[]{:S(2)}, u32[]{:S(2)}) collective-permute-start(bf16[280,256]{1,0:T(8,128)(2,1)S(1)} %get-tuple-element.68), channel_id=1, source_target_pairs={{0,6},{2,4},{4,2},{6,0},{8,14},{10,12},{12,10},{14,8},{16,22},{18,... | collective-permute-start | bytes 430088 | tf_op jit(solution)/shard_map/ppermute | solution.py:45
  47.1 18.5 %copy-start.13 = (f32[64,256]{1,0:T(8,128)}, f32[64,256]{1,0:T(8,128)S(1)}, u32[]{:S(2)}) copy-start(f32[64,256]{1,0:T(8,128)S(1)} %reshape.285) | copy-start | bytes 196612
  53.0 12.7 %copy-start.8 = (f32[1,64,256]{2,1,0:T(8,128)S(1)}, f32[1,64,256]{2,1,0:T(8,128)}, u32[]{:S(2)}) copy-start(f32[1,64,256]{2,1,0:T(8,128)} %param.8) | copy-start | bytes 196612
  53.1 17.1 %copy-start.18 = (f32[64,64]{1,0:T(8,128)S(1)}, f32[64,64]{1,0:T(8,128)}, u32[]{:S(2)}) copy-start(f32[64,64]{1,0:T(8,128)} %param.10) | copy-start | bytes 49156
  53.2 19.0 %copy-start.3 = (f32[1,384,256]{2,1,0:T(8,128)S(1)}, f32[1,384,256]{2,1,0:T(8,128)}, u32[]{:S(2)}) copy-start(f32[1,384,256]{2,1,0:T(8,128)} %param.7) | copy-start | bytes 1179652
  53.3 4.6 %collective-permute-start.10 = (f32[72,256]{1,0:T(8,128)S(1)}, f32[72,256]{1,0:T(8,128)S(1)}, u32[]{:S(2)}, u32[]{:S(2)}) collective-permute-start(f32[72,256]{1,0:T(8,128)S(1)} %get-tuple-element.72), channel_id=1, source_target_pairs={{0,8},{2,10},{4,12},{6,14},{8,0},{10,2},{12,4},{14,6},{16,24},{18,... | collective-permute-start | bytes 221192 | tf_op jit(solution)/shard_map/ppermute | solution.py:45
  54.0 7.4 %collective-permute-start.11 = (f32[72,256]{1,0:T(8,128)S(1)}, f32[72,256]{1,0:T(8,128)S(1)}, u32[]{:S(2)}, u32[]{:S(2)}) collective-permute-start(f32[72,256]{1,0:T(8,128)S(1)} %get-tuple-element.73), channel_id=1, source_target_pairs={{0,16},{2,18},{4,20},{6,22},{8,24},{10,26},{12,28},{14,30},{16,0},... | collective-permute-start | bytes 221192 | tf_op jit(solution)/shard_map/ppermute | solution.py:45
  57.5 6.2 %collective-permute-start.12 = (f32[72,256]{1,0:T(8,128)S(1)}, f32[72,256]{1,0:T(8,128)S(1)}, u32[]{:S(2)}, u32[]{:S(2)}) collective-permute-start(f32[72,256]{1,0:T(8,128)S(1)} %get-tuple-element.74), channel_id=1, source_target_pairs={{0,24},{2,26},{4,28},{6,30},{8,16},{10,18},{12,20},{14,22},{16,8},... | collective-permute-start | bytes 221192 | tf_op jit(solution)/shard_map/ppermute | solution.py:45
  57.7 14.4 %collective-permute-start.14 = (bf16[384,256]{1,0:T(8,128)(2,1)S(1)}, bf16[384,256]{1,0:T(8,128)(2,1)S(1)}, u32[]{:S(2)}, u32[]{:S(2)}) collective-permute-start(bf16[384,256]{1,0:T(8,128)(2,1)S(1)} %fusion.25), channel_id=1, source_target_pairs={{0,1},{1,0},{2,3},{3,2},{4,5},{5,4},{6,7},{7,6},{8,9},{9,8},{10,11... | collective-permute-start | bytes 589832 | tf_op jit(solution)/shard_map/ppermute | solution.py:45
  63.7 8.9 %copy-start.15 = (f32[72,256]{1,0:T(8,128)}, f32[72,256]{1,0:T(8,128)S(1)}, u32[]{:S(2)}) copy-start(f32[72,256]{1,0:T(8,128)S(1)} %fusion.32) | copy-start | bytes 221188
  63.7 1.2 %collective-permute-start.13 = (f32[8]{0:T(128)S(1)}, f32[8]{0:T(128)S(1)}, u32[]{:S(2)}, u32[]{:S(2)}) collective-permute-start(f32[8]{0:T(128)S(1)} %slice_bitcast_fusion.1), channel_id=1, source_target_pairs={{0,1},{1,0},{2,3},{3,2},{4,5},{5,4},{6,7},{7,6},{8,9},{9,8},{10,11... | collective-permute-start | bytes 104 | tf_op jit(solution)/shard_map/ppermute | solution.py:45
  64.9 0.6 copy-start.20
  65.7 8.2 %collective-permute-start.18 = (bf16[1,64,256]{2,1,0:T(8,128)(2,1)S(1)}, bf16[1,64,256]{2,1,0:T(8,128)(2,1)}, u32[]{:S(2)}, u32[]{:S(2)}) collective-permute-start(bf16[1,64,256]{2,1,0:T(8,128)(2,1)S(1)} %get-tuple-element.22), channel_id=1, source_target_pairs={{0,8},{2,10},{4,12},{6,14},{8,0},{10,2},{12,4},{14,6},{16,24},{18,... | collective-permute-start | bytes 98312 | tf_op jit(solution)/shard_map/ppermute | solution.py:45
  65.8 8.1 %collective-permute-start.17 = (bf16[1,64,256]{2,1,0:T(8,128)(2,1)S(1)}, bf16[1,64,256]{2,1,0:T(8,128)(2,1)}, u32[]{:S(2)}, u32[]{:S(2)}) collective-permute-start(bf16[1,64,256]{2,1,0:T(8,128)(2,1)S(1)} %get-tuple-element.22), channel_id=1, source_target_pairs={{0,16},{2,18},{4,20},{6,22},{8,24},{10,26},{12,28},{14,30},{16,0},... | collective-permute-start | bytes 98312 | tf_op jit(solution)/shard_map/ppermute | solution.py:45
  67.2 6.7 %collective-permute-start.16 = (bf16[1,64,256]{2,1,0:T(8,128)(2,1)S(1)}, bf16[1,64,256]{2,1,0:T(8,128)(2,1)}, u32[]{:S(2)}, u32[]{:S(2)}) collective-permute-start(bf16[1,64,256]{2,1,0:T(8,128)(2,1)S(1)} %get-tuple-element.22), channel_id=1, source_target_pairs={{0,24},{2,26},{4,28},{6,30},{8,16},{10,18},{12,20},{14,22},{16,8},... | collective-permute-start | bytes 98312 | tf_op jit(solution)/shard_map/ppermute | solution.py:45
  70.6 1.9 %copy-start.11 = (f32[64,256]{1,0:T(8,128)}, f32[64,256]{1,0:T(8,128)S(1)}, u32[]{:S(2)}) copy-start(f32[64,256]{1,0:T(8,128)S(1)} %reshape.292) | copy-start | bytes 196612
  72.2 0.7 copy-start.9
  72.3 11.7 %collective-permute-start.15 = (bf16[1,384,256]{2,1,0:T(8,128)(2,1)S(1)}, bf16[1,384,256]{2,1,0:T(8,128)(2,1)}, u32[]{:S(2)}, u32[]{:S(2)}) collective-permute-start(bf16[1,384,256]{2,1,0:T(8,128)(2,1)S(1)} %get-tuple-element.20), channel_id=1, source_target_pairs={{0,1},{1,0},{2,3},{3,2},{4,5},{5,4},{6,7},{7,6},{8,9},{9,8},{10,11... | collective-permute-start | bytes 589832 | tf_op jit(solution)/shard_map/ppermute | solution.py:45
  73.6 5.2 %copy-start.27 = (f32[4]{0:T(128)S(1)}, f32[4]{0:T(128)}, u32[]{:S(2)}) copy-start(f32[4]{0:T(128)} %reduce_sum.255) | copy-start | bytes 52
  74.8 6.4 %collective-permute-start.21 = (bf16[4,64,256]{2,1,0:T(8,128)(2,1)S(1)}, bf16[4,64,256]{2,1,0:T(8,128)(2,1)S(1)}, u32[]{:S(2)}, u32[]{:S(2)}) collective-permute-start(bf16[4,64,256]{2,1,0:T(8,128)(2,1)S(1)} %maximum_bitcast_fusion.1), channel_id=1, source_target_pairs={{0,2},{2,0},{4,6},{6,4},{8,10},{10,8},{12,14},{14,12},{16,18},{18,... | collective-permute-start | bytes 393224 | tf_op jit(solution)/shard_map/ppermute | solution.py:45
  75.6 8.1 %collective-permute-start.20 = (bf16[4,64,256]{2,1,0:T(8,128)(2,1)S(1)}, bf16[4,64,256]{2,1,0:T(8,128)(2,1)S(1)}, u32[]{:S(2)}, u32[]{:S(2)}) collective-permute-start(bf16[4,64,256]{2,1,0:T(8,128)(2,1)S(1)} %maximum_bitcast_fusion.1), channel_id=1, source_target_pairs={{0,4},{2,6},{4,0},{6,2},{8,12},{10,14},{12,8},{14,10},{16,20},{18,... | collective-permute-start | bytes 393224 | tf_op jit(solution)/shard_map/ppermute | solution.py:45
  77.0 6.8 %collective-permute-start.19 = (bf16[4,64,256]{2,1,0:T(8,128)(2,1)S(1)}, bf16[4,64,256]{2,1,0:T(8,128)(2,1)S(1)}, u32[]{:S(2)}, u32[]{:S(2)}) collective-permute-start(bf16[4,64,256]{2,1,0:T(8,128)(2,1)S(1)} %maximum_bitcast_fusion.1), channel_id=1, source_target_pairs={{0,6},{2,4},{4,2},{6,0},{8,14},{10,12},{12,10},{14,8},{16,22},{18,... | collective-permute-start | bytes 393224 | tf_op jit(solution)/shard_map/ppermute | solution.py:45
  83.9 1.5 %copy-start.5 = (bf16[96,8,4,256]{3,1,2,0:T(8,128)(2,1)S(1)}, bf16[96,8,4,256]{3,1,2,0:T(8,128)(2,1)}, u32[]{:S(2)}) copy-start(bf16[96,8,4,256]{3,1,2,0:T(8,128)(2,1)} %copy-done.4) | copy-start | bytes 4718596
  87.1 2.1 %copy-start.23 = (f32[4]{0:T(128)S(1)}, f32[4]{0:T(128)}, u32[]{:S(2)}) copy-start(f32[4]{0:T(128)} %reduce_sum.261) | copy-start | bytes 52
  90.6 6.3 %collective-permute-start.22 = (bf16[280,256]{1,0:T(8,128)(2,1)S(1)}, bf16[280,256]{1,0:T(8,128)(2,1)S(1)}, u32[]{:S(2)}, u32[]{:S(2)}) collective-permute-start(bf16[280,256]{1,0:T(8,128)(2,1)S(1)} %get-tuple-element.63), channel_id=1, source_target_pairs={{0,2},{2,0},{4,6},{6,4},{8,10},{10,8},{12,14},{14,12},{16,18},{18,... | collective-permute-start | bytes 430088 | tf_op jit(solution)/shard_map/ppermute | solution.py:45
  91.9 7.7 %collective-permute-start.23 = (bf16[280,256]{1,0:T(8,128)(2,1)S(1)}, bf16[280,256]{1,0:T(8,128)(2,1)S(1)}, u32[]{:S(2)}, u32[]{:S(2)}) collective-permute-start(bf16[280,256]{1,0:T(8,128)(2,1)S(1)} %get-tuple-element.64), channel_id=1, source_target_pairs={{0,4},{2,6},{4,0},{6,2},{8,12},{10,14},{12,8},{14,10},{16,20},{18,... | collective-permute-start | bytes 430088 | tf_op jit(solution)/shard_map/ppermute | solution.py:45
  92.7 6.9 %collective-permute-start.24 = (bf16[280,256]{1,0:T(8,128)(2,1)S(1)}, bf16[280,256]{1,0:T(8,128)(2,1)S(1)}, u32[]{:S(2)}, u32[]{:S(2)}) collective-permute-start(bf16[280,256]{1,0:T(8,128)(2,1)S(1)} %get-tuple-element.65), channel_id=1, source_target_pairs={{0,6},{2,4},{4,2},{6,0},{8,14},{10,12},{12,10},{14,8},{16,22},{18,... | collective-permute-start | bytes 430088 | tf_op jit(solution)/shard_map/ppermute | solution.py:45
  99.6 9.2 %copy-start.21 = (f32[8]{0:T(128)S(1)}, f32[8]{0:T(128)}, u32[]{:S(2)}) copy-start(f32[8]{0:T(128)} %copy-done.20) | copy-start | bytes 100
  99.6 9.6 %copy-start.12 = (f32[64,256]{1,0:T(8,128)S(1)}, f32[64,256]{1,0:T(8,128)}, u32[]{:S(2)}) copy-start(f32[64,256]{1,0:T(8,128)} %copy-done.11) | copy-start | bytes 196612
  99.6 9.6 %copy-start.14 = (f32[64,256]{1,0:T(8,128)S(1)}, f32[64,256]{1,0:T(8,128)}, u32[]{:S(2)}) copy-start(f32[64,256]{1,0:T(8,128)} %copy-done.13) | copy-start | bytes 196612
  99.6 9.6 %copy-start.16 = (f32[72,256]{1,0:T(8,128)S(1)}, f32[72,256]{1,0:T(8,128)}, u32[]{:S(2)}) copy-start(f32[72,256]{1,0:T(8,128)} %copy-done.15) | copy-start | bytes 221188
  99.8 10.1 %copy-start.7 = (f32[768,256]{1,0:T(8,128)S(1)}, f32[768,256]{1,0:T(8,128)}, u32[]{:S(2)}) copy-start(f32[768,256]{1,0:T(8,128)} %copy-done.6) | copy-start | bytes 2359300
  99.8 10.1 %copy-start.10 = (bf16[384,256]{1,0:T(8,128)(2,1)S(1)}, bf16[384,256]{1,0:T(8,128)(2,1)}, u32[]{:S(2)}) copy-start(bf16[384,256]{1,0:T(8,128)(2,1)} %copy-done.9) | copy-start | bytes 589828
  99.9 6.0 %collective-permute-start.25 = (f32[72,256]{1,0:T(8,128)S(1)}, f32[72,256]{1,0:T(8,128)S(1)}, u32[]{:S(2)}, u32[]{:S(2)}) collective-permute-start(f32[72,256]{1,0:T(8,128)S(1)} %get-tuple-element.69), channel_id=1, source_target_pairs={{0,8},{2,10},{4,12},{6,14},{8,0},{10,2},{12,4},{14,6},{16,24},{18,... | collective-permute-start | bytes 221192 | tf_op jit(solution)/shard_map/ppermute | solution.py:45
  100.0 5.9 %collective-permute-start.26 = (f32[72,256]{1,0:T(8,128)S(1)}, f32[72,256]{1,0:T(8,128)S(1)}, u32[]{:S(2)}, u32[]{:S(2)}) collective-permute-start(f32[72,256]{1,0:T(8,128)S(1)} %get-tuple-element.70), channel_id=1, source_target_pairs={{0,16},{2,18},{4,20},{6,22},{8,24},{10,26},{12,28},{14,30},{16,0},... | collective-permute-start | bytes 221192 | tf_op jit(solution)/shard_map/ppermute | solution.py:45
  101.3 6.3 %collective-permute-start.27 = (f32[72,256]{1,0:T(8,128)S(1)}, f32[72,256]{1,0:T(8,128)S(1)}, u32[]{:S(2)}, u32[]{:S(2)}) collective-permute-start(f32[72,256]{1,0:T(8,128)S(1)} %get-tuple-element.71), channel_id=1, source_target_pairs={{0,24},{2,26},{4,28},{6,30},{8,16},{10,18},{12,20},{14,22},{16,8},... | collective-permute-start | bytes 221192 | tf_op jit(solution)/shard_map/ppermute | solution.py:45
  105.4 4.5 %collective-permute-start.29 = (bf16[384,256]{1,0:T(8,128)(2,1)S(1)}, bf16[384,256]{1,0:T(8,128)(2,1)S(1)}, u32[]{:S(2)}, u32[]{:S(2)}) collective-permute-start(bf16[384,256]{1,0:T(8,128)(2,1)S(1)} %fusion.26), channel_id=1, source_target_pairs={{0,1},{1,0},{2,3},{3,2},{4,5},{5,4},{6,7},{7,6},{8,9},{9,8},{10,11... | collective-permute-start | bytes 589832 | tf_op jit(solution)/shard_map/ppermute | solution.py:45
  107.6 1.2 %collective-permute-start.28 = (f32[8]{0:T(128)S(1)}, f32[8]{0:T(128)S(1)}, u32[]{:S(2)}, u32[]{:S(2)}) collective-permute-start(f32[8]{0:T(128)S(1)} %slice_bitcast_fusion), channel_id=1, source_target_pairs={{0,1},{1,0},{2,3},{3,2},{4,5},{5,4},{6,7},{7,6},{8,9},{9,8},{10,11... | collective-permute-start | bytes 104 | tf_op jit(solution)/shard_map/ppermute | solution.py:45

commit v14 on v13

--- a/solution.py
+++ b/solution.py
@@ -147,19 +147,20 @@
         counts_bf = jnp.einsum(
             "trc,tij->ricj", place, tiles_bf, preferred_element_type=jnp.bfloat16
         ).reshape(RB * TILE, CB * TILE)
+        counts_t = jnp.einsum(
+            "trc,tij->cjri", place, tiles_bf, preferred_element_type=jnp.bfloat16
+        ).reshape(CB * TILE, RB * TILE)
         tile_rows = jnp.sum(tiles_bf, axis=2, dtype=jnp.float32)
         tile_cols = jnp.sum(tiles_bf, axis=1, dtype=jnp.float32)
         user_deg = jnp.sum(jnp.where(row_pick[:, :, None], tile_rows[:, None, :], 0.0), axis=0)
         item_deg = jnp.sum(jnp.where(col_pick[:, :, None], tile_cols[:, None, :], 0.0), axis=0)
-        return (counts_bf, user_deg.reshape(-1), item_deg.reshape(-1))
+        return (counts_bf, counts_t, user_deg.reshape(-1), item_deg.reshape(-1))
 
     def cross_parts(user_range, item_range, counts):
-        counts_bf, user_deg, item_deg = counts
+        counts_bf, counts_t, user_deg, item_deg = counts
         to_users = jnp.dot(counts_bf, item_range, preferred_element_type=jnp.float32)
         to_users = to_users + user_deg[:, None] * user_range.astype(jnp.float32)
-        to_items = lax.dot_general(
-            counts_bf, user_range, (((0,), (0,)), ((), ())), preferred_element_type=jnp.float32
-        )
+        to_items = jnp.dot(counts_t, user_range, preferred_element_type=jnp.float32)
         to_items = to_items + item_deg[:, None] * item_range.astype(jnp.float32)
         return (to_users, to_items)
 

time: 113 us -> 113 us (level)
    unnamed x60 -> x65, local copies, waits for them, and re-layouts: 2.14 us -> 2.32 us
  transfers between devices with their start and end apart: 30 -> 30, of which waited for: 13 -> 13; matrix products, arithmetic and copies ran while one was open for 26% -> 27% of each run, Pallas kernels for 0% -> 0%
where the time goes in v14:
time: 113 us; the launch traced here: 112 us
  starting transfers between devices  33.5 us (30%)
  waiting for transfers between devices  26.5 us (23%)
  local copies, waits for them, and re-layouts  18.6 us (16%)
  other arithmetic  18.2 us (16%)
  matrix products  12.9 us (11%)
  between operations  2.14 us (2%)
    ppermute x30, starting transfers between devices, swap_with(): return lax.ppermute(value, axis, pairs)  33.5 us
    ppermute x30, waiting for transfers between devices, swap_with(): return lax.ppermute(value, axis, pairs)  26.5 us
    reduce_sum x16, other arithmetic, per_draw(): return jnp.sum(product, axis=(0, 2))  6.51 us
    another operation x11, other arithmetic, double_gather(): buf = jnp.stack(ordered, axis=1).reshape((-1,) + piece.shape)  5.12 us
    dot_general x4, matrix products, prior_term(): mixed = jnp.dot(grouped, prior_mat, precision=top_prec)  4.96 us
    convert_element_type x4, local copies, waits for them, and re-layouts, halve_sum(): send = block_of(digit ^ k).astype(stage_type)  3.53 us
    dot_general x2, matrix products, cross_parts(): to_items = jnp.dot(counts_t, user_range, preferred_element_type=jnp.float32)  3.47 us
    dot_general x2, matrix products, cross_parts(): jnp.dot(counts_bf, item_range, preferred_element_type=jnp.float32)  3.17 us
  transfers between devices with their start and end apart: 30, of which 13 were waited for; matrix products, arithmetic and copies ran while one was open for 27% of the time, Pallas kernels for 0%

profile of v14, /device:TPU:0, one launch (start us, length us, event | category | flops | bytes accessed | tf_op | source)
XLA Modules:
  0.0 111.9 jit_solution(3029239466569728836)
XLA Ops:
  0.6 0.9 reshape_squeeze.7
  1.6 1.0 fusion.51
  2.7 0.9 multiply_reduce_fusion.7
  3.6 3.1 %collective-permute-start.2 = (bf16[1,64,256]{2,1,0:T(8,128)(2,1)S(1)}, bf16[1,64,256]{2,1,0:T(8,128)(2,1)}, u32[]{:S(2)}, u32[]{:S(2)}) collective-permute-start(bf16[1,64,256]{2,1,0:T(8,128)(2,1)S(1)} %get-tuple-element.62), channel_id=1, source_target_pairs={{0,8},{2,10},{4,12},{6,14},{8,0},{10,2},{12,4},{14,6},{16,24},{18,... | collective-permute-start | bytes 98312 | tf_op jit(solution)/shard_map/ppermute | solution.py:45
  6.7 2.6 %collective-permute-start.1 = (bf16[1,64,256]{2,1,0:T(8,128)(2,1)S(1)}, bf16[1,64,256]{2,1,0:T(8,128)(2,1)}, u32[]{:S(2)}, u32[]{:S(2)}) collective-permute-start(bf16[1,64,256]{2,1,0:T(8,128)(2,1)S(1)} %get-tuple-element.62), channel_id=1, source_target_pairs={{0,16},{2,18},{4,20},{6,22},{8,24},{10,26},{12,28},{14,30},{16,0},... | collective-permute-start | bytes 98312 | tf_op jit(solution)/shard_map/ppermute | solution.py:45
  9.3 2.0 %reshape_squeeze.6 = f32[1536,64]{1,0:T(8,128)} reshape(f32[1,384,256]{2,1,0:T(8,128)} %param.7) | data formatting | bytes 786432 | tf_op jit(solution)/shard_map/reshape;squeeze | solution.py:21
  11.4 2.9 %fusion.50 = f32[1536,64]{1,0:T(8,128)} fusion(f32[1536,64]{1,0:T(8,128)} %reshape_squeeze.6, f32[64,64]{1,0:T(8,128)S(1)} %copy-done), kind=kOutput, calls=%fused_computation.183 | convolution fusion | flops 75497472 | bytes 802816 | tf_op jit(solution)/shard_map/dot_general | solution.py:22
  14.3 2.1 %reshape.282 = f32[1,384,256]{2,1,0:T(8,128)} reshape(f32[1536,64]{1,0:T(8,128)} %fusion.50) | data formatting | bytes 786432 | tf_op jit(solution)/shard_map/reshape | solution.py:23
  16.4 1.9 %multiply_reduce_fusion.3 = (f32[256]{0:T(256)}, f32[256]{0:T(256)}, bf16[1,384,256]{2,1,0:T(8,128)(2,1)S(1)}) fusion(f32[1,384,256]{2,1,0:T(8,128)} %param.7, f32[1,384,256]{2,1,0:T(8,128)} %reshape.282), kind=kLoop, calls=%fused_computation.46 | loop fusion | flops 491008 | bytes 985088 | tf_op jit(solution)/shard_map/reduce_sum | solution.py:28
  20.5 0.6 reduce_sum.195
  21.1 0.8 reduce_sum.179
  22.0 0.8 reduce_sum.188
  22.7 0.6 reduce_sum.192
  23.9 0.8 select_bitcast_fusion.19
  24.7 0.7 maximum_bitcast_fusion
  25.4 1.7 %collective-permute-start.6 = (bf16[4,64,256]{2,1,0:T(8,128)(2,1)}, bf16[4,64,256]{2,1,0:T(8,128)(2,1)}, u32[]{:S(2)}, u32[]{:S(2)}) collective-permute-start(bf16[4,64,256]{2,1,0:T(8,128)(2,1)} %maximum_bitcast_fusion), channel_id=1, source_target_pairs={{0,2},{2,0},{4,6},{6,4},{8,10},{10,8},{12,14},{14,12},{16,18},{18,... | collective-permute-start | bytes 393224 | tf_op jit(solution)/shard_map/ppermute | solution.py:45
  27.1 1.5 %collective-permute-start.5 = (bf16[4,64,256]{2,1,0:T(8,128)(2,1)}, bf16[4,64,256]{2,1,0:T(8,128)(2,1)}, u32[]{:S(2)}, u32[]{:S(2)}) collective-permute-start(bf16[4,64,256]{2,1,0:T(8,128)(2,1)} %maximum_bitcast_fusion), channel_id=1, source_target_pairs={{0,4},{2,6},{4,0},{6,2},{8,12},{10,14},{12,8},{14,10},{16,20},{18,... | collective-permute-start | bytes 393224 | tf_op jit(solution)/shard_map/ppermute | solution.py:45
  28.9 0.6 convert_reduce_fusion.1
  30.1 1.3 %fusion = bf16[256,256,3,4]{1,3,2,0:T(4,128)(2,1)S(1)} fusion(bf16[12,256,256,1]{2,1,0,3:T(8,128)(2,1)S(1)} %convert_bitcast_fusion.2, pred[12,4]{0,1:T(4,128)(4,1)S(1)} %copy-done.21, pred[12,3]{0,1:T(4,128)(4,1)S(1)} %copy-done.24), kind=kOutput, calls=%fused_computation.2 | convolution fusion | flops 18874512 | bytes 3145812 | tf_op jit(solution)/shard_map/trc,tij->cjri/dot_general | solution.py:150
  33.5 2.3 %collective-permute-done.5 = bf16[4,64,256]{2,1,0:T(8,128)(2,1)} collective-permute-done((bf16[4,64,256]{2,1,0:T(8,128)(2,1)}, bf16[4,64,256]{2,1,0:T(8,128)(2,1)}, u32[]{:S(2)}, u32[]{:S(2)}) %collective-permute-start.5) | collective-permute-done | bytes 131104 | tf_op jit(solution)/shard_map/ppermute | solution.py:45
  35.8 1.2 %select_bitcast_fusion.11 = (bf16[4,1,64,256]{3,2,0,1:T(8,128)(2,1)S(1)}, bf16[4,1,64,256]{3,2,0,1:T(8,128)(2,1)S(1)}, bf16[4,1,64,256]{3,2,0,1:T(8,128)(2,1)S(1)}, bf16[4,1,64,256]{3,2,0,1:T(8,128)(2,1)S(1)}) fusion(bf16[4,64,256]{2,1,0:T(8,128)(2,1)} %collective-permute-done.4, bf16[4,64,256]{2,1,0:T(8,128)(2,1)} %collective-permute-done.5, ...), kind=kLoop, calls=%fused_computation.101 | loop fusion | flops 786432 | bytes 1048579 | tf_op jit(solution)/shard_map/stack | solution.py:128
  37.1 1.0 select_bitcast_fusion.3
  38.2 1.7 %fusion.2 = (f32[256]{0:T(256)S(1)}, f32[1024,256]{1,0:T(8,128)}) fusion(bf16[4,4,64,256]{3,2,1,0:T(8,128)(2,1)S(1)} %copy.32, bf16[1024,256]{1,0:T(8,128)(2,1)S(1)} %bitcast.232, f32[1024]{0:T(1024)S(1)} %bitcast.251, bf16[1024,768]{0,1:T(8,128)(2,1)S(1)} %bitcast.219, bf16[768,256]{1,0:T(8,128)(2,1)S(1)} %bitcast.246), kind=kOutput, calls=%fused_computation.12 | convolution fusion | flops 404225792 | bytes 4068352 | tf_op jit(solution)/shard_map/dot_general | solution.py:163
  40.2 1.7 %fusion.4 = (f32[256]{0:T(256)S(1)}, f32[768,256]{1,0:T(8,128)S(1)}) fusion(bf16[1,2,384,256]{3,2,1,0:T(8,128)(2,1)} %copy-done.19, bf16[768,256]{1,0:T(8,128)(2,1)} %bitcast.247, f32[768]{0:T(1024)S(1)} %mul.194, bf16[768,1024]{1,0:T(8,128)(2,1)S(1)} %bitcast.221, bf16[1024,256]{1,0:T(8,128)(2,1)S(1)} %bitcast.233), kind=kOutput, calls=%fused_computation.18 | convolution fusion | flops 403832576 | bytes 3674112 | tf_op jit(solution)/shard_map/dot_general | solution.py:161
  42.2 1.3 %dynamic-slice_convert_fusion.7 = (bf16[2,2,1,1,64,256]{5,4,3,2,1,0:T(8,128)(2,1)S(1)}, bf16[2,2,1,1,64,256]{5,4,3,2,1,0:T(8,128)(2,1)S(1)}, bf16[2,2,1,1,64,256]{5,4,3,2,1,0:T(8,128)(2,1)S(1)}) fusion(f32[2,2,2,2,64,256]{5,4,3,2,1,0:T(8,128)} %bitcast.242, s32[]{:T(128)S(6)} %select_n.385, s32[]{:T(128)S(6)} %select_n.387, s32[]{:T(128)S(6)} %select_n.393, ...), kind=kLoop, calls=%fused_computation.58 | loop fusion | bytes 786456 | tf_op jit(solution)/shard_map/convert_element_type | solution.py:90
  43.6 1.3 %collective-permute-start.7 = (bf16[280,256]{1,0:T(8,128)(2,1)S(1)}, bf16[280,256]{1,0:T(8,128)(2,1)S(1)}, u32[]{:S(2)}, u32[]{:S(2)}) collective-permute-start(bf16[280,256]{1,0:T(8,128)(2,1)S(1)} %get-tuple-element.66), channel_id=1, source_target_pairs={{0,2},{2,0},{4,6},{6,4},{8,10},{10,8},{12,14},{14,12},{16,18},{18,... | collective-permute-start | bytes 430088 | tf_op jit(solution)/shard_map/ppermute | solution.py:45
  44.9 0.8 collective-permute-start.8
  45.7 1.4 %collective-permute-start.9 = (bf16[280,256]{1,0:T(8,128)(2,1)S(1)}, bf16[280,256]{1,0:T(8,128)(2,1)S(1)}, u32[]{:S(2)}, u32[]{:S(2)}) collective-permute-start(bf16[280,256]{1,0:T(8,128)(2,1)S(1)} %get-tuple-element.68), channel_id=1, source_target_pairs={{0,6},{2,4},{4,2},{6,0},{8,14},{10,12},{12,10},{14,8},{16,22},{18,... | collective-permute-start | bytes 430088 | tf_op jit(solution)/shard_map/ppermute | solution.py:45
  47.6 1.0 constant_dynamic-slice_fusion.1
  48.6 0.8 collective-permute-done.7
  49.4 3.7 %collective-permute-done.8 = bf16[280,256]{1,0:T(8,128)(2,1)S(1)} collective-permute-done((bf16[280,256]{1,0:T(8,128)(2,1)S(1)}, bf16[280,256]{1,0:T(8,128)(2,1)S(1)}, u32[]{:S(2)}, u32[]{:S(2)}) %collective-permute-start.8) | collective-permute-done | bytes 143392 | tf_op jit(solution)/shard_map/ppermute | solution.py:45
  53.4 0.7 collective-permute-start.10
  54.1 3.5 %collective-permute-start.11 = (f32[72,256]{1,0:T(8,128)S(1)}, f32[72,256]{1,0:T(8,128)S(1)}, u32[]{:S(2)}, u32[]{:S(2)}) collective-permute-start(f32[72,256]{1,0:T(8,128)S(1)} %get-tuple-element.73), channel_id=1, source_target_pairs={{0,16},{2,18},{4,20},{6,22},{8,24},{10,26},{12,28},{14,30},{16,0},... | collective-permute-start | bytes 221192 | tf_op jit(solution)/shard_map/ppermute | solution.py:45
  58.0 3.5 %collective-permute-done.11 = f32[72,256]{1,0:T(8,128)S(1)} collective-permute-done((f32[72,256]{1,0:T(8,128)S(1)}, f32[72,256]{1,0:T(8,128)S(1)}, u32[]{:S(2)}, u32[]{:S(2)}) %collective-permute-start.11) | collective-permute-done | bytes 73760 | tf_op jit(solution)/shard_map/ppermute | solution.py:45
  61.5 2.2 %collective-permute-done.12 = f32[72,256]{1,0:T(8,128)S(1)} collective-permute-done((f32[72,256]{1,0:T(8,128)S(1)}, f32[72,256]{1,0:T(8,128)S(1)}, u32[]{:S(2)}, u32[]{:S(2)}) %collective-permute-start.12) | collective-permute-done | bytes 73760 | tf_op jit(solution)/shard_map/ppermute | solution.py:45
  63.9 1.1 collective-permute-done.13
  65.9 1.4 %collective-permute-start.17 = (bf16[1,64,256]{2,1,0:T(8,128)(2,1)S(1)}, bf16[1,64,256]{2,1,0:T(8,128)(2,1)}, u32[]{:S(2)}, u32[]{:S(2)}) collective-permute-start(bf16[1,64,256]{2,1,0:T(8,128)(2,1)S(1)} %get-tuple-element.22), channel_id=1, source_target_pairs={{0,16},{2,18},{4,20},{6,22},{8,24},{10,26},{12,28},{14,30},{16,0},... | collective-permute-start | bytes 98312 | tf_op jit(solution)/shard_map/ppermute | solution.py:45
  67.3 2.9 %collective-permute-start.16 = (bf16[1,64,256]{2,1,0:T(8,128)(2,1)S(1)}, bf16[1,64,256]{2,1,0:T(8,128)(2,1)}, u32[]{:S(2)}, u32[]{:S(2)}) collective-permute-start(bf16[1,64,256]{2,1,0:T(8,128)(2,1)S(1)} %get-tuple-element.22), channel_id=1, source_target_pairs={{0,24},{2,26},{4,28},{6,30},{8,16},{10,18},{12,20},{14,22},{16,8},... | collective-permute-start | bytes 98312 | tf_op jit(solution)/shard_map/ppermute | solution.py:45
  70.8 0.7 reduce_sum.255
  71.6 0.6 reduce_sum.261
  72.9 0.8 fusion.52
  74.0 0.8 select_bitcast_fusion.15
  74.8 0.8 collective-permute-start.21
  75.6 1.4 %collective-permute-start.20 = (bf16[4,64,256]{2,1,0:T(8,128)(2,1)S(1)}, bf16[4,64,256]{2,1,0:T(8,128)(2,1)S(1)}, u32[]{:S(2)}, u32[]{:S(2)}) collective-permute-start(bf16[4,64,256]{2,1,0:T(8,128)(2,1)S(1)} %maximum_bitcast_fusion.1), channel_id=1, source_target_pairs={{0,4},{2,6},{4,0},{6,2},{8,12},{10,14},{12,8},{14,10},{16,20},{18,... | collective-permute-start | bytes 393224 | tf_op jit(solution)/shard_map/ppermute | solution.py:45
  77.0 1.3 %collective-permute-start.19 = (bf16[4,64,256]{2,1,0:T(8,128)(2,1)S(1)}, bf16[4,64,256]{2,1,0:T(8,128)(2,1)S(1)}, u32[]{:S(2)}, u32[]{:S(2)}) collective-permute-start(bf16[4,64,256]{2,1,0:T(8,128)(2,1)S(1)} %maximum_bitcast_fusion.1), channel_id=1, source_target_pairs={{0,6},{2,4},{4,2},{6,0},{8,14},{10,12},{12,10},{14,8},{16,22},{18,... | collective-permute-start | bytes 393224 | tf_op jit(solution)/shard_map/ppermute | solution.py:45
  78.9 2.3 %collective-permute-done.21 = bf16[4,64,256]{2,1,0:T(8,128)(2,1)S(1)} collective-permute-done((bf16[4,64,256]{2,1,0:T(8,128)(2,1)S(1)}, bf16[4,64,256]{2,1,0:T(8,128)(2,1)S(1)}, u32[]{:S(2)}, u32[]{:S(2)}) %collective-permute-start.21) | collective-permute-done | bytes 131104 | tf_op jit(solution)/shard_map/ppermute | solution.py:45
  81.2 2.6 %collective-permute-done.20 = bf16[4,64,256]{2,1,0:T(8,128)(2,1)S(1)} collective-permute-done((bf16[4,64,256]{2,1,0:T(8,128)(2,1)S(1)}, bf16[4,64,256]{2,1,0:T(8,128)(2,1)S(1)}, u32[]{:S(2)}, u32[]{:S(2)}) %collective-permute-start.20) | collective-permute-done | bytes 131104 | tf_op jit(solution)/shard_map/ppermute | solution.py:45
  84.0 1.1 select_bitcast_fusion.1
  85.5 1.5 %fusion.5 = (f32[256]{0:T(256)S(1)}, f32[768,256]{1,0:T(8,128)}) fusion(bf16[1,2,384,256]{3,2,1,0:T(8,128)(2,1)S(1)} %pad_maximum_fusion.3, bf16[768,256]{1,0:T(8,128)(2,1)S(1)} %bitcast.248, f32[768]{0:T(1024)S(1)} %mul.194, bf16[768,1024]{1,0:T(8,128)(2,1)S(1)} %bitcast.222, bf16[1024,256]{1,0:T(8,128)(2,1)S(1)} %bitcast.230), kind=kOutput, calls=%fused_computation.19 | convolution fusion | flops 403832576 | bytes 3674112 | tf_op jit(solution)/shard_map/dot_general | solution.py:161
  86.9 1.7 %fusion.3 = (f32[256]{0:T(256)S(1)}, f32[1024,256]{1,0:T(8,128)}) fusion(bf16[4,4,64,256]{3,2,1,0:T(8,128)(2,1)S(1)} %copy.38, bf16[1024,256]{1,0:T(8,128)(2,1)S(1)} %bitcast.231, f32[1024]{0:T(1024)S(1)} %bitcast.252, bf16[1024,768]{0,1:T(8,128)(2,1)S(1)} %bitcast.220, bf16[768,256]{1,0:T(8,128)(2,1)S(1)} %bitcast.249), kind=kOutput, calls=%fused_computation.13 | convolution fusion | flops 404225792 | bytes 4068352 | tf_op jit(solution)/shard_map/dot_general | solution.py:163
  89.2 1.2 %dynamic-slice_convert_fusion.4 = (bf16[2,2,1,1,64,256]{5,4,3,2,1,0:T(8,128)(2,1)S(1)}, bf16[2,2,1,1,64,256]{5,4,3,2,1,0:T(8,128)(2,1)S(1)}, bf16[2,2,1,1,64,256]{5,4,3,2,1,0:T(8,128)(2,1)S(1)}) fusion(f32[2,2,2,2,64,256]{5,4,3,2,1,0:T(8,128)} %bitcast.244, s32[]{:T(128)S(6)} %select_n.385, s32[]{:T(128)S(6)} %select_n.387, s32[]{:T(128)S(6)} %select_n.393, ...), kind=kLoop, calls=%fused_computation.55 | loop fusion | bytes 786456 | tf_op jit(solution)/shard_map/convert_element_type | solution.py:90
  90.4 1.3 %collective-permute-start.22 = (bf16[280,256]{1,0:T(8,128)(2,1)S(1)}, bf16[280,256]{1,0:T(8,128)(2,1)S(1)}, u32[]{:S(2)}, u32[]{:S(2)}) collective-permute-start(bf16[280,256]{1,0:T(8,128)(2,1)S(1)} %get-tuple-element.63), channel_id=1, source_target_pairs={{0,2},{2,0},{4,6},{6,4},{8,10},{10,8},{12,14},{14,12},{16,18},{18,... | collective-permute-start | bytes 430088 | tf_op jit(solution)/shard_map/ppermute | solution.py:45
  91.7 0.8 collective-permute-start.23
  92.5 1.4 %collective-permute-start.24 = (bf16[280,256]{1,0:T(8,128)(2,1)S(1)}, bf16[280,256]{1,0:T(8,128)(2,1)S(1)}, u32[]{:S(2)}, u32[]{:S(2)}) collective-permute-start(bf16[280,256]{1,0:T(8,128)(2,1)S(1)} %get-tuple-element.65), channel_id=1, source_target_pairs={{0,6},{2,4},{4,2},{6,0},{8,14},{10,12},{12,10},{14,8},{16,22},{18,... | collective-permute-start | bytes 430088 | tf_op jit(solution)/shard_map/ppermute | solution.py:45
  94.0 1.0 constant_dynamic-slice_fusion
  94.9 1.8 %collective-permute-done.22 = bf16[280,256]{1,0:T(8,128)(2,1)S(1)} collective-permute-done((bf16[280,256]{1,0:T(8,128)(2,1)S(1)}, bf16[280,256]{1,0:T(8,128)(2,1)S(1)}, u32[]{:S(2)}, u32[]{:S(2)}) %collective-permute-start.22) | collective-permute-done | bytes 143392 | tf_op jit(solution)/shard_map/ppermute | solution.py:45
  96.7 2.7 %collective-permute-done.23 = bf16[280,256]{1,0:T(8,128)(2,1)S(1)} collective-permute-done((bf16[280,256]{1,0:T(8,128)(2,1)S(1)}, bf16[280,256]{1,0:T(8,128)(2,1)S(1)}, u32[]{:S(2)}, u32[]{:S(2)}) %collective-permute-start.23) | collective-permute-done | bytes 143392 | tf_op jit(solution)/shard_map/ppermute | solution.py:45
  99.8 1.3 %collective-permute-start.26 = (f32[72,256]{1,0:T(8,128)S(1)}, f32[72,256]{1,0:T(8,128)S(1)}, u32[]{:S(2)}, u32[]{:S(2)}) collective-permute-start(f32[72,256]{1,0:T(8,128)S(1)} %get-tuple-element.70), channel_id=1, source_target_pairs={{0,16},{2,18},{4,20},{6,22},{8,24},{10,26},{12,28},{14,30},{16,0},... | collective-permute-start | bytes 221192 | tf_op jit(solution)/shard_map/ppermute | solution.py:45
  101.2 3.1 %collective-permute-start.27 = (f32[72,256]{1,0:T(8,128)S(1)}, f32[72,256]{1,0:T(8,128)S(1)}, u32[]{:S(2)}, u32[]{:S(2)}) collective-permute-start(f32[72,256]{1,0:T(8,128)S(1)} %get-tuple-element.71), channel_id=1, source_target_pairs={{0,24},{2,26},{4,28},{6,30},{8,16},{10,18},{12,20},{14,22},{16,8},... | collective-permute-start | bytes 221192 | tf_op jit(solution)/shard_map/ppermute | solution.py:45
  104.2 1.0 fusion.23
  105.8 1.7 %collective-permute-done.27 = f32[72,256]{1,0:T(8,128)S(1)} collective-permute-done((f32[72,256]{1,0:T(8,128)S(1)}, f32[72,256]{1,0:T(8,128)S(1)}, u32[]{:S(2)}, u32[]{:S(2)}) %collective-permute-start.27) | collective-permute-done | bytes 73760 | tf_op jit(solution)/shard_map/ppermute | solution.py:45
  107.5 1.1 collective-permute-done.28
  109.1 0.7 fusion.34
  109.8 2.1 %fusion.11 = (f32[1,384,256]{2,1,0:T(8,128)}, f32[1,384,256]{2,1,0:T(8,128)}) fusion(f32[384,256]{1,0:T(8,128)S(1)} %get-tuple-element.21, f32[384,256]{1,0:T(8,128)S(1)} %reshape.294, bf16[384,256]{1,0:T(8,128)(2,1)S(1)} %collective-permute-done.29, f32[2,384,256]{2,1,0:T(8,128)} %bitcast.241, s32[]{:T(128)S(6)} %select_n.412, f32[256]{0:T(256)S(1)} %mul.220, ...), kind=kLoop, calls=%fused_computation.30 | loop fusion | flops 1671168 | bytes 3542020 | tf_op jit(solution)/shard_map/broadcast_in_dim | solution.py:222
  (183 shorter events, 12.2 us)
Async XLA Ops:
  0.6 10.7 %copy-start = (f32[64,64]{1,0:T(8,128)S(1)}, f32[64,64]{1,0:T(8,128)}, u32[]{:S(2)}) copy-start(f32[64,64]{1,0:T(8,128)} %param.9) | copy-start | bytes 49156
  3.6 20.2 %collective-permute-start.2 = (bf16[1,64,256]{2,1,0:T(8,128)(2,1)S(1)}, bf16[1,64,256]{2,1,0:T(8,128)(2,1)}, u32[]{:S(2)}, u32[]{:S(2)}) collective-permute-start(bf16[1,64,256]{2,1,0:T(8,128)(2,1)S(1)} %get-tuple-element.62), channel_id=1, source_target_pairs={{0,8},{2,10},{4,12},{6,14},{8,0},{10,2},{12,4},{14,6},{16,24},{18,... | collective-permute-start | bytes 98312 | tf_op jit(solution)/shard_map/ppermute | solution.py:45
  6.7 17.2 %collective-permute-start.1 = (bf16[1,64,256]{2,1,0:T(8,128)(2,1)S(1)}, bf16[1,64,256]{2,1,0:T(8,128)(2,1)}, u32[]{:S(2)}, u32[]{:S(2)}) collective-permute-start(bf16[1,64,256]{2,1,0:T(8,128)(2,1)S(1)} %get-tuple-element.62), channel_id=1, source_target_pairs={{0,16},{2,18},{4,20},{6,22},{8,24},{10,26},{12,28},{14,30},{16,0},... | collective-permute-start | bytes 98312 | tf_op jit(solution)/shard_map/ppermute | solution.py:45
  9.3 14.6 %collective-permute-start = (bf16[1,64,256]{2,1,0:T(8,128)(2,1)S(1)}, bf16[1,64,256]{2,1,0:T(8,128)(2,1)}, u32[]{:S(2)}, u32[]{:S(2)}) collective-permute-start(bf16[1,64,256]{2,1,0:T(8,128)(2,1)S(1)} %get-tuple-element.62), channel_id=1, source_target_pairs={{0,24},{2,26},{4,28},{6,30},{8,16},{10,18},{12,20},{14,22},{16,8},... | collective-permute-start | bytes 98312 | tf_op jit(solution)/shard_map/ppermute | solution.py:45
  11.4 7.6 %copy-start.28 = (s32[1,1,12,2]{2,3,1,0:T(2,128)S(1)}, s32[1,1,12,2]{2,3,1,0:T(2,128)}, u32[]{:S(2)}) copy-start(s32[1,1,12,2]{2,3,1,0:T(2,128)} %param.12) | copy-start | bytes 292
  11.4 17.5 %copy-start.1 = (s32[1,1,12,256,256]{4,3,2,1,0:T(8,128)S(1)}, s32[1,1,12,256,256]{4,3,2,1,0:T(8,128)}, u32[]{:S(2)}) copy-start(s32[1,1,12,256,256]{4,3,2,1,0:T(8,128)} %param.11) | copy-start | bytes 9437188
  18.3 18.8 %collective-permute-start.3 = (bf16[1,384,256]{2,1,0:T(8,128)(2,1)S(1)}, bf16[1,384,256]{2,1,0:T(8,128)(2,1)}, u32[]{:S(2)}, u32[]{:S(2)}) collective-permute-start(bf16[1,384,256]{2,1,0:T(8,128)(2,1)S(1)} %get-tuple-element.41), channel_id=1, source_target_pairs={{0,1},{1,0},{2,3},{3,2},{4,5},{5,4},{6,7},{7,6},{8,9},{9,8},{10,11... | collective-permute-start | bytes 589832 | tf_op jit(solution)/shard_map/ppermute | solution.py:45
  25.4 8.1 %collective-permute-start.6 = (bf16[4,64,256]{2,1,0:T(8,128)(2,1)}, bf16[4,64,256]{2,1,0:T(8,128)(2,1)}, u32[]{:S(2)}, u32[]{:S(2)}) collective-permute-start(bf16[4,64,256]{2,1,0:T(8,128)(2,1)} %maximum_bitcast_fusion), channel_id=1, source_target_pairs={{0,2},{2,0},{4,6},{6,4},{8,10},{10,8},{12,14},{14,12},{16,18},{18,... | collective-permute-start | bytes 393224 | tf_op jit(solution)/shard_map/ppermute | solution.py:45
  27.1 8.8 %collective-permute-start.5 = (bf16[4,64,256]{2,1,0:T(8,128)(2,1)}, bf16[4,64,256]{2,1,0:T(8,128)(2,1)}, u32[]{:S(2)}, u32[]{:S(2)}) collective-permute-start(bf16[4,64,256]{2,1,0:T(8,128)(2,1)} %maximum_bitcast_fusion), channel_id=1, source_target_pairs={{0,4},{2,6},{4,0},{6,2},{8,12},{10,14},{12,8},{14,10},{16,20},{18,... | collective-permute-start | bytes 393224 | tf_op jit(solution)/shard_map/ppermute | solution.py:45
  28.6 7.2 %collective-permute-start.4 = (bf16[4,64,256]{2,1,0:T(8,128)(2,1)}, bf16[4,64,256]{2,1,0:T(8,128)(2,1)}, u32[]{:S(2)}, u32[]{:S(2)}) collective-permute-start(bf16[4,64,256]{2,1,0:T(8,128)(2,1)} %maximum_bitcast_fusion), channel_id=1, source_target_pairs={{0,6},{2,4},{4,2},{6,0},{8,14},{10,12},{12,10},{14,8},{16,22},{18,... | collective-permute-start | bytes 393224 | tf_op jit(solution)/shard_map/ppermute | solution.py:45
  29.5 0.6 copy-start.21
  29.5 0.7 copy-start.24
  32.6 5.6 %copy-start.4 = (bf16[96,8,4,256]{3,1,2,0:T(8,128)(2,1)}, bf16[96,8,4,256]{3,1,2,0:T(8,128)(2,1)S(1)}, u32[]{:S(2)}) copy-start(bf16[96,8,4,256]{3,1,2,0:T(8,128)(2,1)S(1)} %copy.48) | copy-start | bytes 4718596
  33.5 6.7 %copy-start.6 = (bf16[96,8,4,256]{3,1,2,0:T(8,128)(2,1)}, bf16[96,8,4,256]{3,1,2,0:T(8,128)(2,1)S(1)}, u32[]{:S(2)}) copy-start(bf16[96,8,4,256]{3,1,2,0:T(8,128)(2,1)S(1)} %copy.50) | copy-start | bytes 4718596
  38.1 1.8 %copy-start.19 = (bf16[1,2,384,256]{3,2,1,0:T(8,128)(2,1)}, bf16[1,2,384,256]{3,2,1,0:T(8,128)(2,1)S(1)}, u32[]{:S(2)}) copy-start(bf16[1,2,384,256]{3,2,1,0:T(8,128)(2,1)S(1)} %pad_maximum_fusion.2) | copy-start | bytes 1179652
  40.1 2.0 %copy-start.26 = (f32[4]{0:T(128)S(1)}, f32[4]{0:T(128)}, u32[]{:S(2)}) copy-start(f32[4]{0:T(128)} %reduce_sum.195) | copy-start | bytes 52
  40.1 2.0 %copy-start.27 = (f32[4]{0:T(128)S(1)}, f32[4]{0:T(128)}, u32[]{:S(2)}) copy-start(f32[4]{0:T(128)} %reduce_sum.192) | copy-start | bytes 52
  40.1 2.0 %copy-start.30 = (f32[4]{0:T(128)S(1)}, f32[4]{0:T(128)}, u32[]{:S(2)}) copy-start(f32[4]{0:T(128)} %add.304) | copy-start | bytes 52
  41.9 30.4 %copy-start.8 = (f32[768,256]{1,0:T(8,128)}, f32[768,256]{1,0:T(8,128)S(1)}, u32[]{:S(2)}) copy-start(f32[768,256]{1,0:T(8,128)S(1)} %get-tuple-element.84) | copy-start | bytes 2359300
  41.9 5.4 %copy-start.2 = (f32[1536,64]{1,0:T(8,128)S(1)}, f32[1536,64]{1,0:T(8,128)}, u32[]{:S(2)}) copy-start(f32[1536,64]{1,0:T(8,128)} %fusion.50) | copy-start | bytes 1179652
  43.6 5.8 %collective-permute-start.7 = (bf16[280,256]{1,0:T(8,128)(2,1)S(1)}, bf16[280,256]{1,0:T(8,128)(2,1)S(1)}, u32[]{:S(2)}, u32[]{:S(2)}) collective-permute-start(bf16[280,256]{1,0:T(8,128)(2,1)S(1)} %get-tuple-element.66), channel_id=1, source_target_pairs={{0,2},{2,0},{4,6},{6,4},{8,10},{10,8},{12,14},{14,12},{16,18},{18,... | collective-permute-start | bytes 430088 | tf_op jit(solution)/shard_map/ppermute | solution.py:45
  44.9 8.2 %collective-permute-start.8 = (bf16[280,256]{1,0:T(8,128)(2,1)S(1)}, bf16[280,256]{1,0:T(8,128)(2,1)S(1)}, u32[]{:S(2)}, u32[]{:S(2)}) collective-permute-start(bf16[280,256]{1,0:T(8,128)(2,1)S(1)} %get-tuple-element.67), channel_id=1, source_target_pairs={{0,4},{2,6},{4,0},{6,2},{8,12},{10,14},{12,8},{14,10},{16,20},{18,... | collective-permute-start | bytes 430088 | tf_op jit(solution)/shard_map/ppermute | solution.py:45
  45.7 7.4 %collective-permute-start.9 = (bf16[280,256]{1,0:T(8,128)(2,1)S(1)}, bf16[280,256]{1,0:T(8,128)(2,1)S(1)}, u32[]{:S(2)}, u32[]{:S(2)}) collective-permute-start(bf16[280,256]{1,0:T(8,128)(2,1)S(1)} %get-tuple-element.68), channel_id=1, source_target_pairs={{0,6},{2,4},{4,2},{6,0},{8,14},{10,12},{12,10},{14,8},{16,22},{18,... | collective-permute-start | bytes 430088 | tf_op jit(solution)/shard_map/ppermute | solution.py:45
  47.3 18.5 %copy-start.15 = (f32[64,256]{1,0:T(8,128)}, f32[64,256]{1,0:T(8,128)S(1)}, u32[]{:S(2)}) copy-start(f32[64,256]{1,0:T(8,128)S(1)} %reshape.289) | copy-start | bytes 196612
  53.1 12.7 %copy-start.10 = (f32[1,64,256]{2,1,0:T(8,128)S(1)}, f32[1,64,256]{2,1,0:T(8,128)}, u32[]{:S(2)}) copy-start(f32[1,64,256]{2,1,0:T(8,128)} %param.8) | copy-start | bytes 196612
  53.2 17.1 %copy-start.20 = (f32[64,64]{1,0:T(8,128)S(1)}, f32[64,64]{1,0:T(8,128)}, u32[]{:S(2)}) copy-start(f32[64,64]{1,0:T(8,128)} %param.10) | copy-start | bytes 49156
  53.3 18.9 %copy-start.3 = (f32[1,384,256]{2,1,0:T(8,128)S(1)}, f32[1,384,256]{2,1,0:T(8,128)}, u32[]{:S(2)}) copy-start(f32[1,384,256]{2,1,0:T(8,128)} %param.7) | copy-start | bytes 1179652
  53.4 4.6 %collective-permute-start.10 = (f32[72,256]{1,0:T(8,128)S(1)}, f32[72,256]{1,0:T(8,128)S(1)}, u32[]{:S(2)}, u32[]{:S(2)}) collective-permute-start(f32[72,256]{1,0:T(8,128)S(1)} %get-tuple-element.72), channel_id=1, source_target_pairs={{0,8},{2,10},{4,12},{6,14},{8,0},{10,2},{12,4},{14,6},{16,24},{18,... | collective-permute-start | bytes 221192 | tf_op jit(solution)/shard_map/ppermute | solution.py:45
  54.1 7.4 %collective-permute-start.11 = (f32[72,256]{1,0:T(8,128)S(1)}, f32[72,256]{1,0:T(8,128)S(1)}, u32[]{:S(2)}, u32[]{:S(2)}) collective-permute-start(f32[72,256]{1,0:T(8,128)S(1)} %get-tuple-element.73), channel_id=1, source_target_pairs={{0,16},{2,18},{4,20},{6,22},{8,24},{10,26},{12,28},{14,30},{16,0},... | collective-permute-start | bytes 221192 | tf_op jit(solution)/shard_map/ppermute | solution.py:45
  57.6 6.2 %collective-permute-start.12 = (f32[72,256]{1,0:T(8,128)S(1)}, f32[72,256]{1,0:T(8,128)S(1)}, u32[]{:S(2)}, u32[]{:S(2)}) collective-permute-start(f32[72,256]{1,0:T(8,128)S(1)} %get-tuple-element.74), channel_id=1, source_target_pairs={{0,24},{2,26},{4,28},{6,30},{8,16},{10,18},{12,20},{14,22},{16,8},... | collective-permute-start | bytes 221192 | tf_op jit(solution)/shard_map/ppermute | solution.py:45
  57.9 14.4 %collective-permute-start.14 = (bf16[384,256]{1,0:T(8,128)(2,1)S(1)}, bf16[384,256]{1,0:T(8,128)(2,1)S(1)}, u32[]{:S(2)}, u32[]{:S(2)}) collective-permute-start(bf16[384,256]{1,0:T(8,128)(2,1)S(1)} %fusion.22), channel_id=1, source_target_pairs={{0,1},{1,0},{2,3},{3,2},{4,5},{5,4},{6,7},{7,6},{8,9},{9,8},{10,11... | collective-permute-start | bytes 589832 | tf_op jit(solution)/shard_map/ppermute | solution.py:45
  63.8 8.8 %copy-start.17 = (f32[72,256]{1,0:T(8,128)}, f32[72,256]{1,0:T(8,128)S(1)}, u32[]{:S(2)}) copy-start(f32[72,256]{1,0:T(8,128)S(1)} %fusion.29) | copy-start | bytes 221188
  63.8 1.2 %collective-permute-start.13 = (f32[8]{0:T(128)S(1)}, f32[8]{0:T(128)S(1)}, u32[]{:S(2)}, u32[]{:S(2)}) collective-permute-start(f32[8]{0:T(128)S(1)} %slice_bitcast_fusion.1), channel_id=1, source_target_pairs={{0,1},{1,0},{2,3},{3,2},{4,5},{5,4},{6,7},{7,6},{8,9},{9,8},{10,11... | collective-permute-start | bytes 104 | tf_op jit(solution)/shard_map/ppermute | solution.py:45
  65.0 0.5 copy-start.22
  65.8 8.1 %collective-permute-start.18 = (bf16[1,64,256]{2,1,0:T(8,128)(2,1)S(1)}, bf16[1,64,256]{2,1,0:T(8,128)(2,1)}, u32[]{:S(2)}, u32[]{:S(2)}) collective-permute-start(bf16[1,64,256]{2,1,0:T(8,128)(2,1)S(1)} %get-tuple-element.22), channel_id=1, source_target_pairs={{0,8},{2,10},{4,12},{6,14},{8,0},{10,2},{12,4},{14,6},{16,24},{18,... | collective-permute-start | bytes 98312 | tf_op jit(solution)/shard_map/ppermute | solution.py:45
  65.9 8.1 %collective-permute-start.17 = (bf16[1,64,256]{2,1,0:T(8,128)(2,1)S(1)}, bf16[1,64,256]{2,1,0:T(8,128)(2,1)}, u32[]{:S(2)}, u32[]{:S(2)}) collective-permute-start(bf16[1,64,256]{2,1,0:T(8,128)(2,1)S(1)} %get-tuple-element.22), channel_id=1, source_target_pairs={{0,16},{2,18},{4,20},{6,22},{8,24},{10,26},{12,28},{14,30},{16,0},... | collective-permute-start | bytes 98312 | tf_op jit(solution)/shard_map/ppermute | solution.py:45
  67.3 6.6 %collective-permute-start.16 = (bf16[1,64,256]{2,1,0:T(8,128)(2,1)S(1)}, bf16[1,64,256]{2,1,0:T(8,128)(2,1)}, u32[]{:S(2)}, u32[]{:S(2)}) collective-permute-start(bf16[1,64,256]{2,1,0:T(8,128)(2,1)S(1)} %get-tuple-element.22), channel_id=1, source_target_pairs={{0,24},{2,26},{4,28},{6,30},{8,16},{10,18},{12,20},{14,22},{16,8},... | collective-permute-start | bytes 98312 | tf_op jit(solution)/shard_map/ppermute | solution.py:45
  70.7 1.9 %copy-start.13 = (f32[64,256]{1,0:T(8,128)}, f32[64,256]{1,0:T(8,128)S(1)}, u32[]{:S(2)}) copy-start(f32[64,256]{1,0:T(8,128)S(1)} %reshape.296) | copy-start | bytes 196612
  72.2 0.7 copy-start.11
  72.3 11.7 %collective-permute-start.15 = (bf16[1,384,256]{2,1,0:T(8,128)(2,1)S(1)}, bf16[1,384,256]{2,1,0:T(8,128)(2,1)}, u32[]{:S(2)}, u32[]{:S(2)}) collective-permute-start(bf16[1,384,256]{2,1,0:T(8,128)(2,1)S(1)} %get-tuple-element.20), channel_id=1, source_target_pairs={{0,1},{1,0},{2,3},{3,2},{4,5},{5,4},{6,7},{7,6},{8,9},{9,8},{10,11... | collective-permute-start | bytes 589832 | tf_op jit(solution)/shard_map/ppermute | solution.py:45
  73.7 5.2 %copy-start.29 = (f32[4]{0:T(128)S(1)}, f32[4]{0:T(128)}, u32[]{:S(2)}) copy-start(f32[4]{0:T(128)} %reduce_sum.255) | copy-start | bytes 52
  74.8 6.4 %collective-permute-start.21 = (bf16[4,64,256]{2,1,0:T(8,128)(2,1)S(1)}, bf16[4,64,256]{2,1,0:T(8,128)(2,1)S(1)}, u32[]{:S(2)}, u32[]{:S(2)}) collective-permute-start(bf16[4,64,256]{2,1,0:T(8,128)(2,1)S(1)} %maximum_bitcast_fusion.1), channel_id=1, source_target_pairs={{0,2},{2,0},{4,6},{6,4},{8,10},{10,8},{12,14},{14,12},{16,18},{18,... | collective-permute-start | bytes 393224 | tf_op jit(solution)/shard_map/ppermute | solution.py:45
  75.6 8.1 %collective-permute-start.20 = (bf16[4,64,256]{2,1,0:T(8,128)(2,1)S(1)}, bf16[4,64,256]{2,1,0:T(8,128)(2,1)S(1)}, u32[]{:S(2)}, u32[]{:S(2)}) collective-permute-start(bf16[4,64,256]{2,1,0:T(8,128)(2,1)S(1)} %maximum_bitcast_fusion.1), channel_id=1, source_target_pairs={{0,4},{2,6},{4,0},{6,2},{8,12},{10,14},{12,8},{14,10},{16,20},{18,... | collective-permute-start | bytes 393224 | tf_op jit(solution)/shard_map/ppermute | solution.py:45
  77.0 6.8 %collective-permute-start.19 = (bf16[4,64,256]{2,1,0:T(8,128)(2,1)S(1)}, bf16[4,64,256]{2,1,0:T(8,128)(2,1)S(1)}, u32[]{:S(2)}, u32[]{:S(2)}) collective-permute-start(bf16[4,64,256]{2,1,0:T(8,128)(2,1)S(1)} %maximum_bitcast_fusion.1), channel_id=1, source_target_pairs={{0,6},{2,4},{4,2},{6,0},{8,14},{10,12},{12,10},{14,8},{16,22},{18,... | collective-permute-start | bytes 393224 | tf_op jit(solution)/shard_map/ppermute | solution.py:45
  84.0 1.5 %copy-start.7 = (bf16[96,8,4,256]{3,1,2,0:T(8,128)(2,1)S(1)}, bf16[96,8,4,256]{3,1,2,0:T(8,128)(2,1)}, u32[]{:S(2)}) copy-start(bf16[96,8,4,256]{3,1,2,0:T(8,128)(2,1)} %copy-done.6) | copy-start | bytes 4718596
  85.5 1.5 %copy-start.5 = (bf16[96,8,4,256]{3,1,2,0:T(8,128)(2,1)S(1)}, bf16[96,8,4,256]{3,1,2,0:T(8,128)(2,1)}, u32[]{:S(2)}) copy-start(bf16[96,8,4,256]{3,1,2,0:T(8,128)(2,1)} %copy-done.4) | copy-start | bytes 4718596
  86.9 2.1 %copy-start.25 = (f32[4]{0:T(128)S(1)}, f32[4]{0:T(128)}, u32[]{:S(2)}) copy-start(f32[4]{0:T(128)} %reduce_sum.261) | copy-start | bytes 52
  90.4 6.3 %collective-permute-start.22 = (bf16[280,256]{1,0:T(8,128)(2,1)S(1)}, bf16[280,256]{1,0:T(8,128)(2,1)S(1)}, u32[]{:S(2)}, u32[]{:S(2)}) collective-permute-start(bf16[280,256]{1,0:T(8,128)(2,1)S(1)} %get-tuple-element.63), channel_id=1, source_target_pairs={{0,2},{2,0},{4,6},{6,4},{8,10},{10,8},{12,14},{14,12},{16,18},{18,... | collective-permute-start | bytes 430088 | tf_op jit(solution)/shard_map/ppermute | solution.py:45
  91.7 7.7 %collective-permute-start.23 = (bf16[280,256]{1,0:T(8,128)(2,1)S(1)}, bf16[280,256]{1,0:T(8,128)(2,1)S(1)}, u32[]{:S(2)}, u32[]{:S(2)}) collective-permute-start(bf16[280,256]{1,0:T(8,128)(2,1)S(1)} %get-tuple-element.64), channel_id=1, source_target_pairs={{0,4},{2,6},{4,0},{6,2},{8,12},{10,14},{12,8},{14,10},{16,20},{18,... | collective-permute-start | bytes 430088 | tf_op jit(solution)/shard_map/ppermute | solution.py:45
  92.5 6.9 %collective-permute-start.24 = (bf16[280,256]{1,0:T(8,128)(2,1)S(1)}, bf16[280,256]{1,0:T(8,128)(2,1)S(1)}, u32[]{:S(2)}, u32[]{:S(2)}) collective-permute-start(bf16[280,256]{1,0:T(8,128)(2,1)S(1)} %get-tuple-element.65), channel_id=1, source_target_pairs={{0,6},{2,4},{4,2},{6,0},{8,14},{10,12},{12,10},{14,8},{16,22},{18,... | collective-permute-start | bytes 430088 | tf_op jit(solution)/shard_map/ppermute | solution.py:45
  99.5 9.2 %copy-start.23 = (f32[8]{0:T(128)S(1)}, f32[8]{0:T(128)}, u32[]{:S(2)}) copy-start(f32[8]{0:T(128)} %copy-done.22) | copy-start | bytes 100
  99.5 9.6 %copy-start.14 = (f32[64,256]{1,0:T(8,128)S(1)}, f32[64,256]{1,0:T(8,128)}, u32[]{:S(2)}) copy-start(f32[64,256]{1,0:T(8,128)} %copy-done.13) | copy-start | bytes 196612
  99.5 9.6 %copy-start.16 = (f32[64,256]{1,0:T(8,128)S(1)}, f32[64,256]{1,0:T(8,128)}, u32[]{:S(2)}) copy-start(f32[64,256]{1,0:T(8,128)} %copy-done.15) | copy-start | bytes 196612
  99.5 9.6 %copy-start.18 = (f32[72,256]{1,0:T(8,128)S(1)}, f32[72,256]{1,0:T(8,128)}, u32[]{:S(2)}) copy-start(f32[72,256]{1,0:T(8,128)} %copy-done.17) | copy-start | bytes 221188
  99.6 10.1 %copy-start.9 = (f32[768,256]{1,0:T(8,128)S(1)}, f32[768,256]{1,0:T(8,128)}, u32[]{:S(2)}) copy-start(f32[768,256]{1,0:T(8,128)} %copy-done.8) | copy-start | bytes 2359300
  99.6 10.1 %copy-start.12 = (bf16[384,256]{1,0:T(8,128)(2,1)S(1)}, bf16[384,256]{1,0:T(8,128)(2,1)}, u32[]{:S(2)}) copy-start(bf16[384,256]{1,0:T(8,128)(2,1)} %copy-done.11) | copy-start | bytes 589828
  99.8 6.0 %collective-permute-start.25 = (f32[72,256]{1,0:T(8,128)S(1)}, f32[72,256]{1,0:T(8,128)S(1)}, u32[]{:S(2)}, u32[]{:S(2)}) collective-permute-start(f32[72,256]{1,0:T(8,128)S(1)} %get-tuple-element.69), channel_id=1, source_target_pairs={{0,8},{2,10},{4,12},{6,14},{8,0},{10,2},{12,4},{14,6},{16,24},{18,... | collective-permute-start | bytes 221192 | tf_op jit(solution)/shard_map/ppermute | solution.py:45
  99.8 5.9 %collective-permute-start.26 = (f32[72,256]{1,0:T(8,128)S(1)}, f32[72,256]{1,0:T(8,128)S(1)}, u32[]{:S(2)}, u32[]{:S(2)}) collective-permute-start(f32[72,256]{1,0:T(8,128)S(1)} %get-tuple-element.70), channel_id=1, source_target_pairs={{0,16},{2,18},{4,20},{6,22},{8,24},{10,26},{12,28},{14,30},{16,0},... | collective-permute-start | bytes 221192 | tf_op jit(solution)/shard_map/ppermute | solution.py:45
  101.2 6.3 %collective-permute-start.27 = (f32[72,256]{1,0:T(8,128)S(1)}, f32[72,256]{1,0:T(8,128)S(1)}, u32[]{:S(2)}, u32[]{:S(2)}) collective-permute-start(f32[72,256]{1,0:T(8,128)S(1)} %get-tuple-element.71), channel_id=1, source_target_pairs={{0,24},{2,26},{4,28},{6,30},{8,16},{10,18},{12,20},{14,22},{16,8},... | collective-permute-start | bytes 221192 | tf_op jit(solution)/shard_map/ppermute | solution.py:45
  105.2 4.5 %collective-permute-start.29 = (bf16[384,256]{1,0:T(8,128)(2,1)S(1)}, bf16[384,256]{1,0:T(8,128)(2,1)S(1)}, u32[]{:S(2)}, u32[]{:S(2)}) collective-permute-start(bf16[384,256]{1,0:T(8,128)(2,1)S(1)} %fusion.23), channel_id=1, source_target_pairs={{0,1},{1,0},{2,3},{3,2},{4,5},{5,4},{6,7},{7,6},{8,9},{9,8},{10,11... | collective-permute-start | bytes 589832 | tf_op jit(solution)/shard_map/ppermute | solution.py:45
  107.5 1.2 %collective-permute-start.28 = (f32[8]{0:T(128)S(1)}, f32[8]{0:T(128)S(1)}, u32[]{:S(2)}, u32[]{:S(2)}) collective-permute-start(f32[8]{0:T(128)S(1)} %slice_bitcast_fusion), channel_id=1, source_target_pairs={{0,1},{1,0},{2,3},{3,2},{4,5},{5,4},{6,7},{7,6},{8,9},{9,8},{10,11... | collective-permute-start | bytes 104 | tf_op jit(solution)/shard_map/ppermute | solution.py:45

commit v15 on v14

--- a/solution.py
+++ b/solution.py
@@ -79,8 +79,8 @@
                 out = lax.dynamic_index_in_dim(out, (value >> j) & 1, left.index(group[j]), keepdims=False)
             return out
 
-        coded = extra is not None and stage == 0 and first_type is not None
-        stage_type = first_type if (stage == 0 and first_type is not None) else send_type
+        coded = extra is not None and first_type is not None
+        stage_type = send_type if first_type is None else first_type
         total = block_of(digit)
         shape = total.shape
         if extra is not None:

time: 113 us -> 107 us (0.947)
  matrix products: 12.9 us -> 9.66 us
  other arithmetic: 18.2 us -> 16 us
  waiting for transfers between devices: 26.5 us -> 24.9 us
    dot_general x4, matrix products: 4.96 us -> 2.77 us  [prior_term(): mixed = jnp.dot(grouped, prior_mat, precision=top_prec)]
    ppermute x30, waiting for transfers between devices: 26.5 us -> 24.9 us  [swap_with(): return lax.ppermute(value, axis, pairs)]
    reshape x6, local copies, waits for them, and re-layouts: 2.85 us -> 4.23 us  [prior_term(): return mixed.reshape(row_total, DRAWS * DIM)]
    unnamed x65 -> x71, local copies, waits for them, and re-layouts: 2.32 us -> 3.11 us
    convert_element_type x4 -> x6, local copies, waits for them, and re-layouts: 3.53 us -> 4.1 us  [halve_sum(): send = block_of(digit ^ k).astype(stage_type)]
  transfers between devices with their start and end apart: 30 -> 30, of which waited for: 13 -> 13; matrix products, arithmetic and copies ran while one was open for 27% -> 25% of each run, Pallas kernels for 0% -> 0%
where the time goes in v15:
time: 107 us; the launch traced here: 106 us
  starting transfers between devices  33.6 us (31%)
  waiting for transfers between devices  24.9 us (23%)
  local copies, waits for them, and re-layouts  19.7 us (18%)
  other arithmetic  16 us (15%)
  matrix products  9.66 us (9%)
  between operations  2.17 us (2%)
    ppermute x30, starting transfers between devices, swap_with(): return lax.ppermute(value, axis, pairs)  33.6 us
    ppermute x30, waiting for transfers between devices, swap_with(): return lax.ppermute(value, axis, pairs)  24.9 us
    reduce_sum x16, other arithmetic, per_draw(): return jnp.sum(product, axis=(0, 2))  5.55 us
    another operation x11, other arithmetic, double_gather(): buf = jnp.stack(ordered, axis=1).reshape((-1,) + piece.shape)  5.05 us
    reshape x6, local copies, waits for them, and re-layouts, prior_term(): return mixed.reshape(row_total, DRAWS * DIM)  4.23 us
    convert_element_type x6, local copies, waits for them, and re-layouts, halve_sum(): send = block_of(digit ^ k).astype(stage_type)  4.1 us
    dot_general x2, matrix products, cross_parts(): to_items = jnp.dot(counts_t, user_range, preferred_element_type=jnp.float32)  3.52 us
    unnamed x71, local copies, waits for them, and re-layouts  3.11 us
  transfers between devices with their start and end apart: 30, of which 13 were waited for; matrix products, arithmetic and copies ran while one was open for 25% of the time, Pallas kernels for 0%

profile of v15, /device:TPU:0, one launch (start us, length us, event | category | flops | bytes accessed | tf_op | source)
XLA Modules:
  0.0 106.1 jit_solution(14787988066905154687)
XLA Ops:
  0.6 0.9 reshape_squeeze.7
  1.6 1.0 fusion.65
  2.7 0.9 multiply_reduce_fusion.7
  3.6 3.1 %collective-permute-start.2 = (bf16[1,64,256]{2,1,0:T(8,128)(2,1)S(1)}, bf16[1,64,256]{2,1,0:T(8,128)(2,1)}, u32[]{:S(2)}, u32[]{:S(2)}) collective-permute-start(bf16[1,64,256]{2,1,0:T(8,128)(2,1)S(1)} %get-tuple-element.70), channel_id=1, source_target_pairs={{0,8},{2,10},{4,12},{6,14},{8,0},{10,2},{12,4},{14,6},{16,24},{18,... | collective-permute-start | bytes 98312 | tf_op jit(solution)/shard_map/ppermute | solution.py:45
  6.7 2.6 %collective-permute-start.1 = (bf16[1,64,256]{2,1,0:T(8,128)(2,1)S(1)}, bf16[1,64,256]{2,1,0:T(8,128)(2,1)}, u32[]{:S(2)}, u32[]{:S(2)}) collective-permute-start(bf16[1,64,256]{2,1,0:T(8,128)(2,1)S(1)} %get-tuple-element.70), channel_id=1, source_target_pairs={{0,16},{2,18},{4,20},{6,22},{8,24},{10,26},{12,28},{14,30},{16,0},... | collective-permute-start | bytes 98312 | tf_op jit(solution)/shard_map/ppermute | solution.py:45
  9.3 1.2 %reshape_squeeze.6 = f32[1536,64]{1,0:T(8,128)S(1)} reshape(f32[1,384,256]{2,1,0:T(8,128)} %param.7) | data formatting | bytes 786432 | tf_op jit(solution)/shard_map/reshape;squeeze | solution.py:21
  10.5 0.8 fusion.64
  11.3 0.9 copy-done.2
  12.2 1.0 reshape.288
  13.1 2.0 %multiply_reduce_fusion.3 = (f32[256]{0:T(256)}, f32[256]{0:T(256)S(1)}, bf16[1,384,256]{2,1,0:T(8,128)(2,1)S(1)}) fusion(f32[1,384,256]{2,1,0:T(8,128)} %param.7, f32[1,384,256]{2,1,0:T(8,128)} %reshape.288), kind=kLoop, calls=%fused_computation.48 | loop fusion | flops 491008 | bytes 985088 | tf_op jit(solution)/shard_map/reduce_sum | solution.py:28
  16.5 0.7 reshape.295
  17.2 2.1 %reshape.293 = f32[384,256]{1,0:T(8,128)} reshape(f32[1536,64]{1,0:T(8,128)} %copy-done.2) | data formatting | bytes 786432 | tf_op jit(solution)/shard_map/reshape | solution.py:23
  19.3 0.6 copy.29
  20.3 0.8 reduce_sum.179
  21.4 0.8 select_bitcast_fusion.19
  22.2 1.8 %collective-permute-start.6 = (bf16[4,64,256]{2,1,0:T(8,128)(2,1)S(1)}, bf16[4,64,256]{2,1,0:T(8,128)(2,1)}, u32[]{:S(2)}, u32[]{:S(2)}) collective-permute-start(bf16[4,64,256]{2,1,0:T(8,128)(2,1)S(1)} %maximum_bitcast_fusion), channel_id=1, source_target_pairs={{0,2},{2,0},{4,6},{6,4},{8,10},{10,8},{12,14},{14,12},{16,18},{18,... | collective-permute-start | bytes 393224 | tf_op jit(solution)/shard_map/ppermute | solution.py:45
  24.0 1.5 %collective-permute-start.5 = (bf16[4,64,256]{2,1,0:T(8,128)(2,1)S(1)}, bf16[4,64,256]{2,1,0:T(8,128)(2,1)}, u32[]{:S(2)}, u32[]{:S(2)}) collective-permute-start(bf16[4,64,256]{2,1,0:T(8,128)(2,1)S(1)} %maximum_bitcast_fusion), channel_id=1, source_target_pairs={{0,4},{2,6},{4,0},{6,2},{8,12},{10,14},{12,8},{14,10},{16,20},{18,... | collective-permute-start | bytes 393224 | tf_op jit(solution)/shard_map/ppermute | solution.py:45
  25.8 0.6 convert_reduce_fusion.1
  27.1 1.3 %fusion = bf16[256,256,3,4]{1,3,2,0:T(4,128)(2,1)S(1)} fusion(bf16[12,256,256,1]{2,1,0,3:T(8,128)(2,1)S(1)} %convert_bitcast_fusion.2, pred[12,4]{0,1:T(4,128)(4,1)S(1)} %copy-done.27, pred[12,3]{0,1:T(4,128)(4,1)S(1)} %copy-done.28), kind=kOutput, calls=%fused_computation.2 | convolution fusion | flops 18874512 | bytes 3145812 | tf_op jit(solution)/shard_map/trc,tij->cjri/dot_general | solution.py:150
  28.6 0.5 copy.31
  30.4 2.1 %collective-permute-done.5 = bf16[4,64,256]{2,1,0:T(8,128)(2,1)} collective-permute-done((bf16[4,64,256]{2,1,0:T(8,128)(2,1)S(1)}, bf16[4,64,256]{2,1,0:T(8,128)(2,1)}, u32[]{:S(2)}, u32[]{:S(2)}) %collective-permute-start.5) | collective-permute-done | bytes 131104 | tf_op jit(solution)/shard_map/ppermute | solution.py:45
  32.6 1.1 %select_bitcast_fusion.11 = (bf16[4,1,64,256]{3,2,0,1:T(8,128)(2,1)S(1)}, bf16[4,1,64,256]{3,2,0,1:T(8,128)(2,1)S(1)}, bf16[4,1,64,256]{3,2,0,1:T(8,128)(2,1)S(1)}, bf16[4,1,64,256]{3,2,0,1:T(8,128)(2,1)S(1)}) fusion(bf16[4,64,256]{2,1,0:T(8,128)(2,1)} %collective-permute-done.4, bf16[4,64,256]{2,1,0:T(8,128)(2,1)} %collective-permute-done.5, ...), kind=kLoop, calls=%fused_computation.95 | loop fusion | flops 786432 | bytes 1048579 | tf_op jit(solution)/shard_map/stack | solution.py:128
  33.8 1.0 select_bitcast_fusion.3
  34.8 1.8 %fusion.2 = (f32[256]{0:T(256)S(1)}, f32[1024,256]{1,0:T(8,128)}) fusion(bf16[4,4,64,256]{3,2,1,0:T(8,128)(2,1)S(1)} %copy.32, bf16[1024,256]{1,0:T(8,128)(2,1)S(1)} %bitcast.230, f32[1024]{0:T(1024)S(1)} %bitcast.249, bf16[1024,768]{0,1:T(8,128)(2,1)S(1)} %bitcast.215, bf16[768,256]{1,0:T(8,128)(2,1)S(1)} %bitcast.244), kind=kOutput, calls=%fused_computation.12 | convolution fusion | flops 404225792 | bytes 4068352 | tf_op jit(solution)/shard_map/dot_general | solution.py:163
  36.8 0.6 fusion.4
  37.7 1.2 %dynamic-slice_convert_fusion.7 = (bf16[2,2,1,1,64,256]{5,4,3,2,1,0:T(8,128)(2,1)S(1)}, bf16[2,2,1,1,64,256]{5,4,3,2,1,0:T(8,128)(2,1)S(1)}, bf16[2,2,1,1,64,256]{5,4,3,2,1,0:T(8,128)(2,1)S(1)}) fusion(f32[2,2,2,2,64,256]{5,4,3,2,1,0:T(8,128)} %bitcast.242, s32[]{:T(128)S(6)} %select_n.385, s32[]{:T(128)S(6)} %select_n.387, s32[]{:T(128)S(6)} %select_n.393, ...), kind=kLoop, calls=%fused_computation.60 | loop fusion | bytes 786456 | tf_op jit(solution)/shard_map/convert_element_type | solution.py:90
  38.9 1.3 %collective-permute-start.7 = (bf16[280,256]{1,0:T(8,128)(2,1)S(1)}, bf16[280,256]{1,0:T(8,128)(2,1)S(1)}, u32[]{:S(2)}, u32[]{:S(2)}) collective-permute-start(bf16[280,256]{1,0:T(8,128)(2,1)S(1)} %get-tuple-element.80), channel_id=1, source_target_pairs={{0,2},{2,0},{4,6},{6,4},{8,10},{10,8},{12,14},{14,12},{16,18},{18,... | collective-permute-start | bytes 430088 | tf_op jit(solution)/shard_map/ppermute | solution.py:45
  40.2 0.8 collective-permute-start.8
  41.1 1.4 %collective-permute-start.9 = (bf16[280,256]{1,0:T(8,128)(2,1)S(1)}, bf16[280,256]{1,0:T(8,128)(2,1)S(1)}, u32[]{:S(2)}, u32[]{:S(2)}) collective-permute-start(bf16[280,256]{1,0:T(8,128)(2,1)S(1)} %get-tuple-element.82), channel_id=1, source_target_pairs={{0,6},{2,4},{4,2},{6,0},{8,14},{10,12},{12,10},{14,8},{16,22},{18,... | collective-permute-start | bytes 430088 | tf_op jit(solution)/shard_map/ppermute | solution.py:45
  42.6 1.0 constant_dynamic-slice_fusion.1
  43.6 1.2 %collective-permute-done.7 = bf16[280,256]{1,0:T(8,128)(2,1)S(1)} collective-permute-done((bf16[280,256]{1,0:T(8,128)(2,1)S(1)}, bf16[280,256]{1,0:T(8,128)(2,1)S(1)}, u32[]{:S(2)}, u32[]{:S(2)}) %collective-permute-start.7) | collective-permute-done | bytes 143392 | tf_op jit(solution)/shard_map/ppermute | solution.py:45
  44.8 3.6 %collective-permute-done.8 = bf16[280,256]{1,0:T(8,128)(2,1)S(1)} collective-permute-done((bf16[280,256]{1,0:T(8,128)(2,1)S(1)}, bf16[280,256]{1,0:T(8,128)(2,1)S(1)}, u32[]{:S(2)}, u32[]{:S(2)}) %collective-permute-start.8) | collective-permute-done | bytes 143392 | tf_op jit(solution)/shard_map/ppermute | solution.py:45
  48.6 0.8 collective-permute-start.10
  49.4 3.5 %collective-permute-start.11 = (bf16[88,256]{1,0:T(8,128)(2,1)S(1)}, bf16[88,256]{1,0:T(8,128)(2,1)S(1)}, u32[]{:S(2)}, u32[]{:S(2)}) collective-permute-start(bf16[88,256]{1,0:T(8,128)(2,1)S(1)} %get-tuple-element.78), channel_id=1, source_target_pairs={{0,16},{2,18},{4,20},{6,22},{8,24},{10,26},{12,28},{14,30},{16,0},... | collective-permute-start | bytes 135176 | tf_op jit(solution)/shard_map/ppermute | solution.py:45
  53.1 2.8 %collective-permute-done.11 = bf16[88,256]{1,0:T(8,128)(2,1)S(1)} collective-permute-done((bf16[88,256]{1,0:T(8,128)(2,1)S(1)}, bf16[88,256]{1,0:T(8,128)(2,1)S(1)}, u32[]{:S(2)}, u32[]{:S(2)}) %collective-permute-start.11) | collective-permute-done | bytes 45088 | tf_op jit(solution)/shard_map/ppermute | solution.py:45
  55.9 2.9 %collective-permute-done.12 = bf16[88,256]{1,0:T(8,128)(2,1)S(1)} collective-permute-done((bf16[88,256]{1,0:T(8,128)(2,1)S(1)}, bf16[88,256]{1,0:T(8,128)(2,1)S(1)}, u32[]{:S(2)}, u32[]{:S(2)}) %collective-permute-start.12) | collective-permute-done | bytes 45088 | tf_op jit(solution)/shard_map/ppermute | solution.py:45
  58.9 1.1 %collective-permute-done.13 = f32[8]{0:T(128)S(1)} collective-permute-done((f32[8]{0:T(128)S(1)}, f32[8]{0:T(128)S(1)}, u32[]{:S(2)}, u32[]{:S(2)}) %collective-permute-start.13) | collective-permute-done | bytes 64 | tf_op jit(solution)/shard_map/ppermute | solution.py:45
  60.8 1.0 collective-permute-start.17
  61.8 3.3 %collective-permute-start.16 = (bf16[1,64,256]{2,1,0:T(8,128)(2,1)S(1)}, bf16[1,64,256]{2,1,0:T(8,128)(2,1)}, u32[]{:S(2)}, u32[]{:S(2)}) collective-permute-start(bf16[1,64,256]{2,1,0:T(8,128)(2,1)S(1)} %get-tuple-element.24), channel_id=1, source_target_pairs={{0,24},{2,26},{4,28},{6,30},{8,16},{10,18},{12,20},{14,22},{16,8},... | collective-permute-start | bytes 98312 | tf_op jit(solution)/shard_map/ppermute | solution.py:45
  65.7 0.6 reduce_sum.255
  66.4 0.7 reduce_sum.261
  67.7 0.8 fusion.66
  68.8 0.8 select_bitcast_fusion.15
  69.6 0.8 collective-permute-start.21
  70.5 1.4 %collective-permute-start.20 = (bf16[4,64,256]{2,1,0:T(8,128)(2,1)S(1)}, bf16[4,64,256]{2,1,0:T(8,128)(2,1)S(1)}, u32[]{:S(2)}, u32[]{:S(2)}) collective-permute-start(bf16[4,64,256]{2,1,0:T(8,128)(2,1)S(1)} %maximum_bitcast_fusion.1), channel_id=1, source_target_pairs={{0,4},{2,6},{4,0},{6,2},{8,12},{10,14},{12,8},{14,10},{16,20},{18,... | collective-permute-start | bytes 393224 | tf_op jit(solution)/shard_map/ppermute | solution.py:45
  71.9 1.3 %collective-permute-start.19 = (bf16[4,64,256]{2,1,0:T(8,128)(2,1)S(1)}, bf16[4,64,256]{2,1,0:T(8,128)(2,1)S(1)}, u32[]{:S(2)}, u32[]{:S(2)}) collective-permute-start(bf16[4,64,256]{2,1,0:T(8,128)(2,1)S(1)} %maximum_bitcast_fusion.1), channel_id=1, source_target_pairs={{0,6},{2,4},{4,2},{6,0},{8,14},{10,12},{12,10},{14,8},{16,22},{18,... | collective-permute-start | bytes 393224 | tf_op jit(solution)/shard_map/ppermute | solution.py:45
  73.7 2.3 %collective-permute-done.21 = bf16[4,64,256]{2,1,0:T(8,128)(2,1)S(1)} collective-permute-done((bf16[4,64,256]{2,1,0:T(8,128)(2,1)S(1)}, bf16[4,64,256]{2,1,0:T(8,128)(2,1)S(1)}, u32[]{:S(2)}, u32[]{:S(2)}) %collective-permute-start.21) | collective-permute-done | bytes 131104 | tf_op jit(solution)/shard_map/ppermute | solution.py:45
  76.0 2.6 %collective-permute-done.20 = bf16[4,64,256]{2,1,0:T(8,128)(2,1)S(1)} collective-permute-done((bf16[4,64,256]{2,1,0:T(8,128)(2,1)S(1)}, bf16[4,64,256]{2,1,0:T(8,128)(2,1)S(1)}, u32[]{:S(2)}, u32[]{:S(2)}) %collective-permute-start.20) | collective-permute-done | bytes 131104 | tf_op jit(solution)/shard_map/ppermute | solution.py:45
  78.9 1.1 %select_bitcast_fusion.1 = (bf16[1,1,384,256]{3,2,1,0:T(8,128)(2,1)S(1)}, bf16[1,1,384,256]{3,2,1,0:T(8,128)(2,1)S(1)}) fusion(bf16[1,384,256]{2,1,0:T(8,128)(2,1)} %collective-permute-done.15, bf16[1,384,256]{2,1,0:T(8,128)(2,1)S(1)} %get-tuple-element.22, pred[]{:T(512)S(6)} %eq.53), kind=kLoop, calls=%fused_computation.82 | loop fusion | flops 196608 | bytes 786433 | tf_op jit(solution)/shard_map/stack | solution.py:128
  80.3 1.5 %fusion.5 = (f32[256]{0:T(256)S(1)}, f32[768,256]{1,0:T(8,128)}) fusion(bf16[1,2,384,256]{3,2,1,0:T(8,128)(2,1)S(1)} %pad_maximum_fusion.5, bf16[768,256]{1,0:T(8,128)(2,1)S(1)} %bitcast.246, f32[768]{0:T(1024)S(1)} %copy-done.26, bf16[768,1024]{1,0:T(8,128)(2,1)S(1)} %bitcast.218, bf16[1024,256]{1,0:T(8,128)(2,1)S(1)} %bitcast.228), kind=kOutput, calls=%fused_computation.19 | convolution fusion | flops 403832576 | bytes 3674112 | tf_op jit(solution)/shard_map/dot_general | solution.py:161
  81.8 1.7 %fusion.3 = (f32[256]{0:T(256)S(1)}, f32[1024,256]{1,0:T(8,128)}) fusion(bf16[4,4,64,256]{3,2,1,0:T(8,128)(2,1)S(1)} %copy.38, bf16[1024,256]{1,0:T(8,128)(2,1)S(1)} %bitcast.229, f32[1024]{0:T(1024)S(1)} %bitcast.250, bf16[1024,768]{0,1:T(8,128)(2,1)S(1)} %bitcast.216, bf16[768,256]{1,0:T(8,128)(2,1)S(1)} %bitcast.247), kind=kOutput, calls=%fused_computation.13 | convolution fusion | flops 404225792 | bytes 4068352 | tf_op jit(solution)/shard_map/dot_general | solution.py:163
  84.1 1.2 %dynamic-slice_convert_fusion.4 = (bf16[2,2,1,1,64,256]{5,4,3,2,1,0:T(8,128)(2,1)S(1)}, bf16[2,2,1,1,64,256]{5,4,3,2,1,0:T(8,128)(2,1)S(1)}, bf16[2,2,1,1,64,256]{5,4,3,2,1,0:T(8,128)(2,1)S(1)}) fusion(f32[2,2,2,2,64,256]{5,4,3,2,1,0:T(8,128)} %bitcast.240, s32[]{:T(128)S(6)} %select_n.385, s32[]{:T(128)S(6)} %select_n.387, s32[]{:T(128)S(6)} %select_n.393, ...), kind=kLoop, calls=%fused_computation.57 | loop fusion | bytes 786456 | tf_op jit(solution)/shard_map/convert_element_type | solution.py:90
  85.3 1.3 %collective-permute-start.22 = (bf16[280,256]{1,0:T(8,128)(2,1)S(1)}, bf16[280,256]{1,0:T(8,128)(2,1)S(1)}, u32[]{:S(2)}, u32[]{:S(2)}) collective-permute-start(bf16[280,256]{1,0:T(8,128)(2,1)S(1)} %get-tuple-element.74), channel_id=1, source_target_pairs={{0,2},{2,0},{4,6},{6,4},{8,10},{10,8},{12,14},{14,12},{16,18},{18,... | collective-permute-start | bytes 430088 | tf_op jit(solution)/shard_map/ppermute | solution.py:45
  86.6 0.8 collective-permute-start.23
  87.4 1.4 %collective-permute-start.24 = (bf16[280,256]{1,0:T(8,128)(2,1)S(1)}, bf16[280,256]{1,0:T(8,128)(2,1)S(1)}, u32[]{:S(2)}, u32[]{:S(2)}) collective-permute-start(bf16[280,256]{1,0:T(8,128)(2,1)S(1)} %get-tuple-element.76), channel_id=1, source_target_pairs={{0,6},{2,4},{4,2},{6,0},{8,14},{10,12},{12,10},{14,8},{16,22},{18,... | collective-permute-start | bytes 430088 | tf_op jit(solution)/shard_map/ppermute | solution.py:45
  88.8 1.7 %fusion.25 = bf16[384,256]{1,0:T(8,128)(2,1)} fusion(f32[2,384,256]{2,1,0:T(8,128)} %bitcast.238, s32[]{:T(128)S(6)} %select_n.413), kind=kLoop, calls=%fused_computation.80 | loop fusion | bytes 393220 | tf_op jit(solution)/shard_map/convert_element_type | solution.py:90
  90.6 1.0 constant_dynamic-slice_fusion
  91.6 2.7 %collective-permute-done.23 = bf16[280,256]{1,0:T(8,128)(2,1)S(1)} collective-permute-done((bf16[280,256]{1,0:T(8,128)(2,1)S(1)}, bf16[280,256]{1,0:T(8,128)(2,1)S(1)}, u32[]{:S(2)}, u32[]{:S(2)}) %collective-permute-start.23) | collective-permute-done | bytes 143392 | tf_op jit(solution)/shard_map/ppermute | solution.py:45
  94.6 0.8 collective-permute-start.26
  95.4 3.6 %collective-permute-start.27 = (bf16[88,256]{1,0:T(8,128)(2,1)S(1)}, bf16[88,256]{1,0:T(8,128)(2,1)S(1)}, u32[]{:S(2)}, u32[]{:S(2)}) collective-permute-start(bf16[88,256]{1,0:T(8,128)(2,1)S(1)} %get-tuple-element.73), channel_id=1, source_target_pairs={{0,24},{2,26},{4,28},{6,30},{8,16},{10,18},{12,20},{14,22},{16,8},... | collective-permute-start | bytes 135176 | tf_op jit(solution)/shard_map/ppermute | solution.py:45
  99.6 1.9 %collective-permute-done.27 = bf16[88,256]{1,0:T(8,128)(2,1)S(1)} collective-permute-done((bf16[88,256]{1,0:T(8,128)(2,1)S(1)}, bf16[88,256]{1,0:T(8,128)(2,1)S(1)}, u32[]{:S(2)}, u32[]{:S(2)}) %collective-permute-start.27) | collective-permute-done | bytes 45088 | tf_op jit(solution)/shard_map/ppermute | solution.py:45
  101.6 1.1 %collective-permute-done.28 = f32[8]{0:T(128)S(1)} collective-permute-done((f32[8]{0:T(128)S(1)}, f32[8]{0:T(128)S(1)}, u32[]{:S(2)}, u32[]{:S(2)}) %collective-permute-start.28) | collective-permute-done | bytes 64 | tf_op jit(solution)/shard_map/ppermute | solution.py:45
  103.1 0.7 fusion.36
  103.9 2.2 %fusion.11 = (f32[1,384,256]{2,1,0:T(8,128)}, f32[1,384,256]{2,1,0:T(8,128)}) fusion(f32[384,256]{1,0:T(8,128)S(1)} %get-tuple-element.23, f32[384,256]{1,0:T(8,128)S(1)} %reshape.300, bf16[384,256]{1,0:T(8,128)(2,1)} %collective-permute-done.29, f32[2,384,256]{2,1,0:T(8,128)} %bitcast.239, s32[]{:T(128)S(6)} %select_n.412, f32[256]{0:T(256)S(1)} %mul.220, ...), kind=kLoop, calls=%fused_computation.32 | loop fusion | flops 1671168 | bytes 3542020 | tf_op jit(solution)/shard_map/broadcast_in_dim | solution.py:222
  (194 shorter events, 10.5 us)
Async XLA Ops:
  0.6 9.8 %copy-start = (f32[64,64]{1,0:T(8,128)S(1)}, f32[64,64]{1,0:T(8,128)}, u32[]{:S(2)}) copy-start(f32[64,64]{1,0:T(8,128)} %param.9) | copy-start | bytes 49156
  3.6 17.7 %collective-permute-start.2 = (bf16[1,64,256]{2,1,0:T(8,128)(2,1)S(1)}, bf16[1,64,256]{2,1,0:T(8,128)(2,1)}, u32[]{:S(2)}, u32[]{:S(2)}) collective-permute-start(bf16[1,64,256]{2,1,0:T(8,128)(2,1)S(1)} %get-tuple-element.70), channel_id=1, source_target_pairs={{0,8},{2,10},{4,12},{6,14},{8,0},{10,2},{12,4},{14,6},{16,24},{18,... | collective-permute-start | bytes 98312 | tf_op jit(solution)/shard_map/ppermute | solution.py:45
  6.7 14.6 %collective-permute-start.1 = (bf16[1,64,256]{2,1,0:T(8,128)(2,1)S(1)}, bf16[1,64,256]{2,1,0:T(8,128)(2,1)}, u32[]{:S(2)}, u32[]{:S(2)}) collective-permute-start(bf16[1,64,256]{2,1,0:T(8,128)(2,1)S(1)} %get-tuple-element.70), channel_id=1, source_target_pairs={{0,16},{2,18},{4,20},{6,22},{8,24},{10,26},{12,28},{14,30},{16,0},... | collective-permute-start | bytes 98312 | tf_op jit(solution)/shard_map/ppermute | solution.py:45
  9.3 12.1 %collective-permute-start = (bf16[1,64,256]{2,1,0:T(8,128)(2,1)S(1)}, bf16[1,64,256]{2,1,0:T(8,128)(2,1)}, u32[]{:S(2)}, u32[]{:S(2)}) collective-permute-start(bf16[1,64,256]{2,1,0:T(8,128)(2,1)S(1)} %get-tuple-element.70), channel_id=1, source_target_pairs={{0,24},{2,26},{4,28},{6,30},{8,16},{10,18},{12,20},{14,22},{16,8},... | collective-permute-start | bytes 98312 | tf_op jit(solution)/shard_map/ppermute | solution.py:45
  10.5 5.4 %copy-start.32 = (s32[1,1,12,2]{2,3,1,0:T(2,128)S(1)}, s32[1,1,12,2]{2,3,1,0:T(2,128)}, u32[]{:S(2)}) copy-start(s32[1,1,12,2]{2,3,1,0:T(2,128)} %param.12) | copy-start | bytes 292
  11.3 0.9 copy-start.2
  13.1 12.6 %copy-start.1 = (s32[1,1,12,256,256]{4,3,2,1,0:T(8,128)S(1)}, s32[1,1,12,256,256]{4,3,2,1,0:T(8,128)}, u32[]{:S(2)}) copy-start(s32[1,1,12,256,256]{4,3,2,1,0:T(8,128)} %param.11) | copy-start | bytes 9437188
  15.2 18.6 %collective-permute-start.3 = (bf16[1,384,256]{2,1,0:T(8,128)(2,1)S(1)}, bf16[1,384,256]{2,1,0:T(8,128)(2,1)}, u32[]{:S(2)}, u32[]{:S(2)}) collective-permute-start(bf16[1,384,256]{2,1,0:T(8,128)(2,1)S(1)} %get-tuple-element.45), channel_id=1, source_target_pairs={{0,1},{1,0},{2,3},{3,2},{4,5},{5,4},{6,7},{7,6},{8,9},{9,8},{10,11... | collective-permute-start | bytes 589832 | tf_op jit(solution)/shard_map/ppermute | solution.py:45
  22.2 8.2 %collective-permute-start.6 = (bf16[4,64,256]{2,1,0:T(8,128)(2,1)S(1)}, bf16[4,64,256]{2,1,0:T(8,128)(2,1)}, u32[]{:S(2)}, u32[]{:S(2)}) collective-permute-start(bf16[4,64,256]{2,1,0:T(8,128)(2,1)S(1)} %maximum_bitcast_fusion), channel_id=1, source_target_pairs={{0,2},{2,0},{4,6},{6,4},{8,10},{10,8},{12,14},{14,12},{16,18},{18,... | collective-permute-start | bytes 393224 | tf_op jit(solution)/shard_map/ppermute | solution.py:45
  24.0 8.5 %collective-permute-start.5 = (bf16[4,64,256]{2,1,0:T(8,128)(2,1)S(1)}, bf16[4,64,256]{2,1,0:T(8,128)(2,1)}, u32[]{:S(2)}, u32[]{:S(2)}) collective-permute-start(bf16[4,64,256]{2,1,0:T(8,128)(2,1)S(1)} %maximum_bitcast_fusion), channel_id=1, source_target_pairs={{0,4},{2,6},{4,0},{6,2},{8,12},{10,14},{12,8},{14,10},{16,20},{18,... | collective-permute-start | bytes 393224 | tf_op jit(solution)/shard_map/ppermute | solution.py:45
  25.5 7.0 %collective-permute-start.4 = (bf16[4,64,256]{2,1,0:T(8,128)(2,1)S(1)}, bf16[4,64,256]{2,1,0:T(8,128)(2,1)}, u32[]{:S(2)}, u32[]{:S(2)}) collective-permute-start(bf16[4,64,256]{2,1,0:T(8,128)(2,1)S(1)} %maximum_bitcast_fusion), channel_id=1, source_target_pairs={{0,6},{2,4},{4,2},{6,0},{8,14},{10,12},{12,10},{14,8},{16,22},{18,... | collective-permute-start | bytes 393224 | tf_op jit(solution)/shard_map/ppermute | solution.py:45
  26.4 0.6 copy-start.27
  26.4 0.7 copy-start.28
  28.5 6.3 %copy-start.23 = (f32[1,2,4,128]{3,1,2,0:T(2,128)}, f32[1,2,4,128]{3,1,2,0:T(2,128)S(1)}, u32[]{:S(2)}) copy-start(f32[1,2,4,128]{3,1,2,0:T(2,128)S(1)} %copy.49) | copy-start | bytes 12292
  28.6 8.2 %copy-start.25 = (f32[768]{0:T(1024)}, f32[768]{0:T(1024)S(1)}, u32[]{:S(2)}) copy-start(f32[768]{0:T(1024)S(1)} %mul.194) | copy-start | bytes 9220
  29.5 5.3 %copy-start.5 = (bf16[96,8,4,256]{3,1,2,0:T(8,128)(2,1)}, bf16[96,8,4,256]{3,1,2,0:T(8,128)(2,1)S(1)}, u32[]{:S(2)}) copy-start(bf16[96,8,4,256]{3,1,2,0:T(8,128)(2,1)S(1)} %copy.48) | copy-start | bytes 4718596
  30.4 6.4 %copy-start.7 = (bf16[96,8,4,256]{3,1,2,0:T(8,128)(2,1)}, bf16[96,8,4,256]{3,1,2,0:T(8,128)(2,1)S(1)}, u32[]{:S(2)}) copy-start(bf16[96,8,4,256]{3,1,2,0:T(8,128)(2,1)S(1)} %copy.50) | copy-start | bytes 4718596
  37.4 29.6 %copy-start.9 = (f32[768,256]{1,0:T(8,128)}, f32[768,256]{1,0:T(8,128)S(1)}, u32[]{:S(2)}) copy-start(f32[768,256]{1,0:T(8,128)S(1)} %get-tuple-element.96) | copy-start | bytes 2359300
  38.9 5.8 %collective-permute-start.7 = (bf16[280,256]{1,0:T(8,128)(2,1)S(1)}, bf16[280,256]{1,0:T(8,128)(2,1)S(1)}, u32[]{:S(2)}, u32[]{:S(2)}) collective-permute-start(bf16[280,256]{1,0:T(8,128)(2,1)S(1)} %get-tuple-element.80), channel_id=1, source_target_pairs={{0,2},{2,0},{4,6},{6,4},{8,10},{10,8},{12,14},{14,12},{16,18},{18,... | collective-permute-start | bytes 430088 | tf_op jit(solution)/shard_map/ppermute | solution.py:45
  40.2 8.2 %collective-permute-start.8 = (bf16[280,256]{1,0:T(8,128)(2,1)S(1)}, bf16[280,256]{1,0:T(8,128)(2,1)S(1)}, u32[]{:S(2)}, u32[]{:S(2)}) collective-permute-start(bf16[280,256]{1,0:T(8,128)(2,1)S(1)} %get-tuple-element.81), channel_id=1, source_target_pairs={{0,4},{2,6},{4,0},{6,2},{8,12},{10,14},{12,8},{14,10},{16,20},{18,... | collective-permute-start | bytes 430088 | tf_op jit(solution)/shard_map/ppermute | solution.py:45
  41.1 7.4 %collective-permute-start.9 = (bf16[280,256]{1,0:T(8,128)(2,1)S(1)}, bf16[280,256]{1,0:T(8,128)(2,1)S(1)}, u32[]{:S(2)}, u32[]{:S(2)}) collective-permute-start(bf16[280,256]{1,0:T(8,128)(2,1)S(1)} %get-tuple-element.82), channel_id=1, source_target_pairs={{0,6},{2,4},{4,2},{6,0},{8,14},{10,12},{12,10},{14,8},{16,22},{18,... | collective-permute-start | bytes 430088 | tf_op jit(solution)/shard_map/ppermute | solution.py:45
  42.5 18.1 %copy-start.11 = (f32[1,64,256]{2,1,0:T(8,128)S(1)}, f32[1,64,256]{2,1,0:T(8,128)}, u32[]{:S(2)}) copy-start(f32[1,64,256]{2,1,0:T(8,128)} %param.8) | copy-start | bytes 196612
  42.5 18.1 %copy-start.18 = (f32[64,256]{1,0:T(8,128)S(1)}, f32[64,256]{1,0:T(8,128)}, u32[]{:S(2)}) copy-start(f32[64,256]{1,0:T(8,128)} %reshape.295) | copy-start | bytes 196612
  42.5 24.5 %collective-permute-start.14 = (bf16[384,256]{1,0:T(8,128)(2,1)S(1)}, bf16[384,256]{1,0:T(8,128)(2,1)S(1)}, u32[]{:S(2)}, u32[]{:S(2)}) collective-permute-start(bf16[384,256]{1,0:T(8,128)(2,1)S(1)} %fusion.24), channel_id=1, source_target_pairs={{0,1},{1,0},{2,3},{3,2},{4,5},{5,4},{6,7},{7,6},{8,9},{9,8},{10,11... | collective-permute-start | bytes 589832 | tf_op jit(solution)/shard_map/ppermute | solution.py:45
  43.6 21.6 %copy-start.20 = (f32[64,64]{1,0:T(8,128)S(1)}, f32[64,64]{1,0:T(8,128)}, u32[]{:S(2)}) copy-start(f32[64,64]{1,0:T(8,128)} %param.10) | copy-start | bytes 49156
  48.5 18.5 %copy-start.3 = (f32[1,384,256]{2,1,0:T(8,128)S(1)}, f32[1,384,256]{2,1,0:T(8,128)}, u32[]{:S(2)}) copy-start(f32[1,384,256]{2,1,0:T(8,128)} %param.7) | copy-start | bytes 1179652
  48.5 18.5 %copy-start.4 = (f32[384,256]{1,0:T(8,128)S(1)}, f32[384,256]{1,0:T(8,128)}, u32[]{:S(2)}) copy-start(f32[384,256]{1,0:T(8,128)} %reshape.293) | copy-start | bytes 1179652
  48.6 4.5 %collective-permute-start.10 = (bf16[88,256]{1,0:T(8,128)(2,1)S(1)}, bf16[88,256]{1,0:T(8,128)(2,1)S(1)}, u32[]{:S(2)}, u32[]{:S(2)}) collective-permute-start(bf16[88,256]{1,0:T(8,128)(2,1)S(1)} %get-tuple-element.77), channel_id=1, source_target_pairs={{0,8},{2,10},{4,12},{6,14},{8,0},{10,2},{12,4},{14,6},{16,24},{18,... | collective-permute-start | bytes 135176 | tf_op jit(solution)/shard_map/ppermute | solution.py:45
  49.4 6.5 %collective-permute-start.11 = (bf16[88,256]{1,0:T(8,128)(2,1)S(1)}, bf16[88,256]{1,0:T(8,128)(2,1)S(1)}, u32[]{:S(2)}, u32[]{:S(2)}) collective-permute-start(bf16[88,256]{1,0:T(8,128)(2,1)S(1)} %get-tuple-element.78), channel_id=1, source_target_pairs={{0,16},{2,18},{4,20},{6,22},{8,24},{10,26},{12,28},{14,30},{16,0},... | collective-permute-start | bytes 135176 | tf_op jit(solution)/shard_map/ppermute | solution.py:45
  52.9 5.8 %collective-permute-start.12 = (bf16[88,256]{1,0:T(8,128)(2,1)S(1)}, bf16[88,256]{1,0:T(8,128)(2,1)S(1)}, u32[]{:S(2)}, u32[]{:S(2)}) collective-permute-start(bf16[88,256]{1,0:T(8,128)(2,1)S(1)} %get-tuple-element.79), channel_id=1, source_target_pairs={{0,24},{2,26},{4,28},{6,30},{8,16},{10,18},{12,20},{14,22},{16,8},... | collective-permute-start | bytes 135176 | tf_op jit(solution)/shard_map/ppermute | solution.py:45
  58.8 8.3 %copy-start.14 = (f32[88,256]{1,0:T(8,128)}, f32[88,256]{1,0:T(8,128)S(1)}, u32[]{:S(2)}) copy-start(f32[88,256]{1,0:T(8,128)S(1)} %fusion.28) | copy-start | bytes 270340
  58.8 1.2 %collective-permute-start.13 = (f32[8]{0:T(128)S(1)}, f32[8]{0:T(128)S(1)}, u32[]{:S(2)}, u32[]{:S(2)}) collective-permute-start(f32[8]{0:T(128)S(1)} %fusion.59), channel_id=1, source_target_pairs={{0,1},{1,0},{2,3},{3,2},{4,5},{5,4},{6,7},{7,6},{8,9},{9,8},{10,11... | collective-permute-start | bytes 104 | tf_op jit(solution)/shard_map/ppermute | solution.py:45
  60.0 0.5 copy-start.29
  60.7 6.8 %copy-start.21 = (f32[256]{0:T(256)}, f32[256]{0:T(256)S(1)}, u32[]{:S(2)}) copy-start(f32[256]{0:T(256)S(1)} %mul.200) | copy-start | bytes 3076
  60.7 8.1 %collective-permute-start.18 = (bf16[1,64,256]{2,1,0:T(8,128)(2,1)S(1)}, bf16[1,64,256]{2,1,0:T(8,128)(2,1)}, u32[]{:S(2)}, u32[]{:S(2)}) collective-permute-start(bf16[1,64,256]{2,1,0:T(8,128)(2,1)S(1)} %get-tuple-element.24), channel_id=1, source_target_pairs={{0,8},{2,10},{4,12},{6,14},{8,0},{10,2},{12,4},{14,6},{16,24},{18,... | collective-permute-start | bytes 98312 | tf_op jit(solution)/shard_map/ppermute | solution.py:45
  60.8 8.0 %collective-permute-start.17 = (bf16[1,64,256]{2,1,0:T(8,128)(2,1)S(1)}, bf16[1,64,256]{2,1,0:T(8,128)(2,1)}, u32[]{:S(2)}, u32[]{:S(2)}) collective-permute-start(bf16[1,64,256]{2,1,0:T(8,128)(2,1)S(1)} %get-tuple-element.24), channel_id=1, source_target_pairs={{0,16},{2,18},{4,20},{6,22},{8,24},{10,26},{12,28},{14,30},{16,0},... | collective-permute-start | bytes 98312 | tf_op jit(solution)/shard_map/ppermute | solution.py:45
  61.8 7.0 %collective-permute-start.16 = (bf16[1,64,256]{2,1,0:T(8,128)(2,1)S(1)}, bf16[1,64,256]{2,1,0:T(8,128)(2,1)}, u32[]{:S(2)}, u32[]{:S(2)}) collective-permute-start(bf16[1,64,256]{2,1,0:T(8,128)(2,1)S(1)} %get-tuple-element.24), channel_id=1, source_target_pairs={{0,24},{2,26},{4,28},{6,30},{8,16},{10,18},{12,20},{14,22},{16,8},... | collective-permute-start | bytes 98312 | tf_op jit(solution)/shard_map/ppermute | solution.py:45
  65.6 1.5 %copy-start.16 = (f32[64,256]{1,0:T(8,128)}, f32[64,256]{1,0:T(8,128)S(1)}, u32[]{:S(2)}) copy-start(f32[64,256]{1,0:T(8,128)S(1)} %reshape.302) | copy-start | bytes 196612
  67.1 0.7 copy-start.12
  67.2 11.7 %collective-permute-start.15 = (bf16[1,384,256]{2,1,0:T(8,128)(2,1)S(1)}, bf16[1,384,256]{2,1,0:T(8,128)(2,1)}, u32[]{:S(2)}, u32[]{:S(2)}) collective-permute-start(bf16[1,384,256]{2,1,0:T(8,128)(2,1)S(1)} %get-tuple-element.22), channel_id=1, source_target_pairs={{0,1},{1,0},{2,3},{3,2},{4,5},{5,4},{6,7},{7,6},{8,9},{9,8},{10,11... | collective-permute-start | bytes 589832 | tf_op jit(solution)/shard_map/ppermute | solution.py:45
  68.5 5.2 %copy-start.33 = (f32[4]{0:T(128)S(1)}, f32[4]{0:T(128)}, u32[]{:S(2)}) copy-start(f32[4]{0:T(128)} %reduce_sum.255) | copy-start | bytes 52
  69.6 6.4 %collective-permute-start.21 = (bf16[4,64,256]{2,1,0:T(8,128)(2,1)S(1)}, bf16[4,64,256]{2,1,0:T(8,128)(2,1)S(1)}, u32[]{:S(2)}, u32[]{:S(2)}) collective-permute-start(bf16[4,64,256]{2,1,0:T(8,128)(2,1)S(1)} %maximum_bitcast_fusion.1), channel_id=1, source_target_pairs={{0,2},{2,0},{4,6},{6,4},{8,10},{10,8},{12,14},{14,12},{16,18},{18,... | collective-permute-start | bytes 393224 | tf_op jit(solution)/shard_map/ppermute | solution.py:45
  70.5 8.2 %collective-permute-start.20 = (bf16[4,64,256]{2,1,0:T(8,128)(2,1)S(1)}, bf16[4,64,256]{2,1,0:T(8,128)(2,1)S(1)}, u32[]{:S(2)}, u32[]{:S(2)}) collective-permute-start(bf16[4,64,256]{2,1,0:T(8,128)(2,1)S(1)} %maximum_bitcast_fusion.1), channel_id=1, source_target_pairs={{0,4},{2,6},{4,0},{6,2},{8,12},{10,14},{12,8},{14,10},{16,20},{18,... | collective-permute-start | bytes 393224 | tf_op jit(solution)/shard_map/ppermute | solution.py:45
  71.9 6.8 %collective-permute-start.19 = (bf16[4,64,256]{2,1,0:T(8,128)(2,1)S(1)}, bf16[4,64,256]{2,1,0:T(8,128)(2,1)S(1)}, u32[]{:S(2)}, u32[]{:S(2)}) collective-permute-start(bf16[4,64,256]{2,1,0:T(8,128)(2,1)S(1)} %maximum_bitcast_fusion.1), channel_id=1, source_target_pairs={{0,6},{2,4},{4,2},{6,0},{8,14},{10,12},{12,10},{14,8},{16,22},{18,... | collective-permute-start | bytes 393224 | tf_op jit(solution)/shard_map/ppermute | solution.py:45
  78.8 1.5 %copy-start.8 = (bf16[96,8,4,256]{3,1,2,0:T(8,128)(2,1)S(1)}, bf16[96,8,4,256]{3,1,2,0:T(8,128)(2,1)}, u32[]{:S(2)}) copy-start(bf16[96,8,4,256]{3,1,2,0:T(8,128)(2,1)} %copy-done.7) | copy-start | bytes 4718596
  78.8 1.5 %copy-start.26 = (f32[768]{0:T(1024)S(1)}, f32[768]{0:T(1024)}, u32[]{:S(2)}) copy-start(f32[768]{0:T(1024)} %copy-done.25) | copy-start | bytes 9220
  80.3 1.5 %copy-start.6 = (bf16[96,8,4,256]{3,1,2,0:T(8,128)(2,1)S(1)}, bf16[96,8,4,256]{3,1,2,0:T(8,128)(2,1)}, u32[]{:S(2)}) copy-start(bf16[96,8,4,256]{3,1,2,0:T(8,128)(2,1)} %copy-done.5) | copy-start | bytes 4718596
  80.3 1.5 %copy-start.24 = (f32[1,2,4,128]{3,1,2,0:T(2,128)S(1)}, f32[1,2,4,128]{3,1,2,0:T(2,128)}, u32[]{:S(2)}) copy-start(f32[1,2,4,128]{3,1,2,0:T(2,128)} %copy-done.23) | copy-start | bytes 12292
  81.8 2.2 %copy-start.31 = (f32[4]{0:T(128)S(1)}, f32[4]{0:T(128)}, u32[]{:S(2)}) copy-start(f32[4]{0:T(128)} %reduce_sum.261) | copy-start | bytes 52
  85.3 6.4 %collective-permute-start.22 = (bf16[280,256]{1,0:T(8,128)(2,1)S(1)}, bf16[280,256]{1,0:T(8,128)(2,1)S(1)}, u32[]{:S(2)}, u32[]{:S(2)}) collective-permute-start(bf16[280,256]{1,0:T(8,128)(2,1)S(1)} %get-tuple-element.74), channel_id=1, source_target_pairs={{0,2},{2,0},{4,6},{6,4},{8,10},{10,8},{12,14},{14,12},{16,18},{18,... | collective-permute-start | bytes 430088 | tf_op jit(solution)/shard_map/ppermute | solution.py:45
  86.6 7.8 %collective-permute-start.23 = (bf16[280,256]{1,0:T(8,128)(2,1)S(1)}, bf16[280,256]{1,0:T(8,128)(2,1)S(1)}, u32[]{:S(2)}, u32[]{:S(2)}) collective-permute-start(bf16[280,256]{1,0:T(8,128)(2,1)S(1)} %get-tuple-element.75), channel_id=1, source_target_pairs={{0,4},{2,6},{4,0},{6,2},{8,12},{10,14},{12,8},{14,10},{16,20},{18,... | collective-permute-start | bytes 430088 | tf_op jit(solution)/shard_map/ppermute | solution.py:45
  87.4 6.9 %collective-permute-start.24 = (bf16[280,256]{1,0:T(8,128)(2,1)S(1)}, bf16[280,256]{1,0:T(8,128)(2,1)S(1)}, u32[]{:S(2)}, u32[]{:S(2)}) collective-permute-start(bf16[280,256]{1,0:T(8,128)(2,1)S(1)} %get-tuple-element.76), channel_id=1, source_target_pairs={{0,6},{2,4},{4,2},{6,0},{8,14},{10,12},{12,10},{14,8},{16,22},{18,... | collective-permute-start | bytes 430088 | tf_op jit(solution)/shard_map/ppermute | solution.py:45
  90.5 12.2 %copy-start.30 = (f32[8]{0:T(128)S(1)}, f32[8]{0:T(128)}, u32[]{:S(2)}) copy-start(f32[8]{0:T(128)} %copy-done.29) | copy-start | bytes 100
  90.5 12.6 %copy-start.15 = (f32[88,256]{1,0:T(8,128)S(1)}, f32[88,256]{1,0:T(8,128)}, u32[]{:S(2)}) copy-start(f32[88,256]{1,0:T(8,128)} %copy-done.14) | copy-start | bytes 270340
  90.5 12.6 %copy-start.17 = (f32[64,256]{1,0:T(8,128)S(1)}, f32[64,256]{1,0:T(8,128)}, u32[]{:S(2)}) copy-start(f32[64,256]{1,0:T(8,128)} %copy-done.16) | copy-start | bytes 196612
  90.5 12.6 %copy-start.19 = (f32[64,256]{1,0:T(8,128)S(1)}, f32[64,256]{1,0:T(8,128)}, u32[]{:S(2)}) copy-start(f32[64,256]{1,0:T(8,128)} %reshape.295) | copy-start | bytes 196612
  90.5 12.6 %copy-start.22 = (f32[256]{0:T(256)S(1)}, f32[256]{0:T(256)}, u32[]{:S(2)}) copy-start(f32[256]{0:T(256)} %copy-done.21) | copy-start | bytes 3076
  90.5 13.3 %collective-permute-start.29 = (bf16[384,256]{1,0:T(8,128)(2,1)}, bf16[384,256]{1,0:T(8,128)(2,1)}, u32[]{:S(2)}, u32[]{:S(2)}) collective-permute-start(bf16[384,256]{1,0:T(8,128)(2,1)} %fusion.25), channel_id=1, source_target_pairs={{0,1},{1,0},{2,3},{3,2},{4,5},{5,4},{6,7},{7,6},{8,9},{9,8},{10,11... | collective-permute-start | bytes 589832 | tf_op jit(solution)/shard_map/ppermute | solution.py:45
  91.6 12.2 %copy-start.10 = (f32[768,256]{1,0:T(8,128)S(1)}, f32[768,256]{1,0:T(8,128)}, u32[]{:S(2)}) copy-start(f32[768,256]{1,0:T(8,128)} %copy-done.9) | copy-start | bytes 2359300
  91.6 12.2 %copy-start.13 = (bf16[384,256]{1,0:T(8,128)(2,1)S(1)}, bf16[384,256]{1,0:T(8,128)(2,1)}, u32[]{:S(2)}) copy-start(bf16[384,256]{1,0:T(8,128)(2,1)} %copy-done.12) | copy-start | bytes 589828
  94.5 4.6 %collective-permute-start.25 = (bf16[88,256]{1,0:T(8,128)(2,1)S(1)}, bf16[88,256]{1,0:T(8,128)(2,1)S(1)}, u32[]{:S(2)}, u32[]{:S(2)}) collective-permute-start(bf16[88,256]{1,0:T(8,128)(2,1)S(1)} %get-tuple-element.71), channel_id=1, source_target_pairs={{0,8},{2,10},{4,12},{6,14},{8,0},{10,2},{12,4},{14,6},{16,24},{18,... | collective-permute-start | bytes 135176 | tf_op jit(solution)/shard_map/ppermute | solution.py:45
  94.6 5.0 %collective-permute-start.26 = (bf16[88,256]{1,0:T(8,128)(2,1)S(1)}, bf16[88,256]{1,0:T(8,128)(2,1)S(1)}, u32[]{:S(2)}, u32[]{:S(2)}) collective-permute-start(bf16[88,256]{1,0:T(8,128)(2,1)S(1)} %get-tuple-element.72), channel_id=1, source_target_pairs={{0,16},{2,18},{4,20},{6,22},{8,24},{10,26},{12,28},{14,30},{16,0},... | collective-permute-start | bytes 135176 | tf_op jit(solution)/shard_map/ppermute | solution.py:45
  95.4 6.1 %collective-permute-start.27 = (bf16[88,256]{1,0:T(8,128)(2,1)S(1)}, bf16[88,256]{1,0:T(8,128)(2,1)S(1)}, u32[]{:S(2)}, u32[]{:S(2)}) collective-permute-start(bf16[88,256]{1,0:T(8,128)(2,1)S(1)} %get-tuple-element.73), channel_id=1, source_target_pairs={{0,24},{2,26},{4,28},{6,30},{8,16},{10,18},{12,20},{14,22},{16,8},... | collective-permute-start | bytes 135176 | tf_op jit(solution)/shard_map/ppermute | solution.py:45
  101.5 1.2 %collective-permute-start.28 = (f32[8]{0:T(128)S(1)}, f32[8]{0:T(128)S(1)}, u32[]{:S(2)}, u32[]{:S(2)}) collective-permute-start(f32[8]{0:T(128)S(1)} %fusion.58), channel_id=1, source_target_pairs={{0,1},{1,0},{2,3},{3,2},{4,5},{5,4},{6,7},{7,6},{8,9},{9,8},{10,11... | collective-permute-start | bytes 104 | tf_op jit(solution)/shard_map/ppermute | solution.py:45

commit v16 on v15

--- a/solution.py
+++ b/solution.py
@@ -18,8 +18,8 @@
 
 def prior_term(field_vec, prior_mat):
     row_total = field_vec.shape[0]
-    grouped = field_vec.reshape(row_total * DRAWS, DIM)
-    mixed = jnp.dot(grouped, prior_mat, precision=top_prec)
+    grouped = field_vec.reshape(row_total, DRAWS, DIM)
+    mixed = jnp.einsum("nde,ef->ndf", grouped, prior_mat, precision=top_prec)
     return mixed.reshape(row_total, DRAWS * DIM)
 
 

time: 107 us -> 112 us (1.047)
  matrix products: 9.66 us -> 14.3 us
  local copies, waits for them, and re-layouts: 19.7 us -> 21.7 us
    unnamed x71 -> x54, local copies, waits for them, and re-layouts: 3.11 us -> 7.29 us
    dot_general x2, matrix products: 2.06 us -> 6.18 us  [cross_parts(): jnp.dot(counts_bf, item_range, preferred_element_type=jnp.float32)]
    reshape x6 -> x2, local copies, waits for them, and re-layouts: 4.23 us -> 0.28 us  [prior_term(): return mixed.reshape(row_total, DRAWS * DIM)]
    another operation x2 -> x4, local copies, waits for them, and re-layouts: 0.07 us -> 3.53 us  [double_gather(): buf = jnp.stack(ordered, axis=1).reshape((-1,) + piece.shape)]
    another operation x11, other arithmetic: 5.05 us -> 2.42 us  [double_gather(): buf = jnp.stack(ordered, axis=1).reshape((-1,) + piece.shape)]
    dynamic_slice x2 -> x8, local copies, waits for them, and re-layouts: 1.96 us -> 4.41 us  [block_of(): lax.dynamic_index_in_dim(out, value >> j & 1, left.index(group[j]), keepd...]
    reduce_sum x16 -> x14, other arithmetic: 5.55 us -> 3.42 us  [per_draw(): return jnp.sum(product, axis=(0, 2))]
    add x4, other arithmetic: 0.2 us -> 2.29 us  [halve_sum(): total + swap_with(send, axis, size, None, masks[k]).astype(jnp.float32)]
  transfers between devices with their start and end apart: 30 -> 30, of which waited for: 13 -> 15; matrix products, arithmetic and copies ran while one was open for 25% -> 26% of each run, Pallas kernels for 0% -> 0%
where the time goes in v16:
time: 112 us
  starting transfers between devices  33.8 us (30%)
  waiting for transfers between devices  24 us (21%)
  local copies, waits for them, and re-layouts  21.7 us (19%)
  other arithmetic  15.8 us (14%)
  matrix products  14.3 us (13%)
  between operations  2.11 us (2%)
    ppermute x30, starting transfers between devices, swap_with(): return lax.ppermute(value, axis, pairs)  33.8 us
    ppermute x30, waiting for transfers between devices, swap_with(): return lax.ppermute(value, axis, pairs)  24 us
    unnamed x54, local copies, waits for them, and re-layouts  7.29 us
    dot_general x2, matrix products, cross_parts(): jnp.dot(counts_bf, item_range, preferred_element_type=jnp.float32)  6.18 us
    dot_general x2, matrix products, cross_parts(): to_items = jnp.dot(counts_t, user_range, preferred_element_type=jnp.float32)  5.01 us
    dynamic_slice x8, local copies, waits for them, and re-layouts, block_of(): lax.dynamic_index_in_dim(out, value >> j & 1, left.index(group[j]), keepd...  4.41 us
    another operation x4, local copies, waits for them, and re-layouts, double_gather(): buf = jnp.stack(ordered, axis=1).reshape((-1,) + piece.shape)  3.53 us
    reduce_sum x14, other arithmetic, per_draw(): return jnp.sum(product, axis=(0, 2))  3.42 us
  transfers between devices with their start and end apart: 30, of which 15 were waited for; matrix products, arithmetic and copies ran while one was open for 26% of the time, Pallas kernels for 0%

profile of v16, /device:TPU:0, one launch (start us, length us, event | category | flops | bytes accessed | tf_op | source)
XLA Modules:
  0.0 111.7 jit_solution(14620625388573053964)
XLA Ops:
  0.7 0.9 multiply_reduce_fusion.6
  1.6 5.1 %collective-permute-start = (bf16[1,64,256]{2,1,0:T(8,128)(2,1)S(1)}, bf16[1,64,256]{2,1,0:T(8,128)(2,1)S(1)}, u32[]{:S(2)}, u32[]{:S(2)}) collective-permute-start(bf16[1,64,256]{2,1,0:T(8,128)(2,1)S(1)} %get-tuple-element.74), channel_id=1, source_target_pairs={{0,24},{2,26},{4,28},{6,30},{8,16},{10,18},{12,20},{14,22},{16,8},... | collective-permute-start | bytes 98312 | tf_op jit(solution)/shard_map/ppermute | solution.py:45
  6.7 0.6 collective-permute-start.2
  7.4 1.2 %copy.52 = f32[1,384,256]{1,2,0:T(8,128)S(1)} copy(f32[1,384,256]{2,1,0:T(8,128)} %param.7) | data formatting | bytes 786432 | tf_op args[0]
  8.5 0.7 convert_element_type.275
  9.2 0.9 squeeze.74
  11.0 0.6 multiply_reduce_fusion.1
  13.0 2.6 %convert_reduce_fusion.1 = (f32[12,256]{1,0:T(8,128)S(1)}, f32[12,256]{1,0:T(8,128)S(1)}) fusion(s32[12,256,256]{2,1,0:T(8,128)} %bitcast.237), kind=kLoop, calls=%fused_computation.1 | loop fusion | flops 3139584 | bytes 3170304 | tf_op jit(solution)/shard_map/reduce_sum | solution.py:154
  16.2 2.7 %collective-permute-start.4 = (bf16[4,64,256]{2,1,0:T(8,128)(2,1)S(1)}, bf16[4,64,256]{2,1,0:T(8,128)(2,1)S(1)}, u32[]{:S(2)}, u32[]{:S(2)}) collective-permute-start(bf16[4,64,256]{2,1,0:T(8,128)(2,1)S(1)} %maximum_bitcast_fusion), channel_id=1, source_target_pairs={{0,6},{2,4},{4,2},{6,0},{8,14},{10,12},{12,10},{14,8},{16,22},{18,... | collective-permute-start | bytes 393224 | tf_op jit(solution)/shard_map/ppermute | solution.py:45
  19.7 1.3 %fusion = bf16[256,256,3,4]{1,3,2,0:T(4,128)(2,1)S(1)} fusion(bf16[12,256,256,1]{2,1,0,3:T(8,128)(2,1)S(1)} %convert_bitcast_fusion.4, pred[12,4]{0,1:T(4,128)(4,1)S(1)} %copy.49, pred[12,3]{0,1:T(4,128)(4,1)S(1)} %fusion.66), kind=kOutput, calls=%fused_computation.2 | convolution fusion | flops 18874512 | bytes 3145812 | tf_op jit(solution)/shard_map/trc,tij->cjri/dot_general | solution.py:150
  21.2 0.5 copy.59
  21.7 1.5 %copy.84 = bf16[96,8,4,256]{3,1,2,0:T(8,128)(2,1)} copy(bf16[96,8,4,256]{3,2,1,0:T(4,128)(2,1)S(1)} %bitcast.240) | data formatting | bytes 3145728
  23.9 1.5 %copy.82 = bf16[96,8,4,256]{3,1,2,0:T(8,128)(2,1)} copy(bf16[96,8,4,256]{3,2,1,0:T(4,128)(2,1)S(1)} %bitcast.239) | data formatting | bytes 3145728
  25.9 0.7 copy-done.12
  26.5 1.0 select_bitcast_fusion.11
  27.6 0.9 copy.54
  28.6 0.9 copy.53
  29.5 2.8 %fusion.4 = (f32[256]{0:T(256)S(1)}, f32[768,256]{1,0:T(8,128)}) fusion(bf16[1,2,384,256]{3,2,1,0:T(8,128)(2,1)} %copy.53, bf16[768,256]{1,0:T(8,128)(2,1)} %bitcast.270, f32[768]{0:T(1024)S(1)} %mul.192, bf16[768,1024]{1,0:T(8,128)(2,1)S(1)} %bitcast.243, bf16[1024,256]{1,0:T(8,128)(2,1)} %bitcast.254), kind=kOutput, calls=%fused_computation.18 | convolution fusion | flops 403832576 | bytes 3674112 | tf_op jit(solution)/shard_map/dot_general | solution.py:161
  32.6 3.3 %fusion.2 = (f32[256]{0:T(256)S(1)}, f32[1024,256]{1,0:T(8,128)}) fusion(bf16[4,4,64,256]{3,2,1,0:T(8,128)(2,1)S(1)} %copy-done.9, bf16[1024,256]{1,0:T(8,128)(2,1)S(1)} %bitcast.255, f32[1024]{0:T(1024)S(1)} %bitcast.277, bf16[1024,768]{0,1:T(8,128)(2,1)} %bitcast.244, bf16[768,256]{1,0:T(8,128)(2,1)} %bitcast.271), kind=kOutput, calls=%fused_computation.12 | convolution fusion | flops 404225792 | bytes 4068352 | tf_op jit(solution)/shard_map/dot_general | solution.py:163
  36.6 1.2 %dynamic-slice_convert_fusion.5 = (bf16[2,2,1,1,64,256]{5,4,3,2,1,0:T(8,128)(2,1)S(1)}, bf16[2,2,1,1,64,256]{5,4,3,2,1,0:T(8,128)(2,1)S(1)}, bf16[2,2,1,1,64,256]{5,4,3,2,1,0:T(8,128)(2,1)S(1)}) fusion(f32[2,2,2,2,64,256]{5,4,3,2,1,0:T(8,128)} %bitcast.268, s32[]{:T(128)S(6)} %select_n.385, s32[]{:T(128)S(6)} %select_n.387, s32[]{:T(128)S(6)} %select_n.393, ...), kind=kLoop, calls=%fused_computation.59 | loop fusion | bytes 786456 | tf_op jit(solution)/shard_map/convert_element_type | solution.py:90
  37.8 2.1 %collective-permute-start.9 = (bf16[280,256]{1,0:T(8,128)(2,1)S(1)}, bf16[280,256]{1,0:T(8,128)(2,1)}, u32[]{:S(2)}, u32[]{:S(2)}) collective-permute-start(bf16[280,256]{1,0:T(8,128)(2,1)S(1)} %get-tuple-element.86), channel_id=1, source_target_pairs={{0,6},{2,4},{4,2},{6,0},{8,14},{10,12},{12,10},{14,8},{16,22},{18,... | collective-permute-start | bytes 430088 | tf_op jit(solution)/shard_map/ppermute | solution.py:45
  39.8 1.1 collective-permute-start.8
  41.5 1.0 constant_dynamic-slice_fusion.5
  42.6 2.9 %collective-permute-done.9 = bf16[280,256]{1,0:T(8,128)(2,1)} collective-permute-done((bf16[280,256]{1,0:T(8,128)(2,1)S(1)}, bf16[280,256]{1,0:T(8,128)(2,1)}, u32[]{:S(2)}, u32[]{:S(2)}) %collective-permute-start.9) | collective-permute-done | bytes 143392 | tf_op jit(solution)/shard_map/ppermute | solution.py:45
  45.4 2.5 %collective-permute-done.8 = bf16[280,256]{1,0:T(8,128)(2,1)} collective-permute-done((bf16[280,256]{1,0:T(8,128)(2,1)S(1)}, bf16[280,256]{1,0:T(8,128)(2,1)}, u32[]{:S(2)}, u32[]{:S(2)}) %collective-permute-start.8) | collective-permute-done | bytes 143392 | tf_op jit(solution)/shard_map/ppermute | solution.py:45
  48.2 1.1 %fusion.21 = f32[280,256]{1,0:T(8,128)S(1)} fusion(f32[16,256]{1,0:T(8,128)S(1)} %broadcast.87, f32[8,256]{1,0:T(8,128)S(1)} %get-tuple-element.98, f32[256,256]{1,0:T(8,128)S(1)} %bitcast.247, bf16[280,256]{1,0:T(8,128)(2,1)} %collective-permute-done.9, bf16[280,256]{1,0:T(8,128)(2,1)} %collective-permute-done.8, bf16[280,256]{1,0:T(8,128)(2,1)} %collective-permute-done.7), kind=kLoop, calls=%fused_computation.50 | loop fusion | flops 573440 | bytes 1003520 | tf_op jit(solution)/shard_map/add | solution.py:94
  49.4 3.7 %collective-permute-start.12 = (bf16[88,256]{1,0:T(8,128)(2,1)S(1)}, bf16[88,256]{1,0:T(8,128)(2,1)S(1)}, u32[]{:S(2)}, u32[]{:S(2)}) collective-permute-start(bf16[88,256]{1,0:T(8,128)(2,1)S(1)} %get-tuple-element.83), channel_id=1, source_target_pairs={{0,24},{2,26},{4,28},{6,30},{8,16},{10,18},{12,20},{14,22},{16,8},... | collective-permute-start | bytes 135176 | tf_op jit(solution)/shard_map/ppermute | solution.py:45
  53.1 0.8 collective-permute-start.10
  53.9 2.0 %collective-permute-done.12 = bf16[88,256]{1,0:T(8,128)(2,1)S(1)} collective-permute-done((bf16[88,256]{1,0:T(8,128)(2,1)S(1)}, bf16[88,256]{1,0:T(8,128)(2,1)S(1)}, u32[]{:S(2)}, u32[]{:S(2)}) %collective-permute-start.12) | collective-permute-done | bytes 45088 | tf_op jit(solution)/shard_map/ppermute | solution.py:45
  55.9 2.2 %collective-permute-done.11 = bf16[88,256]{1,0:T(8,128)(2,1)S(1)} collective-permute-done((bf16[88,256]{1,0:T(8,128)(2,1)S(1)}, bf16[88,256]{1,0:T(8,128)(2,1)S(1)}, u32[]{:S(2)}, u32[]{:S(2)}) %collective-permute-start.11) | collective-permute-done | bytes 45088 | tf_op jit(solution)/shard_map/ppermute | solution.py:45
  58.2 1.1 collective-permute-done.13
  59.5 1.9 %collective-permute-start.16 = (bf16[1,64,256]{2,1,0:T(8,128)(2,1)S(1)}, bf16[1,64,256]{2,1,0:T(8,128)(2,1)S(1)}, u32[]{:S(2)}, u32[]{:S(2)}) collective-permute-start(bf16[1,64,256]{2,1,0:T(8,128)(2,1)S(1)} %get-tuple-element.28), channel_id=1, source_target_pairs={{0,24},{2,26},{4,28},{6,30},{8,16},{10,18},{12,20},{14,22},{16,8},... | collective-permute-start | bytes 98312 | tf_op jit(solution)/shard_map/ppermute | solution.py:45
  61.7 2.3 %collective-permute-start.18 = (bf16[1,64,256]{2,1,0:T(8,128)(2,1)S(1)}, bf16[1,64,256]{2,1,0:T(8,128)(2,1)S(1)}, u32[]{:S(2)}, u32[]{:S(2)}) collective-permute-start(bf16[1,64,256]{2,1,0:T(8,128)(2,1)S(1)} %get-tuple-element.28), channel_id=1, source_target_pairs={{0,8},{2,10},{4,12},{6,14},{8,0},{10,2},{12,4},{14,6},{16,24},{18,... | collective-permute-start | bytes 98312 | tf_op jit(solution)/shard_map/ppermute | solution.py:45
  64.7 0.6 reduce_sum.243
  66.5 1.6 %collective-permute-start.19 = (bf16[4,64,256]{2,1,0:T(8,128)(2,1)S(1)}, bf16[4,64,256]{2,1,0:T(8,128)(2,1)S(1)}, u32[]{:S(2)}, u32[]{:S(2)}) collective-permute-start(bf16[4,64,256]{2,1,0:T(8,128)(2,1)S(1)} %maximum_bitcast_fusion.1), channel_id=1, source_target_pairs={{0,6},{2,4},{4,2},{6,0},{8,14},{10,12},{12,10},{14,8},{16,22},{18,... | collective-permute-start | bytes 393224 | tf_op jit(solution)/shard_map/ppermute | solution.py:45
  68.1 1.4 %collective-permute-start.20 = (bf16[4,64,256]{2,1,0:T(8,128)(2,1)S(1)}, bf16[4,64,256]{2,1,0:T(8,128)(2,1)S(1)}, u32[]{:S(2)}, u32[]{:S(2)}) collective-permute-start(bf16[4,64,256]{2,1,0:T(8,128)(2,1)S(1)} %maximum_bitcast_fusion.1), channel_id=1, source_target_pairs={{0,4},{2,6},{4,0},{6,2},{8,12},{10,14},{12,8},{14,10},{16,20},{18,... | collective-permute-start | bytes 393224 | tf_op jit(solution)/shard_map/ppermute | solution.py:45
  70.3 0.6 reduce_sum.240
  71.6 2.2 %collective-permute-done.19 = bf16[4,64,256]{2,1,0:T(8,128)(2,1)S(1)} collective-permute-done((bf16[4,64,256]{2,1,0:T(8,128)(2,1)S(1)}, bf16[4,64,256]{2,1,0:T(8,128)(2,1)S(1)}, u32[]{:S(2)}, u32[]{:S(2)}) %collective-permute-start.19) | collective-permute-done | bytes 131104 | tf_op jit(solution)/shard_map/ppermute | solution.py:45
  73.8 2.3 %collective-permute-done.20 = bf16[4,64,256]{2,1,0:T(8,128)(2,1)S(1)} collective-permute-done((bf16[4,64,256]{2,1,0:T(8,128)(2,1)S(1)}, bf16[4,64,256]{2,1,0:T(8,128)(2,1)S(1)}, u32[]{:S(2)}, u32[]{:S(2)}) %collective-permute-start.20) | collective-permute-done | bytes 131104 | tf_op jit(solution)/shard_map/ppermute | solution.py:45
  76.3 0.8 copy.65
  77.1 1.0 select_bitcast_fusion.1
  78.1 0.9 copy.63
  79.1 3.4 %fusion.5 = (f32[256]{0:T(256)S(1)}, f32[768,256]{1,0:T(8,128)}) fusion(bf16[1,2,384,256]{3,2,1,0:T(8,128)(2,1)} %copy.63, bf16[768,256]{1,0:T(8,128)(2,1)} %bitcast.272, f32[768]{0:T(1024)S(1)} %mul.192, bf16[768,1024]{1,0:T(8,128)(2,1)} %bitcast.242, bf16[1024,256]{1,0:T(8,128)(2,1)} %bitcast.252), kind=kOutput, calls=%fused_computation.19 | convolution fusion | flops 403832576 | bytes 3674112 | tf_op jit(solution)/shard_map/dot_general | solution.py:161
  82.5 1.7 %fusion.3 = (f32[256]{0:T(256)S(1)}, f32[1024,256]{1,0:T(8,128)}) fusion(bf16[4,4,64,256]{3,2,1,0:T(8,128)(2,1)S(1)} %copy-done.8, bf16[1024,256]{1,0:T(8,128)(2,1)S(1)} %bitcast.253, f32[1024]{0:T(1024)S(1)} %bitcast.278, bf16[1024,768]{0,1:T(8,128)(2,1)S(1)} %bitcast.245, bf16[768,256]{1,0:T(8,128)(2,1)S(1)} %bitcast.273), kind=kOutput, calls=%fused_computation.13 | convolution fusion | flops 404225792 | bytes 4068352 | tf_op jit(solution)/shard_map/dot_general | solution.py:163
  84.8 1.0 constant_dynamic-slice_fusion.1
  85.8 1.2 %dynamic-slice_convert_fusion.2 = (bf16[2,2,1,1,64,256]{5,4,3,2,1,0:T(8,128)(2,1)S(1)}, bf16[2,2,1,1,64,256]{5,4,3,2,1,0:T(8,128)(2,1)S(1)}, bf16[2,2,1,1,64,256]{5,4,3,2,1,0:T(8,128)(2,1)S(1)}) fusion(f32[2,2,2,2,64,256]{5,4,3,2,1,0:T(8,128)} %bitcast.266, s32[]{:T(128)S(6)} %select_n.385, s32[]{:T(128)S(6)} %select_n.387, s32[]{:T(128)S(6)} %select_n.393, ...), kind=kLoop, calls=%fused_computation.56 | loop fusion | bytes 786456 | tf_op jit(solution)/shard_map/convert_element_type | solution.py:90
  87.0 0.8 pad_maximum_fusion.17
  87.7 1.6 %collective-permute-start.24 = (bf16[280,256]{1,0:T(8,128)(2,1)}, bf16[280,256]{1,0:T(8,128)(2,1)}, u32[]{:S(2)}, u32[]{:S(2)}) collective-permute-start(bf16[280,256]{1,0:T(8,128)(2,1)} %get-tuple-element.80), channel_id=1, source_target_pairs={{0,6},{2,4},{4,2},{6,0},{8,14},{10,12},{12,10},{14,8},{16,22},{18,... | collective-permute-start | bytes 430088 | tf_op jit(solution)/shard_map/ppermute | solution.py:45
  89.4 1.2 %collective-permute-start.23 = (bf16[280,256]{1,0:T(8,128)(2,1)}, bf16[280,256]{1,0:T(8,128)(2,1)}, u32[]{:S(2)}, u32[]{:S(2)}) collective-permute-start(bf16[280,256]{1,0:T(8,128)(2,1)} %get-tuple-element.79), channel_id=1, source_target_pairs={{0,4},{2,6},{4,0},{6,2},{8,12},{10,14},{12,8},{14,10},{16,20},{18,... | collective-permute-start | bytes 430088 | tf_op jit(solution)/shard_map/ppermute | solution.py:45
  90.6 0.6 collective-permute-start.22
  91.2 1.0 constant_dynamic-slice_fusion
  92.7 1.0 constant_dynamic-slice_fusion.2
  93.7 1.9 %collective-permute-done.24 = bf16[280,256]{1,0:T(8,128)(2,1)} collective-permute-done((bf16[280,256]{1,0:T(8,128)(2,1)}, bf16[280,256]{1,0:T(8,128)(2,1)}, u32[]{:S(2)}, u32[]{:S(2)}) %collective-permute-start.24) | collective-permute-done | bytes 143392 | tf_op jit(solution)/shard_map/ppermute | solution.py:45
  95.6 2.1 %collective-permute-done.23 = bf16[280,256]{1,0:T(8,128)(2,1)} collective-permute-done((bf16[280,256]{1,0:T(8,128)(2,1)}, bf16[280,256]{1,0:T(8,128)(2,1)}, u32[]{:S(2)}, u32[]{:S(2)}) %collective-permute-start.23) | collective-permute-done | bytes 143392 | tf_op jit(solution)/shard_map/ppermute | solution.py:45
  97.7 1.1 %fusion.24 = f32[280,256]{1,0:T(8,128)S(1)} fusion(f32[16,256]{1,0:T(8,128)S(1)} %broadcast.87, f32[8,256]{1,0:T(8,128)S(1)} %get-tuple-element.95, f32[256,256]{1,0:T(8,128)S(1)} %bitcast.246, bf16[280,256]{1,0:T(8,128)(2,1)} %collective-permute-done.24, bf16[280,256]{1,0:T(8,128)(2,1)} %collective-permute-done.23, bf16[280,256]{1,0:T(8,128)(2,1)} %collective-permute-done.22), kind=kLoop, calls=%fused_computation.53 | loop fusion | flops 573440 | bytes 1003520 | tf_op jit(solution)/shard_map/add | solution.py:94
  99.0 1.9 %collective-permute-start.27 = (bf16[88,256]{1,0:T(8,128)(2,1)S(1)}, bf16[88,256]{1,0:T(8,128)(2,1)S(1)}, u32[]{:S(2)}, u32[]{:S(2)}) collective-permute-start(bf16[88,256]{1,0:T(8,128)(2,1)S(1)} %get-tuple-element.77), channel_id=1, source_target_pairs={{0,24},{2,26},{4,28},{6,30},{8,16},{10,18},{12,20},{14,22},{16,8},... | collective-permute-start | bytes 135176 | tf_op jit(solution)/shard_map/ppermute | solution.py:45
  100.9 2.5 %collective-permute-start.25 = (bf16[88,256]{1,0:T(8,128)(2,1)S(1)}, bf16[88,256]{1,0:T(8,128)(2,1)S(1)}, u32[]{:S(2)}, u32[]{:S(2)}) collective-permute-start(bf16[88,256]{1,0:T(8,128)(2,1)S(1)} %get-tuple-element.75), channel_id=1, source_target_pairs={{0,8},{2,10},{4,12},{6,14},{8,0},{10,2},{12,4},{14,6},{16,24},{18,... | collective-permute-start | bytes 135176 | tf_op jit(solution)/shard_map/ppermute | solution.py:45
  103.4 1.6 %collective-permute-done.27 = bf16[88,256]{1,0:T(8,128)(2,1)S(1)} collective-permute-done((bf16[88,256]{1,0:T(8,128)(2,1)S(1)}, bf16[88,256]{1,0:T(8,128)(2,1)S(1)}, u32[]{:S(2)}, u32[]{:S(2)}) %collective-permute-start.27) | collective-permute-done | bytes 45088 | tf_op jit(solution)/shard_map/ppermute | solution.py:45
  105.0 1.4 %collective-permute-done.26 = bf16[88,256]{1,0:T(8,128)(2,1)S(1)} collective-permute-done((bf16[88,256]{1,0:T(8,128)(2,1)S(1)}, bf16[88,256]{1,0:T(8,128)(2,1)S(1)}, u32[]{:S(2)}, u32[]{:S(2)}) %collective-permute-start.26) | collective-permute-done | bytes 45088 | tf_op jit(solution)/shard_map/ppermute | solution.py:45
  106.5 1.1 collective-permute-done.28
  108.0 0.7 fusion.39
  108.7 1.2 %fusion.11 = (f32[1,384,256]{1,2,0:T(8,128)S(1)}, f32[1,384,256]{1,2,0:T(8,128)S(1)}) fusion(f32[384,256]{0,1:T(8,128)S(1)} %get-tuple-element.27, f32[1,384,256]{1,2,0:T(8,128)S(1)} %copy.69, f32[384,4,64]{0,2,1:T(8,128)S(1)} %fusion.53, bf16[384,256]{0,1:T(8,128)(2,1)} %collective-permute-done.29, f32[256]{0:T(256)S(1)} %mul.218, f32[256]{0:T(256)S(1)} %mul.216, ...), kind=kLoop, calls=%fused_computation.32 | loop fusion | flops 1671168 | bytes 3542016 | tf_op jit(solution)/shard_map/broadcast_in_dim | solution.py:222
  109.9 0.9 copy.71
  110.8 0.9 copy.72
  (176 shorter events, 11.6 us)
Async XLA Ops:
  0.6 10.3 %copy-start = (f32[64,64]{1,0:T(8,128)S(1)}, f32[64,64]{1,0:T(8,128)}, u32[]{:S(2)}) copy-start(f32[64,64]{1,0:T(8,128)} %param.9) | copy-start | bytes 49156
  0.6 11.3 %copy-start.4 = (f32[1,384,256]{2,1,0:T(8,128)S(1)}, f32[1,384,256]{2,1,0:T(8,128)}, u32[]{:S(2)}) copy-start(f32[1,384,256]{2,1,0:T(8,128)} %param.7) | copy-start | bytes 1179652
  0.7 9.5 %copy-start.21 = (s32[1,1,12,2]{2,3,1,0:T(2,128)S(1)}, s32[1,1,12,2]{2,3,1,0:T(2,128)}, u32[]{:S(2)}) copy-start(s32[1,1,12,2]{2,3,1,0:T(2,128)} %param.12) | copy-start | bytes 292
  0.7 10.9 %copy-start.13 = (f32[64,64]{1,0:T(8,128)S(1)}, f32[64,64]{1,0:T(8,128)}, u32[]{:S(2)}) copy-start(f32[64,64]{1,0:T(8,128)} %param.10) | copy-start | bytes 49156
  1.6 11.3 %collective-permute-start = (bf16[1,64,256]{2,1,0:T(8,128)(2,1)S(1)}, bf16[1,64,256]{2,1,0:T(8,128)(2,1)S(1)}, u32[]{:S(2)}, u32[]{:S(2)}) collective-permute-start(bf16[1,64,256]{2,1,0:T(8,128)(2,1)S(1)} %get-tuple-element.74), channel_id=1, source_target_pairs={{0,24},{2,26},{4,28},{6,30},{8,16},{10,18},{12,20},{14,22},{16,8},... | collective-permute-start | bytes 98312 | tf_op jit(solution)/shard_map/ppermute | solution.py:45
  6.7 6.2 %collective-permute-start.1 = (bf16[1,64,256]{2,1,0:T(8,128)(2,1)S(1)}, bf16[1,64,256]{2,1,0:T(8,128)(2,1)S(1)}, u32[]{:S(2)}, u32[]{:S(2)}) collective-permute-start(bf16[1,64,256]{2,1,0:T(8,128)(2,1)S(1)} %get-tuple-element.74), channel_id=1, source_target_pairs={{0,16},{2,18},{4,20},{6,22},{8,24},{10,26},{12,28},{14,30},{16,0},... | collective-permute-start | bytes 98312 | tf_op jit(solution)/shard_map/ppermute | solution.py:45
  6.7 6.2 %collective-permute-start.2 = (bf16[1,64,256]{2,1,0:T(8,128)(2,1)S(1)}, bf16[1,64,256]{2,1,0:T(8,128)(2,1)S(1)}, u32[]{:S(2)}, u32[]{:S(2)}) collective-permute-start(bf16[1,64,256]{2,1,0:T(8,128)(2,1)S(1)} %get-tuple-element.74), channel_id=1, source_target_pairs={{0,8},{2,10},{4,12},{6,14},{8,0},{10,2},{12,4},{14,6},{16,24},{18,... | collective-permute-start | bytes 98312 | tf_op jit(solution)/shard_map/ppermute | solution.py:45
  9.2 19.2 %collective-permute-start.3 = (bf16[1,384,256]{1,2,0:T(8,128)(2,1)}, bf16[1,384,256]{1,2,0:T(8,128)(2,1)S(1)}, u32[]{:S(2)}, u32[]{:S(2)}) collective-permute-start(bf16[1,384,256]{1,2,0:T(8,128)(2,1)} %convert_element_type.275), channel_id=1, source_target_pairs={{0,1},{1,0},{2,3},{3,2},{4,5},{5,4},{6,7},{7,6},{8,9},{9,8},{10,11... | collective-permute-start | bytes 589832 | tf_op jit(solution)/shard_map/ppermute | solution.py:45
  12.9 46.6 %copy-start.6 = (f32[64,256]{1,0:T(8,128)}, f32[64,256]{1,0:T(8,128)S(1)}, u32[]{:S(2)}) copy-start(f32[64,256]{1,0:T(8,128)S(1)} %reshape.283) | copy-start | bytes 196612
  13.0 2.8 %copy-start.1 = (s32[1,1,12,256,256]{4,3,2,1,0:T(8,128)S(1)}, s32[1,1,12,256,256]{4,3,2,1,0:T(8,128)}, u32[]{:S(2)}) copy-start(s32[1,1,12,256,256]{4,3,2,1,0:T(8,128)} %param.11) | copy-start | bytes 9437188
  16.2 9.2 %collective-permute-start.4 = (bf16[4,64,256]{2,1,0:T(8,128)(2,1)S(1)}, bf16[4,64,256]{2,1,0:T(8,128)(2,1)S(1)}, u32[]{:S(2)}, u32[]{:S(2)}) collective-permute-start(bf16[4,64,256]{2,1,0:T(8,128)(2,1)S(1)} %maximum_bitcast_fusion), channel_id=1, source_target_pairs={{0,6},{2,4},{4,2},{6,0},{8,14},{10,12},{12,10},{14,8},{16,22},{18,... | collective-permute-start | bytes 393224 | tf_op jit(solution)/shard_map/ppermute | solution.py:45
  18.8 7.0 %collective-permute-start.5 = (bf16[4,64,256]{2,1,0:T(8,128)(2,1)S(1)}, bf16[4,64,256]{2,1,0:T(8,128)(2,1)S(1)}, u32[]{:S(2)}, u32[]{:S(2)}) collective-permute-start(bf16[4,64,256]{2,1,0:T(8,128)(2,1)S(1)} %maximum_bitcast_fusion), channel_id=1, source_target_pairs={{0,4},{2,6},{4,0},{6,2},{8,12},{10,14},{12,8},{14,10},{16,20},{18,... | collective-permute-start | bytes 393224 | tf_op jit(solution)/shard_map/ppermute | solution.py:45
  19.3 7.2 %collective-permute-start.6 = (bf16[4,64,256]{2,1,0:T(8,128)(2,1)S(1)}, bf16[4,64,256]{2,1,0:T(8,128)(2,1)}, u32[]{:S(2)}, u32[]{:S(2)}) collective-permute-start(bf16[4,64,256]{2,1,0:T(8,128)(2,1)S(1)} %maximum_bitcast_fusion), channel_id=1, source_target_pairs={{0,2},{2,0},{4,6},{6,4},{8,10},{10,8},{12,14},{14,12},{16,18},{18,... | collective-permute-start | bytes 393224 | tf_op jit(solution)/shard_map/ppermute | solution.py:45
  25.9 0.7 copy-start.12
  27.6 1.9 %copy-start.2 = (bf16[96,8,4,256]{3,1,2,0:T(8,128)(2,1)S(1)}, bf16[96,8,4,256]{3,1,2,0:T(8,128)(2,1)}, u32[]{:S(2)}) copy-start(bf16[96,8,4,256]{3,1,2,0:T(8,128)(2,1)} %copy.84) | copy-start | bytes 4718596
  29.5 3.0 %copy-start.9 = (bf16[4,4,64,256]{3,2,1,0:T(8,128)(2,1)S(1)}, bf16[4,4,64,256]{3,2,1,0:T(8,128)(2,1)}, u32[]{:S(2)}) copy-start(bf16[4,4,64,256]{3,2,1,0:T(8,128)(2,1)} %copy.54) | copy-start | bytes 1572868
  32.5 3.6 %copy-start.10 = (f32[768,256]{1,0:T(8,128)S(1)}, f32[768,256]{1,0:T(8,128)}, u32[]{:S(2)}) copy-start(f32[768,256]{1,0:T(8,128)} %get-tuple-element.100) | copy-start | bytes 2359300
  36.4 29.2 %collective-permute-start.14 = (bf16[384,256]{0,1:T(8,128)(2,1)S(1)}, bf16[384,256]{0,1:T(8,128)(2,1)S(1)}, u32[]{:S(2)}, u32[]{:S(2)}) collective-permute-start(bf16[384,256]{0,1:T(8,128)(2,1)S(1)} %bitcast.274), channel_id=1, source_target_pairs={{0,1},{1,0},{2,3},{3,2},{4,5},{5,4},{6,7},{7,6},{8,9},{9,8},{10,11... | collective-permute-start | bytes 589832 | tf_op jit(solution)/shard_map/ppermute | solution.py:45
  37.8 7.7 %collective-permute-start.9 = (bf16[280,256]{1,0:T(8,128)(2,1)S(1)}, bf16[280,256]{1,0:T(8,128)(2,1)}, u32[]{:S(2)}, u32[]{:S(2)}) collective-permute-start(bf16[280,256]{1,0:T(8,128)(2,1)S(1)} %get-tuple-element.86), channel_id=1, source_target_pairs={{0,6},{2,4},{4,2},{6,0},{8,14},{10,12},{12,10},{14,8},{16,22},{18,... | collective-permute-start | bytes 430088 | tf_op jit(solution)/shard_map/ppermute | solution.py:45
  39.8 8.1 %collective-permute-start.8 = (bf16[280,256]{1,0:T(8,128)(2,1)S(1)}, bf16[280,256]{1,0:T(8,128)(2,1)}, u32[]{:S(2)}, u32[]{:S(2)}) collective-permute-start(bf16[280,256]{1,0:T(8,128)(2,1)S(1)} %get-tuple-element.85), channel_id=1, source_target_pairs={{0,4},{2,6},{4,0},{6,2},{8,12},{10,14},{12,8},{14,10},{16,20},{18,... | collective-permute-start | bytes 430088 | tf_op jit(solution)/shard_map/ppermute | solution.py:45
  40.9 7.2 %collective-permute-start.7 = (bf16[280,256]{1,0:T(8,128)(2,1)S(1)}, bf16[280,256]{1,0:T(8,128)(2,1)}, u32[]{:S(2)}, u32[]{:S(2)}) collective-permute-start(bf16[280,256]{1,0:T(8,128)(2,1)S(1)} %get-tuple-element.84), channel_id=1, source_target_pairs={{0,2},{2,0},{4,6},{6,4},{8,10},{10,8},{12,14},{14,12},{16,18},{18,... | collective-permute-start | bytes 430088 | tf_op jit(solution)/shard_map/ppermute | solution.py:45
  41.5 18.0 %copy-start.5 = (f32[1,64,256]{2,1,0:T(8,128)S(1)}, f32[1,64,256]{2,1,0:T(8,128)}, u32[]{:S(2)}) copy-start(f32[1,64,256]{2,1,0:T(8,128)} %param.8) | copy-start | bytes 196612
  42.6 21.6 %copy-start.14 = (f32[64,64]{1,0:T(8,128)S(1)}, f32[64,64]{1,0:T(8,128)}, u32[]{:S(2)}) copy-start(f32[64,64]{1,0:T(8,128)} %param.10) | copy-start | bytes 49156
  49.4 6.4 %collective-permute-start.12 = (bf16[88,256]{1,0:T(8,128)(2,1)S(1)}, bf16[88,256]{1,0:T(8,128)(2,1)S(1)}, u32[]{:S(2)}, u32[]{:S(2)}) collective-permute-start(bf16[88,256]{1,0:T(8,128)(2,1)S(1)} %get-tuple-element.83), channel_id=1, source_target_pairs={{0,24},{2,26},{4,28},{6,30},{8,16},{10,18},{12,20},{14,22},{16,8},... | collective-permute-start | bytes 135176 | tf_op jit(solution)/shard_map/ppermute | solution.py:45
  53.1 4.9 %collective-permute-start.11 = (bf16[88,256]{1,0:T(8,128)(2,1)S(1)}, bf16[88,256]{1,0:T(8,128)(2,1)S(1)}, u32[]{:S(2)}, u32[]{:S(2)}) collective-permute-start(bf16[88,256]{1,0:T(8,128)(2,1)S(1)} %get-tuple-element.82), channel_id=1, source_target_pairs={{0,16},{2,18},{4,20},{6,22},{8,24},{10,26},{12,28},{14,30},{16,0},... | collective-permute-start | bytes 135176 | tf_op jit(solution)/shard_map/ppermute | solution.py:45
  53.1 4.9 %collective-permute-start.10 = (bf16[88,256]{1,0:T(8,128)(2,1)S(1)}, bf16[88,256]{1,0:T(8,128)(2,1)S(1)}, u32[]{:S(2)}, u32[]{:S(2)}) collective-permute-start(bf16[88,256]{1,0:T(8,128)(2,1)S(1)} %get-tuple-element.81), channel_id=1, source_target_pairs={{0,8},{2,10},{4,12},{6,14},{8,0},{10,2},{12,4},{14,6},{16,24},{18,... | collective-permute-start | bytes 135176 | tf_op jit(solution)/shard_map/ppermute | solution.py:45
  58.1 1.2 %collective-permute-start.13 = (f32[8]{0:T(128)S(1)}, f32[8]{0:T(128)S(1)}, u32[]{:S(2)}, u32[]{:S(2)}) collective-permute-start(f32[8]{0:T(128)S(1)} %fusion.68), channel_id=1, source_target_pairs={{0,1},{1,0},{2,3},{3,2},{4,5},{5,4},{6,7},{7,6},{8,9},{9,8},{10,11... | collective-permute-start | bytes 104 | tf_op jit(solution)/shard_map/ppermute | solution.py:45
  59.3 6.4 %copy-start.17 = (f32[8]{0:T(128)}, f32[8]{0:T(128)S(1)}, u32[]{:S(2)}) copy-start(f32[8]{0:T(128)S(1)} %add.345) | copy-start | bytes 100
  59.5 6.2 %copy-start.15 = (f32[256]{0:T(256)}, f32[256]{0:T(256)S(1)}, u32[]{:S(2)}) copy-start(f32[256]{0:T(256)S(1)} %mul.198) | copy-start | bytes 3076
  59.5 6.8 %collective-permute-start.16 = (bf16[1,64,256]{2,1,0:T(8,128)(2,1)S(1)}, bf16[1,64,256]{2,1,0:T(8,128)(2,1)S(1)}, u32[]{:S(2)}, u32[]{:S(2)}) collective-permute-start(bf16[1,64,256]{2,1,0:T(8,128)(2,1)S(1)} %get-tuple-element.28), channel_id=1, source_target_pairs={{0,24},{2,26},{4,28},{6,30},{8,16},{10,18},{12,20},{14,22},{16,8},... | collective-permute-start | bytes 98312 | tf_op jit(solution)/shard_map/ppermute | solution.py:45
  61.4 5.0 %collective-permute-start.17 = (bf16[1,64,256]{2,1,0:T(8,128)(2,1)S(1)}, bf16[1,64,256]{2,1,0:T(8,128)(2,1)S(1)}, u32[]{:S(2)}, u32[]{:S(2)}) collective-permute-start(bf16[1,64,256]{2,1,0:T(8,128)(2,1)S(1)} %get-tuple-element.28), channel_id=1, source_target_pairs={{0,16},{2,18},{4,20},{6,22},{8,24},{10,26},{12,28},{14,30},{16,0},... | collective-permute-start | bytes 98312 | tf_op jit(solution)/shard_map/ppermute | solution.py:45
  61.7 4.7 %collective-permute-start.18 = (bf16[1,64,256]{2,1,0:T(8,128)(2,1)S(1)}, bf16[1,64,256]{2,1,0:T(8,128)(2,1)S(1)}, u32[]{:S(2)}, u32[]{:S(2)}) collective-permute-start(bf16[1,64,256]{2,1,0:T(8,128)(2,1)S(1)} %get-tuple-element.28), channel_id=1, source_target_pairs={{0,8},{2,10},{4,12},{6,14},{8,0},{10,2},{12,4},{14,6},{16,24},{18,... | collective-permute-start | bytes 98312 | tf_op jit(solution)/shard_map/ppermute | solution.py:45
  65.7 11.4 %collective-permute-start.15 = (bf16[1,384,256]{1,2,0:T(8,128)(2,1)S(1)}, bf16[1,384,256]{1,2,0:T(8,128)(2,1)}, u32[]{:S(2)}, u32[]{:S(2)}) collective-permute-start(bf16[1,384,256]{1,2,0:T(8,128)(2,1)S(1)} %get-tuple-element.26), channel_id=1, source_target_pairs={{0,1},{1,0},{2,3},{3,2},{4,5},{5,4},{6,7},{7,6},{8,9},{9,8},{10,11... | collective-permute-start | bytes 589832 | tf_op jit(solution)/shard_map/ppermute | solution.py:45
  66.5 7.3 %collective-permute-start.19 = (bf16[4,64,256]{2,1,0:T(8,128)(2,1)S(1)}, bf16[4,64,256]{2,1,0:T(8,128)(2,1)S(1)}, u32[]{:S(2)}, u32[]{:S(2)}) collective-permute-start(bf16[4,64,256]{2,1,0:T(8,128)(2,1)S(1)} %maximum_bitcast_fusion.1), channel_id=1, source_target_pairs={{0,6},{2,4},{4,2},{6,0},{8,14},{10,12},{12,10},{14,8},{16,22},{18,... | collective-permute-start | bytes 393224 | tf_op jit(solution)/shard_map/ppermute | solution.py:45
  68.1 8.0 %collective-permute-start.20 = (bf16[4,64,256]{2,1,0:T(8,128)(2,1)S(1)}, bf16[4,64,256]{2,1,0:T(8,128)(2,1)S(1)}, u32[]{:S(2)}, u32[]{:S(2)}) collective-permute-start(bf16[4,64,256]{2,1,0:T(8,128)(2,1)S(1)} %maximum_bitcast_fusion.1), channel_id=1, source_target_pairs={{0,4},{2,6},{4,0},{6,2},{8,12},{10,14},{12,8},{14,10},{16,20},{18,... | collective-permute-start | bytes 393224 | tf_op jit(solution)/shard_map/ppermute | solution.py:45
  69.6 6.5 %collective-permute-start.21 = (bf16[4,64,256]{2,1,0:T(8,128)(2,1)S(1)}, bf16[4,64,256]{2,1,0:T(8,128)(2,1)S(1)}, u32[]{:S(2)}, u32[]{:S(2)}) collective-permute-start(bf16[4,64,256]{2,1,0:T(8,128)(2,1)S(1)} %maximum_bitcast_fusion.1), channel_id=1, source_target_pairs={{0,2},{2,0},{4,6},{6,4},{8,10},{10,8},{12,14},{14,12},{16,18},{18,... | collective-permute-start | bytes 393224 | tf_op jit(solution)/shard_map/ppermute | solution.py:45
  79.1 3.4 %copy-start.3 = (bf16[96,8,4,256]{3,1,2,0:T(8,128)(2,1)S(1)}, bf16[96,8,4,256]{3,1,2,0:T(8,128)(2,1)}, u32[]{:S(2)}) copy-start(bf16[96,8,4,256]{3,1,2,0:T(8,128)(2,1)} %copy.82) | copy-start | bytes 4718596
  79.1 3.4 %copy-start.8 = (bf16[4,4,64,256]{3,2,1,0:T(8,128)(2,1)S(1)}, bf16[4,4,64,256]{3,2,1,0:T(8,128)(2,1)}, u32[]{:S(2)}) copy-start(bf16[4,4,64,256]{3,2,1,0:T(8,128)(2,1)} %copy.65) | copy-start | bytes 1572868
  79.1 3.4 %copy-start.11 = (bf16[1,2,384,256]{3,2,1,0:T(8,128)(2,1)S(1)}, bf16[1,2,384,256]{3,2,1,0:T(8,128)(2,1)}, u32[]{:S(2)}) copy-start(bf16[1,2,384,256]{3,2,1,0:T(8,128)(2,1)} %copy.63) | copy-start | bytes 1179652
  82.5 2.2 %copy-start.19 = (f32[4]{0:T(128)S(1)}, f32[4]{0:T(128)}, u32[]{:S(2)}) copy-start(f32[4]{0:T(128)} %reduce_sum.243) | copy-start | bytes 52
  82.5 2.2 %copy-start.20 = (f32[4]{0:T(128)S(1)}, f32[4]{0:T(128)}, u32[]{:S(2)}) copy-start(f32[4]{0:T(128)} %reduce_sum.240) | copy-start | bytes 52
  82.5 2.2 %copy-start.22 = (f32[4]{0:T(128)S(1)}, f32[4]{0:T(128)}, u32[]{:S(2)}) copy-start(f32[4]{0:T(128)} %add.352) | copy-start | bytes 52
  87.7 7.9 %collective-permute-start.24 = (bf16[280,256]{1,0:T(8,128)(2,1)}, bf16[280,256]{1,0:T(8,128)(2,1)}, u32[]{:S(2)}, u32[]{:S(2)}) collective-permute-start(bf16[280,256]{1,0:T(8,128)(2,1)} %get-tuple-element.80), channel_id=1, source_target_pairs={{0,6},{2,4},{4,2},{6,0},{8,14},{10,12},{12,10},{14,8},{16,22},{18,... | collective-permute-start | bytes 430088 | tf_op jit(solution)/shard_map/ppermute | solution.py:45
  89.4 8.4 %collective-permute-start.23 = (bf16[280,256]{1,0:T(8,128)(2,1)}, bf16[280,256]{1,0:T(8,128)(2,1)}, u32[]{:S(2)}, u32[]{:S(2)}) collective-permute-start(bf16[280,256]{1,0:T(8,128)(2,1)} %get-tuple-element.79), channel_id=1, source_target_pairs={{0,4},{2,6},{4,0},{6,2},{8,12},{10,14},{12,8},{14,10},{16,20},{18,... | collective-permute-start | bytes 430088 | tf_op jit(solution)/shard_map/ppermute | solution.py:45
  90.6 7.2 %collective-permute-start.22 = (bf16[280,256]{1,0:T(8,128)(2,1)}, bf16[280,256]{1,0:T(8,128)(2,1)}, u32[]{:S(2)}, u32[]{:S(2)}) collective-permute-start(bf16[280,256]{1,0:T(8,128)(2,1)} %get-tuple-element.78), channel_id=1, source_target_pairs={{0,2},{2,0},{4,6},{6,4},{8,10},{10,8},{12,14},{14,12},{16,18},{18,... | collective-permute-start | bytes 430088 | tf_op jit(solution)/shard_map/ppermute | solution.py:45
  92.6 15.0 %copy-start.18 = (f32[8]{0:T(128)S(1)}, f32[8]{0:T(128)}, u32[]{:S(2)}) copy-start(f32[8]{0:T(128)} %copy-done.17) | copy-start | bytes 100
  92.6 15.4 %copy-start.7 = (f32[64,256]{1,0:T(8,128)S(1)}, f32[64,256]{1,0:T(8,128)}, u32[]{:S(2)}) copy-start(f32[64,256]{1,0:T(8,128)} %copy-done.6) | copy-start | bytes 196612
  92.6 15.4 %copy-start.16 = (f32[256]{0:T(256)S(1)}, f32[256]{0:T(256)}, u32[]{:S(2)}) copy-start(f32[256]{0:T(256)} %copy-done.15) | copy-start | bytes 3076
  92.6 16.1 %collective-permute-start.29 = (bf16[384,256]{0,1:T(8,128)(2,1)S(1)}, bf16[384,256]{0,1:T(8,128)(2,1)}, u32[]{:S(2)}, u32[]{:S(2)}) collective-permute-start(bf16[384,256]{0,1:T(8,128)(2,1)S(1)} %bitcast.275), channel_id=1, source_target_pairs={{0,1},{1,0},{2,3},{3,2},{4,5},{5,4},{6,7},{7,6},{8,9},{9,8},{10,11... | collective-permute-start | bytes 589832 | tf_op jit(solution)/shard_map/ppermute | solution.py:45
  99.0 6.0 %collective-permute-start.27 = (bf16[88,256]{1,0:T(8,128)(2,1)S(1)}, bf16[88,256]{1,0:T(8,128)(2,1)S(1)}, u32[]{:S(2)}, u32[]{:S(2)}) collective-permute-start(bf16[88,256]{1,0:T(8,128)(2,1)S(1)} %get-tuple-element.77), channel_id=1, source_target_pairs={{0,24},{2,26},{4,28},{6,30},{8,16},{10,18},{12,20},{14,22},{16,8},... | collective-permute-start | bytes 135176 | tf_op jit(solution)/shard_map/ppermute | solution.py:45
  100.9 5.5 %collective-permute-start.26 = (bf16[88,256]{1,0:T(8,128)(2,1)S(1)}, bf16[88,256]{1,0:T(8,128)(2,1)S(1)}, u32[]{:S(2)}, u32[]{:S(2)}) collective-permute-start(bf16[88,256]{1,0:T(8,128)(2,1)S(1)} %get-tuple-element.76), channel_id=1, source_target_pairs={{0,16},{2,18},{4,20},{6,22},{8,24},{10,26},{12,28},{14,30},{16,0},... | collective-permute-start | bytes 135176 | tf_op jit(solution)/shard_map/ppermute | solution.py:45
  100.9 5.5 %collective-permute-start.25 = (bf16[88,256]{1,0:T(8,128)(2,1)S(1)}, bf16[88,256]{1,0:T(8,128)(2,1)S(1)}, u32[]{:S(2)}, u32[]{:S(2)}) collective-permute-start(bf16[88,256]{1,0:T(8,128)(2,1)S(1)} %get-tuple-element.75), channel_id=1, source_target_pairs={{0,8},{2,10},{4,12},{6,14},{8,0},{10,2},{12,4},{14,6},{16,24},{18,... | collective-permute-start | bytes 135176 | tf_op jit(solution)/shard_map/ppermute | solution.py:45
  106.4 1.2 %collective-permute-start.28 = (f32[8]{0:T(128)S(1)}, f32[8]{0:T(128)S(1)}, u32[]{:S(2)}, u32[]{:S(2)}) collective-permute-start(f32[8]{0:T(128)S(1)} %fusion.67), channel_id=1, source_target_pairs={{0,1},{1,0},{2,3},{3,2},{4,5},{5,4},{6,7},{7,6},{8,9},{9,8},{10,11... | collective-permute-start | bytes 104 | tf_op jit(solution)/shard_map/ppermute | solution.py:45

commit v17 on v15

--- a/solution.py
+++ b/solution.py
@@ -170,7 +170,9 @@
     def operate(user_vec, item_vec, counts):
         user_range = user_range_of(user_vec)
         if counts is None:
-            item_range, tiles = double_gather(item_vec.astype(jnp.bfloat16), "user", count_tiles[0, 0])
+            item_range, (tiles, user_vec, item_vec) = double_gather(
+                item_vec.astype(jnp.bfloat16), "user", (count_tiles[0, 0], user_vec, item_vec)
+            )
             counts = build_counts(tiles)
         else:
             item_range = double_gather(item_vec.astype(jnp.bfloat16), "user")

time: 107 us -> 104 us (0.972)
  local copies, waits for them, and re-layouts: 19.7 us -> 13 us
  other arithmetic: 16 us -> 19 us
  matrix products: 9.66 us -> 11.6 us
    reshape x6 -> x4, local copies, waits for them, and re-layouts: 4.23 us -> 0.65 us  [prior_term(): return mixed.reshape(row_total, DRAWS * DIM)]
    reduce_sum x16, other arithmetic: 5.55 us -> 2.69 us  [per_draw(): return jnp.sum(product, axis=(0, 2))]
    convert_element_type x0 -> x2, other arithmetic: none -> 2.54 us  [the longest x1 1.69 us: user_range_of(): return double_gather(user_vec.astype(jnp.bfloat16), 'item')]
    another operation x3 -> x1, local copies, waits for them, and re-layouts: 2.09 us -> 0.01 us  [the longest x2 2.09 us: prior_term(): grouped = field_vec.reshape(row_total * DRAWS, DIM)]
    reduce_sum x1, other arithmetic: 0.59 us -> 2.48 us  [build_counts(): tile_cols = jnp.sum(tiles_bf, axis=1, dtype=jnp.float32)]
    dot_general x1, matrix products: 1.3 us -> 2.71 us  [build_counts(): jnp.einsum('trc,tij->cjri', place, tiles_bf, preferred_element_type=jnp.b...]
    dot_general x2, matrix products: 2.06 us -> 3.36 us  [cross_parts(): jnp.dot(counts_bf, item_range, preferred_element_type=jnp.float32)]
    broadcast_in_dim x2, other arithmetic: 0.13 us -> 1.4 us  [double_gather(): buf = piece[None]]
  transfers between devices with their start and end apart: 30 -> 30, of which waited for: 13 -> 16; matrix products, arithmetic and copies ran while one was open for 25% -> 26% of each run, Pallas kernels for 0% -> 0%
where the time goes in v17:
time: 104 us
  starting transfers between devices  33.3 us (32%)
  waiting for transfers between devices  24.7 us (24%)
  other arithmetic  19 us (18%)
  local copies, waits for them, and re-layouts  13 us (12%)
  matrix products  11.6 us (11%)
  between operations  2.13 us (2%)
    ppermute x30, starting transfers between devices, swap_with(): return lax.ppermute(value, axis, pairs)  33.3 us
    ppermute x30, waiting for transfers between devices, swap_with(): return lax.ppermute(value, axis, pairs)  24.7 us
    another operation x11, other arithmetic, double_gather(): buf = jnp.stack(ordered, axis=1).reshape((-1,) + piece.shape)  4.41 us
    convert_element_type x6, local copies, waits for them, and re-layouts, halve_sum(): send = block_of(digit ^ k).astype(stage_type)  4.1 us
    dot_general x2, matrix products, cross_parts(): to_items = jnp.dot(counts_t, user_range, preferred_element_type=jnp.float32)  3.49 us
    dot_general x2, matrix products, cross_parts(): jnp.dot(counts_bf, item_range, preferred_element_type=jnp.float32)  3.36 us
    broadcast_in_dim x2, other arithmetic, per_device(): return (sol_user[None], sol_item[None], res_user[None], res_item[None])  2.94 us
    dot_general x1, matrix products, build_counts(): jnp.einsum('trc,tij->cjri', place, tiles_bf, preferred_element_type=jnp.b...  2.71 us
  transfers between devices with their start and end apart: 30, of which 16 were waited for; matrix products, arithmetic and copies ran while one was open for 26% of the time, Pallas kernels for 0%

profile of v17, /device:TPU:0, one launch (start us, length us, event | category | flops | bytes accessed | tf_op | source)
XLA Modules:
  0.0 103.7 jit_solution(13207409311180802555)
XLA Ops:
  0.6 0.9 convert_element_type.273
  1.5 3.0 %collective-permute-start.2 = (bf16[1,64,256]{2,1,0:T(8,128)(2,1)S(1)}, bf16[1,64,256]{2,1,0:T(8,128)(2,1)S(1)}, u32[]{:S(2)}, u32[]{:S(2)}) collective-permute-start(bf16[1,64,256]{2,1,0:T(8,128)(2,1)S(1)} %convert_element_type.273), channel_id=1, source_target_pairs={{0,8},{2,10},{4,12},{6,14},{8,0},{10,2},{12,4},{14,6},{16,24},{18,... | collective-permute-start | bytes 98312 | tf_op jit(solution)/shard_map/ppermute | solution.py:45
  4.5 2.6 %collective-permute-start.1 = (bf16[1,64,256]{2,1,0:T(8,128)(2,1)S(1)}, bf16[1,64,256]{2,1,0:T(8,128)(2,1)S(1)}, u32[]{:S(2)}, u32[]{:S(2)}) collective-permute-start(bf16[1,64,256]{2,1,0:T(8,128)(2,1)S(1)} %convert_element_type.273), channel_id=1, source_target_pairs={{0,16},{2,18},{4,20},{6,22},{8,24},{10,26},{12,28},{14,30},{16,0},... | collective-permute-start | bytes 98312 | tf_op jit(solution)/shard_map/ppermute | solution.py:45
  7.1 1.7 %convert_element_type.275 = bf16[1,384,256]{2,1,0:T(8,128)(2,1)} convert(f32[1,384,256]{2,1,0:T(8,128)} %param.7) | non-fusion elementwise | flops 98304 | bytes 589824 | tf_op jit(solution)/shard_map/convert_element_type | solution.py:168
  9.5 0.8 slice_bitcast_fusion.1
  10.5 2.3 %collective-permute-done = bf16[1,64,256]{2,1,0:T(8,128)(2,1)S(1)} collective-permute-done((bf16[1,64,256]{2,1,0:T(8,128)(2,1)S(1)}, bf16[1,64,256]{2,1,0:T(8,128)(2,1)S(1)}, u32[]{:S(2)}, u32[]{:S(2)}) %collective-permute-start) | collective-permute-done | bytes 32800 | tf_op jit(solution)/shard_map/ppermute | solution.py:45
  12.8 0.9 select_bitcast_fusion.19
  13.7 1.6 %collective-permute-start.6 = (bf16[4,64,256]{2,1,0:T(8,128)(2,1)S(1)}, bf16[4,64,256]{2,1,0:T(8,128)(2,1)S(1)}, u32[]{:S(2)}, u32[]{:S(2)}) collective-permute-start(bf16[4,64,256]{2,1,0:T(8,128)(2,1)S(1)} %maximum_bitcast_fusion), channel_id=1, source_target_pairs={{0,2},{2,0},{4,6},{6,4},{8,10},{10,8},{12,14},{14,12},{16,18},{18,... | collective-permute-start | bytes 393224 | tf_op jit(solution)/shard_map/ppermute | solution.py:45
  15.3 1.5 %collective-permute-start.5 = (bf16[4,64,256]{2,1,0:T(8,128)(2,1)S(1)}, bf16[4,64,256]{2,1,0:T(8,128)(2,1)S(1)}, u32[]{:S(2)}, u32[]{:S(2)}) collective-permute-start(bf16[4,64,256]{2,1,0:T(8,128)(2,1)S(1)} %maximum_bitcast_fusion), channel_id=1, source_target_pairs={{0,4},{2,6},{4,0},{6,2},{8,12},{10,14},{12,8},{14,10},{16,20},{18,... | collective-permute-start | bytes 393224 | tf_op jit(solution)/shard_map/ppermute | solution.py:45
  16.8 0.5 collective-permute-start.4
  17.3 2.5 %convert_reduce_fusion.1 = (f32[12,256]{1,0:T(8,128)S(1)}, f32[12,256]{1,0:T(8,128)S(1)}) fusion(s32[12,256,256]{2,1,0:T(8,128)} %bitcast.191), kind=kLoop, calls=%fused_computation.1 | loop fusion | flops 3139584 | bytes 3170304 | tf_op jit(solution)/shard_map/reduce_sum | solution.py:154
  19.8 1.5 %convert_bitcast_fusion.2 = bf16[12,256,256,1]{2,1,0,3:T(8,128)(2,1)} fusion(s32[12,256,256]{2,1,0:T(8,128)S(1)} %bitcast.192), kind=kLoop, calls=%fused_computation.200 | loop fusion | flops 786432 | bytes 4718592 | tf_op jit(solution)/shard_map/convert_element_type | solution.py:146
  22.6 0.8 fusion.56
  23.6 2.7 %fusion = bf16[256,256,3,4]{1,3,2,0:T(4,128)(2,1)S(1)} fusion(bf16[12,256,256,1]{2,1,0,3:T(8,128)(2,1)} %convert_bitcast_fusion.2, pred[12,4]{0,1:T(4,128)(4,1)S(1)} %copy.27, pred[12,3]{0,1:T(4,128)(4,1)S(1)} %fusion.49), kind=kOutput, calls=%fused_computation.2 | convolution fusion | flops 18874512 | bytes 3145812 | tf_op jit(solution)/shard_map/trc,tij->cjri/dot_general | solution.py:150
  26.8 0.5 copy.29
  27.7 0.5 copy.33
  28.7 0.7 copy-done.14
  29.4 1.0 select_bitcast_fusion.11
  30.7 1.8 %fusion.2 = (f32[256]{0:T(256)S(1)}, f32[1024,256]{1,0:T(8,128)}) fusion(bf16[4,4,64,256]{3,2,1,0:T(8,128)(2,1)S(1)} %copy.30, bf16[1024,256]{1,0:T(8,128)(2,1)S(1)} %bitcast.212, f32[1024]{0:T(1024)S(1)} %bitcast.231, bf16[1024,768]{0,1:T(8,128)(2,1)S(1)} %bitcast.197, bf16[768,256]{1,0:T(8,128)(2,1)S(1)} %bitcast.226), kind=kOutput, calls=%fused_computation.12 | convolution fusion | flops 404225792 | bytes 4068352 | tf_op jit(solution)/shard_map/dot_general | solution.py:163
  32.7 1.9 %fusion.4 = (f32[256]{0:T(256)S(1)}, f32[768,256]{1,0:T(8,128)S(1)}) fusion(bf16[1,2,384,256]{3,2,1,0:T(8,128)(2,1)} %copy-done.13, bf16[768,256]{1,0:T(8,128)(2,1)} %bitcast.227, f32[768]{0:T(1024)S(1)} %mul.186, bf16[768,1024]{1,0:T(8,128)(2,1)S(1)} %bitcast.199, bf16[1024,256]{1,0:T(8,128)(2,1)} %bitcast.213), kind=kOutput, calls=%fused_computation.18 | convolution fusion | flops 403832576 | bytes 3674112 | tf_op jit(solution)/shard_map/dot_general | solution.py:161
  34.9 1.2 %dynamic-slice_convert_fusion.7 = (bf16[2,2,1,1,64,256]{5,4,3,2,1,0:T(8,128)(2,1)S(1)}, bf16[2,2,1,1,64,256]{5,4,3,2,1,0:T(8,128)(2,1)S(1)}, bf16[2,2,1,1,64,256]{5,4,3,2,1,0:T(8,128)(2,1)S(1)}) fusion(f32[2,2,2,2,64,256]{5,4,3,2,1,0:T(8,128)} %bitcast.224, s32[]{:T(128)S(6)} %select_n.385, s32[]{:T(128)S(6)} %select_n.387, s32[]{:T(128)S(6)} %select_n.393, ...), kind=kLoop, calls=%fused_computation.55 | loop fusion | bytes 786456 | tf_op jit(solution)/shard_map/convert_element_type | solution.py:90
  36.1 1.6 %collective-permute-start.7 = (bf16[280,256]{1,0:T(8,128)(2,1)S(1)}, bf16[280,256]{1,0:T(8,128)(2,1)S(1)}, u32[]{:S(2)}, u32[]{:S(2)}) collective-permute-start(bf16[280,256]{1,0:T(8,128)(2,1)S(1)} %get-tuple-element.82), channel_id=1, source_target_pairs={{0,2},{2,0},{4,6},{6,4},{8,10},{10,8},{12,14},{14,12},{16,18},{18,... | collective-permute-start | bytes 430088 | tf_op jit(solution)/shard_map/ppermute | solution.py:45
  37.7 1.5 %collective-permute-start.8 = (bf16[280,256]{1,0:T(8,128)(2,1)S(1)}, bf16[280,256]{1,0:T(8,128)(2,1)S(1)}, u32[]{:S(2)}, u32[]{:S(2)}) collective-permute-start(bf16[280,256]{1,0:T(8,128)(2,1)S(1)} %get-tuple-element.83), channel_id=1, source_target_pairs={{0,4},{2,6},{4,0},{6,2},{8,12},{10,14},{12,8},{14,10},{16,20},{18,... | collective-permute-start | bytes 430088 | tf_op jit(solution)/shard_map/ppermute | solution.py:45
  39.8 1.0 constant_dynamic-slice_fusion.1
  40.8 1.1 %collective-permute-done.7 = bf16[280,256]{1,0:T(8,128)(2,1)S(1)} collective-permute-done((bf16[280,256]{1,0:T(8,128)(2,1)S(1)}, bf16[280,256]{1,0:T(8,128)(2,1)S(1)}, u32[]{:S(2)}, u32[]{:S(2)}) %collective-permute-start.7) | collective-permute-done | bytes 143392 | tf_op jit(solution)/shard_map/ppermute | solution.py:45
  41.9 1.2 %collective-permute-done.8 = bf16[280,256]{1,0:T(8,128)(2,1)S(1)} collective-permute-done((bf16[280,256]{1,0:T(8,128)(2,1)S(1)}, bf16[280,256]{1,0:T(8,128)(2,1)S(1)}, u32[]{:S(2)}, u32[]{:S(2)}) %collective-permute-start.8) | collective-permute-done | bytes 143392 | tf_op jit(solution)/shard_map/ppermute | solution.py:45
  43.1 2.1 %collective-permute-done.9 = bf16[280,256]{1,0:T(8,128)(2,1)S(1)} collective-permute-done((bf16[280,256]{1,0:T(8,128)(2,1)S(1)}, bf16[280,256]{1,0:T(8,128)(2,1)S(1)}, u32[]{:S(2)}, u32[]{:S(2)}) %collective-permute-start.9) | collective-permute-done | bytes 143392 | tf_op jit(solution)/shard_map/ppermute | solution.py:45
  45.5 2.7 %collective-permute-start.11 = (bf16[88,256]{1,0:T(8,128)(2,1)S(1)}, bf16[88,256]{1,0:T(8,128)(2,1)S(1)}, u32[]{:S(2)}, u32[]{:S(2)}) collective-permute-start(bf16[88,256]{1,0:T(8,128)(2,1)S(1)} %get-tuple-element.80), channel_id=1, source_target_pairs={{0,16},{2,18},{4,20},{6,22},{8,24},{10,26},{12,28},{14,30},{16,0},... | collective-permute-start | bytes 135176 | tf_op jit(solution)/shard_map/ppermute | solution.py:45
  48.2 1.6 %collective-permute-start.12 = (bf16[88,256]{1,0:T(8,128)(2,1)S(1)}, bf16[88,256]{1,0:T(8,128)(2,1)S(1)}, u32[]{:S(2)}, u32[]{:S(2)}) collective-permute-start(bf16[88,256]{1,0:T(8,128)(2,1)S(1)} %get-tuple-element.81), channel_id=1, source_target_pairs={{0,24},{2,26},{4,28},{6,30},{8,16},{10,18},{12,20},{14,22},{16,8},... | collective-permute-start | bytes 135176 | tf_op jit(solution)/shard_map/ppermute | solution.py:45
  49.9 0.6 collective-permute-done.11
  50.5 3.6 %collective-permute-done.12 = bf16[88,256]{1,0:T(8,128)(2,1)S(1)} collective-permute-done((bf16[88,256]{1,0:T(8,128)(2,1)S(1)}, bf16[88,256]{1,0:T(8,128)(2,1)S(1)}, u32[]{:S(2)}, u32[]{:S(2)}) %collective-permute-start.12) | collective-permute-done | bytes 45088 | tf_op jit(solution)/shard_map/ppermute | solution.py:45
  54.2 1.1 %collective-permute-done.13 = f32[8]{0:T(128)S(1)} collective-permute-done((f32[8]{0:T(128)S(1)}, f32[8]{0:T(128)S(1)}, u32[]{:S(2)}, u32[]{:S(2)}) %collective-permute-start.13) | collective-permute-done | bytes 64 | tf_op jit(solution)/shard_map/ppermute | solution.py:45
  55.9 0.6 convert_bitcast_fusion.1
  56.6 2.2 %collective-permute-start.17 = (bf16[1,64,256]{2,1,0:T(8,128)(2,1)}, bf16[1,64,256]{2,1,0:T(8,128)(2,1)}, u32[]{:S(2)}, u32[]{:S(2)}) collective-permute-start(bf16[1,64,256]{2,1,0:T(8,128)(2,1)} %get-tuple-element.28), channel_id=1, source_target_pairs={{0,16},{2,18},{4,20},{6,22},{8,24},{10,26},{12,28},{14,30},{16,0},... | collective-permute-start | bytes 98312 | tf_op jit(solution)/shard_map/ppermute | solution.py:45
  58.8 2.2 %collective-permute-start.16 = (bf16[1,64,256]{2,1,0:T(8,128)(2,1)}, bf16[1,64,256]{2,1,0:T(8,128)(2,1)}, u32[]{:S(2)}, u32[]{:S(2)}) collective-permute-start(bf16[1,64,256]{2,1,0:T(8,128)(2,1)} %get-tuple-element.28), channel_id=1, source_target_pairs={{0,24},{2,26},{4,28},{6,30},{8,16},{10,18},{12,20},{14,22},{16,8},... | collective-permute-start | bytes 98312 | tf_op jit(solution)/shard_map/ppermute | solution.py:45
  61.5 0.6 reduce_sum.255
  62.2 0.6 reduce_sum.261
  62.8 0.8 convert_bitcast_fusion
  63.8 0.8 fusion.58
  64.8 0.8 select_bitcast_fusion.15
  65.7 1.2 %collective-permute-start.21 = (bf16[4,64,256]{2,1,0:T(8,128)(2,1)S(1)}, bf16[4,64,256]{2,1,0:T(8,128)(2,1)S(1)}, u32[]{:S(2)}, u32[]{:S(2)}) collective-permute-start(bf16[4,64,256]{2,1,0:T(8,128)(2,1)S(1)} %maximum_bitcast_fusion.1), channel_id=1, source_target_pairs={{0,2},{2,0},{4,6},{6,4},{8,10},{10,8},{12,14},{14,12},{16,18},{18,... | collective-permute-start | bytes 393224 | tf_op jit(solution)/shard_map/ppermute | solution.py:45
  66.9 0.8 collective-permute-start.20
  67.8 1.5 %collective-permute-start.19 = (bf16[4,64,256]{2,1,0:T(8,128)(2,1)S(1)}, bf16[4,64,256]{2,1,0:T(8,128)(2,1)S(1)}, u32[]{:S(2)}, u32[]{:S(2)}) collective-permute-start(bf16[4,64,256]{2,1,0:T(8,128)(2,1)S(1)} %maximum_bitcast_fusion.1), channel_id=1, source_target_pairs={{0,6},{2,4},{4,2},{6,0},{8,14},{10,12},{12,10},{14,8},{16,22},{18,... | collective-permute-start | bytes 393224 | tf_op jit(solution)/shard_map/ppermute | solution.py:45
  69.8 2.3 %collective-permute-done.21 = bf16[4,64,256]{2,1,0:T(8,128)(2,1)S(1)} collective-permute-done((bf16[4,64,256]{2,1,0:T(8,128)(2,1)S(1)}, bf16[4,64,256]{2,1,0:T(8,128)(2,1)S(1)}, u32[]{:S(2)}, u32[]{:S(2)}) %collective-permute-start.21) | collective-permute-done | bytes 131104 | tf_op jit(solution)/shard_map/ppermute | solution.py:45
  72.1 0.9 collective-permute-done.20
  73.0 2.4 %collective-permute-done.19 = bf16[4,64,256]{2,1,0:T(8,128)(2,1)S(1)} collective-permute-done((bf16[4,64,256]{2,1,0:T(8,128)(2,1)S(1)}, bf16[4,64,256]{2,1,0:T(8,128)(2,1)S(1)}, u32[]{:S(2)}, u32[]{:S(2)}) %collective-permute-start.19) | collective-permute-done | bytes 131104 | tf_op jit(solution)/shard_map/ppermute | solution.py:45
  75.8 1.2 %select_bitcast_fusion.1 = (bf16[1,1,384,256]{3,2,1,0:T(8,128)(2,1)S(1)}, bf16[1,1,384,256]{3,2,1,0:T(8,128)(2,1)S(1)}) fusion(bf16[1,384,256]{2,1,0:T(8,128)(2,1)} %collective-permute-done.15, bf16[1,384,256]{2,1,0:T(8,128)(2,1)} %get-tuple-element.26, pred[]{:T(512)S(6)} %eq.53), kind=kLoop, calls=%fused_computation.77 | loop fusion | flops 196608 | bytes 786433 | tf_op jit(solution)/shard_map/stack | solution.py:128
  77.4 1.5 %fusion.5 = (f32[256]{0:T(256)S(1)}, f32[768,256]{1,0:T(8,128)}) fusion(bf16[1,2,384,256]{3,2,1,0:T(8,128)(2,1)S(1)} %pad_maximum_fusion.5, bf16[768,256]{1,0:T(8,128)(2,1)S(1)} %bitcast.228, f32[768]{0:T(1024)S(1)} %copy-done.18, bf16[768,1024]{1,0:T(8,128)(2,1)S(1)} %bitcast.200, bf16[1024,256]{1,0:T(8,128)(2,1)S(1)} %bitcast.210), kind=kOutput, calls=%fused_computation.19 | convolution fusion | flops 403832576 | bytes 3674112 | tf_op jit(solution)/shard_map/dot_general | solution.py:161
  78.8 1.7 %fusion.3 = (f32[256]{0:T(256)S(1)}, f32[1024,256]{1,0:T(8,128)}) fusion(bf16[4,4,64,256]{3,2,1,0:T(8,128)(2,1)S(1)} %copy.34, bf16[1024,256]{1,0:T(8,128)(2,1)S(1)} %bitcast.211, f32[1024]{0:T(1024)S(1)} %bitcast.232, bf16[1024,768]{0,1:T(8,128)(2,1)S(1)} %bitcast.198, bf16[768,256]{1,0:T(8,128)(2,1)S(1)} %bitcast.229), kind=kOutput, calls=%fused_computation.13 | convolution fusion | flops 404225792 | bytes 4068352 | tf_op jit(solution)/shard_map/dot_general | solution.py:163
  81.1 1.2 %dynamic-slice_convert_fusion.4 = (bf16[2,2,1,1,64,256]{5,4,3,2,1,0:T(8,128)(2,1)S(1)}, bf16[2,2,1,1,64,256]{5,4,3,2,1,0:T(8,128)(2,1)S(1)}, bf16[2,2,1,1,64,256]{5,4,3,2,1,0:T(8,128)(2,1)S(1)}) fusion(f32[2,2,2,2,64,256]{5,4,3,2,1,0:T(8,128)} %bitcast.222, s32[]{:T(128)S(6)} %select_n.385, s32[]{:T(128)S(6)} %select_n.387, s32[]{:T(128)S(6)} %select_n.393, ...), kind=kLoop, calls=%fused_computation.52 | loop fusion | bytes 786456 | tf_op jit(solution)/shard_map/convert_element_type | solution.py:90
  82.3 0.9 collective-permute-start.22
  83.2 1.5 %collective-permute-start.23 = (bf16[280,256]{1,0:T(8,128)(2,1)S(1)}, bf16[280,256]{1,0:T(8,128)(2,1)S(1)}, u32[]{:S(2)}, u32[]{:S(2)}) collective-permute-start(bf16[280,256]{1,0:T(8,128)(2,1)S(1)} %get-tuple-element.77), channel_id=1, source_target_pairs={{0,4},{2,6},{4,0},{6,2},{8,12},{10,14},{12,8},{14,10},{16,20},{18,... | collective-permute-start | bytes 430088 | tf_op jit(solution)/shard_map/ppermute | solution.py:45
  84.7 1.2 %collective-permute-start.24 = (bf16[280,256]{1,0:T(8,128)(2,1)S(1)}, bf16[280,256]{1,0:T(8,128)(2,1)S(1)}, u32[]{:S(2)}, u32[]{:S(2)}) collective-permute-start(bf16[280,256]{1,0:T(8,128)(2,1)S(1)} %get-tuple-element.78), channel_id=1, source_target_pairs={{0,6},{2,4},{4,2},{6,0},{8,14},{10,12},{12,10},{14,8},{16,22},{18,... | collective-permute-start | bytes 430088 | tf_op jit(solution)/shard_map/ppermute | solution.py:45
  85.8 1.7 %fusion.21 = bf16[384,256]{1,0:T(8,128)(2,1)} fusion(f32[2,384,256]{2,1,0:T(8,128)} %bitcast.220, s32[]{:T(128)S(6)} %select_n.413), kind=kLoop, calls=%fused_computation.75 | loop fusion | bytes 393220 | tf_op jit(solution)/shard_map/convert_element_type | solution.py:90
  87.5 1.0 constant_dynamic-slice_fusion
  88.5 0.5 collective-permute-done.22
  89.0 2.3 %collective-permute-done.23 = bf16[280,256]{1,0:T(8,128)(2,1)S(1)} collective-permute-done((bf16[280,256]{1,0:T(8,128)(2,1)S(1)}, bf16[280,256]{1,0:T(8,128)(2,1)S(1)}, u32[]{:S(2)}, u32[]{:S(2)}) %collective-permute-start.23) | collective-permute-done | bytes 143392 | tf_op jit(solution)/shard_map/ppermute | solution.py:45
  91.6 1.6 %collective-permute-start.26 = (bf16[88,256]{1,0:T(8,128)(2,1)S(1)}, bf16[88,256]{1,0:T(8,128)(2,1)S(1)}, u32[]{:S(2)}, u32[]{:S(2)}) collective-permute-start(bf16[88,256]{1,0:T(8,128)(2,1)S(1)} %get-tuple-element.74), channel_id=1, source_target_pairs={{0,16},{2,18},{4,20},{6,22},{8,24},{10,26},{12,28},{14,30},{16,0},... | collective-permute-start | bytes 135176 | tf_op jit(solution)/shard_map/ppermute | solution.py:45
  93.2 2.8 %collective-permute-start.27 = (bf16[88,256]{1,0:T(8,128)(2,1)S(1)}, bf16[88,256]{1,0:T(8,128)(2,1)S(1)}, u32[]{:S(2)}, u32[]{:S(2)}) collective-permute-start(bf16[88,256]{1,0:T(8,128)(2,1)S(1)} %get-tuple-element.75), channel_id=1, source_target_pairs={{0,24},{2,26},{4,28},{6,30},{8,16},{10,18},{12,20},{14,22},{16,8},... | collective-permute-start | bytes 135176 | tf_op jit(solution)/shard_map/ppermute | solution.py:45
  96.1 0.5 collective-permute-done.26
  96.7 2.4 %collective-permute-done.27 = bf16[88,256]{1,0:T(8,128)(2,1)S(1)} collective-permute-done((bf16[88,256]{1,0:T(8,128)(2,1)S(1)}, bf16[88,256]{1,0:T(8,128)(2,1)S(1)}, u32[]{:S(2)}, u32[]{:S(2)}) %collective-permute-start.27) | collective-permute-done | bytes 45088 | tf_op jit(solution)/shard_map/ppermute | solution.py:45
  99.2 1.1 %collective-permute-done.28 = f32[8]{0:T(128)S(1)} collective-permute-done((f32[8]{0:T(128)S(1)}, f32[8]{0:T(128)S(1)}, u32[]{:S(2)}, u32[]{:S(2)}) %collective-permute-start.28) | collective-permute-done | bytes 64 | tf_op jit(solution)/shard_map/ppermute | solution.py:45
  100.7 0.7 fusion.32
  101.4 2.2 %fusion.11 = (f32[1,384,256]{2,1,0:T(8,128)}, f32[1,384,256]{2,1,0:T(8,128)}) fusion(f32[384,256]{1,0:T(8,128)S(1)} %get-tuple-element.27, f32[384,256]{1,0:T(8,128)S(1)} %reshape.294, bf16[384,256]{1,0:T(8,128)(2,1)} %collective-permute-done.29, f32[2,384,256]{2,1,0:T(8,128)} %bitcast.221, s32[]{:T(128)S(6)} %select_n.412, f32[256]{0:T(256)S(1)} %mul.212, ...), kind=kLoop, calls=%fused_computation.32 | loop fusion | flops 1671168 | bytes 3542020 | tf_op jit(solution)/shard_map/broadcast_in_dim | solution.py:224
  (172 shorter events, 8.9 us)
Async XLA Ops:
  0.6 22.0 %copy-start = (f32[64,64]{1,0:T(8,128)S(1)}, f32[64,64]{1,0:T(8,128)}, u32[]{:S(2)}) copy-start(f32[64,64]{1,0:T(8,128)} %param.9) | copy-start | bytes 49156
  1.5 9.0 %collective-permute-start.2 = (bf16[1,64,256]{2,1,0:T(8,128)(2,1)S(1)}, bf16[1,64,256]{2,1,0:T(8,128)(2,1)S(1)}, u32[]{:S(2)}, u32[]{:S(2)}) collective-permute-start(bf16[1,64,256]{2,1,0:T(8,128)(2,1)S(1)} %convert_element_type.273), channel_id=1, source_target_pairs={{0,8},{2,10},{4,12},{6,14},{8,0},{10,2},{12,4},{14,6},{16,24},{18,... | collective-permute-start | bytes 98312 | tf_op jit(solution)/shard_map/ppermute | solution.py:45
  4.5 6.0 %collective-permute-start.1 = (bf16[1,64,256]{2,1,0:T(8,128)(2,1)S(1)}, bf16[1,64,256]{2,1,0:T(8,128)(2,1)S(1)}, u32[]{:S(2)}, u32[]{:S(2)}) collective-permute-start(bf16[1,64,256]{2,1,0:T(8,128)(2,1)S(1)} %convert_element_type.273), channel_id=1, source_target_pairs={{0,16},{2,18},{4,20},{6,22},{8,24},{10,26},{12,28},{14,30},{16,0},... | collective-permute-start | bytes 98312 | tf_op jit(solution)/shard_map/ppermute | solution.py:45
  7.1 5.7 %collective-permute-start = (bf16[1,64,256]{2,1,0:T(8,128)(2,1)S(1)}, bf16[1,64,256]{2,1,0:T(8,128)(2,1)S(1)}, u32[]{:S(2)}, u32[]{:S(2)}) collective-permute-start(bf16[1,64,256]{2,1,0:T(8,128)(2,1)S(1)} %convert_element_type.273), channel_id=1, source_target_pairs={{0,24},{2,26},{4,28},{6,30},{8,16},{10,18},{12,20},{14,22},{16,8},... | collective-permute-start | bytes 98312 | tf_op jit(solution)/shard_map/ppermute | solution.py:45
  8.8 21.8 %collective-permute-start.3 = (bf16[1,384,256]{2,1,0:T(8,128)(2,1)}, bf16[1,384,256]{2,1,0:T(8,128)(2,1)S(1)}, u32[]{:S(2)}, u32[]{:S(2)}) collective-permute-start(bf16[1,384,256]{2,1,0:T(8,128)(2,1)} %convert_element_type.275), channel_id=1, source_target_pairs={{0,1},{1,0},{2,3},{3,2},{4,5},{5,4},{6,7},{7,6},{8,9},{9,8},{10,11... | collective-permute-start | bytes 589832 | tf_op jit(solution)/shard_map/ppermute | solution.py:45
  13.7 6.0 %copy-start.2 = (s32[1,1,12,256,256]{4,3,2,1,0:T(8,128)S(1)}, s32[1,1,12,256,256]{4,3,2,1,0:T(8,128)}, u32[]{:S(2)}) copy-start(s32[1,1,12,256,256]{4,3,2,1,0:T(8,128)} %param.11) | copy-start | bytes 9437188
  13.7 14.9 %collective-permute-start.6 = (bf16[4,64,256]{2,1,0:T(8,128)(2,1)S(1)}, bf16[4,64,256]{2,1,0:T(8,128)(2,1)S(1)}, u32[]{:S(2)}, u32[]{:S(2)}) collective-permute-start(bf16[4,64,256]{2,1,0:T(8,128)(2,1)S(1)} %maximum_bitcast_fusion), channel_id=1, source_target_pairs={{0,2},{2,0},{4,6},{6,4},{8,10},{10,8},{12,14},{14,12},{16,18},{18,... | collective-permute-start | bytes 393224 | tf_op jit(solution)/shard_map/ppermute | solution.py:45
  15.3 13.4 %collective-permute-start.5 = (bf16[4,64,256]{2,1,0:T(8,128)(2,1)S(1)}, bf16[4,64,256]{2,1,0:T(8,128)(2,1)S(1)}, u32[]{:S(2)}, u32[]{:S(2)}) collective-permute-start(bf16[4,64,256]{2,1,0:T(8,128)(2,1)S(1)} %maximum_bitcast_fusion), channel_id=1, source_target_pairs={{0,4},{2,6},{4,0},{6,2},{8,12},{10,14},{12,8},{14,10},{16,20},{18,... | collective-permute-start | bytes 393224 | tf_op jit(solution)/shard_map/ppermute | solution.py:45
  16.8 12.6 %collective-permute-start.4 = (bf16[4,64,256]{2,1,0:T(8,128)(2,1)S(1)}, bf16[4,64,256]{2,1,0:T(8,128)(2,1)}, u32[]{:S(2)}, u32[]{:S(2)}) collective-permute-start(bf16[4,64,256]{2,1,0:T(8,128)(2,1)S(1)} %maximum_bitcast_fusion), channel_id=1, source_target_pairs={{0,6},{2,4},{4,2},{6,0},{8,14},{10,12},{12,10},{14,8},{16,22},{18,... | collective-permute-start | bytes 393224 | tf_op jit(solution)/shard_map/ppermute | solution.py:45
  19.8 1.7 %copy-start.3 = (f32[1,64,256]{2,1,0:T(8,128)S(1)}, f32[1,64,256]{2,1,0:T(8,128)}, u32[]{:S(2)}) copy-start(f32[1,64,256]{2,1,0:T(8,128)} %param.8) | copy-start | bytes 196612
  19.8 1.8 %copy-start.15 = (f32[64,64]{1,0:T(8,128)S(1)}, f32[64,64]{1,0:T(8,128)}, u32[]{:S(2)}) copy-start(f32[64,64]{1,0:T(8,128)} %param.10) | copy-start | bytes 49156
  19.8 2.6 %copy-start.1 = (f32[1,384,256]{2,1,0:T(8,128)S(1)}, f32[1,384,256]{2,1,0:T(8,128)}, u32[]{:S(2)}) copy-start(f32[1,384,256]{2,1,0:T(8,128)} %param.7) | copy-start | bytes 1179652
  21.5 11.2 %copy-start.17 = (f32[768]{0:T(1024)}, f32[768]{0:T(1024)S(1)}, u32[]{:S(2)}) copy-start(f32[768]{0:T(1024)S(1)} %mul.186) | copy-start | bytes 9220
  27.7 3.0 %copy-start.4 = (bf16[96,8,4,256]{3,1,2,0:T(8,128)(2,1)}, bf16[96,8,4,256]{3,1,2,0:T(8,128)(2,1)S(1)}, u32[]{:S(2)}) copy-start(bf16[96,8,4,256]{3,1,2,0:T(8,128)(2,1)S(1)} %copy.44) | copy-start | bytes 4718596
  28.6 4.0 %copy-start.6 = (bf16[96,8,4,256]{3,1,2,0:T(8,128)(2,1)}, bf16[96,8,4,256]{3,1,2,0:T(8,128)(2,1)S(1)}, u32[]{:S(2)}) copy-start(bf16[96,8,4,256]{3,1,2,0:T(8,128)(2,1)S(1)} %copy.46) | copy-start | bytes 4718596
  28.7 0.7 copy-start.14
  30.6 1.9 %copy-start.12 = (bf16[4,4,64,256]{3,2,1,0:T(8,128)(2,1)}, bf16[4,4,64,256]{3,2,1,0:T(8,128)(2,1)S(1)}, u32[]{:S(2)}) copy-start(bf16[4,4,64,256]{3,2,1,0:T(8,128)(2,1)S(1)} %copy.30) | copy-start | bytes 1572868
  30.7 1.8 %copy-start.13 = (bf16[1,2,384,256]{3,2,1,0:T(8,128)(2,1)}, bf16[1,2,384,256]{3,2,1,0:T(8,128)(2,1)S(1)}, u32[]{:S(2)}) copy-start(bf16[1,2,384,256]{3,2,1,0:T(8,128)(2,1)S(1)} %pad_maximum_fusion.4) | copy-start | bytes 1179652
  34.6 28.2 %copy-start.8 = (f32[768,256]{1,0:T(8,128)}, f32[768,256]{1,0:T(8,128)S(1)}, u32[]{:S(2)}) copy-start(f32[768,256]{1,0:T(8,128)S(1)} %get-tuple-element.98) | copy-start | bytes 2359300
  36.1 5.7 %collective-permute-start.7 = (bf16[280,256]{1,0:T(8,128)(2,1)S(1)}, bf16[280,256]{1,0:T(8,128)(2,1)S(1)}, u32[]{:S(2)}, u32[]{:S(2)}) collective-permute-start(bf16[280,256]{1,0:T(8,128)(2,1)S(1)} %get-tuple-element.82), channel_id=1, source_target_pairs={{0,2},{2,0},{4,6},{6,4},{8,10},{10,8},{12,14},{14,12},{16,18},{18,... | collective-permute-start | bytes 430088 | tf_op jit(solution)/shard_map/ppermute | solution.py:45
  37.7 5.4 %collective-permute-start.8 = (bf16[280,256]{1,0:T(8,128)(2,1)S(1)}, bf16[280,256]{1,0:T(8,128)(2,1)S(1)}, u32[]{:S(2)}, u32[]{:S(2)}) collective-permute-start(bf16[280,256]{1,0:T(8,128)(2,1)S(1)} %get-tuple-element.83), channel_id=1, source_target_pairs={{0,4},{2,6},{4,0},{6,2},{8,12},{10,14},{12,8},{14,10},{16,20},{18,... | collective-permute-start | bytes 430088 | tf_op jit(solution)/shard_map/ppermute | solution.py:45
  39.2 6.0 %collective-permute-start.9 = (bf16[280,256]{1,0:T(8,128)(2,1)S(1)}, bf16[280,256]{1,0:T(8,128)(2,1)S(1)}, u32[]{:S(2)}, u32[]{:S(2)}) collective-permute-start(bf16[280,256]{1,0:T(8,128)(2,1)S(1)} %get-tuple-element.84), channel_id=1, source_target_pairs={{0,6},{2,4},{4,2},{6,0},{8,14},{10,12},{12,10},{14,8},{16,22},{18,... | collective-permute-start | bytes 430088 | tf_op jit(solution)/shard_map/ppermute | solution.py:45
  39.7 23.1 %collective-permute-start.14 = (bf16[384,256]{1,0:T(8,128)(2,1)S(1)}, bf16[384,256]{1,0:T(8,128)(2,1)S(1)}, u32[]{:S(2)}, u32[]{:S(2)}) collective-permute-start(bf16[384,256]{1,0:T(8,128)(2,1)S(1)} %fusion.20), channel_id=1, source_target_pairs={{0,1},{1,0},{2,3},{3,2},{4,5},{5,4},{6,7},{7,6},{8,9},{9,8},{10,11... | collective-permute-start | bytes 589832 | tf_op jit(solution)/shard_map/ppermute | solution.py:45
  40.8 20.3 %copy-start.16 = (f32[64,64]{1,0:T(8,128)S(1)}, f32[64,64]{1,0:T(8,128)}, u32[]{:S(2)}) copy-start(f32[64,64]{1,0:T(8,128)} %param.10) | copy-start | bytes 49156
  45.4 4.5 %collective-permute-start.10 = (bf16[88,256]{1,0:T(8,128)(2,1)S(1)}, bf16[88,256]{1,0:T(8,128)(2,1)S(1)}, u32[]{:S(2)}, u32[]{:S(2)}) collective-permute-start(bf16[88,256]{1,0:T(8,128)(2,1)S(1)} %get-tuple-element.79), channel_id=1, source_target_pairs={{0,8},{2,10},{4,12},{6,14},{8,0},{10,2},{12,4},{14,6},{16,24},{18,... | collective-permute-start | bytes 135176 | tf_op jit(solution)/shard_map/ppermute | solution.py:45
  45.5 5.0 %collective-permute-start.11 = (bf16[88,256]{1,0:T(8,128)(2,1)S(1)}, bf16[88,256]{1,0:T(8,128)(2,1)S(1)}, u32[]{:S(2)}, u32[]{:S(2)}) collective-permute-start(bf16[88,256]{1,0:T(8,128)(2,1)S(1)} %get-tuple-element.80), channel_id=1, source_target_pairs={{0,16},{2,18},{4,20},{6,22},{8,24},{10,26},{12,28},{14,30},{16,0},... | collective-permute-start | bytes 135176 | tf_op jit(solution)/shard_map/ppermute | solution.py:45
  48.2 5.8 %collective-permute-start.12 = (bf16[88,256]{1,0:T(8,128)(2,1)S(1)}, bf16[88,256]{1,0:T(8,128)(2,1)S(1)}, u32[]{:S(2)}, u32[]{:S(2)}) collective-permute-start(bf16[88,256]{1,0:T(8,128)(2,1)S(1)} %get-tuple-element.81), channel_id=1, source_target_pairs={{0,24},{2,26},{4,28},{6,30},{8,16},{10,18},{12,20},{14,22},{16,8},... | collective-permute-start | bytes 135176 | tf_op jit(solution)/shard_map/ppermute | solution.py:45
  54.1 1.2 %collective-permute-start.13 = (f32[8]{0:T(128)S(1)}, f32[8]{0:T(128)S(1)}, u32[]{:S(2)}, u32[]{:S(2)}) collective-permute-start(f32[8]{0:T(128)S(1)} %fusion.51), channel_id=1, source_target_pairs={{0,1},{1,0},{2,3},{3,2},{4,5},{5,4},{6,7},{7,6},{8,9},{9,8},{10,11... | collective-permute-start | bytes 104 | tf_op jit(solution)/shard_map/ppermute | solution.py:45
  55.3 0.5 copy-start.19
  56.6 8.2 %collective-permute-start.18 = (bf16[1,64,256]{2,1,0:T(8,128)(2,1)}, bf16[1,64,256]{2,1,0:T(8,128)(2,1)}, u32[]{:S(2)}, u32[]{:S(2)}) collective-permute-start(bf16[1,64,256]{2,1,0:T(8,128)(2,1)} %get-tuple-element.28), channel_id=1, source_target_pairs={{0,8},{2,10},{4,12},{6,14},{8,0},{10,2},{12,4},{14,6},{16,24},{18,... | collective-permute-start | bytes 98312 | tf_op jit(solution)/shard_map/ppermute | solution.py:45
  56.6 8.3 %collective-permute-start.17 = (bf16[1,64,256]{2,1,0:T(8,128)(2,1)}, bf16[1,64,256]{2,1,0:T(8,128)(2,1)}, u32[]{:S(2)}, u32[]{:S(2)}) collective-permute-start(bf16[1,64,256]{2,1,0:T(8,128)(2,1)} %get-tuple-element.28), channel_id=1, source_target_pairs={{0,16},{2,18},{4,20},{6,22},{8,24},{10,26},{12,28},{14,30},{16,0},... | collective-permute-start | bytes 98312 | tf_op jit(solution)/shard_map/ppermute | solution.py:45
  58.8 6.1 %collective-permute-start.16 = (bf16[1,64,256]{2,1,0:T(8,128)(2,1)}, bf16[1,64,256]{2,1,0:T(8,128)(2,1)}, u32[]{:S(2)}, u32[]{:S(2)}) collective-permute-start(bf16[1,64,256]{2,1,0:T(8,128)(2,1)} %get-tuple-element.28), channel_id=1, source_target_pairs={{0,24},{2,26},{4,28},{6,30},{8,16},{10,18},{12,20},{14,22},{16,8},... | collective-permute-start | bytes 98312 | tf_op jit(solution)/shard_map/ppermute | solution.py:45
  62.8 0.9 copy-start.10
  63.6 12.2 %collective-permute-start.15 = (bf16[1,384,256]{2,1,0:T(8,128)(2,1)}, bf16[1,384,256]{2,1,0:T(8,128)(2,1)}, u32[]{:S(2)}, u32[]{:S(2)}) collective-permute-start(bf16[1,384,256]{2,1,0:T(8,128)(2,1)} %get-tuple-element.26), channel_id=1, source_target_pairs={{0,1},{1,0},{2,3},{3,2},{4,5},{5,4},{6,7},{7,6},{8,9},{9,8},{10,11... | collective-permute-start | bytes 589832 | tf_op jit(solution)/shard_map/ppermute | solution.py:45
  64.6 5.2 %copy-start.22 = (f32[4]{0:T(128)S(1)}, f32[4]{0:T(128)}, u32[]{:S(2)}) copy-start(f32[4]{0:T(128)} %reduce_sum.255) | copy-start | bytes 52
  65.7 6.4 %collective-permute-start.21 = (bf16[4,64,256]{2,1,0:T(8,128)(2,1)S(1)}, bf16[4,64,256]{2,1,0:T(8,128)(2,1)S(1)}, u32[]{:S(2)}, u32[]{:S(2)}) collective-permute-start(bf16[4,64,256]{2,1,0:T(8,128)(2,1)S(1)} %maximum_bitcast_fusion.1), channel_id=1, source_target_pairs={{0,2},{2,0},{4,6},{6,4},{8,10},{10,8},{12,14},{14,12},{16,18},{18,... | collective-permute-start | bytes 393224 | tf_op jit(solution)/shard_map/ppermute | solution.py:45
  66.9 6.0 %collective-permute-start.20 = (bf16[4,64,256]{2,1,0:T(8,128)(2,1)S(1)}, bf16[4,64,256]{2,1,0:T(8,128)(2,1)S(1)}, u32[]{:S(2)}, u32[]{:S(2)}) collective-permute-start(bf16[4,64,256]{2,1,0:T(8,128)(2,1)S(1)} %maximum_bitcast_fusion.1), channel_id=1, source_target_pairs={{0,4},{2,6},{4,0},{6,2},{8,12},{10,14},{12,8},{14,10},{16,20},{18,... | collective-permute-start | bytes 393224 | tf_op jit(solution)/shard_map/ppermute | solution.py:45
  67.8 7.6 %collective-permute-start.19 = (bf16[4,64,256]{2,1,0:T(8,128)(2,1)S(1)}, bf16[4,64,256]{2,1,0:T(8,128)(2,1)S(1)}, u32[]{:S(2)}, u32[]{:S(2)}) collective-permute-start(bf16[4,64,256]{2,1,0:T(8,128)(2,1)S(1)} %maximum_bitcast_fusion.1), channel_id=1, source_target_pairs={{0,6},{2,4},{4,2},{6,0},{8,14},{10,12},{12,10},{14,8},{16,22},{18,... | collective-permute-start | bytes 393224 | tf_op jit(solution)/shard_map/ppermute | solution.py:45
  75.7 1.6 %copy-start.7 = (bf16[96,8,4,256]{3,1,2,0:T(8,128)(2,1)S(1)}, bf16[96,8,4,256]{3,1,2,0:T(8,128)(2,1)}, u32[]{:S(2)}) copy-start(bf16[96,8,4,256]{3,1,2,0:T(8,128)(2,1)} %copy-done.6) | copy-start | bytes 4718596
  75.8 1.6 %copy-start.18 = (f32[768]{0:T(1024)S(1)}, f32[768]{0:T(1024)}, u32[]{:S(2)}) copy-start(f32[768]{0:T(1024)} %copy-done.17) | copy-start | bytes 9220
  77.3 1.5 %copy-start.5 = (bf16[96,8,4,256]{3,1,2,0:T(8,128)(2,1)S(1)}, bf16[96,8,4,256]{3,1,2,0:T(8,128)(2,1)}, u32[]{:S(2)}) copy-start(bf16[96,8,4,256]{3,1,2,0:T(8,128)(2,1)} %copy-done.4) | copy-start | bytes 4718596
  78.8 2.1 %copy-start.21 = (f32[4]{0:T(128)S(1)}, f32[4]{0:T(128)}, u32[]{:S(2)}) copy-start(f32[4]{0:T(128)} %reduce_sum.261) | copy-start | bytes 52
  82.3 6.7 %collective-permute-start.22 = (bf16[280,256]{1,0:T(8,128)(2,1)S(1)}, bf16[280,256]{1,0:T(8,128)(2,1)S(1)}, u32[]{:S(2)}, u32[]{:S(2)}) collective-permute-start(bf16[280,256]{1,0:T(8,128)(2,1)S(1)} %get-tuple-element.76), channel_id=1, source_target_pairs={{0,2},{2,0},{4,6},{6,4},{8,10},{10,8},{12,14},{14,12},{16,18},{18,... | collective-permute-start | bytes 430088 | tf_op jit(solution)/shard_map/ppermute | solution.py:45
  83.2 8.2 %collective-permute-start.23 = (bf16[280,256]{1,0:T(8,128)(2,1)S(1)}, bf16[280,256]{1,0:T(8,128)(2,1)S(1)}, u32[]{:S(2)}, u32[]{:S(2)}) collective-permute-start(bf16[280,256]{1,0:T(8,128)(2,1)S(1)} %get-tuple-element.77), channel_id=1, source_target_pairs={{0,4},{2,6},{4,0},{6,2},{8,12},{10,14},{12,8},{14,10},{16,20},{18,... | collective-permute-start | bytes 430088 | tf_op jit(solution)/shard_map/ppermute | solution.py:45
  84.7 6.7 %collective-permute-start.24 = (bf16[280,256]{1,0:T(8,128)(2,1)S(1)}, bf16[280,256]{1,0:T(8,128)(2,1)S(1)}, u32[]{:S(2)}, u32[]{:S(2)}) collective-permute-start(bf16[280,256]{1,0:T(8,128)(2,1)S(1)} %get-tuple-element.78), channel_id=1, source_target_pairs={{0,6},{2,4},{4,2},{6,0},{8,14},{10,12},{12,10},{14,8},{16,22},{18,... | collective-permute-start | bytes 430088 | tf_op jit(solution)/shard_map/ppermute | solution.py:45
  87.5 12.8 %copy-start.20 = (f32[8]{0:T(128)S(1)}, f32[8]{0:T(128)}, u32[]{:S(2)}) copy-start(f32[8]{0:T(128)} %copy-done.19) | copy-start | bytes 100
  87.5 13.9 %collective-permute-start.29 = (bf16[384,256]{1,0:T(8,128)(2,1)}, bf16[384,256]{1,0:T(8,128)(2,1)}, u32[]{:S(2)}, u32[]{:S(2)}) collective-permute-start(bf16[384,256]{1,0:T(8,128)(2,1)} %fusion.21), channel_id=1, source_target_pairs={{0,1},{1,0},{2,3},{3,2},{4,5},{5,4},{6,7},{7,6},{8,9},{9,8},{10,11... | collective-permute-start | bytes 589832 | tf_op jit(solution)/shard_map/ppermute | solution.py:45
  88.5 12.9 %copy-start.9 = (f32[768,256]{1,0:T(8,128)S(1)}, f32[768,256]{1,0:T(8,128)}, u32[]{:S(2)}) copy-start(f32[768,256]{1,0:T(8,128)} %copy-done.8) | copy-start | bytes 2359300
  88.5 12.9 %copy-start.11 = (bf16[384,256]{1,0:T(8,128)(2,1)S(1)}, bf16[384,256]{1,0:T(8,128)(2,1)}, u32[]{:S(2)}) copy-start(bf16[384,256]{1,0:T(8,128)(2,1)} %copy-done.10) | copy-start | bytes 589828
  91.6 4.6 %collective-permute-start.25 = (bf16[88,256]{1,0:T(8,128)(2,1)S(1)}, bf16[88,256]{1,0:T(8,128)(2,1)S(1)}, u32[]{:S(2)}, u32[]{:S(2)}) collective-permute-start(bf16[88,256]{1,0:T(8,128)(2,1)S(1)} %get-tuple-element.73), channel_id=1, source_target_pairs={{0,8},{2,10},{4,12},{6,14},{8,0},{10,2},{12,4},{14,6},{16,24},{18,... | collective-permute-start | bytes 135176 | tf_op jit(solution)/shard_map/ppermute | solution.py:45
  91.6 5.0 %collective-permute-start.26 = (bf16[88,256]{1,0:T(8,128)(2,1)S(1)}, bf16[88,256]{1,0:T(8,128)(2,1)S(1)}, u32[]{:S(2)}, u32[]{:S(2)}) collective-permute-start(bf16[88,256]{1,0:T(8,128)(2,1)S(1)} %get-tuple-element.74), channel_id=1, source_target_pairs={{0,16},{2,18},{4,20},{6,22},{8,24},{10,26},{12,28},{14,30},{16,0},... | collective-permute-start | bytes 135176 | tf_op jit(solution)/shard_map/ppermute | solution.py:45
  93.2 5.8 %collective-permute-start.27 = (bf16[88,256]{1,0:T(8,128)(2,1)S(1)}, bf16[88,256]{1,0:T(8,128)(2,1)S(1)}, u32[]{:S(2)}, u32[]{:S(2)}) collective-permute-start(bf16[88,256]{1,0:T(8,128)(2,1)S(1)} %get-tuple-element.75), channel_id=1, source_target_pairs={{0,24},{2,26},{4,28},{6,30},{8,16},{10,18},{12,20},{14,22},{16,8},... | collective-permute-start | bytes 135176 | tf_op jit(solution)/shard_map/ppermute | solution.py:45
  99.1 1.2 %collective-permute-start.28 = (f32[8]{0:T(128)S(1)}, f32[8]{0:T(128)S(1)}, u32[]{:S(2)}, u32[]{:S(2)}) collective-permute-start(f32[8]{0:T(128)S(1)} %fusion.50), channel_id=1, source_target_pairs={{0,1},{1,0},{2,3},{3,2},{4,5},{5,4},{6,7},{7,6},{8,9},{9,8},{10,11... | collective-permute-start | bytes 104 | tf_op jit(solution)/shard_map/ppermute | solution.py:45

commit v18 on v17

--- a/solution.py
+++ b/solution.py
@@ -189,7 +189,7 @@
             + noise_prec * cross_dot
         )
         sums = jnp.concatenate([norm_part, curve_part]).reshape(1, 2 * DRAWS)
-        sums = jnp.pad(sums, ((0, 7), (0, width - 2 * DRAWS)))
+        sums = jnp.pad(sums, ((0, 0), (0, width - 2 * DRAWS)))
         total_user, _ = halve_sum(part_user, "item", jnp.bfloat16)
         total_item, sums = halve_sum(part_item, "user", jnp.float32, sums, jnp.bfloat16)
         sums = sums[0, : 2 * DRAWS]

time: 104 us -> 104 us (level)
  no operation moved by 1% of the time
where the time goes in v18:
time: 104 us; the launch traced here: 103 us
  starting transfers between devices  33.3 us (32%)
  waiting for transfers between devices  24.4 us (23%)
  other arithmetic  18.5 us (18%)
  local copies, waits for them, and re-layouts  13.2 us (13%)
  matrix products  11.6 us (11%)
  between operations  2.1 us (2%)
    ppermute x30, starting transfers between devices, swap_with(): return lax.ppermute(value, axis, pairs)  33.3 us
    ppermute x30, waiting for transfers between devices, swap_with(): return lax.ppermute(value, axis, pairs)  24.4 us
    another operation x11, other arithmetic, double_gather(): buf = jnp.stack(ordered, axis=1).reshape((-1,) + piece.shape)  4.4 us
    convert_element_type x6, local copies, waits for them, and re-layouts, halve_sum(): send = block_of(digit ^ k).astype(stage_type)  4.1 us
    dot_general x2, matrix products, cross_parts(): to_items = jnp.dot(counts_t, user_range, preferred_element_type=jnp.float32)  3.49 us
    dot_general x2, matrix products, cross_parts(): jnp.dot(counts_bf, item_range, preferred_element_type=jnp.float32)  3.36 us
    broadcast_in_dim x2, other arithmetic, per_device(): return (sol_user[None], sol_item[None], res_user[None], res_item[None])  2.93 us
    dot_general x1, matrix products, build_counts(): jnp.einsum('trc,tij->cjri', place, tiles_bf, preferred_element_type=jnp.b...  2.71 us
  transfers between devices with their start and end apart: 30, of which 16 were waited for; matrix products, arithmetic and copies ran while one was open for 26% of the time, Pallas kernels for 0%

profile of v18, /device:TPU:0, one launch (start us, length us, event | category | flops | bytes accessed | tf_op | source)
XLA Modules:
  0.0 103.1 jit_solution(6139852503093559097)
XLA Ops:
  0.6 0.9 convert_element_type.273
  1.5 3.0 %collective-permute-start.2 = (bf16[1,64,256]{2,1,0:T(8,128)(2,1)S(1)}, bf16[1,64,256]{2,1,0:T(8,128)(2,1)S(1)}, u32[]{:S(2)}, u32[]{:S(2)}) collective-permute-start(bf16[1,64,256]{2,1,0:T(8,128)(2,1)S(1)} %convert_element_type.273), channel_id=1, source_target_pairs={{0,8},{2,10},{4,12},{6,14},{8,0},{10,2},{12,4},{14,6},{16,24},{18,... | collective-permute-start | bytes 98312 | tf_op jit(solution)/shard_map/ppermute | solution.py:45
  4.5 2.6 %collective-permute-start.1 = (bf16[1,64,256]{2,1,0:T(8,128)(2,1)S(1)}, bf16[1,64,256]{2,1,0:T(8,128)(2,1)S(1)}, u32[]{:S(2)}, u32[]{:S(2)}) collective-permute-start(bf16[1,64,256]{2,1,0:T(8,128)(2,1)S(1)} %convert_element_type.273), channel_id=1, source_target_pairs={{0,16},{2,18},{4,20},{6,22},{8,24},{10,26},{12,28},{14,30},{16,0},... | collective-permute-start | bytes 98312 | tf_op jit(solution)/shard_map/ppermute | solution.py:45
  7.1 1.7 %convert_element_type.275 = bf16[1,384,256]{2,1,0:T(8,128)(2,1)} convert(f32[1,384,256]{2,1,0:T(8,128)} %param.7) | non-fusion elementwise | flops 98304 | bytes 589824 | tf_op jit(solution)/shard_map/convert_element_type | solution.py:168
  9.5 0.8 slice_bitcast_fusion.1
  10.5 2.3 %collective-permute-done = bf16[1,64,256]{2,1,0:T(8,128)(2,1)S(1)} collective-permute-done((bf16[1,64,256]{2,1,0:T(8,128)(2,1)S(1)}, bf16[1,64,256]{2,1,0:T(8,128)(2,1)S(1)}, u32[]{:S(2)}, u32[]{:S(2)}) %collective-permute-start) | collective-permute-done | bytes 32800 | tf_op jit(solution)/shard_map/ppermute | solution.py:45
  12.8 0.9 select_bitcast_fusion.19
  13.7 1.6 %collective-permute-start.6 = (bf16[4,64,256]{2,1,0:T(8,128)(2,1)S(1)}, bf16[4,64,256]{2,1,0:T(8,128)(2,1)S(1)}, u32[]{:S(2)}, u32[]{:S(2)}) collective-permute-start(bf16[4,64,256]{2,1,0:T(8,128)(2,1)S(1)} %maximum_bitcast_fusion), channel_id=1, source_target_pairs={{0,2},{2,0},{4,6},{6,4},{8,10},{10,8},{12,14},{14,12},{16,18},{18,... | collective-permute-start | bytes 393224 | tf_op jit(solution)/shard_map/ppermute | solution.py:45
  15.3 1.5 %collective-permute-start.5 = (bf16[4,64,256]{2,1,0:T(8,128)(2,1)S(1)}, bf16[4,64,256]{2,1,0:T(8,128)(2,1)S(1)}, u32[]{:S(2)}, u32[]{:S(2)}) collective-permute-start(bf16[4,64,256]{2,1,0:T(8,128)(2,1)S(1)} %maximum_bitcast_fusion), channel_id=1, source_target_pairs={{0,4},{2,6},{4,0},{6,2},{8,12},{10,14},{12,8},{14,10},{16,20},{18,... | collective-permute-start | bytes 393224 | tf_op jit(solution)/shard_map/ppermute | solution.py:45
  16.8 0.5 collective-permute-start.4
  17.3 2.5 %convert_reduce_fusion.1 = (f32[12,256]{1,0:T(8,128)S(1)}, f32[12,256]{1,0:T(8,128)S(1)}) fusion(s32[12,256,256]{2,1,0:T(8,128)} %bitcast.191), kind=kLoop, calls=%fused_computation.1 | loop fusion | flops 3139584 | bytes 3170304 | tf_op jit(solution)/shard_map/reduce_sum | solution.py:154
  19.8 1.5 %convert_bitcast_fusion.2 = bf16[12,256,256,1]{2,1,0,3:T(8,128)(2,1)} fusion(s32[12,256,256]{2,1,0:T(8,128)S(1)} %bitcast.192), kind=kLoop, calls=%fused_computation.198 | loop fusion | flops 786432 | bytes 4718592 | tf_op jit(solution)/shard_map/convert_element_type | solution.py:146
  22.3 0.6 reduce_sum.195
  23.1 0.8 fusion.56
  24.1 2.7 %fusion = bf16[256,256,3,4]{1,3,2,0:T(4,128)(2,1)S(1)} fusion(bf16[12,256,256,1]{2,1,0,3:T(8,128)(2,1)} %convert_bitcast_fusion.2, pred[12,4]{0,1:T(4,128)(4,1)S(1)} %copy.27, pred[12,3]{0,1:T(4,128)(4,1)S(1)} %fusion.45), kind=kOutput, calls=%fused_computation.2 | convolution fusion | flops 18874512 | bytes 3145812 | tf_op jit(solution)/shard_map/trc,tij->cjri/dot_general | solution.py:150
  27.3 0.5 copy.29
  28.3 0.5 copy.33
  29.2 0.7 copy-done.14
  29.9 1.0 %select_bitcast_fusion.11 = (bf16[4,1,64,256]{3,2,0,1:T(8,128)(2,1)S(1)}, bf16[4,1,64,256]{3,2,0,1:T(8,128)(2,1)S(1)}, bf16[4,1,64,256]{3,2,0,1:T(8,128)(2,1)S(1)}, bf16[4,1,64,256]{3,2,0,1:T(8,128)(2,1)S(1)}) fusion(bf16[4,64,256]{2,1,0:T(8,128)(2,1)} %collective-permute-done.4, bf16[4,64,256]{2,1,0:T(8,128)(2,1)} %copy-done.14, ...), kind=kLoop, calls=%fused_computation.90 | loop fusion | flops 786432 | bytes 1048579 | tf_op jit(solution)/shard_map/stack | solution.py:128
  31.2 1.8 %fusion.2 = (f32[256]{0:T(256)S(1)}, f32[1024,256]{1,0:T(8,128)}) fusion(bf16[4,4,64,256]{3,2,1,0:T(8,128)(2,1)S(1)} %copy.30, bf16[1024,256]{1,0:T(8,128)(2,1)S(1)} %bitcast.212, f32[1024]{0:T(1024)S(1)} %bitcast.231, bf16[1024,768]{0,1:T(8,128)(2,1)S(1)} %bitcast.197, bf16[768,256]{1,0:T(8,128)(2,1)S(1)} %bitcast.226), kind=kOutput, calls=%fused_computation.12 | convolution fusion | flops 404225792 | bytes 4068352 | tf_op jit(solution)/shard_map/dot_general | solution.py:163
  33.2 1.9 %fusion.4 = (f32[256]{0:T(256)S(1)}, f32[768,256]{1,0:T(8,128)S(1)}) fusion(bf16[1,2,384,256]{3,2,1,0:T(8,128)(2,1)} %copy-done.13, bf16[768,256]{1,0:T(8,128)(2,1)} %bitcast.227, f32[768]{0:T(1024)S(1)} %mul.186, bf16[768,1024]{1,0:T(8,128)(2,1)S(1)} %bitcast.199, bf16[1024,256]{1,0:T(8,128)(2,1)} %bitcast.213), kind=kOutput, calls=%fused_computation.18 | convolution fusion | flops 403832576 | bytes 3674112 | tf_op jit(solution)/shard_map/dot_general | solution.py:161
  35.5 1.2 %dynamic-slice_convert_fusion.7 = (bf16[2,2,1,1,64,256]{5,4,3,2,1,0:T(8,128)(2,1)S(1)}, bf16[2,2,1,1,64,256]{5,4,3,2,1,0:T(8,128)(2,1)S(1)}, bf16[2,2,1,1,64,256]{5,4,3,2,1,0:T(8,128)(2,1)S(1)}) fusion(f32[2,2,2,2,64,256]{5,4,3,2,1,0:T(8,128)} %bitcast.224, s32[]{:T(128)S(6)} %select_n.385, s32[]{:T(128)S(6)} %select_n.387, s32[]{:T(128)S(6)} %select_n.393, ...), kind=kLoop, calls=%fused_computation.55 | loop fusion | bytes 786456 | tf_op jit(solution)/shard_map/convert_element_type | solution.py:90
  36.7 1.6 %collective-permute-start.7 = (bf16[259,256]{1,0:T(8,128)(2,1)S(1)}, bf16[259,256]{1,0:T(8,128)(2,1)S(1)}, u32[]{:S(2)}, u32[]{:S(2)}) collective-permute-start(bf16[259,256]{1,0:T(8,128)(2,1)S(1)} %get-tuple-element.82), channel_id=1, source_target_pairs={{0,2},{2,0},{4,6},{6,4},{8,10},{10,8},{12,14},{14,12},{16,18},{18,... | collective-permute-start | bytes 397832 | tf_op jit(solution)/shard_map/ppermute | solution.py:45
  38.2 1.5 %collective-permute-start.8 = (bf16[259,256]{1,0:T(8,128)(2,1)S(1)}, bf16[259,256]{1,0:T(8,128)(2,1)S(1)}, u32[]{:S(2)}, u32[]{:S(2)}) collective-permute-start(bf16[259,256]{1,0:T(8,128)(2,1)S(1)} %get-tuple-element.83), channel_id=1, source_target_pairs={{0,4},{2,6},{4,0},{6,2},{8,12},{10,14},{12,8},{14,10},{16,20},{18,... | collective-permute-start | bytes 397832 | tf_op jit(solution)/shard_map/ppermute | solution.py:45
  39.7 0.5 collective-permute-start.9
  40.3 1.0 constant_dynamic-slice_fusion.1
  41.3 0.9 collective-permute-done.7
  42.2 1.2 %collective-permute-done.8 = bf16[259,256]{1,0:T(8,128)(2,1)S(1)} collective-permute-done((bf16[259,256]{1,0:T(8,128)(2,1)S(1)}, bf16[259,256]{1,0:T(8,128)(2,1)S(1)}, u32[]{:S(2)}, u32[]{:S(2)}) %collective-permute-start.8) | collective-permute-done | bytes 132640 | tf_op jit(solution)/shard_map/ppermute | solution.py:45
  43.4 2.2 %collective-permute-done.9 = bf16[259,256]{1,0:T(8,128)(2,1)S(1)} collective-permute-done((bf16[259,256]{1,0:T(8,128)(2,1)S(1)}, bf16[259,256]{1,0:T(8,128)(2,1)S(1)}, u32[]{:S(2)}, u32[]{:S(2)}) %collective-permute-start.9) | collective-permute-done | bytes 132640 | tf_op jit(solution)/shard_map/ppermute | solution.py:45
  45.9 2.5 %collective-permute-start.11 = (bf16[67,256]{1,0:T(8,128)(2,1)S(1)}, bf16[67,256]{1,0:T(8,128)(2,1)S(1)}, u32[]{:S(2)}, u32[]{:S(2)}) collective-permute-start(bf16[67,256]{1,0:T(8,128)(2,1)S(1)} %get-tuple-element.80), channel_id=1, source_target_pairs={{0,16},{2,18},{4,20},{6,22},{8,24},{10,26},{12,28},{14,30},{16,0},... | collective-permute-start | bytes 102920 | tf_op jit(solution)/shard_map/ppermute | solution.py:45
  48.5 1.8 %collective-permute-start.12 = (bf16[67,256]{1,0:T(8,128)(2,1)S(1)}, bf16[67,256]{1,0:T(8,128)(2,1)S(1)}, u32[]{:S(2)}, u32[]{:S(2)}) collective-permute-start(bf16[67,256]{1,0:T(8,128)(2,1)S(1)} %get-tuple-element.81), channel_id=1, source_target_pairs={{0,24},{2,26},{4,28},{6,30},{8,16},{10,18},{12,20},{14,22},{16,8},... | collective-permute-start | bytes 102920 | tf_op jit(solution)/shard_map/ppermute | solution.py:45
  50.3 0.9 collective-permute-done.11
  51.2 3.0 %collective-permute-done.12 = bf16[67,256]{1,0:T(8,128)(2,1)S(1)} collective-permute-done((bf16[67,256]{1,0:T(8,128)(2,1)S(1)}, bf16[67,256]{1,0:T(8,128)(2,1)S(1)}, u32[]{:S(2)}, u32[]{:S(2)}) %collective-permute-start.12) | collective-permute-done | bytes 34336 | tf_op jit(solution)/shard_map/ppermute | solution.py:45
  54.4 1.1 %collective-permute-done.13 = f32[8]{0:T(128)S(1)} collective-permute-done((f32[8]{0:T(128)S(1)}, f32[8]{0:T(128)S(1)}, u32[]{:S(2)}, u32[]{:S(2)}) %collective-permute-start.13) | collective-permute-done | bytes 64 | tf_op jit(solution)/shard_map/ppermute | solution.py:45
  55.5 0.5 copy-done.20
  56.2 0.6 convert_bitcast_fusion.1
  56.8 2.4 %collective-permute-start.17 = (bf16[1,64,256]{2,1,0:T(8,128)(2,1)}, bf16[1,64,256]{2,1,0:T(8,128)(2,1)}, u32[]{:S(2)}, u32[]{:S(2)}) collective-permute-start(bf16[1,64,256]{2,1,0:T(8,128)(2,1)} %get-tuple-element.28), channel_id=1, source_target_pairs={{0,16},{2,18},{4,20},{6,22},{8,24},{10,26},{12,28},{14,30},{16,0},... | collective-permute-start | bytes 98312 | tf_op jit(solution)/shard_map/ppermute | solution.py:45
  59.2 2.0 %collective-permute-start.16 = (bf16[1,64,256]{2,1,0:T(8,128)(2,1)}, bf16[1,64,256]{2,1,0:T(8,128)(2,1)}, u32[]{:S(2)}, u32[]{:S(2)}) collective-permute-start(bf16[1,64,256]{2,1,0:T(8,128)(2,1)} %get-tuple-element.28), channel_id=1, source_target_pairs={{0,24},{2,26},{4,28},{6,30},{8,16},{10,18},{12,20},{14,22},{16,8},... | collective-permute-start | bytes 98312 | tf_op jit(solution)/shard_map/ppermute | solution.py:45
  62.1 0.8 convert_bitcast_fusion
  63.1 0.8 fusion.58
  64.1 1.1 %collective-permute-done.16 = bf16[1,64,256]{2,1,0:T(8,128)(2,1)} collective-permute-done((bf16[1,64,256]{2,1,0:T(8,128)(2,1)}, bf16[1,64,256]{2,1,0:T(8,128)(2,1)}, u32[]{:S(2)}, u32[]{:S(2)}) %collective-permute-start.16) | collective-permute-done | bytes 32800 | tf_op jit(solution)/shard_map/ppermute | solution.py:45
  65.3 0.8 select_bitcast_fusion.15
  66.1 0.6 collective-permute-start.21
  66.7 0.5 collective-permute-start.20
  67.2 2.4 %collective-permute-start.19 = (bf16[4,64,256]{2,1,0:T(8,128)(2,1)S(1)}, bf16[4,64,256]{2,1,0:T(8,128)(2,1)S(1)}, u32[]{:S(2)}, u32[]{:S(2)}) collective-permute-start(bf16[4,64,256]{2,1,0:T(8,128)(2,1)S(1)} %maximum_bitcast_fusion.1), channel_id=1, source_target_pairs={{0,6},{2,4},{4,2},{6,0},{8,14},{10,12},{12,10},{14,8},{16,22},{18,... | collective-permute-start | bytes 393224 | tf_op jit(solution)/shard_map/ppermute | solution.py:45
  70.2 2.0 %collective-permute-done.21 = bf16[4,64,256]{2,1,0:T(8,128)(2,1)S(1)} collective-permute-done((bf16[4,64,256]{2,1,0:T(8,128)(2,1)S(1)}, bf16[4,64,256]{2,1,0:T(8,128)(2,1)S(1)}, u32[]{:S(2)}, u32[]{:S(2)}) %collective-permute-start.21) | collective-permute-done | bytes 131104 | tf_op jit(solution)/shard_map/ppermute | solution.py:45
  72.5 2.1 %collective-permute-done.19 = bf16[4,64,256]{2,1,0:T(8,128)(2,1)S(1)} collective-permute-done((bf16[4,64,256]{2,1,0:T(8,128)(2,1)S(1)}, bf16[4,64,256]{2,1,0:T(8,128)(2,1)S(1)}, u32[]{:S(2)}, u32[]{:S(2)}) %collective-permute-start.19) | collective-permute-done | bytes 131104 | tf_op jit(solution)/shard_map/ppermute | solution.py:45
  75.0 1.2 %select_bitcast_fusion.1 = (bf16[1,1,384,256]{3,2,1,0:T(8,128)(2,1)S(1)}, bf16[1,1,384,256]{3,2,1,0:T(8,128)(2,1)S(1)}) fusion(bf16[1,384,256]{2,1,0:T(8,128)(2,1)} %collective-permute-done.15, bf16[1,384,256]{2,1,0:T(8,128)(2,1)} %get-tuple-element.26, pred[]{:T(512)S(6)} %eq.53), kind=kLoop, calls=%fused_computation.77 | loop fusion | flops 196608 | bytes 786433 | tf_op jit(solution)/shard_map/stack | solution.py:128
  76.5 1.5 %fusion.5 = (f32[256]{0:T(256)S(1)}, f32[768,256]{1,0:T(8,128)}) fusion(bf16[1,2,384,256]{3,2,1,0:T(8,128)(2,1)S(1)} %pad_maximum_fusion.3, bf16[768,256]{1,0:T(8,128)(2,1)S(1)} %bitcast.228, f32[768]{0:T(1024)S(1)} %copy-done.19, bf16[768,1024]{1,0:T(8,128)(2,1)S(1)} %bitcast.200, bf16[1024,256]{1,0:T(8,128)(2,1)S(1)} %bitcast.210), kind=kOutput, calls=%fused_computation.19 | convolution fusion | flops 403832576 | bytes 3674112 | tf_op jit(solution)/shard_map/dot_general | solution.py:161
  78.0 1.7 %fusion.3 = (f32[256]{0:T(256)S(1)}, f32[1024,256]{1,0:T(8,128)}) fusion(bf16[4,4,64,256]{3,2,1,0:T(8,128)(2,1)S(1)} %copy.34, bf16[1024,256]{1,0:T(8,128)(2,1)S(1)} %bitcast.211, f32[1024]{0:T(1024)S(1)} %bitcast.232, bf16[1024,768]{0,1:T(8,128)(2,1)S(1)} %bitcast.198, bf16[768,256]{1,0:T(8,128)(2,1)S(1)} %bitcast.229), kind=kOutput, calls=%fused_computation.13 | convolution fusion | flops 404225792 | bytes 4068352 | tf_op jit(solution)/shard_map/dot_general | solution.py:163
  80.3 1.2 %dynamic-slice_convert_fusion.4 = (bf16[2,2,1,1,64,256]{5,4,3,2,1,0:T(8,128)(2,1)S(1)}, bf16[2,2,1,1,64,256]{5,4,3,2,1,0:T(8,128)(2,1)S(1)}, bf16[2,2,1,1,64,256]{5,4,3,2,1,0:T(8,128)(2,1)S(1)}) fusion(f32[2,2,2,2,64,256]{5,4,3,2,1,0:T(8,128)} %bitcast.222, s32[]{:T(128)S(6)} %select_n.385, s32[]{:T(128)S(6)} %select_n.387, s32[]{:T(128)S(6)} %select_n.393, ...), kind=kLoop, calls=%fused_computation.52 | loop fusion | bytes 786456 | tf_op jit(solution)/shard_map/convert_element_type | solution.py:90
  81.5 1.5 %collective-permute-start.22 = (bf16[259,256]{1,0:T(8,128)(2,1)S(1)}, bf16[259,256]{1,0:T(8,128)(2,1)S(1)}, u32[]{:S(2)}, u32[]{:S(2)}) collective-permute-start(bf16[259,256]{1,0:T(8,128)(2,1)S(1)} %get-tuple-element.76), channel_id=1, source_target_pairs={{0,2},{2,0},{4,6},{6,4},{8,10},{10,8},{12,14},{14,12},{16,18},{18,... | collective-permute-start | bytes 397832 | tf_op jit(solution)/shard_map/ppermute | solution.py:45
  82.9 0.9 collective-permute-start.23
  83.9 1.2 %collective-permute-start.24 = (bf16[259,256]{1,0:T(8,128)(2,1)S(1)}, bf16[259,256]{1,0:T(8,128)(2,1)S(1)}, u32[]{:S(2)}, u32[]{:S(2)}) collective-permute-start(bf16[259,256]{1,0:T(8,128)(2,1)S(1)} %get-tuple-element.78), channel_id=1, source_target_pairs={{0,6},{2,4},{4,2},{6,0},{8,14},{10,12},{12,10},{14,8},{16,22},{18,... | collective-permute-start | bytes 397832 | tf_op jit(solution)/shard_map/ppermute | solution.py:45
  85.0 1.7 %fusion.21 = bf16[384,256]{1,0:T(8,128)(2,1)} fusion(f32[2,384,256]{2,1,0:T(8,128)} %bitcast.220, s32[]{:T(128)S(6)} %select_n.413), kind=kLoop, calls=%fused_computation.75 | loop fusion | bytes 393220 | tf_op jit(solution)/shard_map/convert_element_type | solution.py:90
  86.7 1.1 %constant_dynamic-slice_fusion = f32[2,2,1,1,64,256]{5,4,3,2,1,0:T(8,128)S(1)} fusion(f32[2,2,2,2,64,256]{5,4,3,2,1,0:T(8,128)} %bitcast.223, s32[]{:T(128)S(6)} %select_n.380, s32[]{:T(128)S(6)} %select_n.382), kind=kLoop, calls=%fused_computation.160 | loop fusion | bytes 524296 | tf_op jit(solution)/shard_map/jit(dynamic_index_in_dim)/dynamic_slice | solution.py:79
  87.9 2.1 %collective-permute-done.23 = bf16[259,256]{1,0:T(8,128)(2,1)S(1)} collective-permute-done((bf16[259,256]{1,0:T(8,128)(2,1)S(1)}, bf16[259,256]{1,0:T(8,128)(2,1)S(1)}, u32[]{:S(2)}, u32[]{:S(2)}) %collective-permute-start.23) | collective-permute-done | bytes 132640 | tf_op jit(solution)/shard_map/ppermute | solution.py:45
  90.3 2.5 %collective-permute-start.26 = (bf16[67,256]{1,0:T(8,128)(2,1)S(1)}, bf16[67,256]{1,0:T(8,128)(2,1)S(1)}, u32[]{:S(2)}, u32[]{:S(2)}) collective-permute-start(bf16[67,256]{1,0:T(8,128)(2,1)S(1)} %get-tuple-element.74), channel_id=1, source_target_pairs={{0,16},{2,18},{4,20},{6,22},{8,24},{10,26},{12,28},{14,30},{16,0},... | collective-permute-start | bytes 102920 | tf_op jit(solution)/shard_map/ppermute | solution.py:45
  92.7 1.9 %collective-permute-start.27 = (bf16[67,256]{1,0:T(8,128)(2,1)S(1)}, bf16[67,256]{1,0:T(8,128)(2,1)S(1)}, u32[]{:S(2)}, u32[]{:S(2)}) collective-permute-start(bf16[67,256]{1,0:T(8,128)(2,1)S(1)} %get-tuple-element.75), channel_id=1, source_target_pairs={{0,24},{2,26},{4,28},{6,30},{8,16},{10,18},{12,20},{14,22},{16,8},... | collective-permute-start | bytes 102920 | tf_op jit(solution)/shard_map/ppermute | solution.py:45
  94.7 0.6 collective-permute-done.26
  95.2 3.3 %collective-permute-done.27 = bf16[67,256]{1,0:T(8,128)(2,1)S(1)} collective-permute-done((bf16[67,256]{1,0:T(8,128)(2,1)S(1)}, bf16[67,256]{1,0:T(8,128)(2,1)S(1)}, u32[]{:S(2)}, u32[]{:S(2)}) %collective-permute-start.27) | collective-permute-done | bytes 34336 | tf_op jit(solution)/shard_map/ppermute | solution.py:45
  98.6 1.1 %collective-permute-done.28 = f32[8]{0:T(128)S(1)} collective-permute-done((f32[8]{0:T(128)S(1)}, f32[8]{0:T(128)S(1)}, u32[]{:S(2)}, u32[]{:S(2)}) %collective-permute-start.28) | collective-permute-done | bytes 64 | tf_op jit(solution)/shard_map/ppermute | solution.py:45
  100.1 0.7 fusion.32
  100.8 2.2 %fusion.11 = (f32[1,384,256]{2,1,0:T(8,128)}, f32[1,384,256]{2,1,0:T(8,128)}) fusion(f32[384,256]{1,0:T(8,128)S(1)} %get-tuple-element.27, f32[384,256]{1,0:T(8,128)S(1)} %reshape.294, bf16[384,256]{1,0:T(8,128)(2,1)} %collective-permute-done.29, f32[2,384,256]{2,1,0:T(8,128)} %bitcast.221, s32[]{:T(128)S(6)} %select_n.412, f32[256]{0:T(256)S(1)} %mul.212, ...), kind=kLoop, calls=%fused_computation.30 | loop fusion | flops 1671168 | bytes 3542020 | tf_op jit(solution)/shard_map/broadcast_in_dim | solution.py:224
  (172 shorter events, 8.4 us)
Async XLA Ops:
  0.6 22.5 %copy-start = (f32[64,64]{1,0:T(8,128)S(1)}, f32[64,64]{1,0:T(8,128)}, u32[]{:S(2)}) copy-start(f32[64,64]{1,0:T(8,128)} %param.9) | copy-start | bytes 49156
  1.5 9.0 %collective-permute-start.2 = (bf16[1,64,256]{2,1,0:T(8,128)(2,1)S(1)}, bf16[1,64,256]{2,1,0:T(8,128)(2,1)S(1)}, u32[]{:S(2)}, u32[]{:S(2)}) collective-permute-start(bf16[1,64,256]{2,1,0:T(8,128)(2,1)S(1)} %convert_element_type.273), channel_id=1, source_target_pairs={{0,8},{2,10},{4,12},{6,14},{8,0},{10,2},{12,4},{14,6},{16,24},{18,... | collective-permute-start | bytes 98312 | tf_op jit(solution)/shard_map/ppermute | solution.py:45
  4.5 6.0 %collective-permute-start.1 = (bf16[1,64,256]{2,1,0:T(8,128)(2,1)S(1)}, bf16[1,64,256]{2,1,0:T(8,128)(2,1)S(1)}, u32[]{:S(2)}, u32[]{:S(2)}) collective-permute-start(bf16[1,64,256]{2,1,0:T(8,128)(2,1)S(1)} %convert_element_type.273), channel_id=1, source_target_pairs={{0,16},{2,18},{4,20},{6,22},{8,24},{10,26},{12,28},{14,30},{16,0},... | collective-permute-start | bytes 98312 | tf_op jit(solution)/shard_map/ppermute | solution.py:45
  7.1 5.7 %collective-permute-start = (bf16[1,64,256]{2,1,0:T(8,128)(2,1)S(1)}, bf16[1,64,256]{2,1,0:T(8,128)(2,1)S(1)}, u32[]{:S(2)}, u32[]{:S(2)}) collective-permute-start(bf16[1,64,256]{2,1,0:T(8,128)(2,1)S(1)} %convert_element_type.273), channel_id=1, source_target_pairs={{0,24},{2,26},{4,28},{6,30},{8,16},{10,18},{12,20},{14,22},{16,8},... | collective-permute-start | bytes 98312 | tf_op jit(solution)/shard_map/ppermute | solution.py:45
  8.8 22.3 %collective-permute-start.3 = (bf16[1,384,256]{2,1,0:T(8,128)(2,1)}, bf16[1,384,256]{2,1,0:T(8,128)(2,1)S(1)}, u32[]{:S(2)}, u32[]{:S(2)}) collective-permute-start(bf16[1,384,256]{2,1,0:T(8,128)(2,1)} %convert_element_type.275), channel_id=1, source_target_pairs={{0,1},{1,0},{2,3},{3,2},{4,5},{5,4},{6,7},{7,6},{8,9},{9,8},{10,11... | collective-permute-start | bytes 589832 | tf_op jit(solution)/shard_map/ppermute | solution.py:45
  13.7 6.0 %copy-start.2 = (s32[1,1,12,256,256]{4,3,2,1,0:T(8,128)S(1)}, s32[1,1,12,256,256]{4,3,2,1,0:T(8,128)}, u32[]{:S(2)}) copy-start(s32[1,1,12,256,256]{4,3,2,1,0:T(8,128)} %param.11) | copy-start | bytes 9437188
  13.7 15.5 %collective-permute-start.6 = (bf16[4,64,256]{2,1,0:T(8,128)(2,1)S(1)}, bf16[4,64,256]{2,1,0:T(8,128)(2,1)S(1)}, u32[]{:S(2)}, u32[]{:S(2)}) collective-permute-start(bf16[4,64,256]{2,1,0:T(8,128)(2,1)S(1)} %maximum_bitcast_fusion), channel_id=1, source_target_pairs={{0,2},{2,0},{4,6},{6,4},{8,10},{10,8},{12,14},{14,12},{16,18},{18,... | collective-permute-start | bytes 393224 | tf_op jit(solution)/shard_map/ppermute | solution.py:45
  15.3 13.9 %collective-permute-start.5 = (bf16[4,64,256]{2,1,0:T(8,128)(2,1)S(1)}, bf16[4,64,256]{2,1,0:T(8,128)(2,1)S(1)}, u32[]{:S(2)}, u32[]{:S(2)}) collective-permute-start(bf16[4,64,256]{2,1,0:T(8,128)(2,1)S(1)} %maximum_bitcast_fusion), channel_id=1, source_target_pairs={{0,4},{2,6},{4,0},{6,2},{8,12},{10,14},{12,8},{14,10},{16,20},{18,... | collective-permute-start | bytes 393224 | tf_op jit(solution)/shard_map/ppermute | solution.py:45
  16.8 13.1 %collective-permute-start.4 = (bf16[4,64,256]{2,1,0:T(8,128)(2,1)S(1)}, bf16[4,64,256]{2,1,0:T(8,128)(2,1)}, u32[]{:S(2)}, u32[]{:S(2)}) collective-permute-start(bf16[4,64,256]{2,1,0:T(8,128)(2,1)S(1)} %maximum_bitcast_fusion), channel_id=1, source_target_pairs={{0,6},{2,4},{4,2},{6,0},{8,14},{10,12},{12,10},{14,8},{16,22},{18,... | collective-permute-start | bytes 393224 | tf_op jit(solution)/shard_map/ppermute | solution.py:45
  19.8 1.8 %copy-start.3 = (f32[1,64,256]{2,1,0:T(8,128)S(1)}, f32[1,64,256]{2,1,0:T(8,128)}, u32[]{:S(2)}) copy-start(f32[1,64,256]{2,1,0:T(8,128)} %param.8) | copy-start | bytes 196612
  19.8 1.9 %copy-start.15 = (f32[64,64]{1,0:T(8,128)S(1)}, f32[64,64]{1,0:T(8,128)}, u32[]{:S(2)}) copy-start(f32[64,64]{1,0:T(8,128)} %param.10) | copy-start | bytes 49156
  19.8 3.1 %copy-start.1 = (f32[1,384,256]{2,1,0:T(8,128)S(1)}, f32[1,384,256]{2,1,0:T(8,128)}, u32[]{:S(2)}) copy-start(f32[1,384,256]{2,1,0:T(8,128)} %param.7) | copy-start | bytes 1179652
  21.4 9.8 %copy-start.16 = (f32[1,2,4,128]{3,1,2,0:T(2,128)}, f32[1,2,4,128]{3,1,2,0:T(2,128)S(1)}, u32[]{:S(2)}) copy-start(f32[1,2,4,128]{3,1,2,0:T(2,128)S(1)} %copy.45) | copy-start | bytes 12292
  21.5 11.7 %copy-start.18 = (f32[768]{0:T(1024)}, f32[768]{0:T(1024)S(1)}, u32[]{:S(2)}) copy-start(f32[768]{0:T(1024)S(1)} %mul.186) | copy-start | bytes 9220
  28.2 3.0 %copy-start.4 = (bf16[96,8,4,256]{3,1,2,0:T(8,128)(2,1)}, bf16[96,8,4,256]{3,1,2,0:T(8,128)(2,1)S(1)}, u32[]{:S(2)}) copy-start(bf16[96,8,4,256]{3,1,2,0:T(8,128)(2,1)S(1)} %copy.44) | copy-start | bytes 4718596
  29.2 4.1 %copy-start.6 = (bf16[96,8,4,256]{3,1,2,0:T(8,128)(2,1)}, bf16[96,8,4,256]{3,1,2,0:T(8,128)(2,1)S(1)}, u32[]{:S(2)}) copy-start(bf16[96,8,4,256]{3,1,2,0:T(8,128)(2,1)S(1)} %copy.46) | copy-start | bytes 4718596
  29.2 0.7 copy-start.14
  31.1 1.9 %copy-start.12 = (bf16[4,4,64,256]{3,2,1,0:T(8,128)(2,1)}, bf16[4,4,64,256]{3,2,1,0:T(8,128)(2,1)S(1)}, u32[]{:S(2)}) copy-start(bf16[4,4,64,256]{3,2,1,0:T(8,128)(2,1)S(1)} %copy.30) | copy-start | bytes 1572868
  31.2 1.8 %copy-start.13 = (bf16[1,2,384,256]{3,2,1,0:T(8,128)(2,1)}, bf16[1,2,384,256]{3,2,1,0:T(8,128)(2,1)S(1)}, u32[]{:S(2)}) copy-start(bf16[1,2,384,256]{3,2,1,0:T(8,128)(2,1)S(1)} %pad_maximum_fusion.2) | copy-start | bytes 1179652
  33.2 2.1 %copy-start.22 = (f32[4]{0:T(128)S(1)}, f32[4]{0:T(128)}, u32[]{:S(2)}) copy-start(f32[4]{0:T(128)} %reduce_sum.195) | copy-start | bytes 52
  35.1 27.0 %copy-start.8 = (f32[768,256]{1,0:T(8,128)}, f32[768,256]{1,0:T(8,128)S(1)}, u32[]{:S(2)}) copy-start(f32[768,256]{1,0:T(8,128)S(1)} %get-tuple-element.98) | copy-start | bytes 2359300
  36.7 5.6 %collective-permute-start.7 = (bf16[259,256]{1,0:T(8,128)(2,1)S(1)}, bf16[259,256]{1,0:T(8,128)(2,1)S(1)}, u32[]{:S(2)}, u32[]{:S(2)}) collective-permute-start(bf16[259,256]{1,0:T(8,128)(2,1)S(1)} %get-tuple-element.82), channel_id=1, source_target_pairs={{0,2},{2,0},{4,6},{6,4},{8,10},{10,8},{12,14},{14,12},{16,18},{18,... | collective-permute-start | bytes 397832 | tf_op jit(solution)/shard_map/ppermute | solution.py:45
  38.2 5.2 %collective-permute-start.8 = (bf16[259,256]{1,0:T(8,128)(2,1)S(1)}, bf16[259,256]{1,0:T(8,128)(2,1)S(1)}, u32[]{:S(2)}, u32[]{:S(2)}) collective-permute-start(bf16[259,256]{1,0:T(8,128)(2,1)S(1)} %get-tuple-element.83), channel_id=1, source_target_pairs={{0,4},{2,6},{4,0},{6,2},{8,12},{10,14},{12,8},{14,10},{16,20},{18,... | collective-permute-start | bytes 397832 | tf_op jit(solution)/shard_map/ppermute | solution.py:45
  39.7 5.9 %collective-permute-start.9 = (bf16[259,256]{1,0:T(8,128)(2,1)S(1)}, bf16[259,256]{1,0:T(8,128)(2,1)S(1)}, u32[]{:S(2)}, u32[]{:S(2)}) collective-permute-start(bf16[259,256]{1,0:T(8,128)(2,1)S(1)} %get-tuple-element.84), channel_id=1, source_target_pairs={{0,6},{2,4},{4,2},{6,0},{8,14},{10,12},{12,10},{14,8},{16,22},{18,... | collective-permute-start | bytes 397832 | tf_op jit(solution)/shard_map/ppermute | solution.py:45
  40.2 21.9 %collective-permute-start.14 = (bf16[384,256]{1,0:T(8,128)(2,1)S(1)}, bf16[384,256]{1,0:T(8,128)(2,1)S(1)}, u32[]{:S(2)}, u32[]{:S(2)}) collective-permute-start(bf16[384,256]{1,0:T(8,128)(2,1)S(1)} %fusion.20), channel_id=1, source_target_pairs={{0,1},{1,0},{2,3},{3,2},{4,5},{5,4},{6,7},{7,6},{8,9},{9,8},{10,11... | collective-permute-start | bytes 589832 | tf_op jit(solution)/shard_map/ppermute | solution.py:45
  45.9 4.5 %collective-permute-start.10 = (bf16[67,256]{1,0:T(8,128)(2,1)S(1)}, bf16[67,256]{1,0:T(8,128)(2,1)S(1)}, u32[]{:S(2)}, u32[]{:S(2)}) collective-permute-start(bf16[67,256]{1,0:T(8,128)(2,1)S(1)} %get-tuple-element.79), channel_id=1, source_target_pairs={{0,8},{2,10},{4,12},{6,14},{8,0},{10,2},{12,4},{14,6},{16,24},{18,... | collective-permute-start | bytes 102920 | tf_op jit(solution)/shard_map/ppermute | solution.py:45
  45.9 5.3 %collective-permute-start.11 = (bf16[67,256]{1,0:T(8,128)(2,1)S(1)}, bf16[67,256]{1,0:T(8,128)(2,1)S(1)}, u32[]{:S(2)}, u32[]{:S(2)}) collective-permute-start(bf16[67,256]{1,0:T(8,128)(2,1)S(1)} %get-tuple-element.80), channel_id=1, source_target_pairs={{0,16},{2,18},{4,20},{6,22},{8,24},{10,26},{12,28},{14,30},{16,0},... | collective-permute-start | bytes 102920 | tf_op jit(solution)/shard_map/ppermute | solution.py:45
  48.5 5.8 %collective-permute-start.12 = (bf16[67,256]{1,0:T(8,128)(2,1)S(1)}, bf16[67,256]{1,0:T(8,128)(2,1)S(1)}, u32[]{:S(2)}, u32[]{:S(2)}) collective-permute-start(bf16[67,256]{1,0:T(8,128)(2,1)S(1)} %get-tuple-element.81), channel_id=1, source_target_pairs={{0,24},{2,26},{4,28},{6,30},{8,16},{10,18},{12,20},{14,22},{16,8},... | collective-permute-start | bytes 102920 | tf_op jit(solution)/shard_map/ppermute | solution.py:45
  54.3 1.2 %collective-permute-start.13 = (f32[8]{0:T(128)S(1)}, f32[8]{0:T(128)S(1)}, u32[]{:S(2)}, u32[]{:S(2)}) collective-permute-start(f32[8]{0:T(128)S(1)} %fusion.47), channel_id=1, source_target_pairs={{0,1},{1,0},{2,3},{3,2},{4,5},{5,4},{6,7},{7,6},{8,9},{9,8},{10,11... | collective-permute-start | bytes 104 | tf_op jit(solution)/shard_map/ppermute | solution.py:45
  55.5 0.5 copy-start.20
  56.8 7.3 %collective-permute-start.18 = (bf16[1,64,256]{2,1,0:T(8,128)(2,1)}, bf16[1,64,256]{2,1,0:T(8,128)(2,1)}, u32[]{:S(2)}, u32[]{:S(2)}) collective-permute-start(bf16[1,64,256]{2,1,0:T(8,128)(2,1)} %get-tuple-element.28), channel_id=1, source_target_pairs={{0,8},{2,10},{4,12},{6,14},{8,0},{10,2},{12,4},{14,6},{16,24},{18,... | collective-permute-start | bytes 98312 | tf_op jit(solution)/shard_map/ppermute | solution.py:45
  56.8 7.3 %collective-permute-start.17 = (bf16[1,64,256]{2,1,0:T(8,128)(2,1)}, bf16[1,64,256]{2,1,0:T(8,128)(2,1)}, u32[]{:S(2)}, u32[]{:S(2)}) collective-permute-start(bf16[1,64,256]{2,1,0:T(8,128)(2,1)} %get-tuple-element.28), channel_id=1, source_target_pairs={{0,16},{2,18},{4,20},{6,22},{8,24},{10,26},{12,28},{14,30},{16,0},... | collective-permute-start | bytes 98312 | tf_op jit(solution)/shard_map/ppermute | solution.py:45
  59.2 6.0 %collective-permute-start.16 = (bf16[1,64,256]{2,1,0:T(8,128)(2,1)}, bf16[1,64,256]{2,1,0:T(8,128)(2,1)}, u32[]{:S(2)}, u32[]{:S(2)}) collective-permute-start(bf16[1,64,256]{2,1,0:T(8,128)(2,1)} %get-tuple-element.28), channel_id=1, source_target_pairs={{0,24},{2,26},{4,28},{6,30},{8,16},{10,18},{12,20},{14,22},{16,8},... | collective-permute-start | bytes 98312 | tf_op jit(solution)/shard_map/ppermute | solution.py:45
  62.1 1.0 copy-start.10
  62.9 12.1 %collective-permute-start.15 = (bf16[1,384,256]{2,1,0:T(8,128)(2,1)}, bf16[1,384,256]{2,1,0:T(8,128)(2,1)}, u32[]{:S(2)}, u32[]{:S(2)}) collective-permute-start(bf16[1,384,256]{2,1,0:T(8,128)(2,1)} %get-tuple-element.26), channel_id=1, source_target_pairs={{0,1},{1,0},{2,3},{3,2},{4,5},{5,4},{6,7},{7,6},{8,9},{9,8},{10,11... | collective-permute-start | bytes 589832 | tf_op jit(solution)/shard_map/ppermute | solution.py:45
  66.1 6.1 %collective-permute-start.21 = (bf16[4,64,256]{2,1,0:T(8,128)(2,1)S(1)}, bf16[4,64,256]{2,1,0:T(8,128)(2,1)S(1)}, u32[]{:S(2)}, u32[]{:S(2)}) collective-permute-start(bf16[4,64,256]{2,1,0:T(8,128)(2,1)S(1)} %maximum_bitcast_fusion.1), channel_id=1, source_target_pairs={{0,2},{2,0},{4,6},{6,4},{8,10},{10,8},{12,14},{14,12},{16,18},{18,... | collective-permute-start | bytes 393224 | tf_op jit(solution)/shard_map/ppermute | solution.py:45
  66.7 5.8 %collective-permute-start.20 = (bf16[4,64,256]{2,1,0:T(8,128)(2,1)S(1)}, bf16[4,64,256]{2,1,0:T(8,128)(2,1)S(1)}, u32[]{:S(2)}, u32[]{:S(2)}) collective-permute-start(bf16[4,64,256]{2,1,0:T(8,128)(2,1)S(1)} %maximum_bitcast_fusion.1), channel_id=1, source_target_pairs={{0,4},{2,6},{4,0},{6,2},{8,12},{10,14},{12,8},{14,10},{16,20},{18,... | collective-permute-start | bytes 393224 | tf_op jit(solution)/shard_map/ppermute | solution.py:45
  67.2 7.3 %collective-permute-start.19 = (bf16[4,64,256]{2,1,0:T(8,128)(2,1)S(1)}, bf16[4,64,256]{2,1,0:T(8,128)(2,1)S(1)}, u32[]{:S(2)}, u32[]{:S(2)}) collective-permute-start(bf16[4,64,256]{2,1,0:T(8,128)(2,1)S(1)} %maximum_bitcast_fusion.1), channel_id=1, source_target_pairs={{0,6},{2,4},{4,2},{6,0},{8,14},{10,12},{12,10},{14,8},{16,22},{18,... | collective-permute-start | bytes 393224 | tf_op jit(solution)/shard_map/ppermute | solution.py:45
  74.9 1.6 %copy-start.7 = (bf16[96,8,4,256]{3,1,2,0:T(8,128)(2,1)S(1)}, bf16[96,8,4,256]{3,1,2,0:T(8,128)(2,1)}, u32[]{:S(2)}) copy-start(bf16[96,8,4,256]{3,1,2,0:T(8,128)(2,1)} %copy-done.6) | copy-start | bytes 4718596
  75.0 1.6 %copy-start.19 = (f32[768]{0:T(1024)S(1)}, f32[768]{0:T(1024)}, u32[]{:S(2)}) copy-start(f32[768]{0:T(1024)} %copy-done.18) | copy-start | bytes 9220
  76.5 1.5 %copy-start.5 = (bf16[96,8,4,256]{3,1,2,0:T(8,128)(2,1)S(1)}, bf16[96,8,4,256]{3,1,2,0:T(8,128)(2,1)}, u32[]{:S(2)}) copy-start(bf16[96,8,4,256]{3,1,2,0:T(8,128)(2,1)} %copy-done.4) | copy-start | bytes 4718596
  76.5 1.5 %copy-start.17 = (f32[1,2,4,128]{3,1,2,0:T(2,128)S(1)}, f32[1,2,4,128]{3,1,2,0:T(2,128)}, u32[]{:S(2)}) copy-start(f32[1,2,4,128]{3,1,2,0:T(2,128)} %copy-done.16) | copy-start | bytes 12292
  81.5 6.4 %collective-permute-start.22 = (bf16[259,256]{1,0:T(8,128)(2,1)S(1)}, bf16[259,256]{1,0:T(8,128)(2,1)S(1)}, u32[]{:S(2)}, u32[]{:S(2)}) collective-permute-start(bf16[259,256]{1,0:T(8,128)(2,1)S(1)} %get-tuple-element.76), channel_id=1, source_target_pairs={{0,2},{2,0},{4,6},{6,4},{8,10},{10,8},{12,14},{14,12},{16,18},{18,... | collective-permute-start | bytes 397832 | tf_op jit(solution)/shard_map/ppermute | solution.py:45
  82.9 7.1 %collective-permute-start.23 = (bf16[259,256]{1,0:T(8,128)(2,1)S(1)}, bf16[259,256]{1,0:T(8,128)(2,1)S(1)}, u32[]{:S(2)}, u32[]{:S(2)}) collective-permute-start(bf16[259,256]{1,0:T(8,128)(2,1)S(1)} %get-tuple-element.77), channel_id=1, source_target_pairs={{0,4},{2,6},{4,0},{6,2},{8,12},{10,14},{12,8},{14,10},{16,20},{18,... | collective-permute-start | bytes 397832 | tf_op jit(solution)/shard_map/ppermute | solution.py:45
  83.9 6.1 %collective-permute-start.24 = (bf16[259,256]{1,0:T(8,128)(2,1)S(1)}, bf16[259,256]{1,0:T(8,128)(2,1)S(1)}, u32[]{:S(2)}, u32[]{:S(2)}) collective-permute-start(bf16[259,256]{1,0:T(8,128)(2,1)S(1)} %get-tuple-element.78), channel_id=1, source_target_pairs={{0,6},{2,4},{4,2},{6,0},{8,14},{10,12},{12,10},{14,8},{16,22},{18,... | collective-permute-start | bytes 397832 | tf_op jit(solution)/shard_map/ppermute | solution.py:45
  85.0 14.7 %copy-start.21 = (f32[8]{0:T(128)S(1)}, f32[8]{0:T(128)}, u32[]{:S(2)}) copy-start(f32[8]{0:T(128)} %copy-done.20) | copy-start | bytes 100
  86.7 14.1 %copy-start.9 = (f32[768,256]{1,0:T(8,128)S(1)}, f32[768,256]{1,0:T(8,128)}, u32[]{:S(2)}) copy-start(f32[768,256]{1,0:T(8,128)} %copy-done.8) | copy-start | bytes 2359300
  86.7 14.1 %copy-start.11 = (bf16[384,256]{1,0:T(8,128)(2,1)S(1)}, bf16[384,256]{1,0:T(8,128)(2,1)}, u32[]{:S(2)}) copy-start(bf16[384,256]{1,0:T(8,128)(2,1)} %copy-done.10) | copy-start | bytes 589828
  86.7 14.1 %collective-permute-start.29 = (bf16[384,256]{1,0:T(8,128)(2,1)}, bf16[384,256]{1,0:T(8,128)(2,1)}, u32[]{:S(2)}, u32[]{:S(2)}) collective-permute-start(bf16[384,256]{1,0:T(8,128)(2,1)} %fusion.21), channel_id=1, source_target_pairs={{0,1},{1,0},{2,3},{3,2},{4,5},{5,4},{6,7},{7,6},{8,9},{9,8},{10,11... | collective-permute-start | bytes 589832 | tf_op jit(solution)/shard_map/ppermute | solution.py:45
  90.2 4.5 %collective-permute-start.25 = (bf16[67,256]{1,0:T(8,128)(2,1)S(1)}, bf16[67,256]{1,0:T(8,128)(2,1)S(1)}, u32[]{:S(2)}, u32[]{:S(2)}) collective-permute-start(bf16[67,256]{1,0:T(8,128)(2,1)S(1)} %get-tuple-element.73), channel_id=1, source_target_pairs={{0,8},{2,10},{4,12},{6,14},{8,0},{10,2},{12,4},{14,6},{16,24},{18,... | collective-permute-start | bytes 102920 | tf_op jit(solution)/shard_map/ppermute | solution.py:45
  90.3 5.0 %collective-permute-start.26 = (bf16[67,256]{1,0:T(8,128)(2,1)S(1)}, bf16[67,256]{1,0:T(8,128)(2,1)S(1)}, u32[]{:S(2)}, u32[]{:S(2)}) collective-permute-start(bf16[67,256]{1,0:T(8,128)(2,1)S(1)} %get-tuple-element.74), channel_id=1, source_target_pairs={{0,16},{2,18},{4,20},{6,22},{8,24},{10,26},{12,28},{14,30},{16,0},... | collective-permute-start | bytes 102920 | tf_op jit(solution)/shard_map/ppermute | solution.py:45
  92.7 5.8 %collective-permute-start.27 = (bf16[67,256]{1,0:T(8,128)(2,1)S(1)}, bf16[67,256]{1,0:T(8,128)(2,1)S(1)}, u32[]{:S(2)}, u32[]{:S(2)}) collective-permute-start(bf16[67,256]{1,0:T(8,128)(2,1)S(1)} %get-tuple-element.75), channel_id=1, source_target_pairs={{0,24},{2,26},{4,28},{6,30},{8,16},{10,18},{12,20},{14,22},{16,8},... | collective-permute-start | bytes 102920 | tf_op jit(solution)/shard_map/ppermute | solution.py:45
  98.6 1.2 %collective-permute-start.28 = (f32[8]{0:T(128)S(1)}, f32[8]{0:T(128)S(1)}, u32[]{:S(2)}, u32[]{:S(2)}) collective-permute-start(f32[8]{0:T(128)S(1)} %fusion.46), channel_id=1, source_target_pairs={{0,1},{1,0},{2,3},{3,2},{4,5},{5,4},{6,7},{7,6},{8,9},{9,8},{10,11... | collective-permute-start | bytes 104 | tf_op jit(solution)/shard_map/ppermute | solution.py:45

commit v19 on v18

--- a/solution.py
+++ b/solution.py
@@ -175,7 +175,9 @@
             )
             counts = build_counts(tiles)
         else:
-            item_range = double_gather(item_vec.astype(jnp.bfloat16), "user")
+            item_range, (user_vec, item_vec) = double_gather(
+                item_vec.astype(jnp.bfloat16), "user", (user_vec, item_vec)
+            )
         part_user, part_item = cross_parts(user_range, item_range, counts)
         prior_user_part = prior_term(user_vec, prior_user)
         prior_item_part = prior_term(item_vec, prior_item)

time: 104 us -> 103 us (level)
    another operation x11 -> x10, other arithmetic: 4.4 us -> 4.66 us  [double_gather(): buf = jnp.stack(ordered, axis=1).reshape((-1,) + piece.shape)]
  transfers between devices with their start and end apart: 30 -> 30, of which waited for: 16 -> 15; matrix products, arithmetic and copies ran while one was open for 26% -> 27% of each run, Pallas kernels for 0% -> 0%
where the time goes in v19:
time: 103 us
  starting transfers between devices  33.3 us (32%)
  waiting for transfers between devices  23.7 us (23%)
  other arithmetic  18.8 us (18%)
  local copies, waits for them, and re-layouts  13.2 us (13%)
  matrix products  11.6 us (11%)
  between operations  2.08 us (2%)
    ppermute x30, starting transfers between devices, swap_with(): return lax.ppermute(value, axis, pairs)  33.3 us
    ppermute x30, waiting for transfers between devices, swap_with(): return lax.ppermute(value, axis, pairs)  23.7 us
    another operation x10, other arithmetic, double_gather(): buf = jnp.stack(ordered, axis=1).reshape((-1,) + piece.shape)  4.66 us
    convert_element_type x6, local copies, waits for them, and re-layouts, halve_sum(): send = block_of(digit ^ k).astype(stage_type)  4.1 us
    dot_general x2, matrix products, cross_parts(): to_items = jnp.dot(counts_t, user_range, preferred_element_type=jnp.float32)  3.49 us
    dot_general x2, matrix products, cross_parts(): jnp.dot(counts_bf, item_range, preferred_element_type=jnp.float32)  3.36 us
    broadcast_in_dim x2, other arithmetic, per_device(): return (sol_user[None], sol_item[None], res_user[None], res_item[None])  2.93 us
    dot_general x1, matrix products, build_counts(): jnp.einsum('trc,tij->cjri', place, tiles_bf, preferred_element_type=jnp.b...  2.71 us
  transfers between devices with their start and end apart: 30, of which 15 were waited for; matrix products, arithmetic and copies ran while one was open for 27% of the time, Pallas kernels for 0%

profile of v19, /device:TPU:0, one launch (start us, length us, event | category | flops | bytes accessed | tf_op | source)
XLA Modules:
  0.0 102.7 jit_solution(7028226893367117102)
XLA Ops:
  0.6 0.9 convert_element_type.273
  1.5 3.0 %collective-permute-start.2 = (bf16[1,64,256]{2,1,0:T(8,128)(2,1)S(1)}, bf16[1,64,256]{2,1,0:T(8,128)(2,1)S(1)}, u32[]{:S(2)}, u32[]{:S(2)}) collective-permute-start(bf16[1,64,256]{2,1,0:T(8,128)(2,1)S(1)} %convert_element_type.273), channel_id=1, source_target_pairs={{0,8},{2,10},{4,12},{6,14},{8,0},{10,2},{12,4},{14,6},{16,24},{18,... | collective-permute-start | bytes 98312 | tf_op jit(solution)/shard_map/ppermute | solution.py:45
  4.5 2.6 %collective-permute-start.1 = (bf16[1,64,256]{2,1,0:T(8,128)(2,1)S(1)}, bf16[1,64,256]{2,1,0:T(8,128)(2,1)S(1)}, u32[]{:S(2)}, u32[]{:S(2)}) collective-permute-start(bf16[1,64,256]{2,1,0:T(8,128)(2,1)S(1)} %convert_element_type.273), channel_id=1, source_target_pairs={{0,16},{2,18},{4,20},{6,22},{8,24},{10,26},{12,28},{14,30},{16,0},... | collective-permute-start | bytes 98312 | tf_op jit(solution)/shard_map/ppermute | solution.py:45
  7.1 1.7 %convert_element_type.275 = bf16[1,384,256]{2,1,0:T(8,128)(2,1)} convert(f32[1,384,256]{2,1,0:T(8,128)} %param.7) | non-fusion elementwise | flops 98304 | bytes 589824 | tf_op jit(solution)/shard_map/convert_element_type | solution.py:168
  9.5 0.8 slice_bitcast_fusion.1
  10.5 2.3 %collective-permute-done = bf16[1,64,256]{2,1,0:T(8,128)(2,1)S(1)} collective-permute-done((bf16[1,64,256]{2,1,0:T(8,128)(2,1)S(1)}, bf16[1,64,256]{2,1,0:T(8,128)(2,1)S(1)}, u32[]{:S(2)}, u32[]{:S(2)}) %collective-permute-start) | collective-permute-done | bytes 32800 | tf_op jit(solution)/shard_map/ppermute | solution.py:45
  12.8 0.9 select_bitcast_fusion.19
  13.7 1.6 %collective-permute-start.6 = (bf16[4,64,256]{2,1,0:T(8,128)(2,1)S(1)}, bf16[4,64,256]{2,1,0:T(8,128)(2,1)S(1)}, u32[]{:S(2)}, u32[]{:S(2)}) collective-permute-start(bf16[4,64,256]{2,1,0:T(8,128)(2,1)S(1)} %maximum_bitcast_fusion), channel_id=1, source_target_pairs={{0,2},{2,0},{4,6},{6,4},{8,10},{10,8},{12,14},{14,12},{16,18},{18,... | collective-permute-start | bytes 393224 | tf_op jit(solution)/shard_map/ppermute | solution.py:45
  15.3 1.5 %collective-permute-start.5 = (bf16[4,64,256]{2,1,0:T(8,128)(2,1)S(1)}, bf16[4,64,256]{2,1,0:T(8,128)(2,1)S(1)}, u32[]{:S(2)}, u32[]{:S(2)}) collective-permute-start(bf16[4,64,256]{2,1,0:T(8,128)(2,1)S(1)} %maximum_bitcast_fusion), channel_id=1, source_target_pairs={{0,4},{2,6},{4,0},{6,2},{8,12},{10,14},{12,8},{14,10},{16,20},{18,... | collective-permute-start | bytes 393224 | tf_op jit(solution)/shard_map/ppermute | solution.py:45
  16.8 0.5 collective-permute-start.4
  17.3 2.5 %convert_reduce_fusion.1 = (f32[12,256]{1,0:T(8,128)S(1)}, f32[12,256]{1,0:T(8,128)S(1)}) fusion(s32[12,256,256]{2,1,0:T(8,128)} %bitcast.183), kind=kLoop, calls=%fused_computation.1 | loop fusion | flops 3139584 | bytes 3170304 | tf_op jit(solution)/shard_map/reduce_sum | solution.py:154
  19.8 1.5 %convert_bitcast_fusion.2 = bf16[12,256,256,1]{2,1,0,3:T(8,128)(2,1)} fusion(s32[12,256,256]{2,1,0:T(8,128)S(1)} %bitcast.184), kind=kLoop, calls=%fused_computation.198 | loop fusion | flops 786432 | bytes 4718592 | tf_op jit(solution)/shard_map/convert_element_type | solution.py:146
  22.3 0.7 reduce_sum.195
  23.1 0.8 fusion.56
  24.2 2.7 %fusion = bf16[256,256,3,4]{1,3,2,0:T(4,128)(2,1)S(1)} fusion(bf16[12,256,256,1]{2,1,0,3:T(8,128)(2,1)} %convert_bitcast_fusion.2, pred[12,4]{0,1:T(4,128)(4,1)S(1)} %copy.27, pred[12,3]{0,1:T(4,128)(4,1)S(1)} %fusion.45), kind=kOutput, calls=%fused_computation.2 | convolution fusion | flops 18874512 | bytes 3145812 | tf_op jit(solution)/shard_map/trc,tij->cjri/dot_general | solution.py:150
  27.4 0.5 copy.29
  28.3 0.5 copy.33
  29.2 0.7 copy-done.14
  30.0 1.0 %select_bitcast_fusion.11 = (bf16[4,1,64,256]{3,2,0,1:T(8,128)(2,1)S(1)}, bf16[4,1,64,256]{3,2,0,1:T(8,128)(2,1)S(1)}, bf16[4,1,64,256]{3,2,0,1:T(8,128)(2,1)S(1)}, bf16[4,1,64,256]{3,2,0,1:T(8,128)(2,1)S(1)}) fusion(bf16[4,64,256]{2,1,0:T(8,128)(2,1)} %collective-permute-done.4, bf16[4,64,256]{2,1,0:T(8,128)(2,1)} %copy-done.14, ...), kind=kLoop, calls=%fused_computation.90 | loop fusion | flops 786432 | bytes 1048579 | tf_op jit(solution)/shard_map/stack | solution.py:128
  31.3 1.8 %fusion.2 = (f32[256]{0:T(256)S(1)}, f32[1024,256]{1,0:T(8,128)}) fusion(bf16[4,4,64,256]{3,2,1,0:T(8,128)(2,1)S(1)} %copy.30, bf16[1024,256]{1,0:T(8,128)(2,1)S(1)} %bitcast.204, f32[1024]{0:T(1024)S(1)} %bitcast.223, bf16[1024,768]{0,1:T(8,128)(2,1)S(1)} %bitcast.189, bf16[768,256]{1,0:T(8,128)(2,1)S(1)} %bitcast.218), kind=kOutput, calls=%fused_computation.12 | convolution fusion | flops 404225792 | bytes 4068352 | tf_op jit(solution)/shard_map/dot_general | solution.py:163
  33.3 1.9 %fusion.4 = (f32[256]{0:T(256)S(1)}, f32[768,256]{1,0:T(8,128)S(1)}) fusion(bf16[1,2,384,256]{3,2,1,0:T(8,128)(2,1)} %copy-done.13, bf16[768,256]{1,0:T(8,128)(2,1)} %bitcast.219, f32[768]{0:T(1024)S(1)} %mul.186, bf16[768,1024]{1,0:T(8,128)(2,1)S(1)} %bitcast.191, bf16[1024,256]{1,0:T(8,128)(2,1)} %bitcast.205), kind=kOutput, calls=%fused_computation.18 | convolution fusion | flops 403832576 | bytes 3674112 | tf_op jit(solution)/shard_map/dot_general | solution.py:161
  35.5 1.2 %dynamic-slice_convert_fusion.7 = (bf16[2,2,1,1,64,256]{5,4,3,2,1,0:T(8,128)(2,1)S(1)}, bf16[2,2,1,1,64,256]{5,4,3,2,1,0:T(8,128)(2,1)S(1)}, bf16[2,2,1,1,64,256]{5,4,3,2,1,0:T(8,128)(2,1)S(1)}) fusion(f32[2,2,2,2,64,256]{5,4,3,2,1,0:T(8,128)} %bitcast.216, s32[]{:T(128)S(6)} %select_n.385, s32[]{:T(128)S(6)} %select_n.387, s32[]{:T(128)S(6)} %select_n.393, ...), kind=kLoop, calls=%fused_computation.55 | loop fusion | bytes 786456 | tf_op jit(solution)/shard_map/convert_element_type | solution.py:90
  36.7 1.6 %collective-permute-start.7 = (bf16[259,256]{1,0:T(8,128)(2,1)S(1)}, bf16[259,256]{1,0:T(8,128)(2,1)S(1)}, u32[]{:S(2)}, u32[]{:S(2)}) collective-permute-start(bf16[259,256]{1,0:T(8,128)(2,1)S(1)} %get-tuple-element.89), channel_id=1, source_target_pairs={{0,2},{2,0},{4,6},{6,4},{8,10},{10,8},{12,14},{14,12},{16,18},{18,... | collective-permute-start | bytes 397832 | tf_op jit(solution)/shard_map/ppermute | solution.py:45
  38.3 1.5 %collective-permute-start.8 = (bf16[259,256]{1,0:T(8,128)(2,1)S(1)}, bf16[259,256]{1,0:T(8,128)(2,1)S(1)}, u32[]{:S(2)}, u32[]{:S(2)}) collective-permute-start(bf16[259,256]{1,0:T(8,128)(2,1)S(1)} %get-tuple-element.90), channel_id=1, source_target_pairs={{0,4},{2,6},{4,0},{6,2},{8,12},{10,14},{12,8},{14,10},{16,20},{18,... | collective-permute-start | bytes 397832 | tf_op jit(solution)/shard_map/ppermute | solution.py:45
  39.8 0.5 collective-permute-start.9
  40.3 1.0 constant_dynamic-slice_fusion.1
  41.3 0.9 collective-permute-done.7
  42.3 1.2 %collective-permute-done.8 = bf16[259,256]{1,0:T(8,128)(2,1)S(1)} collective-permute-done((bf16[259,256]{1,0:T(8,128)(2,1)S(1)}, bf16[259,256]{1,0:T(8,128)(2,1)S(1)}, u32[]{:S(2)}, u32[]{:S(2)}) %collective-permute-start.8) | collective-permute-done | bytes 132640 | tf_op jit(solution)/shard_map/ppermute | solution.py:45
  43.5 2.2 %collective-permute-done.9 = bf16[259,256]{1,0:T(8,128)(2,1)S(1)} collective-permute-done((bf16[259,256]{1,0:T(8,128)(2,1)S(1)}, bf16[259,256]{1,0:T(8,128)(2,1)S(1)}, u32[]{:S(2)}, u32[]{:S(2)}) %collective-permute-start.9) | collective-permute-done | bytes 132640 | tf_op jit(solution)/shard_map/ppermute | solution.py:45
  45.9 2.6 %collective-permute-start.11 = (bf16[67,256]{1,0:T(8,128)(2,1)S(1)}, bf16[67,256]{1,0:T(8,128)(2,1)S(1)}, u32[]{:S(2)}, u32[]{:S(2)}) collective-permute-start(bf16[67,256]{1,0:T(8,128)(2,1)S(1)} %get-tuple-element.87), channel_id=1, source_target_pairs={{0,16},{2,18},{4,20},{6,22},{8,24},{10,26},{12,28},{14,30},{16,0},... | collective-permute-start | bytes 102920 | tf_op jit(solution)/shard_map/ppermute | solution.py:45
  48.5 1.8 %collective-permute-start.12 = (bf16[67,256]{1,0:T(8,128)(2,1)S(1)}, bf16[67,256]{1,0:T(8,128)(2,1)S(1)}, u32[]{:S(2)}, u32[]{:S(2)}) collective-permute-start(bf16[67,256]{1,0:T(8,128)(2,1)S(1)} %get-tuple-element.88), channel_id=1, source_target_pairs={{0,24},{2,26},{4,28},{6,30},{8,16},{10,18},{12,20},{14,22},{16,8},... | collective-permute-start | bytes 102920 | tf_op jit(solution)/shard_map/ppermute | solution.py:45
  50.3 0.9 collective-permute-done.11
  51.3 3.0 %collective-permute-done.12 = bf16[67,256]{1,0:T(8,128)(2,1)S(1)} collective-permute-done((bf16[67,256]{1,0:T(8,128)(2,1)S(1)}, bf16[67,256]{1,0:T(8,128)(2,1)S(1)}, u32[]{:S(2)}, u32[]{:S(2)}) %collective-permute-start.12) | collective-permute-done | bytes 34336 | tf_op jit(solution)/shard_map/ppermute | solution.py:45
  54.4 1.1 %collective-permute-done.13 = f32[8]{0:T(128)S(1)} collective-permute-done((f32[8]{0:T(128)S(1)}, f32[8]{0:T(128)S(1)}, u32[]{:S(2)}, u32[]{:S(2)}) %collective-permute-start.13) | collective-permute-done | bytes 64 | tf_op jit(solution)/shard_map/ppermute | solution.py:45
  55.5 0.5 copy-done.20
  56.4 2.4 %collective-permute-start.17 = (bf16[1,64,256]{2,1,0:T(8,128)(2,1)S(1)}, bf16[1,64,256]{2,1,0:T(8,128)(2,1)S(1)}, u32[]{:S(2)}, u32[]{:S(2)}) collective-permute-start(bf16[1,64,256]{2,1,0:T(8,128)(2,1)S(1)} %get-tuple-element.34), channel_id=1, source_target_pairs={{0,16},{2,18},{4,20},{6,22},{8,24},{10,26},{12,28},{14,30},{16,0},... | collective-permute-start | bytes 98312 | tf_op jit(solution)/shard_map/ppermute | solution.py:45
  58.8 2.0 %collective-permute-start.16 = (bf16[1,64,256]{2,1,0:T(8,128)(2,1)S(1)}, bf16[1,64,256]{2,1,0:T(8,128)(2,1)S(1)}, u32[]{:S(2)}, u32[]{:S(2)}) collective-permute-start(bf16[1,64,256]{2,1,0:T(8,128)(2,1)S(1)} %get-tuple-element.34), channel_id=1, source_target_pairs={{0,24},{2,26},{4,28},{6,30},{8,16},{10,18},{12,20},{14,22},{16,8},... | collective-permute-start | bytes 98312 | tf_op jit(solution)/shard_map/ppermute | solution.py:45
  60.8 0.8 convert_bitcast_fusion
  61.8 2.6 %collective-permute-done.16 = bf16[1,64,256]{2,1,0:T(8,128)(2,1)S(1)} collective-permute-done((bf16[1,64,256]{2,1,0:T(8,128)(2,1)S(1)}, bf16[1,64,256]{2,1,0:T(8,128)(2,1)S(1)}, u32[]{:S(2)}, u32[]{:S(2)}) %collective-permute-start.16) | collective-permute-done | bytes 32800 | tf_op jit(solution)/shard_map/ppermute | solution.py:45
  64.5 0.7 maximum_bitcast_fusion.1
  65.2 0.5 collective-permute-start.21
  65.7 0.5 collective-permute-start.20
  66.3 2.4 %collective-permute-start.19 = (bf16[4,64,256]{2,1,0:T(8,128)(2,1)}, bf16[4,64,256]{2,1,0:T(8,128)(2,1)}, u32[]{:S(2)}, u32[]{:S(2)}) collective-permute-start(bf16[4,64,256]{2,1,0:T(8,128)(2,1)} %maximum_bitcast_fusion.1), channel_id=1, source_target_pairs={{0,6},{2,4},{4,2},{6,0},{8,14},{10,12},{12,10},{14,8},{16,22},{18,... | collective-permute-start | bytes 393224 | tf_op jit(solution)/shard_map/ppermute | solution.py:45
  69.7 0.8 fusion.58
  71.2 1.5 %collective-permute-done.20 = bf16[4,64,256]{2,1,0:T(8,128)(2,1)} collective-permute-done((bf16[4,64,256]{2,1,0:T(8,128)(2,1)}, bf16[4,64,256]{2,1,0:T(8,128)(2,1)}, u32[]{:S(2)}, u32[]{:S(2)}) %collective-permute-start.20) | collective-permute-done | bytes 131104 | tf_op jit(solution)/shard_map/ppermute | solution.py:45
  72.8 1.2 %select_bitcast_fusion.7 = (bf16[4,1,64,256]{3,2,0,1:T(8,128)(2,1)S(1)}, bf16[4,1,64,256]{3,2,0,1:T(8,128)(2,1)S(1)}, bf16[4,1,64,256]{3,2,0,1:T(8,128)(2,1)S(1)}, bf16[4,1,64,256]{3,2,0,1:T(8,128)(2,1)S(1)}) fusion(bf16[4,64,256]{2,1,0:T(8,128)(2,1)} %collective-permute-done.19, bf16[4,64,256]{2,1,0:T(8,128)(2,1)} %collective-permute-done.20, ...), kind=kLoop, calls=%fused_computation.86 | loop fusion | flops 786432 | bytes 1048579 | tf_op jit(solution)/shard_map/stack | solution.py:128
  74.3 1.2 %select_bitcast_fusion.1 = (bf16[1,1,384,256]{3,2,1,0:T(8,128)(2,1)S(1)}, bf16[1,1,384,256]{3,2,1,0:T(8,128)(2,1)S(1)}) fusion(bf16[1,384,256]{2,1,0:T(8,128)(2,1)} %collective-permute-done.15, bf16[1,384,256]{2,1,0:T(8,128)(2,1)} %get-tuple-element.32, pred[]{:T(512)S(6)} %eq.53), kind=kLoop, calls=%fused_computation.77 | loop fusion | flops 196608 | bytes 786433 | tf_op jit(solution)/shard_map/stack | solution.py:128
  75.8 1.5 %fusion.5 = (f32[256]{0:T(256)S(1)}, f32[768,256]{1,0:T(8,128)}) fusion(bf16[1,2,384,256]{3,2,1,0:T(8,128)(2,1)S(1)} %pad_maximum_fusion.3, bf16[768,256]{1,0:T(8,128)(2,1)S(1)} %bitcast.220, f32[768]{0:T(1024)S(1)} %copy-done.19, bf16[768,1024]{1,0:T(8,128)(2,1)S(1)} %bitcast.192, bf16[1024,256]{1,0:T(8,128)(2,1)S(1)} %bitcast.202), kind=kOutput, calls=%fused_computation.19 | convolution fusion | flops 403832576 | bytes 3674112 | tf_op jit(solution)/shard_map/dot_general | solution.py:161
  77.3 1.7 %fusion.3 = (f32[256]{0:T(256)S(1)}, f32[1024,256]{1,0:T(8,128)}) fusion(bf16[4,4,64,256]{3,2,1,0:T(8,128)(2,1)S(1)} %copy.34, bf16[1024,256]{1,0:T(8,128)(2,1)S(1)} %bitcast.203, f32[1024]{0:T(1024)S(1)} %bitcast.224, bf16[1024,768]{0,1:T(8,128)(2,1)S(1)} %bitcast.190, bf16[768,256]{1,0:T(8,128)(2,1)S(1)} %bitcast.221), kind=kOutput, calls=%fused_computation.13 | convolution fusion | flops 404225792 | bytes 4068352 | tf_op jit(solution)/shard_map/dot_general | solution.py:163
  79.5 1.2 %dynamic-slice_convert_fusion.4 = (bf16[2,2,1,1,64,256]{5,4,3,2,1,0:T(8,128)(2,1)S(1)}, bf16[2,2,1,1,64,256]{5,4,3,2,1,0:T(8,128)(2,1)S(1)}, bf16[2,2,1,1,64,256]{5,4,3,2,1,0:T(8,128)(2,1)S(1)}) fusion(f32[2,2,2,2,64,256]{5,4,3,2,1,0:T(8,128)} %bitcast.214, s32[]{:T(128)S(6)} %select_n.385, s32[]{:T(128)S(6)} %select_n.387, s32[]{:T(128)S(6)} %select_n.393, ...), kind=kLoop, calls=%fused_computation.52 | loop fusion | bytes 786456 | tf_op jit(solution)/shard_map/convert_element_type | solution.py:90
  80.7 1.8 %collective-permute-start.22 = (bf16[259,256]{1,0:T(8,128)(2,1)S(1)}, bf16[259,256]{1,0:T(8,128)(2,1)S(1)}, u32[]{:S(2)}, u32[]{:S(2)}) collective-permute-start(bf16[259,256]{1,0:T(8,128)(2,1)S(1)} %get-tuple-element.83), channel_id=1, source_target_pairs={{0,2},{2,0},{4,6},{6,4},{8,10},{10,8},{12,14},{14,12},{16,18},{18,... | collective-permute-start | bytes 397832 | tf_op jit(solution)/shard_map/ppermute | solution.py:45
  82.5 1.0 collective-permute-start.23
  83.5 0.8 collective-permute-start.24
  84.3 1.7 %fusion.21 = bf16[384,256]{1,0:T(8,128)(2,1)} fusion(f32[2,384,256]{2,1,0:T(8,128)} %bitcast.212, s32[]{:T(128)S(6)} %select_n.413), kind=kLoop, calls=%fused_computation.75 | loop fusion | bytes 393220 | tf_op jit(solution)/shard_map/convert_element_type | solution.py:90
  86.0 1.1 %constant_dynamic-slice_fusion = f32[2,2,1,1,64,256]{5,4,3,2,1,0:T(8,128)S(1)} fusion(f32[2,2,2,2,64,256]{5,4,3,2,1,0:T(8,128)} %bitcast.215, s32[]{:T(128)S(6)} %select_n.380, s32[]{:T(128)S(6)} %select_n.382), kind=kLoop, calls=%fused_computation.160 | loop fusion | bytes 524296 | tf_op jit(solution)/shard_map/jit(dynamic_index_in_dim)/dynamic_slice | solution.py:79
  87.0 0.9 collective-permute-done.23
  87.9 1.5 %collective-permute-done.24 = bf16[259,256]{1,0:T(8,128)(2,1)S(1)} collective-permute-done((bf16[259,256]{1,0:T(8,128)(2,1)S(1)}, bf16[259,256]{1,0:T(8,128)(2,1)S(1)}, u32[]{:S(2)}, u32[]{:S(2)}) %collective-permute-start.24) | collective-permute-done | bytes 132640 | tf_op jit(solution)/shard_map/ppermute | solution.py:45
  89.7 2.7 %collective-permute-start.26 = (bf16[67,256]{1,0:T(8,128)(2,1)S(1)}, bf16[67,256]{1,0:T(8,128)(2,1)S(1)}, u32[]{:S(2)}, u32[]{:S(2)}) collective-permute-start(bf16[67,256]{1,0:T(8,128)(2,1)S(1)} %get-tuple-element.81), channel_id=1, source_target_pairs={{0,16},{2,18},{4,20},{6,22},{8,24},{10,26},{12,28},{14,30},{16,0},... | collective-permute-start | bytes 102920 | tf_op jit(solution)/shard_map/ppermute | solution.py:45
  92.4 1.6 %collective-permute-start.27 = (bf16[67,256]{1,0:T(8,128)(2,1)S(1)}, bf16[67,256]{1,0:T(8,128)(2,1)S(1)}, u32[]{:S(2)}, u32[]{:S(2)}) collective-permute-start(bf16[67,256]{1,0:T(8,128)(2,1)S(1)} %get-tuple-element.82), channel_id=1, source_target_pairs={{0,24},{2,26},{4,28},{6,30},{8,16},{10,18},{12,20},{14,22},{16,8},... | collective-permute-start | bytes 102920 | tf_op jit(solution)/shard_map/ppermute | solution.py:45
  94.1 0.5 collective-permute-done.26
  94.6 3.6 %collective-permute-done.27 = bf16[67,256]{1,0:T(8,128)(2,1)S(1)} collective-permute-done((bf16[67,256]{1,0:T(8,128)(2,1)S(1)}, bf16[67,256]{1,0:T(8,128)(2,1)S(1)}, u32[]{:S(2)}, u32[]{:S(2)}) %collective-permute-start.27) | collective-permute-done | bytes 34336 | tf_op jit(solution)/shard_map/ppermute | solution.py:45
  98.3 1.1 %collective-permute-done.28 = f32[8]{0:T(128)S(1)} collective-permute-done((f32[8]{0:T(128)S(1)}, f32[8]{0:T(128)S(1)}, u32[]{:S(2)}, u32[]{:S(2)}) %collective-permute-start.28) | collective-permute-done | bytes 64 | tf_op jit(solution)/shard_map/ppermute | solution.py:45
  99.8 0.7 fusion.32
  100.5 2.2 %fusion.11 = (f32[1,384,256]{2,1,0:T(8,128)}, f32[1,384,256]{2,1,0:T(8,128)}) fusion(f32[384,256]{1,0:T(8,128)S(1)} %get-tuple-element.16, f32[384,256]{1,0:T(8,128)S(1)} %reshape.294, bf16[384,256]{1,0:T(8,128)(2,1)} %collective-permute-done.29, f32[2,384,256]{2,1,0:T(8,128)} %bitcast.213, s32[]{:T(128)S(6)} %select_n.412, f32[256]{0:T(256)S(1)} %mul.212, ...), kind=kLoop, calls=%fused_computation.30 | loop fusion | flops 1671168 | bytes 3542020 | tf_op jit(solution)/shard_map/broadcast_in_dim | solution.py:226
  (171 shorter events, 8.4 us)
Async XLA Ops:
  0.6 22.5 %copy-start = (f32[64,64]{1,0:T(8,128)S(1)}, f32[64,64]{1,0:T(8,128)}, u32[]{:S(2)}) copy-start(f32[64,64]{1,0:T(8,128)} %param.9) | copy-start | bytes 49156
  1.5 9.0 %collective-permute-start.2 = (bf16[1,64,256]{2,1,0:T(8,128)(2,1)S(1)}, bf16[1,64,256]{2,1,0:T(8,128)(2,1)S(1)}, u32[]{:S(2)}, u32[]{:S(2)}) collective-permute-start(bf16[1,64,256]{2,1,0:T(8,128)(2,1)S(1)} %convert_element_type.273), channel_id=1, source_target_pairs={{0,8},{2,10},{4,12},{6,14},{8,0},{10,2},{12,4},{14,6},{16,24},{18,... | collective-permute-start | bytes 98312 | tf_op jit(solution)/shard_map/ppermute | solution.py:45
  4.5 6.0 %collective-permute-start.1 = (bf16[1,64,256]{2,1,0:T(8,128)(2,1)S(1)}, bf16[1,64,256]{2,1,0:T(8,128)(2,1)S(1)}, u32[]{:S(2)}, u32[]{:S(2)}) collective-permute-start(bf16[1,64,256]{2,1,0:T(8,128)(2,1)S(1)} %convert_element_type.273), channel_id=1, source_target_pairs={{0,16},{2,18},{4,20},{6,22},{8,24},{10,26},{12,28},{14,30},{16,0},... | collective-permute-start | bytes 98312 | tf_op jit(solution)/shard_map/ppermute | solution.py:45
  7.1 5.7 %collective-permute-start = (bf16[1,64,256]{2,1,0:T(8,128)(2,1)S(1)}, bf16[1,64,256]{2,1,0:T(8,128)(2,1)S(1)}, u32[]{:S(2)}, u32[]{:S(2)}) collective-permute-start(bf16[1,64,256]{2,1,0:T(8,128)(2,1)S(1)} %convert_element_type.273), channel_id=1, source_target_pairs={{0,24},{2,26},{4,28},{6,30},{8,16},{10,18},{12,20},{14,22},{16,8},... | collective-permute-start | bytes 98312 | tf_op jit(solution)/shard_map/ppermute | solution.py:45
  8.8 22.3 %collective-permute-start.3 = (bf16[1,384,256]{2,1,0:T(8,128)(2,1)}, bf16[1,384,256]{2,1,0:T(8,128)(2,1)S(1)}, u32[]{:S(2)}, u32[]{:S(2)}) collective-permute-start(bf16[1,384,256]{2,1,0:T(8,128)(2,1)} %convert_element_type.275), channel_id=1, source_target_pairs={{0,1},{1,0},{2,3},{3,2},{4,5},{5,4},{6,7},{7,6},{8,9},{9,8},{10,11... | collective-permute-start | bytes 589832 | tf_op jit(solution)/shard_map/ppermute | solution.py:45
  13.7 6.0 %copy-start.2 = (s32[1,1,12,256,256]{4,3,2,1,0:T(8,128)S(1)}, s32[1,1,12,256,256]{4,3,2,1,0:T(8,128)}, u32[]{:S(2)}) copy-start(s32[1,1,12,256,256]{4,3,2,1,0:T(8,128)} %param.11) | copy-start | bytes 9437188
  13.7 15.5 %collective-permute-start.6 = (bf16[4,64,256]{2,1,0:T(8,128)(2,1)S(1)}, bf16[4,64,256]{2,1,0:T(8,128)(2,1)S(1)}, u32[]{:S(2)}, u32[]{:S(2)}) collective-permute-start(bf16[4,64,256]{2,1,0:T(8,128)(2,1)S(1)} %maximum_bitcast_fusion), channel_id=1, source_target_pairs={{0,2},{2,0},{4,6},{6,4},{8,10},{10,8},{12,14},{14,12},{16,18},{18,... | collective-permute-start | bytes 393224 | tf_op jit(solution)/shard_map/ppermute | solution.py:45
  15.3 13.9 %collective-permute-start.5 = (bf16[4,64,256]{2,1,0:T(8,128)(2,1)S(1)}, bf16[4,64,256]{2,1,0:T(8,128)(2,1)S(1)}, u32[]{:S(2)}, u32[]{:S(2)}) collective-permute-start(bf16[4,64,256]{2,1,0:T(8,128)(2,1)S(1)} %maximum_bitcast_fusion), channel_id=1, source_target_pairs={{0,4},{2,6},{4,0},{6,2},{8,12},{10,14},{12,8},{14,10},{16,20},{18,... | collective-permute-start | bytes 393224 | tf_op jit(solution)/shard_map/ppermute | solution.py:45
  16.8 13.2 %collective-permute-start.4 = (bf16[4,64,256]{2,1,0:T(8,128)(2,1)S(1)}, bf16[4,64,256]{2,1,0:T(8,128)(2,1)}, u32[]{:S(2)}, u32[]{:S(2)}) collective-permute-start(bf16[4,64,256]{2,1,0:T(8,128)(2,1)S(1)} %maximum_bitcast_fusion), channel_id=1, source_target_pairs={{0,6},{2,4},{4,2},{6,0},{8,14},{10,12},{12,10},{14,8},{16,22},{18,... | collective-permute-start | bytes 393224 | tf_op jit(solution)/shard_map/ppermute | solution.py:45
  19.8 1.8 %copy-start.3 = (f32[1,64,256]{2,1,0:T(8,128)S(1)}, f32[1,64,256]{2,1,0:T(8,128)}, u32[]{:S(2)}) copy-start(f32[1,64,256]{2,1,0:T(8,128)} %param.8) | copy-start | bytes 196612
  19.8 1.9 %copy-start.15 = (f32[64,64]{1,0:T(8,128)S(1)}, f32[64,64]{1,0:T(8,128)}, u32[]{:S(2)}) copy-start(f32[64,64]{1,0:T(8,128)} %param.10) | copy-start | bytes 49156
  19.8 3.2 %copy-start.1 = (f32[1,384,256]{2,1,0:T(8,128)S(1)}, f32[1,384,256]{2,1,0:T(8,128)}, u32[]{:S(2)}) copy-start(f32[1,384,256]{2,1,0:T(8,128)} %param.7) | copy-start | bytes 1179652
  21.4 9.8 %copy-start.16 = (f32[1,2,4,128]{3,1,2,0:T(2,128)}, f32[1,2,4,128]{3,1,2,0:T(2,128)S(1)}, u32[]{:S(2)}) copy-start(f32[1,2,4,128]{3,1,2,0:T(2,128)S(1)} %copy.45) | copy-start | bytes 12292
  21.5 11.7 %copy-start.18 = (f32[768]{0:T(1024)}, f32[768]{0:T(1024)S(1)}, u32[]{:S(2)}) copy-start(f32[768]{0:T(1024)S(1)} %mul.186) | copy-start | bytes 9220
  28.3 3.0 %copy-start.4 = (bf16[96,8,4,256]{3,1,2,0:T(8,128)(2,1)}, bf16[96,8,4,256]{3,1,2,0:T(8,128)(2,1)S(1)}, u32[]{:S(2)}) copy-start(bf16[96,8,4,256]{3,1,2,0:T(8,128)(2,1)S(1)} %copy.44) | copy-start | bytes 4718596
  29.2 4.1 %copy-start.6 = (bf16[96,8,4,256]{3,1,2,0:T(8,128)(2,1)}, bf16[96,8,4,256]{3,1,2,0:T(8,128)(2,1)S(1)}, u32[]{:S(2)}) copy-start(bf16[96,8,4,256]{3,1,2,0:T(8,128)(2,1)S(1)} %copy.46) | copy-start | bytes 4718596
  29.2 0.7 copy-start.14
  31.1 1.9 %copy-start.12 = (bf16[4,4,64,256]{3,2,1,0:T(8,128)(2,1)}, bf16[4,4,64,256]{3,2,1,0:T(8,128)(2,1)S(1)}, u32[]{:S(2)}) copy-start(bf16[4,4,64,256]{3,2,1,0:T(8,128)(2,1)S(1)} %copy.30) | copy-start | bytes 1572868
  31.2 1.8 %copy-start.13 = (bf16[1,2,384,256]{3,2,1,0:T(8,128)(2,1)}, bf16[1,2,384,256]{3,2,1,0:T(8,128)(2,1)S(1)}, u32[]{:S(2)}) copy-start(bf16[1,2,384,256]{3,2,1,0:T(8,128)(2,1)S(1)} %pad_maximum_fusion.2) | copy-start | bytes 1179652
  33.3 2.1 %copy-start.22 = (f32[4]{0:T(128)S(1)}, f32[4]{0:T(128)}, u32[]{:S(2)}) copy-start(f32[4]{0:T(128)} %reduce_sum.195) | copy-start | bytes 52
  35.2 25.6 %copy-start.8 = (f32[768,256]{1,0:T(8,128)}, f32[768,256]{1,0:T(8,128)S(1)}, u32[]{:S(2)}) copy-start(f32[768,256]{1,0:T(8,128)S(1)} %get-tuple-element.105) | copy-start | bytes 2359300
  36.7 5.6 %collective-permute-start.7 = (bf16[259,256]{1,0:T(8,128)(2,1)S(1)}, bf16[259,256]{1,0:T(8,128)(2,1)S(1)}, u32[]{:S(2)}, u32[]{:S(2)}) collective-permute-start(bf16[259,256]{1,0:T(8,128)(2,1)S(1)} %get-tuple-element.89), channel_id=1, source_target_pairs={{0,2},{2,0},{4,6},{6,4},{8,10},{10,8},{12,14},{14,12},{16,18},{18,... | collective-permute-start | bytes 397832 | tf_op jit(solution)/shard_map/ppermute | solution.py:45
  38.3 5.2 %collective-permute-start.8 = (bf16[259,256]{1,0:T(8,128)(2,1)S(1)}, bf16[259,256]{1,0:T(8,128)(2,1)S(1)}, u32[]{:S(2)}, u32[]{:S(2)}) collective-permute-start(bf16[259,256]{1,0:T(8,128)(2,1)S(1)} %get-tuple-element.90), channel_id=1, source_target_pairs={{0,4},{2,6},{4,0},{6,2},{8,12},{10,14},{12,8},{14,10},{16,20},{18,... | collective-permute-start | bytes 397832 | tf_op jit(solution)/shard_map/ppermute | solution.py:45
  39.8 5.9 %collective-permute-start.9 = (bf16[259,256]{1,0:T(8,128)(2,1)S(1)}, bf16[259,256]{1,0:T(8,128)(2,1)S(1)}, u32[]{:S(2)}, u32[]{:S(2)}) collective-permute-start(bf16[259,256]{1,0:T(8,128)(2,1)S(1)} %get-tuple-element.91), channel_id=1, source_target_pairs={{0,6},{2,4},{4,2},{6,0},{8,14},{10,12},{12,10},{14,8},{16,22},{18,... | collective-permute-start | bytes 397832 | tf_op jit(solution)/shard_map/ppermute | solution.py:45
  40.3 20.5 %collective-permute-start.14 = (bf16[384,256]{1,0:T(8,128)(2,1)S(1)}, bf16[384,256]{1,0:T(8,128)(2,1)S(1)}, u32[]{:S(2)}, u32[]{:S(2)}) collective-permute-start(bf16[384,256]{1,0:T(8,128)(2,1)S(1)} %fusion.20), channel_id=1, source_target_pairs={{0,1},{1,0},{2,3},{3,2},{4,5},{5,4},{6,7},{7,6},{8,9},{9,8},{10,11... | collective-permute-start | bytes 589832 | tf_op jit(solution)/shard_map/ppermute | solution.py:45
  45.9 4.5 %collective-permute-start.10 = (bf16[67,256]{1,0:T(8,128)(2,1)S(1)}, bf16[67,256]{1,0:T(8,128)(2,1)S(1)}, u32[]{:S(2)}, u32[]{:S(2)}) collective-permute-start(bf16[67,256]{1,0:T(8,128)(2,1)S(1)} %get-tuple-element.86), channel_id=1, source_target_pairs={{0,8},{2,10},{4,12},{6,14},{8,0},{10,2},{12,4},{14,6},{16,24},{18,... | collective-permute-start | bytes 102920 | tf_op jit(solution)/shard_map/ppermute | solution.py:45
  45.9 5.3 %collective-permute-start.11 = (bf16[67,256]{1,0:T(8,128)(2,1)S(1)}, bf16[67,256]{1,0:T(8,128)(2,1)S(1)}, u32[]{:S(2)}, u32[]{:S(2)}) collective-permute-start(bf16[67,256]{1,0:T(8,128)(2,1)S(1)} %get-tuple-element.87), channel_id=1, source_target_pairs={{0,16},{2,18},{4,20},{6,22},{8,24},{10,26},{12,28},{14,30},{16,0},... | collective-permute-start | bytes 102920 | tf_op jit(solution)/shard_map/ppermute | solution.py:45
  48.5 5.8 %collective-permute-start.12 = (bf16[67,256]{1,0:T(8,128)(2,1)S(1)}, bf16[67,256]{1,0:T(8,128)(2,1)S(1)}, u32[]{:S(2)}, u32[]{:S(2)}) collective-permute-start(bf16[67,256]{1,0:T(8,128)(2,1)S(1)} %get-tuple-element.88), channel_id=1, source_target_pairs={{0,24},{2,26},{4,28},{6,30},{8,16},{10,18},{12,20},{14,22},{16,8},... | collective-permute-start | bytes 102920 | tf_op jit(solution)/shard_map/ppermute | solution.py:45
  54.3 1.2 %collective-permute-start.13 = (f32[8]{0:T(128)S(1)}, f32[8]{0:T(128)S(1)}, u32[]{:S(2)}, u32[]{:S(2)}) collective-permute-start(f32[8]{0:T(128)S(1)} %fusion.47), channel_id=1, source_target_pairs={{0,1},{1,0},{2,3},{3,2},{4,5},{5,4},{6,7},{7,6},{8,9},{9,8},{10,11... | collective-permute-start | bytes 104 | tf_op jit(solution)/shard_map/ppermute | solution.py:45
  55.5 0.5 copy-start.20
  56.3 5.2 %collective-permute-start.18 = (bf16[1,64,256]{2,1,0:T(8,128)(2,1)S(1)}, bf16[1,64,256]{2,1,0:T(8,128)(2,1)S(1)}, u32[]{:S(2)}, u32[]{:S(2)}) collective-permute-start(bf16[1,64,256]{2,1,0:T(8,128)(2,1)S(1)} %get-tuple-element.34), channel_id=1, source_target_pairs={{0,8},{2,10},{4,12},{6,14},{8,0},{10,2},{12,4},{14,6},{16,24},{18,... | collective-permute-start | bytes 98312 | tf_op jit(solution)/shard_map/ppermute | solution.py:45
  56.4 5.5 %collective-permute-start.17 = (bf16[1,64,256]{2,1,0:T(8,128)(2,1)S(1)}, bf16[1,64,256]{2,1,0:T(8,128)(2,1)S(1)}, u32[]{:S(2)}, u32[]{:S(2)}) collective-permute-start(bf16[1,64,256]{2,1,0:T(8,128)(2,1)S(1)} %get-tuple-element.34), channel_id=1, source_target_pairs={{0,16},{2,18},{4,20},{6,22},{8,24},{10,26},{12,28},{14,30},{16,0},... | collective-permute-start | bytes 98312 | tf_op jit(solution)/shard_map/ppermute | solution.py:45
  58.8 5.7 %collective-permute-start.16 = (bf16[1,64,256]{2,1,0:T(8,128)(2,1)S(1)}, bf16[1,64,256]{2,1,0:T(8,128)(2,1)S(1)}, u32[]{:S(2)}, u32[]{:S(2)}) collective-permute-start(bf16[1,64,256]{2,1,0:T(8,128)(2,1)S(1)} %get-tuple-element.34), channel_id=1, source_target_pairs={{0,24},{2,26},{4,28},{6,30},{8,16},{10,18},{12,20},{14,22},{16,8},... | collective-permute-start | bytes 98312 | tf_op jit(solution)/shard_map/ppermute | solution.py:45
  60.8 8.3 %copy-start.10 = (bf16[384,256]{1,0:T(8,128)(2,1)}, bf16[384,256]{1,0:T(8,128)(2,1)S(1)}, u32[]{:S(2)}) copy-start(bf16[384,256]{1,0:T(8,128)(2,1)S(1)} %collective-permute-done.14) | copy-start | bytes 589828
  61.5 12.7 %collective-permute-start.15 = (bf16[1,384,256]{2,1,0:T(8,128)(2,1)}, bf16[1,384,256]{2,1,0:T(8,128)(2,1)}, u32[]{:S(2)}, u32[]{:S(2)}) collective-permute-start(bf16[1,384,256]{2,1,0:T(8,128)(2,1)} %get-tuple-element.32), channel_id=1, source_target_pairs={{0,1},{1,0},{2,3},{3,2},{4,5},{5,4},{6,7},{7,6},{8,9},{9,8},{10,11... | collective-permute-start | bytes 589832 | tf_op jit(solution)/shard_map/ppermute | solution.py:45
  65.2 6.0 %collective-permute-start.21 = (bf16[4,64,256]{2,1,0:T(8,128)(2,1)}, bf16[4,64,256]{2,1,0:T(8,128)(2,1)}, u32[]{:S(2)}, u32[]{:S(2)}) collective-permute-start(bf16[4,64,256]{2,1,0:T(8,128)(2,1)} %maximum_bitcast_fusion.1), channel_id=1, source_target_pairs={{0,2},{2,0},{4,6},{6,4},{8,10},{10,8},{12,14},{14,12},{16,18},{18,... | collective-permute-start | bytes 393224 | tf_op jit(solution)/shard_map/ppermute | solution.py:45
  65.7 7.0 %collective-permute-start.20 = (bf16[4,64,256]{2,1,0:T(8,128)(2,1)}, bf16[4,64,256]{2,1,0:T(8,128)(2,1)}, u32[]{:S(2)}, u32[]{:S(2)}) collective-permute-start(bf16[4,64,256]{2,1,0:T(8,128)(2,1)} %maximum_bitcast_fusion.1), channel_id=1, source_target_pairs={{0,4},{2,6},{4,0},{6,2},{8,12},{10,14},{12,8},{14,10},{16,20},{18,... | collective-permute-start | bytes 393224 | tf_op jit(solution)/shard_map/ppermute | solution.py:45
  66.3 6.5 %collective-permute-start.19 = (bf16[4,64,256]{2,1,0:T(8,128)(2,1)}, bf16[4,64,256]{2,1,0:T(8,128)(2,1)}, u32[]{:S(2)}, u32[]{:S(2)}) collective-permute-start(bf16[4,64,256]{2,1,0:T(8,128)(2,1)} %maximum_bitcast_fusion.1), channel_id=1, source_target_pairs={{0,6},{2,4},{4,2},{6,0},{8,14},{10,12},{12,10},{14,8},{16,22},{18,... | collective-permute-start | bytes 393224 | tf_op jit(solution)/shard_map/ppermute | solution.py:45
  74.2 1.6 %copy-start.7 = (bf16[96,8,4,256]{3,1,2,0:T(8,128)(2,1)S(1)}, bf16[96,8,4,256]{3,1,2,0:T(8,128)(2,1)}, u32[]{:S(2)}) copy-start(bf16[96,8,4,256]{3,1,2,0:T(8,128)(2,1)} %copy-done.6) | copy-start | bytes 4718596
  74.2 1.6 %copy-start.19 = (f32[768]{0:T(1024)S(1)}, f32[768]{0:T(1024)}, u32[]{:S(2)}) copy-start(f32[768]{0:T(1024)} %copy-done.18) | copy-start | bytes 9220
  75.8 1.5 %copy-start.5 = (bf16[96,8,4,256]{3,1,2,0:T(8,128)(2,1)S(1)}, bf16[96,8,4,256]{3,1,2,0:T(8,128)(2,1)}, u32[]{:S(2)}) copy-start(bf16[96,8,4,256]{3,1,2,0:T(8,128)(2,1)} %copy-done.4) | copy-start | bytes 4718596
  75.8 1.5 %copy-start.17 = (f32[1,2,4,128]{3,1,2,0:T(2,128)S(1)}, f32[1,2,4,128]{3,1,2,0:T(2,128)}, u32[]{:S(2)}) copy-start(f32[1,2,4,128]{3,1,2,0:T(2,128)} %copy-done.16) | copy-start | bytes 12292
  80.7 6.3 %collective-permute-start.22 = (bf16[259,256]{1,0:T(8,128)(2,1)S(1)}, bf16[259,256]{1,0:T(8,128)(2,1)S(1)}, u32[]{:S(2)}, u32[]{:S(2)}) collective-permute-start(bf16[259,256]{1,0:T(8,128)(2,1)S(1)} %get-tuple-element.83), channel_id=1, source_target_pairs={{0,2},{2,0},{4,6},{6,4},{8,10},{10,8},{12,14},{14,12},{16,18},{18,... | collective-permute-start | bytes 397832 | tf_op jit(solution)/shard_map/ppermute | solution.py:45
  82.5 5.4 %collective-permute-start.23 = (bf16[259,256]{1,0:T(8,128)(2,1)S(1)}, bf16[259,256]{1,0:T(8,128)(2,1)S(1)}, u32[]{:S(2)}, u32[]{:S(2)}) collective-permute-start(bf16[259,256]{1,0:T(8,128)(2,1)S(1)} %get-tuple-element.84), channel_id=1, source_target_pairs={{0,4},{2,6},{4,0},{6,2},{8,12},{10,14},{12,8},{14,10},{16,20},{18,... | collective-permute-start | bytes 397832 | tf_op jit(solution)/shard_map/ppermute | solution.py:45
  83.5 5.9 %collective-permute-start.24 = (bf16[259,256]{1,0:T(8,128)(2,1)S(1)}, bf16[259,256]{1,0:T(8,128)(2,1)S(1)}, u32[]{:S(2)}, u32[]{:S(2)}) collective-permute-start(bf16[259,256]{1,0:T(8,128)(2,1)S(1)} %get-tuple-element.85), channel_id=1, source_target_pairs={{0,6},{2,4},{4,2},{6,0},{8,14},{10,12},{12,10},{14,8},{16,22},{18,... | collective-permute-start | bytes 397832 | tf_op jit(solution)/shard_map/ppermute | solution.py:45
  84.3 15.1 %copy-start.21 = (f32[8]{0:T(128)S(1)}, f32[8]{0:T(128)}, u32[]{:S(2)}) copy-start(f32[8]{0:T(128)} %copy-done.20) | copy-start | bytes 100
  86.0 14.5 %copy-start.9 = (f32[768,256]{1,0:T(8,128)S(1)}, f32[768,256]{1,0:T(8,128)}, u32[]{:S(2)}) copy-start(f32[768,256]{1,0:T(8,128)} %copy-done.8) | copy-start | bytes 2359300
  86.0 14.5 %copy-start.11 = (bf16[384,256]{1,0:T(8,128)(2,1)S(1)}, bf16[384,256]{1,0:T(8,128)(2,1)}, u32[]{:S(2)}) copy-start(bf16[384,256]{1,0:T(8,128)(2,1)} %copy-done.10) | copy-start | bytes 589828
  86.0 14.5 %collective-permute-start.29 = (bf16[384,256]{1,0:T(8,128)(2,1)}, bf16[384,256]{1,0:T(8,128)(2,1)}, u32[]{:S(2)}, u32[]{:S(2)}) collective-permute-start(bf16[384,256]{1,0:T(8,128)(2,1)} %fusion.21), channel_id=1, source_target_pairs={{0,1},{1,0},{2,3},{3,2},{4,5},{5,4},{6,7},{7,6},{8,9},{9,8},{10,11... | collective-permute-start | bytes 589832 | tf_op jit(solution)/shard_map/ppermute | solution.py:45
  89.6 4.5 %collective-permute-start.25 = (bf16[67,256]{1,0:T(8,128)(2,1)S(1)}, bf16[67,256]{1,0:T(8,128)(2,1)S(1)}, u32[]{:S(2)}, u32[]{:S(2)}) collective-permute-start(bf16[67,256]{1,0:T(8,128)(2,1)S(1)} %get-tuple-element.80), channel_id=1, source_target_pairs={{0,8},{2,10},{4,12},{6,14},{8,0},{10,2},{12,4},{14,6},{16,24},{18,... | collective-permute-start | bytes 102920 | tf_op jit(solution)/shard_map/ppermute | solution.py:45
  89.7 4.9 %collective-permute-start.26 = (bf16[67,256]{1,0:T(8,128)(2,1)S(1)}, bf16[67,256]{1,0:T(8,128)(2,1)S(1)}, u32[]{:S(2)}, u32[]{:S(2)}) collective-permute-start(bf16[67,256]{1,0:T(8,128)(2,1)S(1)} %get-tuple-element.81), channel_id=1, source_target_pairs={{0,16},{2,18},{4,20},{6,22},{8,24},{10,26},{12,28},{14,30},{16,0},... | collective-permute-start | bytes 102920 | tf_op jit(solution)/shard_map/ppermute | solution.py:45
  92.4 5.8 %collective-permute-start.27 = (bf16[67,256]{1,0:T(8,128)(2,1)S(1)}, bf16[67,256]{1,0:T(8,128)(2,1)S(1)}, u32[]{:S(2)}, u32[]{:S(2)}) collective-permute-start(bf16[67,256]{1,0:T(8,128)(2,1)S(1)} %get-tuple-element.82), channel_id=1, source_target_pairs={{0,24},{2,26},{4,28},{6,30},{8,16},{10,18},{12,20},{14,22},{16,8},... | collective-permute-start | bytes 102920 | tf_op jit(solution)/shard_map/ppermute | solution.py:45
  98.2 1.2 %collective-permute-start.28 = (f32[8]{0:T(128)S(1)}, f32[8]{0:T(128)S(1)}, u32[]{:S(2)}, u32[]{:S(2)}) collective-permute-start(f32[8]{0:T(128)S(1)} %fusion.46), channel_id=1, source_target_pairs={{0,1},{1,0},{2,3},{3,2},{4,5},{5,4},{6,7},{7,6},{8,9},{9,8},{10,11... | collective-permute-start | bytes 104 | tf_op jit(solution)/shard_map/ppermute | solution.py:45

commit v20 on v19

--- a/solution.py
+++ b/solution.py
@@ -110,22 +110,20 @@
 def double_gather(piece, axis, hold=None):
     size, bits = bit_count(axis)
     me = lax.axis_index(axis)
-    order = list(range(bits))[::-1]
-    groups = [order[:1]] if bits % 2 else []
-    groups += [order[i : i + 2] for i in range(bits % 2, bits, 2)]
+    groups = [list(range(bits))[i : i + 2] for i in range(0, bits, 2)]
     buf = piece[None]
     kept = None
     for group in groups:
-        masks = [sum(1 << group[-1 - j] for j in range(len(group)) if (k >> j) & 1) for k in range(1 << len(group))]
+        masks = [sum(1 << group[j] for j in range(len(group)) if (k >> j) & 1) for k in range(1 << len(group))]
         pieces = [buf] + [swap_with(buf, axis, size, None, mask) for mask in masks[1:]]
-        digit = sum(((me >> group[-1 - j]) & 1) << j for j in range(len(group)))
+        digit = sum(((me >> group[j]) & 1) << j for j in range(len(group)))
         ordered = []
         for place in range(len(masks)):
             pick = pieces[place]
             for held in range(1, len(masks)):
                 pick = jnp.where(digit == held, pieces[place ^ held], pick)
             ordered.append(pick)
-        buf = jnp.stack(ordered, axis=1).reshape((-1,) + piece.shape)
+        buf = jnp.stack(ordered, axis=0).reshape((-1,) + piece.shape)
         if hold is not None and kept is None:
             buf, kept = lax.optimization_barrier((buf, hold))
     result = buf.reshape((size * piece.shape[0],) + piece.shape[1:])

time: 103 us -> 105 us (1.019)
  waiting for transfers between devices: 23.7 us -> 26.1 us
    ppermute x30, waiting for transfers between devices: 23.7 us -> 26.1 us  [swap_with(): return lax.ppermute(value, axis, pairs)]
  transfers between devices with their start and end apart: 30 -> 30, of which waited for: 15 -> 15; matrix products, arithmetic and copies ran while one was open for 27% -> 26% of each run, Pallas kernels for 0% -> 0%
where the time goes in v20:
time: 105 us
  starting transfers between devices  33.1 us (32%)
  waiting for transfers between devices  26.1 us (25%)
  other arithmetic  18.8 us (18%)
  local copies, waits for them, and re-layouts  12.9 us (12%)
  matrix products  11.6 us (11%)
  between operations  2.03 us (2%)
    ppermute x30, starting transfers between devices, swap_with(): return lax.ppermute(value, axis, pairs)  33.1 us
    ppermute x30, waiting for transfers between devices, swap_with(): return lax.ppermute(value, axis, pairs)  26.1 us
    another operation x10, other arithmetic, double_gather(): buf = jnp.stack(ordered, axis=0).reshape((-1,) + piece.shape)  4.7 us
    convert_element_type x6, local copies, waits for them, and re-layouts, halve_sum(): send = block_of(digit ^ k).astype(stage_type)  4.1 us
    dot_general x2, matrix products, cross_parts(): to_items = jnp.dot(counts_t, user_range, preferred_element_type=jnp.float32)  3.49 us
    dot_general x2, matrix products, cross_parts(): jnp.dot(counts_bf, item_range, preferred_element_type=jnp.float32)  3.36 us
    broadcast_in_dim x2, other arithmetic, per_device(): return (sol_user[None], sol_item[None], res_user[None], res_item[None])  2.93 us
    dot_general x1, matrix products, build_counts(): jnp.einsum('trc,tij->cjri', place, tiles_bf, preferred_element_type=jnp.b...  2.71 us
  transfers between devices with their start and end apart: 30, of which 15 were waited for; matrix products, arithmetic and copies ran while one was open for 26% of the time, Pallas kernels for 0%

profile of v20, /device:TPU:0, one launch (start us, length us, event | category | flops | bytes accessed | tf_op | source)
XLA Modules:
  0.0 104.6 jit_solution(12930632144976573953)
XLA Ops:
  0.6 0.9 convert_element_type.273
  1.5 2.9 %collective-permute-start.2 = (bf16[1,64,256]{2,1,0:T(8,128)(2,1)S(1)}, bf16[1,64,256]{2,1,0:T(8,128)(2,1)S(1)}, u32[]{:S(2)}, u32[]{:S(2)}) collective-permute-start(bf16[1,64,256]{2,1,0:T(8,128)(2,1)S(1)} %convert_element_type.273), channel_id=1, source_target_pairs={{0,2},{2,0},{4,6},{6,4},{8,10},{10,8},{12,14},{14,12},{16,18},{18,... | collective-permute-start | bytes 98312 | tf_op jit(solution)/shard_map/ppermute | solution.py:45
  4.4 1.5 %collective-permute-start.1 = (bf16[1,64,256]{2,1,0:T(8,128)(2,1)S(1)}, bf16[1,64,256]{2,1,0:T(8,128)(2,1)S(1)}, u32[]{:S(2)}, u32[]{:S(2)}) collective-permute-start(bf16[1,64,256]{2,1,0:T(8,128)(2,1)S(1)} %convert_element_type.273), channel_id=1, source_target_pairs={{0,4},{2,6},{4,0},{6,2},{8,12},{10,14},{12,8},{14,10},{16,20},{18,... | collective-permute-start | bytes 98312 | tf_op jit(solution)/shard_map/ppermute | solution.py:45
  6.0 1.7 %convert_element_type.275 = bf16[1,384,256]{2,1,0:T(8,128)(2,1)} convert(f32[1,384,256]{2,1,0:T(8,128)} %param.7) | non-fusion elementwise | flops 98304 | bytes 589824 | tf_op jit(solution)/shard_map/convert_element_type | solution.py:166
  8.3 0.8 slice_bitcast_fusion.1
  9.4 1.4 %collective-permute-done = bf16[1,64,256]{2,1,0:T(8,128)(2,1)S(1)} collective-permute-done((bf16[1,64,256]{2,1,0:T(8,128)(2,1)S(1)}, bf16[1,64,256]{2,1,0:T(8,128)(2,1)S(1)}, u32[]{:S(2)}, u32[]{:S(2)}) %collective-permute-start) | collective-permute-done | bytes 32800 | tf_op jit(solution)/shard_map/ppermute | solution.py:45
  10.8 0.9 select_bitcast_fusion.19
  11.7 1.6 %collective-permute-start.6 = (bf16[4,64,256]{2,1,0:T(8,128)(2,1)S(1)}, bf16[4,64,256]{2,1,0:T(8,128)(2,1)S(1)}, u32[]{:S(2)}, u32[]{:S(2)}) collective-permute-start(bf16[4,64,256]{2,1,0:T(8,128)(2,1)S(1)} %maximum_bitcast_fusion), channel_id=1, source_target_pairs={{0,8},{2,10},{4,12},{6,14},{8,0},{10,2},{12,4},{14,6},{16,24},{18,... | collective-permute-start | bytes 393224 | tf_op jit(solution)/shard_map/ppermute | solution.py:45
  13.3 2.6 %collective-permute-start.5 = (bf16[4,64,256]{2,1,0:T(8,128)(2,1)S(1)}, bf16[4,64,256]{2,1,0:T(8,128)(2,1)S(1)}, u32[]{:S(2)}, u32[]{:S(2)}) collective-permute-start(bf16[4,64,256]{2,1,0:T(8,128)(2,1)S(1)} %maximum_bitcast_fusion), channel_id=1, source_target_pairs={{0,16},{2,18},{4,20},{6,22},{8,24},{10,26},{12,28},{14,30},{16,0},... | collective-permute-start | bytes 393224 | tf_op jit(solution)/shard_map/ppermute | solution.py:45
  16.1 2.5 %convert_reduce_fusion.1 = (f32[12,256]{1,0:T(8,128)S(1)}, f32[12,256]{1,0:T(8,128)S(1)}) fusion(s32[12,256,256]{2,1,0:T(8,128)} %bitcast.189), kind=kLoop, calls=%fused_computation.1 | loop fusion | flops 3139584 | bytes 3170304 | tf_op jit(solution)/shard_map/reduce_sum | solution.py:152
  18.7 1.5 %convert_bitcast_fusion.2 = bf16[12,256,256,1]{2,1,0,3:T(8,128)(2,1)} fusion(s32[12,256,256]{2,1,0:T(8,128)S(1)} %bitcast.190), kind=kLoop, calls=%fused_computation.198 | loop fusion | flops 786432 | bytes 4718592 | tf_op jit(solution)/shard_map/convert_element_type | solution.py:144
  21.2 0.7 reduce_sum.195
  22.0 0.8 fusion.56
  23.0 2.7 %fusion = bf16[256,256,3,4]{1,3,2,0:T(4,128)(2,1)S(1)} fusion(bf16[12,256,256,1]{2,1,0,3:T(8,128)(2,1)} %convert_bitcast_fusion.2, pred[12,4]{0,1:T(4,128)(4,1)S(1)} %copy.32, pred[12,3]{0,1:T(4,128)(4,1)S(1)} %fusion.45), kind=kOutput, calls=%fused_computation.2 | convolution fusion | flops 18874512 | bytes 3145812 | tf_op jit(solution)/shard_map/trc,tij->cjri/dot_general | solution.py:148
  26.2 0.5 copy.34
  26.8 0.4 copy.47
  27.1 0.5 copy.37
  27.7 0.3 copy.49
  28.1 0.7 copy-done.14
  28.8 1.0 select_bitcast_fusion.11
  30.1 1.8 %fusion.2 = (f32[256]{0:T(256)S(1)}, f32[1024,256]{1,0:T(8,128)}) fusion(bf16[4,4,64,256]{3,2,1,0:T(8,128)(2,1)S(1)} %pad_maximum_fusion, bf16[1024,256]{1,0:T(8,128)(2,1)S(1)} %bitcast.210, f32[1024]{0:T(1024)S(1)} %bitcast.229, bf16[1024,768]{0,1:T(8,128)(2,1)S(1)} %bitcast.195, bf16[768,256]{1,0:T(8,128)(2,1)S(1)} %bitcast.224), kind=kOutput, calls=%fused_computation.12 | convolution fusion | flops 404225792 | bytes 4068352 | tf_op jit(solution)/shard_map/dot_general | solution.py:161
  32.0 1.9 %fusion.4 = (f32[256]{0:T(256)S(1)}, f32[768,256]{1,0:T(8,128)S(1)}) fusion(bf16[2,1,384,256]{3,2,1,0:T(8,128)(2,1)} %copy-done.13, bf16[768,256]{1,0:T(8,128)(2,1)} %bitcast.225, f32[768]{0:T(1024)S(1)} %mul.186, bf16[768,1024]{1,0:T(8,128)(2,1)S(1)} %bitcast.197, bf16[1024,256]{1,0:T(8,128)(2,1)} %bitcast.211), kind=kOutput, calls=%fused_computation.18 | convolution fusion | flops 403832576 | bytes 3674112 | tf_op jit(solution)/shard_map/dot_general | solution.py:159
  34.3 1.2 %dynamic-slice_convert_fusion.7 = (bf16[2,2,1,1,64,256]{5,4,3,2,1,0:T(8,128)(2,1)S(1)}, bf16[2,2,1,1,64,256]{5,4,3,2,1,0:T(8,128)(2,1)S(1)}, bf16[2,2,1,1,64,256]{5,4,3,2,1,0:T(8,128)(2,1)S(1)}) fusion(f32[2,2,2,2,64,256]{5,4,3,2,1,0:T(8,128)} %bitcast.222, s32[]{:T(128)S(6)} %select_n.385, s32[]{:T(128)S(6)} %select_n.387, s32[]{:T(128)S(6)} %select_n.393, ...), kind=kLoop, calls=%fused_computation.55 | loop fusion | bytes 786456 | tf_op jit(solution)/shard_map/convert_element_type | solution.py:90
  35.5 0.6 collective-permute-start.7
  36.1 1.5 %collective-permute-start.8 = (bf16[259,256]{1,0:T(8,128)(2,1)S(1)}, bf16[259,256]{1,0:T(8,128)(2,1)S(1)}, u32[]{:S(2)}, u32[]{:S(2)}) collective-permute-start(bf16[259,256]{1,0:T(8,128)(2,1)S(1)} %get-tuple-element.90), channel_id=1, source_target_pairs={{0,4},{2,6},{4,0},{6,2},{8,12},{10,14},{12,8},{14,10},{16,20},{18,... | collective-permute-start | bytes 397832 | tf_op jit(solution)/shard_map/ppermute | solution.py:45
  37.6 1.4 %collective-permute-start.9 = (bf16[259,256]{1,0:T(8,128)(2,1)S(1)}, bf16[259,256]{1,0:T(8,128)(2,1)S(1)}, u32[]{:S(2)}, u32[]{:S(2)}) collective-permute-start(bf16[259,256]{1,0:T(8,128)(2,1)S(1)} %get-tuple-element.91), channel_id=1, source_target_pairs={{0,6},{2,4},{4,2},{6,0},{8,14},{10,12},{12,10},{14,8},{16,22},{18,... | collective-permute-start | bytes 397832 | tf_op jit(solution)/shard_map/ppermute | solution.py:45
  39.1 1.0 constant_dynamic-slice_fusion.1
  40.1 1.6 %collective-permute-done.7 = bf16[259,256]{1,0:T(8,128)(2,1)S(1)} collective-permute-done((bf16[259,256]{1,0:T(8,128)(2,1)S(1)}, bf16[259,256]{1,0:T(8,128)(2,1)S(1)}, u32[]{:S(2)}, u32[]{:S(2)}) %collective-permute-start.7) | collective-permute-done | bytes 132640 | tf_op jit(solution)/shard_map/ppermute | solution.py:45
  41.8 2.3 %collective-permute-done.8 = bf16[259,256]{1,0:T(8,128)(2,1)S(1)} collective-permute-done((bf16[259,256]{1,0:T(8,128)(2,1)S(1)}, bf16[259,256]{1,0:T(8,128)(2,1)S(1)}, u32[]{:S(2)}, u32[]{:S(2)}) %collective-permute-start.8) | collective-permute-done | bytes 132640 | tf_op jit(solution)/shard_map/ppermute | solution.py:45
  44.2 0.7 collective-permute-start.10
  45.0 3.5 %collective-permute-start.11 = (bf16[67,256]{1,0:T(8,128)(2,1)S(1)}, bf16[67,256]{1,0:T(8,128)(2,1)S(1)}, u32[]{:S(2)}, u32[]{:S(2)}) collective-permute-start(bf16[67,256]{1,0:T(8,128)(2,1)S(1)} %get-tuple-element.87), channel_id=1, source_target_pairs={{0,16},{2,18},{4,20},{6,22},{8,24},{10,26},{12,28},{14,30},{16,0},... | collective-permute-start | bytes 102920 | tf_op jit(solution)/shard_map/ppermute | solution.py:45
  48.7 2.5 %collective-permute-done.11 = bf16[67,256]{1,0:T(8,128)(2,1)S(1)} collective-permute-done((bf16[67,256]{1,0:T(8,128)(2,1)S(1)}, bf16[67,256]{1,0:T(8,128)(2,1)S(1)}, u32[]{:S(2)}, u32[]{:S(2)}) %collective-permute-start.11) | collective-permute-done | bytes 34336 | tf_op jit(solution)/shard_map/ppermute | solution.py:45
  51.2 3.0 %collective-permute-done.12 = bf16[67,256]{1,0:T(8,128)(2,1)S(1)} collective-permute-done((bf16[67,256]{1,0:T(8,128)(2,1)S(1)}, bf16[67,256]{1,0:T(8,128)(2,1)S(1)}, u32[]{:S(2)}, u32[]{:S(2)}) %collective-permute-start.12) | collective-permute-done | bytes 34336 | tf_op jit(solution)/shard_map/ppermute | solution.py:45
  54.3 1.1 %collective-permute-done.13 = f32[8]{0:T(128)S(1)} collective-permute-done((f32[8]{0:T(128)S(1)}, f32[8]{0:T(128)S(1)}, u32[]{:S(2)}, u32[]{:S(2)}) %collective-permute-start.13) | collective-permute-done | bytes 64 | tf_op jit(solution)/shard_map/ppermute | solution.py:45
  55.5 0.5 copy-done.20
  56.3 1.4 %collective-permute-start.18 = (bf16[1,64,256]{2,1,0:T(8,128)(2,1)S(1)}, bf16[1,64,256]{2,1,0:T(8,128)(2,1)S(1)}, u32[]{:S(2)}, u32[]{:S(2)}) collective-permute-start(bf16[1,64,256]{2,1,0:T(8,128)(2,1)S(1)} %get-tuple-element.34), channel_id=1, source_target_pairs={{0,2},{2,0},{4,6},{6,4},{8,10},{10,8},{12,14},{14,12},{16,18},{18,... | collective-permute-start | bytes 98312 | tf_op jit(solution)/shard_map/ppermute | solution.py:45
  57.7 0.6 collective-permute-start.17
  58.2 1.6 %collective-permute-start.16 = (bf16[1,64,256]{2,1,0:T(8,128)(2,1)S(1)}, bf16[1,64,256]{2,1,0:T(8,128)(2,1)S(1)}, u32[]{:S(2)}, u32[]{:S(2)}) collective-permute-start(bf16[1,64,256]{2,1,0:T(8,128)(2,1)S(1)} %get-tuple-element.34), channel_id=1, source_target_pairs={{0,6},{2,4},{4,2},{6,0},{8,14},{10,12},{12,10},{14,8},{16,22},{18,... | collective-permute-start | bytes 98312 | tf_op jit(solution)/shard_map/ppermute | solution.py:45
  59.8 0.8 convert_bitcast_fusion
  60.6 1.3 %collective-permute-done.17 = bf16[1,64,256]{2,1,0:T(8,128)(2,1)S(1)} collective-permute-done((bf16[1,64,256]{2,1,0:T(8,128)(2,1)S(1)}, bf16[1,64,256]{2,1,0:T(8,128)(2,1)S(1)}, u32[]{:S(2)}, u32[]{:S(2)}) %collective-permute-start.17) | collective-permute-done | bytes 32800 | tf_op jit(solution)/shard_map/ppermute | solution.py:45
  61.9 1.1 %collective-permute-done.16 = bf16[1,64,256]{2,1,0:T(8,128)(2,1)S(1)} collective-permute-done((bf16[1,64,256]{2,1,0:T(8,128)(2,1)S(1)}, bf16[1,64,256]{2,1,0:T(8,128)(2,1)S(1)}, u32[]{:S(2)}, u32[]{:S(2)}) %collective-permute-start.16) | collective-permute-done | bytes 32800 | tf_op jit(solution)/shard_map/ppermute | solution.py:45
  63.1 0.7 maximum_bitcast_fusion.1
  63.8 1.0 collective-permute-start.20
  64.7 3.4 %collective-permute-start.19 = (bf16[4,64,256]{2,1,0:T(8,128)(2,1)}, bf16[4,64,256]{2,1,0:T(8,128)(2,1)}, u32[]{:S(2)}, u32[]{:S(2)}) collective-permute-start(bf16[4,64,256]{2,1,0:T(8,128)(2,1)} %maximum_bitcast_fusion.1), channel_id=1, source_target_pairs={{0,24},{2,26},{4,28},{6,30},{8,16},{10,18},{12,20},{14,22},{16,8},... | collective-permute-start | bytes 393224 | tf_op jit(solution)/shard_map/ppermute | solution.py:45
  69.2 0.8 fusion.58
  70.9 5.2 %collective-permute-done.20 = bf16[4,64,256]{2,1,0:T(8,128)(2,1)} collective-permute-done((bf16[4,64,256]{2,1,0:T(8,128)(2,1)}, bf16[4,64,256]{2,1,0:T(8,128)(2,1)}, u32[]{:S(2)}, u32[]{:S(2)}) %collective-permute-start.20) | collective-permute-done | bytes 131104 | tf_op jit(solution)/shard_map/ppermute | solution.py:45
  76.1 1.2 %select_bitcast_fusion.7 = (bf16[1,4,64,256]{3,2,1,0:T(8,128)(2,1)S(1)}, bf16[1,4,64,256]{3,2,1,0:T(8,128)(2,1)S(1)}, bf16[1,4,64,256]{3,2,1,0:T(8,128)(2,1)S(1)}, bf16[1,4,64,256]{3,2,1,0:T(8,128)(2,1)S(1)}) fusion(bf16[4,64,256]{2,1,0:T(8,128)(2,1)} %collective-permute-done.19, bf16[4,64,256]{2,1,0:T(8,128)(2,1)} %collective-permute-done.20, ...), kind=kLoop, calls=%fused_computation.86 | loop fusion | flops 786432 | bytes 1048579 | tf_op jit(solution)/shard_map/stack | solution.py:126
  77.5 1.2 %select_bitcast_fusion.1 = (bf16[1,1,384,256]{3,2,1,0:T(8,128)(2,1)S(1)}, bf16[1,1,384,256]{3,2,1,0:T(8,128)(2,1)S(1)}) fusion(bf16[1,384,256]{2,1,0:T(8,128)(2,1)} %collective-permute-done.15, bf16[1,384,256]{2,1,0:T(8,128)(2,1)} %get-tuple-element.32, pred[]{:T(512)S(6)} %eq.53), kind=kLoop, calls=%fused_computation.77 | loop fusion | flops 196608 | bytes 786433 | tf_op jit(solution)/shard_map/stack | solution.py:126
  78.8 1.5 %fusion.5 = (f32[256]{0:T(256)S(1)}, f32[768,256]{1,0:T(8,128)}) fusion(bf16[2,1,384,256]{3,2,1,0:T(8,128)(2,1)S(1)} %pad_maximum_fusion.3, bf16[768,256]{1,0:T(8,128)(2,1)S(1)} %bitcast.226, f32[768]{0:T(1024)S(1)} %copy-done.19, bf16[768,1024]{1,0:T(8,128)(2,1)S(1)} %bitcast.198, bf16[1024,256]{1,0:T(8,128)(2,1)S(1)} %bitcast.208), kind=kOutput, calls=%fused_computation.19 | convolution fusion | flops 403832576 | bytes 3674112 | tf_op jit(solution)/shard_map/dot_general | solution.py:159
  80.3 1.7 %fusion.3 = (f32[256]{0:T(256)S(1)}, f32[1024,256]{1,0:T(8,128)}) fusion(bf16[4,4,64,256]{3,2,1,0:T(8,128)(2,1)S(1)} %pad_maximum_fusion.1, bf16[1024,256]{1,0:T(8,128)(2,1)S(1)} %bitcast.209, f32[1024]{0:T(1024)S(1)} %bitcast.230, bf16[1024,768]{0,1:T(8,128)(2,1)S(1)} %bitcast.196, bf16[768,256]{1,0:T(8,128)(2,1)S(1)} %bitcast.227), kind=kOutput, calls=%fused_computation.13 | convolution fusion | flops 404225792 | bytes 4068352 | tf_op jit(solution)/shard_map/dot_general | solution.py:161
  82.5 1.2 %dynamic-slice_convert_fusion.4 = (bf16[2,2,1,1,64,256]{5,4,3,2,1,0:T(8,128)(2,1)S(1)}, bf16[2,2,1,1,64,256]{5,4,3,2,1,0:T(8,128)(2,1)S(1)}, bf16[2,2,1,1,64,256]{5,4,3,2,1,0:T(8,128)(2,1)S(1)}) fusion(f32[2,2,2,2,64,256]{5,4,3,2,1,0:T(8,128)} %bitcast.220, s32[]{:T(128)S(6)} %select_n.385, s32[]{:T(128)S(6)} %select_n.387, s32[]{:T(128)S(6)} %select_n.393, ...), kind=kLoop, calls=%fused_computation.52 | loop fusion | bytes 786456 | tf_op jit(solution)/shard_map/convert_element_type | solution.py:90
  83.7 1.5 %collective-permute-start.22 = (bf16[259,256]{1,0:T(8,128)(2,1)S(1)}, bf16[259,256]{1,0:T(8,128)(2,1)S(1)}, u32[]{:S(2)}, u32[]{:S(2)}) collective-permute-start(bf16[259,256]{1,0:T(8,128)(2,1)S(1)} %get-tuple-element.83), channel_id=1, source_target_pairs={{0,2},{2,0},{4,6},{6,4},{8,10},{10,8},{12,14},{14,12},{16,18},{18,... | collective-permute-start | bytes 397832 | tf_op jit(solution)/shard_map/ppermute | solution.py:45
  85.2 0.7 collective-permute-start.23
  86.0 1.3 %collective-permute-start.24 = (bf16[259,256]{1,0:T(8,128)(2,1)S(1)}, bf16[259,256]{1,0:T(8,128)(2,1)S(1)}, u32[]{:S(2)}, u32[]{:S(2)}) collective-permute-start(bf16[259,256]{1,0:T(8,128)(2,1)S(1)} %get-tuple-element.85), channel_id=1, source_target_pairs={{0,6},{2,4},{4,2},{6,0},{8,14},{10,12},{12,10},{14,8},{16,22},{18,... | collective-permute-start | bytes 397832 | tf_op jit(solution)/shard_map/ppermute | solution.py:45
  87.3 1.7 %fusion.21 = bf16[384,256]{1,0:T(8,128)(2,1)} fusion(f32[2,384,256]{2,1,0:T(8,128)} %bitcast.218, s32[]{:T(128)S(6)} %select_n.413), kind=kLoop, calls=%fused_computation.75 | loop fusion | bytes 393220 | tf_op jit(solution)/shard_map/convert_element_type | solution.py:90
  89.0 1.1 %constant_dynamic-slice_fusion = f32[2,2,1,1,64,256]{5,4,3,2,1,0:T(8,128)S(1)} fusion(f32[2,2,2,2,64,256]{5,4,3,2,1,0:T(8,128)} %bitcast.221, s32[]{:T(128)S(6)} %select_n.380, s32[]{:T(128)S(6)} %select_n.382), kind=kLoop, calls=%fused_computation.160 | loop fusion | bytes 524296 | tf_op jit(solution)/shard_map/jit(dynamic_index_in_dim)/dynamic_slice | solution.py:79
  90.2 1.6 %collective-permute-done.24 = bf16[259,256]{1,0:T(8,128)(2,1)S(1)} collective-permute-done((bf16[259,256]{1,0:T(8,128)(2,1)S(1)}, bf16[259,256]{1,0:T(8,128)(2,1)S(1)}, u32[]{:S(2)}, u32[]{:S(2)}) %collective-permute-start.24) | collective-permute-done | bytes 132640 | tf_op jit(solution)/shard_map/ppermute | solution.py:45
  92.1 2.0 %collective-permute-start.25 = (bf16[67,256]{1,0:T(8,128)(2,1)S(1)}, bf16[67,256]{1,0:T(8,128)(2,1)S(1)}, u32[]{:S(2)}, u32[]{:S(2)}) collective-permute-start(bf16[67,256]{1,0:T(8,128)(2,1)S(1)} %get-tuple-element.80), channel_id=1, source_target_pairs={{0,8},{2,10},{4,12},{6,14},{8,0},{10,2},{12,4},{14,6},{16,24},{18,... | collective-permute-start | bytes 102920 | tf_op jit(solution)/shard_map/ppermute | solution.py:45
  94.2 2.3 %collective-permute-start.27 = (bf16[67,256]{1,0:T(8,128)(2,1)S(1)}, bf16[67,256]{1,0:T(8,128)(2,1)S(1)}, u32[]{:S(2)}, u32[]{:S(2)}) collective-permute-start(bf16[67,256]{1,0:T(8,128)(2,1)S(1)} %get-tuple-element.82), channel_id=1, source_target_pairs={{0,24},{2,26},{4,28},{6,30},{8,16},{10,18},{12,20},{14,22},{16,8},... | collective-permute-start | bytes 102920 | tf_op jit(solution)/shard_map/ppermute | solution.py:45
  96.5 2.4 %collective-permute-done.26 = bf16[67,256]{1,0:T(8,128)(2,1)S(1)} collective-permute-done((bf16[67,256]{1,0:T(8,128)(2,1)S(1)}, bf16[67,256]{1,0:T(8,128)(2,1)S(1)}, u32[]{:S(2)}, u32[]{:S(2)}) %collective-permute-start.26) | collective-permute-done | bytes 34336 | tf_op jit(solution)/shard_map/ppermute | solution.py:45
  98.9 1.1 %collective-permute-done.27 = bf16[67,256]{1,0:T(8,128)(2,1)S(1)} collective-permute-done((bf16[67,256]{1,0:T(8,128)(2,1)S(1)}, bf16[67,256]{1,0:T(8,128)(2,1)S(1)}, u32[]{:S(2)}, u32[]{:S(2)}) %collective-permute-start.27) | collective-permute-done | bytes 34336 | tf_op jit(solution)/shard_map/ppermute | solution.py:45
  100.1 1.1 %collective-permute-done.28 = f32[8]{0:T(128)S(1)} collective-permute-done((f32[8]{0:T(128)S(1)}, f32[8]{0:T(128)S(1)}, u32[]{:S(2)}, u32[]{:S(2)}) %collective-permute-start.28) | collective-permute-done | bytes 64 | tf_op jit(solution)/shard_map/ppermute | solution.py:45
  101.6 0.7 fusion.32
  102.3 2.2 %fusion.11 = (f32[1,384,256]{2,1,0:T(8,128)}, f32[1,384,256]{2,1,0:T(8,128)}) fusion(f32[384,256]{1,0:T(8,128)S(1)} %get-tuple-element.16, f32[384,256]{1,0:T(8,128)S(1)} %reshape.294, bf16[384,256]{1,0:T(8,128)(2,1)} %collective-permute-done.29, f32[2,384,256]{2,1,0:T(8,128)} %bitcast.219, s32[]{:T(128)S(6)} %select_n.412, f32[256]{0:T(256)S(1)} %mul.212, ...), kind=kLoop, calls=%fused_computation.30 | loop fusion | flops 1671168 | bytes 3542020 | tf_op jit(solution)/shard_map/broadcast_in_dim | solution.py:224
  (169 shorter events, 7.7 us)
Async XLA Ops:
  0.6 21.4 %copy-start = (f32[64,64]{1,0:T(8,128)S(1)}, f32[64,64]{1,0:T(8,128)}, u32[]{:S(2)}) copy-start(f32[64,64]{1,0:T(8,128)} %param.9) | copy-start | bytes 49156
  1.5 7.9 %collective-permute-start.2 = (bf16[1,64,256]{2,1,0:T(8,128)(2,1)S(1)}, bf16[1,64,256]{2,1,0:T(8,128)(2,1)S(1)}, u32[]{:S(2)}, u32[]{:S(2)}) collective-permute-start(bf16[1,64,256]{2,1,0:T(8,128)(2,1)S(1)} %convert_element_type.273), channel_id=1, source_target_pairs={{0,2},{2,0},{4,6},{6,4},{8,10},{10,8},{12,14},{14,12},{16,18},{18,... | collective-permute-start | bytes 98312 | tf_op jit(solution)/shard_map/ppermute | solution.py:45
  4.4 4.9 %collective-permute-start.1 = (bf16[1,64,256]{2,1,0:T(8,128)(2,1)S(1)}, bf16[1,64,256]{2,1,0:T(8,128)(2,1)S(1)}, u32[]{:S(2)}, u32[]{:S(2)}) collective-permute-start(bf16[1,64,256]{2,1,0:T(8,128)(2,1)S(1)} %convert_element_type.273), channel_id=1, source_target_pairs={{0,4},{2,6},{4,0},{6,2},{8,12},{10,14},{12,8},{14,10},{16,20},{18,... | collective-permute-start | bytes 98312 | tf_op jit(solution)/shard_map/ppermute | solution.py:45
  6.0 4.8 %collective-permute-start = (bf16[1,64,256]{2,1,0:T(8,128)(2,1)S(1)}, bf16[1,64,256]{2,1,0:T(8,128)(2,1)S(1)}, u32[]{:S(2)}, u32[]{:S(2)}) collective-permute-start(bf16[1,64,256]{2,1,0:T(8,128)(2,1)S(1)} %convert_element_type.273), channel_id=1, source_target_pairs={{0,6},{2,4},{4,2},{6,0},{8,14},{10,12},{12,10},{14,8},{16,22},{18,... | collective-permute-start | bytes 98312 | tf_op jit(solution)/shard_map/ppermute | solution.py:45
  7.7 22.3 %collective-permute-start.3 = (bf16[1,384,256]{2,1,0:T(8,128)(2,1)}, bf16[1,384,256]{2,1,0:T(8,128)(2,1)S(1)}, u32[]{:S(2)}, u32[]{:S(2)}) collective-permute-start(bf16[1,384,256]{2,1,0:T(8,128)(2,1)} %convert_element_type.275), channel_id=1, source_target_pairs={{0,1},{1,0},{2,3},{3,2},{4,5},{5,4},{6,7},{7,6},{8,9},{9,8},{10,11... | collective-permute-start | bytes 589832 | tf_op jit(solution)/shard_map/ppermute | solution.py:45
  11.7 6.9 %copy-start.2 = (s32[1,1,12,256,256]{4,3,2,1,0:T(8,128)S(1)}, s32[1,1,12,256,256]{4,3,2,1,0:T(8,128)}, u32[]{:S(2)}) copy-start(s32[1,1,12,256,256]{4,3,2,1,0:T(8,128)} %param.11) | copy-start | bytes 9437188
  11.7 16.4 %collective-permute-start.6 = (bf16[4,64,256]{2,1,0:T(8,128)(2,1)S(1)}, bf16[4,64,256]{2,1,0:T(8,128)(2,1)S(1)}, u32[]{:S(2)}, u32[]{:S(2)}) collective-permute-start(bf16[4,64,256]{2,1,0:T(8,128)(2,1)S(1)} %maximum_bitcast_fusion), channel_id=1, source_target_pairs={{0,8},{2,10},{4,12},{6,14},{8,0},{10,2},{12,4},{14,6},{16,24},{18,... | collective-permute-start | bytes 393224 | tf_op jit(solution)/shard_map/ppermute | solution.py:45
  13.3 14.7 %collective-permute-start.5 = (bf16[4,64,256]{2,1,0:T(8,128)(2,1)S(1)}, bf16[4,64,256]{2,1,0:T(8,128)(2,1)S(1)}, u32[]{:S(2)}, u32[]{:S(2)}) collective-permute-start(bf16[4,64,256]{2,1,0:T(8,128)(2,1)S(1)} %maximum_bitcast_fusion), channel_id=1, source_target_pairs={{0,16},{2,18},{4,20},{6,22},{8,24},{10,26},{12,28},{14,30},{16,0},... | collective-permute-start | bytes 393224 | tf_op jit(solution)/shard_map/ppermute | solution.py:45
  15.9 12.9 %collective-permute-start.4 = (bf16[4,64,256]{2,1,0:T(8,128)(2,1)S(1)}, bf16[4,64,256]{2,1,0:T(8,128)(2,1)}, u32[]{:S(2)}, u32[]{:S(2)}) collective-permute-start(bf16[4,64,256]{2,1,0:T(8,128)(2,1)S(1)} %maximum_bitcast_fusion), channel_id=1, source_target_pairs={{0,24},{2,26},{4,28},{6,30},{8,16},{10,18},{12,20},{14,22},{16,8},... | collective-permute-start | bytes 393224 | tf_op jit(solution)/shard_map/ppermute | solution.py:45
  18.6 1.8 %copy-start.3 = (f32[1,64,256]{2,1,0:T(8,128)S(1)}, f32[1,64,256]{2,1,0:T(8,128)}, u32[]{:S(2)}) copy-start(f32[1,64,256]{2,1,0:T(8,128)} %param.8) | copy-start | bytes 196612
  18.6 1.9 %copy-start.15 = (f32[64,64]{1,0:T(8,128)S(1)}, f32[64,64]{1,0:T(8,128)}, u32[]{:S(2)}) copy-start(f32[64,64]{1,0:T(8,128)} %param.10) | copy-start | bytes 49156
  18.6 3.2 %copy-start.1 = (f32[1,384,256]{2,1,0:T(8,128)S(1)}, f32[1,384,256]{2,1,0:T(8,128)}, u32[]{:S(2)}) copy-start(f32[1,384,256]{2,1,0:T(8,128)} %param.7) | copy-start | bytes 1179652
  20.3 9.8 %copy-start.16 = (f32[1,2,4,128]{3,1,2,0:T(2,128)}, f32[1,2,4,128]{3,1,2,0:T(2,128)S(1)}, u32[]{:S(2)}) copy-start(f32[1,2,4,128]{3,1,2,0:T(2,128)S(1)} %copy.48) | copy-start | bytes 12292
  20.4 11.6 %copy-start.18 = (f32[768]{0:T(1024)}, f32[768]{0:T(1024)S(1)}, u32[]{:S(2)}) copy-start(f32[768]{0:T(1024)S(1)} %mul.186) | copy-start | bytes 9220
  27.1 2.9 %copy-start.4 = (bf16[96,8,4,256]{3,1,2,0:T(8,128)(2,1)}, bf16[96,8,4,256]{3,1,2,0:T(8,128)(2,1)S(1)}, u32[]{:S(2)}) copy-start(bf16[96,8,4,256]{3,1,2,0:T(8,128)(2,1)S(1)} %copy.47) | copy-start | bytes 4718596
  28.0 4.0 %copy-start.6 = (bf16[96,8,4,256]{3,1,2,0:T(8,128)(2,1)}, bf16[96,8,4,256]{3,1,2,0:T(8,128)(2,1)S(1)}, u32[]{:S(2)}) copy-start(bf16[96,8,4,256]{3,1,2,0:T(8,128)(2,1)S(1)} %copy.49) | copy-start | bytes 4718596
  28.1 0.7 copy-start.14
  29.9 1.9 %copy-start.12 = (bf16[4,4,64,256]{3,2,1,0:T(8,128)(2,1)}, bf16[4,4,64,256]{3,2,1,0:T(8,128)(2,1)S(1)}, u32[]{:S(2)}) copy-start(bf16[4,4,64,256]{3,2,1,0:T(8,128)(2,1)S(1)} %pad_maximum_fusion) | copy-start | bytes 1572868
  30.0 1.8 %copy-start.13 = (bf16[2,1,384,256]{3,2,1,0:T(8,128)(2,1)}, bf16[2,1,384,256]{3,2,1,0:T(8,128)(2,1)S(1)}, u32[]{:S(2)}) copy-start(bf16[2,1,384,256]{3,2,1,0:T(8,128)(2,1)S(1)} %pad_maximum_fusion.2) | copy-start | bytes 1179652
  32.0 2.1 %copy-start.22 = (f32[4]{0:T(128)S(1)}, f32[4]{0:T(128)}, u32[]{:S(2)}) copy-start(f32[4]{0:T(128)} %reduce_sum.195) | copy-start | bytes 52
  33.9 25.9 %copy-start.8 = (f32[768,256]{1,0:T(8,128)}, f32[768,256]{1,0:T(8,128)S(1)}, u32[]{:S(2)}) copy-start(f32[768,256]{1,0:T(8,128)S(1)} %get-tuple-element.105) | copy-start | bytes 2359300
  35.5 6.3 %collective-permute-start.7 = (bf16[259,256]{1,0:T(8,128)(2,1)S(1)}, bf16[259,256]{1,0:T(8,128)(2,1)S(1)}, u32[]{:S(2)}, u32[]{:S(2)}) collective-permute-start(bf16[259,256]{1,0:T(8,128)(2,1)S(1)} %get-tuple-element.89), channel_id=1, source_target_pairs={{0,2},{2,0},{4,6},{6,4},{8,10},{10,8},{12,14},{14,12},{16,18},{18,... | collective-permute-start | bytes 397832 | tf_op jit(solution)/shard_map/ppermute | solution.py:45
  36.1 7.9 %collective-permute-start.8 = (bf16[259,256]{1,0:T(8,128)(2,1)S(1)}, bf16[259,256]{1,0:T(8,128)(2,1)S(1)}, u32[]{:S(2)}, u32[]{:S(2)}) collective-permute-start(bf16[259,256]{1,0:T(8,128)(2,1)S(1)} %get-tuple-element.90), channel_id=1, source_target_pairs={{0,4},{2,6},{4,0},{6,2},{8,12},{10,14},{12,8},{14,10},{16,20},{18,... | collective-permute-start | bytes 397832 | tf_op jit(solution)/shard_map/ppermute | solution.py:45
  37.6 6.4 %collective-permute-start.9 = (bf16[259,256]{1,0:T(8,128)(2,1)S(1)}, bf16[259,256]{1,0:T(8,128)(2,1)S(1)}, u32[]{:S(2)}, u32[]{:S(2)}) collective-permute-start(bf16[259,256]{1,0:T(8,128)(2,1)S(1)} %get-tuple-element.91), channel_id=1, source_target_pairs={{0,6},{2,4},{4,2},{6,0},{8,14},{10,12},{12,10},{14,8},{16,22},{18,... | collective-permute-start | bytes 397832 | tf_op jit(solution)/shard_map/ppermute | solution.py:45
  39.1 20.8 %collective-permute-start.14 = (bf16[384,256]{1,0:T(8,128)(2,1)S(1)}, bf16[384,256]{1,0:T(8,128)(2,1)S(1)}, u32[]{:S(2)}, u32[]{:S(2)}) collective-permute-start(bf16[384,256]{1,0:T(8,128)(2,1)S(1)} %fusion.20), channel_id=1, source_target_pairs={{0,1},{1,0},{2,3},{3,2},{4,5},{5,4},{6,7},{7,6},{8,9},{9,8},{10,11... | collective-permute-start | bytes 589832 | tf_op jit(solution)/shard_map/ppermute | solution.py:45
  44.2 4.5 %collective-permute-start.10 = (bf16[67,256]{1,0:T(8,128)(2,1)S(1)}, bf16[67,256]{1,0:T(8,128)(2,1)S(1)}, u32[]{:S(2)}, u32[]{:S(2)}) collective-permute-start(bf16[67,256]{1,0:T(8,128)(2,1)S(1)} %get-tuple-element.86), channel_id=1, source_target_pairs={{0,8},{2,10},{4,12},{6,14},{8,0},{10,2},{12,4},{14,6},{16,24},{18,... | collective-permute-start | bytes 102920 | tf_op jit(solution)/shard_map/ppermute | solution.py:45
  45.0 6.2 %collective-permute-start.11 = (bf16[67,256]{1,0:T(8,128)(2,1)S(1)}, bf16[67,256]{1,0:T(8,128)(2,1)S(1)}, u32[]{:S(2)}, u32[]{:S(2)}) collective-permute-start(bf16[67,256]{1,0:T(8,128)(2,1)S(1)} %get-tuple-element.87), channel_id=1, source_target_pairs={{0,16},{2,18},{4,20},{6,22},{8,24},{10,26},{12,28},{14,30},{16,0},... | collective-permute-start | bytes 102920 | tf_op jit(solution)/shard_map/ppermute | solution.py:45
  48.5 5.8 %collective-permute-start.12 = (bf16[67,256]{1,0:T(8,128)(2,1)S(1)}, bf16[67,256]{1,0:T(8,128)(2,1)S(1)}, u32[]{:S(2)}, u32[]{:S(2)}) collective-permute-start(bf16[67,256]{1,0:T(8,128)(2,1)S(1)} %get-tuple-element.88), channel_id=1, source_target_pairs={{0,24},{2,26},{4,28},{6,30},{8,16},{10,18},{12,20},{14,22},{16,8},... | collective-permute-start | bytes 102920 | tf_op jit(solution)/shard_map/ppermute | solution.py:45
  54.3 1.2 %collective-permute-start.13 = (f32[8]{0:T(128)S(1)}, f32[8]{0:T(128)S(1)}, u32[]{:S(2)}, u32[]{:S(2)}) collective-permute-start(f32[8]{0:T(128)S(1)} %fusion.47), channel_id=1, source_target_pairs={{0,1},{1,0},{2,3},{3,2},{4,5},{5,4},{6,7},{7,6},{8,9},{9,8},{10,11... | collective-permute-start | bytes 104 | tf_op jit(solution)/shard_map/ppermute | solution.py:45
  55.5 0.5 copy-start.20
  56.3 4.3 %collective-permute-start.18 = (bf16[1,64,256]{2,1,0:T(8,128)(2,1)S(1)}, bf16[1,64,256]{2,1,0:T(8,128)(2,1)S(1)}, u32[]{:S(2)}, u32[]{:S(2)}) collective-permute-start(bf16[1,64,256]{2,1,0:T(8,128)(2,1)S(1)} %get-tuple-element.34), channel_id=1, source_target_pairs={{0,2},{2,0},{4,6},{6,4},{8,10},{10,8},{12,14},{14,12},{16,18},{18,... | collective-permute-start | bytes 98312 | tf_op jit(solution)/shard_map/ppermute | solution.py:45
  57.7 4.3 %collective-permute-start.17 = (bf16[1,64,256]{2,1,0:T(8,128)(2,1)S(1)}, bf16[1,64,256]{2,1,0:T(8,128)(2,1)S(1)}, u32[]{:S(2)}, u32[]{:S(2)}) collective-permute-start(bf16[1,64,256]{2,1,0:T(8,128)(2,1)S(1)} %get-tuple-element.34), channel_id=1, source_target_pairs={{0,4},{2,6},{4,0},{6,2},{8,12},{10,14},{12,8},{14,10},{16,20},{18,... | collective-permute-start | bytes 98312 | tf_op jit(solution)/shard_map/ppermute | solution.py:45
  58.2 4.8 %collective-permute-start.16 = (bf16[1,64,256]{2,1,0:T(8,128)(2,1)S(1)}, bf16[1,64,256]{2,1,0:T(8,128)(2,1)S(1)}, u32[]{:S(2)}, u32[]{:S(2)}) collective-permute-start(bf16[1,64,256]{2,1,0:T(8,128)(2,1)S(1)} %get-tuple-element.34), channel_id=1, source_target_pairs={{0,6},{2,4},{4,2},{6,0},{8,14},{10,12},{12,10},{14,8},{16,22},{18,... | collective-permute-start | bytes 98312 | tf_op jit(solution)/shard_map/ppermute | solution.py:45
  59.8 8.8 %copy-start.10 = (bf16[384,256]{1,0:T(8,128)(2,1)}, bf16[384,256]{1,0:T(8,128)(2,1)S(1)}, u32[]{:S(2)}) copy-start(bf16[384,256]{1,0:T(8,128)(2,1)S(1)} %collective-permute-done.14) | copy-start | bytes 589828
  60.6 16.9 %collective-permute-start.15 = (bf16[1,384,256]{2,1,0:T(8,128)(2,1)}, bf16[1,384,256]{2,1,0:T(8,128)(2,1)}, u32[]{:S(2)}, u32[]{:S(2)}) collective-permute-start(bf16[1,384,256]{2,1,0:T(8,128)(2,1)} %get-tuple-element.32), channel_id=1, source_target_pairs={{0,1},{1,0},{2,3},{3,2},{4,5},{5,4},{6,7},{7,6},{8,9},{9,8},{10,11... | collective-permute-start | bytes 589832 | tf_op jit(solution)/shard_map/ppermute | solution.py:45
  63.8 7.1 %collective-permute-start.21 = (bf16[4,64,256]{2,1,0:T(8,128)(2,1)}, bf16[4,64,256]{2,1,0:T(8,128)(2,1)}, u32[]{:S(2)}, u32[]{:S(2)}) collective-permute-start(bf16[4,64,256]{2,1,0:T(8,128)(2,1)} %maximum_bitcast_fusion.1), channel_id=1, source_target_pairs={{0,8},{2,10},{4,12},{6,14},{8,0},{10,2},{12,4},{14,6},{16,24},{18,... | collective-permute-start | bytes 393224 | tf_op jit(solution)/shard_map/ppermute | solution.py:45
  63.8 12.3 %collective-permute-start.20 = (bf16[4,64,256]{2,1,0:T(8,128)(2,1)}, bf16[4,64,256]{2,1,0:T(8,128)(2,1)}, u32[]{:S(2)}, u32[]{:S(2)}) collective-permute-start(bf16[4,64,256]{2,1,0:T(8,128)(2,1)} %maximum_bitcast_fusion.1), channel_id=1, source_target_pairs={{0,16},{2,18},{4,20},{6,22},{8,24},{10,26},{12,28},{14,30},{16,0},... | collective-permute-start | bytes 393224 | tf_op jit(solution)/shard_map/ppermute | solution.py:45
  64.7 11.3 %collective-permute-start.19 = (bf16[4,64,256]{2,1,0:T(8,128)(2,1)}, bf16[4,64,256]{2,1,0:T(8,128)(2,1)}, u32[]{:S(2)}, u32[]{:S(2)}) collective-permute-start(bf16[4,64,256]{2,1,0:T(8,128)(2,1)} %maximum_bitcast_fusion.1), channel_id=1, source_target_pairs={{0,24},{2,26},{4,28},{6,30},{8,16},{10,18},{12,20},{14,22},{16,8},... | collective-permute-start | bytes 393224 | tf_op jit(solution)/shard_map/ppermute | solution.py:45
  77.2 1.6 %copy-start.7 = (bf16[96,8,4,256]{3,1,2,0:T(8,128)(2,1)S(1)}, bf16[96,8,4,256]{3,1,2,0:T(8,128)(2,1)}, u32[]{:S(2)}) copy-start(bf16[96,8,4,256]{3,1,2,0:T(8,128)(2,1)} %copy-done.6) | copy-start | bytes 4718596
  77.2 1.6 %copy-start.19 = (f32[768]{0:T(1024)S(1)}, f32[768]{0:T(1024)}, u32[]{:S(2)}) copy-start(f32[768]{0:T(1024)} %copy-done.18) | copy-start | bytes 9220
  78.8 1.5 %copy-start.5 = (bf16[96,8,4,256]{3,1,2,0:T(8,128)(2,1)S(1)}, bf16[96,8,4,256]{3,1,2,0:T(8,128)(2,1)}, u32[]{:S(2)}) copy-start(bf16[96,8,4,256]{3,1,2,0:T(8,128)(2,1)} %copy-done.4) | copy-start | bytes 4718596
  78.8 1.5 %copy-start.17 = (f32[1,2,4,128]{3,1,2,0:T(2,128)S(1)}, f32[1,2,4,128]{3,1,2,0:T(2,128)}, u32[]{:S(2)}) copy-start(f32[1,2,4,128]{3,1,2,0:T(2,128)} %copy-done.16) | copy-start | bytes 12292
  83.7 6.3 %collective-permute-start.22 = (bf16[259,256]{1,0:T(8,128)(2,1)S(1)}, bf16[259,256]{1,0:T(8,128)(2,1)S(1)}, u32[]{:S(2)}, u32[]{:S(2)}) collective-permute-start(bf16[259,256]{1,0:T(8,128)(2,1)S(1)} %get-tuple-element.83), channel_id=1, source_target_pairs={{0,2},{2,0},{4,6},{6,4},{8,10},{10,8},{12,14},{14,12},{16,18},{18,... | collective-permute-start | bytes 397832 | tf_op jit(solution)/shard_map/ppermute | solution.py:45
  85.2 5.0 %collective-permute-start.23 = (bf16[259,256]{1,0:T(8,128)(2,1)S(1)}, bf16[259,256]{1,0:T(8,128)(2,1)S(1)}, u32[]{:S(2)}, u32[]{:S(2)}) collective-permute-start(bf16[259,256]{1,0:T(8,128)(2,1)S(1)} %get-tuple-element.84), channel_id=1, source_target_pairs={{0,4},{2,6},{4,0},{6,2},{8,12},{10,14},{12,8},{14,10},{16,20},{18,... | collective-permute-start | bytes 397832 | tf_op jit(solution)/shard_map/ppermute | solution.py:45
  86.0 5.9 %collective-permute-start.24 = (bf16[259,256]{1,0:T(8,128)(2,1)S(1)}, bf16[259,256]{1,0:T(8,128)(2,1)S(1)}, u32[]{:S(2)}, u32[]{:S(2)}) collective-permute-start(bf16[259,256]{1,0:T(8,128)(2,1)S(1)} %get-tuple-element.85), channel_id=1, source_target_pairs={{0,6},{2,4},{4,2},{6,0},{8,14},{10,12},{12,10},{14,8},{16,22},{18,... | collective-permute-start | bytes 397832 | tf_op jit(solution)/shard_map/ppermute | solution.py:45
  87.3 13.9 %copy-start.21 = (f32[8]{0:T(128)S(1)}, f32[8]{0:T(128)}, u32[]{:S(2)}) copy-start(f32[8]{0:T(128)} %copy-done.20) | copy-start | bytes 100
  89.0 13.3 %copy-start.9 = (f32[768,256]{1,0:T(8,128)S(1)}, f32[768,256]{1,0:T(8,128)}, u32[]{:S(2)}) copy-start(f32[768,256]{1,0:T(8,128)} %copy-done.8) | copy-start | bytes 2359300
  89.0 13.3 %copy-start.11 = (bf16[384,256]{1,0:T(8,128)(2,1)S(1)}, bf16[384,256]{1,0:T(8,128)(2,1)}, u32[]{:S(2)}) copy-start(bf16[384,256]{1,0:T(8,128)(2,1)} %copy-done.10) | copy-start | bytes 589828
  89.0 13.3 %collective-permute-start.29 = (bf16[384,256]{1,0:T(8,128)(2,1)}, bf16[384,256]{1,0:T(8,128)(2,1)}, u32[]{:S(2)}, u32[]{:S(2)}) collective-permute-start(bf16[384,256]{1,0:T(8,128)(2,1)} %fusion.21), channel_id=1, source_target_pairs={{0,1},{1,0},{2,3},{3,2},{4,5},{5,4},{6,7},{7,6},{8,9},{9,8},{10,11... | collective-permute-start | bytes 589832 | tf_op jit(solution)/shard_map/ppermute | solution.py:45
  92.1 4.5 %collective-permute-start.25 = (bf16[67,256]{1,0:T(8,128)(2,1)S(1)}, bf16[67,256]{1,0:T(8,128)(2,1)S(1)}, u32[]{:S(2)}, u32[]{:S(2)}) collective-permute-start(bf16[67,256]{1,0:T(8,128)(2,1)S(1)} %get-tuple-element.80), channel_id=1, source_target_pairs={{0,8},{2,10},{4,12},{6,14},{8,0},{10,2},{12,4},{14,6},{16,24},{18,... | collective-permute-start | bytes 102920 | tf_op jit(solution)/shard_map/ppermute | solution.py:45
  94.1 4.9 %collective-permute-start.26 = (bf16[67,256]{1,0:T(8,128)(2,1)S(1)}, bf16[67,256]{1,0:T(8,128)(2,1)S(1)}, u32[]{:S(2)}, u32[]{:S(2)}) collective-permute-start(bf16[67,256]{1,0:T(8,128)(2,1)S(1)} %get-tuple-element.81), channel_id=1, source_target_pairs={{0,16},{2,18},{4,20},{6,22},{8,24},{10,26},{12,28},{14,30},{16,0},... | collective-permute-start | bytes 102920 | tf_op jit(solution)/shard_map/ppermute | solution.py:45
  94.2 5.8 %collective-permute-start.27 = (bf16[67,256]{1,0:T(8,128)(2,1)S(1)}, bf16[67,256]{1,0:T(8,128)(2,1)S(1)}, u32[]{:S(2)}, u32[]{:S(2)}) collective-permute-start(bf16[67,256]{1,0:T(8,128)(2,1)S(1)} %get-tuple-element.82), channel_id=1, source_target_pairs={{0,24},{2,26},{4,28},{6,30},{8,16},{10,18},{12,20},{14,22},{16,8},... | collective-permute-start | bytes 102920 | tf_op jit(solution)/shard_map/ppermute | solution.py:45
  100.1 1.2 %collective-permute-start.28 = (f32[8]{0:T(128)S(1)}, f32[8]{0:T(128)S(1)}, u32[]{:S(2)}, u32[]{:S(2)}) collective-permute-start(f32[8]{0:T(128)S(1)} %fusion.46), channel_id=1, source_target_pairs={{0,1},{1,0},{2,3},{3,2},{4,5},{5,4},{6,7},{7,6},{8,9},{9,8},{10,11... | collective-permute-start | bytes 104 | tf_op jit(solution)/shard_map/ppermute | solution.py:45

commit v21 on v19

--- a/solution.py
+++ b/solution.py
@@ -62,7 +62,7 @@
     return jnp.concatenate([high, mid, low])
 
 
-def halve_sum(part, axis, send_type, extra=None, first_type=None):
+def halve_sum(part, axis, send_type, extra=None, first_type=None, relative=False):
     size, bits = bit_count(axis)
     me = lax.axis_index(axis)
     rows, width = part.shape[0] // size, part.shape[1]
@@ -76,18 +76,21 @@
         def block_of(value):
             out = buf
             for j in sorted(range(len(group)), key=lambda j: -left.index(group[j])):
-                out = lax.dynamic_index_in_dim(out, (value >> j) & 1, left.index(group[j]), keepdims=False)
+                if relative:
+                    out = lax.index_in_dim(out, (value >> j) & 1, left.index(group[j]), keepdims=False)
+                else:
+                    out = lax.dynamic_index_in_dim(out, (value >> j) & 1, left.index(group[j]), keepdims=False)
             return out
 
         coded = extra is not None and first_type is not None
         stage_type = send_type if first_type is None else first_type
-        total = block_of(digit)
+        total = block_of(0 if relative else digit)
         shape = total.shape
         if extra is not None:
             tail = jnp.concatenate([extra, jnp.zeros((2 * extra.shape[0], width), extra.dtype)]) if coded else extra
             total = jnp.concatenate([total.reshape(-1, width), tail])
         for k in range(1, len(masks)):
-            send = block_of(digit ^ k).astype(stage_type)
+            send = block_of(k if relative else digit ^ k).astype(stage_type)
             if extra is not None:
                 tail = code_rows(extra) if coded else extra
                 send = jnp.concatenate([send.reshape(-1, width), tail.astype(stage_type)])
@@ -131,6 +134,23 @@
     result = buf.reshape((size * piece.shape[0],) + piece.shape[1:])
     return result if hold is None else (result, kept)
 
+def xor_gather(piece, axis):
+    size, bits = bit_count(axis)
+    buf = piece[None]
+    for bit in reversed(range(bits)):
+        buf = jnp.stack([buf, swap_with(buf, axis, size, bit)], axis=1).reshape((-1,) + piece.shape)
+    return buf.reshape((size * piece.shape[0],) + piece.shape[1:])
+
+
+def xor_order(value, axis, dim):
+    size = lax.axis_size(axis)
+    me = lax.axis_index(axis)
+    shape = value.shape
+    split = shape[:dim] + (size, shape[dim] // size) + shape[dim + 1 :]
+    picked = jnp.take(value.reshape(split), jnp.arange(size) ^ me, axis=dim)
+    return picked.reshape(shape)
+
+
 def per_device(
     draws_user, draws_item, prior_user, prior_item, count_tiles, tile_blocks, tile_count
 ):
@@ -154,7 +174,10 @@
         tile_cols = jnp.sum(tiles_bf, axis=1, dtype=jnp.float32)
         user_deg = jnp.sum(jnp.where(row_pick[:, :, None], tile_rows[:, None, :], 0.0), axis=0)
         item_deg = jnp.sum(jnp.where(col_pick[:, :, None], tile_cols[:, None, :], 0.0), axis=0)
-        return (counts_bf, counts_t, user_deg.reshape(-1), item_deg.reshape(-1))
+        counts_bf = xor_order(counts_bf, "item", 0)
+        counts_t = xor_order(counts_t, "item", 1)
+        user_deg = xor_order(user_deg.reshape(-1), "item", 0)
+        return (counts_bf, counts_t, user_deg, item_deg.reshape(-1))
 
     def cross_parts(user_range, item_range, counts):
         counts_bf, counts_t, user_deg, item_deg = counts
@@ -165,7 +188,7 @@
         return (to_users, to_items)
 
     def user_range_of(user_vec):
-        return double_gather(user_vec.astype(jnp.bfloat16), "item")
+        return xor_gather(user_vec.astype(jnp.bfloat16), "item")
 
     def operate(user_vec, item_vec, counts):
         user_range = user_range_of(user_vec)
@@ -192,7 +215,7 @@
         )
         sums = jnp.concatenate([norm_part, curve_part]).reshape(1, 2 * DRAWS)
         sums = jnp.pad(sums, ((0, 0), (0, width - 2 * DRAWS)))
-        total_user, _ = halve_sum(part_user, "item", jnp.bfloat16)
+        total_user, _ = halve_sum(part_user, "item", jnp.bfloat16, relative=True)
         total_item, sums = halve_sum(part_item, "user", jnp.float32, sums, jnp.bfloat16)
         sums = sums[0, : 2 * DRAWS]
         size, bits = bit_count("item")

time: 103 us -> 130 us (1.26)
  local copies, waits for them, and re-layouts: 13.2 us -> 33.3 us
  other arithmetic: 18.8 us -> 25.9 us
    another operation x1 -> x5, local copies, waits for them, and re-layouts: 0.01 us -> 9.22 us  [the longest x4 9.22 us: xor_order(): picked = jnp.take(value.reshape(split), jnp.arange(size) ^ me, axis=dim)]
    select_n x0 -> x4, other arithmetic: none -> 5.77 us  [xor_order(): picked = jnp.take(value.reshape(split), jnp.arange(size) ^ me, axis=dim)]
    gather x0 -> x3, local copies, waits for them, and re-layouts: none -> 5.68 us  [xor_order(): picked = jnp.take(value.reshape(split), jnp.arange(size) ^ me, axis=dim)]
    select_n x0 -> x2, local copies, waits for them, and re-layouts: none -> 2.25 us  [xor_order(): picked = jnp.take(value.reshape(split), jnp.arange(size) ^ me, axis=dim)]
    another operation x0 -> x3, other arithmetic: none -> 1.86 us  [xor_gather(): jnp.stack([buf, swap_with(buf, axis, size, bit)], axis=1)]
    slice x0 -> x2, local copies, waits for them, and re-layouts: none -> 1.71 us  [block_of(): lax.index_in_dim(out, value >> j & 1, left.index(group[j]), keepdims=False)]
    convert_element_type x6 -> x4, local copies, waits for them, and re-layouts: 4.1 us -> 2.39 us  [halve_sum(): send = block_of(k if relative else digit ^ k).astype(stage_type)]
    another operation x10 -> x6, other arithmetic: 4.66 us -> 3.21 us  [double_gather(): buf = jnp.stack(ordered, axis=1).reshape((-1,) + piece.shape)]
  transfers between devices with their start and end apart: 30 -> 30, of which waited for: 15 -> 13; matrix products, arithmetic and copies ran while one was open for 27% -> 42% of each run, Pallas kernels for 0% -> 0%
where the time goes in v21:
time: 130 us; the launch traced here: 129 us
  local copies, waits for them, and re-layouts  33.3 us (26%)
  starting transfers between devices  33.3 us (26%)
  other arithmetic  25.9 us (20%)
  waiting for transfers between devices  23 us (18%)
  matrix products  11.6 us (9%)
  between operations  2.04 us (2%)
    ppermute x30, starting transfers between devices, swap_with(): return lax.ppermute(value, axis, pairs)  33.3 us
    ppermute x30, waiting for transfers between devices, swap_with(): return lax.ppermute(value, axis, pairs)  23 us
    another operation x4, local copies, waits for them, and re-layouts, xor_order(): picked = jnp.take(value.reshape(split), jnp.arange(size) ^ me, axis=dim)  9.22 us
    select_n x4, other arithmetic, xor_order(): picked = jnp.take(value.reshape(split), jnp.arange(size) ^ me, axis=dim)  5.77 us
    gather x3, local copies, waits for them, and re-layouts, xor_order(): picked = jnp.take(value.reshape(split), jnp.arange(size) ^ me, axis=dim)  5.68 us
    dot_general x2, matrix products, cross_parts(): to_items = jnp.dot(counts_t, user_range, preferred_element_type=jnp.float32)  3.46 us
    dot_general x2, matrix products, cross_parts(): jnp.dot(counts_bf, item_range, preferred_element_type=jnp.float32)  3.36 us
    another operation x6, other arithmetic, double_gather(): buf = jnp.stack(ordered, axis=1).reshape((-1,) + piece.shape)  3.21 us
  transfers between devices with their start and end apart: 30, of which 13 were waited for; matrix products, arithmetic and copies ran while one was open for 42% of the time, Pallas kernels for 0%

profile of v21, /device:TPU:0, one launch (start us, length us, event | category | flops | bytes accessed | tf_op | source)
XLA Modules:
  0.0 129.1 jit_solution(10609167994852795782)
XLA Ops:
  0.6 0.9 convert_element_type.273
  1.5 3.0 %collective-permute-start.2 = (bf16[1,64,256]{2,1,0:T(8,128)(2,1)S(1)}, bf16[1,64,256]{2,1,0:T(8,128)(2,1)S(1)}, u32[]{:S(2)}, u32[]{:S(2)}) collective-permute-start(bf16[1,64,256]{2,1,0:T(8,128)(2,1)S(1)} %convert_element_type.273), channel_id=1, source_target_pairs={{0,8},{2,10},{4,12},{6,14},{8,0},{10,2},{12,4},{14,6},{16,24},{18,... | collective-permute-start | bytes 98312 | tf_op jit(solution)/shard_map/ppermute | solution.py:45
  4.5 2.6 %collective-permute-start.1 = (bf16[1,64,256]{2,1,0:T(8,128)(2,1)S(1)}, bf16[1,64,256]{2,1,0:T(8,128)(2,1)S(1)}, u32[]{:S(2)}, u32[]{:S(2)}) collective-permute-start(bf16[1,64,256]{2,1,0:T(8,128)(2,1)S(1)} %convert_element_type.273), channel_id=1, source_target_pairs={{0,16},{2,18},{4,20},{6,22},{8,24},{10,26},{12,28},{14,30},{16,0},... | collective-permute-start | bytes 98312 | tf_op jit(solution)/shard_map/ppermute | solution.py:45
  7.1 1.7 %convert_element_type.275 = bf16[1,384,256]{2,1,0:T(8,128)(2,1)} convert(f32[1,384,256]{2,1,0:T(8,128)} %param.7) | non-fusion elementwise | flops 98304 | bytes 589824 | tf_op jit(solution)/shard_map/convert_element_type | solution.py:191
  8.8 1.0 convert_bitcast_fusion.4
  10.5 0.8 slice_bitcast_fusion.1
  12.1 0.8 collective-permute-done
  12.8 0.9 select_bitcast_fusion.16
  13.7 1.6 %collective-permute-start.6 = (bf16[4,64,256]{2,1,0:T(8,128)(2,1)S(1)}, bf16[4,64,256]{2,1,0:T(8,128)(2,1)S(1)}, u32[]{:S(2)}, u32[]{:S(2)}) collective-permute-start(bf16[4,64,256]{2,1,0:T(8,128)(2,1)S(1)} %maximum_bitcast_fusion), channel_id=1, source_target_pairs={{0,2},{2,0},{4,6},{6,4},{8,10},{10,8},{12,14},{14,12},{16,18},{18,... | collective-permute-start | bytes 393224 | tf_op jit(solution)/shard_map/ppermute | solution.py:45
  15.3 1.5 %collective-permute-start.5 = (bf16[4,64,256]{2,1,0:T(8,128)(2,1)S(1)}, bf16[4,64,256]{2,1,0:T(8,128)(2,1)}, u32[]{:S(2)}, u32[]{:S(2)}) collective-permute-start(bf16[4,64,256]{2,1,0:T(8,128)(2,1)S(1)} %maximum_bitcast_fusion), channel_id=1, source_target_pairs={{0,4},{2,6},{4,0},{6,2},{8,12},{10,14},{12,8},{14,10},{16,20},{18,... | collective-permute-start | bytes 393224 | tf_op jit(solution)/shard_map/ppermute | solution.py:45
  17.3 2.5 %convert_reduce_fusion.1 = (f32[12,256]{1,0:T(8,128)S(1)}, f32[12,256]{1,0:T(8,128)S(1)}) fusion(s32[12,256,256]{2,1,0:T(8,128)} %bitcast.150), kind=kLoop, calls=%fused_computation.4 | loop fusion | flops 3139584 | bytes 3170304 | tf_op jit(solution)/shard_map/reduce_sum | solution.py:174
  19.8 1.5 %convert_bitcast_fusion.3 = bf16[12,256,256,1]{2,1,0,3:T(8,128)(2,1)} fusion(s32[12,256,256]{2,1,0:T(8,128)S(1)} %bitcast.151), kind=kLoop, calls=%fused_computation.204 | loop fusion | flops 786432 | bytes 4718592 | tf_op jit(solution)/shard_map/convert_element_type | solution.py:166
  24.4 0.8 fusion.55
  25.5 2.7 %fusion = bf16[256,256,3,4]{1,3,2,0:T(4,128)(2,1)S(1)} fusion(bf16[12,256,256,1]{2,1,0,3:T(8,128)(2,1)} %convert_bitcast_fusion.3, pred[12,4]{0,1:T(4,128)(4,1)S(1)} %copy-done.21, pred[12,3]{0,1:T(4,128)(4,1)S(1)} %copy-done.25), kind=kOutput, calls=%fused_computation.5 | convolution fusion | flops 18874512 | bytes 3145812 | tf_op jit(solution)/shard_map/trc,tij->cjri/dot_general | solution.py:170
  28.2 1.7 %copy.32 = bf16[4,256,3,256]{1,0,3,2:T(4,128)(2,1)} copy(bf16[4,256,3,256]{1,0,2,3:T(4,128)(2,1)S(1)} %bitcast.148) | data formatting | bytes 3145728 | tf_op jit(solution)/shard_map/trc,tij->cjri/transpose | solution.py:170
  29.9 3.8 %reshape_reshape.21 = bf16[1024,2,384]{0,2,1:T(8,128)(2,1)} reshape(bf16[4,256,3,256]{1,0,3,2:T(4,128)(2,1)} %copy.32) | data formatting | bytes 3145728 | tf_op jit(solution)/shard_map/reshape;reshape | solution.py:150
  33.7 2.6 %copy.33 = bf16[1024,2,384]{2,0,1:T(8,128)(2,1)} copy(bf16[1024,2,384]{0,2,1:T(8,128)(2,1)} %reshape_reshape.21) | data formatting | bytes 3145728 | tf_op jit(solution)/shard_map/reshape;reshape | solution.py:150
  36.3 3.3 %gather_fusion = bf16[2,1024,384]{2,1,0:T(8,128)(2,1)} fusion(bf16[1024,2,384]{2,0,1:T(8,128)(2,1)} %copy.33, s32[1024]{0:T(1024)S(1)} %pad_clamp_fusion), kind=kCustom, calls=%fused_computation | custom fusion | bytes 3145736 | tf_op jit(solution)/shard_map/jit(_take)/gather | solution.py:150
  39.6 2.8 %select_bitcast_fusion = bf16[1024,2,384]{2,0,1:T(8,128)(2,1)} fusion(bf16[2,1024,384]{2,1,0:T(8,128)(2,1)} %gather_fusion, pred[2]{0:T(512)(128)(4,1)S(1)} %compare_and_fusion), kind=kLoop, calls=%fused_computation.7 | loop fusion | flops 786432 | bytes 3145730 | tf_op jit(solution)/shard_map/jit(_take)/select_n | solution.py:150
  42.4 1.7 %copy.38 = bf16[3,256,4,256]{3,2,1,0:T(4,128)(2,1)} copy(bf16[3,256,4,256]{3,2,0,1:T(4,128)(2,1)S(1)} %bitcast.149) | data formatting | bytes 3145728 | tf_op jit(solution)/shard_map/trc,tij->ricj/transpose | solution.py:167
  44.1 2.8 %reshape_reshape.24 = bf16[2,384,1024]{2,1,0:T(8,128)(2,1)S(1)} reshape(bf16[3,256,4,256]{3,2,1,0:T(4,128)(2,1)} %copy.38) | data formatting | bytes 3145728 | tf_op jit(solution)/shard_map/reshape;reshape | solution.py:150
  46.9 1.8 %gather_fusion.1 = bf16[2,384,1024]{2,1,0:T(8,128)(2,1)} fusion(bf16[2,384,1024]{2,1,0:T(8,128)(2,1)S(1)} %reshape_reshape.24, s32[1024]{0:T(1024)S(1)} %pad_clamp_fusion), kind=kCustom, calls=%fused_computation.1 | custom fusion | bytes 3145736 | tf_op jit(solution)/shard_map/jit(_take)/gather | solution.py:150
  48.7 2.9 %broadcast_select_fusion = bf16[2,384,1024]{2,1,0:T(8,128)(2,1)} fusion(bf16[2,384,1024]{2,1,0:T(8,128)(2,1)} %gather_fusion.1, pred[2]{0:T(512)(128)(4,1)S(1)} %compare_and_fusion), kind=kLoop, calls=%fused_computation.8 | loop fusion | flops 786432 | bytes 3145730 | tf_op jit(solution)/shard_map/jit(_take)/select_n | solution.py:150
  52.1 1.6 %copy.34 = bf16[1024,2,384]{0,2,1:T(8,128)(2,1)} copy(bf16[1024,2,384]{2,0,1:T(8,128)(2,1)S(1)} %copy-done.3) | data formatting | bytes 3145728 | tf_op jit(solution)/shard_map/jit(_take)/select_n | solution.py:150
  53.8 1.0 select_bitcast_fusion.8
  55.0 1.5 %copy-done.5 = bf16[1024,2,384]{0,2,1:T(8,128)(2,1)S(1)} copy-done((bf16[1024,2,384]{0,2,1:T(8,128)(2,1)S(1)}, bf16[1024,2,384]{0,2,1:T(8,128)(2,1)}, u32[]{:S(2)}) %copy-start.5) | copy-done | bytes 1572888
  56.6 1.7 %fusion.2 = (f32[256]{0:T(256)S(1)}, f32[1024,256]{1,0:T(8,128)}) fusion(bf16[4,4,64,256]{3,2,1,0:T(8,128)(2,1)S(1)} %copy.35, bf16[1024,256]{1,0:T(8,128)(2,1)S(1)} %bitcast.166, f32[1024]{0:T(1024)S(1)} %bitcast.184, bf16[1024,768]{0,1:T(8,128)(2,1)S(1)} %bitcast.154, bf16[768,256]{1,0:T(8,128)(2,1)S(1)} %bitcast.178), kind=kOutput, calls=%fused_computation.17 | convolution fusion | flops 404225792 | bytes 4068352 | tf_op jit(solution)/shard_map/dot_general | solution.py:186
  58.5 1.9 %fusion.4 = (f32[256]{0:T(256)S(1)}, f32[768,256]{1,0:T(8,128)S(1)}) fusion(bf16[1,2,384,256]{3,2,1,0:T(8,128)(2,1)} %copy-done.15, bf16[768,256]{1,0:T(8,128)(2,1)} %bitcast.179, f32[768]{0:T(1024)S(1)} %copy-done.17, bf16[768,1024]{1,0:T(8,128)(2,1)S(1)} %bitcast.156, bf16[1024,256]{1,0:T(8,128)(2,1)} %bitcast.167), kind=kOutput, calls=%fused_computation.23 | convolution fusion | flops 403832576 | bytes 3674112 | tf_op jit(solution)/shard_map/dot_general | solution.py:184
  60.8 1.2 dynamic-slice_convert_fusion.5
  62.0 1.6 %collective-permute-start.7 = (bf16[259,256]{1,0:T(8,128)(2,1)S(1)}, bf16[259,256]{1,0:T(8,128)(2,1)S(1)}, u32[]{:S(2)}, u32[]{:S(2)}) collective-permute-start(bf16[259,256]{1,0:T(8,128)(2,1)S(1)} %get-tuple-element.85), channel_id=1, source_target_pairs={{0,2},{2,0},{4,6},{6,4},{8,10},{10,8},{12,14},{14,12},{16,18},{18,... | collective-permute-start | bytes 397832 | tf_op jit(solution)/shard_map/ppermute | solution.py:45
  63.5 1.5 %collective-permute-start.8 = (bf16[259,256]{1,0:T(8,128)(2,1)S(1)}, bf16[259,256]{1,0:T(8,128)(2,1)S(1)}, u32[]{:S(2)}, u32[]{:S(2)}) collective-permute-start(bf16[259,256]{1,0:T(8,128)(2,1)S(1)} %get-tuple-element.86), channel_id=1, source_target_pairs={{0,4},{2,6},{4,0},{6,2},{8,12},{10,14},{12,8},{14,10},{16,20},{18,... | collective-permute-start | bytes 397832 | tf_op jit(solution)/shard_map/ppermute | solution.py:45
  65.6 1.0 constant_dynamic-slice_fusion.1
  66.6 1.4 %collective-permute-done.7 = bf16[259,256]{1,0:T(8,128)(2,1)S(1)} collective-permute-done((bf16[259,256]{1,0:T(8,128)(2,1)S(1)}, bf16[259,256]{1,0:T(8,128)(2,1)S(1)}, u32[]{:S(2)}, u32[]{:S(2)}) %collective-permute-start.7) | collective-permute-done | bytes 132640 | tf_op jit(solution)/shard_map/ppermute | solution.py:45
  68.0 3.4 %collective-permute-done.8 = bf16[259,256]{1,0:T(8,128)(2,1)S(1)} collective-permute-done((bf16[259,256]{1,0:T(8,128)(2,1)S(1)}, bf16[259,256]{1,0:T(8,128)(2,1)S(1)}, u32[]{:S(2)}, u32[]{:S(2)}) %collective-permute-start.8) | collective-permute-done | bytes 132640 | tf_op jit(solution)/shard_map/ppermute | solution.py:45
  71.8 3.5 %collective-permute-start.11 = (bf16[67,256]{1,0:T(8,128)(2,1)S(1)}, bf16[67,256]{1,0:T(8,128)(2,1)S(1)}, u32[]{:S(2)}, u32[]{:S(2)}) collective-permute-start(bf16[67,256]{1,0:T(8,128)(2,1)S(1)} %get-tuple-element.83), channel_id=1, source_target_pairs={{0,16},{2,18},{4,20},{6,22},{8,24},{10,26},{12,28},{14,30},{16,0},... | collective-permute-start | bytes 102920 | tf_op jit(solution)/shard_map/ppermute | solution.py:45
  75.3 0.8 collective-permute-start.12
  76.1 1.2 collective-permute-done.11
  77.3 3.8 %collective-permute-done.12 = bf16[67,256]{1,0:T(8,128)(2,1)S(1)} collective-permute-done((bf16[67,256]{1,0:T(8,128)(2,1)S(1)}, bf16[67,256]{1,0:T(8,128)(2,1)S(1)}, u32[]{:S(2)}, u32[]{:S(2)}) %collective-permute-start.12) | collective-permute-done | bytes 34336 | tf_op jit(solution)/shard_map/ppermute | solution.py:45
  81.2 1.1 collective-permute-done.13
  83.2 1.3 %collective-permute-start.17 = (bf16[1,64,256]{2,1,0:T(8,128)(2,1)S(1)}, bf16[1,64,256]{2,1,0:T(8,128)(2,1)S(1)}, u32[]{:S(2)}, u32[]{:S(2)}) collective-permute-start(bf16[1,64,256]{2,1,0:T(8,128)(2,1)S(1)} %get-tuple-element.34), channel_id=1, source_target_pairs={{0,16},{2,18},{4,20},{6,22},{8,24},{10,26},{12,28},{14,30},{16,0},... | collective-permute-start | bytes 98312 | tf_op jit(solution)/shard_map/ppermute | solution.py:45
  84.5 3.1 %collective-permute-start.16 = (bf16[1,64,256]{2,1,0:T(8,128)(2,1)S(1)}, bf16[1,64,256]{2,1,0:T(8,128)(2,1)S(1)}, u32[]{:S(2)}, u32[]{:S(2)}) collective-permute-start(bf16[1,64,256]{2,1,0:T(8,128)(2,1)S(1)} %get-tuple-element.34), channel_id=1, source_target_pairs={{0,24},{2,26},{4,28},{6,30},{8,16},{10,18},{12,20},{14,22},{16,8},... | collective-permute-start | bytes 98312 | tf_op jit(solution)/shard_map/ppermute | solution.py:45
  87.6 0.8 convert_bitcast_fusion.1
  89.1 1.2 collective-permute-done.16
  90.9 0.7 collective-permute-start.21
  91.7 0.8 collective-permute-start.20
  92.5 1.9 %collective-permute-start.19 = (bf16[4,64,256]{2,1,0:T(8,128)(2,1)}, bf16[4,64,256]{2,1,0:T(8,128)(2,1)}, u32[]{:S(2)}, u32[]{:S(2)}) collective-permute-start(bf16[4,64,256]{2,1,0:T(8,128)(2,1)} %maximum_bitcast_fusion.1), channel_id=1, source_target_pairs={{0,6},{2,4},{4,2},{6,0},{8,14},{10,12},{12,10},{14,8},{16,22},{18,... | collective-permute-start | bytes 393224 | tf_op jit(solution)/shard_map/ppermute | solution.py:45
  95.5 0.8 fusion.57
  97.3 2.4 %collective-permute-done.20 = bf16[4,64,256]{2,1,0:T(8,128)(2,1)} collective-permute-done((bf16[4,64,256]{2,1,0:T(8,128)(2,1)}, bf16[4,64,256]{2,1,0:T(8,128)(2,1)}, u32[]{:S(2)}, u32[]{:S(2)}) %collective-permute-start.20) | collective-permute-done | bytes 131104 | tf_op jit(solution)/shard_map/ppermute | solution.py:45
  99.8 1.2 select_bitcast_fusion.4
  101.1 1.1 pad_maximum_fusion.3
  102.4 1.5 %fusion.5 = (f32[256]{0:T(256)S(1)}, f32[768,256]{1,0:T(8,128)}) fusion(bf16[1,2,384,256]{3,2,1,0:T(8,128)(2,1)S(1)} %pad_maximum_fusion.3, bf16[768,256]{1,0:T(8,128)(2,1)S(1)} %bitcast.180, f32[768]{0:T(1024)S(1)} %copy-done.18, bf16[768,1024]{1,0:T(8,128)(2,1)S(1)} %bitcast.157, bf16[1024,256]{1,0:T(8,128)(2,1)S(1)} %bitcast.164), kind=kOutput, calls=%fused_computation.24 | convolution fusion | flops 403832576 | bytes 3674112 | tf_op jit(solution)/shard_map/dot_general | solution.py:184
  103.9 1.7 %fusion.3 = (f32[256]{0:T(256)S(1)}, f32[1024,256]{1,0:T(8,128)}) fusion(bf16[4,4,64,256]{3,2,1,0:T(8,128)(2,1)S(1)} %copy.39, bf16[1024,256]{1,0:T(8,128)(2,1)S(1)} %bitcast.165, f32[1024]{0:T(1024)S(1)} %bitcast.185, bf16[1024,768]{0,1:T(8,128)(2,1)S(1)} %bitcast.155, bf16[768,256]{1,0:T(8,128)(2,1)S(1)} %bitcast.181), kind=kOutput, calls=%fused_computation.18 | convolution fusion | flops 404225792 | bytes 4068352 | tf_op jit(solution)/shard_map/dot_general | solution.py:186
  106.1 1.2 dynamic-slice_convert_fusion.2
  107.3 1.4 %collective-permute-start.22 = (bf16[259,256]{1,0:T(8,128)(2,1)S(1)}, bf16[259,256]{1,0:T(8,128)(2,1)S(1)}, u32[]{:S(2)}, u32[]{:S(2)}) collective-permute-start(bf16[259,256]{1,0:T(8,128)(2,1)S(1)} %get-tuple-element.79), channel_id=1, source_target_pairs={{0,2},{2,0},{4,6},{6,4},{8,10},{10,8},{12,14},{14,12},{16,18},{18,... | collective-permute-start | bytes 397832 | tf_op jit(solution)/shard_map/ppermute | solution.py:45
  108.7 0.9 collective-permute-start.23
  109.6 1.3 %collective-permute-start.24 = (bf16[259,256]{1,0:T(8,128)(2,1)S(1)}, bf16[259,256]{1,0:T(8,128)(2,1)S(1)}, u32[]{:S(2)}, u32[]{:S(2)}) collective-permute-start(bf16[259,256]{1,0:T(8,128)(2,1)S(1)} %get-tuple-element.81), channel_id=1, source_target_pairs={{0,6},{2,4},{4,2},{6,0},{8,14},{10,12},{12,10},{14,8},{16,22},{18,... | collective-permute-start | bytes 397832 | tf_op jit(solution)/shard_map/ppermute | solution.py:45
  110.9 1.7 %slice.242 = bf16[384,256]{1,0:T(8,128)(2,1)} slice(f32[768,256]{1,0:T(8,128)} %get-tuple-element.105), slice={[384:768], [0:256]} | slice | bytes 393216 | tf_op jit(solution)/shard_map/slice | solution.py:80
  112.6 1.1 constant_dynamic-slice_fusion
  113.7 2.0 %collective-permute-done.23 = bf16[259,256]{1,0:T(8,128)(2,1)S(1)} collective-permute-done((bf16[259,256]{1,0:T(8,128)(2,1)S(1)}, bf16[259,256]{1,0:T(8,128)(2,1)S(1)}, u32[]{:S(2)}, u32[]{:S(2)}) %collective-permute-start.23) | collective-permute-done | bytes 132640 | tf_op jit(solution)/shard_map/ppermute | solution.py:45
  116.0 2.9 %collective-permute-start.26 = (bf16[67,256]{1,0:T(8,128)(2,1)S(1)}, bf16[67,256]{1,0:T(8,128)(2,1)S(1)}, u32[]{:S(2)}, u32[]{:S(2)}) collective-permute-start(bf16[67,256]{1,0:T(8,128)(2,1)S(1)} %get-tuple-element.77), channel_id=1, source_target_pairs={{0,16},{2,18},{4,20},{6,22},{8,24},{10,26},{12,28},{14,30},{16,0},... | collective-permute-start | bytes 102920 | tf_op jit(solution)/shard_map/ppermute | solution.py:45
  118.9 1.5 %collective-permute-start.27 = (bf16[67,256]{1,0:T(8,128)(2,1)S(1)}, bf16[67,256]{1,0:T(8,128)(2,1)S(1)}, u32[]{:S(2)}, u32[]{:S(2)}) collective-permute-start(bf16[67,256]{1,0:T(8,128)(2,1)S(1)} %get-tuple-element.78), channel_id=1, source_target_pairs={{0,24},{2,26},{4,28},{6,30},{8,16},{10,18},{12,20},{14,22},{16,8},... | collective-permute-start | bytes 102920 | tf_op jit(solution)/shard_map/ppermute | solution.py:45
  120.9 3.7 %collective-permute-done.27 = bf16[67,256]{1,0:T(8,128)(2,1)S(1)} collective-permute-done((bf16[67,256]{1,0:T(8,128)(2,1)S(1)}, bf16[67,256]{1,0:T(8,128)(2,1)S(1)}, u32[]{:S(2)}, u32[]{:S(2)}) %collective-permute-start.27) | collective-permute-done | bytes 34336 | tf_op jit(solution)/shard_map/ppermute | solution.py:45
  124.7 1.1 collective-permute-done.28
  126.9 2.2 %fusion.11 = (f32[1,384,256]{2,1,0:T(8,128)}, f32[1,384,256]{2,1,0:T(8,128)}) fusion(f32[384,256]{1,0:T(8,128)S(1)} %get-tuple-element.16, f32[384,256]{1,0:T(8,128)S(1)} %reshape.445, f32[768,256]{1,0:T(8,128)} %get-tuple-element.105, bf16[384,256]{1,0:T(8,128)(2,1)} %collective-permute-done.29, f32[256]{0:T(256)S(1)} %mul.209, f32[256]{0:T(256)S(1)} %mul.207, ...), kind=kLoop, calls=%fused_computation.34 | loop fusion | flops 1671168 | bytes 3542016 | tf_op jit(solution)/shard_map/broadcast_in_dim | solution.py:249
  (191 shorter events, 14.1 us)
Async XLA Ops:
  0.6 23.8 %copy-start = (f32[64,64]{1,0:T(8,128)S(1)}, f32[64,64]{1,0:T(8,128)}, u32[]{:S(2)}) copy-start(f32[64,64]{1,0:T(8,128)} %param.9) | copy-start | bytes 49156
  1.5 10.6 %collective-permute-start.2 = (bf16[1,64,256]{2,1,0:T(8,128)(2,1)S(1)}, bf16[1,64,256]{2,1,0:T(8,128)(2,1)S(1)}, u32[]{:S(2)}, u32[]{:S(2)}) collective-permute-start(bf16[1,64,256]{2,1,0:T(8,128)(2,1)S(1)} %convert_element_type.273), channel_id=1, source_target_pairs={{0,8},{2,10},{4,12},{6,14},{8,0},{10,2},{12,4},{14,6},{16,24},{18,... | collective-permute-start | bytes 98312 | tf_op jit(solution)/shard_map/ppermute | solution.py:45
  4.5 7.5 %collective-permute-start.1 = (bf16[1,64,256]{2,1,0:T(8,128)(2,1)S(1)}, bf16[1,64,256]{2,1,0:T(8,128)(2,1)S(1)}, u32[]{:S(2)}, u32[]{:S(2)}) collective-permute-start(bf16[1,64,256]{2,1,0:T(8,128)(2,1)S(1)} %convert_element_type.273), channel_id=1, source_target_pairs={{0,16},{2,18},{4,20},{6,22},{8,24},{10,26},{12,28},{14,30},{16,0},... | collective-permute-start | bytes 98312 | tf_op jit(solution)/shard_map/ppermute | solution.py:45
  7.1 5.7 %collective-permute-start = (bf16[1,64,256]{2,1,0:T(8,128)(2,1)S(1)}, bf16[1,64,256]{2,1,0:T(8,128)(2,1)S(1)}, u32[]{:S(2)}, u32[]{:S(2)}) collective-permute-start(bf16[1,64,256]{2,1,0:T(8,128)(2,1)S(1)} %convert_element_type.273), channel_id=1, source_target_pairs={{0,24},{2,26},{4,28},{6,30},{8,16},{10,18},{12,20},{14,22},{16,8},... | collective-permute-start | bytes 98312 | tf_op jit(solution)/shard_map/ppermute | solution.py:45
  8.8 46.2 %collective-permute-start.3 = (bf16[1,384,256]{2,1,0:T(8,128)(2,1)}, bf16[1,384,256]{2,1,0:T(8,128)(2,1)S(1)}, u32[]{:S(2)}, u32[]{:S(2)}) collective-permute-start(bf16[1,384,256]{2,1,0:T(8,128)(2,1)} %convert_element_type.275), channel_id=1, source_target_pairs={{0,1},{1,0},{2,3},{3,2},{4,5},{5,4},{6,7},{7,6},{8,9},{9,8},{10,11... | collective-permute-start | bytes 589832 | tf_op jit(solution)/shard_map/ppermute | solution.py:45
  11.3 10.1 %copy-start.24 = (pred[12,3]{0,1:T(4,128)(4,1)}, pred[12,3]{0,1:T(4,128)(4,1)S(1)}, u32[]{:S(2)}) copy-start(pred[12,3]{0,1:T(4,128)(4,1)S(1)} %fusion.43) | copy-start | bytes 112
  13.7 6.0 %copy-start.2 = (s32[1,1,12,256,256]{4,3,2,1,0:T(8,128)S(1)}, s32[1,1,12,256,256]{4,3,2,1,0:T(8,128)}, u32[]{:S(2)}) copy-start(s32[1,1,12,256,256]{4,3,2,1,0:T(8,128)} %param.11) | copy-start | bytes 9437188
  13.7 40.0 %collective-permute-start.6 = (bf16[4,64,256]{2,1,0:T(8,128)(2,1)S(1)}, bf16[4,64,256]{2,1,0:T(8,128)(2,1)S(1)}, u32[]{:S(2)}, u32[]{:S(2)}) collective-permute-start(bf16[4,64,256]{2,1,0:T(8,128)(2,1)S(1)} %maximum_bitcast_fusion), channel_id=1, source_target_pairs={{0,2},{2,0},{4,6},{6,4},{8,10},{10,8},{12,14},{14,12},{16,18},{18,... | collective-permute-start | bytes 393224 | tf_op jit(solution)/shard_map/ppermute | solution.py:45
  15.3 38.5 %collective-permute-start.5 = (bf16[4,64,256]{2,1,0:T(8,128)(2,1)S(1)}, bf16[4,64,256]{2,1,0:T(8,128)(2,1)}, u32[]{:S(2)}, u32[]{:S(2)}) collective-permute-start(bf16[4,64,256]{2,1,0:T(8,128)(2,1)S(1)} %maximum_bitcast_fusion), channel_id=1, source_target_pairs={{0,4},{2,6},{4,0},{6,2},{8,12},{10,14},{12,8},{14,10},{16,20},{18,... | collective-permute-start | bytes 393224 | tf_op jit(solution)/shard_map/ppermute | solution.py:45
  16.8 37.0 %collective-permute-start.4 = (bf16[4,64,256]{2,1,0:T(8,128)(2,1)S(1)}, bf16[4,64,256]{2,1,0:T(8,128)(2,1)}, u32[]{:S(2)}, u32[]{:S(2)}) collective-permute-start(bf16[4,64,256]{2,1,0:T(8,128)(2,1)S(1)} %maximum_bitcast_fusion), channel_id=1, source_target_pairs={{0,6},{2,4},{4,2},{6,0},{8,14},{10,12},{12,10},{14,8},{16,22},{18,... | collective-permute-start | bytes 393224 | tf_op jit(solution)/shard_map/ppermute | solution.py:45
  19.8 3.0 %copy-start.4 = (f32[1,64,256]{2,1,0:T(8,128)S(1)}, f32[1,64,256]{2,1,0:T(8,128)}, u32[]{:S(2)}) copy-start(f32[1,64,256]{2,1,0:T(8,128)} %param.8) | copy-start | bytes 196612
  19.8 3.1 %copy-start.16 = (f32[64,64]{1,0:T(8,128)S(1)}, f32[64,64]{1,0:T(8,128)}, u32[]{:S(2)}) copy-start(f32[64,64]{1,0:T(8,128)} %param.10) | copy-start | bytes 49156
  19.8 4.4 %copy-start.1 = (f32[1,384,256]{2,1,0:T(8,128)S(1)}, f32[1,384,256]{2,1,0:T(8,128)}, u32[]{:S(2)}) copy-start(f32[1,384,256]{2,1,0:T(8,128)} %param.7) | copy-start | bytes 1179652
  21.4 33.6 %copy-start.19 = (f32[1,2,4,128]{3,1,2,0:T(2,128)}, f32[1,2,4,128]{3,1,2,0:T(2,128)S(1)}, u32[]{:S(2)}) copy-start(f32[1,2,4,128]{3,1,2,0:T(2,128)S(1)} %copy.49) | copy-start | bytes 12292
  24.4 1.0 copy-start.21
  24.4 1.0 copy-start.25
  48.7 3.4 %copy-start.3 = (bf16[1024,2,384]{2,0,1:T(8,128)(2,1)S(1)}, bf16[1024,2,384]{2,0,1:T(8,128)(2,1)}, u32[]{:S(2)}) copy-start(bf16[1024,2,384]{2,0,1:T(8,128)(2,1)} %select_bitcast_fusion) | copy-start | bytes 4718596
  54.8 1.7 %copy-start.5 = (bf16[1024,2,384]{0,2,1:T(8,128)(2,1)S(1)}, bf16[1024,2,384]{0,2,1:T(8,128)(2,1)}, u32[]{:S(2)}) copy-start(bf16[1024,2,384]{0,2,1:T(8,128)(2,1)} %copy.34) | copy-start | bytes 4718596
  54.9 3.3 %copy-start.14 = (bf16[4,4,64,256]{3,2,1,0:T(8,128)(2,1)}, bf16[4,4,64,256]{3,2,1,0:T(8,128)(2,1)S(1)}, u32[]{:S(2)}) copy-start(bf16[4,4,64,256]{3,2,1,0:T(8,128)(2,1)S(1)} %copy.35) | copy-start | bytes 1572868
  55.0 3.3 %copy-start.15 = (bf16[1,2,384,256]{3,2,1,0:T(8,128)(2,1)}, bf16[1,2,384,256]{3,2,1,0:T(8,128)(2,1)S(1)}, u32[]{:S(2)}) copy-start(bf16[1,2,384,256]{3,2,1,0:T(8,128)(2,1)S(1)} %pad_maximum_fusion.2) | copy-start | bytes 1179652
  56.6 2.0 %copy-start.7 = (bf16[2,384,1024]{2,1,0:T(8,128)(2,1)S(1)}, bf16[2,384,1024]{2,1,0:T(8,128)(2,1)}, u32[]{:S(2)}) copy-start(bf16[2,384,1024]{2,1,0:T(8,128)(2,1)} %broadcast_select_fusion) | copy-start | bytes 4718596
  56.6 2.0 %copy-start.17 = (f32[768]{0:T(1024)S(1)}, f32[768]{0:T(1024)}, u32[]{:S(2)}) copy-start(f32[768]{0:T(1024)} %select_n.426) | copy-start | bytes 9220
  58.5 2.1 %copy-start.26 = (f32[4]{0:T(128)S(1)}, f32[4]{0:T(128)}, u32[]{:S(2)}) copy-start(f32[4]{0:T(128)} %reduce_sum.195) | copy-start | bytes 52
  60.4 27.2 %copy-start.9 = (f32[768,256]{1,0:T(8,128)}, f32[768,256]{1,0:T(8,128)S(1)}, u32[]{:S(2)}) copy-start(f32[768,256]{1,0:T(8,128)S(1)} %get-tuple-element.101) | copy-start | bytes 2359300
  62.0 6.0 %collective-permute-start.7 = (bf16[259,256]{1,0:T(8,128)(2,1)S(1)}, bf16[259,256]{1,0:T(8,128)(2,1)S(1)}, u32[]{:S(2)}, u32[]{:S(2)}) collective-permute-start(bf16[259,256]{1,0:T(8,128)(2,1)S(1)} %get-tuple-element.85), channel_id=1, source_target_pairs={{0,2},{2,0},{4,6},{6,4},{8,10},{10,8},{12,14},{14,12},{16,18},{18,... | collective-permute-start | bytes 397832 | tf_op jit(solution)/shard_map/ppermute | solution.py:45
  63.5 7.9 %collective-permute-start.8 = (bf16[259,256]{1,0:T(8,128)(2,1)S(1)}, bf16[259,256]{1,0:T(8,128)(2,1)S(1)}, u32[]{:S(2)}, u32[]{:S(2)}) collective-permute-start(bf16[259,256]{1,0:T(8,128)(2,1)S(1)} %get-tuple-element.86), channel_id=1, source_target_pairs={{0,4},{2,6},{4,0},{6,2},{8,12},{10,14},{12,8},{14,10},{16,20},{18,... | collective-permute-start | bytes 397832 | tf_op jit(solution)/shard_map/ppermute | solution.py:45
  65.0 6.4 %collective-permute-start.9 = (bf16[259,256]{1,0:T(8,128)(2,1)S(1)}, bf16[259,256]{1,0:T(8,128)(2,1)S(1)}, u32[]{:S(2)}, u32[]{:S(2)}) collective-permute-start(bf16[259,256]{1,0:T(8,128)(2,1)S(1)} %get-tuple-element.87), channel_id=1, source_target_pairs={{0,6},{2,4},{4,2},{6,0},{8,14},{10,12},{12,10},{14,8},{16,22},{18,... | collective-permute-start | bytes 397832 | tf_op jit(solution)/shard_map/ppermute | solution.py:45
  65.5 22.0 %collective-permute-start.14 = (bf16[384,256]{1,0:T(8,128)(2,1)S(1)}, bf16[384,256]{1,0:T(8,128)(2,1)S(1)}, u32[]{:S(2)}, u32[]{:S(2)}) collective-permute-start(bf16[384,256]{1,0:T(8,128)(2,1)S(1)} %slice.243), channel_id=1, source_target_pairs={{0,1},{1,0},{2,3},{3,2},{4,5},{5,4},{6,7},{7,6},{8,9},{9,8},{10,11... | collective-permute-start | bytes 589832 | tf_op jit(solution)/shard_map/ppermute | solution.py:45
  71.6 4.5 %collective-permute-start.10 = (bf16[67,256]{1,0:T(8,128)(2,1)S(1)}, bf16[67,256]{1,0:T(8,128)(2,1)S(1)}, u32[]{:S(2)}, u32[]{:S(2)}) collective-permute-start(bf16[67,256]{1,0:T(8,128)(2,1)S(1)} %get-tuple-element.82), channel_id=1, source_target_pairs={{0,8},{2,10},{4,12},{6,14},{8,0},{10,2},{12,4},{14,6},{16,24},{18,... | collective-permute-start | bytes 102920 | tf_op jit(solution)/shard_map/ppermute | solution.py:45
  71.8 5.4 %collective-permute-start.11 = (bf16[67,256]{1,0:T(8,128)(2,1)S(1)}, bf16[67,256]{1,0:T(8,128)(2,1)S(1)}, u32[]{:S(2)}, u32[]{:S(2)}) collective-permute-start(bf16[67,256]{1,0:T(8,128)(2,1)S(1)} %get-tuple-element.83), channel_id=1, source_target_pairs={{0,16},{2,18},{4,20},{6,22},{8,24},{10,26},{12,28},{14,30},{16,0},... | collective-permute-start | bytes 102920 | tf_op jit(solution)/shard_map/ppermute | solution.py:45
  75.3 5.8 %collective-permute-start.12 = (bf16[67,256]{1,0:T(8,128)(2,1)S(1)}, bf16[67,256]{1,0:T(8,128)(2,1)S(1)}, u32[]{:S(2)}, u32[]{:S(2)}) collective-permute-start(bf16[67,256]{1,0:T(8,128)(2,1)S(1)} %get-tuple-element.84), channel_id=1, source_target_pairs={{0,24},{2,26},{4,28},{6,30},{8,16},{10,18},{12,20},{14,22},{16,8},... | collective-permute-start | bytes 102920 | tf_op jit(solution)/shard_map/ppermute | solution.py:45
  81.1 1.2 collective-permute-start.13
  82.3 0.5 copy-start.22
  83.1 5.9 %collective-permute-start.18 = (bf16[1,64,256]{2,1,0:T(8,128)(2,1)S(1)}, bf16[1,64,256]{2,1,0:T(8,128)(2,1)S(1)}, u32[]{:S(2)}, u32[]{:S(2)}) collective-permute-start(bf16[1,64,256]{2,1,0:T(8,128)(2,1)S(1)} %get-tuple-element.34), channel_id=1, source_target_pairs={{0,8},{2,10},{4,12},{6,14},{8,0},{10,2},{12,4},{14,6},{16,24},{18,... | collective-permute-start | bytes 98312 | tf_op jit(solution)/shard_map/ppermute | solution.py:45
  83.2 5.9 %collective-permute-start.17 = (bf16[1,64,256]{2,1,0:T(8,128)(2,1)S(1)}, bf16[1,64,256]{2,1,0:T(8,128)(2,1)S(1)}, u32[]{:S(2)}, u32[]{:S(2)}) collective-permute-start(bf16[1,64,256]{2,1,0:T(8,128)(2,1)S(1)} %get-tuple-element.34), channel_id=1, source_target_pairs={{0,16},{2,18},{4,20},{6,22},{8,24},{10,26},{12,28},{14,30},{16,0},... | collective-permute-start | bytes 98312 | tf_op jit(solution)/shard_map/ppermute | solution.py:45
  84.5 5.7 %collective-permute-start.16 = (bf16[1,64,256]{2,1,0:T(8,128)(2,1)S(1)}, bf16[1,64,256]{2,1,0:T(8,128)(2,1)S(1)}, u32[]{:S(2)}, u32[]{:S(2)}) collective-permute-start(bf16[1,64,256]{2,1,0:T(8,128)(2,1)S(1)} %get-tuple-element.34), channel_id=1, source_target_pairs={{0,24},{2,26},{4,28},{6,30},{8,16},{10,18},{12,20},{14,22},{16,8},... | collective-permute-start | bytes 98312 | tf_op jit(solution)/shard_map/ppermute | solution.py:45
  87.6 6.9 %copy-start.11 = (bf16[384,256]{1,0:T(8,128)(2,1)}, bf16[384,256]{1,0:T(8,128)(2,1)S(1)}, u32[]{:S(2)}) copy-start(bf16[384,256]{1,0:T(8,128)(2,1)S(1)} %collective-permute-done.14) | copy-start | bytes 589828
  89.1 12.0 %collective-permute-start.15 = (bf16[1,384,256]{2,1,0:T(8,128)(2,1)}, bf16[1,384,256]{2,1,0:T(8,128)(2,1)}, u32[]{:S(2)}, u32[]{:S(2)}) collective-permute-start(bf16[1,384,256]{2,1,0:T(8,128)(2,1)} %convert_bitcast_fusion), channel_id=1, source_target_pairs={{0,1},{1,0},{2,3},{3,2},{4,5},{5,4},{6,7},{7,6},{8,9},{9,8},{10,11... | collective-permute-start | bytes 589832 | tf_op jit(solution)/shard_map/ppermute | solution.py:45
  90.9 6.4 %collective-permute-start.21 = (bf16[4,64,256]{2,1,0:T(8,128)(2,1)}, bf16[4,64,256]{2,1,0:T(8,128)(2,1)}, u32[]{:S(2)}, u32[]{:S(2)}) collective-permute-start(bf16[4,64,256]{2,1,0:T(8,128)(2,1)} %maximum_bitcast_fusion.1), channel_id=1, source_target_pairs={{0,2},{2,0},{4,6},{6,4},{8,10},{10,8},{12,14},{14,12},{16,18},{18,... | collective-permute-start | bytes 393224 | tf_op jit(solution)/shard_map/ppermute | solution.py:45
  91.7 8.1 %collective-permute-start.20 = (bf16[4,64,256]{2,1,0:T(8,128)(2,1)}, bf16[4,64,256]{2,1,0:T(8,128)(2,1)}, u32[]{:S(2)}, u32[]{:S(2)}) collective-permute-start(bf16[4,64,256]{2,1,0:T(8,128)(2,1)} %maximum_bitcast_fusion.1), channel_id=1, source_target_pairs={{0,4},{2,6},{4,0},{6,2},{8,12},{10,14},{12,8},{14,10},{16,20},{18,... | collective-permute-start | bytes 393224 | tf_op jit(solution)/shard_map/ppermute | solution.py:45
  92.5 7.3 %collective-permute-start.19 = (bf16[4,64,256]{2,1,0:T(8,128)(2,1)}, bf16[4,64,256]{2,1,0:T(8,128)(2,1)}, u32[]{:S(2)}, u32[]{:S(2)}) collective-permute-start(bf16[4,64,256]{2,1,0:T(8,128)(2,1)} %maximum_bitcast_fusion.1), channel_id=1, source_target_pairs={{0,6},{2,4},{4,2},{6,0},{8,14},{10,12},{12,10},{14,8},{16,22},{18,... | collective-permute-start | bytes 393224 | tf_op jit(solution)/shard_map/ppermute | solution.py:45
  97.0 4.1 %copy-start.13 = (bf16[1,1,384,256]{3,2,1,0:T(8,128)(2,1)S(1)}, bf16[1,1,384,256]{3,2,1,0:T(8,128)(2,1)}, u32[]{:S(2)}) copy-start(bf16[1,1,384,256]{3,2,1,0:T(8,128)(2,1)} %get-tuple-element.32) | copy-start | bytes 589828
  100.9 1.5 %copy-start.8 = (bf16[2,384,1024]{2,1,0:T(8,128)(2,1)S(1)}, bf16[2,384,1024]{2,1,0:T(8,128)(2,1)}, u32[]{:S(2)}) copy-start(bf16[2,384,1024]{2,1,0:T(8,128)(2,1)} %broadcast_select_fusion) | copy-start | bytes 4718596
  100.9 1.5 %copy-start.18 = (f32[768]{0:T(1024)S(1)}, f32[768]{0:T(1024)}, u32[]{:S(2)}) copy-start(f32[768]{0:T(1024)} %select_n.426) | copy-start | bytes 9220
  102.4 1.5 %copy-start.6 = (bf16[1024,2,384]{0,2,1:T(8,128)(2,1)S(1)}, bf16[1024,2,384]{0,2,1:T(8,128)(2,1)}, u32[]{:S(2)}) copy-start(bf16[1024,2,384]{0,2,1:T(8,128)(2,1)} %copy.34) | copy-start | bytes 4718596
  102.4 1.5 %copy-start.20 = (f32[1,2,4,128]{3,1,2,0:T(2,128)S(1)}, f32[1,2,4,128]{3,1,2,0:T(2,128)}, u32[]{:S(2)}) copy-start(f32[1,2,4,128]{3,1,2,0:T(2,128)} %copy-done.19) | copy-start | bytes 12292
  107.3 6.3 %collective-permute-start.22 = (bf16[259,256]{1,0:T(8,128)(2,1)S(1)}, bf16[259,256]{1,0:T(8,128)(2,1)S(1)}, u32[]{:S(2)}, u32[]{:S(2)}) collective-permute-start(bf16[259,256]{1,0:T(8,128)(2,1)S(1)} %get-tuple-element.79), channel_id=1, source_target_pairs={{0,2},{2,0},{4,6},{6,4},{8,10},{10,8},{12,14},{14,12},{16,18},{18,... | collective-permute-start | bytes 397832 | tf_op jit(solution)/shard_map/ppermute | solution.py:45
  108.7 7.0 %collective-permute-start.23 = (bf16[259,256]{1,0:T(8,128)(2,1)S(1)}, bf16[259,256]{1,0:T(8,128)(2,1)S(1)}, u32[]{:S(2)}, u32[]{:S(2)}) collective-permute-start(bf16[259,256]{1,0:T(8,128)(2,1)S(1)} %get-tuple-element.80), channel_id=1, source_target_pairs={{0,4},{2,6},{4,0},{6,2},{8,12},{10,14},{12,8},{14,10},{16,20},{18,... | collective-permute-start | bytes 397832 | tf_op jit(solution)/shard_map/ppermute | solution.py:45
  109.6 6.1 %collective-permute-start.24 = (bf16[259,256]{1,0:T(8,128)(2,1)S(1)}, bf16[259,256]{1,0:T(8,128)(2,1)S(1)}, u32[]{:S(2)}, u32[]{:S(2)}) collective-permute-start(bf16[259,256]{1,0:T(8,128)(2,1)S(1)} %get-tuple-element.81), channel_id=1, source_target_pairs={{0,6},{2,4},{4,2},{6,0},{8,14},{10,12},{12,10},{14,8},{16,22},{18,... | collective-permute-start | bytes 397832 | tf_op jit(solution)/shard_map/ppermute | solution.py:45
  110.9 15.0 %copy-start.23 = (f32[8]{0:T(128)S(1)}, f32[8]{0:T(128)}, u32[]{:S(2)}) copy-start(f32[8]{0:T(128)} %copy-done.22) | copy-start | bytes 100
  112.6 14.3 %copy-start.10 = (f32[768,256]{1,0:T(8,128)S(1)}, f32[768,256]{1,0:T(8,128)}, u32[]{:S(2)}) copy-start(f32[768,256]{1,0:T(8,128)} %copy-done.9) | copy-start | bytes 2359300
  112.6 14.3 %copy-start.12 = (bf16[384,256]{1,0:T(8,128)(2,1)S(1)}, bf16[384,256]{1,0:T(8,128)(2,1)}, u32[]{:S(2)}) copy-start(bf16[384,256]{1,0:T(8,128)(2,1)} %copy-done.11) | copy-start | bytes 589828
  112.6 14.3 %collective-permute-start.29 = (bf16[384,256]{1,0:T(8,128)(2,1)}, bf16[384,256]{1,0:T(8,128)(2,1)}, u32[]{:S(2)}, u32[]{:S(2)}) collective-permute-start(bf16[384,256]{1,0:T(8,128)(2,1)} %slice.242), channel_id=1, source_target_pairs={{0,1},{1,0},{2,3},{3,2},{4,5},{5,4},{6,7},{7,6},{8,9},{9,8},{10,11... | collective-permute-start | bytes 589832 | tf_op jit(solution)/shard_map/ppermute | solution.py:45
  115.9 4.5 %collective-permute-start.25 = (bf16[67,256]{1,0:T(8,128)(2,1)S(1)}, bf16[67,256]{1,0:T(8,128)(2,1)S(1)}, u32[]{:S(2)}, u32[]{:S(2)}) collective-permute-start(bf16[67,256]{1,0:T(8,128)(2,1)S(1)} %get-tuple-element.76), channel_id=1, source_target_pairs={{0,8},{2,10},{4,12},{6,14},{8,0},{10,2},{12,4},{14,6},{16,24},{18,... | collective-permute-start | bytes 102920 | tf_op jit(solution)/shard_map/ppermute | solution.py:45
  116.0 4.9 %collective-permute-start.26 = (bf16[67,256]{1,0:T(8,128)(2,1)S(1)}, bf16[67,256]{1,0:T(8,128)(2,1)S(1)}, u32[]{:S(2)}, u32[]{:S(2)}) collective-permute-start(bf16[67,256]{1,0:T(8,128)(2,1)S(1)} %get-tuple-element.77), channel_id=1, source_target_pairs={{0,16},{2,18},{4,20},{6,22},{8,24},{10,26},{12,28},{14,30},{16,0},... | collective-permute-start | bytes 102920 | tf_op jit(solution)/shard_map/ppermute | solution.py:45
  118.9 5.8 %collective-permute-start.27 = (bf16[67,256]{1,0:T(8,128)(2,1)S(1)}, bf16[67,256]{1,0:T(8,128)(2,1)S(1)}, u32[]{:S(2)}, u32[]{:S(2)}) collective-permute-start(bf16[67,256]{1,0:T(8,128)(2,1)S(1)} %get-tuple-element.78), channel_id=1, source_target_pairs={{0,24},{2,26},{4,28},{6,30},{8,16},{10,18},{12,20},{14,22},{16,8},... | collective-permute-start | bytes 102920 | tf_op jit(solution)/shard_map/ppermute | solution.py:45
  124.7 1.2 collective-permute-start.28

commit v22 on v19

--- a/solution.py
+++ b/solution.py
@@ -76,7 +76,13 @@
         def block_of(value):
             out = buf
             for j in sorted(range(len(group)), key=lambda j: -left.index(group[j])):
-                out = lax.dynamic_index_in_dim(out, (value >> j) & 1, left.index(group[j]), keepdims=False)
+                pos = left.index(group[j])
+                upper = ((value >> j) & 1) == 1
+                out = jnp.where(
+                    upper,
+                    lax.index_in_dim(out, 1, pos, keepdims=False),
+                    lax.index_in_dim(out, 0, pos, keepdims=False),
+                )
             return out
 
         coded = extra is not None and first_type is not None

time: 103 us -> 99.9 us (0.970)
  matrix products: 11.6 us -> 9.22 us
  waiting for transfers between devices: 23.7 us -> 25.6 us
  local copies, waits for them, and re-layouts: 13.2 us -> 11.3 us
  other arithmetic: 18.8 us -> 17.7 us
    convert_element_type x6 -> x0, local copies, waits for them, and re-layouts: 4.1 us -> none  [halve_sum(): send = block_of(digit ^ k).astype(stage_type)]
    unnamed x49 -> x45, local copies, waits for them, and re-layouts: 2.38 us -> 6.48 us
    dot_general x2, matrix products: 3.36 us -> 1.19 us  [cross_parts(): jnp.dot(counts_bf, item_range, preferred_element_type=jnp.float32)]
    dynamic_slice x2 -> x0, local copies, waits for them, and re-layouts: 2.04 us -> none  [block_of(): lax.dynamic_index_in_dim(out, value >> j & 1, left.index(group[j]), keepd...]
    ppermute x30, waiting for transfers between devices: 23.7 us -> 25.6 us  [swap_with(): return lax.ppermute(value, axis, pairs)]
    broadcast_in_dim x2, other arithmetic: 2.93 us -> 1.76 us  [per_device(): return (sol_user[None], sol_item[None], res_user[None], res_item[None])]
  transfers between devices with their start and end apart: 30 -> 30, of which waited for: 15 -> 19; matrix products, arithmetic and copies ran while one was open for 27% -> 26% of each run, Pallas kernels for 0% -> 0%
where the time goes in v22:
time: 99.9 us; the launch traced here: 99.4 us
  starting transfers between devices  33.5 us (34%)
  waiting for transfers between devices  25.6 us (26%)
  other arithmetic  17.7 us (18%)
  local copies, waits for them, and re-layouts  11.3 us (11%)
  matrix products  9.22 us (9%)
  between operations  2.12 us (2%)
    ppermute x30, starting transfers between devices, swap_with(): return lax.ppermute(value, axis, pairs)  33.5 us
    ppermute x30, waiting for transfers between devices, swap_with(): return lax.ppermute(value, axis, pairs)  25.6 us
    unnamed x45, local copies, waits for them, and re-layouts  6.48 us
    another operation x10, other arithmetic, double_gather(): buf = jnp.stack(ordered, axis=1).reshape((-1,) + piece.shape)  4.46 us
    dot_general x2, matrix products, cross_parts(): to_items = jnp.dot(counts_t, user_range, preferred_element_type=jnp.float32)  3.31 us
    dot_general x1, matrix products, build_counts(): jnp.einsum('trc,tij->cjri', place, tiles_bf, preferred_element_type=jnp.b...  2.71 us
    reduce_sum x1, other arithmetic, build_counts(): tile_cols = jnp.sum(tiles_bf, axis=1, dtype=jnp.float32)  2.63 us
    dot_general x4, matrix products, prior_term(): mixed = jnp.dot(grouped, prior_mat, precision=top_prec)  2.01 us
  transfers between devices with their start and end apart: 30, of which 19 were waited for; matrix products, arithmetic and copies ran while one was open for 26% of the time, Pallas kernels for 0%

profile of v22, /device:TPU:0, one launch (start us, length us, event | category | flops | bytes accessed | tf_op | source)
XLA Modules:
  0.0 99.4 jit_solution(8655292027008865404)
XLA Ops:
  0.6 0.9 convert_element_type.273
  1.5 5.0 %collective-permute-start = (bf16[1,64,256]{2,1,0:T(8,128)(2,1)S(1)}, bf16[1,64,256]{2,1,0:T(8,128)(2,1)S(1)}, u32[]{:S(2)}, u32[]{:S(2)}) collective-permute-start(bf16[1,64,256]{2,1,0:T(8,128)(2,1)S(1)} %convert_element_type.273), channel_id=1, source_target_pairs={{0,24},{2,26},{4,28},{6,30},{8,16},{10,18},{12,20},{14,22},{16,8},... | collective-permute-start | bytes 98312 | tf_op jit(solution)/shard_map/ppermute | solution.py:45
  6.5 0.6 collective-permute-start.2
  7.2 1.7 %convert_element_type.275 = bf16[1,384,256]{2,1,0:T(8,128)(2,1)} convert(f32[1,384,256]{2,1,0:T(8,128)} %param.7) | non-fusion elementwise | flops 98304 | bytes 589824 | tf_op jit(solution)/shard_map/convert_element_type | solution.py:174
  8.9 0.8 slice_bitcast_fusion.3
  10.5 0.8 collective-permute-done.1
  11.4 0.9 select_bitcast_fusion.24
  12.3 2.6 %convert_reduce_fusion.1 = (f32[12,256]{1,0:T(8,128)S(1)}, f32[12,256]{1,0:T(8,128)S(1)}) fusion(s32[12,256,256]{2,1,0:T(8,128)} %bitcast.208), kind=kLoop, calls=%fused_computation.1 | loop fusion | flops 3139584 | bytes 3170304 | tf_op jit(solution)/shard_map/reduce_sum | solution.py:160
  15.1 1.5 %convert_bitcast_fusion.2 = bf16[12,256,256,1]{2,1,0,3:T(8,128)(2,1)} fusion(s32[12,256,256]{2,1,0:T(8,128)S(1)} %bitcast.209), kind=kLoop, calls=%fused_computation.223 | loop fusion | flops 786432 | bytes 4718592 | tf_op jit(solution)/shard_map/convert_element_type | solution.py:152
  16.6 2.4 %collective-permute-start.4 = (bf16[4,64,256]{2,1,0:T(8,128)(2,1)S(1)}, bf16[4,64,256]{2,1,0:T(8,128)(2,1)}, u32[]{:S(2)}, u32[]{:S(2)}) collective-permute-start(bf16[4,64,256]{2,1,0:T(8,128)(2,1)S(1)} %maximum_bitcast_fusion), channel_id=1, source_target_pairs={{0,6},{2,4},{4,2},{6,0},{8,14},{10,12},{12,10},{14,8},{16,22},{18,... | collective-permute-start | bytes 393224 | tf_op jit(solution)/shard_map/ppermute | solution.py:45
  19.1 0.5 collective-permute-start.5
  19.6 0.5 collective-permute-start.6
  20.4 0.8 fusion.63
  21.9 2.7 %fusion = bf16[256,256,3,4]{1,3,2,0:T(4,128)(2,1)S(1)} fusion(bf16[12,256,256,1]{2,1,0,3:T(8,128)(2,1)} %convert_bitcast_fusion.2, pred[12,4]{0,1:T(4,128)(4,1)S(1)} %copy.44, pred[12,3]{0,1:T(4,128)(4,1)S(1)} %fusion.52), kind=kOutput, calls=%fused_computation.2 | convolution fusion | flops 18874512 | bytes 3145812 | tf_op jit(solution)/shard_map/trc,tij->cjri/dot_general | solution.py:156
  24.7 0.5 copy.52
  25.2 1.5 %copy.74 = bf16[96,8,4,256]{3,1,2,0:T(8,128)(2,1)} copy(bf16[96,8,4,256]{3,2,1,0:T(4,128)(2,1)S(1)} %bitcast.211) | data formatting | bytes 3145728
  26.7 0.5 copy.46
  27.3 1.5 %copy.72 = bf16[96,8,4,256]{3,1,2,0:T(8,128)(2,1)} copy(bf16[96,8,4,256]{3,2,1,0:T(4,128)(2,1)S(1)} %bitcast.210) | data formatting | bytes 3145728
  29.7 0.5 add.157
  30.2 1.1 %select_bitcast_fusion.16 = (bf16[4,1,64,256]{3,2,0,1:T(8,128)(2,1)S(1)}, bf16[4,1,64,256]{3,2,0,1:T(8,128)(2,1)S(1)}, bf16[4,1,64,256]{3,2,0,1:T(8,128)(2,1)S(1)}, bf16[4,1,64,256]{3,2,0,1:T(8,128)(2,1)S(1)}) fusion(bf16[4,64,256]{2,1,0:T(8,128)(2,1)} %collective-permute-done.4, bf16[4,64,256]{2,1,0:T(8,128)(2,1)} %collective-permute-done.5, ...), kind=kLoop, calls=%fused_computation.101 | loop fusion | flops 786432 | bytes 1048579 | tf_op jit(solution)/shard_map/stack | solution.py:134
  31.6 1.6 %copy-done.4 = bf16[96,8,4,256]{3,1,2,0:T(8,128)(2,1)S(1)} copy-done((bf16[96,8,4,256]{3,1,2,0:T(8,128)(2,1)S(1)}, bf16[96,8,4,256]{3,1,2,0:T(8,128)(2,1)}, u32[]{:S(2)}) %copy-start.4) | copy-done | bytes 1572888
  33.2 0.6 fusion.4
  34.0 2.5 %fusion.2 = (f32[256]{0:T(256)S(1)}, f32[1024,256]{1,0:T(8,128)S(1)}) fusion(bf16[4,4,64,256]{3,2,1,0:T(8,128)(2,1)} %copy-done.15, bf16[1024,256]{1,0:T(8,128)(2,1)} %bitcast.236, f32[1024]{0:T(1024)S(1)} %bitcast.244, bf16[1024,768]{0,1:T(8,128)(2,1)} %bitcast.225, bf16[768,256]{1,0:T(8,128)(2,1)} %bitcast.240), kind=kOutput, calls=%fused_computation.12 | convolution fusion | flops 404225792 | bytes 4068352 | tf_op jit(solution)/shard_map/dot_general | solution.py:169
  37.1 2.5 %collective-permute-start.9 = (bf16[259,256]{1,0:T(8,128)(2,1)S(1)}, bf16[259,256]{1,0:T(8,128)(2,1)S(1)}, u32[]{:S(2)}, u32[]{:S(2)}) collective-permute-start(bf16[259,256]{1,0:T(8,128)(2,1)S(1)} %get-tuple-element.91), channel_id=1, source_target_pairs={{0,6},{2,4},{4,2},{6,0},{8,14},{10,12},{12,10},{14,8},{16,22},{18,... | collective-permute-start | bytes 397832 | tf_op jit(solution)/shard_map/ppermute | solution.py:45
  39.6 0.5 collective-permute-start.8
  40.1 0.5 collective-permute-start.7
  40.8 3.3 %collective-permute-done.9 = bf16[259,256]{1,0:T(8,128)(2,1)S(1)} collective-permute-done((bf16[259,256]{1,0:T(8,128)(2,1)S(1)}, bf16[259,256]{1,0:T(8,128)(2,1)S(1)}, u32[]{:S(2)}, u32[]{:S(2)}) %collective-permute-start.9) | collective-permute-done | bytes 132640 | tf_op jit(solution)/shard_map/ppermute | solution.py:45
  44.1 1.2 %collective-permute-done.8 = bf16[259,256]{1,0:T(8,128)(2,1)S(1)} collective-permute-done((bf16[259,256]{1,0:T(8,128)(2,1)S(1)}, bf16[259,256]{1,0:T(8,128)(2,1)S(1)}, u32[]{:S(2)}, u32[]{:S(2)}) %collective-permute-start.8) | collective-permute-done | bytes 132640 | tf_op jit(solution)/shard_map/ppermute | solution.py:45
  45.8 3.7 %collective-permute-start.12 = (bf16[67,256]{1,0:T(8,128)(2,1)S(1)}, bf16[67,256]{1,0:T(8,128)(2,1)S(1)}, u32[]{:S(2)}, u32[]{:S(2)}) collective-permute-start(bf16[67,256]{1,0:T(8,128)(2,1)S(1)} %get-tuple-element.88), channel_id=1, source_target_pairs={{0,24},{2,26},{4,28},{6,30},{8,16},{10,18},{12,20},{14,22},{16,8},... | collective-permute-start | bytes 102920 | tf_op jit(solution)/shard_map/ppermute | solution.py:45
  49.5 0.8 collective-permute-start.10
  50.3 1.4 %collective-permute-done.12 = bf16[67,256]{1,0:T(8,128)(2,1)S(1)} collective-permute-done((bf16[67,256]{1,0:T(8,128)(2,1)S(1)}, bf16[67,256]{1,0:T(8,128)(2,1)S(1)}, u32[]{:S(2)}, u32[]{:S(2)}) %collective-permute-start.12) | collective-permute-done | bytes 34336 | tf_op jit(solution)/shard_map/ppermute | solution.py:45
  51.7 2.7 %collective-permute-done.11 = bf16[67,256]{1,0:T(8,128)(2,1)S(1)} collective-permute-done((bf16[67,256]{1,0:T(8,128)(2,1)S(1)}, bf16[67,256]{1,0:T(8,128)(2,1)S(1)}, u32[]{:S(2)}, u32[]{:S(2)}) %collective-permute-start.11) | collective-permute-done | bytes 34336 | tf_op jit(solution)/shard_map/ppermute | solution.py:45
  54.5 1.1 %collective-permute-done.13 = f32[8]{0:T(128)S(1)} collective-permute-done((f32[8]{0:T(128)S(1)}, f32[8]{0:T(128)S(1)}, u32[]{:S(2)}, u32[]{:S(2)}) %collective-permute-start.13) | collective-permute-done | bytes 64 | tf_op jit(solution)/shard_map/ppermute | solution.py:45
  55.7 0.5 copy-done.18
  56.4 1.5 %collective-permute-start.16 = (bf16[1,64,256]{2,1,0:T(8,128)(2,1)S(1)}, bf16[1,64,256]{2,1,0:T(8,128)(2,1)S(1)}, u32[]{:S(2)}, u32[]{:S(2)}) collective-permute-start(bf16[1,64,256]{2,1,0:T(8,128)(2,1)S(1)} %get-tuple-element.35), channel_id=1, source_target_pairs={{0,24},{2,26},{4,28},{6,30},{8,16},{10,18},{12,20},{14,22},{16,8},... | collective-permute-start | bytes 98312 | tf_op jit(solution)/shard_map/ppermute | solution.py:45
  57.9 0.6 collective-permute-start.17
  58.5 2.3 %collective-permute-start.18 = (bf16[1,64,256]{2,1,0:T(8,128)(2,1)S(1)}, bf16[1,64,256]{2,1,0:T(8,128)(2,1)S(1)}, u32[]{:S(2)}, u32[]{:S(2)}) collective-permute-start(bf16[1,64,256]{2,1,0:T(8,128)(2,1)S(1)} %get-tuple-element.35), channel_id=1, source_target_pairs={{0,8},{2,10},{4,12},{6,14},{8,0},{10,2},{12,4},{14,6},{16,24},{18,... | collective-permute-start | bytes 98312 | tf_op jit(solution)/shard_map/ppermute | solution.py:45
  61.0 1.4 %collective-permute-done.16 = bf16[1,64,256]{2,1,0:T(8,128)(2,1)S(1)} collective-permute-done((bf16[1,64,256]{2,1,0:T(8,128)(2,1)S(1)}, bf16[1,64,256]{2,1,0:T(8,128)(2,1)S(1)}, u32[]{:S(2)}, u32[]{:S(2)}) %collective-permute-start.16) | collective-permute-done | bytes 32800 | tf_op jit(solution)/shard_map/ppermute | solution.py:45
  62.4 0.5 collective-permute-done.17
  63.2 0.7 maximum_bitcast_fusion.1
  63.8 1.7 %collective-permute-start.19 = (bf16[4,64,256]{2,1,0:T(8,128)(2,1)}, bf16[4,64,256]{2,1,0:T(8,128)(2,1)}, u32[]{:S(2)}, u32[]{:S(2)}) collective-permute-start(bf16[4,64,256]{2,1,0:T(8,128)(2,1)} %maximum_bitcast_fusion.1), channel_id=1, source_target_pairs={{0,6},{2,4},{4,2},{6,0},{8,14},{10,12},{12,10},{14,8},{16,22},{18,... | collective-permute-start | bytes 393224 | tf_op jit(solution)/shard_map/ppermute | solution.py:45
  65.5 1.3 %collective-permute-start.20 = (bf16[4,64,256]{2,1,0:T(8,128)(2,1)}, bf16[4,64,256]{2,1,0:T(8,128)(2,1)}, u32[]{:S(2)}, u32[]{:S(2)}) collective-permute-start(bf16[4,64,256]{2,1,0:T(8,128)(2,1)} %maximum_bitcast_fusion.1), channel_id=1, source_target_pairs={{0,4},{2,6},{4,0},{6,2},{8,12},{10,14},{12,8},{14,10},{16,20},{18,... | collective-permute-start | bytes 393224 | tf_op jit(solution)/shard_map/ppermute | solution.py:45
  66.8 0.5 collective-permute-start.21
  67.5 0.8 fusion.65
  70.1 1.2 %collective-permute-done.19 = bf16[4,64,256]{2,1,0:T(8,128)(2,1)} collective-permute-done((bf16[4,64,256]{2,1,0:T(8,128)(2,1)}, bf16[4,64,256]{2,1,0:T(8,128)(2,1)}, u32[]{:S(2)}, u32[]{:S(2)}) %collective-permute-start.19) | collective-permute-done | bytes 131104 | tf_op jit(solution)/shard_map/ppermute | solution.py:45
  71.2 1.5 %collective-permute-done.20 = bf16[4,64,256]{2,1,0:T(8,128)(2,1)} collective-permute-done((bf16[4,64,256]{2,1,0:T(8,128)(2,1)}, bf16[4,64,256]{2,1,0:T(8,128)(2,1)}, u32[]{:S(2)}, u32[]{:S(2)}) %collective-permute-start.20) | collective-permute-done | bytes 131104 | tf_op jit(solution)/shard_map/ppermute | solution.py:45
  72.8 1.2 %select_bitcast_fusion.12 = (bf16[4,1,64,256]{3,2,0,1:T(8,128)(2,1)S(1)}, bf16[4,1,64,256]{3,2,0,1:T(8,128)(2,1)S(1)}, bf16[4,1,64,256]{3,2,0,1:T(8,128)(2,1)S(1)}, bf16[4,1,64,256]{3,2,0,1:T(8,128)(2,1)S(1)}) fusion(bf16[4,64,256]{2,1,0:T(8,128)(2,1)} %collective-permute-done.19, bf16[4,64,256]{2,1,0:T(8,128)(2,1)} %collective-permute-done.20, ...), kind=kLoop, calls=%fused_computation.97 | loop fusion | flops 786432 | bytes 1048579 | tf_op jit(solution)/shard_map/stack | solution.py:134
  74.1 1.1 %select_bitcast_fusion.6 = (bf16[1,1,384,256]{3,2,1,0:T(8,128)(2,1)S(1)}, bf16[1,1,384,256]{3,2,1,0:T(8,128)(2,1)S(1)}) fusion(bf16[1,384,256]{2,1,0:T(8,128)(2,1)} %collective-permute-done.15, bf16[1,384,256]{2,1,0:T(8,128)(2,1)S(1)} %get-tuple-element.32, pred[]{:T(512)S(6)} %eq.93), kind=kLoop, calls=%fused_computation.88 | loop fusion | flops 196608 | bytes 786433 | tf_op jit(solution)/shard_map/stack | solution.py:134
  75.6 0.6 fusion.5
  76.2 0.8 copy-done.6
  77.0 0.8 fusion.3
  78.7 1.6 %collective-permute-start.24 = (bf16[259,256]{1,0:T(8,128)(2,1)S(1)}, bf16[259,256]{1,0:T(8,128)(2,1)S(1)}, u32[]{:S(2)}, u32[]{:S(2)}) collective-permute-start(bf16[259,256]{1,0:T(8,128)(2,1)S(1)} %get-tuple-element.85), channel_id=1, source_target_pairs={{0,6},{2,4},{4,2},{6,0},{8,14},{10,12},{12,10},{14,8},{16,22},{18,... | collective-permute-start | bytes 397832 | tf_op jit(solution)/shard_map/ppermute | solution.py:45
  80.4 1.3 %collective-permute-start.23 = (bf16[259,256]{1,0:T(8,128)(2,1)S(1)}, bf16[259,256]{1,0:T(8,128)(2,1)S(1)}, u32[]{:S(2)}, u32[]{:S(2)}) collective-permute-start(bf16[259,256]{1,0:T(8,128)(2,1)S(1)} %get-tuple-element.84), channel_id=1, source_target_pairs={{0,4},{2,6},{4,0},{6,2},{8,12},{10,14},{12,8},{14,10},{16,20},{18,... | collective-permute-start | bytes 397832 | tf_op jit(solution)/shard_map/ppermute | solution.py:45
  81.7 0.6 collective-permute-start.22
  82.3 3.8 %collective-permute-done.24 = bf16[259,256]{1,0:T(8,128)(2,1)S(1)} collective-permute-done((bf16[259,256]{1,0:T(8,128)(2,1)S(1)}, bf16[259,256]{1,0:T(8,128)(2,1)S(1)}, u32[]{:S(2)}, u32[]{:S(2)}) %collective-permute-start.24) | collective-permute-done | bytes 132640 | tf_op jit(solution)/shard_map/ppermute | solution.py:45
  86.1 2.5 %collective-permute-done.23 = bf16[259,256]{1,0:T(8,128)(2,1)S(1)} collective-permute-done((bf16[259,256]{1,0:T(8,128)(2,1)S(1)}, bf16[259,256]{1,0:T(8,128)(2,1)S(1)}, u32[]{:S(2)}, u32[]{:S(2)}) %collective-permute-start.23) | collective-permute-done | bytes 132640 | tf_op jit(solution)/shard_map/ppermute | solution.py:45
  88.9 2.0 %collective-permute-start.27 = (bf16[67,256]{1,0:T(8,128)(2,1)S(1)}, bf16[67,256]{1,0:T(8,128)(2,1)S(1)}, u32[]{:S(2)}, u32[]{:S(2)}) collective-permute-start(bf16[67,256]{1,0:T(8,128)(2,1)S(1)} %get-tuple-element.82), channel_id=1, source_target_pairs={{0,24},{2,26},{4,28},{6,30},{8,16},{10,18},{12,20},{14,22},{16,8},... | collective-permute-start | bytes 102920 | tf_op jit(solution)/shard_map/ppermute | solution.py:45
  90.9 0.5 collective-permute-start.26
  91.4 2.0 %collective-permute-start.25 = (bf16[67,256]{1,0:T(8,128)(2,1)S(1)}, bf16[67,256]{1,0:T(8,128)(2,1)S(1)}, u32[]{:S(2)}, u32[]{:S(2)}) collective-permute-start(bf16[67,256]{1,0:T(8,128)(2,1)S(1)} %get-tuple-element.80), channel_id=1, source_target_pairs={{0,8},{2,10},{4,12},{6,14},{8,0},{10,2},{12,4},{14,6},{16,24},{18,... | collective-permute-start | bytes 102920 | tf_op jit(solution)/shard_map/ppermute | solution.py:45
  93.3 1.4 %collective-permute-done.27 = bf16[67,256]{1,0:T(8,128)(2,1)S(1)} collective-permute-done((bf16[67,256]{1,0:T(8,128)(2,1)S(1)}, bf16[67,256]{1,0:T(8,128)(2,1)S(1)}, u32[]{:S(2)}, u32[]{:S(2)}) %collective-permute-start.27) | collective-permute-done | bytes 34336 | tf_op jit(solution)/shard_map/ppermute | solution.py:45
  94.7 1.1 %collective-permute-done.26 = bf16[67,256]{1,0:T(8,128)(2,1)S(1)} collective-permute-done((bf16[67,256]{1,0:T(8,128)(2,1)S(1)}, bf16[67,256]{1,0:T(8,128)(2,1)S(1)}, u32[]{:S(2)}, u32[]{:S(2)}) %collective-permute-start.26) | collective-permute-done | bytes 34336 | tf_op jit(solution)/shard_map/ppermute | solution.py:45
  96.1 1.1 %collective-permute-done.28 = f32[8]{0:T(128)S(1)} collective-permute-done((f32[8]{0:T(128)S(1)}, f32[8]{0:T(128)S(1)}, u32[]{:S(2)}, u32[]{:S(2)}) %collective-permute-start.28) | collective-permute-done | bytes 64 | tf_op jit(solution)/shard_map/ppermute | solution.py:45
  97.6 0.7 fusion.31
  98.3 1.1 %subtract_bitcast_fusion = (f32[1,384,256]{2,1,0:T(8,128)}, f32[1,384,256]{2,1,0:T(8,128)}) fusion(f32[384,256]{1,0:T(8,128)S(1)} %get-tuple-element.16, f32[384,256]{1,0:T(8,128)S(1)} %get-tuple-element.34, f32[384,256]{1,0:T(8,128)S(1)} %reshape.375, bf16[384,256]{1,0:T(8,128)(2,1)S(1)} %collective-permute-done.29, f32[768,256]{1,0:T(8,128)S(1)} %get-tuple-element.109, ...), kind=kLoop, calls=%fused_computation.37 | loop fusion | flops 1376256 | bytes 3345409 | tf_op jit(solution)/shard_map/broadcast_in_dim | solution.py:232
  (183 shorter events, 9.1 us)
Async XLA Ops:
  0.6 19.7 %copy-start = (f32[64,64]{1,0:T(8,128)S(1)}, f32[64,64]{1,0:T(8,128)}, u32[]{:S(2)}) copy-start(f32[64,64]{1,0:T(8,128)} %param.9) | copy-start | bytes 49156
  1.5 9.0 %collective-permute-start = (bf16[1,64,256]{2,1,0:T(8,128)(2,1)S(1)}, bf16[1,64,256]{2,1,0:T(8,128)(2,1)S(1)}, u32[]{:S(2)}, u32[]{:S(2)}) collective-permute-start(bf16[1,64,256]{2,1,0:T(8,128)(2,1)S(1)} %convert_element_type.273), channel_id=1, source_target_pairs={{0,24},{2,26},{4,28},{6,30},{8,16},{10,18},{12,20},{14,22},{16,8},... | collective-permute-start | bytes 98312 | tf_op jit(solution)/shard_map/ppermute | solution.py:45
  6.5 4.8 %collective-permute-start.1 = (bf16[1,64,256]{2,1,0:T(8,128)(2,1)S(1)}, bf16[1,64,256]{2,1,0:T(8,128)(2,1)S(1)}, u32[]{:S(2)}, u32[]{:S(2)}) collective-permute-start(bf16[1,64,256]{2,1,0:T(8,128)(2,1)S(1)} %convert_element_type.273), channel_id=1, source_target_pairs={{0,16},{2,18},{4,20},{6,22},{8,24},{10,26},{12,28},{14,30},{16,0},... | collective-permute-start | bytes 98312 | tf_op jit(solution)/shard_map/ppermute | solution.py:45
  6.5 4.8 %collective-permute-start.2 = (bf16[1,64,256]{2,1,0:T(8,128)(2,1)S(1)}, bf16[1,64,256]{2,1,0:T(8,128)(2,1)S(1)}, u32[]{:S(2)}, u32[]{:S(2)}) collective-permute-start(bf16[1,64,256]{2,1,0:T(8,128)(2,1)S(1)} %convert_element_type.273), channel_id=1, source_target_pairs={{0,8},{2,10},{4,12},{6,14},{8,0},{10,2},{12,4},{14,6},{16,24},{18,... | collective-permute-start | bytes 98312 | tf_op jit(solution)/shard_map/ppermute | solution.py:45
  8.9 22.6 %collective-permute-start.3 = (bf16[1,384,256]{2,1,0:T(8,128)(2,1)}, bf16[1,384,256]{2,1,0:T(8,128)(2,1)S(1)}, u32[]{:S(2)}, u32[]{:S(2)}) collective-permute-start(bf16[1,384,256]{2,1,0:T(8,128)(2,1)} %convert_element_type.275), channel_id=1, source_target_pairs={{0,1},{1,0},{2,3},{3,2},{4,5},{5,4},{6,7},{7,6},{8,9},{9,8},{10,11... | collective-permute-start | bytes 589832 | tf_op jit(solution)/shard_map/ppermute | solution.py:45
  12.3 2.8 %copy-start.2 = (s32[1,1,12,256,256]{4,3,2,1,0:T(8,128)S(1)}, s32[1,1,12,256,256]{4,3,2,1,0:T(8,128)}, u32[]{:S(2)}) copy-start(s32[1,1,12,256,256]{4,3,2,1,0:T(8,128)} %param.11) | copy-start | bytes 9437188
  15.1 5.1 %copy-start.1 = (f32[1,384,256]{2,1,0:T(8,128)S(1)}, f32[1,384,256]{2,1,0:T(8,128)}, u32[]{:S(2)}) copy-start(f32[1,384,256]{2,1,0:T(8,128)} %param.7) | copy-start | bytes 1179652
  16.6 13.6 %collective-permute-start.4 = (bf16[4,64,256]{2,1,0:T(8,128)(2,1)S(1)}, bf16[4,64,256]{2,1,0:T(8,128)(2,1)}, u32[]{:S(2)}, u32[]{:S(2)}) collective-permute-start(bf16[4,64,256]{2,1,0:T(8,128)(2,1)S(1)} %maximum_bitcast_fusion), channel_id=1, source_target_pairs={{0,6},{2,4},{4,2},{6,0},{8,14},{10,12},{12,10},{14,8},{16,22},{18,... | collective-permute-start | bytes 393224 | tf_op jit(solution)/shard_map/ppermute | solution.py:45
  19.1 11.2 %collective-permute-start.5 = (bf16[4,64,256]{2,1,0:T(8,128)(2,1)S(1)}, bf16[4,64,256]{2,1,0:T(8,128)(2,1)}, u32[]{:S(2)}, u32[]{:S(2)}) collective-permute-start(bf16[4,64,256]{2,1,0:T(8,128)(2,1)S(1)} %maximum_bitcast_fusion), channel_id=1, source_target_pairs={{0,4},{2,6},{4,0},{6,2},{8,12},{10,14},{12,8},{14,10},{16,20},{18,... | collective-permute-start | bytes 393224 | tf_op jit(solution)/shard_map/ppermute | solution.py:45
  19.6 10.7 %collective-permute-start.6 = (bf16[4,64,256]{2,1,0:T(8,128)(2,1)S(1)}, bf16[4,64,256]{2,1,0:T(8,128)(2,1)}, u32[]{:S(2)}, u32[]{:S(2)}) collective-permute-start(bf16[4,64,256]{2,1,0:T(8,128)(2,1)S(1)} %maximum_bitcast_fusion), channel_id=1, source_target_pairs={{0,2},{2,0},{4,6},{6,4},{8,10},{10,8},{12,14},{14,12},{16,18},{18,... | collective-permute-start | bytes 393224 | tf_op jit(solution)/shard_map/ppermute | solution.py:45
  20.4 1.1 %copy-start.3 = (f32[1,64,256]{2,1,0:T(8,128)S(1)}, f32[1,64,256]{2,1,0:T(8,128)}, u32[]{:S(2)}) copy-start(f32[1,64,256]{2,1,0:T(8,128)} %param.8) | copy-start | bytes 196612
  20.4 1.2 %copy-start.17 = (f32[64,64]{1,0:T(8,128)S(1)}, f32[64,64]{1,0:T(8,128)}, u32[]{:S(2)}) copy-start(f32[64,64]{1,0:T(8,128)} %param.10) | copy-start | bytes 49156
  29.0 27.4 %copy-start.7 = (f32[64,256]{1,0:T(8,128)}, f32[64,256]{1,0:T(8,128)S(1)}, u32[]{:S(2)}) copy-start(f32[64,256]{1,0:T(8,128)S(1)} %reshape.368) | copy-start | bytes 196612
  31.4 1.7 %copy-start.4 = (bf16[96,8,4,256]{3,1,2,0:T(8,128)(2,1)S(1)}, bf16[96,8,4,256]{3,1,2,0:T(8,128)(2,1)}, u32[]{:S(2)}) copy-start(bf16[96,8,4,256]{3,1,2,0:T(8,128)(2,1)} %copy.74) | copy-start | bytes 4718596
  31.5 2.3 %copy-start.15 = (bf16[4,4,64,256]{3,2,1,0:T(8,128)(2,1)}, bf16[4,4,64,256]{3,2,1,0:T(8,128)(2,1)S(1)}, u32[]{:S(2)}) copy-start(bf16[4,4,64,256]{3,2,1,0:T(8,128)(2,1)S(1)} %copy.47) | copy-start | bytes 1572868
  31.6 2.2 %copy-start.16 = (bf16[1,2,384,256]{3,2,1,0:T(8,128)(2,1)}, bf16[1,2,384,256]{3,2,1,0:T(8,128)(2,1)S(1)}, u32[]{:S(2)}) copy-start(bf16[1,2,384,256]{3,2,1,0:T(8,128)(2,1)S(1)} %pad_maximum_fusion.2) | copy-start | bytes 1179652
  34.0 2.8 %copy-start.20 = (f32[4]{0:T(128)S(1)}, f32[4]{0:T(128)}, u32[]{:S(2)}) copy-start(f32[4]{0:T(128)} %add.157) | copy-start | bytes 52
  37.1 7.0 %collective-permute-start.9 = (bf16[259,256]{1,0:T(8,128)(2,1)S(1)}, bf16[259,256]{1,0:T(8,128)(2,1)S(1)}, u32[]{:S(2)}, u32[]{:S(2)}) collective-permute-start(bf16[259,256]{1,0:T(8,128)(2,1)S(1)} %get-tuple-element.91), channel_id=1, source_target_pairs={{0,6},{2,4},{4,2},{6,0},{8,14},{10,12},{12,10},{14,8},{16,22},{18,... | collective-permute-start | bytes 397832 | tf_op jit(solution)/shard_map/ppermute | solution.py:45
  39.6 5.7 %collective-permute-start.8 = (bf16[259,256]{1,0:T(8,128)(2,1)S(1)}, bf16[259,256]{1,0:T(8,128)(2,1)S(1)}, u32[]{:S(2)}, u32[]{:S(2)}) collective-permute-start(bf16[259,256]{1,0:T(8,128)(2,1)S(1)} %get-tuple-element.90), channel_id=1, source_target_pairs={{0,4},{2,6},{4,0},{6,2},{8,12},{10,14},{12,8},{14,10},{16,20},{18,... | collective-permute-start | bytes 397832 | tf_op jit(solution)/shard_map/ppermute | solution.py:45
  40.1 5.4 %collective-permute-start.7 = (bf16[259,256]{1,0:T(8,128)(2,1)S(1)}, bf16[259,256]{1,0:T(8,128)(2,1)S(1)}, u32[]{:S(2)}, u32[]{:S(2)}) collective-permute-start(bf16[259,256]{1,0:T(8,128)(2,1)S(1)} %get-tuple-element.89), channel_id=1, source_target_pairs={{0,2},{2,0},{4,6},{6,4},{8,10},{10,8},{12,14},{14,12},{16,18},{18,... | collective-permute-start | bytes 397832 | tf_op jit(solution)/shard_map/ppermute | solution.py:45
  40.7 20.1 %collective-permute-start.14 = (bf16[384,256]{1,0:T(8,128)(2,1)S(1)}, bf16[384,256]{1,0:T(8,128)(2,1)S(1)}, u32[]{:S(2)}, u32[]{:S(2)}) collective-permute-start(bf16[384,256]{1,0:T(8,128)(2,1)S(1)} %select_convert_fusion.1), channel_id=1, source_target_pairs={{0,1},{1,0},{2,3},{3,2},{4,5},{5,4},{6,7},{7,6},{8,9},{9,8},{10,11... | collective-permute-start | bytes 589832 | tf_op jit(solution)/shard_map/ppermute | solution.py:45
  45.8 5.9 %collective-permute-start.12 = (bf16[67,256]{1,0:T(8,128)(2,1)S(1)}, bf16[67,256]{1,0:T(8,128)(2,1)S(1)}, u32[]{:S(2)}, u32[]{:S(2)}) collective-permute-start(bf16[67,256]{1,0:T(8,128)(2,1)S(1)} %get-tuple-element.88), channel_id=1, source_target_pairs={{0,24},{2,26},{4,28},{6,30},{8,16},{10,18},{12,20},{14,22},{16,8},... | collective-permute-start | bytes 102920 | tf_op jit(solution)/shard_map/ppermute | solution.py:45
  49.5 4.9 %collective-permute-start.11 = (bf16[67,256]{1,0:T(8,128)(2,1)S(1)}, bf16[67,256]{1,0:T(8,128)(2,1)S(1)}, u32[]{:S(2)}, u32[]{:S(2)}) collective-permute-start(bf16[67,256]{1,0:T(8,128)(2,1)S(1)} %get-tuple-element.87), channel_id=1, source_target_pairs={{0,16},{2,18},{4,20},{6,22},{8,24},{10,26},{12,28},{14,30},{16,0},... | collective-permute-start | bytes 102920 | tf_op jit(solution)/shard_map/ppermute | solution.py:45
  49.5 4.9 %collective-permute-start.10 = (bf16[67,256]{1,0:T(8,128)(2,1)S(1)}, bf16[67,256]{1,0:T(8,128)(2,1)S(1)}, u32[]{:S(2)}, u32[]{:S(2)}) collective-permute-start(bf16[67,256]{1,0:T(8,128)(2,1)S(1)} %get-tuple-element.86), channel_id=1, source_target_pairs={{0,8},{2,10},{4,12},{6,14},{8,0},{10,2},{12,4},{14,6},{16,24},{18,... | collective-permute-start | bytes 102920 | tf_op jit(solution)/shard_map/ppermute | solution.py:45
  54.4 6.4 %copy-start.13 = (f32[67,256]{1,0:T(8,128)}, f32[67,256]{1,0:T(8,128)S(1)}, u32[]{:S(2)}) copy-start(f32[67,256]{1,0:T(8,128)S(1)} %fusion.23) | copy-start | bytes 205828
  54.4 1.2 %collective-permute-start.13 = (f32[8]{0:T(128)S(1)}, f32[8]{0:T(128)S(1)}, u32[]{:S(2)}, u32[]{:S(2)}) collective-permute-start(f32[8]{0:T(128)S(1)} %fusion.54), channel_id=1, source_target_pairs={{0,1},{1,0},{2,3},{3,2},{4,5},{5,4},{6,7},{7,6},{8,9},{9,8},{10,11... | collective-permute-start | bytes 104 | tf_op jit(solution)/shard_map/ppermute | solution.py:45
  55.6 0.6 copy-start.18
  56.3 12.9 %copy-start.9 = (f32[64,256]{1,0:T(8,128)}, f32[64,256]{1,0:T(8,128)S(1)}, u32[]{:S(2)}) copy-start(f32[64,256]{1,0:T(8,128)S(1)} %get-tuple-element.17) | copy-start | bytes 196612
  56.4 6.1 %collective-permute-start.16 = (bf16[1,64,256]{2,1,0:T(8,128)(2,1)S(1)}, bf16[1,64,256]{2,1,0:T(8,128)(2,1)S(1)}, u32[]{:S(2)}, u32[]{:S(2)}) collective-permute-start(bf16[1,64,256]{2,1,0:T(8,128)(2,1)S(1)} %get-tuple-element.35), channel_id=1, source_target_pairs={{0,24},{2,26},{4,28},{6,30},{8,16},{10,18},{12,20},{14,22},{16,8},... | collective-permute-start | bytes 98312 | tf_op jit(solution)/shard_map/ppermute | solution.py:45
  57.9 5.0 %collective-permute-start.17 = (bf16[1,64,256]{2,1,0:T(8,128)(2,1)S(1)}, bf16[1,64,256]{2,1,0:T(8,128)(2,1)S(1)}, u32[]{:S(2)}, u32[]{:S(2)}) collective-permute-start(bf16[1,64,256]{2,1,0:T(8,128)(2,1)S(1)} %get-tuple-element.35), channel_id=1, source_target_pairs={{0,16},{2,18},{4,20},{6,22},{8,24},{10,26},{12,28},{14,30},{16,0},... | collective-permute-start | bytes 98312 | tf_op jit(solution)/shard_map/ppermute | solution.py:45
  58.5 4.6 %collective-permute-start.18 = (bf16[1,64,256]{2,1,0:T(8,128)(2,1)S(1)}, bf16[1,64,256]{2,1,0:T(8,128)(2,1)S(1)}, u32[]{:S(2)}, u32[]{:S(2)}) collective-permute-start(bf16[1,64,256]{2,1,0:T(8,128)(2,1)S(1)} %get-tuple-element.35), channel_id=1, source_target_pairs={{0,8},{2,10},{4,12},{6,14},{8,0},{10,2},{12,4},{14,6},{16,24},{18,... | collective-permute-start | bytes 98312 | tf_op jit(solution)/shard_map/ppermute | solution.py:45
  60.9 13.2 %collective-permute-start.15 = (bf16[1,384,256]{2,1,0:T(8,128)(2,1)S(1)}, bf16[1,384,256]{2,1,0:T(8,128)(2,1)}, u32[]{:S(2)}, u32[]{:S(2)}) collective-permute-start(bf16[1,384,256]{2,1,0:T(8,128)(2,1)S(1)} %get-tuple-element.32), channel_id=1, source_target_pairs={{0,1},{1,0},{2,3},{3,2},{4,5},{5,4},{6,7},{7,6},{8,9},{9,8},{10,11... | collective-permute-start | bytes 589832 | tf_op jit(solution)/shard_map/ppermute | solution.py:45
  63.8 7.4 %collective-permute-start.19 = (bf16[4,64,256]{2,1,0:T(8,128)(2,1)}, bf16[4,64,256]{2,1,0:T(8,128)(2,1)}, u32[]{:S(2)}, u32[]{:S(2)}) collective-permute-start(bf16[4,64,256]{2,1,0:T(8,128)(2,1)} %maximum_bitcast_fusion.1), channel_id=1, source_target_pairs={{0,6},{2,4},{4,2},{6,0},{8,14},{10,12},{12,10},{14,8},{16,22},{18,... | collective-permute-start | bytes 393224 | tf_op jit(solution)/shard_map/ppermute | solution.py:45
  65.5 7.2 %collective-permute-start.20 = (bf16[4,64,256]{2,1,0:T(8,128)(2,1)}, bf16[4,64,256]{2,1,0:T(8,128)(2,1)}, u32[]{:S(2)}, u32[]{:S(2)}) collective-permute-start(bf16[4,64,256]{2,1,0:T(8,128)(2,1)} %maximum_bitcast_fusion.1), channel_id=1, source_target_pairs={{0,4},{2,6},{4,0},{6,2},{8,12},{10,14},{12,8},{14,10},{16,20},{18,... | collective-permute-start | bytes 393224 | tf_op jit(solution)/shard_map/ppermute | solution.py:45
  66.8 6.0 %collective-permute-start.21 = (bf16[4,64,256]{2,1,0:T(8,128)(2,1)}, bf16[4,64,256]{2,1,0:T(8,128)(2,1)}, u32[]{:S(2)}, u32[]{:S(2)}) collective-permute-start(bf16[4,64,256]{2,1,0:T(8,128)(2,1)} %maximum_bitcast_fusion.1), channel_id=1, source_target_pairs={{0,2},{2,0},{4,6},{6,4},{8,10},{10,8},{12,14},{14,12},{16,18},{18,... | collective-permute-start | bytes 393224 | tf_op jit(solution)/shard_map/ppermute | solution.py:45
  69.2 4.9 %copy-start.11 = (f32[64,256]{1,0:T(8,128)}, f32[64,256]{1,0:T(8,128)S(1)}, u32[]{:S(2)}) copy-start(f32[64,256]{1,0:T(8,128)S(1)} %reshape.377) | copy-start | bytes 196612
  74.1 1.5 %copy-start.5 = (bf16[96,8,4,256]{3,1,2,0:T(8,128)(2,1)S(1)}, bf16[96,8,4,256]{3,1,2,0:T(8,128)(2,1)}, u32[]{:S(2)}) copy-start(bf16[96,8,4,256]{3,1,2,0:T(8,128)(2,1)} %copy.74) | copy-start | bytes 4718596
  75.6 1.4 %copy-start.6 = (bf16[96,8,4,256]{3,1,2,0:T(8,128)(2,1)S(1)}, bf16[96,8,4,256]{3,1,2,0:T(8,128)(2,1)}, u32[]{:S(2)}) copy-start(bf16[96,8,4,256]{3,1,2,0:T(8,128)(2,1)} %copy.72) | copy-start | bytes 4718596
  78.5 19.8 %collective-permute-start.29 = (bf16[384,256]{1,0:T(8,128)(2,1)S(1)}, bf16[384,256]{1,0:T(8,128)(2,1)S(1)}, u32[]{:S(2)}, u32[]{:S(2)}) collective-permute-start(bf16[384,256]{1,0:T(8,128)(2,1)S(1)} %select_convert_fusion), channel_id=1, source_target_pairs={{0,1},{1,0},{2,3},{3,2},{4,5},{5,4},{6,7},{7,6},{8,9},{9,8},{10,11... | collective-permute-start | bytes 589832 | tf_op jit(solution)/shard_map/ppermute | solution.py:45
  78.7 7.4 %collective-permute-start.24 = (bf16[259,256]{1,0:T(8,128)(2,1)S(1)}, bf16[259,256]{1,0:T(8,128)(2,1)S(1)}, u32[]{:S(2)}, u32[]{:S(2)}) collective-permute-start(bf16[259,256]{1,0:T(8,128)(2,1)S(1)} %get-tuple-element.85), channel_id=1, source_target_pairs={{0,6},{2,4},{4,2},{6,0},{8,14},{10,12},{12,10},{14,8},{16,22},{18,... | collective-permute-start | bytes 397832 | tf_op jit(solution)/shard_map/ppermute | solution.py:45
  80.4 8.2 %collective-permute-start.23 = (bf16[259,256]{1,0:T(8,128)(2,1)S(1)}, bf16[259,256]{1,0:T(8,128)(2,1)S(1)}, u32[]{:S(2)}, u32[]{:S(2)}) collective-permute-start(bf16[259,256]{1,0:T(8,128)(2,1)S(1)} %get-tuple-element.84), channel_id=1, source_target_pairs={{0,4},{2,6},{4,0},{6,2},{8,12},{10,14},{12,8},{14,10},{16,20},{18,... | collective-permute-start | bytes 397832 | tf_op jit(solution)/shard_map/ppermute | solution.py:45
  81.7 6.9 %collective-permute-start.22 = (bf16[259,256]{1,0:T(8,128)(2,1)S(1)}, bf16[259,256]{1,0:T(8,128)(2,1)S(1)}, u32[]{:S(2)}, u32[]{:S(2)}) collective-permute-start(bf16[259,256]{1,0:T(8,128)(2,1)S(1)} %get-tuple-element.83), channel_id=1, source_target_pairs={{0,2},{2,0},{4,6},{6,4},{8,10},{10,8},{12,14},{14,12},{16,18},{18,... | collective-permute-start | bytes 397832 | tf_op jit(solution)/shard_map/ppermute | solution.py:45
  88.6 8.6 %copy-start.19 = (f32[8]{0:T(128)S(1)}, f32[8]{0:T(128)}, u32[]{:S(2)}) copy-start(f32[8]{0:T(128)} %copy-done.18) | copy-start | bytes 100
  88.6 9.0 %copy-start.8 = (f32[64,256]{1,0:T(8,128)S(1)}, f32[64,256]{1,0:T(8,128)}, u32[]{:S(2)}) copy-start(f32[64,256]{1,0:T(8,128)} %copy-done.7) | copy-start | bytes 196612
  88.6 9.0 %copy-start.10 = (f32[64,256]{1,0:T(8,128)S(1)}, f32[64,256]{1,0:T(8,128)}, u32[]{:S(2)}) copy-start(f32[64,256]{1,0:T(8,128)} %copy-done.9) | copy-start | bytes 196612
  88.6 9.0 %copy-start.12 = (f32[64,256]{1,0:T(8,128)S(1)}, f32[64,256]{1,0:T(8,128)}, u32[]{:S(2)}) copy-start(f32[64,256]{1,0:T(8,128)} %copy-done.11) | copy-start | bytes 196612
  88.6 9.0 %copy-start.14 = (f32[67,256]{1,0:T(8,128)S(1)}, f32[67,256]{1,0:T(8,128)}, u32[]{:S(2)}) copy-start(f32[67,256]{1,0:T(8,128)} %copy-done.13) | copy-start | bytes 205828
  88.9 5.8 %collective-permute-start.27 = (bf16[67,256]{1,0:T(8,128)(2,1)S(1)}, bf16[67,256]{1,0:T(8,128)(2,1)S(1)}, u32[]{:S(2)}, u32[]{:S(2)}) collective-permute-start(bf16[67,256]{1,0:T(8,128)(2,1)S(1)} %get-tuple-element.82), channel_id=1, source_target_pairs={{0,24},{2,26},{4,28},{6,30},{8,16},{10,18},{12,20},{14,22},{16,8},... | collective-permute-start | bytes 102920 | tf_op jit(solution)/shard_map/ppermute | solution.py:45
  90.9 4.9 %collective-permute-start.26 = (bf16[67,256]{1,0:T(8,128)(2,1)S(1)}, bf16[67,256]{1,0:T(8,128)(2,1)S(1)}, u32[]{:S(2)}, u32[]{:S(2)}) collective-permute-start(bf16[67,256]{1,0:T(8,128)(2,1)S(1)} %get-tuple-element.81), channel_id=1, source_target_pairs={{0,16},{2,18},{4,20},{6,22},{8,24},{10,26},{12,28},{14,30},{16,0},... | collective-permute-start | bytes 102920 | tf_op jit(solution)/shard_map/ppermute | solution.py:45
  91.4 4.6 %collective-permute-start.25 = (bf16[67,256]{1,0:T(8,128)(2,1)S(1)}, bf16[67,256]{1,0:T(8,128)(2,1)S(1)}, u32[]{:S(2)}, u32[]{:S(2)}) collective-permute-start(bf16[67,256]{1,0:T(8,128)(2,1)S(1)} %get-tuple-element.80), channel_id=1, source_target_pairs={{0,8},{2,10},{4,12},{6,14},{8,0},{10,2},{12,4},{14,6},{16,24},{18,... | collective-permute-start | bytes 102920 | tf_op jit(solution)/shard_map/ppermute | solution.py:45
  96.0 1.2 %collective-permute-start.28 = (f32[8]{0:T(128)S(1)}, f32[8]{0:T(128)S(1)}, u32[]{:S(2)}, u32[]{:S(2)}) collective-permute-start(f32[8]{0:T(128)S(1)} %fusion.53), channel_id=1, source_target_pairs={{0,1},{1,0},{2,3},{3,2},{4,5},{5,4},{6,7},{7,6},{8,9},{9,8},{10,11... | collective-permute-start | bytes 104 | tf_op jit(solution)/shard_map/ppermute | solution.py:45
